TPU v7x, 32 devices: a whole 2x2x4 slice. The times are simulated.
32 devices in a mesh: layer: 4 (over x, core), row: 4 (over z), col: 2 (over y).
Axes of the slice: x: 2, y: 2, z: 4, core: 2. Of those that a mesh axis runs over, the one named last changes fastest.
Arguments:
- sources: float32 [8, 256, 1024], P('layer', 'row', 'col'), may hold values from -14 to 14
- conduct: float32 [8, 256, 1024], P('layer', 'row', 'col'), may hold values from 0.5 to 4
- via_cond: float32 [8, 256, 1024], P('layer', 'row', 'col'), may hold values from 0.5 to 4
- via_map: int32 [8, 256, 1024], P('layer', 'row', 'col'), may hold values 0 or 1
- pad_map: int32 [256, 1024], P('row', 'col'), may hold values 0 or 1
- port_tile: int32 [4, 512], replicated, may hold values from 0 to 1023
- pivots: float32 [4, 512, 512], P(None, 'col'), may hold values from -1 to 2, as said below
- coupling: float32 [3, 512, 512], P(None, 'col'), may hold values from -0.109375 to 0.109375
Outputs:
- drop: float32 [8, 256, 1024], P('layer', 'row', 'col')
- ports: float32 [4, 512], replicated
Inputs may be any that keep to these rules, and one draw needn't show every extreme that they name: `pivots`: each block is symmetric.
All inputs are finite; a program needn't handle non-finite values. No bound on the sum of `via_map` or of `pad_map` on one device may be relied on, other than what follows from the above.
Results may differ from a plain program's by a relative error of at most 0.00023.
Values sent between devices are 32-bit elements; how exact they have to be, the bound alone decides.
No kernel may reach another device: no remote copies, remote signals or barrier semaphores. Data moves between devices by JAX's collectives and lax.ppermute only.
A program may use at most 64 MiB of HBM per device.

v0:
```python
import jax
import jax.numpy as jnp
from jax import lax
from jax.sharding import PartitionSpec as P

TILE = 16
PANEL = 512
NPANEL = 4
DEG = 3
ITERS = 2


pad_gain = 8.0
bound_low = 0.1
bound_high = 1.9
restrict_scale = 0.25
prolong_scale = 0.5


def padded(cells, sides, width):
    for axis, dim in sides:
        count = lax.axis_size(axis)
        ends = count - 1
        head = lax.slice_in_dim(cells, 0, width, axis=dim)
        tail = lax.slice_in_dim(cells, cells.shape[dim] - width, cells.shape[dim], axis=dim)
        cells = jnp.concatenate(
            [
                lax.ppermute(tail, axis, [(i, (i + 1) % count) for i in range(ends)]),
                cells,
                lax.ppermute(head, axis, [((i + 1) % count, i) for i in range(ends)]),
            ],
            axis=dim,
        )
    return cells


def shifted(grown):
    return (
        grown[2:, 1:-1, 1:-1],
        grown[:-2, 1:-1, 1:-1],
        grown[1:-1, 2:, 1:-1],
        grown[1:-1, :-2, 1:-1],
        grown[1:-1, 1:-1, 2:],
        grown[1:-1, 1:-1, :-2],
    )


def layer_grow(stack):
    return padded(stack, (("layer", 1), ("row", 2), ("col", 3)), 1)


def apply_grid(field, weights, pad_term, grow):
    grown = grow(field[None])[0]
    result = pad_term * field
    for weight, other in zip(weights, shifted(grown)):
        result = result + weight * (field - other)
    return result


def smooth(resid, weights, pad_term, inverse, grow):
    theta = (bound_high + bound_low) / 2.0
    delta = (bound_high - bound_low) / 2.0
    sigma = theta / delta
    rho = 1.0 / sigma
    change = inverse * resid / theta
    total = change
    for sweep in range(DEG - 1):
        remain = resid - apply_grid(total, weights, pad_term, grow)
        rho_new = 1.0 / (2.0 * sigma - rho)
        change = rho_new * rho * change + 2.0 * rho_new / delta * inverse * remain
        total = total + change
        rho = rho_new
    return total


def shards(sources, conduct, via_cond, via_map, pad_map, port_tile, pivots, coupling):
    highest = lax.Precision.HIGHEST
    layer_count = lax.axis_size("layer")
    vertical = via_cond * via_map.astype(jnp.float32)
    block_rows = sources.shape[1]
    currents, plane_cond, plane_vert = (sources, conduct, vertical)
    row_start = lax.axis_index("row") * block_rows
    top_flag = (lax.axis_index("layer") == layer_count - 1).astype(jnp.float32)
    local_layers, grid_rows, grid_cols = currents.shape
    grown = layer_grow(jnp.stack((plane_cond, plane_vert)))
    near_plane = shifted(grown[0])
    near_vert = shifted(grown[1])
    weights = (
        jnp.sqrt(plane_vert * near_vert[0]),
        jnp.sqrt(plane_vert * near_vert[1]),
        jnp.sqrt(plane_cond * near_plane[2]),
        jnp.sqrt(plane_cond * near_plane[3]),
        jnp.sqrt(plane_cond * near_plane[4]),
        jnp.sqrt(plane_cond * near_plane[5]),
    )
    top_layer = pad_gain * pad_map.astype(jnp.float32) * top_flag
    pad_term = jnp.concatenate(
        (jnp.zeros((local_layers - 1, grid_rows, grid_cols), jnp.float32), top_layer[None]), 0
    )
    diagonal = pad_term
    for weight in weights:
        diagonal = diagonal + weight
    inverse = 1.0 / diagonal
    total_tile_cols = grid_cols * lax.axis_size("col") // TILE
    row_tiles = (row_start + jnp.arange(grid_rows, dtype=jnp.int32)) // TILE
    col_tiles = (lax.axis_index("col") * grid_cols + jnp.arange(grid_cols, dtype=jnp.int32)) // TILE
    flat_tiles = port_tile.reshape(-1)
    row_select = (flat_tiles[:, None] // total_tile_cols == row_tiles[None, :]).astype(jnp.float32)
    col_select = (flat_tiles[:, None] % total_tile_cols == col_tiles[None, :]).astype(jnp.float32)
    share = PANEL // lax.axis_size("col")
    start = lax.axis_index("col") * share
    drop = jnp.zeros((local_layers, grid_rows, grid_cols), jnp.float32)
    ports = jnp.zeros((NPANEL, PANEL), jnp.float32)
    for outer in range(ITERS):
        resid = currents - apply_grid(drop, weights, pad_term, layer_grow)
        plane = jnp.sum(resid, axis=0)
        row_sums = jnp.dot(row_select, plane, precision=highest)
        local_rhs = jnp.sum(row_sums * col_select, axis=1).reshape(NPANEL, PANEL)
        rhs = lax.psum(local_rhs, ("layer", "row", "col")) * (restrict_scale / TILE)
        full = rhs[0]
        forward = [full]
        for section in range(1, NPANEL):
            piece = lax.dynamic_slice_in_dim(rhs[section], start, share) - jnp.dot(
                coupling[section - 1], full, precision=highest
            )
            full = lax.all_gather(piece, "col", axis=0, tiled=True)
            forward.append(full)
        scaled = [
            jnp.dot(pivots[section], forward[section], precision=highest)
            for section in range(NPANEL)
        ]
        results = [None] * NPANEL
        for section in range(NPANEL - 1, -1, -1):
            placed = lax.dynamic_update_slice_in_dim(
                jnp.zeros((PANEL,), jnp.float32), scaled[section], start, 0
            )
            if section < NPANEL - 1:
                later_rows = lax.dynamic_slice_in_dim(results[section + 1], start, share)
                placed = placed - jnp.dot(later_rows, coupling[section], precision=highest)
            results[section] = lax.psum(placed, "col")
        ports = jnp.stack(results)
        weighted_rows = jnp.transpose(row_select) * ports.reshape(-1)[None, :]
        field = jnp.dot(weighted_rows, col_select, precision=highest) * prolong_scale
        lifted = jnp.broadcast_to(field[None], (local_layers, grid_rows, grid_cols))
        drop = drop + lifted + smooth(resid, weights, pad_term, inverse, layer_grow)
    return (drop, ports)


def solution(mesh):
    placed = (
        P("layer", "row", "col"),
        P("layer", "row", "col"),
        P("layer", "row", "col"),
        P("layer", "row", "col"),
        P("row", "col"),
        P(),
        P(None, "col", None),
        P(None, "col", None),
    )
    return jax.shard_map(
        shards,
        mesh=mesh,
        in_specs=placed,
        out_specs=(P("layer", "row", "col"), P()),
        check_vma=False,
    )
```

profile of v0, /device:TPU:0, one launch (start us, length us, event | category | flops | bytes accessed | tf_op | source)
XLA Modules:
  0.0 357.5 jit_solution(15294549524432224454)
XLA Ops:
  7.2 4.5 %collective-permute-start = (f32[2,1,64,512]{3,2,1,0:T(8,128)S(1)}, f32[2,1,64,512]{3,2,1,0:T(8,128)S(1)}, u32[]{:S(2)}, u32[]{:S(2)}) collective-permute-start(f32[2,1,64,512]{3,2,1,0:T(8,128)S(1)} %get-tuple-element.40), channel_id=1, source_target_pairs={{0,8},{8,16},{16,24},{1,9},{9,17},{17,25},{2,10},{10,18},{18,26},{... | collective-permute-start | bytes 786440 | tf_op jit(solution)/shard_map/ppermute | solution.py:28
  13.3 3.5 collective-permute-start.8
  18.1 4.5 %collective-permute-start.2 = (f32[2,4,1,512]{3,2,1,0:T(1,128)S(1)}, f32[2,4,1,512]{3,2,1,0:T(1,128)S(1)}, u32[]{:S(2)}, u32[]{:S(2)}) collective-permute-start(f32[2,4,1,512]{3,2,1,0:T(1,128)S(1)} %get-tuple-element.16), channel_id=1, source_target_pairs={{0,2},{2,4},{4,6},{1,3},{3,5},{5,7},{8,10},{10,12},{12,14},{9,11},... | collective-permute-start | bytes 49160 | tf_op jit(solution)/shard_map/ppermute | solution.py:28
  24.1 3.4 collective-permute-start.10
  29.1 4.6 %collective-permute-start.4 = (f32[2,4,66,1]{3,2,1,0:T(8,128)S(1)}, f32[2,4,66,1]{3,2,1,0:T(8,128)S(1)}, u32[]{:S(2)}, u32[]{:S(2)}) collective-permute-start(f32[2,4,66,1]{3,2,1,0:T(8,128)S(1)} %get-tuple-element.14), channel_id=1, source_target_pairs={{0,1},{2,3},{4,5},{6,7},{8,9},{10,11},{12,13},{14,15},{16,17},{18,... | collective-permute-start | bytes 6344 | tf_op jit(solution)/shard_map/ppermute | solution.py:28
  35.8 4.2 %collective-permute-done.4 = f32[2,4,66,1]{3,2,1,0:T(8,128)S(1)} collective-permute-done((f32[2,4,66,1]{3,2,1,0:T(8,128)S(1)}, f32[2,4,66,1]{3,2,1,0:T(8,128)S(1)}, u32[]{:S(2)}, u32[]{:S(2)}) %collective-permute-start.4) | collective-permute-done | bytes 2144 | tf_op jit(solution)/shard_map/ppermute | solution.py:28
  40.0 4.1 %collective-permute-done.5 = f32[2,4,66,1]{3,2,1,0:T(8,128)S(1)} collective-permute-done((f32[2,4,66,1]{3,2,1,0:T(8,128)S(1)}, f32[2,4,66,1]{3,2,1,0:T(8,128)S(1)}, u32[]{:S(2)}, u32[]{:S(2)}) %collective-permute-start.5) | collective-permute-done | bytes 2144 | tf_op jit(solution)/shard_map/ppermute | solution.py:30
  50.2 40.4 %psum.70 = f32[4,512]{1,0:T(4,128)S(1)} all-reduce(f32[4,512]{1,0:T(4,128)S(1)} %reshape.145), channel_id=1, replica_groups=mesh['layer'=4,'row'=4,'col'=2] {'layer','row','col'}, use_global_device_ids=true, to_apply=%region_2.3 | all-reduce | flops 2048 | bytes 16384 | tf_op jit(solution)/shard_map/psum | solution.py:119
  93.3 4.5 %all-gather = f32[2,1,256]{2,1,0:T(1,128)S(1)} all-gather(f32[1,1,256]{2,1,0:T(1,128)S(1)} %bitcast.242), channel_id=1, replica_groups=mesh['layer'=4,'row'=4,'col'=2] {'col'}, dimensions={0}, use_global_device_ids=true | all-gather | bytes 3072 | tf_op jit(solution)/shard_map/all_gather | solution.py:126
  98.3 4.2 %all-gather.1 = f32[2,1,256]{2,1,0:T(1,128)S(1)} all-gather(f32[1,1,256]{2,1,0:T(1,128)S(1)} %bitcast.243), channel_id=1, replica_groups=mesh['layer'=4,'row'=4,'col'=2] {'col'}, dimensions={0}, use_global_device_ids=true | all-gather | bytes 3072 | tf_op jit(solution)/shard_map/all_gather | solution.py:126
  103.6 4.2 %all-gather.2 = f32[2,1,256]{2,1,0:T(1,128)S(1)} all-gather(f32[1,1,256]{2,1,0:T(1,128)S(1)} %bitcast.244), channel_id=1, replica_groups=mesh['layer'=4,'row'=4,'col'=2] {'col'}, dimensions={0}, use_global_device_ids=true | all-gather | bytes 3072 | tf_op jit(solution)/shard_map/all_gather | solution.py:126
  108.6 4.9 %psum.71 = f32[512]{0:T(512)S(1)} all-reduce(f32[512]{0:T(512)S(1)} %dynamic_update_slice.27), channel_id=1, replica_groups=mesh['layer'=4,'row'=4,'col'=2] {'col'}, use_global_device_ids=true, to_apply=%region_3.4 | all-reduce | flops 512 | bytes 4096 | tf_op jit(solution)/shard_map/psum | solution.py:140
  114.2 4.9 %psum.72 = f32[512]{0:T(512)S(1)} all-reduce(f32[512]{0:T(512)S(1)} %sub.193), channel_id=1, replica_groups=mesh['layer'=4,'row'=4,'col'=2] {'col'}, use_global_device_ids=true, to_apply=%region_4.5 | all-reduce | flops 512 | bytes 4096 | tf_op jit(solution)/shard_map/psum | solution.py:140
  127.7 3.4 collective-permute-start.14
  141.9 6.8 %psum.73 = f32[512]{0:T(512)S(1)} all-reduce(f32[512]{0:T(512)S(1)} %sub.194), channel_id=1, replica_groups=mesh['layer'=4,'row'=4,'col'=2] {'col'}, use_global_device_ids=true, to_apply=%region_5.6 | all-reduce | flops 512 | bytes 4096 | tf_op jit(solution)/shard_map/psum | solution.py:140
  161.0 4.9 %psum.74 = f32[1,512]{1,0:T(1,128)S(1)} all-reduce(f32[1,512]{1,0:T(1,128)S(1)} %bitcast.217), channel_id=1, replica_groups=mesh['layer'=4,'row'=4,'col'=2] {'col'}, use_global_device_ids=true, to_apply=%region_6.7 | all-reduce | flops 512 | bytes 4096 | tf_op jit(solution)/shard_map/psum | solution.py:140
  171.4 4.2 %collective-permute-done.21 = f32[1,4,1,512]{3,2,1,0:T(1,128)S(1)} collective-permute-done((f32[1,4,1,512]{3,2,1,0:T(1,128)S(1)}, f32[1,4,1,512]{3,2,1,0:T(1,128)S(1)}, u32[]{:S(2)}, u32[]{:S(2)}) %collective-permute-start.21) | collective-permute-done | bytes 8224 | tf_op jit(solution)/shard_map/ppermute | solution.py:30
  184.0 4.1 %collective-permute-done.23 = f32[1,4,66,1]{3,2,1,0:T(8,128)S(1)} collective-permute-done((f32[1,4,66,1]{3,2,1,0:T(8,128)S(1)}, f32[1,4,66,1]{3,2,1,0:T(8,128)S(1)}, u32[]{:S(2)}, u32[]{:S(2)}) %collective-permute-start.23) | collective-permute-done | bytes 1088 | tf_op jit(solution)/shard_map/ppermute | solution.py:30
  193.6 5.2 %collective-permute-done.25 = f32[1,1,64,512]{3,2,1,0:T(8,128)S(1)} collective-permute-done((f32[1,1,64,512]{3,2,1,0:T(8,128)S(1)}, f32[1,1,64,512]{3,2,1,0:T(8,128)S(1)}, u32[]{:S(2)}, u32[]{:S(2)}) %collective-permute-start.25) | collective-permute-done | bytes 131104 | tf_op jit(solution)/shard_map/ppermute | solution.py:30
  202.6 4.2 %collective-permute-done.27 = f32[1,4,1,512]{3,2,1,0:T(1,128)S(1)} collective-permute-done((f32[1,4,1,512]{3,2,1,0:T(1,128)S(1)}, f32[1,4,1,512]{3,2,1,0:T(1,128)S(1)}, u32[]{:S(2)}, u32[]{:S(2)}) %collective-permute-start.27) | collective-permute-done | bytes 8224 | tf_op jit(solution)/shard_map/ppermute | solution.py:30
  211.3 4.7 %collective-permute-done.29 = f32[1,4,66,1]{3,2,1,0:T(8,128)S(1)} collective-permute-done((f32[1,4,66,1]{3,2,1,0:T(8,128)S(1)}, f32[1,4,66,1]{3,2,1,0:T(8,128)S(1)}, u32[]{:S(2)}, u32[]{:S(2)}) %collective-permute-start.29) | collective-permute-done | bytes 1088 | tf_op jit(solution)/shard_map/ppermute | solution.py:30
  220.1 38.6 %psum.75 = f32[4,512]{1,0:T(4,128)S(1)} all-reduce(f32[4,512]{1,0:T(4,128)S(1)} %reshape.146), channel_id=1, replica_groups=mesh['layer'=4,'row'=4,'col'=2] {'layer','row','col'}, use_global_device_ids=true, to_apply=%region_9.10 | all-reduce | flops 2048 | bytes 16384 | tf_op jit(solution)/shard_map/psum | solution.py:119
  261.4 4.5 %all-gather.3 = f32[2,1,256]{2,1,0:T(1,128)S(1)} all-gather(f32[1,1,256]{2,1,0:T(1,128)S(1)} %bitcast.245), channel_id=1, replica_groups=mesh['layer'=4,'row'=4,'col'=2] {'col'}, dimensions={0}, use_global_device_ids=true | all-gather | bytes 3072 | tf_op jit(solution)/shard_map/all_gather | solution.py:126
  266.5 4.2 %all-gather.4 = f32[2,1,256]{2,1,0:T(1,128)S(1)} all-gather(f32[1,1,256]{2,1,0:T(1,128)S(1)} %bitcast.246), channel_id=1, replica_groups=mesh['layer'=4,'row'=4,'col'=2] {'col'}, dimensions={0}, use_global_device_ids=true | all-gather | bytes 3072 | tf_op jit(solution)/shard_map/all_gather | solution.py:126
  271.8 4.2 %all-gather.5 = f32[2,1,256]{2,1,0:T(1,128)S(1)} all-gather(f32[1,1,256]{2,1,0:T(1,128)S(1)} %bitcast.247), channel_id=1, replica_groups=mesh['layer'=4,'row'=4,'col'=2] {'col'}, dimensions={0}, use_global_device_ids=true | all-gather | bytes 3072 | tf_op jit(solution)/shard_map/all_gather | solution.py:126
  276.8 4.9 %psum.76 = f32[512]{0:T(512)S(1)} all-reduce(f32[512]{0:T(512)S(1)} %dynamic_update_slice.31), channel_id=1, replica_groups=mesh['layer'=4,'row'=4,'col'=2] {'col'}, use_global_device_ids=true, to_apply=%region_10.11 | all-reduce | flops 512 | bytes 4096 | tf_op jit(solution)/shard_map/psum | solution.py:140
  282.3 5.1 %psum.77 = f32[512]{0:T(512)S(1)} all-reduce(f32[512]{0:T(512)S(1)} %sub.220), channel_id=1, replica_groups=mesh['layer'=4,'row'=4,'col'=2] {'col'}, use_global_device_ids=true, to_apply=%region_11.12 | all-reduce | flops 512 | bytes 4096 | tf_op jit(solution)/shard_map/psum | solution.py:140
  296.0 3.8 %collective-permute-start.32 = (f32[1,4,1,512]{3,2,1,0:T(1,128)S(1)}, f32[1,4,1,512]{3,2,1,0:T(1,128)S(1)}, u32[]{:S(2)}, u32[]{:S(2)}) collective-permute-start(f32[1,4,1,512]{3,2,1,0:T(1,128)S(1)} %get-tuple-element.32), channel_id=1, source_target_pairs={{0,2},{2,4},{4,6},{1,3},{3,5},{5,7},{8,10},{10,12},{12,14},{9,11},... | collective-permute-start | bytes 24584 | tf_op jit(solution)/shard_map/ppermute | solution.py:28
  306.2 3.9 %collective-permute-start.34 = (f32[1,4,66,1]{3,2,1,0:T(8,128)}, f32[1,4,66,1]{3,2,1,0:T(8,128)S(1)}, u32[]{:S(2)}, u32[]{:S(2)}) collective-permute-start(f32[1,4,66,1]{3,2,1,0:T(8,128)} %get-tuple-element.20), channel_id=1, source_target_pairs={{0,1},{2,3},{4,5},{6,7},{8,9},{10,11},{12,13},{14,15},{16,17},{18,... | collective-permute-start | bytes 3176 | tf_op jit(solution)/shard_map/ppermute | solution.py:28
  311.4 6.8 %psum.78 = f32[512]{0:T(512)S(1)} all-reduce(f32[512]{0:T(512)S(1)} %sub.221), channel_id=1, replica_groups=mesh['layer'=4,'row'=4,'col'=2] {'col'}, use_global_device_ids=true, to_apply=%region_12.13 | all-reduce | flops 512 | bytes 4096 | tf_op jit(solution)/shard_map/psum | solution.py:140
  328.6 4.9 %psum.79 = f32[1,512]{1,0:T(1,128)S(1)} all-reduce(f32[1,512]{1,0:T(1,128)S(1)} %bitcast.218), channel_id=1, replica_groups=mesh['layer'=4,'row'=4,'col'=2] {'col'}, use_global_device_ids=true, to_apply=%region_13.14 | all-reduce | flops 512 | bytes 4096 | tf_op jit(solution)/shard_map/psum | solution.py:140
  350.3 4.1 %collective-permute-done.41 = f32[1,4,66,1]{3,2,1,0:T(8,128)S(1)} collective-permute-done((f32[1,4,66,1]{3,2,1,0:T(8,128)S(1)}, f32[1,4,66,1]{3,2,1,0:T(8,128)S(1)}, u32[]{:S(2)}, u32[]{:S(2)}) %collective-permute-start.41) | collective-permute-done | bytes 1088 | tf_op jit(solution)/shard_map/ppermute | solution.py:30
  (313 shorter events, 140.7 us)
Async XLA Ops:
  0.7 12.5 %collective-permute-start.7 = (f32[1,1,64,512]{3,2,1,0:T(8,128)S(1)}, f32[1,1,64,512]{3,2,1,0:T(8,128)S(1)}, u32[]{:S(2)}, u32[]{:S(2)}) collective-permute-start(f32[1,1,64,512]{3,2,1,0:T(8,128)S(1)} %broadcast.185), channel_id=1, source_target_pairs={{8,0},{16,8},{24,16},{9,1},{17,9},{25,17},{10,2},{18,10},{26,18},{... | collective-permute-start | bytes 393224 | tf_op jit(solution)/shard_map/ppermute | solution.py:30
  2.1 11.1 %collective-permute-start.6 = (f32[1,1,64,512]{3,2,1,0:T(8,128)S(1)}, f32[1,1,64,512]{3,2,1,0:T(8,128)S(1)}, u32[]{:S(2)}, u32[]{:S(2)}) collective-permute-start(f32[1,1,64,512]{3,2,1,0:T(8,128)S(1)} %broadcast.185), channel_id=1, source_target_pairs={{0,8},{8,16},{16,24},{1,9},{9,17},{17,25},{2,10},{10,18},{18,26},{... | collective-permute-start | bytes 393224 | tf_op jit(solution)/shard_map/ppermute | solution.py:28
  7.2 10.8 %collective-permute-start = (f32[2,1,64,512]{3,2,1,0:T(8,128)S(1)}, f32[2,1,64,512]{3,2,1,0:T(8,128)S(1)}, u32[]{:S(2)}, u32[]{:S(2)}) collective-permute-start(f32[2,1,64,512]{3,2,1,0:T(8,128)S(1)} %get-tuple-element.40), channel_id=1, source_target_pairs={{0,8},{8,16},{16,24},{1,9},{9,17},{17,25},{2,10},{10,18},{18,26},{... | collective-permute-start | bytes 786440 | tf_op jit(solution)/shard_map/ppermute | solution.py:28
  11.7 6.3 %collective-permute-start.1 = (f32[2,1,64,512]{3,2,1,0:T(8,128)S(1)}, f32[2,1,64,512]{3,2,1,0:T(8,128)S(1)}, u32[]{:S(2)}, u32[]{:S(2)}) collective-permute-start(f32[2,1,64,512]{3,2,1,0:T(8,128)S(1)} %get-tuple-element.41), channel_id=1, source_target_pairs={{8,0},{16,8},{24,16},{9,1},{17,9},{25,17},{10,2},{18,10},{26,18},{... | collective-permute-start | bytes 786440 | tf_op jit(solution)/shard_map/ppermute | solution.py:30
  13.3 10.7 %collective-permute-start.8 = (f32[1,4,1,512]{3,2,1,0:T(1,128)S(1)}, f32[1,4,1,512]{3,2,1,0:T(1,128)S(1)}, u32[]{:S(2)}, u32[]{:S(2)}) collective-permute-start(f32[1,4,1,512]{3,2,1,0:T(1,128)S(1)} %get-tuple-element.42), channel_id=1, source_target_pairs={{0,2},{2,4},{4,6},{1,3},{3,5},{5,7},{8,10},{10,12},{12,14},{9,11},... | collective-permute-start | bytes 24584 | tf_op jit(solution)/shard_map/ppermute | solution.py:28
  16.8 7.2 %collective-permute-start.9 = (f32[1,4,1,512]{3,2,1,0:T(1,128)S(1)}, f32[1,4,1,512]{3,2,1,0:T(1,128)S(1)}, u32[]{:S(2)}, u32[]{:S(2)}) collective-permute-start(f32[1,4,1,512]{3,2,1,0:T(1,128)S(1)} %get-tuple-element.43), channel_id=1, source_target_pairs={{2,0},{4,2},{6,4},{3,1},{5,3},{7,5},{10,8},{12,10},{14,12},{11,9},... | collective-permute-start | bytes 24584 | tf_op jit(solution)/shard_map/ppermute | solution.py:30
  18.1 10.7 %collective-permute-start.2 = (f32[2,4,1,512]{3,2,1,0:T(1,128)S(1)}, f32[2,4,1,512]{3,2,1,0:T(1,128)S(1)}, u32[]{:S(2)}, u32[]{:S(2)}) collective-permute-start(f32[2,4,1,512]{3,2,1,0:T(1,128)S(1)} %get-tuple-element.16), channel_id=1, source_target_pairs={{0,2},{2,4},{4,6},{1,3},{3,5},{5,7},{8,10},{10,12},{12,14},{9,11},... | collective-permute-start | bytes 49160 | tf_op jit(solution)/shard_map/ppermute | solution.py:28
  22.7 6.2 %collective-permute-start.3 = (f32[2,4,1,512]{3,2,1,0:T(1,128)S(1)}, f32[2,4,1,512]{3,2,1,0:T(1,128)S(1)}, u32[]{:S(2)}, u32[]{:S(2)}) collective-permute-start(f32[2,4,1,512]{3,2,1,0:T(1,128)S(1)} %get-tuple-element.17), channel_id=1, source_target_pairs={{2,0},{4,2},{6,4},{3,1},{5,3},{7,5},{10,8},{12,10},{14,12},{11,9},... | collective-permute-start | bytes 49160 | tf_op jit(solution)/shard_map/ppermute | solution.py:30
  24.1 10.8 %collective-permute-start.10 = (f32[1,4,66,1]{3,2,1,0:T(8,128)S(1)}, f32[1,4,66,1]{3,2,1,0:T(8,128)S(1)}, u32[]{:S(2)}, u32[]{:S(2)}) collective-permute-start(f32[1,4,66,1]{3,2,1,0:T(8,128)S(1)} %get-tuple-element.28), channel_id=1, source_target_pairs={{0,1},{2,3},{4,5},{6,7},{8,9},{10,11},{12,13},{14,15},{16,17},{18,... | collective-permute-start | bytes 3176 | tf_op jit(solution)/shard_map/ppermute | solution.py:28
  27.6 7.8 %collective-permute-start.11 = (f32[1,4,66,1]{3,2,1,0:T(8,128)S(1)}, f32[1,4,66,1]{3,2,1,0:T(8,128)S(1)}, u32[]{:S(2)}, u32[]{:S(2)}) collective-permute-start(f32[1,4,66,1]{3,2,1,0:T(8,128)S(1)} %get-tuple-element.29), channel_id=1, source_target_pairs={{1,0},{3,2},{5,4},{7,6},{9,8},{11,10},{13,12},{15,14},{17,16},{19,... | collective-permute-start | bytes 3176 | tf_op jit(solution)/shard_map/ppermute | solution.py:30
  29.1 10.9 %collective-permute-start.4 = (f32[2,4,66,1]{3,2,1,0:T(8,128)S(1)}, f32[2,4,66,1]{3,2,1,0:T(8,128)S(1)}, u32[]{:S(2)}, u32[]{:S(2)}) collective-permute-start(f32[2,4,66,1]{3,2,1,0:T(8,128)S(1)} %get-tuple-element.14), channel_id=1, source_target_pairs={{0,1},{2,3},{4,5},{6,7},{8,9},{10,11},{12,13},{14,15},{16,17},{18,... | collective-permute-start | bytes 6344 | tf_op jit(solution)/shard_map/ppermute | solution.py:28
  33.6 10.4 %collective-permute-start.5 = (f32[2,4,66,1]{3,2,1,0:T(8,128)S(1)}, f32[2,4,66,1]{3,2,1,0:T(8,128)S(1)}, u32[]{:S(2)}, u32[]{:S(2)}) collective-permute-start(f32[2,4,66,1]{3,2,1,0:T(8,128)S(1)} %get-tuple-element.15), channel_id=1, source_target_pairs={{1,0},{3,2},{5,4},{7,6},{9,8},{11,10},{13,12},{15,14},{17,16},{19,... | collective-permute-start | bytes 6344 | tf_op jit(solution)/shard_map/ppermute | solution.py:30
  127.7 5.9 %collective-permute-start.14 = (f32[1,4,1,512]{3,2,1,0:T(1,128)S(1)}, f32[1,4,1,512]{3,2,1,0:T(1,128)S(1)}, u32[]{:S(2)}, u32[]{:S(2)}) collective-permute-start(f32[1,4,1,512]{3,2,1,0:T(1,128)S(1)} %get-tuple-element.38), channel_id=1, source_target_pairs={{0,2},{2,4},{4,6},{1,3},{3,5},{5,7},{8,10},{10,12},{12,14},{9,11},... | collective-permute-start | bytes 24584 | tf_op jit(solution)/shard_map/ppermute | solution.py:28
  131.1 5.5 %collective-permute-start.15 = (f32[1,4,1,512]{3,2,1,0:T(1,128)S(1)}, f32[1,4,1,512]{3,2,1,0:T(1,128)S(1)}, u32[]{:S(2)}, u32[]{:S(2)}) collective-permute-start(f32[1,4,1,512]{3,2,1,0:T(1,128)S(1)} %get-tuple-element.39), channel_id=1, source_target_pairs={{2,0},{4,2},{6,4},{3,1},{5,3},{7,5},{10,8},{12,10},{14,12},{11,9},... | collective-permute-start | bytes 24584 | tf_op jit(solution)/shard_map/ppermute | solution.py:30
  137.4 12.7 %collective-permute-start.16 = (f32[1,4,66,1]{3,2,1,0:T(8,128)}, f32[1,4,66,1]{3,2,1,0:T(8,128)S(1)}, u32[]{:S(2)}, u32[]{:S(2)}) collective-permute-start(f32[1,4,66,1]{3,2,1,0:T(8,128)} %get-tuple-element.26), channel_id=1, source_target_pairs={{0,1},{2,3},{4,5},{6,7},{8,9},{10,11},{12,13},{14,15},{16,17},{18,... | collective-permute-start | bytes 3176 | tf_op jit(solution)/shard_map/ppermute | solution.py:28
  140.6 10.8 %collective-permute-start.17 = (f32[1,4,66,1]{3,2,1,0:T(8,128)}, f32[1,4,66,1]{3,2,1,0:T(8,128)}, u32[]{:S(2)}, u32[]{:S(2)}) collective-permute-start(f32[1,4,66,1]{3,2,1,0:T(8,128)} %get-tuple-element.27), channel_id=1, source_target_pairs={{1,0},{3,2},{5,4},{7,6},{9,8},{11,10},{13,12},{15,14},{17,16},{19,... | collective-permute-start | bytes 3176 | tf_op jit(solution)/shard_map/ppermute | solution.py:30
  156.0 9.9 %collective-permute-start.18 = (f32[1,1,64,512]{3,2,1,0:T(8,128)}, f32[1,1,64,512]{3,2,1,0:T(8,128)}, u32[]{:S(2)}, u32[]{:S(2)}) collective-permute-start(f32[1,1,64,512]{3,2,1,0:T(8,128)} %get-tuple-element.50), channel_id=1, source_target_pairs={{0,8},{8,16},{16,24},{1,9},{9,17},{17,25},{2,10},{10,18},{18,26},{... | collective-permute-start | bytes 393224 | tf_op jit(solution)/shard_map/ppermute | solution.py:28
  159.3 6.6 %collective-permute-start.19 = (f32[1,1,64,512]{3,2,1,0:T(8,128)}, f32[1,1,64,512]{3,2,1,0:T(8,128)}, u32[]{:S(2)}, u32[]{:S(2)}) collective-permute-start(f32[1,1,64,512]{3,2,1,0:T(8,128)} %get-tuple-element.51), channel_id=1, source_target_pairs={{8,0},{16,8},{24,16},{9,1},{17,9},{25,17},{10,2},{18,10},{26,18},{... | collective-permute-start | bytes 393224 | tf_op jit(solution)/shard_map/ppermute | solution.py:30
  170.1 5.5 %collective-permute-start.21 = (f32[1,4,1,512]{3,2,1,0:T(1,128)S(1)}, f32[1,4,1,512]{3,2,1,0:T(1,128)S(1)}, u32[]{:S(2)}, u32[]{:S(2)}) collective-permute-start(f32[1,4,1,512]{3,2,1,0:T(1,128)S(1)} %get-tuple-element.37), channel_id=1, source_target_pairs={{2,0},{4,2},{6,4},{3,1},{5,3},{7,5},{10,8},{12,10},{14,12},{11,9},... | collective-permute-start | bytes 24584 | tf_op jit(solution)/shard_map/ppermute | solution.py:30
  176.7 7.3 %collective-permute-start.22 = (f32[1,4,66,1]{3,2,1,0:T(8,128)S(1)}, f32[1,4,66,1]{3,2,1,0:T(8,128)S(1)}, u32[]{:S(2)}, u32[]{:S(2)}) collective-permute-start(f32[1,4,66,1]{3,2,1,0:T(8,128)S(1)} %get-tuple-element.24), channel_id=1, source_target_pairs={{0,1},{2,3},{4,5},{6,7},{8,9},{10,11},{12,13},{14,15},{16,17},{18,... | collective-permute-start | bytes 3176 | tf_op jit(solution)/shard_map/ppermute | solution.py:28
  179.9 8.2 %collective-permute-start.23 = (f32[1,4,66,1]{3,2,1,0:T(8,128)S(1)}, f32[1,4,66,1]{3,2,1,0:T(8,128)S(1)}, u32[]{:S(2)}, u32[]{:S(2)}) collective-permute-start(f32[1,4,66,1]{3,2,1,0:T(8,128)S(1)} %get-tuple-element.25), channel_id=1, source_target_pairs={{1,0},{3,2},{5,4},{7,6},{9,8},{11,10},{13,12},{15,14},{17,16},{19,... | collective-permute-start | bytes 3176 | tf_op jit(solution)/shard_map/ppermute | solution.py:30
  192.3 6.5 %collective-permute-start.25 = (f32[1,1,64,512]{3,2,1,0:T(8,128)S(1)}, f32[1,1,64,512]{3,2,1,0:T(8,128)S(1)}, u32[]{:S(2)}, u32[]{:S(2)}) collective-permute-start(f32[1,1,64,512]{3,2,1,0:T(8,128)S(1)} %get-tuple-element.49), channel_id=1, source_target_pairs={{8,0},{16,8},{24,16},{9,1},{17,9},{25,17},{10,2},{18,10},{26,18},{... | collective-permute-start | bytes 393224 | tf_op jit(solution)/shard_map/ppermute | solution.py:30
  208.4 7.6 %collective-permute-start.29 = (f32[1,4,66,1]{3,2,1,0:T(8,128)S(1)}, f32[1,4,66,1]{3,2,1,0:T(8,128)S(1)}, u32[]{:S(2)}, u32[]{:S(2)}) collective-permute-start(f32[1,4,66,1]{3,2,1,0:T(8,128)S(1)} %get-tuple-element.23), channel_id=1, source_target_pairs={{1,0},{3,2},{5,4},{7,6},{9,8},{11,10},{13,12},{15,14},{17,16},{19,... | collective-permute-start | bytes 3176 | tf_op jit(solution)/shard_map/ppermute | solution.py:30
  296.0 6.3 %collective-permute-start.32 = (f32[1,4,1,512]{3,2,1,0:T(1,128)S(1)}, f32[1,4,1,512]{3,2,1,0:T(1,128)S(1)}, u32[]{:S(2)}, u32[]{:S(2)}) collective-permute-start(f32[1,4,1,512]{3,2,1,0:T(1,128)S(1)} %get-tuple-element.32), channel_id=1, source_target_pairs={{0,2},{2,4},{4,6},{1,3},{3,5},{5,7},{8,10},{10,12},{12,14},{9,11},... | collective-permute-start | bytes 24584 | tf_op jit(solution)/shard_map/ppermute | solution.py:28
  306.2 12.1 %collective-permute-start.34 = (f32[1,4,66,1]{3,2,1,0:T(8,128)}, f32[1,4,66,1]{3,2,1,0:T(8,128)S(1)}, u32[]{:S(2)}, u32[]{:S(2)}) collective-permute-start(f32[1,4,66,1]{3,2,1,0:T(8,128)} %get-tuple-element.20), channel_id=1, source_target_pairs={{0,1},{2,3},{4,5},{6,7},{8,9},{10,11},{12,13},{14,15},{16,17},{18,... | collective-permute-start | bytes 3176 | tf_op jit(solution)/shard_map/ppermute | solution.py:28
  310.1 9.3 %collective-permute-start.35 = (f32[1,4,66,1]{3,2,1,0:T(8,128)}, f32[1,4,66,1]{3,2,1,0:T(8,128)}, u32[]{:S(2)}, u32[]{:S(2)}) collective-permute-start(f32[1,4,66,1]{3,2,1,0:T(8,128)} %get-tuple-element.21), channel_id=1, source_target_pairs={{1,0},{3,2},{5,4},{7,6},{9,8},{11,10},{13,12},{15,14},{17,16},{19,... | collective-permute-start | bytes 3176 | tf_op jit(solution)/shard_map/ppermute | solution.py:30
  323.4 10.2 %collective-permute-start.36 = (f32[1,1,64,512]{3,2,1,0:T(8,128)}, f32[1,1,64,512]{3,2,1,0:T(8,128)}, u32[]{:S(2)}, u32[]{:S(2)}) collective-permute-start(f32[1,1,64,512]{3,2,1,0:T(8,128)} %get-tuple-element.44), channel_id=1, source_target_pairs={{0,8},{8,16},{16,24},{1,9},{9,17},{17,25},{2,10},{10,18},{18,26},{... | collective-permute-start | bytes 393224 | tf_op jit(solution)/shard_map/ppermute | solution.py:28
  326.6 6.9 %collective-permute-start.37 = (f32[1,1,64,512]{3,2,1,0:T(8,128)}, f32[1,1,64,512]{3,2,1,0:T(8,128)}, u32[]{:S(2)}, u32[]{:S(2)}) collective-permute-start(f32[1,1,64,512]{3,2,1,0:T(8,128)} %get-tuple-element.45), channel_id=1, source_target_pairs={{8,0},{16,8},{24,16},{9,1},{17,9},{25,17},{10,2},{18,10},{26,18},{... | collective-permute-start | bytes 393224 | tf_op jit(solution)/shard_map/ppermute | solution.py:30
  334.4 6.1 %collective-permute-start.38 = (f32[1,4,1,512]{3,2,1,0:T(1,128)S(1)}, f32[1,4,1,512]{3,2,1,0:T(1,128)S(1)}, u32[]{:S(2)}, u32[]{:S(2)}) collective-permute-start(f32[1,4,1,512]{3,2,1,0:T(1,128)S(1)} %get-tuple-element.30), channel_id=1, source_target_pairs={{0,2},{2,4},{4,6},{1,3},{3,5},{5,7},{8,10},{10,12},{12,14},{9,11},... | collective-permute-start | bytes 24584 | tf_op jit(solution)/shard_map/ppermute | solution.py:28
  337.0 5.6 %collective-permute-start.39 = (f32[1,4,1,512]{3,2,1,0:T(1,128)S(1)}, f32[1,4,1,512]{3,2,1,0:T(1,128)S(1)}, u32[]{:S(2)}, u32[]{:S(2)}) collective-permute-start(f32[1,4,1,512]{3,2,1,0:T(1,128)S(1)} %get-tuple-element.31), channel_id=1, source_target_pairs={{2,0},{4,2},{6,4},{3,1},{5,3},{7,5},{10,8},{12,10},{14,12},{11,9},... | collective-permute-start | bytes 24584 | tf_op jit(solution)/shard_map/ppermute | solution.py:30
  343.5 6.8 %collective-permute-start.40 = (f32[1,4,66,1]{3,2,1,0:T(8,128)S(1)}, f32[1,4,66,1]{3,2,1,0:T(8,128)S(1)}, u32[]{:S(2)}, u32[]{:S(2)}) collective-permute-start(f32[1,4,66,1]{3,2,1,0:T(8,128)S(1)} %get-tuple-element.18), channel_id=1, source_target_pairs={{0,1},{2,3},{4,5},{6,7},{8,9},{10,11},{12,13},{14,15},{16,17},{18,... | collective-permute-start | bytes 3176 | tf_op jit(solution)/shard_map/ppermute | solution.py:28
  346.5 8.0 %collective-permute-start.41 = (f32[1,4,66,1]{3,2,1,0:T(8,128)S(1)}, f32[1,4,66,1]{3,2,1,0:T(8,128)S(1)}, u32[]{:S(2)}, u32[]{:S(2)}) collective-permute-start(f32[1,4,66,1]{3,2,1,0:T(8,128)S(1)} %get-tuple-element.19), channel_id=1, source_target_pairs={{1,0},{3,2},{5,4},{7,6},{9,8},{11,10},{13,12},{15,14},{17,16},{19,... | collective-permute-start | bytes 3176 | tf_op jit(solution)/shard_map/ppermute | solution.py:30
  (73 other events, 1146.2 us)
where the time goes:
time: 360 us; the launch traced here: 357 us
  blocking collectives  148 us (41%)
  starting transfers between devices  91.9 us (26%)
  waiting for transfers between devices  51.9 us (14%)
  other arithmetic  26.6 us (7%)
  matrix products  25.4 us (7%)
  local copies, waits for them, and re-layouts  11.5 us (3%)
    psum x2, blocking collectives, shards(): rhs = lax.psum(local_rhs, ('layer', 'row', 'col')) * (restrict_scale / TILE)  78.9 us
    ppermute x21, starting transfers between devices, padded(): lax.ppermute(tail, axis, [(i, (i + 1) % count) for i in range(ends)])  64.6 us
    ppermute x21, waiting for transfers between devices, padded(): lax.ppermute(head, axis, [((i + 1) % count, i) for i in range(ends)])  43.4 us
    psum x8, blocking collectives, shards(): results[section] = lax.psum(placed, 'col')  43.3 us
    ppermute x21, starting transfers between devices, padded(): lax.ppermute(head, axis, [((i + 1) % count, i) for i in range(ends)])  27.2 us
    all_gather x6, blocking collectives, shards(): full = lax.all_gather(piece, 'col', axis=0, tiled=True)  25.9 us
    dot_general x8, matrix products, shards(): jnp.dot(pivots[section], forward[section], precision=highest)  10.7 us
    ppermute x21, waiting for transfers between devices, padded(): lax.ppermute(tail, axis, [(i, (i + 1) % count) for i in range(ends)])  8.44 us
  transfers between devices with their start and end apart: 42, of which 17 were waited for; matrix products, arithmetic and copies ran while one was open for 5% of the time, Pallas kernels for 0%

commit v1 on v0

v1 whole, which is shorter than its diff:
```python
import jax
import jax.numpy as jnp
from jax import lax
from jax.sharding import PartitionSpec as P

TILE = 16
PANEL = 512
NPANEL = 4
DEG = 3
ITERS = 2


pad_gain = 8.0
bound_low = 0.1
bound_high = 1.9
restrict_scale = 0.25
prolong_scale = 0.5

highest = lax.Precision.HIGHEST
GRID_AXES = (("layer", 0), ("row", 1), ("col", 2))


def rims(field, axis, dim):
    count = lax.axis_size(axis)
    size = field.shape[dim]
    head = lax.slice_in_dim(field, 0, 1, axis=dim)
    tail = lax.slice_in_dim(field, size - 1, size, axis=dim)
    below = lax.ppermute(tail, axis, [(i, i + 1) for i in range(count - 1)])
    above = lax.ppermute(head, axis, [(i + 1, i) for i in range(count - 1)])
    return above, below


def neighbours(field, halo):
    out = []
    for (axis, dim), (above, below) in zip(GRID_AXES, halo):
        size = field.shape[dim]
        out.append(jnp.concatenate([lax.slice_in_dim(field, 1, size, axis=dim), above], axis=dim))
        out.append(jnp.concatenate([below, lax.slice_in_dim(field, 0, size - 1, axis=dim)], axis=dim))
    return out


def exchange(field):
    return [rims(field, axis, dim) for axis, dim in GRID_AXES]


def apply_grid(field, near, weights, pad_term):
    result = pad_term * field
    for weight, other in zip(weights, near):
        result = result + weight * (field - other)
    return result


def smooth(resid, weights, pad_term, inverse):
    theta = (bound_high + bound_low) / 2.0
    delta = (bound_high - bound_low) / 2.0
    sigma = theta / delta
    rho = 1.0 / sigma
    change = inverse * resid / theta
    total = change
    for sweep in range(DEG - 1):
        remain = resid - apply_grid(total, neighbours(total, exchange(total)), weights, pad_term)
        rho_new = 1.0 / (2.0 * sigma - rho)
        change = rho_new * rho * change + 2.0 * rho_new / delta * inverse * remain
        total = total + change
        rho = rho_new
    return total


def all_sum(value):
    for axis, _ in GRID_AXES:
        count = lax.axis_size(axis)
        if count & (count - 1):
            value = lax.psum(value, axis)
            continue
        step = 1
        while step < count:
            value = value + lax.ppermute(value, axis, [(i, i ^ step) for i in range(count)])
            step *= 2
    return value


def swap_col(value):
    return lax.ppermute(value, "col", [(0, 1), (1, 0)])


def join_halves(mine, other, low):
    return jnp.where(low, jnp.concatenate([mine, other]), jnp.concatenate([other, mine]))


def coarse_pair(rhs, pivots, coupling):
    share = pivots.shape[1]
    low = lax.axis_index("col") == 0
    start = lax.axis_index("col") * share
    own = lambda vector: lax.dynamic_slice_in_dim(vector, start, share)
    other_half = lambda vector: lax.dynamic_slice_in_dim(vector, share - start, share)
    full = rhs[0]
    forward = [full]
    for section in range(1, NPANEL):
        piece = own(rhs[section]) - jnp.dot(coupling[section - 1], full, precision=highest)
        full = join_halves(piece, swap_col(piece), low)
        forward.append(full)
    scaled = [jnp.dot(pivots[section], forward[section], precision=highest) for section in range(NPANEL)]
    mine = scaled[NPANEL - 1]
    results = [None] * NPANEL
    for section in range(NPANEL - 2, 0, -1):
        partial = jnp.dot(mine, coupling[section], precision=highest)
        got = swap_col(jnp.concatenate([other_half(partial), mine]))
        results[section + 1] = join_halves(mine, got[share:], low)
        mine = scaled[section] - (own(partial) + got[:share])
    partial = jnp.dot(mine, coupling[0], precision=highest)
    got = swap_col(jnp.concatenate([partial, scaled[0], mine]))
    results[1] = join_halves(mine, got[PANEL + share:], low)
    first = join_halves(scaled[0], got[PANEL:PANEL + share], low)
    low_part = jnp.where(low, partial, got[:PANEL])
    high_part = jnp.where(low, got[:PANEL], partial)
    results[0] = first - (low_part + high_part)
    return jnp.stack(results)


def coarse_general(rhs, pivots, coupling):
    share = pivots.shape[1]
    start = lax.axis_index("col") * share
    full = rhs[0]
    forward = [full]
    for section in range(1, NPANEL):
        piece = lax.dynamic_slice_in_dim(rhs[section], start, share) - jnp.dot(
            coupling[section - 1], full, precision=highest
        )
        full = lax.all_gather(piece, "col", axis=0, tiled=True)
        forward.append(full)
    scaled = [jnp.dot(pivots[section], forward[section], precision=highest) for section in range(NPANEL)]
    results = [None] * NPANEL
    for section in range(NPANEL - 1, -1, -1):
        placed = lax.dynamic_update_slice_in_dim(jnp.zeros((PANEL,), jnp.float32), scaled[section], start, 0)
        if section < NPANEL - 1:
            later_rows = lax.dynamic_slice_in_dim(results[section + 1], start, share)
            placed = placed - jnp.dot(later_rows, coupling[section], precision=highest)
        results[section] = lax.psum(placed, "col")
    return jnp.stack(results)


def expand(values, edge):
    inner = values[1:-1] if edge else values
    body = jnp.repeat(inner, TILE, axis=0)
    if edge:
        body = jnp.concatenate([values[:1], body, values[-1:]], axis=0)
    return body


def shards(sources, conduct, via_cond, via_map, pad_map, port_tile, pivots, coupling):
    layer_count = lax.axis_size("layer")
    local_layers, grid_rows, grid_cols = sources.shape
    vertical = via_cond * via_map.astype(jnp.float32)
    vert_above, vert_below = rims(vertical, "layer", 0)
    row_halo = rims(conduct, "row", 1)
    col_halo = rims(conduct, "col", 2)
    near_vert = neighbours(vertical, [(vert_above, vert_below), row_halo, col_halo])
    near_plane = neighbours(conduct, [(vert_above, vert_below), row_halo, col_halo])
    weights = (
        jnp.sqrt(vertical * near_vert[0]),
        jnp.sqrt(vertical * near_vert[1]),
        jnp.sqrt(conduct * near_plane[2]),
        jnp.sqrt(conduct * near_plane[3]),
        jnp.sqrt(conduct * near_plane[4]),
        jnp.sqrt(conduct * near_plane[5]),
    )
    top_flag = (lax.axis_index("layer") == layer_count - 1).astype(jnp.float32)
    top_layer = pad_gain * pad_map.astype(jnp.float32) * top_flag
    pad_term = jnp.concatenate(
        (jnp.zeros((local_layers - 1, grid_rows, grid_cols), jnp.float32), top_layer[None]), 0
    )
    diagonal = pad_term
    for weight in weights:
        diagonal = diagonal + weight
    inverse = 1.0 / diagonal

    col_count = lax.axis_size("col")
    tile_cols = grid_cols * col_count // TILE
    tile_rows = grid_rows * lax.axis_size("row") // TILE
    own_rows = grid_rows // TILE
    own_cols = grid_cols // TILE
    first_row = lax.axis_index("row") * own_rows
    first_col = lax.axis_index("col") * own_cols
    flat_tiles = port_tile.reshape(-1)
    local_ids = (
        (first_row + jnp.arange(own_rows, dtype=jnp.int32))[:, None] * tile_cols
        + (first_col + jnp.arange(own_cols, dtype=jnp.int32))[None, :]
    ).reshape(-1)
    gather_local = (flat_tiles[:, None] == local_ids[None, :]).astype(jnp.float32)
    ring_rows = first_row - 1 + jnp.arange(own_rows + 2, dtype=jnp.int32)
    ring_cols = first_col - 1 + jnp.arange(own_cols + 2, dtype=jnp.int32)
    ring_ok = ((ring_rows >= 0) & (ring_rows < tile_rows))[:, None] & ((ring_cols >= 0) & (ring_cols < tile_cols))[None, :]
    ring_ids = jnp.where(ring_ok, ring_rows[:, None] * tile_cols + ring_cols[None, :], -1).reshape(-1)
    scatter_ring = (ring_ids[:, None] == flat_tiles[None, :]).astype(jnp.float32)
    coarse = coarse_pair if col_count == 2 else coarse_general

    drop = None
    drop_near = None
    for outer in range(ITERS):
        if drop is None:
            resid = sources
        else:
            resid = sources - apply_grid(drop, drop_near, weights, pad_term)
        plane = jnp.sum(resid, axis=0)
        tiles = plane.reshape(own_rows, TILE, own_cols, TILE).sum(axis=(1, 3)).reshape(-1)
        local_rhs = jnp.dot(gather_local, tiles, precision=highest)
        rhs = all_sum(local_rhs).reshape(NPANEL, PANEL) * (restrict_scale / TILE)
        ports = coarse(rhs, pivots, coupling)
        tile_values = jnp.dot(scatter_ring, ports.reshape(-1), precision=highest).reshape(own_rows + 2, own_cols + 2)
        ring = expand(expand(tile_values, True).T, True).T * prolong_scale
        centre = ring[1:-1, 1:-1]
        lifted = jnp.broadcast_to(centre[None], (local_layers, grid_rows, grid_cols))
        total = smooth(resid, weights, pad_term, inverse)
        if outer == ITERS - 1:
            drop = (lifted if drop is None else drop + lifted) + total
            break
        lifted_near = [lifted, lifted]
        for part in (ring[2:, 1:-1], ring[:-2, 1:-1], ring[1:-1, 2:], ring[1:-1, :-2]):
            lifted_near.append(jnp.broadcast_to(part[None], (local_layers, grid_rows, grid_cols)))
        total_near = neighbours(total, exchange(total))
        if drop is None:
            drop = lifted + total
            drop_near = [a + b for a, b in zip(lifted_near, total_near)]
        else:
            drop = drop + lifted + total
            drop_near = [(d + a) + b for d, a, b in zip(drop_near, lifted_near, total_near)]
    return (drop, ports)


def solution(mesh):
    placed = (
        P("layer", "row", "col"),
        P("layer", "row", "col"),
        P("layer", "row", "col"),
        P("layer", "row", "col"),
        P("row", "col"),
        P(),
        P(None, "col", None),
        P(None, "col", None),
    )
    return jax.shard_map(
        shards,
        mesh=mesh,
        in_specs=placed,
        out_specs=(P("layer", "row", "col"), P()),
        check_vma=False,
    )
```

time: 360 us -> 237 us (0.66)
  blocking collectives: 148 us -> 0 us
  starting transfers between devices: 91.9 us -> 128 us
  local copies, waits for them, and re-layouts: 11.5 us -> 33.1 us
  waiting for transfers between devices: 51.9 us -> 37.7 us
  matrix products: 25.4 us -> 13 us
  other arithmetic: 26.6 us -> 21.6 us
    psum x10 -> x0, blocking collectives: 122 us -> none  [the longest x2 78.9 us: shards(): rhs = lax.psum(local_rhs, ('layer', 'row', 'col')) * (restrict_scale / TILE)]
    ppermute x42 -> x58, starting transfers between devices: 91.9 us -> 128 us  [the longest x18 77.4 us: rims(): below = lax.ppermute(tail, axis, [(i, i + 1) for i in range(count - 1)])]
    all_gather x6 -> x0, blocking collectives: 25.9 us -> none  [shards(): full = lax.all_gather(piece, 'col', axis=0, tiled=True)]
    slice x7 -> x57, local copies, waits for them, and re-layouts: 1.5 us -> 26.8 us  [the longest x12 5.16 us: neighbours(): lax.slice_in_dim(field, 1, size, axis=dim)]
    ppermute x42 -> x58, waiting for transfers between devices: 51.9 us -> 37.7 us  [the longest x12 21.9 us: swap_col(): return lax.ppermute(value, 'col', [(0, 1), (1, 0)])]
    dot_general x24, matrix products: 25.4 us -> 13 us  [the longest x8 4.05 us: coarse_pair(): jnp.dot(pivots[section], forward[section], precision=highest)]
    squeeze x6 -> x0, other arithmetic: 6.31 us -> none  [apply_grid(): grown = grow(field[None])[0]]
    mul x2 -> x9, other arithmetic: 0.01 us -> 5.99 us  [the longest x2 3.54 us: smooth(): change = inverse * resid / theta]
  transfers between devices with their start and end apart: 42 -> 58, of which waited for: 17 -> 23; matrix products, arithmetic and copies ran while one was open for 5% -> 18% of each run, Pallas kernels for 0% -> 0%
where the time goes in v1:
time: 237 us; the launch traced here: 235 us
  starting transfers between devices  128 us (54%)
  waiting for transfers between devices  37.7 us (16%)
  local copies, waits for them, and re-layouts  33.1 us (14%)
  other arithmetic  21.6 us (9%)
  matrix products  13 us (5%)
    ppermute x18, starting transfers between devices, rims(): below = lax.ppermute(tail, axis, [(i, i + 1) for i in range(count - 1)])  77.4 us
    ppermute x18, starting transfers between devices, rims(): above = lax.ppermute(head, axis, [(i + 1, i) for i in range(count - 1)])  23.6 us
    ppermute x12, waiting for transfers between devices, swap_col(): return lax.ppermute(value, 'col', [(0, 1), (1, 0)])  21.9 us
    ppermute x10, starting transfers between devices, all_sum(): lax.ppermute(value, axis, [(i, i ^ step) for i in range(count)])  15.3 us
    ppermute x10, waiting for transfers between devices, all_sum(): lax.ppermute(value, axis, [(i, i ^ step) for i in range(count)])  12.2 us
    ppermute x12, starting transfers between devices, swap_col(): return lax.ppermute(value, 'col', [(0, 1), (1, 0)])  11.6 us
    slice x12, local copies, waits for them, and re-layouts, neighbours(): lax.slice_in_dim(field, 1, size, axis=dim)  5.16 us
  transfers between devices with their start and end apart: 58, of which 23 were waited for; matrix products, arithmetic and copies ran while one was open for 18% of the time, Pallas kernels for 0%

profile of v1, /device:TPU:0, one launch (start us, length us, event | category | flops | bytes accessed | tf_op | source)
XLA Modules:
  0.0 235.2 jit_solution(6506734693585772166)
XLA Ops:
  3.3 3.0 %collective-permute-start.12 = (f32[1,64,512]{2,1,0:T(8,128)S(1)}, f32[1,64,512]{2,1,0:T(8,128)S(1)}, u32[]{:S(2)}, u32[]{:S(2)}) collective-permute-start(f32[1,64,512]{2,1,0:T(8,128)S(1)} %get-tuple-element.77), channel_id=1, source_target_pairs={{0,8},{8,16},{16,24},{1,9},{9,17},{17,25},{2,10},{10,18},{18,26},{... | collective-permute-start | bytes 393224 | tf_op jit(solution)/shard_map/ppermute | solution.py:28
  8.6 4.9 %collective-permute-start.16 = (f32[2,64,1]{2,1,0:T(8,128)S(1)}, f32[2,64,1]{2,1,0:T(8,128)S(1)}, u32[]{:S(2)}, u32[]{:S(2)}) collective-permute-start(f32[2,64,1]{2,1,0:T(8,128)S(1)} %get-tuple-element.69), channel_id=1, source_target_pairs={{0,1},{2,3},{4,5},{6,7},{8,9},{10,11},{12,13},{14,15},{16,17},{18,... | collective-permute-start | bytes 1544 | tf_op jit(solution)/shard_map/ppermute | solution.py:28
  17.4 5.2 %collective-permute-start.14 = (f32[2,1,512]{2,1,0:T(1,128)S(1)}, f32[2,1,512]{2,1,0:T(1,128)S(1)}, u32[]{:S(2)}, u32[]{:S(2)}) collective-permute-start(f32[2,1,512]{2,1,0:T(1,128)S(1)} %get-tuple-element.73), channel_id=1, source_target_pairs={{0,2},{2,4},{4,6},{1,3},{3,5},{5,7},{8,10},{10,12},{12,14},{9,11},... | collective-permute-start | bytes 12296 | tf_op jit(solution)/shard_map/ppermute | solution.py:28
  24.7 2.4 %fusion.179 = (f32[2,64,512]{2,1,0:T(8,128)S(1)}, f32[2,64,512]{2,1,0:T(8,128)S(1)}, f32[2,64,512]{2,1,0:T(8,128)S(1)}, f32[2,64,512]{2,1,0:T(8,128)S(1)}, f32[2...) fusion(f32[2,64,512]{2,1,0:T(8,128)S(1)} %copy-done.4, ...), kind=kLoop, calls=%fused_computation.273 | loop fusion | flops 1343488 | bytes 4456448 | tf_op jit(solution)/shard_map/mul | solution.py:58
  39.0 3.5 %collective-permute-start.3 = (f32[2048]{0:T(1024)S(1)}, f32[2048]{0:T(1024)S(1)}, u32[]{:S(2)}, u32[]{:S(2)}) collective-permute-start(f32[2048]{0:T(1024)S(1)} %add.331), channel_id=1, source_target_pairs={{0,4},{2,6},{4,0},{6,2},{1,5},{3,7},{5,1},{7,3},{8,12},{10,14},{12... | collective-permute-start | bytes 24584 | tf_op jit(solution)/shard_map/ppermute | solution.py:77
  44.8 2.9 %collective-permute-done.4 = f32[2048]{0:T(1024)S(1)} collective-permute-done((f32[2048]{0:T(1024)S(1)}, f32[2048]{0:T(1024)S(1)}, u32[]{:S(2)}, u32[]{:S(2)}) %collective-permute-start.4) | collective-permute-done | bytes 8224 | tf_op jit(solution)/shard_map/ppermute | solution.py:77
  50.2 3.7 %collective-permute-start.18 = (f32[1,64,512]{2,1,0:T(8,128)}, f32[1,64,512]{2,1,0:T(8,128)}, u32[]{:S(2)}, u32[]{:S(2)}) collective-permute-start(f32[1,64,512]{2,1,0:T(8,128)} %get-tuple-element.59), channel_id=1, source_target_pairs={{0,8},{8,16},{16,24},{1,9},{9,17},{17,25},{2,10},{10,18},{18,26},{... | collective-permute-start | bytes 393224 | tf_op jit(solution)/shard_map/ppermute | solution.py:28
  57.2 3.3 %collective-permute-start.6 = (f32[256]{0:T(256)S(1)}, f32[256]{0:T(256)S(1)}, u32[]{:S(2)}, u32[]{:S(2)}) collective-permute-start(f32[256]{0:T(256)S(1)} %dynamic-slice_subtract_fusion.4), channel_id=1, source_target_pairs={{0,1},{1,0},{2,3},{3,2},{4,5},{5,4},{6,7},{7,6},{8,9},{9,8},{10,11... | collective-permute-start | bytes 3080 | tf_op jit(solution)/shard_map/ppermute | solution.py:83
  79.0 5.1 %collective-permute-start.20 = (f32[2,1,512]{2,1,0:T(1,128)}, f32[2,1,512]{2,1,0:T(1,128)}, u32[]{:S(2)}, u32[]{:S(2)}) collective-permute-start(f32[2,1,512]{2,1,0:T(1,128)} %get-tuple-element.64), channel_id=1, source_target_pairs={{0,2},{2,4},{4,6},{1,3},{3,5},{5,7},{8,10},{10,12},{12,14},{9,11},... | collective-permute-start | bytes 12296 | tf_op jit(solution)/shard_map/ppermute | solution.py:28
  92.4 4.5 %collective-permute-start.22 = (f32[2,64,1]{2,1,0:T(8,128)}, f32[2,64,1]{2,1,0:T(8,128)}, u32[]{:S(2)}, u32[]{:S(2)}) collective-permute-start(f32[2,64,1]{2,1,0:T(8,128)} %get-tuple-element.68), channel_id=1, source_target_pairs={{0,1},{2,3},{4,5},{6,7},{8,9},{10,11},{12,13},{14,15},{16,17},{18,... | collective-permute-start | bytes 1544 | tf_op jit(solution)/shard_map/ppermute | solution.py:28
  110.4 3.0 %collective-permute-start.24 = (f32[1,64,512]{2,1,0:T(8,128)S(1)}, f32[1,64,512]{2,1,0:T(8,128)S(1)}, u32[]{:S(2)}, u32[]{:S(2)}) collective-permute-start(f32[1,64,512]{2,1,0:T(8,128)S(1)} %get-tuple-element.57), channel_id=1, source_target_pairs={{0,8},{8,16},{16,24},{1,9},{9,17},{17,25},{2,10},{10,18},{18,26},{... | collective-permute-start | bytes 393224 | tf_op jit(solution)/shard_map/ppermute | solution.py:28
  113.5 4.5 %collective-permute-start.28 = (f32[2,64,1]{2,1,0:T(8,128)S(1)}, f32[2,64,1]{2,1,0:T(8,128)S(1)}, u32[]{:S(2)}, u32[]{:S(2)}) collective-permute-start(f32[2,64,1]{2,1,0:T(8,128)S(1)} %get-tuple-element.49), channel_id=1, source_target_pairs={{0,1},{2,3},{4,5},{6,7},{8,9},{10,11},{12,13},{14,15},{16,17},{18,... | collective-permute-start | bytes 1544 | tf_op jit(solution)/shard_map/ppermute | solution.py:28
  119.3 4.5 %collective-permute-start.26 = (f32[2,1,512]{2,1,0:T(1,128)S(1)}, f32[2,1,512]{2,1,0:T(1,128)S(1)}, u32[]{:S(2)}, u32[]{:S(2)}) collective-permute-start(f32[2,1,512]{2,1,0:T(1,128)S(1)} %get-tuple-element.53), channel_id=1, source_target_pairs={{0,2},{2,4},{4,6},{1,3},{3,5},{5,7},{8,10},{10,12},{12,14},{9,11},... | collective-permute-start | bytes 12296 | tf_op jit(solution)/shard_map/ppermute | solution.py:28
  128.7 3.0 %collective-permute-start.30 = (f32[1,64,512]{2,1,0:T(8,128)S(1)}, f32[1,64,512]{2,1,0:T(8,128)S(1)}, u32[]{:S(2)}, u32[]{:S(2)}) collective-permute-start(f32[1,64,512]{2,1,0:T(8,128)S(1)} %get-tuple-element.38), channel_id=1, source_target_pairs={{0,8},{8,16},{16,24},{1,9},{9,17},{17,25},{2,10},{10,18},{18,26},{... | collective-permute-start | bytes 393224 | tf_op jit(solution)/shard_map/ppermute | solution.py:28
  131.8 4.5 %collective-permute-start.34 = (f32[2,64,1]{2,1,0:T(8,128)S(1)}, f32[2,64,1]{2,1,0:T(8,128)S(1)}, u32[]{:S(2)}, u32[]{:S(2)}) collective-permute-start(f32[2,64,1]{2,1,0:T(8,128)S(1)} %get-tuple-element.47), channel_id=1, source_target_pairs={{0,1},{2,3},{4,5},{6,7},{8,9},{10,11},{12,13},{14,15},{16,17},{18,... | collective-permute-start | bytes 1544 | tf_op jit(solution)/shard_map/ppermute | solution.py:28
  137.6 5.0 %collective-permute-start.32 = (f32[2,1,512]{2,1,0:T(1,128)S(1)}, f32[2,1,512]{2,1,0:T(1,128)S(1)}, u32[]{:S(2)}, u32[]{:S(2)}) collective-permute-start(f32[2,1,512]{2,1,0:T(1,128)S(1)} %get-tuple-element.43), channel_id=1, source_target_pairs={{0,2},{2,4},{4,6},{1,3},{3,5},{5,7},{8,10},{10,12},{12,14},{9,11},... | collective-permute-start | bytes 12296 | tf_op jit(solution)/shard_map/ppermute | solution.py:28
  145.8 2.3 reshape.510
  156.2 2.3 collective-permute-start.37
  160.2 3.5 %collective-permute-start.38 = (f32[2048]{0:T(1024)S(1)}, f32[2048]{0:T(1024)S(1)}, u32[]{:S(2)}, u32[]{:S(2)}) collective-permute-start(f32[2048]{0:T(1024)S(1)} %add.376), channel_id=1, source_target_pairs={{0,4},{2,6},{4,0},{6,2},{1,5},{3,7},{5,1},{7,3},{8,12},{10,14},{12... | collective-permute-start | bytes 24584 | tf_op jit(solution)/shard_map/ppermute | solution.py:77
  166.0 2.9 %collective-permute-done.39 = f32[2048]{0:T(1024)S(1)} collective-permute-done((f32[2048]{0:T(1024)S(1)}, f32[2048]{0:T(1024)S(1)}, u32[]{:S(2)}, u32[]{:S(2)}) %collective-permute-start.39) | collective-permute-done | bytes 8224 | tf_op jit(solution)/shard_map/ppermute | solution.py:77
  170.3 2.9 %collective-permute-done.40 = f32[256]{0:T(256)S(1)} collective-permute-done((f32[256]{0:T(256)S(1)}, f32[256]{0:T(256)S(1)}, u32[]{:S(2)}, u32[]{:S(2)}) %collective-permute-start.40) | collective-permute-done | bytes 1056 | tf_op jit(solution)/shard_map/ppermute | solution.py:83
  175.6 3.7 %collective-permute-start.47 = (f32[1,64,512]{2,1,0:T(8,128)}, f32[1,64,512]{2,1,0:T(8,128)}, u32[]{:S(2)}, u32[]{:S(2)}) collective-permute-start(f32[1,64,512]{2,1,0:T(8,128)} %get-tuple-element.28), channel_id=1, source_target_pairs={{0,8},{8,16},{16,24},{1,9},{9,17},{17,25},{2,10},{10,18},{18,26},{... | collective-permute-start | bytes 393224 | tf_op jit(solution)/shard_map/ppermute | solution.py:28
  180.6 5.8 %collective-permute-start.51 = (f32[2,64,1]{2,1,0:T(8,128)}, f32[2,64,1]{2,1,0:T(8,128)}, u32[]{:S(2)}, u32[]{:S(2)}) collective-permute-start(f32[2,64,1]{2,1,0:T(8,128)} %get-tuple-element.37), channel_id=1, source_target_pairs={{0,1},{2,3},{4,5},{6,7},{8,9},{10,11},{12,13},{14,15},{16,17},{18,... | collective-permute-start | bytes 1544 | tf_op jit(solution)/shard_map/ppermute | solution.py:28
  187.5 3.0 %collective-permute-done.42 = f32[256]{0:T(256)S(1)} collective-permute-done((f32[256]{0:T(256)S(1)}, f32[256]{0:T(256)S(1)}, u32[]{:S(2)}, u32[]{:S(2)}) %collective-permute-start.42) | collective-permute-done | bytes 1056 | tf_op jit(solution)/shard_map/ppermute | solution.py:83
  192.1 3.1 %collective-permute-done.43 = f32[512]{0:T(512)S(1)} collective-permute-done((f32[512]{0:T(512)S(1)}, f32[512]{0:T(512)S(1)}, u32[]{:S(2)}, u32[]{:S(2)}) %collective-permute-start.43) | collective-permute-done | bytes 2080 | tf_op jit(solution)/shard_map/ppermute | solution.py:83
  196.2 3.1 %collective-permute-done.44 = f32[512]{0:T(512)S(1)} collective-permute-done((f32[512]{0:T(512)S(1)}, f32[512]{0:T(512)S(1)}, u32[]{:S(2)}, u32[]{:S(2)}) %collective-permute-start.44) | collective-permute-done | bytes 2080 | tf_op jit(solution)/shard_map/ppermute | solution.py:83
  199.8 3.6 %collective-permute-done.45 = f32[1024]{0:T(1024)S(1)} collective-permute-done((f32[1024]{0:T(1024)S(1)}, f32[1024]{0:T(1024)S(1)}, u32[]{:S(2)}, u32[]{:S(2)}) %collective-permute-start.45) | collective-permute-done | bytes 4128 | tf_op jit(solution)/shard_map/ppermute | solution.py:83
  206.4 4.5 %collective-permute-start.49 = (f32[2,1,512]{2,1,0:T(1,128)S(1)}, f32[2,1,512]{2,1,0:T(1,128)S(1)}, u32[]{:S(2)}, u32[]{:S(2)}) collective-permute-start(f32[2,1,512]{2,1,0:T(1,128)S(1)} %get-tuple-element.33), channel_id=1, source_target_pairs={{0,2},{2,4},{4,6},{1,3},{3,5},{5,7},{8,10},{10,12},{12,14},{9,11},... | collective-permute-start | bytes 12296 | tf_op jit(solution)/shard_map/ppermute | solution.py:28
  217.5 3.0 %collective-permute-start.53 = (f32[1,64,512]{2,1,0:T(8,128)S(1)}, f32[1,64,512]{2,1,0:T(8,128)S(1)}, u32[]{:S(2)}, u32[]{:S(2)}) collective-permute-start(f32[1,64,512]{2,1,0:T(8,128)S(1)} %get-tuple-element.26), channel_id=1, source_target_pairs={{0,8},{8,16},{16,24},{1,9},{9,17},{17,25},{2,10},{10,18},{18,26},{... | collective-permute-start | bytes 393224 | tf_op jit(solution)/shard_map/ppermute | solution.py:28
  220.5 4.5 %collective-permute-start.57 = (f32[2,64,1]{2,1,0:T(8,128)S(1)}, f32[2,64,1]{2,1,0:T(8,128)S(1)}, u32[]{:S(2)}, u32[]{:S(2)}) collective-permute-start(f32[2,64,1]{2,1,0:T(8,128)S(1)} %get-tuple-element.18), channel_id=1, source_target_pairs={{0,1},{2,3},{4,5},{6,7},{8,9},{10,11},{12,13},{14,15},{16,17},{18,... | collective-permute-start | bytes 1544 | tf_op jit(solution)/shard_map/ppermute | solution.py:28
  226.4 4.6 %collective-permute-start.55 = (f32[2,1,512]{2,1,0:T(1,128)S(1)}, f32[2,1,512]{2,1,0:T(1,128)S(1)}, u32[]{:S(2)}, u32[]{:S(2)}) collective-permute-start(f32[2,1,512]{2,1,0:T(1,128)S(1)} %get-tuple-element.22), channel_id=1, source_target_pairs={{0,2},{2,4},{4,6},{1,3},{3,5},{5,7},{8,10},{10,12},{12,14},{9,11},... | collective-permute-start | bytes 12296 | tf_op jit(solution)/shard_map/ppermute | solution.py:28
  232.4 2.8 %fusion.129 = f32[2,64,512]{2,1,0:T(8,128)} fusion(f32[2,64,512]{2,1,0:T(8,128)S(1)} %copy-done.6, f32[1,64,512]{2,1,0:T(8,128)S(1)} %multiply_bitcast_fusion, f32[2,64,512]{2,1,0:T(8,128)S(1)} %get-tuple-element.12, f32[1,64,512]{2,1,0:T(8,128)S(1)} %collective-permute-done.52, f32[1,64,512]{2,1,0:T(8,128)S(1)} %get-tuple-element.26, ...), kind=kLoop, calls=%fused_computation.137 | loop fusion | flops 4784128 | bytes 5898240 | tf_op jit(solution)/shard_map/add | solution.py:215
  (314 shorter events, 114.6 us)
Async XLA Ops:
  1.8 22.1 %collective-permute-start.11 = (f32[1,64,512]{2,1,0:T(8,128)S(1)}, f32[1,64,512]{2,1,0:T(8,128)S(1)}, u32[]{:S(2)}, u32[]{:S(2)}) collective-permute-start(f32[1,64,512]{2,1,0:T(8,128)S(1)} %get-tuple-element.78), channel_id=1, source_target_pairs={{8,0},{16,8},{24,16},{9,1},{17,9},{25,17},{10,2},{18,10},{26,18},{... | collective-permute-start | bytes 393224 | tf_op jit(solution)/shard_map/ppermute | solution.py:29
  3.3 20.7 %collective-permute-start.12 = (f32[1,64,512]{2,1,0:T(8,128)S(1)}, f32[1,64,512]{2,1,0:T(8,128)S(1)}, u32[]{:S(2)}, u32[]{:S(2)}) collective-permute-start(f32[1,64,512]{2,1,0:T(8,128)S(1)} %get-tuple-element.77), channel_id=1, source_target_pairs={{0,8},{8,16},{16,24},{1,9},{9,17},{17,25},{2,10},{10,18},{18,26},{... | collective-permute-start | bytes 393224 | tf_op jit(solution)/shard_map/ppermute | solution.py:28
  7.3 10.1 %collective-permute-start.15 = (f32[2,64,1]{2,1,0:T(8,128)S(1)}, f32[2,64,1]{2,1,0:T(8,128)S(1)}, u32[]{:S(2)}, u32[]{:S(2)}) collective-permute-start(f32[2,64,1]{2,1,0:T(8,128)S(1)} %get-tuple-element.70), channel_id=1, source_target_pairs={{1,0},{3,2},{5,4},{7,6},{9,8},{11,10},{13,12},{15,14},{17,16},{19,... | collective-permute-start | bytes 1544 | tf_op jit(solution)/shard_map/ppermute | solution.py:29
  8.6 15.3 %collective-permute-start.16 = (f32[2,64,1]{2,1,0:T(8,128)S(1)}, f32[2,64,1]{2,1,0:T(8,128)S(1)}, u32[]{:S(2)}, u32[]{:S(2)}) collective-permute-start(f32[2,64,1]{2,1,0:T(8,128)S(1)} %get-tuple-element.69), channel_id=1, source_target_pairs={{0,1},{2,3},{4,5},{6,7},{8,9},{10,11},{12,13},{14,15},{16,17},{18,... | collective-permute-start | bytes 1544 | tf_op jit(solution)/shard_map/ppermute | solution.py:28
  13.5 10.4 %collective-permute-start.13 = (f32[2,1,512]{2,1,0:T(1,128)S(1)}, f32[2,1,512]{2,1,0:T(1,128)S(1)}, u32[]{:S(2)}, u32[]{:S(2)}) collective-permute-start(f32[2,1,512]{2,1,0:T(1,128)S(1)} %get-tuple-element.74), channel_id=1, source_target_pairs={{2,0},{4,2},{6,4},{3,1},{5,3},{7,5},{10,8},{12,10},{14,12},{11,9},... | collective-permute-start | bytes 12296 | tf_op jit(solution)/shard_map/ppermute | solution.py:29
  17.4 6.5 %collective-permute-start.14 = (f32[2,1,512]{2,1,0:T(1,128)S(1)}, f32[2,1,512]{2,1,0:T(1,128)S(1)}, u32[]{:S(2)}, u32[]{:S(2)}) collective-permute-start(f32[2,1,512]{2,1,0:T(1,128)S(1)} %get-tuple-element.73), channel_id=1, source_target_pairs={{0,2},{2,4},{4,6},{1,3},{3,5},{5,7},{8,10},{10,12},{12,14},{9,11},... | collective-permute-start | bytes 12296 | tf_op jit(solution)/shard_map/ppermute | solution.py:28
  48.3 8.2 %collective-permute-start.5 = (f32[256]{0:T(256)S(1)}, f32[256]{0:T(256)S(1)}, u32[]{:S(2)}, u32[]{:S(2)}) collective-permute-start(f32[256]{0:T(256)S(1)} %dynamic-slice_subtract_fusion.5), channel_id=1, source_target_pairs={{0,1},{1,0},{2,3},{3,2},{4,5},{5,4},{6,7},{7,6},{8,9},{9,8},{10,11... | collective-permute-start | bytes 3080 | tf_op jit(solution)/shard_map/ppermute | solution.py:83
  49.0 56.7 %collective-permute-start.17 = (f32[1,64,512]{2,1,0:T(8,128)}, f32[1,64,512]{2,1,0:T(8,128)}, u32[]{:S(2)}, u32[]{:S(2)}) collective-permute-start(f32[1,64,512]{2,1,0:T(8,128)} %get-tuple-element.60), channel_id=1, source_target_pairs={{8,0},{16,8},{24,16},{9,1},{17,9},{25,17},{10,2},{18,10},{26,18},{... | collective-permute-start | bytes 393224 | tf_op jit(solution)/shard_map/ppermute | solution.py:29
  50.2 55.4 %collective-permute-start.18 = (f32[1,64,512]{2,1,0:T(8,128)}, f32[1,64,512]{2,1,0:T(8,128)}, u32[]{:S(2)}, u32[]{:S(2)}) collective-permute-start(f32[1,64,512]{2,1,0:T(8,128)} %get-tuple-element.59), channel_id=1, source_target_pairs={{0,8},{8,16},{16,24},{1,9},{9,17},{17,25},{2,10},{10,18},{18,26},{... | collective-permute-start | bytes 393224 | tf_op jit(solution)/shard_map/ppermute | solution.py:28
  53.9 38.5 %collective-permute-start.21 = (f32[2,64,1]{2,1,0:T(8,128)}, f32[2,64,1]{2,1,0:T(8,128)}, u32[]{:S(2)}, u32[]{:S(2)}) collective-permute-start(f32[2,64,1]{2,1,0:T(8,128)} %get-tuple-element.67), channel_id=1, source_target_pairs={{1,0},{3,2},{5,4},{7,6},{9,8},{11,10},{13,12},{15,14},{17,16},{19,... | collective-permute-start | bytes 1544 | tf_op jit(solution)/shard_map/ppermute | solution.py:29
  55.2 50.4 %collective-permute-start.19 = (f32[2,1,512]{2,1,0:T(1,128)}, f32[2,1,512]{2,1,0:T(1,128)}, u32[]{:S(2)}, u32[]{:S(2)}) collective-permute-start(f32[2,1,512]{2,1,0:T(1,128)} %get-tuple-element.63), channel_id=1, source_target_pairs={{2,0},{4,2},{6,4},{3,1},{5,3},{7,5},{10,8},{12,10},{14,12},{11,9},... | collective-permute-start | bytes 12296 | tf_op jit(solution)/shard_map/ppermute | solution.py:29
  79.0 26.6 %collective-permute-start.20 = (f32[2,1,512]{2,1,0:T(1,128)}, f32[2,1,512]{2,1,0:T(1,128)}, u32[]{:S(2)}, u32[]{:S(2)}) collective-permute-start(f32[2,1,512]{2,1,0:T(1,128)} %get-tuple-element.64), channel_id=1, source_target_pairs={{0,2},{2,4},{4,6},{1,3},{3,5},{5,7},{8,10},{10,12},{12,14},{9,11},... | collective-permute-start | bytes 12296 | tf_op jit(solution)/shard_map/ppermute | solution.py:28
  92.4 13.2 %collective-permute-start.22 = (f32[2,64,1]{2,1,0:T(8,128)}, f32[2,64,1]{2,1,0:T(8,128)}, u32[]{:S(2)}, u32[]{:S(2)}) collective-permute-start(f32[2,64,1]{2,1,0:T(8,128)} %get-tuple-element.68), channel_id=1, source_target_pairs={{0,1},{2,3},{4,5},{6,7},{8,9},{10,11},{12,13},{14,15},{16,17},{18,... | collective-permute-start | bytes 1544 | tf_op jit(solution)/shard_map/ppermute | solution.py:28
  107.8 11.5 %collective-permute-start.27 = (f32[2,64,1]{2,1,0:T(8,128)S(1)}, f32[2,64,1]{2,1,0:T(8,128)S(1)}, u32[]{:S(2)}, u32[]{:S(2)}) collective-permute-start(f32[2,64,1]{2,1,0:T(8,128)S(1)} %get-tuple-element.50), channel_id=1, source_target_pairs={{1,0},{3,2},{5,4},{7,6},{9,8},{11,10},{13,12},{15,14},{17,16},{19,... | collective-permute-start | bytes 1544 | tf_op jit(solution)/shard_map/ppermute | solution.py:29
  109.1 16.1 %collective-permute-start.23 = (f32[1,64,512]{2,1,0:T(8,128)S(1)}, f32[1,64,512]{2,1,0:T(8,128)S(1)}, u32[]{:S(2)}, u32[]{:S(2)}) collective-permute-start(f32[1,64,512]{2,1,0:T(8,128)S(1)} %get-tuple-element.58), channel_id=1, source_target_pairs={{8,0},{16,8},{24,16},{9,1},{17,9},{25,17},{10,2},{18,10},{26,18},{... | collective-permute-start | bytes 393224 | tf_op jit(solution)/shard_map/ppermute | solution.py:29
  110.4 14.8 %collective-permute-start.24 = (f32[1,64,512]{2,1,0:T(8,128)S(1)}, f32[1,64,512]{2,1,0:T(8,128)S(1)}, u32[]{:S(2)}, u32[]{:S(2)}) collective-permute-start(f32[1,64,512]{2,1,0:T(8,128)S(1)} %get-tuple-element.57), channel_id=1, source_target_pairs={{0,8},{8,16},{16,24},{1,9},{9,17},{17,25},{2,10},{10,18},{18,26},{... | collective-permute-start | bytes 393224 | tf_op jit(solution)/shard_map/ppermute | solution.py:28
  113.5 10.5 %collective-permute-start.28 = (f32[2,64,1]{2,1,0:T(8,128)S(1)}, f32[2,64,1]{2,1,0:T(8,128)S(1)}, u32[]{:S(2)}, u32[]{:S(2)}) collective-permute-start(f32[2,64,1]{2,1,0:T(8,128)S(1)} %get-tuple-element.49), channel_id=1, source_target_pairs={{0,1},{2,3},{4,5},{6,7},{8,9},{10,11},{12,13},{14,15},{16,17},{18,... | collective-permute-start | bytes 1544 | tf_op jit(solution)/shard_map/ppermute | solution.py:28
  126.0 11.6 %collective-permute-start.33 = (f32[2,64,1]{2,1,0:T(8,128)S(1)}, f32[2,64,1]{2,1,0:T(8,128)S(1)}, u32[]{:S(2)}, u32[]{:S(2)}) collective-permute-start(f32[2,64,1]{2,1,0:T(8,128)S(1)} %get-tuple-element.46), channel_id=1, source_target_pairs={{1,0},{3,2},{5,4},{7,6},{9,8},{11,10},{13,12},{15,14},{17,16},{19,... | collective-permute-start | bytes 1544 | tf_op jit(solution)/shard_map/ppermute | solution.py:29
  127.4 16.3 %collective-permute-start.29 = (f32[1,64,512]{2,1,0:T(8,128)S(1)}, f32[1,64,512]{2,1,0:T(8,128)S(1)}, u32[]{:S(2)}, u32[]{:S(2)}) collective-permute-start(f32[1,64,512]{2,1,0:T(8,128)S(1)} %get-tuple-element.39), channel_id=1, source_target_pairs={{8,0},{16,8},{24,16},{9,1},{17,9},{25,17},{10,2},{18,10},{26,18},{... | collective-permute-start | bytes 393224 | tf_op jit(solution)/shard_map/ppermute | solution.py:29
  128.7 15.0 %collective-permute-start.30 = (f32[1,64,512]{2,1,0:T(8,128)S(1)}, f32[1,64,512]{2,1,0:T(8,128)S(1)}, u32[]{:S(2)}, u32[]{:S(2)}) collective-permute-start(f32[1,64,512]{2,1,0:T(8,128)S(1)} %get-tuple-element.38), channel_id=1, source_target_pairs={{0,8},{8,16},{16,24},{1,9},{9,17},{17,25},{2,10},{10,18},{18,26},{... | collective-permute-start | bytes 393224 | tf_op jit(solution)/shard_map/ppermute | solution.py:28
  131.8 11.0 %collective-permute-start.34 = (f32[2,64,1]{2,1,0:T(8,128)S(1)}, f32[2,64,1]{2,1,0:T(8,128)S(1)}, u32[]{:S(2)}, u32[]{:S(2)}) collective-permute-start(f32[2,64,1]{2,1,0:T(8,128)S(1)} %get-tuple-element.47), channel_id=1, source_target_pairs={{0,1},{2,3},{4,5},{6,7},{8,9},{10,11},{12,13},{14,15},{16,17},{18,... | collective-permute-start | bytes 1544 | tf_op jit(solution)/shard_map/ppermute | solution.py:28
  136.3 6.5 %collective-permute-start.31 = (f32[2,1,512]{2,1,0:T(1,128)S(1)}, f32[2,1,512]{2,1,0:T(1,128)S(1)}, u32[]{:S(2)}, u32[]{:S(2)}) collective-permute-start(f32[2,1,512]{2,1,0:T(1,128)S(1)} %get-tuple-element.42), channel_id=1, source_target_pairs={{2,0},{4,2},{6,4},{3,1},{5,3},{7,5},{10,8},{12,10},{14,12},{11,9},... | collective-permute-start | bytes 12296 | tf_op jit(solution)/shard_map/ppermute | solution.py:29
  173.7 12.7 %collective-permute-start.41 = (f32[256]{0:T(256)S(1)}, f32[256]{0:T(256)S(1)}, u32[]{:S(2)}, u32[]{:S(2)}) collective-permute-start(f32[256]{0:T(256)S(1)} %dynamic-slice_subtract_fusion.1), channel_id=1, source_target_pairs={{0,1},{1,0},{2,3},{3,2},{4,5},{5,4},{6,7},{7,6},{8,9},{9,8},{10,11... | collective-permute-start | bytes 3080 | tf_op jit(solution)/shard_map/ppermute | solution.py:83
  174.3 38.1 %collective-permute-start.46 = (f32[1,64,512]{2,1,0:T(8,128)}, f32[1,64,512]{2,1,0:T(8,128)}, u32[]{:S(2)}, u32[]{:S(2)}) collective-permute-start(f32[1,64,512]{2,1,0:T(8,128)} %get-tuple-element.29), channel_id=1, source_target_pairs={{8,0},{16,8},{24,16},{9,1},{17,9},{25,17},{10,2},{18,10},{26,18},{... | collective-permute-start | bytes 393224 | tf_op jit(solution)/shard_map/ppermute | solution.py:29
  175.6 36.9 %collective-permute-start.47 = (f32[1,64,512]{2,1,0:T(8,128)}, f32[1,64,512]{2,1,0:T(8,128)}, u32[]{:S(2)}, u32[]{:S(2)}) collective-permute-start(f32[1,64,512]{2,1,0:T(8,128)} %get-tuple-element.28), channel_id=1, source_target_pairs={{0,8},{8,16},{16,24},{1,9},{9,17},{17,25},{2,10},{10,18},{18,26},{... | collective-permute-start | bytes 393224 | tf_op jit(solution)/shard_map/ppermute | solution.py:28
  179.3 27.1 %collective-permute-start.50 = (f32[2,64,1]{2,1,0:T(8,128)}, f32[2,64,1]{2,1,0:T(8,128)}, u32[]{:S(2)}, u32[]{:S(2)}) collective-permute-start(f32[2,64,1]{2,1,0:T(8,128)} %get-tuple-element.36), channel_id=1, source_target_pairs={{1,0},{3,2},{5,4},{7,6},{9,8},{11,10},{13,12},{15,14},{17,16},{19,... | collective-permute-start | bytes 1544 | tf_op jit(solution)/shard_map/ppermute | solution.py:29
  180.6 31.9 %collective-permute-start.51 = (f32[2,64,1]{2,1,0:T(8,128)}, f32[2,64,1]{2,1,0:T(8,128)}, u32[]{:S(2)}, u32[]{:S(2)}) collective-permute-start(f32[2,64,1]{2,1,0:T(8,128)} %get-tuple-element.37), channel_id=1, source_target_pairs={{0,1},{2,3},{4,5},{6,7},{8,9},{10,11},{12,13},{14,15},{16,17},{18,... | collective-permute-start | bytes 1544 | tf_op jit(solution)/shard_map/ppermute | solution.py:28
  203.4 9.1 %collective-permute-start.48 = (f32[2,1,512]{2,1,0:T(1,128)}, f32[2,1,512]{2,1,0:T(1,128)S(1)}, u32[]{:S(2)}, u32[]{:S(2)}) collective-permute-start(f32[2,1,512]{2,1,0:T(1,128)} %get-tuple-element.32), channel_id=1, source_target_pairs={{2,0},{4,2},{6,4},{3,1},{5,3},{7,5},{10,8},{12,10},{14,12},{11,9},... | collective-permute-start | bytes 12296 | tf_op jit(solution)/shard_map/ppermute | solution.py:29
  214.7 11.6 %collective-permute-start.56 = (f32[2,64,1]{2,1,0:T(8,128)S(1)}, f32[2,64,1]{2,1,0:T(8,128)S(1)}, u32[]{:S(2)}, u32[]{:S(2)}) collective-permute-start(f32[2,64,1]{2,1,0:T(8,128)S(1)} %get-tuple-element.19), channel_id=1, source_target_pairs={{1,0},{3,2},{5,4},{7,6},{9,8},{11,10},{13,12},{15,14},{17,16},{19,... | collective-permute-start | bytes 1544 | tf_op jit(solution)/shard_map/ppermute | solution.py:29
  216.2 16.1 %collective-permute-start.52 = (f32[1,64,512]{2,1,0:T(8,128)S(1)}, f32[1,64,512]{2,1,0:T(8,128)S(1)}, u32[]{:S(2)}, u32[]{:S(2)}) collective-permute-start(f32[1,64,512]{2,1,0:T(8,128)S(1)} %get-tuple-element.27), channel_id=1, source_target_pairs={{8,0},{16,8},{24,16},{9,1},{17,9},{25,17},{10,2},{18,10},{26,18},{... | collective-permute-start | bytes 393224 | tf_op jit(solution)/shard_map/ppermute | solution.py:29
  217.5 14.8 %collective-permute-start.53 = (f32[1,64,512]{2,1,0:T(8,128)S(1)}, f32[1,64,512]{2,1,0:T(8,128)S(1)}, u32[]{:S(2)}, u32[]{:S(2)}) collective-permute-start(f32[1,64,512]{2,1,0:T(8,128)S(1)} %get-tuple-element.26), channel_id=1, source_target_pairs={{0,8},{8,16},{16,24},{1,9},{9,17},{17,25},{2,10},{10,18},{18,26},{... | collective-permute-start | bytes 393224 | tf_op jit(solution)/shard_map/ppermute | solution.py:28
  220.5 10.5 %collective-permute-start.57 = (f32[2,64,1]{2,1,0:T(8,128)S(1)}, f32[2,64,1]{2,1,0:T(8,128)S(1)}, u32[]{:S(2)}, u32[]{:S(2)}) collective-permute-start(f32[2,64,1]{2,1,0:T(8,128)S(1)} %get-tuple-element.18), channel_id=1, source_target_pairs={{0,1},{2,3},{4,5},{6,7},{8,9},{10,11},{12,13},{14,15},{16,17},{18,... | collective-permute-start | bytes 1544 | tf_op jit(solution)/shard_map/ppermute | solution.py:28
  (59 other events, 642.6 us)

commit v2 on v1

--- a/solution.py
+++ b/solution.py
@@ -18,15 +18,35 @@
 
 highest = lax.Precision.HIGHEST
 GRID_AXES = (("layer", 0), ("row", 1), ("col", 2))
+ROW_AXES = ("layer", "row")
+
+
+def axis_count(axis):
+    names = axis if isinstance(axis, tuple) else (axis,)
+    count = 1
+    for name in names:
+        count *= lax.axis_size(name)
+    return count
 
 
 def rims(field, axis, dim):
-    count = lax.axis_size(axis)
     size = field.shape[dim]
     head = lax.slice_in_dim(field, 0, 1, axis=dim)
     tail = lax.slice_in_dim(field, size - 1, size, axis=dim)
-    below = lax.ppermute(tail, axis, [(i, i + 1) for i in range(count - 1)])
-    above = lax.ppermute(head, axis, [(i + 1, i) for i in range(count - 1)])
+    if axis is None:
+        return jnp.zeros_like(head), jnp.zeros_like(tail)
+    count = axis_count(axis)
+    place = list(range(count))
+    if axis == ROW_AXES:
+        layers, rows = lax.axis_size("layer"), lax.axis_size("row")
+        place = [(b % layers) * rows + b // layers for b in range(count)]
+    if count == 2:
+        low = lax.axis_index(axis) == 0
+        got = lax.ppermute(jnp.where(low, tail, head), axis, [(0, 1), (1, 0)])
+        zero = jnp.zeros_like(got)
+        return jnp.where(low, got, zero), jnp.where(low, zero, got)
+    below = lax.ppermute(tail, axis, [(place[i], place[i + 1]) for i in range(count - 1)])
+    above = lax.ppermute(head, axis, [(place[i + 1], place[i]) for i in range(count - 1)])
     return above, below
 
 
@@ -40,7 +60,7 @@
 
 
 def exchange(field):
-    return [rims(field, axis, dim) for axis, dim in GRID_AXES]
+    return [rims(field, axis, dim) for axis, dim in ((None, 0), (ROW_AXES, 1), ("col", 2))]
 
 
 def apply_grid(field, near, weights, pad_term):
@@ -149,13 +169,16 @@
 
 def shards(sources, conduct, via_cond, via_map, pad_map, port_tile, pivots, coupling):
     layer_count = lax.axis_size("layer")
+    vertical = via_cond * via_map.astype(jnp.float32)
+    packed = lax.all_to_all(jnp.stack((sources, conduct, vertical)), "layer", 2, 1, tiled=True)
+    sources, conduct, vertical = packed[0], packed[1], packed[2]
     local_layers, grid_rows, grid_cols = sources.shape
-    vertical = via_cond * via_map.astype(jnp.float32)
-    vert_above, vert_below = rims(vertical, "layer", 0)
-    row_halo = rims(conduct, "row", 1)
+    pad_rows = lax.dynamic_slice_in_dim(pad_map, lax.axis_index("layer") * grid_rows, grid_rows, 0)
+    row_halo = rims(conduct, ROW_AXES, 1)
     col_halo = rims(conduct, "col", 2)
-    near_vert = neighbours(vertical, [(vert_above, vert_below), row_halo, col_halo])
-    near_plane = neighbours(conduct, [(vert_above, vert_below), row_halo, col_halo])
+    layer_halo = rims(vertical, None, 0)
+    near_vert = neighbours(vertical, [layer_halo, row_halo, col_halo])
+    near_plane = neighbours(conduct, [layer_halo, row_halo, col_halo])
     weights = (
         jnp.sqrt(vertical * near_vert[0]),
         jnp.sqrt(vertical * near_vert[1]),
@@ -164,8 +187,7 @@
         jnp.sqrt(conduct * near_plane[4]),
         jnp.sqrt(conduct * near_plane[5]),
     )
-    top_flag = (lax.axis_index("layer") == layer_count - 1).astype(jnp.float32)
-    top_layer = pad_gain * pad_map.astype(jnp.float32) * top_flag
+    top_layer = pad_gain * pad_rows.astype(jnp.float32)
     pad_term = jnp.concatenate(
         (jnp.zeros((local_layers - 1, grid_rows, grid_cols), jnp.float32), top_layer[None]), 0
     )
@@ -176,10 +198,10 @@
 
     col_count = lax.axis_size("col")
     tile_cols = grid_cols * col_count // TILE
-    tile_rows = grid_rows * lax.axis_size("row") // TILE
+    tile_rows = grid_rows * axis_count(ROW_AXES) // TILE
     own_rows = grid_rows // TILE
     own_cols = grid_cols // TILE
-    first_row = lax.axis_index("row") * own_rows
+    first_row = (lax.axis_index("row") * layer_count + lax.axis_index("layer")) * own_rows
     first_col = lax.axis_index("col") * own_cols
     flat_tiles = port_tile.reshape(-1)
     local_ids = (
@@ -224,6 +246,7 @@
         else:
             drop = drop + lifted + total
             drop_near = [(d + a) + b for d, a, b in zip(drop_near, lifted_near, total_near)]
+    drop = lax.all_to_all(drop, "layer", 0, 1, tiled=True)
     return (drop, ports)
 
 

time: 237 us -> 169 us (0.71)
  starting transfers between devices: 128 us -> 71.8 us
  local copies, waits for them, and re-layouts: 33.1 us -> 16.9 us
  waiting for transfers between devices: 37.7 us -> 47.2 us
  other arithmetic: 21.6 us -> 18.6 us
    ppermute x36 -> x18, starting transfers between devices: 101 us -> 33.3 us  [the longest x6 16.6 us: rims(): lax.ppermute(tail, axis, [(place[i], place[i + 1]) for i in range(count -...]
    all_to_all x0 -> x2, waiting for transfers between devices: none -> 16 us  [the longest x1 10.6 us: shards(): lax.all_to_all(jnp.stack((sources, conduct, vertical)), 'layer', 2, 1, ti...]
    all_to_all x0 -> x2, starting transfers between devices: none -> 9.2 us  [the longest x1 4.96 us: shards(): drop = lax.all_to_all(drop, 'layer', 0, 1, tiled=True)]
    slice x4 -> x3, local copies, waits for them, and re-layouts: 6.9 us -> 0.15 us  [shards(): sources, conduct, vertical = (packed[0], packed[1], packed[2])]
    ppermute x10, waiting for transfers between devices: 12.2 us -> 7.49 us  [all_sum(): lax.ppermute(value, axis, [(i, i ^ step) for i in range(count)])]
    reshape x4 -> x0, local copies, waits for them, and re-layouts: 4.24 us -> none  [shards(): plane.reshape(own_rows, TILE, own_cols, TILE).sum(axis=(1, 3)).reshape(-1)]
    slice x4 -> x2, local copies, waits for them, and re-layouts: 3.96 us -> 0.17 us  [shards(): centre = ring[1:-1, 1:-1]]
    ppermute x12, waiting for transfers between devices: 21.9 us -> 18.3 us  [swap_col(): return lax.ppermute(value, 'col', [(0, 1), (1, 0)])]
  transfers between devices with their start and end apart: 58 -> 42, of which waited for: 23 -> 19; matrix products, arithmetic and copies ran while one was open for 18% -> 18% of each run, Pallas kernels for 0% -> 0%
where the time goes in v2:
time: 169 us; the launch traced here: 168 us
  starting transfers between devices  71.8 us (42%)
  waiting for transfers between devices  47.2 us (28%)
  other arithmetic  18.6 us (11%)
  local copies, waits for them, and re-layouts  16.9 us (10%)
  matrix products  12.4 us (7%)
    ppermute x12, waiting for transfers between devices, swap_col(): return lax.ppermute(value, 'col', [(0, 1), (1, 0)])  18.3 us
    ppermute x6, starting transfers between devices, rims(): lax.ppermute(tail, axis, [(place[i], place[i + 1]) for i in range(count -...  16.6 us
    ppermute x10, starting transfers between devices, all_sum(): lax.ppermute(value, axis, [(i, i ^ step) for i in range(count)])  16.5 us
    ppermute x12, starting transfers between devices, swap_col(): return lax.ppermute(value, 'col', [(0, 1), (1, 0)])  12.8 us
    all_to_all x1, waiting for transfers between devices, shards(): lax.all_to_all(jnp.stack((sources, conduct, vertical)), 'layer', 2, 1, ti...  10.6 us
    ppermute x6, starting transfers between devices, rims(): got = lax.ppermute(jnp.where(low, tail, head), axis, [(0, 1), (1, 0)])  8.96 us
    ppermute x6, starting transfers between devices, rims(): lax.ppermute(head, axis, [(place[i + 1], place[i]) for i in range(count -...  7.72 us
    ppermute x10, waiting for transfers between devices, all_sum(): lax.ppermute(value, axis, [(i, i ^ step) for i in range(count)])  7.49 us
  transfers between devices with their start and end apart: 42, of which 19 were waited for; matrix products, arithmetic and copies ran while one was open for 18% of the time, Pallas kernels for 0%

profile of v2, /device:TPU:0, one launch (start us, length us, event | category | flops | bytes accessed | tf_op | source)
XLA Modules:
  0.0 168.4 jit_solution(10800624828251478956)
XLA Ops:
  4.3 4.2 %all-to-all-start = ((f32[3,2,64,512]{3,1,0,2:T(2,128)}), f32[3,2,64,512]{3,1,0,2:T(2,128)S(1)}, u32[]{:S(2)}, u32[]{:S(2)}) async-start(f32[3,2,64,512]{3,1,0,2:T(2,128)} %copy.22), calls=%async_computation | async-start | bytes 1572864 | tf_op jit(solution)/shard_map/all_to_all | solution.py:173
  9.6 10.6 %all-to-all-done = f32[3,2,64,512]{3,1,0,2:T(2,128)S(1)} async-done(((f32[3,2,64,512]{3,1,0,2:T(2,128)}), f32[3,2,64,512]{3,1,0,2:T(2,128)S(1)}, u32[]{:S(2)}, u32[]{:S(2)}) %all-to-all-start) | async-done | bytes 786464 | tf_op jit(solution)/shard_map/all_to_all | solution.py:173
  23.2 3.0 %collective-permute-start.12 = (f32[8,1,512]{2,1,0:T(1,128)S(1)}, f32[8,1,512]{2,1,0:T(1,128)S(1)}, u32[]{:S(2)}, u32[]{:S(2)}) collective-permute-start(f32[8,1,512]{2,1,0:T(1,128)S(1)} %get-tuple-element.61), channel_id=1, source_target_pairs={{0,8},{8,16},{16,24},{24,2},{2,10},{10,18},{18,26},{26,4},{4,12},{... | collective-permute-start | bytes 49160 | tf_op jit(solution)/shard_map/ppermute | solution.py:48
  26.3 2.3 %collective-permute-start.13 = (f32[8,16,1]{2,1,0:T(8,128)S(1)}, f32[8,16,1]{2,1,0:T(8,128)S(1)}, u32[]{:S(2)}, u32[]{:S(2)}) collective-permute-start(f32[8,16,1]{2,1,0:T(8,128)S(1)} %slice_select_fusion.5), channel_id=1, source_target_pairs={{0,1},{1,0},{2,3},{3,2},{4,5},{5,4},{6,7},{7,6},{8,9},{9,8},{10,11... | collective-permute-start | bytes 1544 | tf_op jit(solution)/shard_map/ppermute | solution.py:45
  28.7 2.1 %collective-permute-done.13 = f32[8,16,1]{2,1,0:T(8,128)S(1)} collective-permute-done((f32[8,16,1]{2,1,0:T(8,128)S(1)}, f32[8,16,1]{2,1,0:T(8,128)S(1)}, u32[]{:S(2)}, u32[]{:S(2)}) %collective-permute-start.13) | collective-permute-done | bytes 544 | tf_op jit(solution)/shard_map/ppermute | solution.py:45
  33.5 2.4 %collective-permute-start.16 = (f32[8,16,1]{2,1,0:T(8,128)S(1)}, f32[8,16,1]{2,1,0:T(8,128)S(1)}, u32[]{:S(2)}, u32[]{:S(2)}) collective-permute-start(f32[8,16,1]{2,1,0:T(8,128)S(1)} %slice_select_fusion.4), channel_id=1, source_target_pairs={{0,1},{1,0},{2,3},{3,2},{4,5},{5,4},{6,7},{7,6},{8,9},{9,8},{10,11... | collective-permute-start | bytes 1544 | tf_op jit(solution)/shard_map/ppermute | solution.py:45
  38.9 3.0 %collective-permute-start.15 = (f32[8,1,512]{2,1,0:T(1,128)S(1)}, f32[8,1,512]{2,1,0:T(1,128)S(1)}, u32[]{:S(2)}, u32[]{:S(2)}) collective-permute-start(f32[8,1,512]{2,1,0:T(1,128)S(1)} %get-tuple-element.55), channel_id=1, source_target_pairs={{0,8},{8,16},{16,24},{24,2},{2,10},{10,18},{18,26},{26,4},{4,12},{... | collective-permute-start | bytes 49160 | tf_op jit(solution)/shard_map/ppermute | solution.py:48
  42.0 2.4 %collective-permute-start.3 = (f32[2048]{0:T(1024)S(1)}, f32[2048]{0:T(1024)S(1)}, u32[]{:S(2)}, u32[]{:S(2)}) collective-permute-start(f32[2048]{0:T(1024)S(1)} %add.341), channel_id=1, source_target_pairs={{0,4},{2,6},{4,0},{6,2},{1,5},{3,7},{5,1},{7,3},{8,12},{10,14},{12... | collective-permute-start | bytes 24584 | tf_op jit(solution)/shard_map/ppermute | solution.py:97
  47.3 2.0 %collective-permute-start.18 = (f32[8,1,512]{2,1,0:T(1,128)S(1)}, f32[8,1,512]{2,1,0:T(1,128)S(1)}, u32[]{:S(2)}, u32[]{:S(2)}) collective-permute-start(f32[8,1,512]{2,1,0:T(1,128)S(1)} %get-tuple-element.46), channel_id=1, source_target_pairs={{0,8},{8,16},{16,24},{24,2},{2,10},{10,18},{18,26},{26,4},{4,12},{... | collective-permute-start | bytes 49160 | tf_op jit(solution)/shard_map/ppermute | solution.py:48
  58.1 1.7 %collective-permute-done.6 = f32[256]{0:T(256)S(1)} collective-permute-done((f32[256]{0:T(256)S(1)}, f32[256]{0:T(256)S(1)}, u32[]{:S(2)}, u32[]{:S(2)}) %collective-permute-start.6) | collective-permute-done | bytes 1056 | tf_op jit(solution)/shard_map/ppermute | solution.py:103
  62.2 1.7 %collective-permute-done.7 = f32[256]{0:T(256)S(1)} collective-permute-done((f32[256]{0:T(256)S(1)}, f32[256]{0:T(256)S(1)}, u32[]{:S(2)}, u32[]{:S(2)}) %collective-permute-start.7) | collective-permute-done | bytes 1056 | tf_op jit(solution)/shard_map/ppermute | solution.py:103
  66.8 1.7 %collective-permute-done.8 = f32[512]{0:T(512)S(1)} collective-permute-done((f32[512]{0:T(512)S(1)}, f32[512]{0:T(512)S(1)}, u32[]{:S(2)}, u32[]{:S(2)}) %collective-permute-start.8) | collective-permute-done | bytes 2080 | tf_op jit(solution)/shard_map/ppermute | solution.py:103
  70.4 2.2 %collective-permute-done.9 = f32[512]{0:T(512)S(1)} collective-permute-done((f32[512]{0:T(512)S(1)}, f32[512]{0:T(512)S(1)}, u32[]{:S(2)}, u32[]{:S(2)}) %collective-permute-start.9) | collective-permute-done | bytes 2080 | tf_op jit(solution)/shard_map/ppermute | solution.py:103
  80.4 3.6 %collective-permute-start.21 = (f32[8,1,512]{2,1,0:T(1,128)}, f32[8,1,512]{2,1,0:T(1,128)}, u32[]{:S(2)}, u32[]{:S(2)}) collective-permute-start(f32[8,1,512]{2,1,0:T(1,128)} %get-tuple-element.39), channel_id=1, source_target_pairs={{0,8},{8,16},{16,24},{24,2},{2,10},{10,18},{18,26},{26,4},{4,12},{... | collective-permute-start | bytes 49160 | tf_op jit(solution)/shard_map/ppermute | solution.py:48
  89.0 2.5 %fusion.165 = (f32[512]{0:T(512)}, f32[8,16,512]{2,1,0:T(8,128)S(1)}) fusion(f32[8,16,512]{2,1,0:T(8,128)S(1)} %get-tuple-element.12, f32[8,16,511]{2,1,0:T(8,128)} %get-tuple-element.41, f32[8,16,1]{2,1,0:T(8,128)} %get-tuple-element.71, f32[16,512]{1,0:T(8,128)S(1)} %get-tuple-element.79, f32[8,16,512]{2,1,0:T(8,128)S(1)} %get-tuple-element.11, ...), kind=kLoop, calls=%fused_computation.270 | loop fusion | flops 2096640 | bytes 4065280 | tf_op jit(solution)/shard_map/reduce_sum | solution.py:227
  97.0 3.4 %collective-permute-start.23 = (f32[2048]{0:T(1024)S(1)}, f32[2048]{0:T(1024)S(1)}, u32[]{:S(2)}, u32[]{:S(2)}) collective-permute-start(f32[2048]{0:T(1024)S(1)} %bitcast.261), channel_id=1, source_target_pairs={{0,8},{8,0},{16,24},{24,16},{1,9},{9,1},{17,25},{25,17},{2,10},{10... | collective-permute-start | bytes 24584 | tf_op jit(solution)/shard_map/ppermute | solution.py:97
  103.2 3.0 %collective-permute-start.35 = (f32[8,1,512]{2,1,0:T(1,128)S(1)}, f32[8,1,512]{2,1,0:T(1,128)S(1)}, u32[]{:S(2)}, u32[]{:S(2)}) collective-permute-start(f32[8,1,512]{2,1,0:T(1,128)S(1)} %get-tuple-element.31), channel_id=1, source_target_pairs={{0,8},{8,16},{16,24},{24,2},{2,10},{10,18},{18,26},{26,4},{4,12},{... | collective-permute-start | bytes 49160 | tf_op jit(solution)/shard_map/ppermute | solution.py:48
  106.3 2.0 %collective-permute-start.24 = (f32[2048]{0:T(1024)S(1)}, f32[2048]{0:T(1024)S(1)}, u32[]{:S(2)}, u32[]{:S(2)}) collective-permute-start(f32[2048]{0:T(1024)S(1)} %add.385), channel_id=1, source_target_pairs={{0,16},{8,24},{16,0},{24,8},{1,17},{9,25},{17,1},{25,9},{2,18},{10... | collective-permute-start | bytes 24584 | tf_op jit(solution)/shard_map/ppermute | solution.py:97
  108.3 1.7 %collective-permute-done.24 = f32[2048]{0:T(1024)S(1)} collective-permute-done((f32[2048]{0:T(1024)S(1)}, f32[2048]{0:T(1024)S(1)}, u32[]{:S(2)}, u32[]{:S(2)}) %collective-permute-start.24) | collective-permute-done | bytes 8224 | tf_op jit(solution)/shard_map/ppermute | solution.py:97
  110.0 2.3 %collective-permute-start.25 = (f32[2048]{0:T(1024)S(1)}, f32[2048]{0:T(1024)S(1)}, u32[]{:S(2)}, u32[]{:S(2)}) collective-permute-start(f32[2048]{0:T(1024)S(1)} %add.386), channel_id=1, source_target_pairs={{0,2},{2,0},{4,6},{6,4},{1,3},{3,1},{5,7},{7,5},{8,10},{10,8},{12,... | collective-permute-start | bytes 24584 | tf_op jit(solution)/shard_map/ppermute | solution.py:97
  112.3 2.1 %fusion.157 = f32[8,16,512]{2,1,0:T(8,128)S(1)} fusion(f32[8,16,512]{2,1,0:T(8,128)S(1)} %mul.264, f32[8,16,512]{2,1,0:T(8,128)} %copy-done.6, f32[8,16,512]{2,1,0:T(8,128)} %copy-done.1, f32[8,16,511]{2,1,0:T(8,128)} %get-tuple-element.33, f32[8,16,1]{2,1,0:T(8,128)S(1)} %get-tuple-element.69, f32[8,16,512]{2,1,0:T(8,128)S(1)} %get-tuple-element.11, ...), kind=kLoop, calls=%fused_computation.215 | loop fusion | flops 1900544 | bytes 4161536 | tf_op jit(solution)/shard_map/add | solution.py:84
  116.1 1.8 %collective-permute-start.26 = (f32[2048]{0:T(1024)S(1)}, f32[2048]{0:T(1024)S(1)}, u32[]{:S(2)}, u32[]{:S(2)}) collective-permute-start(f32[2048]{0:T(1024)S(1)} %add.387), channel_id=1, source_target_pairs={{0,4},{2,6},{4,0},{6,2},{1,5},{3,7},{5,1},{7,3},{8,12},{10,14},{12... | collective-permute-start | bytes 24584 | tf_op jit(solution)/shard_map/ppermute | solution.py:97
  118.7 2.0 %collective-permute-done.26 = f32[2048]{0:T(1024)S(1)} collective-permute-done((f32[2048]{0:T(1024)S(1)}, f32[2048]{0:T(1024)S(1)}, u32[]{:S(2)}, u32[]{:S(2)}) %collective-permute-start.26) | collective-permute-done | bytes 8224 | tf_op jit(solution)/shard_map/ppermute | solution.py:97
  122.0 2.3 %collective-permute-done.27 = f32[2048]{0:T(1024)S(1)} collective-permute-done((f32[2048]{0:T(1024)S(1)}, f32[2048]{0:T(1024)S(1)}, u32[]{:S(2)}, u32[]{:S(2)}) %collective-permute-start.27) | collective-permute-done | bytes 8224 | tf_op jit(solution)/shard_map/ppermute | solution.py:97
  125.8 1.9 %collective-permute-start.38 = (f32[8,1,512]{2,1,0:T(1,128)}, f32[8,1,512]{2,1,0:T(1,128)}, u32[]{:S(2)}, u32[]{:S(2)}) collective-permute-start(f32[8,1,512]{2,1,0:T(1,128)} %get-tuple-element.22), channel_id=1, source_target_pairs={{0,8},{8,16},{16,24},{24,2},{2,10},{10,18},{18,26},{26,4},{4,12},{... | collective-permute-start | bytes 49160 | tf_op jit(solution)/shard_map/ppermute | solution.py:48
  136.4 2.3 %collective-permute-done.30 = f32[256]{0:T(256)S(1)} collective-permute-done((f32[256]{0:T(256)S(1)}, f32[256]{0:T(256)S(1)}, u32[]{:S(2)}, u32[]{:S(2)}) %collective-permute-start.30) | collective-permute-done | bytes 1056 | tf_op jit(solution)/shard_map/ppermute | solution.py:103
  141.0 2.3 %collective-permute-done.31 = f32[512]{0:T(512)S(1)} collective-permute-done((f32[512]{0:T(512)S(1)}, f32[512]{0:T(512)S(1)}, u32[]{:S(2)}, u32[]{:S(2)}) %collective-permute-start.31) | collective-permute-done | bytes 2080 | tf_op jit(solution)/shard_map/ppermute | solution.py:103
  145.1 2.3 %collective-permute-done.32 = f32[512]{0:T(512)S(1)} collective-permute-done((f32[512]{0:T(512)S(1)}, f32[512]{0:T(512)S(1)}, u32[]{:S(2)}, u32[]{:S(2)}) %collective-permute-start.32) | collective-permute-done | bytes 2080 | tf_op jit(solution)/shard_map/ppermute | solution.py:103
  148.7 2.8 %collective-permute-done.33 = f32[1024]{0:T(1024)S(1)} collective-permute-done((f32[1024]{0:T(1024)S(1)}, f32[1024]{0:T(1024)S(1)}, u32[]{:S(2)}, u32[]{:S(2)}) %collective-permute-start.33) | collective-permute-done | bytes 4128 | tf_op jit(solution)/shard_map/ppermute | solution.py:103
  152.9 3.7 %fusion.125 = f32[8,16,512]{2,1,0:T(8,128)} fusion(f32[8,16,512]{2,1,0:T(8,128)} %copy-done.6, f32[1,16,512]{2,1,0:T(8,128)S(1)} %multiply_bitcast_fusion.1, f32[8,16,512]{2,1,0:T(8,128)} %copy-done.2, f32[8,1,512]{2,1,0:T(1,128)} %collective-permute-done.37, f32[8,15,512]{2,1,0:T(8,128)} %get-tuple-element.25, f32[8,16,512]{2,1,0:T(8,128)S(1)} %get-tuple-element.10, ...), kind=kLoop, calls=%fused_computation.134 | loop fusion | flops 3997696 | bytes 5996544 | tf_op jit(solution)/shard_map/add | solution.py:237
  156.7 5.0 %all-to-all-start.1 = ((f32[8,16,512]{2,1,0:T(8,128)}), f32[8,16,512]{2,1,0:T(8,128)S(1)}, u32[]{:S(2)}, u32[]{:S(2)}) async-start(f32[8,16,512]{2,1,0:T(8,128)} %fusion.125), calls=%async_computation.1 | async-start | bytes 524288 | tf_op jit(solution)/shard_map/all_to_all | solution.py:249
  162.2 5.4 %all-to-all-done.1 = f32[8,16,512]{2,1,0:T(8,128)S(1)} async-done(((f32[8,16,512]{2,1,0:T(8,128)}), f32[8,16,512]{2,1,0:T(8,128)S(1)}, u32[]{:S(2)}, u32[]{:S(2)}) %all-to-all-start.1) | async-done | bytes 262176 | tf_op jit(solution)/shard_map/all_to_all | solution.py:249
  (240 shorter events, 75.1 us)
Async XLA Ops:
  4.3 15.9 %all-to-all-start = ((f32[3,2,64,512]{3,1,0,2:T(2,128)}), f32[3,2,64,512]{3,1,0,2:T(2,128)S(1)}, u32[]{:S(2)}, u32[]{:S(2)}) async-start(f32[3,2,64,512]{3,1,0,2:T(2,128)} %copy.22), calls=%async_computation | async-start | bytes 1572864 | tf_op jit(solution)/shard_map/all_to_all | solution.py:173
  21.8 9.1 %collective-permute-start = (f32[2048]{0:T(1024)S(1)}, f32[2048]{0:T(1024)S(1)}, u32[]{:S(2)}, u32[]{:S(2)}) collective-permute-start(f32[2048]{0:T(1024)S(1)} %bitcast.259), channel_id=1, source_target_pairs={{0,8},{8,0},{16,24},{24,16},{1,9},{9,1},{17,25},{25,17},{2,10},{10... | collective-permute-start | bytes 24584 | tf_op jit(solution)/shard_map/ppermute | solution.py:97
  21.9 10.7 %collective-permute-start.11 = (f32[8,1,512]{2,1,0:T(1,128)S(1)}, f32[8,1,512]{2,1,0:T(1,128)S(1)}, u32[]{:S(2)}, u32[]{:S(2)}) collective-permute-start(f32[8,1,512]{2,1,0:T(1,128)S(1)} %get-tuple-element.60), channel_id=1, source_target_pairs={{8,0},{16,8},{24,16},{2,24},{10,2},{18,10},{26,18},{4,26},{12,4},{... | collective-permute-start | bytes 49160 | tf_op jit(solution)/shard_map/ppermute | solution.py:49
  23.2 9.4 %collective-permute-start.12 = (f32[8,1,512]{2,1,0:T(1,128)S(1)}, f32[8,1,512]{2,1,0:T(1,128)S(1)}, u32[]{:S(2)}, u32[]{:S(2)}) collective-permute-start(f32[8,1,512]{2,1,0:T(1,128)S(1)} %get-tuple-element.61), channel_id=1, source_target_pairs={{0,8},{8,16},{16,24},{24,2},{2,10},{10,18},{18,26},{26,4},{4,12},{... | collective-permute-start | bytes 49160 | tf_op jit(solution)/shard_map/ppermute | solution.py:48
  26.3 4.5 %collective-permute-start.13 = (f32[8,16,1]{2,1,0:T(8,128)S(1)}, f32[8,16,1]{2,1,0:T(8,128)S(1)}, u32[]{:S(2)}, u32[]{:S(2)}) collective-permute-start(f32[8,16,1]{2,1,0:T(8,128)S(1)} %slice_select_fusion.5), channel_id=1, source_target_pairs={{0,1},{1,0},{2,3},{3,2},{4,5},{5,4},{6,7},{7,6},{8,9},{9,8},{10,11... | collective-permute-start | bytes 1544 | tf_op jit(solution)/shard_map/ppermute | solution.py:45
  30.9 5.0 %collective-permute-start.1 = (f32[2048]{0:T(1024)S(1)}, f32[2048]{0:T(1024)S(1)}, u32[]{:S(2)}, u32[]{:S(2)}) collective-permute-start(f32[2048]{0:T(1024)S(1)} %add.339), channel_id=1, source_target_pairs={{0,16},{8,24},{16,0},{24,8},{1,17},{9,25},{17,1},{25,9},{2,18},{10... | collective-permute-start | bytes 24584 | tf_op jit(solution)/shard_map/ppermute | solution.py:97
  33.5 8.4 %collective-permute-start.16 = (f32[8,16,1]{2,1,0:T(8,128)S(1)}, f32[8,16,1]{2,1,0:T(8,128)S(1)}, u32[]{:S(2)}, u32[]{:S(2)}) collective-permute-start(f32[8,16,1]{2,1,0:T(8,128)S(1)} %slice_select_fusion.4), channel_id=1, source_target_pairs={{0,1},{1,0},{2,3},{3,2},{4,5},{5,4},{6,7},{7,6},{8,9},{9,8},{10,11... | collective-permute-start | bytes 1544 | tf_op jit(solution)/shard_map/ppermute | solution.py:45
  35.9 6.0 %collective-permute-start.2 = (f32[2048]{0:T(1024)S(1)}, f32[2048]{0:T(1024)S(1)}, u32[]{:S(2)}, u32[]{:S(2)}) collective-permute-start(f32[2048]{0:T(1024)S(1)} %add.340), channel_id=1, source_target_pairs={{0,2},{2,0},{4,6},{6,4},{1,3},{3,1},{5,7},{7,5},{8,10},{10,8},{12,... | collective-permute-start | bytes 24584 | tf_op jit(solution)/shard_map/ppermute | solution.py:97
  37.6 6.8 %collective-permute-start.14 = (f32[8,1,512]{2,1,0:T(1,128)S(1)}, f32[8,1,512]{2,1,0:T(1,128)S(1)}, u32[]{:S(2)}, u32[]{:S(2)}) collective-permute-start(f32[8,1,512]{2,1,0:T(1,128)S(1)} %get-tuple-element.54), channel_id=1, source_target_pairs={{8,0},{16,8},{24,16},{2,24},{10,2},{18,10},{26,18},{4,26},{12,4},{... | collective-permute-start | bytes 49160 | tf_op jit(solution)/shard_map/ppermute | solution.py:49
  38.9 5.5 %collective-permute-start.15 = (f32[8,1,512]{2,1,0:T(1,128)S(1)}, f32[8,1,512]{2,1,0:T(1,128)S(1)}, u32[]{:S(2)}, u32[]{:S(2)}) collective-permute-start(f32[8,1,512]{2,1,0:T(1,128)S(1)} %get-tuple-element.55), channel_id=1, source_target_pairs={{0,8},{8,16},{16,24},{24,2},{2,10},{10,18},{18,26},{26,4},{4,12},{... | collective-permute-start | bytes 49160 | tf_op jit(solution)/shard_map/ppermute | solution.py:48
  42.0 4.6 %collective-permute-start.3 = (f32[2048]{0:T(1024)S(1)}, f32[2048]{0:T(1024)S(1)}, u32[]{:S(2)}, u32[]{:S(2)}) collective-permute-start(f32[2048]{0:T(1024)S(1)} %add.341), channel_id=1, source_target_pairs={{0,4},{2,6},{4,0},{6,2},{1,5},{3,7},{5,1},{7,3},{8,12},{10,14},{12... | collective-permute-start | bytes 24584 | tf_op jit(solution)/shard_map/ppermute | solution.py:97
  46.6 4.8 %collective-permute-start.4 = (f32[2048]{0:T(1024)S(1)}, f32[2048]{0:T(1024)S(1)}, u32[]{:S(2)}, u32[]{:S(2)}) collective-permute-start(f32[2048]{0:T(1024)S(1)} %add.342), channel_id=1, source_target_pairs={{0,1},{1,0},{2,3},{3,2},{4,5},{5,4},{6,7},{7,6},{8,9},{9,8},{10,11... | collective-permute-start | bytes 24584 | tf_op jit(solution)/shard_map/ppermute | solution.py:97
  47.3 27.2 %collective-permute-start.18 = (f32[8,1,512]{2,1,0:T(1,128)S(1)}, f32[8,1,512]{2,1,0:T(1,128)S(1)}, u32[]{:S(2)}, u32[]{:S(2)}) collective-permute-start(f32[8,1,512]{2,1,0:T(1,128)S(1)} %get-tuple-element.46), channel_id=1, source_target_pairs={{0,8},{8,16},{16,24},{24,2},{2,10},{10,18},{18,26},{26,4},{4,12},{... | collective-permute-start | bytes 49160 | tf_op jit(solution)/shard_map/ppermute | solution.py:48
  49.3 25.2 %collective-permute-start.17 = (f32[8,1,512]{2,1,0:T(1,128)S(1)}, f32[8,1,512]{2,1,0:T(1,128)S(1)}, u32[]{:S(2)}, u32[]{:S(2)}) collective-permute-start(f32[8,1,512]{2,1,0:T(1,128)S(1)} %get-tuple-element.47), channel_id=1, source_target_pairs={{8,0},{16,8},{24,16},{2,24},{10,2},{18,10},{26,18},{4,26},{12,4},{... | collective-permute-start | bytes 49160 | tf_op jit(solution)/shard_map/ppermute | solution.py:49
  50.6 4.3 %collective-permute-start.19 = (f32[8,16,1]{2,1,0:T(8,128)S(1)}, f32[8,16,1]{2,1,0:T(8,128)S(1)}, u32[]{:S(2)}, u32[]{:S(2)}) collective-permute-start(f32[8,16,1]{2,1,0:T(8,128)S(1)} %slice_select_fusion.3), channel_id=1, source_target_pairs={{0,1},{1,0},{2,3},{3,2},{4,5},{5,4},{6,7},{7,6},{8,9},{9,8},{10,11... | collective-permute-start | bytes 1544 | tf_op jit(solution)/shard_map/ppermute | solution.py:45
  73.1 11.5 %collective-permute-start.10 = (f32[1024]{0:T(1024)S(1)}, f32[1024]{0:T(1024)S(1)}, u32[]{:S(2)}, u32[]{:S(2)}) collective-permute-start(f32[1024]{0:T(1024)S(1)} %pad_maximum_fusion.2), channel_id=1, source_target_pairs={{0,1},{1,0},{2,3},{3,2},{4,5},{5,4},{6,7},{7,6},{8,9},{9,8},{10,11... | collective-permute-start | bytes 12296 | tf_op jit(solution)/shard_map/ppermute | solution.py:103
  77.8 6.2 %collective-permute-start.22 = (f32[8,16,1]{2,1,0:T(8,128)S(1)}, f32[8,16,1]{2,1,0:T(8,128)S(1)}, u32[]{:S(2)}, u32[]{:S(2)}) collective-permute-start(f32[8,16,1]{2,1,0:T(8,128)S(1)} %slice_select_fusion.2), channel_id=1, source_target_pairs={{0,1},{1,0},{2,3},{3,2},{4,5},{5,4},{6,7},{7,6},{8,9},{9,8},{10,11... | collective-permute-start | bytes 1544 | tf_op jit(solution)/shard_map/ppermute | solution.py:45
  79.1 9.9 %collective-permute-start.20 = (f32[8,1,512]{2,1,0:T(1,128)}, f32[8,1,512]{2,1,0:T(1,128)}, u32[]{:S(2)}, u32[]{:S(2)}) collective-permute-start(f32[8,1,512]{2,1,0:T(1,128)} %get-tuple-element.38), channel_id=1, source_target_pairs={{8,0},{16,8},{24,16},{2,24},{10,2},{18,10},{26,18},{4,26},{12,4},{... | collective-permute-start | bytes 49160 | tf_op jit(solution)/shard_map/ppermute | solution.py:49
  80.4 8.7 %collective-permute-start.21 = (f32[8,1,512]{2,1,0:T(1,128)}, f32[8,1,512]{2,1,0:T(1,128)}, u32[]{:S(2)}, u32[]{:S(2)}) collective-permute-start(f32[8,1,512]{2,1,0:T(1,128)} %get-tuple-element.39), channel_id=1, source_target_pairs={{0,8},{8,16},{16,24},{24,2},{2,10},{10,18},{18,26},{26,4},{4,12},{... | collective-permute-start | bytes 49160 | tf_op jit(solution)/shard_map/ppermute | solution.py:48
  97.0 9.2 %collective-permute-start.23 = (f32[2048]{0:T(1024)S(1)}, f32[2048]{0:T(1024)S(1)}, u32[]{:S(2)}, u32[]{:S(2)}) collective-permute-start(f32[2048]{0:T(1024)S(1)} %bitcast.261), channel_id=1, source_target_pairs={{0,8},{8,0},{16,24},{24,16},{1,9},{9,1},{17,25},{25,17},{2,10},{10... | collective-permute-start | bytes 24584 | tf_op jit(solution)/shard_map/ppermute | solution.py:97
  100.4 7.9 %collective-permute-start.36 = (f32[8,16,1]{2,1,0:T(8,128)S(1)}, f32[8,16,1]{2,1,0:T(8,128)S(1)}, u32[]{:S(2)}, u32[]{:S(2)}) collective-permute-start(f32[8,16,1]{2,1,0:T(8,128)S(1)} %slice_select_fusion.1), channel_id=1, source_target_pairs={{0,1},{1,0},{2,3},{3,2},{4,5},{5,4},{6,7},{7,6},{8,9},{9,8},{10,11... | collective-permute-start | bytes 1544 | tf_op jit(solution)/shard_map/ppermute | solution.py:45
  101.9 10.4 %collective-permute-start.34 = (f32[8,1,512]{2,1,0:T(1,128)S(1)}, f32[8,1,512]{2,1,0:T(1,128)S(1)}, u32[]{:S(2)}, u32[]{:S(2)}) collective-permute-start(f32[8,1,512]{2,1,0:T(1,128)S(1)} %get-tuple-element.30), channel_id=1, source_target_pairs={{8,0},{16,8},{24,16},{2,24},{10,2},{18,10},{26,18},{4,26},{12,4},{... | collective-permute-start | bytes 49160 | tf_op jit(solution)/shard_map/ppermute | solution.py:49
  103.2 9.1 %collective-permute-start.35 = (f32[8,1,512]{2,1,0:T(1,128)S(1)}, f32[8,1,512]{2,1,0:T(1,128)S(1)}, u32[]{:S(2)}, u32[]{:S(2)}) collective-permute-start(f32[8,1,512]{2,1,0:T(1,128)S(1)} %get-tuple-element.31), channel_id=1, source_target_pairs={{0,8},{8,16},{16,24},{24,2},{2,10},{10,18},{18,26},{26,4},{4,12},{... | collective-permute-start | bytes 49160 | tf_op jit(solution)/shard_map/ppermute | solution.py:48
  106.3 3.7 %collective-permute-start.24 = (f32[2048]{0:T(1024)S(1)}, f32[2048]{0:T(1024)S(1)}, u32[]{:S(2)}, u32[]{:S(2)}) collective-permute-start(f32[2048]{0:T(1024)S(1)} %add.385), channel_id=1, source_target_pairs={{0,16},{8,24},{16,0},{24,8},{1,17},{9,25},{17,1},{25,9},{2,18},{10... | collective-permute-start | bytes 24584 | tf_op jit(solution)/shard_map/ppermute | solution.py:97
  110.0 6.1 %collective-permute-start.25 = (f32[2048]{0:T(1024)S(1)}, f32[2048]{0:T(1024)S(1)}, u32[]{:S(2)}, u32[]{:S(2)}) collective-permute-start(f32[2048]{0:T(1024)S(1)} %add.386), channel_id=1, source_target_pairs={{0,2},{2,0},{4,6},{6,4},{1,3},{3,1},{5,7},{7,5},{8,10},{10,8},{12,... | collective-permute-start | bytes 24584 | tf_op jit(solution)/shard_map/ppermute | solution.py:97
  116.1 4.6 %collective-permute-start.26 = (f32[2048]{0:T(1024)S(1)}, f32[2048]{0:T(1024)S(1)}, u32[]{:S(2)}, u32[]{:S(2)}) collective-permute-start(f32[2048]{0:T(1024)S(1)} %add.387), channel_id=1, source_target_pairs={{0,4},{2,6},{4,0},{6,2},{1,5},{3,7},{5,1},{7,3},{8,12},{10,14},{12... | collective-permute-start | bytes 24584 | tf_op jit(solution)/shard_map/ppermute | solution.py:97
  125.0 5.4 %collective-permute-start.28 = (f32[256]{0:T(256)S(1)}, f32[256]{0:T(256)S(1)}, u32[]{:S(2)}, u32[]{:S(2)}) collective-permute-start(f32[256]{0:T(256)S(1)} %dynamic-slice_subtract_fusion.2), channel_id=1, source_target_pairs={{0,1},{1,0},{2,3},{3,2},{4,5},{5,4},{6,7},{7,6},{8,9},{9,8},{10,11... | collective-permute-start | bytes 3080 | tf_op jit(solution)/shard_map/ppermute | solution.py:103
  125.8 27.2 %collective-permute-start.38 = (f32[8,1,512]{2,1,0:T(1,128)}, f32[8,1,512]{2,1,0:T(1,128)}, u32[]{:S(2)}, u32[]{:S(2)}) collective-permute-start(f32[8,1,512]{2,1,0:T(1,128)} %get-tuple-element.22), channel_id=1, source_target_pairs={{0,8},{8,16},{16,24},{24,2},{2,10},{10,18},{18,26},{26,4},{4,12},{... | collective-permute-start | bytes 49160 | tf_op jit(solution)/shard_map/ppermute | solution.py:48
  127.7 25.3 %collective-permute-start.37 = (f32[8,1,512]{2,1,0:T(1,128)}, f32[8,1,512]{2,1,0:T(1,128)}, u32[]{:S(2)}, u32[]{:S(2)}) collective-permute-start(f32[8,1,512]{2,1,0:T(1,128)} %get-tuple-element.23), channel_id=1, source_target_pairs={{8,0},{16,8},{24,16},{2,24},{10,2},{18,10},{26,18},{4,26},{12,4},{... | collective-permute-start | bytes 49160 | tf_op jit(solution)/shard_map/ppermute | solution.py:49
  128.9 4.3 %collective-permute-start.39 = (f32[8,16,1]{2,1,0:T(8,128)S(1)}, f32[8,16,1]{2,1,0:T(8,128)S(1)}, u32[]{:S(2)}, u32[]{:S(2)}) collective-permute-start(f32[8,16,1]{2,1,0:T(8,128)S(1)} %slice_select_fusion), channel_id=1, source_target_pairs={{0,1},{1,0},{2,3},{3,2},{4,5},{5,4},{6,7},{7,6},{8,9},{9,8},{10,11... | collective-permute-start | bytes 1544 | tf_op jit(solution)/shard_map/ppermute | solution.py:45
  147.9 3.7 %collective-permute-start.33 = (f32[1024]{0:T(1024)S(1)}, f32[1024]{0:T(1024)S(1)}, u32[]{:S(2)}, u32[]{:S(2)}) collective-permute-start(f32[1024]{0:T(1024)S(1)} %pad_maximum_fusion.3), channel_id=1, source_target_pairs={{0,1},{1,0},{2,3},{3,2},{4,5},{5,4},{6,7},{7,6},{8,9},{9,8},{10,11... | collective-permute-start | bytes 12296 | tf_op jit(solution)/shard_map/ppermute | solution.py:103
  156.7 11.0 %all-to-all-start.1 = ((f32[8,16,512]{2,1,0:T(8,128)}), f32[8,16,512]{2,1,0:T(8,128)S(1)}, u32[]{:S(2)}, u32[]{:S(2)}) async-start(f32[8,16,512]{2,1,0:T(8,128)} %fusion.125), calls=%async_computation.1 | async-start | bytes 524288 | tf_op jit(solution)/shard_map/all_to_all | solution.py:249
  (25 other events, 431.5 us)

commit v3 on v2

--- a/solution.py
+++ b/solution.py
@@ -169,6 +169,18 @@
 
 def shards(sources, conduct, via_cond, via_map, pad_map, port_tile, pivots, coupling):
     layer_count = lax.axis_size("layer")
+    col_count = lax.axis_size("col")
+    flat_tiles = port_tile.reshape(-1)
+    tile_cols = sources.shape[2] * col_count // TILE
+    start_rows = sources.shape[1] // TILE
+    start_cols = sources.shape[2] // TILE
+    start_ids = (
+        (lax.axis_index("row") * start_rows + jnp.arange(start_rows, dtype=jnp.int32))[:, None] * tile_cols
+        + (lax.axis_index("col") * start_cols + jnp.arange(start_cols, dtype=jnp.int32))[None, :]
+    ).reshape(-1)
+    start_plane = jnp.sum(sources, axis=0)
+    start_tiles = start_plane.reshape(start_rows, TILE, start_cols, TILE).sum(axis=(1, 3)).reshape(-1)
+    start_rhs = jnp.dot((flat_tiles[:, None] == start_ids[None, :]).astype(jnp.float32), start_tiles, precision=highest)
     vertical = via_cond * via_map.astype(jnp.float32)
     packed = lax.all_to_all(jnp.stack((sources, conduct, vertical)), "layer", 2, 1, tiled=True)
     sources, conduct, vertical = packed[0], packed[1], packed[2]
@@ -196,14 +208,11 @@
         diagonal = diagonal + weight
     inverse = 1.0 / diagonal
 
-    col_count = lax.axis_size("col")
-    tile_cols = grid_cols * col_count // TILE
     tile_rows = grid_rows * axis_count(ROW_AXES) // TILE
     own_rows = grid_rows // TILE
     own_cols = grid_cols // TILE
     first_row = (lax.axis_index("row") * layer_count + lax.axis_index("layer")) * own_rows
     first_col = lax.axis_index("col") * own_cols
-    flat_tiles = port_tile.reshape(-1)
     local_ids = (
         (first_row + jnp.arange(own_rows, dtype=jnp.int32))[:, None] * tile_cols
         + (first_col + jnp.arange(own_cols, dtype=jnp.int32))[None, :]
@@ -223,9 +232,12 @@
             resid = sources
         else:
             resid = sources - apply_grid(drop, drop_near, weights, pad_term)
-        plane = jnp.sum(resid, axis=0)
-        tiles = plane.reshape(own_rows, TILE, own_cols, TILE).sum(axis=(1, 3)).reshape(-1)
-        local_rhs = jnp.dot(gather_local, tiles, precision=highest)
+        if drop is None:
+            local_rhs = start_rhs
+        else:
+            plane = jnp.sum(resid, axis=0)
+            tiles = plane.reshape(own_rows, TILE, own_cols, TILE).sum(axis=(1, 3)).reshape(-1)
+            local_rhs = jnp.dot(gather_local, tiles, precision=highest)
         rhs = all_sum(local_rhs).reshape(NPANEL, PANEL) * (restrict_scale / TILE)
         ports = coarse(rhs, pivots, coupling)
         tile_values = jnp.dot(scatter_ring, ports.reshape(-1), precision=highest).reshape(own_rows + 2, own_cols + 2)

time: 169 us -> 177 us (1.047)
  starting transfers between devices: 71.8 us -> 87.1 us
  local copies, waits for them, and re-layouts: 16.9 us -> 13.1 us
  waiting for transfers between devices: 47.2 us -> 44.1 us
  other arithmetic: 18.6 us -> 16 us
  matrix products: 12.4 us -> 14.5 us
    all_to_all x1, waiting for transfers between devices: 10.6 us -> 0.01 us  [shards(): lax.all_to_all(jnp.stack((sources, conduct, vertical)), 'layer', 2, 1, ti...]
    ppermute x10, starting transfers between devices: 16.5 us -> 25.5 us  [all_sum(): lax.ppermute(value, axis, [(i, i ^ step) for i in range(count)])]
    ppermute x10, waiting for transfers between devices: 7.49 us -> 16 us  [all_sum(): lax.ppermute(value, axis, [(i, i ^ step) for i in range(count)])]
    ppermute x12, starting transfers between devices: 12.8 us -> 19.4 us  [swap_col(): return lax.ppermute(value, 'col', [(0, 1), (1, 0)])]
    ppermute x12, waiting for transfers between devices: 18.3 us -> 13.9 us  [swap_col(): return lax.ppermute(value, 'col', [(0, 1), (1, 0)])]
    ppermute x6, waiting for transfers between devices: 0.02 us -> 2.69 us  [rims(): lax.ppermute(head, axis, [(place[i + 1], place[i]) for i in range(count -...]
    slice x12, local copies, waits for them, and re-layouts: 6.23 us -> 3.94 us  [neighbours(): lax.slice_in_dim(field, 1, size, axis=dim)]
    dot_general x8, matrix products: 4.05 us -> 6.13 us  [coarse_pair(): jnp.dot(pivots[section], forward[section], precision=highest)]
  transfers between devices with their start and end apart: 42 -> 42, of which waited for: 19 -> 25; matrix products, arithmetic and copies ran while one was open for 18% -> 14% of each run, Pallas kernels for 0% -> 0%
where the time goes in v3:
time: 177 us; the launch traced here: 176 us
  starting transfers between devices  87.1 us (49%)
  waiting for transfers between devices  44.1 us (25%)
  other arithmetic  16 us (9%)
  matrix products  14.5 us (8%)
  local copies, waits for them, and re-layouts  13.1 us (7%)
    ppermute x10, starting transfers between devices, all_sum(): lax.ppermute(value, axis, [(i, i ^ step) for i in range(count)])  25.5 us
    ppermute x12, starting transfers between devices, swap_col(): return lax.ppermute(value, 'col', [(0, 1), (1, 0)])  19.4 us
    ppermute x6, starting transfers between devices, rims(): lax.ppermute(tail, axis, [(place[i], place[i + 1]) for i in range(count -...  18 us
    ppermute x10, waiting for transfers between devices, all_sum(): lax.ppermute(value, axis, [(i, i ^ step) for i in range(count)])  16 us
    ppermute x12, waiting for transfers between devices, swap_col(): return lax.ppermute(value, 'col', [(0, 1), (1, 0)])  13.9 us
    ppermute x6, starting transfers between devices, rims(): lax.ppermute(head, axis, [(place[i + 1], place[i]) for i in range(count -...  7.74 us
    ppermute x6, starting transfers between devices, rims(): got = lax.ppermute(jnp.where(low, tail, head), axis, [(0, 1), (1, 0)])  7.22 us
    dot_general x8, matrix products, coarse_pair(): jnp.dot(pivots[section], forward[section], precision=highest)  6.13 us
  transfers between devices with their start and end apart: 42, of which 25 were waited for; matrix products, arithmetic and copies ran while one was open for 14% of the time, Pallas kernels for 0%

profile of v3, /device:TPU:0, one launch (start us, length us, event | category | flops | bytes accessed | tf_op | source)
XLA Modules:
  0.0 176.1 jit_solution(9059817910980043240)
XLA Ops:
  4.3 4.2 %all-to-all-start = ((f32[3,2,64,512]{3,1,0,2:T(2,128)}), f32[3,2,64,512]{3,1,0,2:T(2,128)S(1)}, u32[]{:S(2)}, u32[]{:S(2)}) async-start(f32[3,2,64,512]{3,1,0,2:T(2,128)} %copy.22), calls=%async_computation | async-start | bytes 1572864 | tf_op jit(solution)/shard_map/all_to_all | solution.py:185
  11.5 2.1 %collective-permute-start.1 = (f32[2048]{0:T(1024)S(1)}, f32[2048]{0:T(1024)S(1)}, u32[]{:S(2)}, u32[]{:S(2)}) collective-permute-start(f32[2048]{0:T(1024)S(1)} %add.378), channel_id=1, source_target_pairs={{0,16},{8,24},{16,0},{24,8},{1,17},{9,25},{17,1},{25,9},{2,18},{10... | collective-permute-start | bytes 24584 | tf_op jit(solution)/shard_map/ppermute | solution.py:97
  13.6 6.8 %collective-permute-done.1 = f32[2048]{0:T(1024)S(1)} collective-permute-done((f32[2048]{0:T(1024)S(1)}, f32[2048]{0:T(1024)S(1)}, u32[]{:S(2)}, u32[]{:S(2)}) %collective-permute-start.1) | collective-permute-done | bytes 8224 | tf_op jit(solution)/shard_map/ppermute | solution.py:97
  20.4 2.3 %collective-permute-start.2 = (f32[2048]{0:T(1024)S(1)}, f32[2048]{0:T(1024)S(1)}, u32[]{:S(2)}, u32[]{:S(2)}) collective-permute-start(f32[2048]{0:T(1024)S(1)} %add.379), channel_id=1, source_target_pairs={{0,2},{2,0},{4,6},{6,4},{1,3},{3,1},{5,7},{7,5},{8,10},{10,8},{12,... | collective-permute-start | bytes 24584 | tf_op jit(solution)/shard_map/ppermute | solution.py:97
  24.3 3.0 %collective-permute-start.3 = (f32[2048]{0:T(1024)S(1)}, f32[2048]{0:T(1024)S(1)}, u32[]{:S(2)}, u32[]{:S(2)}) collective-permute-start(f32[2048]{0:T(1024)S(1)} %add.380), channel_id=1, source_target_pairs={{0,4},{2,6},{4,0},{6,2},{1,5},{3,7},{5,1},{7,3},{8,12},{10,14},{12... | collective-permute-start | bytes 24584 | tf_op jit(solution)/shard_map/ppermute | solution.py:97
  29.0 1.9 %collective-permute-start.4 = (f32[2048]{0:T(1024)S(1)}, f32[2048]{0:T(1024)S(1)}, u32[]{:S(2)}, u32[]{:S(2)}) collective-permute-start(f32[2048]{0:T(1024)S(1)} %add.381), channel_id=1, source_target_pairs={{0,1},{1,0},{2,3},{3,2},{4,5},{5,4},{6,7},{7,6},{8,9},{9,8},{10,11... | collective-permute-start | bytes 24584 | tf_op jit(solution)/shard_map/ppermute | solution.py:97
  33.2 1.9 %collective-permute-start.5 = (f32[256]{0:T(256)S(1)}, f32[256]{0:T(256)S(1)}, u32[]{:S(2)}, u32[]{:S(2)}) collective-permute-start(f32[256]{0:T(256)S(1)} %dynamic-slice_subtract_fusion.5), channel_id=1, source_target_pairs={{0,1},{1,0},{2,3},{3,2},{4,5},{5,4},{6,7},{7,6},{8,9},{9,8},{10,11... | collective-permute-start | bytes 3080 | tf_op jit(solution)/shard_map/ppermute | solution.py:103
  37.4 1.9 %collective-permute-start.6 = (f32[256]{0:T(256)S(1)}, f32[256]{0:T(256)S(1)}, u32[]{:S(2)}, u32[]{:S(2)}) collective-permute-start(f32[256]{0:T(256)S(1)} %dynamic-slice_subtract_fusion.4), channel_id=1, source_target_pairs={{0,1},{1,0},{2,3},{3,2},{4,5},{5,4},{6,7},{7,6},{8,9},{9,8},{10,11... | collective-permute-start | bytes 3080 | tf_op jit(solution)/shard_map/ppermute | solution.py:103
  41.6 1.9 %collective-permute-start.7 = (f32[256]{0:T(256)S(1)}, f32[256]{0:T(256)S(1)}, u32[]{:S(2)}, u32[]{:S(2)}) collective-permute-start(f32[256]{0:T(256)S(1)} %dynamic-slice_subtract_fusion.3), channel_id=1, source_target_pairs={{0,1},{1,0},{2,3},{3,2},{4,5},{5,4},{6,7},{7,6},{8,9},{9,8},{10,11... | collective-permute-start | bytes 3080 | tf_op jit(solution)/shard_map/ppermute | solution.py:103
  46.2 1.9 %collective-permute-start.8 = (f32[512]{0:T(512)S(1)}, f32[512]{0:T(512)S(1)}, u32[]{:S(2)}, u32[]{:S(2)}) collective-permute-start(f32[512]{0:T(512)S(1)} %pad_maximum_fusion.4), channel_id=1, source_target_pairs={{0,1},{1,0},{2,3},{3,2},{4,5},{5,4},{6,7},{7,6},{8,9},{9,8},{10,11... | collective-permute-start | bytes 6152 | tf_op jit(solution)/shard_map/ppermute | solution.py:103
  50.3 1.9 %collective-permute-start.9 = (f32[512]{0:T(512)S(1)}, f32[512]{0:T(512)S(1)}, u32[]{:S(2)}, u32[]{:S(2)}) collective-permute-start(f32[512]{0:T(512)S(1)} %pad_maximum_fusion.5), channel_id=1, source_target_pairs={{0,1},{1,0},{2,3},{3,2},{4,5},{5,4},{6,7},{7,6},{8,9},{9,8},{10,11... | collective-permute-start | bytes 6152 | tf_op jit(solution)/shard_map/ppermute | solution.py:103
  54.3 1.9 %collective-permute-start.10 = (f32[1024]{0:T(1024)S(1)}, f32[1024]{0:T(1024)S(1)}, u32[]{:S(2)}, u32[]{:S(2)}) collective-permute-start(f32[1024]{0:T(1024)S(1)} %pad_maximum_fusion.2), channel_id=1, source_target_pairs={{0,1},{1,0},{2,3},{3,2},{4,5},{5,4},{6,7},{7,6},{8,9},{9,8},{10,11... | collective-permute-start | bytes 12296 | tf_op jit(solution)/shard_map/ppermute | solution.py:103
  62.0 3.0 %collective-permute-start.12 = (f32[8,1,512]{2,1,0:T(1,128)S(1)}, f32[8,1,512]{2,1,0:T(1,128)S(1)}, u32[]{:S(2)}, u32[]{:S(2)}) collective-permute-start(f32[8,1,512]{2,1,0:T(1,128)S(1)} %get-tuple-element.60), channel_id=1, source_target_pairs={{0,8},{8,16},{16,24},{24,2},{2,10},{10,18},{18,26},{26,4},{4,12},{... | collective-permute-start | bytes 49160 | tf_op jit(solution)/shard_map/ppermute | solution.py:48
  65.0 1.9 %collective-permute-start.13 = (f32[8,16,1]{2,1,0:T(8,128)S(1)}, f32[8,16,1]{2,1,0:T(8,128)S(1)}, u32[]{:S(2)}, u32[]{:S(2)}) collective-permute-start(f32[8,16,1]{2,1,0:T(8,128)S(1)} %slice_select_fusion.5), channel_id=1, source_target_pairs={{0,1},{1,0},{2,3},{3,2},{4,5},{5,4},{6,7},{7,6},{8,9},{9,8},{10,11... | collective-permute-start | bytes 1544 | tf_op jit(solution)/shard_map/ppermute | solution.py:45
  67.1 2.3 %collective-permute-done.13 = f32[8,16,1]{2,1,0:T(8,128)S(1)} collective-permute-done((f32[8,16,1]{2,1,0:T(8,128)S(1)}, f32[8,16,1]{2,1,0:T(8,128)S(1)}, u32[]{:S(2)}, u32[]{:S(2)}) %collective-permute-start.13) | collective-permute-done | bytes 544 | tf_op jit(solution)/shard_map/ppermute | solution.py:45
  70.3 1.9 %collective-permute-start.16 = (f32[8,16,1]{2,1,0:T(8,128)S(1)}, f32[8,16,1]{2,1,0:T(8,128)S(1)}, u32[]{:S(2)}, u32[]{:S(2)}) collective-permute-start(f32[8,16,1]{2,1,0:T(8,128)S(1)} %slice_select_fusion.4), channel_id=1, source_target_pairs={{0,1},{1,0},{2,3},{3,2},{4,5},{5,4},{6,7},{7,6},{8,9},{9,8},{10,11... | collective-permute-start | bytes 1544 | tf_op jit(solution)/shard_map/ppermute | solution.py:45
  73.5 3.0 %collective-permute-start.15 = (f32[8,1,512]{2,1,0:T(1,128)S(1)}, f32[8,1,512]{2,1,0:T(1,128)S(1)}, u32[]{:S(2)}, u32[]{:S(2)}) collective-permute-start(f32[8,1,512]{2,1,0:T(1,128)S(1)} %get-tuple-element.54), channel_id=1, source_target_pairs={{0,8},{8,16},{16,24},{24,2},{2,10},{10,18},{18,26},{26,4},{4,12},{... | collective-permute-start | bytes 49160 | tf_op jit(solution)/shard_map/ppermute | solution.py:48
  78.5 2.1 %collective-permute-start.18 = (f32[8,1,512]{2,1,0:T(1,128)S(1)}, f32[8,1,512]{2,1,0:T(1,128)S(1)}, u32[]{:S(2)}, u32[]{:S(2)}) collective-permute-start(f32[8,1,512]{2,1,0:T(1,128)S(1)} %get-tuple-element.45), channel_id=1, source_target_pairs={{0,8},{8,16},{16,24},{24,2},{2,10},{10,18},{18,26},{26,4},{4,12},{... | collective-permute-start | bytes 49160 | tf_op jit(solution)/shard_map/ppermute | solution.py:48
  82.7 2.7 %collective-permute-done.17 = f32[8,1,512]{2,1,0:T(1,128)S(1)} collective-permute-done((f32[8,1,512]{2,1,0:T(1,128)S(1)}, f32[8,1,512]{2,1,0:T(1,128)S(1)}, u32[]{:S(2)}, u32[]{:S(2)}) %collective-permute-start.17) | collective-permute-done | bytes 16416 | tf_op jit(solution)/shard_map/ppermute | solution.py:49
  86.3 2.1 %collective-permute-start.22 = (f32[8,16,1]{2,1,0:T(8,128)S(1)}, f32[8,16,1]{2,1,0:T(8,128)S(1)}, u32[]{:S(2)}, u32[]{:S(2)}) collective-permute-start(f32[8,16,1]{2,1,0:T(8,128)S(1)} %slice_select_fusion.2), channel_id=1, source_target_pairs={{0,1},{1,0},{2,3},{3,2},{4,5},{5,4},{6,7},{7,6},{8,9},{9,8},{10,11... | collective-permute-start | bytes 1544 | tf_op jit(solution)/shard_map/ppermute | solution.py:45
  89.7 4.9 %collective-permute-start.21 = (f32[8,1,512]{2,1,0:T(1,128)S(1)}, f32[8,1,512]{2,1,0:T(1,128)S(1)}, u32[]{:S(2)}, u32[]{:S(2)}) collective-permute-start(f32[8,1,512]{2,1,0:T(1,128)S(1)} %get-tuple-element.38), channel_id=1, source_target_pairs={{0,8},{8,16},{16,24},{24,2},{2,10},{10,18},{18,26},{26,4},{4,12},{... | collective-permute-start | bytes 49160 | tf_op jit(solution)/shard_map/ppermute | solution.py:48
  101.8 2.1 %collective-permute-start.23 = (f32[2048]{0:T(1024)S(1)}, f32[2048]{0:T(1024)S(1)}, u32[]{:S(2)}, u32[]{:S(2)}) collective-permute-start(f32[2048]{0:T(1024)S(1)} %bitcast.257), channel_id=1, source_target_pairs={{0,8},{8,0},{16,24},{24,16},{1,9},{9,1},{17,25},{25,17},{2,10},{10... | collective-permute-start | bytes 24584 | tf_op jit(solution)/shard_map/ppermute | solution.py:97
  105.7 3.0 %collective-permute-start.35 = (f32[8,1,512]{2,1,0:T(1,128)S(1)}, f32[8,1,512]{2,1,0:T(1,128)S(1)}, u32[]{:S(2)}, u32[]{:S(2)}) collective-permute-start(f32[8,1,512]{2,1,0:T(1,128)S(1)} %get-tuple-element.30), channel_id=1, source_target_pairs={{0,8},{8,16},{16,24},{24,2},{2,10},{10,18},{18,26},{26,4},{4,12},{... | collective-permute-start | bytes 49160 | tf_op jit(solution)/shard_map/ppermute | solution.py:48
  108.8 5.7 %collective-permute-start.24 = (f32[2048]{0:T(1024)S(1)}, f32[2048]{0:T(1024)S(1)}, u32[]{:S(2)}, u32[]{:S(2)}) collective-permute-start(f32[2048]{0:T(1024)S(1)} %add.426), channel_id=1, source_target_pairs={{0,16},{8,24},{16,0},{24,8},{1,17},{9,25},{17,1},{25,9},{2,18},{10... | collective-permute-start | bytes 24584 | tf_op jit(solution)/shard_map/ppermute | solution.py:97
  116.1 3.7 %collective-permute-start.25 = (f32[2048]{0:T(1024)S(1)}, f32[2048]{0:T(1024)S(1)}, u32[]{:S(2)}, u32[]{:S(2)}) collective-permute-start(f32[2048]{0:T(1024)S(1)} %add.427), channel_id=1, source_target_pairs={{0,2},{2,0},{4,6},{6,4},{1,3},{3,1},{5,7},{7,5},{8,10},{10,8},{12,... | collective-permute-start | bytes 24584 | tf_op jit(solution)/shard_map/ppermute | solution.py:97
  119.8 2.1 %fusion.157 = f32[8,16,512]{2,1,0:T(8,128)S(1)} fusion(f32[8,16,512]{2,1,0:T(8,128)S(1)} %mul.275, f32[8,16,512]{2,1,0:T(8,128)} %copy-done.5, f32[8,16,512]{2,1,0:T(8,128)} %copy-done.1, f32[8,16,511]{2,1,0:T(8,128)} %get-tuple-element.32, f32[8,16,1]{2,1,0:T(8,128)S(1)} %get-tuple-element.68, f32[8,16,512]{2,1,0:T(8,128)S(1)} %get-tuple-element.11, ...), kind=kLoop, calls=%fused_computation.215 | loop fusion | flops 1900544 | bytes 4161536 | tf_op jit(solution)/shard_map/add | solution.py:84
  123.6 2.7 %collective-permute-start.26 = (f32[2048]{0:T(1024)S(1)}, f32[2048]{0:T(1024)S(1)}, u32[]{:S(2)}, u32[]{:S(2)}) collective-permute-start(f32[2048]{0:T(1024)S(1)} %add.428), channel_id=1, source_target_pairs={{0,4},{2,6},{4,0},{6,2},{1,5},{3,7},{5,1},{7,3},{8,12},{10,14},{12... | collective-permute-start | bytes 24584 | tf_op jit(solution)/shard_map/ppermute | solution.py:97
  134.1 1.9 %collective-permute-start.38 = (f32[8,1,512]{2,1,0:T(1,128)}, f32[8,1,512]{2,1,0:T(1,128)}, u32[]{:S(2)}, u32[]{:S(2)}) collective-permute-start(f32[8,1,512]{2,1,0:T(1,128)} %get-tuple-element.21), channel_id=1, source_target_pairs={{0,8},{8,16},{16,24},{24,2},{2,10},{10,18},{18,26},{26,4},{4,12},{... | collective-permute-start | bytes 49160 | tf_op jit(solution)/shard_map/ppermute | solution.py:48
  157.0 2.3 %collective-permute-done.33 = f32[1024]{0:T(1024)S(1)} collective-permute-done((f32[1024]{0:T(1024)S(1)}, f32[1024]{0:T(1024)S(1)}, u32[]{:S(2)}, u32[]{:S(2)}) %collective-permute-start.33) | collective-permute-done | bytes 4128 | tf_op jit(solution)/shard_map/ppermute | solution.py:103
  160.7 3.7 %fusion.125 = f32[8,16,512]{2,1,0:T(8,128)} fusion(f32[8,16,512]{2,1,0:T(8,128)} %copy-done.5, f32[1,16,512]{2,1,0:T(8,128)S(1)} %multiply_bitcast_fusion.1, f32[8,16,512]{2,1,0:T(8,128)} %copy-done.2, f32[8,1,512]{2,1,0:T(1,128)} %collective-permute-done.37, f32[8,15,512]{2,1,0:T(8,128)} %get-tuple-element.24, f32[8,16,512]{2,1,0:T(8,128)S(1)} %get-tuple-element.10, ...), kind=kLoop, calls=%fused_computation.134 | loop fusion | flops 3997696 | bytes 5996544 | tf_op jit(solution)/shard_map/add | solution.py:249
  164.5 5.0 %all-to-all-start.1 = ((f32[8,16,512]{2,1,0:T(8,128)}), f32[8,16,512]{2,1,0:T(8,128)S(1)}, u32[]{:S(2)}, u32[]{:S(2)}) async-start(f32[8,16,512]{2,1,0:T(8,128)} %fusion.125), calls=%async_computation.1 | async-start | bytes 524288 | tf_op jit(solution)/shard_map/all_to_all | solution.py:261
  170.0 5.4 %all-to-all-done.1 = f32[8,16,512]{2,1,0:T(8,128)S(1)} async-done(((f32[8,16,512]{2,1,0:T(8,128)}), f32[8,16,512]{2,1,0:T(8,128)S(1)}, u32[]{:S(2)}, u32[]{:S(2)}) %all-to-all-start.1) | async-done | bytes 262176 | tf_op jit(solution)/shard_map/all_to_all | solution.py:261
  (252 shorter events, 81.8 us)
Async XLA Ops:
  4.3 55.7 %all-to-all-start = ((f32[3,2,64,512]{3,1,0,2:T(2,128)}), f32[3,2,64,512]{3,1,0,2:T(2,128)S(1)}, u32[]{:S(2)}, u32[]{:S(2)}) async-start(f32[3,2,64,512]{3,1,0,2:T(2,128)} %copy.22), calls=%async_computation | async-start | bytes 1572864 | tf_op jit(solution)/shard_map/all_to_all | solution.py:185
  11.5 8.8 %collective-permute-start.1 = (f32[2048]{0:T(1024)S(1)}, f32[2048]{0:T(1024)S(1)}, u32[]{:S(2)}, u32[]{:S(2)}) collective-permute-start(f32[2048]{0:T(1024)S(1)} %add.378), channel_id=1, source_target_pairs={{0,16},{8,24},{16,0},{24,8},{1,17},{9,25},{17,1},{25,9},{2,18},{10... | collective-permute-start | bytes 24584 | tf_op jit(solution)/shard_map/ppermute | solution.py:97
  20.4 3.9 %collective-permute-start.2 = (f32[2048]{0:T(1024)S(1)}, f32[2048]{0:T(1024)S(1)}, u32[]{:S(2)}, u32[]{:S(2)}) collective-permute-start(f32[2048]{0:T(1024)S(1)} %add.379), channel_id=1, source_target_pairs={{0,2},{2,0},{4,6},{6,4},{1,3},{3,1},{5,7},{7,5},{8,10},{10,8},{12,... | collective-permute-start | bytes 24584 | tf_op jit(solution)/shard_map/ppermute | solution.py:97
  24.3 4.7 %collective-permute-start.3 = (f32[2048]{0:T(1024)S(1)}, f32[2048]{0:T(1024)S(1)}, u32[]{:S(2)}, u32[]{:S(2)}) collective-permute-start(f32[2048]{0:T(1024)S(1)} %add.380), channel_id=1, source_target_pairs={{0,4},{2,6},{4,0},{6,2},{1,5},{3,7},{5,1},{7,3},{8,12},{10,14},{12... | collective-permute-start | bytes 24584 | tf_op jit(solution)/shard_map/ppermute | solution.py:97
  29.0 3.7 %collective-permute-start.4 = (f32[2048]{0:T(1024)S(1)}, f32[2048]{0:T(1024)S(1)}, u32[]{:S(2)}, u32[]{:S(2)}) collective-permute-start(f32[2048]{0:T(1024)S(1)} %add.381), channel_id=1, source_target_pairs={{0,1},{1,0},{2,3},{3,2},{4,5},{5,4},{6,7},{7,6},{8,9},{9,8},{10,11... | collective-permute-start | bytes 24584 | tf_op jit(solution)/shard_map/ppermute | solution.py:97
  54.3 3.7 %collective-permute-start.10 = (f32[1024]{0:T(1024)S(1)}, f32[1024]{0:T(1024)S(1)}, u32[]{:S(2)}, u32[]{:S(2)}) collective-permute-start(f32[1024]{0:T(1024)S(1)} %pad_maximum_fusion.2), channel_id=1, source_target_pairs={{0,1},{1,0},{2,3},{3,2},{4,5},{5,4},{6,7},{7,6},{8,9},{9,8},{10,11... | collective-permute-start | bytes 12296 | tf_op jit(solution)/shard_map/ppermute | solution.py:103
  60.7 8.7 %collective-permute-start.11 = (f32[8,1,512]{2,1,0:T(1,128)S(1)}, f32[8,1,512]{2,1,0:T(1,128)S(1)}, u32[]{:S(2)}, u32[]{:S(2)}) collective-permute-start(f32[8,1,512]{2,1,0:T(1,128)S(1)} %get-tuple-element.59), channel_id=1, source_target_pairs={{8,0},{16,8},{24,16},{2,24},{10,2},{18,10},{26,18},{4,26},{12,4},{... | collective-permute-start | bytes 49160 | tf_op jit(solution)/shard_map/ppermute | solution.py:49
  62.0 7.4 %collective-permute-start.12 = (f32[8,1,512]{2,1,0:T(1,128)S(1)}, f32[8,1,512]{2,1,0:T(1,128)S(1)}, u32[]{:S(2)}, u32[]{:S(2)}) collective-permute-start(f32[8,1,512]{2,1,0:T(1,128)S(1)} %get-tuple-element.60), channel_id=1, source_target_pairs={{0,8},{8,16},{16,24},{24,2},{2,10},{10,18},{18,26},{26,4},{4,12},{... | collective-permute-start | bytes 49160 | tf_op jit(solution)/shard_map/ppermute | solution.py:48
  65.0 4.3 %collective-permute-start.13 = (f32[8,16,1]{2,1,0:T(8,128)S(1)}, f32[8,16,1]{2,1,0:T(8,128)S(1)}, u32[]{:S(2)}, u32[]{:S(2)}) collective-permute-start(f32[8,16,1]{2,1,0:T(8,128)S(1)} %slice_select_fusion.5), channel_id=1, source_target_pairs={{0,1},{1,0},{2,3},{3,2},{4,5},{5,4},{6,7},{7,6},{8,9},{9,8},{10,11... | collective-permute-start | bytes 1544 | tf_op jit(solution)/shard_map/ppermute | solution.py:45
  70.3 6.3 %collective-permute-start.16 = (f32[8,16,1]{2,1,0:T(8,128)S(1)}, f32[8,16,1]{2,1,0:T(8,128)S(1)}, u32[]{:S(2)}, u32[]{:S(2)}) collective-permute-start(f32[8,16,1]{2,1,0:T(8,128)S(1)} %slice_select_fusion.4), channel_id=1, source_target_pairs={{0,1},{1,0},{2,3},{3,2},{4,5},{5,4},{6,7},{7,6},{8,9},{9,8},{10,11... | collective-permute-start | bytes 1544 | tf_op jit(solution)/shard_map/ppermute | solution.py:45
  72.2 4.4 %collective-permute-start.14 = (f32[8,1,512]{2,1,0:T(1,128)S(1)}, f32[8,1,512]{2,1,0:T(1,128)S(1)}, u32[]{:S(2)}, u32[]{:S(2)}) collective-permute-start(f32[8,1,512]{2,1,0:T(1,128)S(1)} %get-tuple-element.53), channel_id=1, source_target_pairs={{8,0},{16,8},{24,16},{2,24},{10,2},{18,10},{26,18},{4,26},{12,4},{... | collective-permute-start | bytes 49160 | tf_op jit(solution)/shard_map/ppermute | solution.py:49
  73.5 3.9 %collective-permute-start.15 = (f32[8,1,512]{2,1,0:T(1,128)S(1)}, f32[8,1,512]{2,1,0:T(1,128)S(1)}, u32[]{:S(2)}, u32[]{:S(2)}) collective-permute-start(f32[8,1,512]{2,1,0:T(1,128)S(1)} %get-tuple-element.54), channel_id=1, source_target_pairs={{0,8},{8,16},{16,24},{24,2},{2,10},{10,18},{18,26},{26,4},{4,12},{... | collective-permute-start | bytes 49160 | tf_op jit(solution)/shard_map/ppermute | solution.py:48
  78.2 4.4 %collective-permute-start.19 = (f32[8,16,1]{2,1,0:T(8,128)S(1)}, f32[8,16,1]{2,1,0:T(8,128)S(1)}, u32[]{:S(2)}, u32[]{:S(2)}) collective-permute-start(f32[8,16,1]{2,1,0:T(8,128)S(1)} %slice_select_fusion.3), channel_id=1, source_target_pairs={{0,1},{1,0},{2,3},{3,2},{4,5},{5,4},{6,7},{7,6},{8,9},{9,8},{10,11... | collective-permute-start | bytes 1544 | tf_op jit(solution)/shard_map/ppermute | solution.py:45
  78.5 4.2 %collective-permute-start.18 = (f32[8,1,512]{2,1,0:T(1,128)S(1)}, f32[8,1,512]{2,1,0:T(1,128)S(1)}, u32[]{:S(2)}, u32[]{:S(2)}) collective-permute-start(f32[8,1,512]{2,1,0:T(1,128)S(1)} %get-tuple-element.45), channel_id=1, source_target_pairs={{0,8},{8,16},{16,24},{24,2},{2,10},{10,18},{18,26},{26,4},{4,12},{... | collective-permute-start | bytes 49160 | tf_op jit(solution)/shard_map/ppermute | solution.py:48
  80.6 4.7 %collective-permute-start.17 = (f32[8,1,512]{2,1,0:T(1,128)S(1)}, f32[8,1,512]{2,1,0:T(1,128)S(1)}, u32[]{:S(2)}, u32[]{:S(2)}) collective-permute-start(f32[8,1,512]{2,1,0:T(1,128)S(1)} %get-tuple-element.46), channel_id=1, source_target_pairs={{8,0},{16,8},{24,16},{2,24},{10,2},{18,10},{26,18},{4,26},{12,4},{... | collective-permute-start | bytes 49160 | tf_op jit(solution)/shard_map/ppermute | solution.py:49
  86.3 8.3 %collective-permute-start.22 = (f32[8,16,1]{2,1,0:T(8,128)S(1)}, f32[8,16,1]{2,1,0:T(8,128)S(1)}, u32[]{:S(2)}, u32[]{:S(2)}) collective-permute-start(f32[8,16,1]{2,1,0:T(8,128)S(1)} %slice_select_fusion.2), channel_id=1, source_target_pairs={{0,1},{1,0},{2,3},{3,2},{4,5},{5,4},{6,7},{7,6},{8,9},{9,8},{10,11... | collective-permute-start | bytes 1544 | tf_op jit(solution)/shard_map/ppermute | solution.py:45
  88.4 6.3 %collective-permute-start.20 = (f32[8,1,512]{2,1,0:T(1,128)S(1)}, f32[8,1,512]{2,1,0:T(1,128)S(1)}, u32[]{:S(2)}, u32[]{:S(2)}) collective-permute-start(f32[8,1,512]{2,1,0:T(1,128)S(1)} %get-tuple-element.37), channel_id=1, source_target_pairs={{8,0},{16,8},{24,16},{2,24},{10,2},{18,10},{26,18},{4,26},{12,4},{... | collective-permute-start | bytes 49160 | tf_op jit(solution)/shard_map/ppermute | solution.py:49
  89.7 5.6 %collective-permute-start.21 = (f32[8,1,512]{2,1,0:T(1,128)S(1)}, f32[8,1,512]{2,1,0:T(1,128)S(1)}, u32[]{:S(2)}, u32[]{:S(2)}) collective-permute-start(f32[8,1,512]{2,1,0:T(1,128)S(1)} %get-tuple-element.38), channel_id=1, source_target_pairs={{0,8},{8,16},{16,24},{24,2},{2,10},{10,18},{18,26},{26,4},{4,12},{... | collective-permute-start | bytes 49160 | tf_op jit(solution)/shard_map/ppermute | solution.py:48
  101.8 7.0 %collective-permute-start.23 = (f32[2048]{0:T(1024)S(1)}, f32[2048]{0:T(1024)S(1)}, u32[]{:S(2)}, u32[]{:S(2)}) collective-permute-start(f32[2048]{0:T(1024)S(1)} %bitcast.257), channel_id=1, source_target_pairs={{0,8},{8,0},{16,24},{24,16},{1,9},{9,1},{17,25},{25,17},{2,10},{10... | collective-permute-start | bytes 24584 | tf_op jit(solution)/shard_map/ppermute | solution.py:97
  103.9 10.6 %collective-permute-start.36 = (f32[8,16,1]{2,1,0:T(8,128)S(1)}, f32[8,16,1]{2,1,0:T(8,128)S(1)}, u32[]{:S(2)}, u32[]{:S(2)}) collective-permute-start(f32[8,16,1]{2,1,0:T(8,128)S(1)} %slice_select_fusion.1), channel_id=1, source_target_pairs={{0,1},{1,0},{2,3},{3,2},{4,5},{5,4},{6,7},{7,6},{8,9},{9,8},{10,11... | collective-permute-start | bytes 1544 | tf_op jit(solution)/shard_map/ppermute | solution.py:45
  104.4 15.4 %collective-permute-start.34 = (f32[8,1,512]{2,1,0:T(1,128)S(1)}, f32[8,1,512]{2,1,0:T(1,128)S(1)}, u32[]{:S(2)}, u32[]{:S(2)}) collective-permute-start(f32[8,1,512]{2,1,0:T(1,128)S(1)} %get-tuple-element.29), channel_id=1, source_target_pairs={{8,0},{16,8},{24,16},{2,24},{10,2},{18,10},{26,18},{4,26},{12,4},{... | collective-permute-start | bytes 49160 | tf_op jit(solution)/shard_map/ppermute | solution.py:49
  105.7 14.1 %collective-permute-start.35 = (f32[8,1,512]{2,1,0:T(1,128)S(1)}, f32[8,1,512]{2,1,0:T(1,128)S(1)}, u32[]{:S(2)}, u32[]{:S(2)}) collective-permute-start(f32[8,1,512]{2,1,0:T(1,128)S(1)} %get-tuple-element.30), channel_id=1, source_target_pairs={{0,8},{8,16},{16,24},{24,2},{2,10},{10,18},{18,26},{26,4},{4,12},{... | collective-permute-start | bytes 49160 | tf_op jit(solution)/shard_map/ppermute | solution.py:48
  108.8 7.3 %collective-permute-start.24 = (f32[2048]{0:T(1024)S(1)}, f32[2048]{0:T(1024)S(1)}, u32[]{:S(2)}, u32[]{:S(2)}) collective-permute-start(f32[2048]{0:T(1024)S(1)} %add.426), channel_id=1, source_target_pairs={{0,16},{8,24},{16,0},{24,8},{1,17},{9,25},{17,1},{25,9},{2,18},{10... | collective-permute-start | bytes 24584 | tf_op jit(solution)/shard_map/ppermute | solution.py:97
  116.1 7.5 %collective-permute-start.25 = (f32[2048]{0:T(1024)S(1)}, f32[2048]{0:T(1024)S(1)}, u32[]{:S(2)}, u32[]{:S(2)}) collective-permute-start(f32[2048]{0:T(1024)S(1)} %add.427), channel_id=1, source_target_pairs={{0,2},{2,0},{4,6},{6,4},{1,3},{3,1},{5,7},{7,5},{8,10},{10,8},{12,... | collective-permute-start | bytes 24584 | tf_op jit(solution)/shard_map/ppermute | solution.py:97
  123.6 4.6 %collective-permute-start.26 = (f32[2048]{0:T(1024)S(1)}, f32[2048]{0:T(1024)S(1)}, u32[]{:S(2)}, u32[]{:S(2)}) collective-permute-start(f32[2048]{0:T(1024)S(1)} %add.428), channel_id=1, source_target_pairs={{0,4},{2,6},{4,0},{6,2},{1,5},{3,7},{5,1},{7,3},{8,12},{10,14},{12... | collective-permute-start | bytes 24584 | tf_op jit(solution)/shard_map/ppermute | solution.py:97
  132.5 5.4 %collective-permute-start.28 = (f32[256]{0:T(256)S(1)}, f32[256]{0:T(256)S(1)}, u32[]{:S(2)}, u32[]{:S(2)}) collective-permute-start(f32[256]{0:T(256)S(1)} %dynamic-slice_subtract_fusion.2), channel_id=1, source_target_pairs={{0,1},{1,0},{2,3},{3,2},{4,5},{5,4},{6,7},{7,6},{8,9},{9,8},{10,11... | collective-permute-start | bytes 3080 | tf_op jit(solution)/shard_map/ppermute | solution.py:103
  134.1 26.6 %collective-permute-start.38 = (f32[8,1,512]{2,1,0:T(1,128)}, f32[8,1,512]{2,1,0:T(1,128)}, u32[]{:S(2)}, u32[]{:S(2)}) collective-permute-start(f32[8,1,512]{2,1,0:T(1,128)} %get-tuple-element.21), channel_id=1, source_target_pairs={{0,8},{8,16},{16,24},{24,2},{2,10},{10,18},{18,26},{26,4},{4,12},{... | collective-permute-start | bytes 49160 | tf_op jit(solution)/shard_map/ppermute | solution.py:48
  136.0 24.7 %collective-permute-start.37 = (f32[8,1,512]{2,1,0:T(1,128)}, f32[8,1,512]{2,1,0:T(1,128)}, u32[]{:S(2)}, u32[]{:S(2)}) collective-permute-start(f32[8,1,512]{2,1,0:T(1,128)} %get-tuple-element.22), channel_id=1, source_target_pairs={{8,0},{16,8},{24,16},{2,24},{10,2},{18,10},{26,18},{4,26},{12,4},{... | collective-permute-start | bytes 49160 | tf_op jit(solution)/shard_map/ppermute | solution.py:49
  137.3 4.3 %collective-permute-start.39 = (f32[8,16,1]{2,1,0:T(8,128)S(1)}, f32[8,16,1]{2,1,0:T(8,128)S(1)}, u32[]{:S(2)}, u32[]{:S(2)}) collective-permute-start(f32[8,16,1]{2,1,0:T(8,128)S(1)} %slice_select_fusion), channel_id=1, source_target_pairs={{0,1},{1,0},{2,3},{3,2},{4,5},{5,4},{6,7},{7,6},{8,9},{9,8},{10,11... | collective-permute-start | bytes 1544 | tf_op jit(solution)/shard_map/ppermute | solution.py:45
  138.5 3.8 %collective-permute-start.29 = (f32[256]{0:T(256)S(1)}, f32[256]{0:T(256)S(1)}, u32[]{:S(2)}, u32[]{:S(2)}) collective-permute-start(f32[256]{0:T(256)S(1)} %dynamic-slice_subtract_fusion.1), channel_id=1, source_target_pairs={{0,1},{1,0},{2,3},{3,2},{4,5},{5,4},{6,7},{7,6},{8,9},{9,8},{10,11... | collective-permute-start | bytes 3080 | tf_op jit(solution)/shard_map/ppermute | solution.py:103
  155.7 3.7 %collective-permute-start.33 = (f32[1024]{0:T(1024)S(1)}, f32[1024]{0:T(1024)S(1)}, u32[]{:S(2)}, u32[]{:S(2)}) collective-permute-start(f32[1024]{0:T(1024)S(1)} %pad_maximum_fusion.3), channel_id=1, source_target_pairs={{0,1},{1,0},{2,3},{3,2},{4,5},{5,4},{6,7},{7,6},{8,9},{9,8},{10,11... | collective-permute-start | bytes 12296 | tf_op jit(solution)/shard_map/ppermute | solution.py:103
  164.5 11.0 %all-to-all-start.1 = ((f32[8,16,512]{2,1,0:T(8,128)}), f32[8,16,512]{2,1,0:T(8,128)S(1)}, u32[]{:S(2)}, u32[]{:S(2)}) async-start(f32[8,16,512]{2,1,0:T(8,128)} %fusion.125), calls=%async_computation.1 | async-start | bytes 524288 | tf_op jit(solution)/shard_map/all_to_all | solution.py:261
  (28 other events, 296.9 us)

commit v4 on v2

--- a/solution.py
+++ b/solution.py
@@ -137,6 +137,17 @@
     return jnp.stack(results)
 
 
+def coarse_full(rhs, pivots, coupling):
+    forward = [rhs[0]]
+    for section in range(1, NPANEL):
+        forward.append(rhs[section] - jnp.dot(coupling[section - 1], forward[-1], precision=highest))
+    scaled = [jnp.dot(pivots[section], forward[section], precision=highest) for section in range(NPANEL)]
+    results = [scaled[NPANEL - 1]]
+    for section in range(NPANEL - 2, -1, -1):
+        results.insert(0, scaled[section] - jnp.dot(results[0], coupling[section], precision=highest))
+    return jnp.stack(results)
+
+
 def coarse_general(rhs, pivots, coupling):
     share = pivots.shape[1]
     start = lax.axis_index("col") * share
@@ -215,6 +226,12 @@
     ring_ids = jnp.where(ring_ok, ring_rows[:, None] * tile_cols + ring_cols[None, :], -1).reshape(-1)
     scatter_ring = (ring_ids[:, None] == flat_tiles[None, :]).astype(jnp.float32)
     coarse = coarse_pair if col_count == 2 else coarse_general
+    if col_count == 2:
+        low = lax.axis_index("col") == 0
+        got = swap_col(jnp.concatenate([pivots, coupling]))
+        mine = jnp.concatenate([pivots, coupling])
+        whole = jnp.where(low, jnp.concatenate([mine, got], 1), jnp.concatenate([got, mine], 1))
+        whole_pivots, whole_coupling = whole[:NPANEL], whole[NPANEL:]
 
     drop = None
     drop_near = None
@@ -227,7 +244,10 @@
         tiles = plane.reshape(own_rows, TILE, own_cols, TILE).sum(axis=(1, 3)).reshape(-1)
         local_rhs = jnp.dot(gather_local, tiles, precision=highest)
         rhs = all_sum(local_rhs).reshape(NPANEL, PANEL) * (restrict_scale / TILE)
-        ports = coarse(rhs, pivots, coupling)
+        if col_count == 2 and outer > 0:
+            ports = coarse_full(rhs, whole_pivots, whole_coupling)
+        else:
+            ports = coarse(rhs, pivots, coupling)
         tile_values = jnp.dot(scatter_ring, ports.reshape(-1), precision=highest).reshape(own_rows + 2, own_cols + 2)
         ring = expand(expand(tile_values, True).T, True).T * prolong_scale
         centre = ring[1:-1, 1:-1]

time: 169 us -> 219 us (1.30)
  waiting for transfers between devices: 47.2 us -> 95 us
  starting transfers between devices: 71.8 us -> 62.1 us
  other arithmetic: 18.6 us -> 23.6 us
  matrix products: 12.4 us -> 15.9 us
  local copies, waits for them, and re-layouts: 16.9 us -> 20.2 us
    ppermute x6, waiting for transfers between devices: 5.38 us -> 66.7 us  [rims(): got = lax.ppermute(jnp.where(low, tail, head), axis, [(0, 1), (1, 0)])]
    dot_general x0 -> x10, matrix products: none -> 8.81 us  [the longest x4 3.99 us: coarse_full(): jnp.dot(pivots[section], forward[section], precision=highest)]
    ppermute x12 -> x7, starting transfers between devices: 12.8 us -> 5.41 us  [swap_col(): return lax.ppermute(value, 'col', [(0, 1), (1, 0)])]
    all_to_all x1, waiting for transfers between devices: 10.6 us -> 3.83 us  [shards(): lax.all_to_all(jnp.stack((sources, conduct, vertical)), 'layer', 2, 1, ti...]
    select_n x0 -> x1, other arithmetic: none -> 6.24 us  [shards(): jnp.where(low, jnp.concatenate([mine, got], 1), jnp.concatenate([got, min...]
    ppermute x12 -> x7, waiting for transfers between devices: 18.3 us -> 13.8 us  [swap_col(): return lax.ppermute(value, 'col', [(0, 1), (1, 0)])]
    ppermute x10, starting transfers between devices: 16.5 us -> 12.4 us  [all_sum(): lax.ppermute(value, axis, [(i, i ^ step) for i in range(count)])]
    unnamed x33 -> x50, local copies, waits for them, and re-layouts: 0.09 us -> 3.25 us
  transfers between devices with their start and end apart: 42 -> 37, of which waited for: 19 -> 11; matrix products, arithmetic and copies ran while one was open for 18% -> 24% of each run, Pallas kernels for 0% -> 0%
where the time goes in v4:
time: 219 us; the launch traced here: 218 us
  waiting for transfers between devices  95 us (43%)
  starting transfers between devices  62.1 us (28%)
  other arithmetic  23.6 us (11%)
  local copies, waits for them, and re-layouts  20.2 us (9%)
  matrix products  15.9 us (7%)
    ppermute x6, waiting for transfers between devices, rims(): got = lax.ppermute(jnp.where(low, tail, head), axis, [(0, 1), (1, 0)])  66.7 us
    ppermute x6, starting transfers between devices, rims(): lax.ppermute(tail, axis, [(place[i], place[i + 1]) for i in range(count -...  19.4 us
    ppermute x7, waiting for transfers between devices, swap_col(): return lax.ppermute(value, 'col', [(0, 1), (1, 0)])  13.8 us
    ppermute x10, starting transfers between devices, all_sum(): lax.ppermute(value, axis, [(i, i ^ step) for i in range(count)])  12.4 us
    ppermute x6, starting transfers between devices, rims(): got = lax.ppermute(jnp.where(low, tail, head), axis, [(0, 1), (1, 0)])  9.52 us
    ppermute x6, starting transfers between devices, rims(): lax.ppermute(head, axis, [(place[i + 1], place[i]) for i in range(count -...  7.69 us
    select_n x1, other arithmetic, shards(): jnp.where(low, jnp.concatenate([mine, got], 1), jnp.concatenate([got, min...  6.24 us
    ppermute x10, waiting for transfers between devices, all_sum(): lax.ppermute(value, axis, [(i, i ^ step) for i in range(count)])  6.01 us
  transfers between devices with their start and end apart: 37, of which 11 were waited for; matrix products, arithmetic and copies ran while one was open for 24% of the time, Pallas kernels for 0%

profile of v4, /device:TPU:0, one launch (start us, length us, event | category | flops | bytes accessed | tf_op | source)
XLA Modules:
  0.0 218.4 jit_solution(9206210129622076286)
XLA Ops:
  4.4 4.2 %all-to-all-start = ((f32[3,2,64,512]{3,1,0,2:T(2,128)}), f32[3,2,64,512]{3,1,0,2:T(2,128)S(1)}, u32[]{:S(2)}, u32[]{:S(2)}) async-start(f32[3,2,64,512]{3,1,0,2:T(2,128)} %copy.22), calls=%async_computation | async-start | bytes 1572864 | tf_op jit(solution)/shard_map/all_to_all | solution.py:184
  8.6 3.1 %constant_dynamic-update-slice_fusion.1 = f32[7,256,512]{2,1,0:T(8,128)} fusion(f32[4,256,512]{2,1,0:T(8,128)} %param.14), kind=kLoop, calls=%fused_computation.211 | loop fusion | bytes 4194304
  13.1 2.3 %collective-permute-start.20 = (f32[7,256,512]{2,1,0:T(8,128)}, f32[7,256,512]{2,1,0:T(8,128)}, u32[]{:S(2)}, u32[]{:S(2)}) collective-permute-start(f32[7,256,512]{2,1,0:T(8,128)} %constant_dynamic-update-slice_fusion), channel_id=1, source_target_pairs={{0,1},{1,0},{2,3},{3,2},{4,5},{5,4},{6,7},{7,6},{8,9},{9,8},{10,11... | collective-permute-start | bytes 11010056 | tf_op jit(solution)/shard_map/ppermute | solution.py:103
  16.4 3.8 %all-to-all-done = f32[3,2,64,512]{3,1,0,2:T(2,128)S(1)} async-done(((f32[3,2,64,512]{3,1,0,2:T(2,128)}), f32[3,2,64,512]{3,1,0,2:T(2,128)S(1)}, u32[]{:S(2)}, u32[]{:S(2)}) %all-to-all-start) | async-done | bytes 786464 | tf_op jit(solution)/shard_map/all_to_all | solution.py:184
  23.5 2.3 %collective-permute-start.13 = (f32[8,16,1]{2,1,0:T(8,128)S(1)}, f32[8,16,1]{2,1,0:T(8,128)S(1)}, u32[]{:S(2)}, u32[]{:S(2)}) collective-permute-start(f32[8,16,1]{2,1,0:T(8,128)S(1)} %slice_select_fusion.5), channel_id=1, source_target_pairs={{0,1},{1,0},{2,3},{3,2},{4,5},{5,4},{6,7},{7,6},{8,9},{9,8},{10,11... | collective-permute-start | bytes 1544 | tf_op jit(solution)/shard_map/ppermute | solution.py:45
  27.1 3.0 %collective-permute-start.12 = (f32[8,1,512]{2,1,0:T(1,128)S(1)}, f32[8,1,512]{2,1,0:T(1,128)S(1)}, u32[]{:S(2)}, u32[]{:S(2)}) collective-permute-start(f32[8,1,512]{2,1,0:T(1,128)S(1)} %get-tuple-element.61), channel_id=1, source_target_pairs={{0,8},{8,16},{16,24},{24,2},{2,10},{10,18},{18,26},{26,4},{4,12},{... | collective-permute-start | bytes 49160 | tf_op jit(solution)/shard_map/ppermute | solution.py:48
  30.3 66.7 %collective-permute-done.13 = f32[8,16,1]{2,1,0:T(8,128)S(1)} collective-permute-done((f32[8,16,1]{2,1,0:T(8,128)S(1)}, f32[8,16,1]{2,1,0:T(8,128)S(1)}, u32[]{:S(2)}, u32[]{:S(2)}) %collective-permute-start.13) | collective-permute-done | bytes 544 | tf_op jit(solution)/shard_map/ppermute | solution.py:45
  97.0 1.7 collective-permute-start.1
  98.7 1.8 bitcast_multiply_fusion
  100.9 1.8 collective-permute-start.16
  102.7 1.6 collective-permute-start.2
  105.6 3.0 %collective-permute-start.15 = (f32[8,1,512]{2,1,0:T(1,128)S(1)}, f32[8,1,512]{2,1,0:T(1,128)S(1)}, u32[]{:S(2)}, u32[]{:S(2)}) collective-permute-start(f32[8,1,512]{2,1,0:T(1,128)S(1)} %get-tuple-element.55), channel_id=1, source_target_pairs={{0,8},{8,16},{16,24},{24,2},{2,10},{10,18},{18,26},{26,4},{4,12},{... | collective-permute-start | bytes 49160 | tf_op jit(solution)/shard_map/ppermute | solution.py:48
  108.7 2.7 %collective-permute-start.3 = (f32[2048]{0:T(1024)S(1)}, f32[2048]{0:T(1024)S(1)}, u32[]{:S(2)}, u32[]{:S(2)}) collective-permute-start(f32[2048]{0:T(1024)S(1)} %add.325), channel_id=1, source_target_pairs={{0,4},{2,6},{4,0},{6,2},{1,5},{3,7},{5,1},{7,3},{8,12},{10,14},{12... | collective-permute-start | bytes 24584 | tf_op jit(solution)/shard_map/ppermute | solution.py:97
  116.8 3.0 %collective-permute-start.18 = (f32[8,1,512]{2,1,0:T(1,128)S(1)}, f32[8,1,512]{2,1,0:T(1,128)S(1)}, u32[]{:S(2)}, u32[]{:S(2)}) collective-permute-start(f32[8,1,512]{2,1,0:T(1,128)S(1)} %get-tuple-element.46), channel_id=1, source_target_pairs={{0,8},{8,16},{16,24},{24,2},{2,10},{10,18},{18,26},{26,4},{4,12},{... | collective-permute-start | bytes 49160 | tf_op jit(solution)/shard_map/ppermute | solution.py:48
  121.0 3.0 %collective-permute-done.5 = f32[256]{0:T(256)S(1)} collective-permute-done((f32[256]{0:T(256)S(1)}, f32[256]{0:T(256)S(1)}, u32[]{:S(2)}, u32[]{:S(2)}) %collective-permute-start.5) | collective-permute-done | bytes 1056 | tf_op jit(solution)/shard_map/ppermute | solution.py:103
  125.7 2.6 %collective-permute-done.6 = f32[256]{0:T(256)S(1)} collective-permute-done((f32[256]{0:T(256)S(1)}, f32[256]{0:T(256)S(1)}, u32[]{:S(2)}, u32[]{:S(2)}) %collective-permute-start.6) | collective-permute-done | bytes 1056 | tf_op jit(solution)/shard_map/ppermute | solution.py:103
  129.9 2.6 %collective-permute-done.7 = f32[256]{0:T(256)S(1)} collective-permute-done((f32[256]{0:T(256)S(1)}, f32[256]{0:T(256)S(1)}, u32[]{:S(2)}, u32[]{:S(2)}) %collective-permute-start.7) | collective-permute-done | bytes 1056 | tf_op jit(solution)/shard_map/ppermute | solution.py:103
  134.5 2.6 %collective-permute-done.8 = f32[512]{0:T(512)S(1)} collective-permute-done((f32[512]{0:T(512)S(1)}, f32[512]{0:T(512)S(1)}, u32[]{:S(2)}, u32[]{:S(2)}) %collective-permute-start.8) | collective-permute-done | bytes 2080 | tf_op jit(solution)/shard_map/ppermute | solution.py:103
  138.1 3.1 %collective-permute-done.9 = f32[512]{0:T(512)S(1)} collective-permute-done((f32[512]{0:T(512)S(1)}, f32[512]{0:T(512)S(1)}, u32[]{:S(2)}, u32[]{:S(2)}) %collective-permute-start.9) | collective-permute-done | bytes 2080 | tf_op jit(solution)/shard_map/ppermute | solution.py:103
  148.0 3.6 %collective-permute-start.22 = (f32[8,1,512]{2,1,0:T(1,128)}, f32[8,1,512]{2,1,0:T(1,128)}, u32[]{:S(2)}, u32[]{:S(2)}) collective-permute-start(f32[8,1,512]{2,1,0:T(1,128)} %get-tuple-element.39), channel_id=1, source_target_pairs={{0,8},{8,16},{16,24},{24,2},{2,10},{10,18},{18,26},{26,4},{4,12},{... | collective-permute-start | bytes 49160 | tf_op jit(solution)/shard_map/ppermute | solution.py:48
  159.9 3.0 %collective-permute-start.30 = (f32[8,1,512]{2,1,0:T(1,128)S(1)}, f32[8,1,512]{2,1,0:T(1,128)S(1)}, u32[]{:S(2)}, u32[]{:S(2)}) collective-permute-start(f32[8,1,512]{2,1,0:T(1,128)S(1)} %get-tuple-element.31), channel_id=1, source_target_pairs={{0,8},{8,16},{16,24},{24,2},{2,10},{10,18},{18,26},{26,4},{4,12},{... | collective-permute-start | bytes 49160 | tf_op jit(solution)/shard_map/ppermute | solution.py:48
  164.4 2.3 %collective-permute-done.25 = f32[2048]{0:T(1024)S(1)} collective-permute-done((f32[2048]{0:T(1024)S(1)}, f32[2048]{0:T(1024)S(1)}, u32[]{:S(2)}, u32[]{:S(2)}) %collective-permute-start.25) | collective-permute-done | bytes 8224 | tf_op jit(solution)/shard_map/ppermute | solution.py:97
  166.7 1.8 collective-permute-start.26
  171.7 1.7 collective-permute-start.34
  173.4 2.2 %collective-permute-start.27 = (f32[2048]{0:T(1024)S(1)}, f32[2048]{0:T(1024)S(1)}, u32[]{:S(2)}, u32[]{:S(2)}) collective-permute-start(f32[2048]{0:T(1024)S(1)} %add.371), channel_id=1, source_target_pairs={{0,4},{2,6},{4,0},{6,2},{1,5},{3,7},{5,1},{7,3},{8,12},{10,14},{12... | collective-permute-start | bytes 24584 | tf_op jit(solution)/shard_map/ppermute | solution.py:97
  177.5 3.6 %collective-permute-start.33 = (f32[8,1,512]{2,1,0:T(1,128)}, f32[8,1,512]{2,1,0:T(1,128)}, u32[]{:S(2)}, u32[]{:S(2)}) collective-permute-start(f32[8,1,512]{2,1,0:T(1,128)} %get-tuple-element.22), channel_id=1, source_target_pairs={{0,8},{8,16},{16,24},{24,2},{2,10},{10,18},{18,26},{26,4},{4,12},{... | collective-permute-start | bytes 49160 | tf_op jit(solution)/shard_map/ppermute | solution.py:48
  182.3 2.5 %collective-permute-done.28 = f32[2048]{0:T(1024)S(1)} collective-permute-done((f32[2048]{0:T(1024)S(1)}, f32[2048]{0:T(1024)S(1)}, u32[]{:S(2)}, u32[]{:S(2)}) %collective-permute-start.28) | collective-permute-done | bytes 8224 | tf_op jit(solution)/shard_map/ppermute | solution.py:97
  184.8 6.2 %maximum_select_fusion = f32[7,512,512]{2,1,0:T(8,128)S(1)} fusion(f32[7,256,512]{2,1,0:T(8,128)} %collective-permute-done.20, f32[7,256,512]{2,1,0:T(8,128)} %constant_dynamic-update-slice_fusion, pred[]{:T(512)S(6)} %eq.20), kind=kLoop, calls=%fused_computation | loop fusion | flops 5505024 | bytes 14680065 | tf_op jit(solution)/shard_map/jit(_where)/select_n | solution.py:233
  202.3 1.7 reshape.314
  205.0 3.3 %fusion.105 = f32[8,16,512]{2,1,0:T(8,128)} fusion(f32[8,16,512]{2,1,0:T(8,128)S(1)} %get-tuple-element.3, f32[1,16,512]{2,1,0:T(8,128)S(1)} %multiply_bitcast_fusion.1, f32[8,16,512]{2,1,0:T(8,128)S(1)} %copy-done.2, f32[8,1,512]{2,1,0:T(1,128)} %collective-permute-done.32, f32[8,15,512]{2,1,0:T(8,128)} %get-tuple-element.25, ...), kind=kLoop, calls=%fused_computation.122 | loop fusion | flops 3997696 | bytes 5996544 | tf_op jit(solution)/shard_map/add | solution.py:257
  208.3 3.4 %all-to-all-start.1 = ((f32[8,16,512]{2,1,0:T(8,128)}), f32[8,16,512]{2,1,0:T(8,128)S(1)}, u32[]{:S(2)}, u32[]{:S(2)}) async-start(f32[8,16,512]{2,1,0:T(8,128)} %fusion.105), calls=%async_computation.1 | async-start | bytes 524288 | tf_op jit(solution)/shard_map/all_to_all | solution.py:269
  213.0 4.7 %all-to-all-done.1 = f32[8,16,512]{2,1,0:T(8,128)S(1)} async-done(((f32[8,16,512]{2,1,0:T(8,128)}), f32[8,16,512]{2,1,0:T(8,128)S(1)}, u32[]{:S(2)}, u32[]{:S(2)}) %all-to-all-start.1) | async-done | bytes 262176 | tf_op jit(solution)/shard_map/all_to_all | solution.py:269
  (238 shorter events, 61.9 us)
Async XLA Ops:
  4.4 15.9 %all-to-all-start = ((f32[3,2,64,512]{3,1,0,2:T(2,128)}), f32[3,2,64,512]{3,1,0,2:T(2,128)S(1)}, u32[]{:S(2)}, u32[]{:S(2)}) async-start(f32[3,2,64,512]{3,1,0,2:T(2,128)} %copy.22), calls=%async_computation | async-start | bytes 1572864 | tf_op jit(solution)/shard_map/all_to_all | solution.py:184
  13.1 171.7 %collective-permute-start.20 = (f32[7,256,512]{2,1,0:T(8,128)}, f32[7,256,512]{2,1,0:T(8,128)}, u32[]{:S(2)}, u32[]{:S(2)}) collective-permute-start(f32[7,256,512]{2,1,0:T(8,128)} %constant_dynamic-update-slice_fusion), channel_id=1, source_target_pairs={{0,1},{1,0},{2,3},{3,2},{4,5},{5,4},{6,7},{7,6},{8,9},{9,8},{10,11... | collective-permute-start | bytes 11010056 | tf_op jit(solution)/shard_map/ppermute | solution.py:103
  23.4 73.6 %collective-permute-start = (f32[2048]{0:T(1024)S(1)}, f32[2048]{0:T(1024)S(1)}, u32[]{:S(2)}, u32[]{:S(2)}) collective-permute-start(f32[2048]{0:T(1024)S(1)} %bitcast.262), channel_id=1, source_target_pairs={{0,8},{8,0},{16,24},{24,16},{1,9},{9,1},{17,25},{25,17},{2,10},{10... | collective-permute-start | bytes 24584 | tf_op jit(solution)/shard_map/ppermute | solution.py:97
  23.5 73.4 %collective-permute-start.13 = (f32[8,16,1]{2,1,0:T(8,128)S(1)}, f32[8,16,1]{2,1,0:T(8,128)S(1)}, u32[]{:S(2)}, u32[]{:S(2)}) collective-permute-start(f32[8,16,1]{2,1,0:T(8,128)S(1)} %slice_select_fusion.5), channel_id=1, source_target_pairs={{0,1},{1,0},{2,3},{3,2},{4,5},{5,4},{6,7},{7,6},{8,9},{9,8},{10,11... | collective-permute-start | bytes 1544 | tf_op jit(solution)/shard_map/ppermute | solution.py:45
  25.8 72.9 %collective-permute-start.11 = (f32[8,1,512]{2,1,0:T(1,128)S(1)}, f32[8,1,512]{2,1,0:T(1,128)S(1)}, u32[]{:S(2)}, u32[]{:S(2)}) collective-permute-start(f32[8,1,512]{2,1,0:T(1,128)S(1)} %get-tuple-element.60), channel_id=1, source_target_pairs={{8,0},{16,8},{24,16},{2,24},{10,2},{18,10},{26,18},{4,26},{12,4},{... | collective-permute-start | bytes 49160 | tf_op jit(solution)/shard_map/ppermute | solution.py:49
  27.1 71.6 %collective-permute-start.12 = (f32[8,1,512]{2,1,0:T(1,128)S(1)}, f32[8,1,512]{2,1,0:T(1,128)S(1)}, u32[]{:S(2)}, u32[]{:S(2)}) collective-permute-start(f32[8,1,512]{2,1,0:T(1,128)S(1)} %get-tuple-element.61), channel_id=1, source_target_pairs={{0,8},{8,16},{16,24},{24,2},{2,10},{10,18},{18,26},{26,4},{4,12},{... | collective-permute-start | bytes 49160 | tf_op jit(solution)/shard_map/ppermute | solution.py:48
  97.0 5.7 %collective-permute-start.1 = (f32[2048]{0:T(1024)S(1)}, f32[2048]{0:T(1024)S(1)}, u32[]{:S(2)}, u32[]{:S(2)}) collective-permute-start(f32[2048]{0:T(1024)S(1)} %add.323), channel_id=1, source_target_pairs={{0,16},{8,24},{16,0},{24,8},{1,17},{9,25},{17,1},{25,9},{2,18},{10... | collective-permute-start | bytes 24584 | tf_op jit(solution)/shard_map/ppermute | solution.py:97
  100.9 7.8 %collective-permute-start.16 = (f32[8,16,1]{2,1,0:T(8,128)S(1)}, f32[8,16,1]{2,1,0:T(8,128)S(1)}, u32[]{:S(2)}, u32[]{:S(2)}) collective-permute-start(f32[8,16,1]{2,1,0:T(8,128)S(1)} %slice_select_fusion.4), channel_id=1, source_target_pairs={{0,1},{1,0},{2,3},{3,2},{4,5},{5,4},{6,7},{7,6},{8,9},{9,8},{10,11... | collective-permute-start | bytes 1544 | tf_op jit(solution)/shard_map/ppermute | solution.py:45
  102.7 6.0 %collective-permute-start.2 = (f32[2048]{0:T(1024)S(1)}, f32[2048]{0:T(1024)S(1)}, u32[]{:S(2)}, u32[]{:S(2)}) collective-permute-start(f32[2048]{0:T(1024)S(1)} %add.324), channel_id=1, source_target_pairs={{0,2},{2,0},{4,6},{6,4},{1,3},{3,1},{5,7},{7,5},{8,10},{10,8},{12,... | collective-permute-start | bytes 24584 | tf_op jit(solution)/shard_map/ppermute | solution.py:97
  104.4 7.0 %collective-permute-start.14 = (f32[8,1,512]{2,1,0:T(1,128)S(1)}, f32[8,1,512]{2,1,0:T(1,128)S(1)}, u32[]{:S(2)}, u32[]{:S(2)}) collective-permute-start(f32[8,1,512]{2,1,0:T(1,128)S(1)} %get-tuple-element.54), channel_id=1, source_target_pairs={{8,0},{16,8},{24,16},{2,24},{10,2},{18,10},{26,18},{4,26},{12,4},{... | collective-permute-start | bytes 49160 | tf_op jit(solution)/shard_map/ppermute | solution.py:49
  105.6 5.8 %collective-permute-start.15 = (f32[8,1,512]{2,1,0:T(1,128)S(1)}, f32[8,1,512]{2,1,0:T(1,128)S(1)}, u32[]{:S(2)}, u32[]{:S(2)}) collective-permute-start(f32[8,1,512]{2,1,0:T(1,128)S(1)} %get-tuple-element.55), channel_id=1, source_target_pairs={{0,8},{8,16},{16,24},{24,2},{2,10},{10,18},{18,26},{26,4},{4,12},{... | collective-permute-start | bytes 49160 | tf_op jit(solution)/shard_map/ppermute | solution.py:48
  108.7 4.6 %collective-permute-start.3 = (f32[2048]{0:T(1024)S(1)}, f32[2048]{0:T(1024)S(1)}, u32[]{:S(2)}, u32[]{:S(2)}) collective-permute-start(f32[2048]{0:T(1024)S(1)} %add.325), channel_id=1, source_target_pairs={{0,4},{2,6},{4,0},{6,2},{1,5},{3,7},{5,1},{7,3},{8,12},{10,14},{12... | collective-permute-start | bytes 24584 | tf_op jit(solution)/shard_map/ppermute | solution.py:97
  113.4 6.5 %collective-permute-start.4 = (f32[2048]{0:T(1024)S(1)}, f32[2048]{0:T(1024)S(1)}, u32[]{:S(2)}, u32[]{:S(2)}) collective-permute-start(f32[2048]{0:T(1024)S(1)} %add.326), channel_id=1, source_target_pairs={{0,1},{1,0},{2,3},{3,2},{4,5},{5,4},{6,7},{7,6},{8,9},{9,8},{10,11... | collective-permute-start | bytes 24584 | tf_op jit(solution)/shard_map/ppermute | solution.py:97
  114.0 7.1 %collective-permute-start.19 = (f32[8,16,1]{2,1,0:T(8,128)S(1)}, f32[8,16,1]{2,1,0:T(8,128)S(1)}, u32[]{:S(2)}, u32[]{:S(2)}) collective-permute-start(f32[8,16,1]{2,1,0:T(8,128)S(1)} %slice_select_fusion.3), channel_id=1, source_target_pairs={{0,1},{1,0},{2,3},{3,2},{4,5},{5,4},{6,7},{7,6},{8,9},{9,8},{10,11... | collective-permute-start | bytes 1544 | tf_op jit(solution)/shard_map/ppermute | solution.py:45
  115.5 26.6 %collective-permute-start.17 = (f32[8,1,512]{2,1,0:T(1,128)S(1)}, f32[8,1,512]{2,1,0:T(1,128)S(1)}, u32[]{:S(2)}, u32[]{:S(2)}) collective-permute-start(f32[8,1,512]{2,1,0:T(1,128)S(1)} %get-tuple-element.47), channel_id=1, source_target_pairs={{8,0},{16,8},{24,16},{2,24},{10,2},{18,10},{26,18},{4,26},{12,4},{... | collective-permute-start | bytes 49160 | tf_op jit(solution)/shard_map/ppermute | solution.py:49
  116.8 25.4 %collective-permute-start.18 = (f32[8,1,512]{2,1,0:T(1,128)S(1)}, f32[8,1,512]{2,1,0:T(1,128)S(1)}, u32[]{:S(2)}, u32[]{:S(2)}) collective-permute-start(f32[8,1,512]{2,1,0:T(1,128)S(1)} %get-tuple-element.46), channel_id=1, source_target_pairs={{0,8},{8,16},{16,24},{24,2},{2,10},{10,18},{18,26},{26,4},{4,12},{... | collective-permute-start | bytes 49160 | tf_op jit(solution)/shard_map/ppermute | solution.py:48
  141.6 10.7 %collective-permute-start.10 = (f32[1024]{0:T(1024)S(1)}, f32[1024]{0:T(1024)S(1)}, u32[]{:S(2)}, u32[]{:S(2)}) collective-permute-start(f32[1024]{0:T(1024)S(1)} %pad_maximum_fusion.2), channel_id=1, source_target_pairs={{0,1},{1,0},{2,3},{3,2},{4,5},{5,4},{6,7},{7,6},{8,9},{9,8},{10,11... | collective-permute-start | bytes 12296 | tf_op jit(solution)/shard_map/ppermute | solution.py:103
  144.5 7.1 %collective-permute-start.23 = (f32[8,16,1]{2,1,0:T(8,128)S(1)}, f32[8,16,1]{2,1,0:T(8,128)S(1)}, u32[]{:S(2)}, u32[]{:S(2)}) collective-permute-start(f32[8,16,1]{2,1,0:T(8,128)S(1)} %slice_select_fusion.2), channel_id=1, source_target_pairs={{0,1},{1,0},{2,3},{3,2},{4,5},{5,4},{6,7},{7,6},{8,9},{9,8},{10,11... | collective-permute-start | bytes 1544 | tf_op jit(solution)/shard_map/ppermute | solution.py:45
  146.8 8.3 %collective-permute-start.21 = (f32[8,1,512]{2,1,0:T(1,128)}, f32[8,1,512]{2,1,0:T(1,128)}, u32[]{:S(2)}, u32[]{:S(2)}) collective-permute-start(f32[8,1,512]{2,1,0:T(1,128)} %get-tuple-element.38), channel_id=1, source_target_pairs={{8,0},{16,8},{24,16},{2,24},{10,2},{18,10},{26,18},{4,26},{12,4},{... | collective-permute-start | bytes 49160 | tf_op jit(solution)/shard_map/ppermute | solution.py:49
  148.0 7.0 %collective-permute-start.22 = (f32[8,1,512]{2,1,0:T(1,128)}, f32[8,1,512]{2,1,0:T(1,128)}, u32[]{:S(2)}, u32[]{:S(2)}) collective-permute-start(f32[8,1,512]{2,1,0:T(1,128)} %get-tuple-element.39), channel_id=1, source_target_pairs={{0,8},{8,16},{16,24},{24,2},{2,10},{10,18},{18,26},{26,4},{4,12},{... | collective-permute-start | bytes 49160 | tf_op jit(solution)/shard_map/ppermute | solution.py:48
  157.5 5.4 %collective-permute-start.24 = (f32[2048]{0:T(1024)S(1)}, f32[2048]{0:T(1024)S(1)}, u32[]{:S(2)}, u32[]{:S(2)}) collective-permute-start(f32[2048]{0:T(1024)S(1)} %bitcast.264), channel_id=1, source_target_pairs={{0,8},{8,0},{16,24},{24,16},{1,9},{9,1},{17,25},{25,17},{2,10},{10... | collective-permute-start | bytes 24584 | tf_op jit(solution)/shard_map/ppermute | solution.py:97
  157.7 6.6 %collective-permute-start.31 = (f32[8,16,1]{2,1,0:T(8,128)S(1)}, f32[8,16,1]{2,1,0:T(8,128)S(1)}, u32[]{:S(2)}, u32[]{:S(2)}) collective-permute-start(f32[8,16,1]{2,1,0:T(8,128)S(1)} %slice_select_fusion.1), channel_id=1, source_target_pairs={{0,1},{1,0},{2,3},{3,2},{4,5},{5,4},{6,7},{7,6},{8,9},{9,8},{10,11... | collective-permute-start | bytes 1544 | tf_op jit(solution)/shard_map/ppermute | solution.py:45
  158.6 9.9 %collective-permute-start.29 = (f32[8,1,512]{2,1,0:T(1,128)S(1)}, f32[8,1,512]{2,1,0:T(1,128)S(1)}, u32[]{:S(2)}, u32[]{:S(2)}) collective-permute-start(f32[8,1,512]{2,1,0:T(1,128)S(1)} %get-tuple-element.30), channel_id=1, source_target_pairs={{8,0},{16,8},{24,16},{2,24},{10,2},{18,10},{26,18},{4,26},{12,4},{... | collective-permute-start | bytes 49160 | tf_op jit(solution)/shard_map/ppermute | solution.py:49
  159.9 8.6 %collective-permute-start.30 = (f32[8,1,512]{2,1,0:T(1,128)S(1)}, f32[8,1,512]{2,1,0:T(1,128)S(1)}, u32[]{:S(2)}, u32[]{:S(2)}) collective-permute-start(f32[8,1,512]{2,1,0:T(1,128)S(1)} %get-tuple-element.31), channel_id=1, source_target_pairs={{0,8},{8,16},{16,24},{24,2},{2,10},{10,18},{18,26},{26,4},{4,12},{... | collective-permute-start | bytes 49160 | tf_op jit(solution)/shard_map/ppermute | solution.py:48
  163.0 3.7 %collective-permute-start.25 = (f32[2048]{0:T(1024)S(1)}, f32[2048]{0:T(1024)S(1)}, u32[]{:S(2)}, u32[]{:S(2)}) collective-permute-start(f32[2048]{0:T(1024)S(1)} %add.369), channel_id=1, source_target_pairs={{0,16},{8,24},{16,0},{24,8},{1,17},{9,25},{17,1},{25,9},{2,18},{10... | collective-permute-start | bytes 24584 | tf_op jit(solution)/shard_map/ppermute | solution.py:97
  166.7 6.6 %collective-permute-start.26 = (f32[2048]{0:T(1024)S(1)}, f32[2048]{0:T(1024)S(1)}, u32[]{:S(2)}, u32[]{:S(2)}) collective-permute-start(f32[2048]{0:T(1024)S(1)} %add.370), channel_id=1, source_target_pairs={{0,2},{2,0},{4,6},{6,4},{1,3},{3,1},{5,7},{7,5},{8,10},{10,8},{12,... | collective-permute-start | bytes 24584 | tf_op jit(solution)/shard_map/ppermute | solution.py:97
  171.7 9.9 %collective-permute-start.34 = (f32[8,16,1]{2,1,0:T(8,128)S(1)}, f32[8,16,1]{2,1,0:T(8,128)S(1)}, u32[]{:S(2)}, u32[]{:S(2)}) collective-permute-start(f32[8,16,1]{2,1,0:T(8,128)S(1)} %slice_select_fusion), channel_id=1, source_target_pairs={{0,1},{1,0},{2,3},{3,2},{4,5},{5,4},{6,7},{7,6},{8,9},{9,8},{10,11... | collective-permute-start | bytes 1544 | tf_op jit(solution)/shard_map/ppermute | solution.py:45
  173.4 7.8 %collective-permute-start.27 = (f32[2048]{0:T(1024)S(1)}, f32[2048]{0:T(1024)S(1)}, u32[]{:S(2)}, u32[]{:S(2)}) collective-permute-start(f32[2048]{0:T(1024)S(1)} %add.371), channel_id=1, source_target_pairs={{0,4},{2,6},{4,0},{6,2},{1,5},{3,7},{5,1},{7,3},{8,12},{10,14},{12... | collective-permute-start | bytes 24584 | tf_op jit(solution)/shard_map/ppermute | solution.py:97
  176.2 28.8 %collective-permute-start.32 = (f32[8,1,512]{2,1,0:T(1,128)}, f32[8,1,512]{2,1,0:T(1,128)}, u32[]{:S(2)}, u32[]{:S(2)}) collective-permute-start(f32[8,1,512]{2,1,0:T(1,128)} %get-tuple-element.23), channel_id=1, source_target_pairs={{8,0},{16,8},{24,16},{2,24},{10,2},{18,10},{26,18},{4,26},{12,4},{... | collective-permute-start | bytes 49160 | tf_op jit(solution)/shard_map/ppermute | solution.py:49
  177.5 27.5 %collective-permute-start.33 = (f32[8,1,512]{2,1,0:T(1,128)}, f32[8,1,512]{2,1,0:T(1,128)}, u32[]{:S(2)}, u32[]{:S(2)}) collective-permute-start(f32[8,1,512]{2,1,0:T(1,128)} %get-tuple-element.22), channel_id=1, source_target_pairs={{0,8},{8,16},{16,24},{24,2},{2,10},{10,18},{18,26},{26,4},{4,12},{... | collective-permute-start | bytes 49160 | tf_op jit(solution)/shard_map/ppermute | solution.py:48
  181.1 3.7 %collective-permute-start.28 = (f32[2048]{0:T(1024)S(1)}, f32[2048]{0:T(1024)S(1)}, u32[]{:S(2)}, u32[]{:S(2)}) collective-permute-start(f32[2048]{0:T(1024)S(1)} %add.372), channel_id=1, source_target_pairs={{0,1},{1,0},{2,3},{3,2},{4,5},{5,4},{6,7},{7,6},{8,9},{9,8},{10,11... | collective-permute-start | bytes 24584 | tf_op jit(solution)/shard_map/ppermute | solution.py:97
  208.3 9.4 %all-to-all-start.1 = ((f32[8,16,512]{2,1,0:T(8,128)}), f32[8,16,512]{2,1,0:T(8,128)S(1)}, u32[]{:S(2)}, u32[]{:S(2)}) async-start(f32[8,16,512]{2,1,0:T(8,128)} %fusion.105), calls=%async_computation.1 | async-start | bytes 524288 | tf_op jit(solution)/shard_map/all_to_all | solution.py:269
  (28 other events, 698.8 us)

commit v5 on v2

--- a/solution.py
+++ b/solution.py
@@ -1,4 +1,5 @@
 import jax
+import numpy as np
 import jax.numpy as jnp
 from jax import lax
 from jax.sharding import PartitionSpec as P
@@ -97,6 +98,24 @@
             value = value + lax.ppermute(value, axis, [(i, i ^ step) for i in range(count)])
             step *= 2
     return value
+
+
+def share_tiles(tiles, own_rows, own_cols):
+    layers, rows, cols = (lax.axis_size(axis) for axis, _ in GRID_AXES)
+    count = layers * rows * cols
+    payload = jnp.broadcast_to(tiles.reshape(1, -1), (count, tiles.size))
+    got = lax.all_to_all(payload, ("layer", "row", "col"), 0, 0, tiled=True).reshape(-1)
+    tile_cols = cols * own_cols
+    where = np.zeros(count * tiles.size, np.int32)
+    for l in range(layers):
+        for r in range(rows):
+            for c in range(cols):
+                d = (l * rows + r) * cols + c
+                for jr in range(own_rows):
+                    for jc in range(own_cols):
+                        tile = ((r * layers + l) * own_rows + jr) * tile_cols + c * own_cols + jc
+                        where[tile] = d * tiles.size + jr * own_cols + jc
+    return got, where
 
 
 def swap_col(value):
@@ -204,11 +223,6 @@
     first_row = (lax.axis_index("row") * layer_count + lax.axis_index("layer")) * own_rows
     first_col = lax.axis_index("col") * own_cols
     flat_tiles = port_tile.reshape(-1)
-    local_ids = (
-        (first_row + jnp.arange(own_rows, dtype=jnp.int32))[:, None] * tile_cols
-        + (first_col + jnp.arange(own_cols, dtype=jnp.int32))[None, :]
-    ).reshape(-1)
-    gather_local = (flat_tiles[:, None] == local_ids[None, :]).astype(jnp.float32)
     ring_rows = first_row - 1 + jnp.arange(own_rows + 2, dtype=jnp.int32)
     ring_cols = first_col - 1 + jnp.arange(own_cols + 2, dtype=jnp.int32)
     ring_ok = ((ring_rows >= 0) & (ring_rows < tile_rows))[:, None] & ((ring_cols >= 0) & (ring_cols < tile_cols))[None, :]
@@ -225,8 +239,8 @@
             resid = sources - apply_grid(drop, drop_near, weights, pad_term)
         plane = jnp.sum(resid, axis=0)
         tiles = plane.reshape(own_rows, TILE, own_cols, TILE).sum(axis=(1, 3)).reshape(-1)
-        local_rhs = jnp.dot(gather_local, tiles, precision=highest)
-        rhs = all_sum(local_rhs).reshape(NPANEL, PANEL) * (restrict_scale / TILE)
+        got, where = share_tiles(tiles, own_rows, own_cols)
+        rhs = got[jnp.asarray(where)[flat_tiles]].reshape(NPANEL, PANEL) * (restrict_scale / TILE)
         ports = coarse(rhs, pivots, coupling)
         tile_values = jnp.dot(scatter_ring, ports.reshape(-1), precision=highest).reshape(own_rows + 2, own_cols + 2)
         ring = expand(expand(tile_values, True).T, True).T * prolong_scale

time: 169 us -> 191 us (1.13)
  local copies, waits for them, and re-layouts: 16.9 us -> 52.5 us
  waiting for transfers between devices: 47.2 us -> 39.2 us
  starting transfers between devices: 71.8 us -> 64.5 us
    gather x0 -> x3, local copies, waits for them, and re-layouts: none -> 25.7 us  [the longest x2 17.2 us: shards(): got[jnp.asarray(where)[flat_tiles]].reshape(NPANEL, PANEL)]
    ppermute x10 -> x0, starting transfers between devices: 16.5 us -> none  [all_sum(): lax.ppermute(value, axis, [(i, i ^ step) for i in range(count)])]
    all_to_all x0 -> x2, starting transfers between devices: none -> 15.3 us  [share_tiles(): lax.all_to_all(payload, ('layer', 'row', 'col'), 0, 0, tiled=True)]
    all_to_all x1, waiting for transfers between devices: 10.6 us -> 1.36 us  [shards(): lax.all_to_all(jnp.stack((sources, conduct, vertical)), 'layer', 2, 1, ti...]
    ppermute x10 -> x0, waiting for transfers between devices: 7.49 us -> none  [all_sum(): lax.ppermute(value, axis, [(i, i ^ step) for i in range(count)])]
    ppermute x12, starting transfers between devices: 12.8 us -> 5.72 us  [swap_col(): return lax.ppermute(value, 'col', [(0, 1), (1, 0)])]
    all_to_all x0 -> x2, waiting for transfers between devices: none -> 6.49 us  [share_tiles(): lax.all_to_all(payload, ('layer', 'row', 'col'), 0, 0, tiled=True)]
    ppermute x6, waiting for transfers between devices: 5.38 us -> 2.63 us  [rims(): got = lax.ppermute(jnp.where(low, tail, head), axis, [(0, 1), (1, 0)])]
  transfers between devices with their start and end apart: 42 -> 34, of which waited for: 19 -> 16; matrix products, arithmetic and copies ran while one was open for 18% -> 29% of each run, Pallas kernels for 0% -> 0%
where the time goes in v5:
time: 191 us; the launch traced here: 190 us
  starting transfers between devices  64.5 us (34%)
  local copies, waits for them, and re-layouts  52.5 us (27%)
  waiting for transfers between devices  39.2 us (21%)
  other arithmetic  19.3 us (10%)
  matrix products  12.4 us (6%)
    ppermute x12, waiting for transfers between devices, swap_col(): return lax.ppermute(value, 'col', [(0, 1), (1, 0)])  21 us
    ppermute x6, starting transfers between devices, rims(): lax.ppermute(tail, axis, [(place[i], place[i + 1]) for i in range(count -...  18.9 us
    gather x2, local copies, waits for them, and re-layouts, shards(): got[jnp.asarray(where)[flat_tiles]].reshape(NPANEL, PANEL)  17.2 us
    all_to_all x2, starting transfers between devices, share_tiles(): lax.all_to_all(payload, ('layer', 'row', 'col'), 0, 0, tiled=True)  15.3 us
    gather x1, local copies, waits for them, and re-layouts, shards(): jnp.asarray(where)[flat_tiles]  8.58 us
    ppermute x6, starting transfers between devices, rims(): got = lax.ppermute(jnp.where(low, tail, head), axis, [(0, 1), (1, 0)])  8.29 us
    ppermute x6, starting transfers between devices, rims(): lax.ppermute(head, axis, [(place[i + 1], place[i]) for i in range(count -...  7.72 us
    slice x12, local copies, waits for them, and re-layouts, neighbours(): lax.slice_in_dim(field, 1, size, axis=dim)  7.02 us
  transfers between devices with their start and end apart: 34, of which 16 were waited for; matrix products, arithmetic and copies ran while one was open for 29% of the time, Pallas kernels for 0%

profile of v5, /device:TPU:0, one launch (start us, length us, event | category | flops | bytes accessed | tf_op | source)
XLA Modules:
  0.0 189.6 jit_solution(3381086809889548956)
XLA Ops:
  4.3 4.2 %all-to-all-start = ((f32[3,2,64,512]{3,1,0,2:T(2,128)}), f32[3,2,64,512]{3,1,0,2:T(2,128)S(1)}, u32[]{:S(2)}, u32[]{:S(2)}) async-start(f32[3,2,64,512]{3,1,0,2:T(2,128)} %copy.24), calls=%async_computation | async-start | bytes 1572864 | tf_op jit(solution)/shard_map/all_to_all | solution.py:192
  9.4 8.6 %gather_fusion = s32[2048]{0:T(1024)S(1)} fusion(s32[1024]{0:T(1024)S(1)} %copy-done, s32[2048]{0:T(1024)S(1)} %broadcast_clamp_fusion), kind=kCustom, calls=%fused_computation | custom fusion | bytes 24576 | tf_op jit(solution)/shard_map/gather | solution.py:243
  23.2 5.7 %all-to-all-start.1 = ((f32[32,1,32]{2,1,0:T(1,128)}), f32[32,1,32]{2,1,0:T(1,128)S(1)}, u32[]{:S(2)}, u32[]{:S(2)}) async-start(f32[32,1,32]{2,1,0:T(1,128)} %broadcast_in_dim.27), calls=%async_computation.1 | async-start | bytes 32768 | tf_op jit(solution)/shard_map/all_to_all | solution.py:107
  31.0 3.0 %collective-permute-start.7 = (f32[8,1,512]{2,1,0:T(1,128)S(1)}, f32[8,1,512]{2,1,0:T(1,128)S(1)}, u32[]{:S(2)}, u32[]{:S(2)}) collective-permute-start(f32[8,1,512]{2,1,0:T(1,128)S(1)} %get-tuple-element.61), channel_id=1, source_target_pairs={{0,8},{8,16},{16,24},{24,2},{2,10},{10,18},{18,26},{26,4},{4,12},{... | collective-permute-start | bytes 49160 | tf_op jit(solution)/shard_map/ppermute | solution.py:49
  35.0 1.8 collective-permute-start.8
  38.3 8.6 %gather_fusion.1 = f32[2048]{0:T(1024)S(1)} fusion(f32[1024]{0:T(1024)S(1)} %reshape.541, s32[2048]{0:T(1024)S(1)} %broadcast_clamp_fusion.1), kind=kCustom, calls=%fused_computation.1 | custom fusion | bytes 24576 | tf_op jit(solution)/shard_map/gather | solution.py:243
  47.8 3.3 %collective-permute-done = f32[256]{0:T(256)S(1)} collective-permute-done((f32[256]{0:T(256)S(1)}, f32[256]{0:T(256)S(1)}, u32[]{:S(2)}, u32[]{:S(2)}) %collective-permute-start) | collective-permute-done | bytes 1056 | tf_op jit(solution)/shard_map/ppermute | solution.py:122
  52.0 1.5 fusion.40
  53.5 1.8 collective-permute-done.1
  56.8 2.8 %collective-permute-done.2 = f32[256]{0:T(256)S(1)} collective-permute-done((f32[256]{0:T(256)S(1)}, f32[256]{0:T(256)S(1)}, u32[]{:S(2)}, u32[]{:S(2)}) %collective-permute-start.2) | collective-permute-done | bytes 1056 | tf_op jit(solution)/shard_map/ppermute | solution.py:122
  61.3 2.8 %collective-permute-done.3 = f32[512]{0:T(512)S(1)} collective-permute-done((f32[512]{0:T(512)S(1)}, f32[512]{0:T(512)S(1)}, u32[]{:S(2)}, u32[]{:S(2)}) %collective-permute-start.3) | collective-permute-done | bytes 2080 | tf_op jit(solution)/shard_map/ppermute | solution.py:122
  65.0 3.3 %collective-permute-done.4 = f32[512]{0:T(512)S(1)} collective-permute-done((f32[512]{0:T(512)S(1)}, f32[512]{0:T(512)S(1)}, u32[]{:S(2)}, u32[]{:S(2)}) %collective-permute-start.4) | collective-permute-done | bytes 2080 | tf_op jit(solution)/shard_map/ppermute | solution.py:122
  69.7 2.0 %bitcast_multiply_fusion = (f32[8,16,512]{2,1,0:T(8,128)S(1)}, f32[8,16,512]{2,1,0:T(8,128)S(1)}, f32[8,16,512]{2,1,0:T(8,128)S(1)}, f32[8,16,512]{2,1,0:T(8,128...) fusion(f32[1,4,2,16,512]{4,3,2,1,0:T(8,128)S(1)} %copy-done.12,, ...), kind=kLoop, calls=%fused_computation.182 | loop fusion | flops 1179648 | bytes 4423680 | tf_op jit(solution)/shard_map/mul | solution.py:79
  74.4 1.8 collective-permute-start.11
  78.1 3.6 %collective-permute-start.10 = (f32[8,1,512]{2,1,0:T(1,128)}, f32[8,1,512]{2,1,0:T(1,128)}, u32[]{:S(2)}, u32[]{:S(2)}) collective-permute-start(f32[8,1,512]{2,1,0:T(1,128)} %get-tuple-element.55), channel_id=1, source_target_pairs={{0,8},{8,16},{16,24},{24,2},{2,10},{10,18},{18,26},{26,4},{4,12},{... | collective-permute-start | bytes 49160 | tf_op jit(solution)/shard_map/ppermute | solution.py:49
  84.7 1.7 reshape.545
  87.5 2.0 %fusion.146 = (f32[8,16,512]{2,1,0:T(8,128)S(1)}, f32[8,16,512]{2,1,0:T(8,128)S(1)}) fusion(f32[8,16,512]{2,1,0:T(8,128)S(1)} %get-tuple-element.7, f32[1,4,2,16,512]{4,3,2,1,0:T(8,128)} %copy.27, f32[8,16,512]{2,1,0:T(8,128)S(1)} %get-tuple-element.12, f32[8,16,511]{2,1,0:T(8,128)} %get-tuple-element.57, f32[8,16,1]{2,1,0:T(8,128)} %get-tuple-element.75, ...), kind=kLoop, calls=%fused_computation.186 | loop fusion | flops 1966080 | bytes 4161536 | tf_op jit(solution)/shard_map/add | solution.py:85
  90.2 2.4 %collective-permute-start.13 = (f32[8,1,512]{2,1,0:T(1,128)S(1)}, f32[8,1,512]{2,1,0:T(1,128)S(1)}, u32[]{:S(2)}, u32[]{:S(2)}) collective-permute-start(f32[8,1,512]{2,1,0:T(1,128)S(1)} %get-tuple-element.46), channel_id=1, source_target_pairs={{0,8},{8,16},{16,24},{24,2},{2,10},{10,18},{18,26},{26,4},{4,12},{... | collective-permute-start | bytes 49160 | tf_op jit(solution)/shard_map/ppermute | solution.py:49
  94.4 1.6 collective-permute-done.12
  99.7 4.7 %collective-permute-start.16 = (f32[8,1,512]{2,1,0:T(1,128)S(1)}, f32[8,1,512]{2,1,0:T(1,128)S(1)}, u32[]{:S(2)}, u32[]{:S(2)}) collective-permute-start(f32[8,1,512]{2,1,0:T(1,128)S(1)} %get-tuple-element.39), channel_id=1, source_target_pairs={{0,8},{8,16},{16,24},{24,2},{2,10},{10,18},{18,26},{26,4},{4,12},{... | collective-permute-start | bytes 49160 | tf_op jit(solution)/shard_map/ppermute | solution.py:49
  109.1 9.5 %all-to-all-start.2 = ((f32[32,1,32]{2,1,0:T(1,128)}), f32[32,1,32]{2,1,0:T(1,128)S(1)}, u32[]{:S(2)}, u32[]{:S(2)}) async-start(f32[32,1,32]{2,1,0:T(1,128)} %broadcast_in_dim.35), calls=%async_computation.2 | async-start | bytes 32768 | tf_op jit(solution)/shard_map/all_to_all | solution.py:107
  119.3 6.5 %all-to-all-done.2 = f32[32,1,32]{2,1,0:T(1,128)S(1)} async-done(((f32[32,1,32]{2,1,0:T(1,128)}), f32[32,1,32]{2,1,0:T(1,128)S(1)}, u32[]{:S(2)}, u32[]{:S(2)}) %all-to-all-start.2) | async-done | bytes 4128 | tf_op jit(solution)/shard_map/all_to_all | solution.py:107
  126.6 8.6 %gather_fusion.2 = f32[2048]{0:T(1024)S(1)} fusion(f32[1024]{0:T(1024)S(1)} %reshape.546, s32[2048]{0:T(1024)S(1)} %broadcast_clamp_fusion.1), kind=kCustom, calls=%fused_computation.2 | custom fusion | bytes 24576 | tf_op jit(solution)/shard_map/gather | solution.py:243
  137.8 3.0 %collective-permute-start.25 = (f32[8,1,512]{2,1,0:T(1,128)}, f32[8,1,512]{2,1,0:T(1,128)S(1)}, u32[]{:S(2)}, u32[]{:S(2)}) collective-permute-start(f32[8,1,512]{2,1,0:T(1,128)} %get-tuple-element.31), channel_id=1, source_target_pairs={{0,8},{8,16},{16,24},{24,2},{2,10},{10,18},{18,26},{26,4},{4,12},{... | collective-permute-start | bytes 49160 | tf_op jit(solution)/shard_map/ppermute | solution.py:49
  143.6 2.1 %collective-permute-done.26 = f32[8,16,1]{2,1,0:T(8,128)S(1)} collective-permute-done((f32[8,16,1]{2,1,0:T(8,128)S(1)}, f32[8,16,1]{2,1,0:T(8,128)S(1)}, u32[]{:S(2)}, u32[]{:S(2)}) %collective-permute-start.26) | collective-permute-done | bytes 544 | tf_op jit(solution)/shard_map/ppermute | solution.py:46
  153.0 2.4 %collective-permute-done.21 = f32[512]{0:T(512)S(1)} collective-permute-done((f32[512]{0:T(512)S(1)}, f32[512]{0:T(512)S(1)}, u32[]{:S(2)}, u32[]{:S(2)}) %collective-permute-start.21) | collective-permute-done | bytes 2080 | tf_op jit(solution)/shard_map/ppermute | solution.py:122
  157.1 2.4 %collective-permute-done.22 = f32[512]{0:T(512)S(1)} collective-permute-done((f32[512]{0:T(512)S(1)}, f32[512]{0:T(512)S(1)}, u32[]{:S(2)}, u32[]{:S(2)}) %collective-permute-start.22) | collective-permute-done | bytes 2080 | tf_op jit(solution)/shard_map/ppermute | solution.py:122
  166.1 2.0 %collective-permute-start.28 = (f32[8,1,512]{2,1,0:T(1,128)}, f32[8,1,512]{2,1,0:T(1,128)}, u32[]{:S(2)}, u32[]{:S(2)}) collective-permute-start(f32[8,1,512]{2,1,0:T(1,128)} %get-tuple-element.22), channel_id=1, source_target_pairs={{0,8},{8,16},{16,24},{24,2},{2,10},{10,18},{18,26},{26,4},{4,12},{... | collective-permute-start | bytes 49160 | tf_op jit(solution)/shard_map/ppermute | solution.py:49
  172.4 1.7 reshape.549
  175.3 3.3 %fusion.117 = f32[8,16,512]{2,1,0:T(8,128)} fusion(f32[8,16,512]{2,1,0:T(8,128)S(1)} %copy-done.16, f32[1,16,512]{2,1,0:T(8,128)S(1)} %multiply_bitcast_fusion.1, f32[8,16,512]{2,1,0:T(8,128)S(1)} %copy-done.9, f32[8,1,512]{2,1,0:T(1,128)} %collective-permute-done.27, f32[8,15,512]{2,1,0:T(8,128)} %get-tuple-element.25, ...), kind=kLoop, calls=%fused_computation.129 | loop fusion | flops 3997696 | bytes 5996544 | tf_op jit(solution)/shard_map/add | solution.py:251
  178.5 4.4 %all-to-all-start.3 = ((f32[8,16,512]{2,1,0:T(8,128)}), f32[8,16,512]{2,1,0:T(8,128)S(1)}, u32[]{:S(2)}, u32[]{:S(2)}) async-start(f32[8,16,512]{2,1,0:T(8,128)} %fusion.117), calls=%async_computation.3 | async-start | bytes 524288 | tf_op jit(solution)/shard_map/all_to_all | solution.py:263
  183.5 5.4 %all-to-all-done.3 = f32[8,16,512]{2,1,0:T(8,128)S(1)} async-done(((f32[8,16,512]{2,1,0:T(8,128)}), f32[8,16,512]{2,1,0:T(8,128)S(1)}, u32[]{:S(2)}, u32[]{:S(2)}) %all-to-all-start.3) | async-done | bytes 262176 | tf_op jit(solution)/shard_map/all_to_all | solution.py:263
  (298 shorter events, 69.0 us)
Async XLA Ops:
  4.3 15.9 %all-to-all-start = ((f32[3,2,64,512]{3,1,0,2:T(2,128)}), f32[3,2,64,512]{3,1,0,2:T(2,128)S(1)}, u32[]{:S(2)}, u32[]{:S(2)}) async-start(f32[3,2,64,512]{3,1,0,2:T(2,128)} %copy.24), calls=%async_computation | async-start | bytes 1572864 | tf_op jit(solution)/shard_map/all_to_all | solution.py:192
  23.2 13.7 %all-to-all-start.1 = ((f32[32,1,32]{2,1,0:T(1,128)}), f32[32,1,32]{2,1,0:T(1,128)S(1)}, u32[]{:S(2)}, u32[]{:S(2)}) async-start(f32[32,1,32]{2,1,0:T(1,128)} %broadcast_in_dim.27), calls=%async_computation.1 | async-start | bytes 32768 | tf_op jit(solution)/shard_map/all_to_all | solution.py:107
  29.7 39.4 %collective-permute-start.6 = (f32[8,1,512]{2,1,0:T(1,128)S(1)}, f32[8,1,512]{2,1,0:T(1,128)S(1)}, u32[]{:S(2)}, u32[]{:S(2)}) collective-permute-start(f32[8,1,512]{2,1,0:T(1,128)S(1)} %get-tuple-element.60), channel_id=1, source_target_pairs={{8,0},{16,8},{24,16},{2,24},{10,2},{18,10},{26,18},{4,26},{12,4},{... | collective-permute-start | bytes 49160 | tf_op jit(solution)/shard_map/ppermute | solution.py:50
  31.0 38.1 %collective-permute-start.7 = (f32[8,1,512]{2,1,0:T(1,128)S(1)}, f32[8,1,512]{2,1,0:T(1,128)S(1)}, u32[]{:S(2)}, u32[]{:S(2)}) collective-permute-start(f32[8,1,512]{2,1,0:T(1,128)S(1)} %get-tuple-element.61), channel_id=1, source_target_pairs={{0,8},{8,16},{16,24},{24,2},{2,10},{10,18},{18,26},{26,4},{4,12},{... | collective-permute-start | bytes 49160 | tf_op jit(solution)/shard_map/ppermute | solution.py:49
  35.0 12.8 %collective-permute-start.8 = (f32[8,16,1]{2,1,0:T(8,128)S(1)}, f32[8,16,1]{2,1,0:T(8,128)S(1)}, u32[]{:S(2)}, u32[]{:S(2)}) collective-permute-start(f32[8,16,1]{2,1,0:T(8,128)S(1)} %slice_select_fusion.5), channel_id=1, source_target_pairs={{0,1},{1,0},{2,3},{3,2},{4,5},{5,4},{6,7},{7,6},{8,9},{9,8},{10,11... | collective-permute-start | bytes 1544 | tf_op jit(solution)/shard_map/ppermute | solution.py:46
  47.5 3.6 %collective-permute-start = (f32[256]{0:T(256)S(1)}, f32[256]{0:T(256)S(1)}, u32[]{:S(2)}, u32[]{:S(2)}) collective-permute-start(f32[256]{0:T(256)S(1)} %dynamic-slice_subtract_fusion.5), channel_id=1, source_target_pairs={{0,1},{1,0},{2,3},{3,2},{4,5},{5,4},{6,7},{7,6},{8,9},{9,8},{10,11... | collective-permute-start | bytes 3080 | tf_op jit(solution)/shard_map/ppermute | solution.py:122
  51.7 3.6 %collective-permute-start.1 = (f32[256]{0:T(256)S(1)}, f32[256]{0:T(256)S(1)}, u32[]{:S(2)}, u32[]{:S(2)}) collective-permute-start(f32[256]{0:T(256)S(1)} %dynamic-slice_subtract_fusion.4), channel_id=1, source_target_pairs={{0,1},{1,0},{2,3},{3,2},{4,5},{5,4},{6,7},{7,6},{8,9},{9,8},{10,11... | collective-permute-start | bytes 3080 | tf_op jit(solution)/shard_map/ppermute | solution.py:122
  56.0 3.6 %collective-permute-start.2 = (f32[256]{0:T(256)S(1)}, f32[256]{0:T(256)S(1)}, u32[]{:S(2)}, u32[]{:S(2)}) collective-permute-start(f32[256]{0:T(256)S(1)} %dynamic-slice_subtract_fusion.3), channel_id=1, source_target_pairs={{0,1},{1,0},{2,3},{3,2},{4,5},{5,4},{6,7},{7,6},{8,9},{9,8},{10,11... | collective-permute-start | bytes 3080 | tf_op jit(solution)/shard_map/ppermute | solution.py:122
  60.6 3.6 %collective-permute-start.3 = (f32[512]{0:T(512)S(1)}, f32[512]{0:T(512)S(1)}, u32[]{:S(2)}, u32[]{:S(2)}) collective-permute-start(f32[512]{0:T(512)S(1)} %pad_maximum_fusion.4), channel_id=1, source_target_pairs={{0,1},{1,0},{2,3},{3,2},{4,5},{5,4},{6,7},{7,6},{8,9},{9,8},{10,11... | collective-permute-start | bytes 6152 | tf_op jit(solution)/shard_map/ppermute | solution.py:122
  64.7 3.6 %collective-permute-start.4 = (f32[512]{0:T(512)S(1)}, f32[512]{0:T(512)S(1)}, u32[]{:S(2)}, u32[]{:S(2)}) collective-permute-start(f32[512]{0:T(512)S(1)} %pad_maximum_fusion.5), channel_id=1, source_target_pairs={{0,1},{1,0},{2,3},{3,2},{4,5},{5,4},{6,7},{7,6},{8,9},{9,8},{10,11... | collective-permute-start | bytes 6152 | tf_op jit(solution)/shard_map/ppermute | solution.py:122
  68.7 13.6 %collective-permute-start.5 = (f32[1024]{0:T(1024)S(1)}, f32[1024]{0:T(1024)S(1)}, u32[]{:S(2)}, u32[]{:S(2)}) collective-permute-start(f32[1024]{0:T(1024)S(1)} %pad_maximum_fusion.2), channel_id=1, source_target_pairs={{0,1},{1,0},{2,3},{3,2},{4,5},{5,4},{6,7},{7,6},{8,9},{9,8},{10,11... | collective-permute-start | bytes 12296 | tf_op jit(solution)/shard_map/ppermute | solution.py:122
  74.4 7.3 %collective-permute-start.11 = (f32[8,16,1]{2,1,0:T(8,128)S(1)}, f32[8,16,1]{2,1,0:T(8,128)S(1)}, u32[]{:S(2)}, u32[]{:S(2)}) collective-permute-start(f32[8,16,1]{2,1,0:T(8,128)S(1)} %slice_select_fusion.4), channel_id=1, source_target_pairs={{0,1},{1,0},{2,3},{3,2},{4,5},{5,4},{6,7},{7,6},{8,9},{9,8},{10,11... | collective-permute-start | bytes 1544 | tf_op jit(solution)/shard_map/ppermute | solution.py:46
  76.8 10.6 %collective-permute-start.9 = (f32[8,1,512]{2,1,0:T(1,128)}, f32[8,1,512]{2,1,0:T(1,128)}, u32[]{:S(2)}, u32[]{:S(2)}) collective-permute-start(f32[8,1,512]{2,1,0:T(1,128)} %get-tuple-element.54), channel_id=1, source_target_pairs={{8,0},{16,8},{24,16},{2,24},{10,2},{18,10},{26,18},{4,26},{12,4},{... | collective-permute-start | bytes 49160 | tf_op jit(solution)/shard_map/ppermute | solution.py:50
  78.1 9.4 %collective-permute-start.10 = (f32[8,1,512]{2,1,0:T(1,128)}, f32[8,1,512]{2,1,0:T(1,128)}, u32[]{:S(2)}, u32[]{:S(2)}) collective-permute-start(f32[8,1,512]{2,1,0:T(1,128)} %get-tuple-element.55), channel_id=1, source_target_pairs={{0,8},{8,16},{16,24},{24,2},{2,10},{10,18},{18,26},{26,4},{4,12},{... | collective-permute-start | bytes 49160 | tf_op jit(solution)/shard_map/ppermute | solution.py:49
  89.8 4.6 %collective-permute-start.14 = (f32[8,16,1]{2,1,0:T(8,128)S(1)}, f32[8,16,1]{2,1,0:T(8,128)S(1)}, u32[]{:S(2)}, u32[]{:S(2)}) collective-permute-start(f32[8,16,1]{2,1,0:T(8,128)S(1)} %slice_select_fusion.3), channel_id=1, source_target_pairs={{0,1},{1,0},{2,3},{3,2},{4,5},{5,4},{6,7},{7,6},{8,9},{9,8},{10,11... | collective-permute-start | bytes 1544 | tf_op jit(solution)/shard_map/ppermute | solution.py:46
  90.2 4.2 %collective-permute-start.13 = (f32[8,1,512]{2,1,0:T(1,128)S(1)}, f32[8,1,512]{2,1,0:T(1,128)S(1)}, u32[]{:S(2)}, u32[]{:S(2)}) collective-permute-start(f32[8,1,512]{2,1,0:T(1,128)S(1)} %get-tuple-element.46), channel_id=1, source_target_pairs={{0,8},{8,16},{16,24},{24,2},{2,10},{10,18},{18,26},{26,4},{4,12},{... | collective-permute-start | bytes 49160 | tf_op jit(solution)/shard_map/ppermute | solution.py:49
  96.8 7.6 %collective-permute-start.17 = (f32[8,16,1]{2,1,0:T(8,128)S(1)}, f32[8,16,1]{2,1,0:T(8,128)S(1)}, u32[]{:S(2)}, u32[]{:S(2)}) collective-permute-start(f32[8,16,1]{2,1,0:T(8,128)S(1)} %slice_select_fusion.2), channel_id=1, source_target_pairs={{0,1},{1,0},{2,3},{3,2},{4,5},{5,4},{6,7},{7,6},{8,9},{9,8},{10,11... | collective-permute-start | bytes 1544 | tf_op jit(solution)/shard_map/ppermute | solution.py:46
  98.4 6.1 %collective-permute-start.15 = (f32[8,1,512]{2,1,0:T(1,128)S(1)}, f32[8,1,512]{2,1,0:T(1,128)S(1)}, u32[]{:S(2)}, u32[]{:S(2)}) collective-permute-start(f32[8,1,512]{2,1,0:T(1,128)S(1)} %get-tuple-element.38), channel_id=1, source_target_pairs={{8,0},{16,8},{24,16},{2,24},{10,2},{18,10},{26,18},{4,26},{12,4},{... | collective-permute-start | bytes 49160 | tf_op jit(solution)/shard_map/ppermute | solution.py:50
  99.7 5.6 %collective-permute-start.16 = (f32[8,1,512]{2,1,0:T(1,128)S(1)}, f32[8,1,512]{2,1,0:T(1,128)S(1)}, u32[]{:S(2)}, u32[]{:S(2)}) collective-permute-start(f32[8,1,512]{2,1,0:T(1,128)S(1)} %get-tuple-element.39), channel_id=1, source_target_pairs={{0,8},{8,16},{16,24},{24,2},{2,10},{10,18},{18,26},{26,4},{4,12},{... | collective-permute-start | bytes 49160 | tf_op jit(solution)/shard_map/ppermute | solution.py:49
  109.1 16.7 %all-to-all-start.2 = ((f32[32,1,32]{2,1,0:T(1,128)}), f32[32,1,32]{2,1,0:T(1,128)S(1)}, u32[]{:S(2)}, u32[]{:S(2)}) async-start(f32[32,1,32]{2,1,0:T(1,128)} %broadcast_in_dim.35), calls=%async_computation.2 | async-start | bytes 32768 | tf_op jit(solution)/shard_map/all_to_all | solution.py:107
  135.8 6.5 %collective-permute-start.18 = (f32[256]{0:T(256)S(1)}, f32[256]{0:T(256)S(1)}, u32[]{:S(2)}, u32[]{:S(2)}) collective-permute-start(f32[256]{0:T(256)S(1)} %dynamic-slice_subtract_fusion.2), channel_id=1, source_target_pairs={{0,1},{1,0},{2,3},{3,2},{4,5},{5,4},{6,7},{7,6},{8,9},{9,8},{10,11... | collective-permute-start | bytes 3080 | tf_op jit(solution)/shard_map/ppermute | solution.py:122
  136.5 24.2 %collective-permute-start.24 = (f32[8,1,512]{2,1,0:T(1,128)}, f32[8,1,512]{2,1,0:T(1,128)S(1)}, u32[]{:S(2)}, u32[]{:S(2)}) collective-permute-start(f32[8,1,512]{2,1,0:T(1,128)} %get-tuple-element.30), channel_id=1, source_target_pairs={{8,0},{16,8},{24,16},{2,24},{10,2},{18,10},{26,18},{4,26},{12,4},{... | collective-permute-start | bytes 49160 | tf_op jit(solution)/shard_map/ppermute | solution.py:50
  137.8 22.9 %collective-permute-start.25 = (f32[8,1,512]{2,1,0:T(1,128)}, f32[8,1,512]{2,1,0:T(1,128)S(1)}, u32[]{:S(2)}, u32[]{:S(2)}) collective-permute-start(f32[8,1,512]{2,1,0:T(1,128)} %get-tuple-element.31), channel_id=1, source_target_pairs={{0,8},{8,16},{16,24},{24,2},{2,10},{10,18},{18,26},{26,4},{4,12},{... | collective-permute-start | bytes 49160 | tf_op jit(solution)/shard_map/ppermute | solution.py:49
  140.9 4.9 %collective-permute-start.26 = (f32[8,16,1]{2,1,0:T(8,128)S(1)}, f32[8,16,1]{2,1,0:T(8,128)S(1)}, u32[]{:S(2)}, u32[]{:S(2)}) collective-permute-start(f32[8,16,1]{2,1,0:T(8,128)S(1)} %slice_select_fusion.1), channel_id=1, source_target_pairs={{0,1},{1,0},{2,3},{3,2},{4,5},{5,4},{6,7},{7,6},{8,9},{9,8},{10,11... | collective-permute-start | bytes 1544 | tf_op jit(solution)/shard_map/ppermute | solution.py:46
  143.0 3.6 %collective-permute-start.19 = (f32[256]{0:T(256)S(1)}, f32[256]{0:T(256)S(1)}, u32[]{:S(2)}, u32[]{:S(2)}) collective-permute-start(f32[256]{0:T(256)S(1)} %dynamic-slice_subtract_fusion.1), channel_id=1, source_target_pairs={{0,1},{1,0},{2,3},{3,2},{4,5},{5,4},{6,7},{7,6},{8,9},{9,8},{10,11... | collective-permute-start | bytes 3080 | tf_op jit(solution)/shard_map/ppermute | solution.py:122
  151.8 3.6 %collective-permute-start.21 = (f32[512]{0:T(512)S(1)}, f32[512]{0:T(512)S(1)}, u32[]{:S(2)}, u32[]{:S(2)}) collective-permute-start(f32[512]{0:T(512)S(1)} %pad_maximum_fusion.6), channel_id=1, source_target_pairs={{0,1},{1,0},{2,3},{3,2},{4,5},{5,4},{6,7},{7,6},{8,9},{9,8},{10,11... | collective-permute-start | bytes 6152 | tf_op jit(solution)/shard_map/ppermute | solution.py:122
  155.9 3.6 %collective-permute-start.22 = (f32[512]{0:T(512)S(1)}, f32[512]{0:T(512)S(1)}, u32[]{:S(2)}, u32[]{:S(2)}) collective-permute-start(f32[512]{0:T(512)S(1)} %pad_maximum_fusion.7), channel_id=1, source_target_pairs={{0,1},{1,0},{2,3},{3,2},{4,5},{5,4},{6,7},{7,6},{8,9},{9,8},{10,11... | collective-permute-start | bytes 6152 | tf_op jit(solution)/shard_map/ppermute | solution.py:122
  160.0 10.1 %collective-permute-start.23 = (f32[1024]{0:T(1024)S(1)}, f32[1024]{0:T(1024)S(1)}, u32[]{:S(2)}, u32[]{:S(2)}) collective-permute-start(f32[1024]{0:T(1024)S(1)} %pad_maximum_fusion.3), channel_id=1, source_target_pairs={{0,1},{1,0},{2,3},{3,2},{4,5},{5,4},{6,7},{7,6},{8,9},{9,8},{10,11... | collective-permute-start | bytes 12296 | tf_op jit(solution)/shard_map/ppermute | solution.py:122
  164.1 5.3 %collective-permute-start.29 = (f32[8,16,1]{2,1,0:T(8,128)S(1)}, f32[8,16,1]{2,1,0:T(8,128)S(1)}, u32[]{:S(2)}, u32[]{:S(2)}) collective-permute-start(f32[8,16,1]{2,1,0:T(8,128)S(1)} %slice_select_fusion), channel_id=1, source_target_pairs={{0,1},{1,0},{2,3},{3,2},{4,5},{5,4},{6,7},{7,6},{8,9},{9,8},{10,11... | collective-permute-start | bytes 1544 | tf_op jit(solution)/shard_map/ppermute | solution.py:46
  166.1 9.1 %collective-permute-start.28 = (f32[8,1,512]{2,1,0:T(1,128)}, f32[8,1,512]{2,1,0:T(1,128)}, u32[]{:S(2)}, u32[]{:S(2)}) collective-permute-start(f32[8,1,512]{2,1,0:T(1,128)} %get-tuple-element.22), channel_id=1, source_target_pairs={{0,8},{8,16},{16,24},{24,2},{2,10},{10,18},{18,26},{26,4},{4,12},{... | collective-permute-start | bytes 49160 | tf_op jit(solution)/shard_map/ppermute | solution.py:49
  168.1 7.1 %collective-permute-start.27 = (f32[8,1,512]{2,1,0:T(1,128)}, f32[8,1,512]{2,1,0:T(1,128)}, u32[]{:S(2)}, u32[]{:S(2)}) collective-permute-start(f32[8,1,512]{2,1,0:T(1,128)} %get-tuple-element.23), channel_id=1, source_target_pairs={{8,0},{16,8},{24,16},{2,24},{10,2},{18,10},{26,18},{4,26},{12,4},{... | collective-permute-start | bytes 49160 | tf_op jit(solution)/shard_map/ppermute | solution.py:50
  178.5 10.4 %all-to-all-start.3 = ((f32[8,16,512]{2,1,0:T(8,128)}), f32[8,16,512]{2,1,0:T(8,128)S(1)}, u32[]{:S(2)}, u32[]{:S(2)}) async-start(f32[8,16,512]{2,1,0:T(8,128)} %fusion.117), calls=%async_computation.3 | async-start | bytes 524288 | tf_op jit(solution)/shard_map/all_to_all | solution.py:263
  (52 other events, 470.6 us)

commit v6 on v2

--- a/solution.py
+++ b/solution.py
@@ -97,6 +97,21 @@
             value = value + lax.ppermute(value, axis, [(i, i ^ step) for i in range(count)])
             step *= 2
     return value
+
+
+def share_tiles(tiles, own_rows, own_cols, flat_tiles):
+    layers, rows, cols = (lax.axis_size(axis) for axis, _ in GRID_AXES)
+    count = layers * rows * cols
+    payload = jnp.broadcast_to(tiles.reshape(1, -1), (count, tiles.size))
+    got = lax.all_to_all(payload, ("layer", "row", "col"), 0, 0, tiled=True)
+    tile_cols = cols * own_cols
+    tile_row, tile_col = flat_tiles // tile_cols, flat_tiles % tile_cols
+    block = tile_row // own_rows
+    device = ((block % layers) * rows + block // layers) * cols + tile_col // own_cols
+    slot = (tile_row % own_rows) * own_cols + tile_col % own_cols
+    pick_device = (device[:, None] == jnp.arange(count, dtype=jnp.int32)[None, :]).astype(jnp.float32)
+    pick_slot = (slot[:, None] == jnp.arange(tiles.size, dtype=jnp.int32)[None, :]).astype(jnp.float32)
+    return jnp.sum(jnp.dot(pick_device, got, precision=highest) * pick_slot, axis=1)
 
 
 def swap_col(value):
@@ -204,11 +219,6 @@
     first_row = (lax.axis_index("row") * layer_count + lax.axis_index("layer")) * own_rows
     first_col = lax.axis_index("col") * own_cols
     flat_tiles = port_tile.reshape(-1)
-    local_ids = (
-        (first_row + jnp.arange(own_rows, dtype=jnp.int32))[:, None] * tile_cols
-        + (first_col + jnp.arange(own_cols, dtype=jnp.int32))[None, :]
-    ).reshape(-1)
-    gather_local = (flat_tiles[:, None] == local_ids[None, :]).astype(jnp.float32)
     ring_rows = first_row - 1 + jnp.arange(own_rows + 2, dtype=jnp.int32)
     ring_cols = first_col - 1 + jnp.arange(own_cols + 2, dtype=jnp.int32)
     ring_ok = ((ring_rows >= 0) & (ring_rows < tile_rows))[:, None] & ((ring_cols >= 0) & (ring_cols < tile_cols))[None, :]
@@ -225,8 +235,7 @@
             resid = sources - apply_grid(drop, drop_near, weights, pad_term)
         plane = jnp.sum(resid, axis=0)
         tiles = plane.reshape(own_rows, TILE, own_cols, TILE).sum(axis=(1, 3)).reshape(-1)
-        local_rhs = jnp.dot(gather_local, tiles, precision=highest)
-        rhs = all_sum(local_rhs).reshape(NPANEL, PANEL) * (restrict_scale / TILE)
+        rhs = share_tiles(tiles, own_rows, own_cols, flat_tiles).reshape(NPANEL, PANEL) * (restrict_scale / TILE)
         ports = coarse(rhs, pivots, coupling)
         tile_values = jnp.dot(scatter_ring, ports.reshape(-1), precision=highest).reshape(own_rows + 2, own_cols + 2)
         ring = expand(expand(tile_values, True).T, True).T * prolong_scale

time: 169 us -> 171 us (1.012)
  starting transfers between devices: 71.8 us -> 64.3 us
  local copies, waits for them, and re-layouts: 16.9 us -> 24.1 us
    ppermute x10 -> x0, starting transfers between devices: 16.5 us -> none  [all_sum(): lax.ppermute(value, axis, [(i, i ^ step) for i in range(count)])]
    all_to_all x0 -> x2, starting transfers between devices: none -> 15.2 us  [share_tiles(): got = lax.all_to_all(payload, ('layer', 'row', 'col'), 0, 0, tiled=True)]
    ppermute x10 -> x0, waiting for transfers between devices: 7.49 us -> none  [all_sum(): lax.ppermute(value, axis, [(i, i ^ step) for i in range(count)])]
    ppermute x12, starting transfers between devices: 12.8 us -> 5.71 us  [swap_col(): return lax.ppermute(value, 'col', [(0, 1), (1, 0)])]
    all_to_all x0 -> x2, waiting for transfers between devices: none -> 6.51 us  [share_tiles(): got = lax.all_to_all(payload, ('layer', 'row', 'col'), 0, 0, tiled=True)]
    ppermute x12, waiting for transfers between devices: 18.3 us -> 21.1 us  [swap_col(): return lax.ppermute(value, 'col', [(0, 1), (1, 0)])]
    reduce_sum x4, other arithmetic: 3.66 us -> 1.07 us  [shards(): plane.reshape(own_rows, TILE, own_cols, TILE).sum(axis=(1, 3)).reshape(-1)]
    ppermute x6, starting transfers between devices: 16.6 us -> 18.9 us  [rims(): lax.ppermute(tail, axis, [(place[i], place[i + 1]) for i in range(count -...]
  transfers between devices with their start and end apart: 42 -> 34, of which waited for: 19 -> 17; matrix products, arithmetic and copies ran while one was open for 18% -> 21% of each run, Pallas kernels for 0% -> 0%
where the time goes in v6:
time: 171 us; the launch traced here: 170 us
  starting transfers between devices  64.3 us (38%)
  waiting for transfers between devices  48.8 us (29%)
  local copies, waits for them, and re-layouts  24.1 us (14%)
  other arithmetic  17.6 us (10%)
  matrix products  13 us (8%)
  between operations  1.78 us (1%)
    ppermute x12, waiting for transfers between devices, swap_col(): return lax.ppermute(value, 'col', [(0, 1), (1, 0)])  21.1 us
    ppermute x6, starting transfers between devices, rims(): lax.ppermute(tail, axis, [(place[i], place[i + 1]) for i in range(count -...  18.9 us
    all_to_all x2, starting transfers between devices, share_tiles(): got = lax.all_to_all(payload, ('layer', 'row', 'col'), 0, 0, tiled=True)  15.2 us
    all_to_all x1, waiting for transfers between devices, shards(): lax.all_to_all(jnp.stack((sources, conduct, vertical)), 'layer', 2, 1, ti...  10.6 us
    ppermute x6, starting transfers between devices, rims(): got = lax.ppermute(jnp.where(low, tail, head), axis, [(0, 1), (1, 0)])  8.29 us
    ppermute x6, starting transfers between devices, rims(): lax.ppermute(head, axis, [(place[i + 1], place[i]) for i in range(count -...  7.72 us
    slice x12, local copies, waits for them, and re-layouts, neighbours(): lax.slice_in_dim(field, 1, size, axis=dim)  7.01 us
    all_to_all x2, waiting for transfers between devices, share_tiles(): got = lax.all_to_all(payload, ('layer', 'row', 'col'), 0, 0, tiled=True)  6.51 us
  transfers between devices with their start and end apart: 34, of which 17 were waited for; matrix products, arithmetic and copies ran while one was open for 21% of the time, Pallas kernels for 0%

profile of v6, /device:TPU:0, one launch (start us, length us, event | category | flops | bytes accessed | tf_op | source)
XLA Modules:
  0.0 169.7 jit_solution(2222658078517581884)
XLA Ops:
  2.8 1.5 copy.22
  4.3 4.2 %all-to-all-start = ((f32[3,2,64,512]{3,1,0,2:T(2,128)}), f32[3,2,64,512]{3,1,0,2:T(2,128)S(1)}, u32[]{:S(2)}, u32[]{:S(2)}) async-start(f32[3,2,64,512]{3,1,0,2:T(2,128)} %copy.22), calls=%async_computation | async-start | bytes 1572864 | tf_op jit(solution)/shard_map/all_to_all | solution.py:188
  9.6 10.6 %all-to-all-done = f32[3,2,64,512]{3,1,0,2:T(2,128)S(1)} async-done(((f32[3,2,64,512]{3,1,0,2:T(2,128)}), f32[3,2,64,512]{3,1,0,2:T(2,128)S(1)}, u32[]{:S(2)}, u32[]{:S(2)}) %all-to-all-start) | async-done | bytes 786464 | tf_op jit(solution)/shard_map/all_to_all | solution.py:188
  23.2 5.6 %all-to-all-start.1 = ((f32[32,1,32]{2,1,0:T(1,128)}), f32[32,1,32]{2,1,0:T(1,128)S(1)}, u32[]{:S(2)}, u32[]{:S(2)}) async-start(f32[32,1,32]{2,1,0:T(1,128)} %broadcast_in_dim.27), calls=%async_computation.1 | async-start | bytes 32768 | tf_op jit(solution)/shard_map/all_to_all | solution.py:106
  30.9 3.0 %collective-permute-start.7 = (f32[8,1,512]{2,1,0:T(1,128)S(1)}, f32[8,1,512]{2,1,0:T(1,128)S(1)}, u32[]{:S(2)}, u32[]{:S(2)}) collective-permute-start(f32[8,1,512]{2,1,0:T(1,128)S(1)} %get-tuple-element.61), channel_id=1, source_target_pairs={{0,8},{8,16},{16,24},{24,2},{2,10},{10,18},{18,26},{26,4},{4,12},{... | collective-permute-start | bytes 49160 | tf_op jit(solution)/shard_map/ppermute | solution.py:48
  34.9 1.8 %collective-permute-start.8 = (f32[8,16,1]{2,1,0:T(8,128)S(1)}, f32[8,16,1]{2,1,0:T(8,128)S(1)}, u32[]{:S(2)}, u32[]{:S(2)}) collective-permute-start(f32[8,16,1]{2,1,0:T(8,128)S(1)} %slice_select_fusion.5), channel_id=1, source_target_pairs={{0,1},{1,0},{2,3},{3,2},{4,5},{5,4},{6,7},{7,6},{8,9},{9,8},{10,11... | collective-permute-start | bytes 1544 | tf_op jit(solution)/shard_map/ppermute | solution.py:45
  39.4 2.4 %collective-permute-done = f32[256]{0:T(256)S(1)} collective-permute-done((f32[256]{0:T(256)S(1)}, f32[256]{0:T(256)S(1)}, u32[]{:S(2)}, u32[]{:S(2)}) %collective-permute-start) | collective-permute-done | bytes 1056 | tf_op jit(solution)/shard_map/ppermute | solution.py:118
  42.7 1.5 fusion.42
  44.2 1.8 %collective-permute-done.1 = f32[256]{0:T(256)S(1)} collective-permute-done((f32[256]{0:T(256)S(1)}, f32[256]{0:T(256)S(1)}, u32[]{:S(2)}, u32[]{:S(2)}) %collective-permute-start.1) | collective-permute-done | bytes 1056 | tf_op jit(solution)/shard_map/ppermute | solution.py:118
  47.5 2.8 %collective-permute-done.2 = f32[256]{0:T(256)S(1)} collective-permute-done((f32[256]{0:T(256)S(1)}, f32[256]{0:T(256)S(1)}, u32[]{:S(2)}, u32[]{:S(2)}) %collective-permute-start.2) | collective-permute-done | bytes 1056 | tf_op jit(solution)/shard_map/ppermute | solution.py:118
  52.1 2.8 %collective-permute-done.3 = f32[512]{0:T(512)S(1)} collective-permute-done((f32[512]{0:T(512)S(1)}, f32[512]{0:T(512)S(1)}, u32[]{:S(2)}, u32[]{:S(2)}) %collective-permute-start.3) | collective-permute-done | bytes 2080 | tf_op jit(solution)/shard_map/ppermute | solution.py:118
  55.7 3.3 %collective-permute-done.4 = f32[512]{0:T(512)S(1)} collective-permute-done((f32[512]{0:T(512)S(1)}, f32[512]{0:T(512)S(1)}, u32[]{:S(2)}, u32[]{:S(2)}) %collective-permute-start.4) | collective-permute-done | bytes 2080 | tf_op jit(solution)/shard_map/ppermute | solution.py:118
  63.8 1.8 %collective-permute-start.11 = (f32[8,16,1]{2,1,0:T(8,128)S(1)}, f32[8,16,1]{2,1,0:T(8,128)S(1)}, u32[]{:S(2)}, u32[]{:S(2)}) collective-permute-start(f32[8,16,1]{2,1,0:T(8,128)S(1)} %slice_select_fusion.4), channel_id=1, source_target_pairs={{0,1},{1,0},{2,3},{3,2},{4,5},{5,4},{6,7},{7,6},{8,9},{9,8},{10,11... | collective-permute-start | bytes 1544 | tf_op jit(solution)/shard_map/ppermute | solution.py:45
  67.5 3.6 %collective-permute-start.10 = (f32[8,1,512]{2,1,0:T(1,128)}, f32[8,1,512]{2,1,0:T(1,128)}, u32[]{:S(2)}, u32[]{:S(2)}) collective-permute-start(f32[8,1,512]{2,1,0:T(1,128)} %get-tuple-element.55), channel_id=1, source_target_pairs={{0,8},{8,16},{16,24},{24,2},{2,10},{10,18},{18,26},{26,4},{4,12},{... | collective-permute-start | bytes 49160 | tf_op jit(solution)/shard_map/ppermute | solution.py:48
  76.1 1.9 %fusion.150 = (f32[8,16,512]{2,1,0:T(8,128)S(1)}, f32[8,16,512]{2,1,0:T(8,128)S(1)}) fusion(f32[8,16,512]{2,1,0:T(8,128)S(1)} %get-tuple-element.7, f32[1,4,2,16,512]{4,3,2,1,0:T(8,128)} %copy.25, f32[8,16,512]{2,1,0:T(8,128)S(1)} %get-tuple-element.12, f32[8,16,511]{2,1,0:T(8,128)} %get-tuple-element.57, f32[8,16,1]{2,1,0:T(8,128)} %get-tuple-element.75, ...), kind=kLoop, calls=%fused_computation.191 | loop fusion | flops 1966080 | bytes 4161536 | tf_op jit(solution)/shard_map/add | solution.py:84
  78.8 2.4 %collective-permute-start.13 = (f32[8,1,512]{2,1,0:T(1,128)S(1)}, f32[8,1,512]{2,1,0:T(1,128)S(1)}, u32[]{:S(2)}, u32[]{:S(2)}) collective-permute-start(f32[8,1,512]{2,1,0:T(1,128)S(1)} %get-tuple-element.46), channel_id=1, source_target_pairs={{0,8},{8,16},{16,24},{24,2},{2,10},{10,18},{18,26},{26,4},{4,12},{... | collective-permute-start | bytes 49160 | tf_op jit(solution)/shard_map/ppermute | solution.py:48
  83.1 1.6 collective-permute-done.12
  85.5 1.5 collective-permute-start.17
  88.4 4.7 %collective-permute-start.16 = (f32[8,1,512]{2,1,0:T(1,128)S(1)}, f32[8,1,512]{2,1,0:T(1,128)S(1)}, u32[]{:S(2)}, u32[]{:S(2)}) collective-permute-start(f32[8,1,512]{2,1,0:T(1,128)S(1)} %get-tuple-element.39), channel_id=1, source_target_pairs={{0,8},{8,16},{16,24},{24,2},{2,10},{10,18},{18,26},{26,4},{4,12},{... | collective-permute-start | bytes 49160 | tf_op jit(solution)/shard_map/ppermute | solution.py:48
  97.8 9.5 %all-to-all-start.2 = ((f32[32,1,32]{2,1,0:T(1,128)}), f32[32,1,32]{2,1,0:T(1,128)S(1)}, u32[]{:S(2)}, u32[]{:S(2)}) async-start(f32[32,1,32]{2,1,0:T(1,128)} %broadcast_in_dim.35), calls=%async_computation.2 | async-start | bytes 32768 | tf_op jit(solution)/shard_map/all_to_all | solution.py:106
  108.0 6.5 %all-to-all-done.2 = f32[32,1,32]{2,1,0:T(1,128)S(1)} async-done(((f32[32,1,32]{2,1,0:T(1,128)}), f32[32,1,32]{2,1,0:T(1,128)S(1)}, u32[]{:S(2)}, u32[]{:S(2)}) %all-to-all-start.2) | async-done | bytes 4128 | tf_op jit(solution)/shard_map/all_to_all | solution.py:106
  117.9 3.0 %collective-permute-start.25 = (f32[8,1,512]{2,1,0:T(1,128)}, f32[8,1,512]{2,1,0:T(1,128)S(1)}, u32[]{:S(2)}, u32[]{:S(2)}) collective-permute-start(f32[8,1,512]{2,1,0:T(1,128)} %get-tuple-element.31), channel_id=1, source_target_pairs={{0,8},{8,16},{16,24},{24,2},{2,10},{10,18},{18,26},{26,4},{4,12},{... | collective-permute-start | bytes 49160 | tf_op jit(solution)/shard_map/ppermute | solution.py:48
  121.0 1.5 collective-permute-start.26
  123.7 2.1 %collective-permute-done.26 = f32[8,16,1]{2,1,0:T(8,128)S(1)} collective-permute-done((f32[8,16,1]{2,1,0:T(8,128)S(1)}, f32[8,16,1]{2,1,0:T(8,128)S(1)}, u32[]{:S(2)}, u32[]{:S(2)}) %collective-permute-start.26) | collective-permute-done | bytes 544 | tf_op jit(solution)/shard_map/ppermute | solution.py:45
  128.4 2.4 %collective-permute-done.20 = f32[256]{0:T(256)S(1)} collective-permute-done((f32[256]{0:T(256)S(1)}, f32[256]{0:T(256)S(1)}, u32[]{:S(2)}, u32[]{:S(2)}) %collective-permute-start.20) | collective-permute-done | bytes 1056 | tf_op jit(solution)/shard_map/ppermute | solution.py:118
  133.1 2.4 %collective-permute-done.21 = f32[512]{0:T(512)S(1)} collective-permute-done((f32[512]{0:T(512)S(1)}, f32[512]{0:T(512)S(1)}, u32[]{:S(2)}, u32[]{:S(2)}) %collective-permute-start.21) | collective-permute-done | bytes 2080 | tf_op jit(solution)/shard_map/ppermute | solution.py:118
  137.2 2.4 %collective-permute-done.22 = f32[512]{0:T(512)S(1)} collective-permute-done((f32[512]{0:T(512)S(1)}, f32[512]{0:T(512)S(1)}, u32[]{:S(2)}, u32[]{:S(2)}) %collective-permute-start.22) | collective-permute-done | bytes 2080 | tf_op jit(solution)/shard_map/ppermute | solution.py:118
  146.2 2.0 %collective-permute-start.28 = (f32[8,1,512]{2,1,0:T(1,128)}, f32[8,1,512]{2,1,0:T(1,128)}, u32[]{:S(2)}, u32[]{:S(2)}) collective-permute-start(f32[8,1,512]{2,1,0:T(1,128)} %get-tuple-element.22), channel_id=1, source_target_pairs={{0,8},{8,16},{16,24},{24,2},{2,10},{10,18},{18,26},{26,4},{4,12},{... | collective-permute-start | bytes 49160 | tf_op jit(solution)/shard_map/ppermute | solution.py:48
  152.5 1.7 %reshape.594 = f32[512,18]{0,1:T(8,128)} reshape(f32[32,16,18]{1,0,2:T(8,128)} %broadcast_in_dim.36) | data formatting | bytes 73728 | tf_op jit(solution)/shard_map/reshape | solution.py:179
  155.3 3.3 %fusion.121 = f32[8,16,512]{2,1,0:T(8,128)} fusion(f32[8,16,512]{2,1,0:T(8,128)S(1)} %copy-done.15, f32[1,16,512]{2,1,0:T(8,128)S(1)} %multiply_bitcast_fusion.1, f32[8,16,512]{2,1,0:T(8,128)S(1)} %copy-done.8, f32[8,1,512]{2,1,0:T(1,128)} %collective-permute-done.27, f32[8,15,512]{2,1,0:T(8,128)} %get-tuple-element.25, ...), kind=kLoop, calls=%fused_computation.133 | loop fusion | flops 3997696 | bytes 5996544 | tf_op jit(solution)/shard_map/add | solution.py:246
  158.6 4.4 %all-to-all-start.3 = ((f32[8,16,512]{2,1,0:T(8,128)}), f32[8,16,512]{2,1,0:T(8,128)S(1)}, u32[]{:S(2)}, u32[]{:S(2)}) async-start(f32[8,16,512]{2,1,0:T(8,128)} %fusion.121), calls=%async_computation.3 | async-start | bytes 524288 | tf_op jit(solution)/shard_map/all_to_all | solution.py:258
  164.3 4.7 %all-to-all-done.3 = f32[8,16,512]{2,1,0:T(8,128)S(1)} async-done(((f32[8,16,512]{2,1,0:T(8,128)}), f32[8,16,512]{2,1,0:T(8,128)S(1)}, u32[]{:S(2)}, u32[]{:S(2)}) %all-to-all-start.3) | async-done | bytes 262176 | tf_op jit(solution)/shard_map/all_to_all | solution.py:258
  (284 shorter events, 62.9 us)
Async XLA Ops:
  4.3 15.9 %all-to-all-start = ((f32[3,2,64,512]{3,1,0,2:T(2,128)}), f32[3,2,64,512]{3,1,0,2:T(2,128)S(1)}, u32[]{:S(2)}, u32[]{:S(2)}) async-start(f32[3,2,64,512]{3,1,0,2:T(2,128)} %copy.22), calls=%async_computation | async-start | bytes 1572864 | tf_op jit(solution)/shard_map/all_to_all | solution.py:188
  23.2 13.6 %all-to-all-start.1 = ((f32[32,1,32]{2,1,0:T(1,128)}), f32[32,1,32]{2,1,0:T(1,128)S(1)}, u32[]{:S(2)}, u32[]{:S(2)}) async-start(f32[32,1,32]{2,1,0:T(1,128)} %broadcast_in_dim.27), calls=%async_computation.1 | async-start | bytes 32768 | tf_op jit(solution)/shard_map/all_to_all | solution.py:106
  29.6 30.2 %collective-permute-start.6 = (f32[8,1,512]{2,1,0:T(1,128)S(1)}, f32[8,1,512]{2,1,0:T(1,128)S(1)}, u32[]{:S(2)}, u32[]{:S(2)}) collective-permute-start(f32[8,1,512]{2,1,0:T(1,128)S(1)} %get-tuple-element.60), channel_id=1, source_target_pairs={{8,0},{16,8},{24,16},{2,24},{10,2},{18,10},{26,18},{4,26},{12,4},{... | collective-permute-start | bytes 49160 | tf_op jit(solution)/shard_map/ppermute | solution.py:49
  30.9 28.9 %collective-permute-start.7 = (f32[8,1,512]{2,1,0:T(1,128)S(1)}, f32[8,1,512]{2,1,0:T(1,128)S(1)}, u32[]{:S(2)}, u32[]{:S(2)}) collective-permute-start(f32[8,1,512]{2,1,0:T(1,128)S(1)} %get-tuple-element.61), channel_id=1, source_target_pairs={{0,8},{8,16},{16,24},{24,2},{2,10},{10,18},{18,26},{26,4},{4,12},{... | collective-permute-start | bytes 49160 | tf_op jit(solution)/shard_map/ppermute | solution.py:48
  34.9 4.5 %collective-permute-start.8 = (f32[8,16,1]{2,1,0:T(8,128)S(1)}, f32[8,16,1]{2,1,0:T(8,128)S(1)}, u32[]{:S(2)}, u32[]{:S(2)}) collective-permute-start(f32[8,16,1]{2,1,0:T(8,128)S(1)} %slice_select_fusion.5), channel_id=1, source_target_pairs={{0,1},{1,0},{2,3},{3,2},{4,5},{5,4},{6,7},{7,6},{8,9},{9,8},{10,11... | collective-permute-start | bytes 1544 | tf_op jit(solution)/shard_map/ppermute | solution.py:45
  38.2 3.6 %collective-permute-start = (f32[256]{0:T(256)S(1)}, f32[256]{0:T(256)S(1)}, u32[]{:S(2)}, u32[]{:S(2)}) collective-permute-start(f32[256]{0:T(256)S(1)} %dynamic-slice_subtract_fusion.5), channel_id=1, source_target_pairs={{0,1},{1,0},{2,3},{3,2},{4,5},{5,4},{6,7},{7,6},{8,9},{9,8},{10,11... | collective-permute-start | bytes 3080 | tf_op jit(solution)/shard_map/ppermute | solution.py:118
  42.4 3.6 %collective-permute-start.1 = (f32[256]{0:T(256)S(1)}, f32[256]{0:T(256)S(1)}, u32[]{:S(2)}, u32[]{:S(2)}) collective-permute-start(f32[256]{0:T(256)S(1)} %dynamic-slice_subtract_fusion.4), channel_id=1, source_target_pairs={{0,1},{1,0},{2,3},{3,2},{4,5},{5,4},{6,7},{7,6},{8,9},{9,8},{10,11... | collective-permute-start | bytes 3080 | tf_op jit(solution)/shard_map/ppermute | solution.py:118
  46.7 3.6 %collective-permute-start.2 = (f32[256]{0:T(256)S(1)}, f32[256]{0:T(256)S(1)}, u32[]{:S(2)}, u32[]{:S(2)}) collective-permute-start(f32[256]{0:T(256)S(1)} %dynamic-slice_subtract_fusion.3), channel_id=1, source_target_pairs={{0,1},{1,0},{2,3},{3,2},{4,5},{5,4},{6,7},{7,6},{8,9},{9,8},{10,11... | collective-permute-start | bytes 3080 | tf_op jit(solution)/shard_map/ppermute | solution.py:118
  51.3 3.6 %collective-permute-start.3 = (f32[512]{0:T(512)S(1)}, f32[512]{0:T(512)S(1)}, u32[]{:S(2)}, u32[]{:S(2)}) collective-permute-start(f32[512]{0:T(512)S(1)} %pad_maximum_fusion.4), channel_id=1, source_target_pairs={{0,1},{1,0},{2,3},{3,2},{4,5},{5,4},{6,7},{7,6},{8,9},{9,8},{10,11... | collective-permute-start | bytes 6152 | tf_op jit(solution)/shard_map/ppermute | solution.py:118
  55.4 3.6 %collective-permute-start.4 = (f32[512]{0:T(512)S(1)}, f32[512]{0:T(512)S(1)}, u32[]{:S(2)}, u32[]{:S(2)}) collective-permute-start(f32[512]{0:T(512)S(1)} %pad_maximum_fusion.5), channel_id=1, source_target_pairs={{0,1},{1,0},{2,3},{3,2},{4,5},{5,4},{6,7},{7,6},{8,9},{9,8},{10,11... | collective-permute-start | bytes 6152 | tf_op jit(solution)/shard_map/ppermute | solution.py:118
  59.5 12.3 %collective-permute-start.5 = (f32[1024]{0:T(1024)S(1)}, f32[1024]{0:T(1024)S(1)}, u32[]{:S(2)}, u32[]{:S(2)}) collective-permute-start(f32[1024]{0:T(1024)S(1)} %pad_maximum_fusion.2), channel_id=1, source_target_pairs={{0,1},{1,0},{2,3},{3,2},{4,5},{5,4},{6,7},{7,6},{8,9},{9,8},{10,11... | collective-permute-start | bytes 12296 | tf_op jit(solution)/shard_map/ppermute | solution.py:118
  63.8 7.3 %collective-permute-start.11 = (f32[8,16,1]{2,1,0:T(8,128)S(1)}, f32[8,16,1]{2,1,0:T(8,128)S(1)}, u32[]{:S(2)}, u32[]{:S(2)}) collective-permute-start(f32[8,16,1]{2,1,0:T(8,128)S(1)} %slice_select_fusion.4), channel_id=1, source_target_pairs={{0,1},{1,0},{2,3},{3,2},{4,5},{5,4},{6,7},{7,6},{8,9},{9,8},{10,11... | collective-permute-start | bytes 1544 | tf_op jit(solution)/shard_map/ppermute | solution.py:45
  66.2 9.9 %collective-permute-start.9 = (f32[8,1,512]{2,1,0:T(1,128)}, f32[8,1,512]{2,1,0:T(1,128)}, u32[]{:S(2)}, u32[]{:S(2)}) collective-permute-start(f32[8,1,512]{2,1,0:T(1,128)} %get-tuple-element.54), channel_id=1, source_target_pairs={{8,0},{16,8},{24,16},{2,24},{10,2},{18,10},{26,18},{4,26},{12,4},{... | collective-permute-start | bytes 49160 | tf_op jit(solution)/shard_map/ppermute | solution.py:49
  67.5 8.6 %collective-permute-start.10 = (f32[8,1,512]{2,1,0:T(1,128)}, f32[8,1,512]{2,1,0:T(1,128)}, u32[]{:S(2)}, u32[]{:S(2)}) collective-permute-start(f32[8,1,512]{2,1,0:T(1,128)} %get-tuple-element.55), channel_id=1, source_target_pairs={{0,8},{8,16},{16,24},{24,2},{2,10},{10,18},{18,26},{26,4},{4,12},{... | collective-permute-start | bytes 49160 | tf_op jit(solution)/shard_map/ppermute | solution.py:48
  78.5 4.6 %collective-permute-start.14 = (f32[8,16,1]{2,1,0:T(8,128)S(1)}, f32[8,16,1]{2,1,0:T(8,128)S(1)}, u32[]{:S(2)}, u32[]{:S(2)}) collective-permute-start(f32[8,16,1]{2,1,0:T(8,128)S(1)} %slice_select_fusion.3), channel_id=1, source_target_pairs={{0,1},{1,0},{2,3},{3,2},{4,5},{5,4},{6,7},{7,6},{8,9},{9,8},{10,11... | collective-permute-start | bytes 1544 | tf_op jit(solution)/shard_map/ppermute | solution.py:45
  78.8 4.2 %collective-permute-start.13 = (f32[8,1,512]{2,1,0:T(1,128)S(1)}, f32[8,1,512]{2,1,0:T(1,128)S(1)}, u32[]{:S(2)}, u32[]{:S(2)}) collective-permute-start(f32[8,1,512]{2,1,0:T(1,128)S(1)} %get-tuple-element.46), channel_id=1, source_target_pairs={{0,8},{8,16},{16,24},{24,2},{2,10},{10,18},{18,26},{26,4},{4,12},{... | collective-permute-start | bytes 49160 | tf_op jit(solution)/shard_map/ppermute | solution.py:48
  85.5 7.6 %collective-permute-start.17 = (f32[8,16,1]{2,1,0:T(8,128)S(1)}, f32[8,16,1]{2,1,0:T(8,128)S(1)}, u32[]{:S(2)}, u32[]{:S(2)}) collective-permute-start(f32[8,16,1]{2,1,0:T(8,128)S(1)} %slice_select_fusion.2), channel_id=1, source_target_pairs={{0,1},{1,0},{2,3},{3,2},{4,5},{5,4},{6,7},{7,6},{8,9},{9,8},{10,11... | collective-permute-start | bytes 1544 | tf_op jit(solution)/shard_map/ppermute | solution.py:45
  87.1 6.1 %collective-permute-start.15 = (f32[8,1,512]{2,1,0:T(1,128)S(1)}, f32[8,1,512]{2,1,0:T(1,128)S(1)}, u32[]{:S(2)}, u32[]{:S(2)}) collective-permute-start(f32[8,1,512]{2,1,0:T(1,128)S(1)} %get-tuple-element.38), channel_id=1, source_target_pairs={{8,0},{16,8},{24,16},{2,24},{10,2},{18,10},{26,18},{4,26},{12,4},{... | collective-permute-start | bytes 49160 | tf_op jit(solution)/shard_map/ppermute | solution.py:49
  88.4 5.6 %collective-permute-start.16 = (f32[8,1,512]{2,1,0:T(1,128)S(1)}, f32[8,1,512]{2,1,0:T(1,128)S(1)}, u32[]{:S(2)}, u32[]{:S(2)}) collective-permute-start(f32[8,1,512]{2,1,0:T(1,128)S(1)} %get-tuple-element.39), channel_id=1, source_target_pairs={{0,8},{8,16},{16,24},{24,2},{2,10},{10,18},{18,26},{26,4},{4,12},{... | collective-permute-start | bytes 49160 | tf_op jit(solution)/shard_map/ppermute | solution.py:48
  97.8 16.7 %all-to-all-start.2 = ((f32[32,1,32]{2,1,0:T(1,128)}), f32[32,1,32]{2,1,0:T(1,128)S(1)}, u32[]{:S(2)}, u32[]{:S(2)}) async-start(f32[32,1,32]{2,1,0:T(1,128)} %broadcast_in_dim.35), calls=%async_computation.2 | async-start | bytes 32768 | tf_op jit(solution)/shard_map/all_to_all | solution.py:106
  115.9 6.5 %collective-permute-start.18 = (f32[256]{0:T(256)S(1)}, f32[256]{0:T(256)S(1)}, u32[]{:S(2)}, u32[]{:S(2)}) collective-permute-start(f32[256]{0:T(256)S(1)} %dynamic-slice_subtract_fusion.2), channel_id=1, source_target_pairs={{0,1},{1,0},{2,3},{3,2},{4,5},{5,4},{6,7},{7,6},{8,9},{9,8},{10,11... | collective-permute-start | bytes 3080 | tf_op jit(solution)/shard_map/ppermute | solution.py:118
  116.6 24.2 %collective-permute-start.24 = (f32[8,1,512]{2,1,0:T(1,128)}, f32[8,1,512]{2,1,0:T(1,128)S(1)}, u32[]{:S(2)}, u32[]{:S(2)}) collective-permute-start(f32[8,1,512]{2,1,0:T(1,128)} %get-tuple-element.30), channel_id=1, source_target_pairs={{8,0},{16,8},{24,16},{2,24},{10,2},{18,10},{26,18},{4,26},{12,4},{... | collective-permute-start | bytes 49160 | tf_op jit(solution)/shard_map/ppermute | solution.py:49
  117.9 22.9 %collective-permute-start.25 = (f32[8,1,512]{2,1,0:T(1,128)}, f32[8,1,512]{2,1,0:T(1,128)S(1)}, u32[]{:S(2)}, u32[]{:S(2)}) collective-permute-start(f32[8,1,512]{2,1,0:T(1,128)} %get-tuple-element.31), channel_id=1, source_target_pairs={{0,8},{8,16},{16,24},{24,2},{2,10},{10,18},{18,26},{26,4},{4,12},{... | collective-permute-start | bytes 49160 | tf_op jit(solution)/shard_map/ppermute | solution.py:48
  121.0 4.9 %collective-permute-start.26 = (f32[8,16,1]{2,1,0:T(8,128)S(1)}, f32[8,16,1]{2,1,0:T(8,128)S(1)}, u32[]{:S(2)}, u32[]{:S(2)}) collective-permute-start(f32[8,16,1]{2,1,0:T(8,128)S(1)} %slice_select_fusion.1), channel_id=1, source_target_pairs={{0,1},{1,0},{2,3},{3,2},{4,5},{5,4},{6,7},{7,6},{8,9},{9,8},{10,11... | collective-permute-start | bytes 1544 | tf_op jit(solution)/shard_map/ppermute | solution.py:45
  127.3 3.6 %collective-permute-start.20 = (f32[256]{0:T(256)S(1)}, f32[256]{0:T(256)S(1)}, u32[]{:S(2)}, u32[]{:S(2)}) collective-permute-start(f32[256]{0:T(256)S(1)} %dynamic-slice_subtract_fusion), channel_id=1, source_target_pairs={{0,1},{1,0},{2,3},{3,2},{4,5},{5,4},{6,7},{7,6},{8,9},{9,8},{10,11... | collective-permute-start | bytes 3080 | tf_op jit(solution)/shard_map/ppermute | solution.py:118
  131.9 3.6 %collective-permute-start.21 = (f32[512]{0:T(512)S(1)}, f32[512]{0:T(512)S(1)}, u32[]{:S(2)}, u32[]{:S(2)}) collective-permute-start(f32[512]{0:T(512)S(1)} %pad_maximum_fusion.6), channel_id=1, source_target_pairs={{0,1},{1,0},{2,3},{3,2},{4,5},{5,4},{6,7},{7,6},{8,9},{9,8},{10,11... | collective-permute-start | bytes 6152 | tf_op jit(solution)/shard_map/ppermute | solution.py:118
  136.0 3.6 %collective-permute-start.22 = (f32[512]{0:T(512)S(1)}, f32[512]{0:T(512)S(1)}, u32[]{:S(2)}, u32[]{:S(2)}) collective-permute-start(f32[512]{0:T(512)S(1)} %pad_maximum_fusion.7), channel_id=1, source_target_pairs={{0,1},{1,0},{2,3},{3,2},{4,5},{5,4},{6,7},{7,6},{8,9},{9,8},{10,11... | collective-permute-start | bytes 6152 | tf_op jit(solution)/shard_map/ppermute | solution.py:118
  140.1 10.1 %collective-permute-start.23 = (f32[1024]{0:T(1024)S(1)}, f32[1024]{0:T(1024)S(1)}, u32[]{:S(2)}, u32[]{:S(2)}) collective-permute-start(f32[1024]{0:T(1024)S(1)} %pad_maximum_fusion.3), channel_id=1, source_target_pairs={{0,1},{1,0},{2,3},{3,2},{4,5},{5,4},{6,7},{7,6},{8,9},{9,8},{10,11... | collective-permute-start | bytes 12296 | tf_op jit(solution)/shard_map/ppermute | solution.py:118
  144.2 5.3 %collective-permute-start.29 = (f32[8,16,1]{2,1,0:T(8,128)S(1)}, f32[8,16,1]{2,1,0:T(8,128)S(1)}, u32[]{:S(2)}, u32[]{:S(2)}) collective-permute-start(f32[8,16,1]{2,1,0:T(8,128)S(1)} %slice_select_fusion), channel_id=1, source_target_pairs={{0,1},{1,0},{2,3},{3,2},{4,5},{5,4},{6,7},{7,6},{8,9},{9,8},{10,11... | collective-permute-start | bytes 1544 | tf_op jit(solution)/shard_map/ppermute | solution.py:45
  146.2 9.1 %collective-permute-start.28 = (f32[8,1,512]{2,1,0:T(1,128)}, f32[8,1,512]{2,1,0:T(1,128)}, u32[]{:S(2)}, u32[]{:S(2)}) collective-permute-start(f32[8,1,512]{2,1,0:T(1,128)} %get-tuple-element.22), channel_id=1, source_target_pairs={{0,8},{8,16},{16,24},{24,2},{2,10},{10,18},{18,26},{26,4},{4,12},{... | collective-permute-start | bytes 49160 | tf_op jit(solution)/shard_map/ppermute | solution.py:48
  148.2 7.1 %collective-permute-start.27 = (f32[8,1,512]{2,1,0:T(1,128)}, f32[8,1,512]{2,1,0:T(1,128)}, u32[]{:S(2)}, u32[]{:S(2)}) collective-permute-start(f32[8,1,512]{2,1,0:T(1,128)} %get-tuple-element.23), channel_id=1, source_target_pairs={{8,0},{16,8},{24,16},{2,24},{10,2},{18,10},{26,18},{4,26},{12,4},{... | collective-permute-start | bytes 49160 | tf_op jit(solution)/shard_map/ppermute | solution.py:49
  158.6 10.4 %all-to-all-start.3 = ((f32[8,16,512]{2,1,0:T(8,128)}), f32[8,16,512]{2,1,0:T(8,128)S(1)}, u32[]{:S(2)}, u32[]{:S(2)}) async-start(f32[8,16,512]{2,1,0:T(8,128)} %fusion.121), calls=%async_computation.3 | async-start | bytes 524288 | tf_op jit(solution)/shard_map/all_to_all | solution.py:258
  (50 other events, 655.2 us)

commit v7 on v6

--- a/solution.py
+++ b/solution.py
@@ -86,6 +86,40 @@
     return total
 
 
+def col_face(field):
+    low = lax.axis_index("col") == 0
+    return jnp.where(low, field[:, :, -1:], field[:, :, :1]).reshape(-1)
+
+
+def col_halo(field, got):
+    low = lax.axis_index("col") == 0
+    got = got.reshape(field.shape[0], field.shape[1], 1)
+    zero = jnp.zeros_like(got)
+    return jnp.where(low, got, zero), jnp.where(low, zero, got)
+
+
+def smooth_riding(resid, weights, pad_term, inverse, out, halo_after):
+    theta = (bound_high + bound_low) / 2.0
+    delta = (bound_high - bound_low) / 2.0
+    sigma = theta / delta
+    rho = 1.0 / sigma
+    change = inverse * resid / theta
+    total = change
+    for sweep in range(DEG - 1):
+        got = yield col_face(total)
+        halo = [rims(total, None, 0), rims(total, ROW_AXES, 1), col_halo(total, got)]
+        remain = resid - apply_grid(total, neighbours(total, halo), weights, pad_term)
+        rho_new = 1.0 / (2.0 * sigma - rho)
+        change = rho_new * rho * change + 2.0 * rho_new / delta * inverse * remain
+        total = total + change
+        rho = rho_new
+    out["total"] = total
+    if halo_after:
+        got = yield col_face(total)
+        halo = [rims(total, None, 0), rims(total, ROW_AXES, 1), col_halo(total, got)]
+        out["near"] = neighbours(total, halo)
+
+
 def all_sum(value):
     for axis, _ in GRID_AXES:
         count = lax.axis_size(axis)
@@ -122,7 +156,20 @@
     return jnp.where(low, jnp.concatenate([mine, other]), jnp.concatenate([other, mine]))
 
 
-def coarse_pair(rhs, pivots, coupling):
+def coarse_pair(rhs, pivots, coupling, rider=None):
+    carry = [rider.send(None) if rider is not None else None]
+
+    def swap_col(value):
+        extra = carry[0]
+        if extra is None:
+            return lax.ppermute(value, "col", [(0, 1), (1, 0)])
+        got = lax.ppermute(jnp.concatenate([value, extra]), "col", [(0, 1), (1, 0)])
+        try:
+            carry[0] = rider.send(got[value.size:])
+        except StopIteration:
+            carry[0] = None
+        return got[:value.size]
+
     share = pivots.shape[1]
     low = lax.axis_index("col") == 0
     start = lax.axis_index("col") * share
@@ -224,7 +271,6 @@
     ring_ok = ((ring_rows >= 0) & (ring_rows < tile_rows))[:, None] & ((ring_cols >= 0) & (ring_cols < tile_cols))[None, :]
     ring_ids = jnp.where(ring_ok, ring_rows[:, None] * tile_cols + ring_cols[None, :], -1).reshape(-1)
     scatter_ring = (ring_ids[:, None] == flat_tiles[None, :]).astype(jnp.float32)
-    coarse = coarse_pair if col_count == 2 else coarse_general
 
     drop = None
     drop_near = None
@@ -236,19 +282,26 @@
         plane = jnp.sum(resid, axis=0)
         tiles = plane.reshape(own_rows, TILE, own_cols, TILE).sum(axis=(1, 3)).reshape(-1)
         rhs = share_tiles(tiles, own_rows, own_cols, flat_tiles).reshape(NPANEL, PANEL) * (restrict_scale / TILE)
-        ports = coarse(rhs, pivots, coupling)
+        last = outer == ITERS - 1
+        if col_count == 2:
+            out = {}
+            rider = smooth_riding(resid, weights, pad_term, inverse, out, not last)
+            ports = coarse_pair(rhs, pivots, coupling, rider)
+            total = out["total"]
+        else:
+            ports = coarse_general(rhs, pivots, coupling)
+            total = smooth(resid, weights, pad_term, inverse)
         tile_values = jnp.dot(scatter_ring, ports.reshape(-1), precision=highest).reshape(own_rows + 2, own_cols + 2)
         ring = expand(expand(tile_values, True).T, True).T * prolong_scale
         centre = ring[1:-1, 1:-1]
         lifted = jnp.broadcast_to(centre[None], (local_layers, grid_rows, grid_cols))
-        total = smooth(resid, weights, pad_term, inverse)
-        if outer == ITERS - 1:
+        if last:
             drop = (lifted if drop is None else drop + lifted) + total
             break
         lifted_near = [lifted, lifted]
         for part in (ring[2:, 1:-1], ring[:-2, 1:-1], ring[1:-1, 2:], ring[1:-1, :-2]):
             lifted_near.append(jnp.broadcast_to(part[None], (local_layers, grid_rows, grid_cols)))
-        total_near = neighbours(total, exchange(total))
+        total_near = out["near"] if col_count == 2 else neighbours(total, exchange(total))
         if drop is None:
             drop = lifted + total
             drop_near = [a + b for a, b in zip(lifted_near, total_near)]

time: 171 us -> 188 us (1.099)
  waiting for transfers between devices: 48.8 us -> 33.1 us
  other arithmetic: 17.6 us -> 31.8 us
  local copies, waits for them, and re-layouts: 24.1 us -> 36.5 us
  matrix products: 13 us -> 24.1 us
  starting transfers between devices: 64.3 us -> 59.8 us
    ppermute x12 -> x7, waiting for transfers between devices: 21.1 us -> 10.9 us  [swap_col(): return lax.ppermute(value, 'col', [(0, 1), (1, 0)])]
    dot_general x8, matrix products: 5.09 us -> 14.8 us  [coarse_pair(): jnp.dot(pivots[section], forward[section], precision=highest)]
    select_n x0 -> x10, local copies, waits for them, and re-layouts: none -> 6.49 us  [col_halo(): return (jnp.where(low, got, zero), jnp.where(low, zero, got))]
    ppermute x6 -> x1, starting transfers between devices: 8.29 us -> 1.83 us  [rims(): got = lax.ppermute(jnp.where(low, tail, head), axis, [(0, 1), (1, 0)])]
    ppermute x0 -> x5, starting transfers between devices: none -> 5.2 us  [swap_col(): got = lax.ppermute(jnp.concatenate([value, extra]), 'col', [(0, 1), (1, 0)])]
    add x3, other arithmetic: 3 us -> 7.07 us  [smooth_riding(): total = total + change]
    all_to_all x2, waiting for transfers between devices: 6.51 us -> 2.56 us  [share_tiles(): got = lax.all_to_all(payload, ('layer', 'row', 'col'), 0, 0, tiled=True)]
    slice x12, local copies, waits for them, and re-layouts: 7.01 us -> 10.2 us  [neighbours(): lax.slice_in_dim(field, 1, size, axis=dim)]
  transfers between devices with their start and end apart: 34 -> 29, of which waited for: 17 -> 11; matrix products, arithmetic and copies ran while one was open for 21% -> 27% of each run, Pallas kernels for 0% -> 0%
where the time goes in v7:
time: 188 us; the launch traced here: 187 us
  starting transfers between devices  59.8 us (32%)
  local copies, waits for them, and re-layouts  36.5 us (19%)
  waiting for transfers between devices  33.1 us (18%)
  other arithmetic  31.8 us (17%)
  matrix products  24.1 us (13%)
    ppermute x6, starting transfers between devices, rims(): lax.ppermute(tail, axis, [(place[i], place[i + 1]) for i in range(count -...  18.2 us
    dot_general x8, matrix products, coarse_pair(): jnp.dot(pivots[section], forward[section], precision=highest)  14.8 us
    all_to_all x2, starting transfers between devices, share_tiles(): got = lax.all_to_all(payload, ('layer', 'row', 'col'), 0, 0, tiled=True)  12.5 us
    ppermute x7, waiting for transfers between devices, swap_col(): return lax.ppermute(value, 'col', [(0, 1), (1, 0)])  10.9 us
    slice x12, local copies, waits for them, and re-layouts, neighbours(): lax.slice_in_dim(field, 1, size, axis=dim)  10.2 us
    all_to_all x1, waiting for transfers between devices, shards(): lax.all_to_all(jnp.stack((sources, conduct, vertical)), 'layer', 2, 1, ti...  9.47 us
    ppermute x6, starting transfers between devices, rims(): lax.ppermute(head, axis, [(place[i + 1], place[i]) for i in range(count -...  7.71 us
    add x3, other arithmetic, smooth_riding(): total = total + change  7.07 us
  transfers between devices with their start and end apart: 29, of which 11 were waited for; matrix products, arithmetic and copies ran while one was open for 27% of the time, Pallas kernels for 0%

profile of v7, /device:TPU:0, one launch (start us, length us, event | category | flops | bytes accessed | tf_op | source)
XLA Modules:
  0.0 186.6 jit_solution(15189903826302041680)
XLA Ops:
  4.3 4.2 %all-to-all-start = ((f32[3,2,64,512]{3,1,0,2:T(2,128)}), f32[3,2,64,512]{3,1,0,2:T(2,128)S(1)}, u32[]{:S(2)}, u32[]{:S(2)}) async-start(f32[3,2,64,512]{3,1,0,2:T(2,128)} %copy.52), calls=%async_computation | async-start | bytes 1572864 | tf_op jit(solution)/shard_map/all_to_all | solution.py:235
  10.7 9.5 %all-to-all-done = f32[3,2,64,512]{3,1,0,2:T(2,128)S(1)} async-done(((f32[3,2,64,512]{3,1,0,2:T(2,128)}), f32[3,2,64,512]{3,1,0,2:T(2,128)S(1)}, u32[]{:S(2)}, u32[]{:S(2)}) %all-to-all-start) | async-done | bytes 786464 | tf_op jit(solution)/shard_map/all_to_all | solution.py:235
  23.3 5.6 %all-to-all-start.1 = ((f32[32,1,32]{2,1,0:T(1,128)}), f32[32,1,32]{2,1,0:T(1,128)S(1)}, u32[]{:S(2)}, u32[]{:S(2)}) async-start(f32[32,1,32]{2,1,0:T(1,128)} %broadcast_in_dim.27), calls=%async_computation.1 | async-start | bytes 32768 | tf_op jit(solution)/shard_map/all_to_all | solution.py:140
  30.9 3.0 %collective-permute-start.1 = (f32[8,1,512]{2,1,0:T(1,128)S(1)}, f32[8,1,512]{2,1,0:T(1,128)S(1)}, u32[]{:S(2)}, u32[]{:S(2)}) collective-permute-start(f32[8,1,512]{2,1,0:T(1,128)S(1)} %get-tuple-element.61), channel_id=1, source_target_pairs={{0,8},{8,16},{16,24},{24,2},{2,10},{10,18},{18,26},{26,4},{4,12},{... | collective-permute-start | bytes 49160 | tf_op jit(solution)/shard_map/ppermute | solution.py:48
  34.1 1.8 collective-permute-start.2
  36.8 1.8 collective-permute-done.2
  42.9 2.7 %bitcast_multiply_fusion = (f32[8,16,512]{2,1,0:T(8,128)S(1)}, f32[8,16,512]{2,1,0:T(8,128)S(1)}, f32[8,16,512]{2,1,0:T(8,128)S(1)}, f32[8,16,512]{2,1,0:T(8,128...) fusion(f32[1,4,2,16,512]{4,3,2,1,0:T(8,128)} %copy.55, ...), kind=kLoop, calls=%fused_computation.186 | loop fusion | flops 1179648 | bytes 4423680 | tf_op jit(solution)/shard_map/mul | solution.py:106
  48.5 2.0 %collective-permute-start.3 = (f32[384]{0:T(512)S(1)}, f32[384]{0:T(512)S(1)}, u32[]{:S(2)}, u32[]{:S(2)}) collective-permute-start(f32[384]{0:T(512)S(1)} %pad_maximum_fusion.4), channel_id=1, source_target_pairs={{0,1},{1,0},{2,3},{3,2},{4,5},{5,4},{6,7},{7,6},{8,9},{9,8},{10,11... | collective-permute-start | bytes 4616 | tf_op jit(solution)/shard_map/ppermute | solution.py:166
  51.8 3.0 %collective-permute-start.5 = (f32[8,1,512]{2,1,0:T(1,128)S(1)}, f32[8,1,512]{2,1,0:T(1,128)S(1)}, u32[]{:S(2)}, u32[]{:S(2)}) collective-permute-start(f32[8,1,512]{2,1,0:T(1,128)S(1)} %get-tuple-element.55), channel_id=1, source_target_pairs={{0,8},{8,16},{16,24},{24,2},{2,10},{10,18},{18,26},{26,4},{4,12},{... | collective-permute-start | bytes 49160 | tf_op jit(solution)/shard_map/ppermute | solution.py:48
  55.4 2.2 %fusion.30 = f32[1,256]{1,0:T(1,128)} fusion(f32[512,1]{0,1:T(1,128)S(1)} %bitcast.219, f32[4,256,512]{2,1,0:T(8,128)} %param.14), kind=kOutput, calls=%fused_computation.42 | convolution fusion | flops 1572864 | bytes 527360 | tf_op jit(solution)/shard_map/dot_general | solution.py:184
  58.1 2.8 %fusion.150 = (f32[8,16,512]{2,1,0:T(8,128)S(1)}, f32[8,16,512]{2,1,0:T(8,128)}) fusion(f32[8,16,512]{2,1,0:T(8,128)S(1)} %get-tuple-element.7, f32[1,4,2,16,512]{4,3,2,1,0:T(8,128)} %copy.55, f32[8,16,512]{2,1,0:T(8,128)} %get-tuple-element.12, f32[8,16,511]{2,1,0:T(8,128)} %get-tuple-element.57, f32[8,16,1]{2,1,0:T(8,128)S(1)} %select_n.473, ...), kind=kLoop, calls=%fused_computation.191 | loop fusion | flops 1966080 | bytes 4161536 | tf_op jit(solution)/shard_map/add | solution.py:114
  64.5 3.0 %collective-permute-start.8 = (f32[8,1,512]{2,1,0:T(1,128)}, f32[8,1,512]{2,1,0:T(1,128)S(1)}, u32[]{:S(2)}, u32[]{:S(2)}) collective-permute-start(f32[8,1,512]{2,1,0:T(1,128)} %get-tuple-element.46), channel_id=1, source_target_pairs={{0,8},{8,16},{16,24},{24,2},{2,10},{10,18},{18,26},{26,4},{4,12},{... | collective-permute-start | bytes 49160 | tf_op jit(solution)/shard_map/ppermute | solution.py:48
  69.3 2.1 %fusion.18 = f32[1,256]{1,0:T(1,128)} fusion(f32[512,1]{0,1:T(1,128)S(1)} %bitcast.221, f32[4,256,512]{2,1,0:T(8,128)} %param.14), kind=kOutput, calls=%fused_computation.30 | convolution fusion | flops 1572864 | bytes 527360 | tf_op jit(solution)/shard_map/dot_general | solution.py:184
  72.6 2.1 %fusion.94 = f32[8,16,512]{2,1,0:T(8,128)S(1)} fusion(f32[1,16,512]{2,1,0:T(8,128)S(1)} %multiply_bitcast_fusion.1, f32[8,16,512]{2,1,0:T(8,128)} %get-tuple-element.13, f32[8,1,512]{2,1,0:T(1,128)S(1)} %collective-permute-done.7, f32[8,15,512]{2,1,0:T(8,128)} %get-tuple-element.49, f32[8,16,512]{2,1,0:T(8,128)S(1)} %get-tuple-element.10, ...), kind=kLoop, calls=%fused_computation.106 | loop fusion | flops 2031616 | bytes 4161536 | tf_op jit(solution)/shard_map/add | solution.py:114
  77.5 1.8 collective-permute-start.9
  81.2 4.3 %collective-permute-start.14 = (f32[8,1,512]{2,1,0:T(1,128)}, f32[8,1,512]{2,1,0:T(1,128)}, u32[]{:S(2)}, u32[]{:S(2)}) collective-permute-start(f32[8,1,512]{2,1,0:T(1,128)} %get-tuple-element.39), channel_id=1, source_target_pairs={{0,8},{8,16},{16,24},{24,2},{2,10},{10,18},{18,26},{26,4},{4,12},{... | collective-permute-start | bytes 49160 | tf_op jit(solution)/shard_map/ppermute | solution.py:48
  89.2 2.0 %collective-permute-done.10 = f32[512]{0:T(512)S(1)} collective-permute-done((f32[512]{0:T(512)S(1)}, f32[512]{0:T(512)S(1)}, u32[]{:S(2)}, u32[]{:S(2)}) %collective-permute-start.10) | collective-permute-done | bytes 2080 | tf_op jit(solution)/shard_map/ppermute | solution.py:165
  92.3 3.0 %collective-permute-done.11 = f32[512]{0:T(512)S(1)} collective-permute-done((f32[512]{0:T(512)S(1)}, f32[512]{0:T(512)S(1)}, u32[]{:S(2)}, u32[]{:S(2)}) %collective-permute-start.11) | collective-permute-done | bytes 2080 | tf_op jit(solution)/shard_map/ppermute | solution.py:165
  96.4 3.0 %collective-permute-done.12 = f32[1024]{0:T(1024)S(1)} collective-permute-done((f32[1024]{0:T(1024)S(1)}, f32[1024]{0:T(1024)S(1)}, u32[]{:S(2)}, u32[]{:S(2)}) %collective-permute-start.12) | collective-permute-done | bytes 4128 | tf_op jit(solution)/shard_map/ppermute | solution.py:165
  104.4 1.9 %fusion.175 = (f32[512]{0:T(512)S(1)}, f32[8,16,512]{2,1,0:T(8,128)S(1)}) fusion(f32[8,16,512]{2,1,0:T(8,128)S(1)} %copy-done.3, f32[8,16,511]{2,1,0:T(8,128)} %get-tuple-element.41, f32[8,16,1]{2,1,0:T(8,128)} %select_n.477, f32[16,512]{1,0:T(8,128)S(1)} %get-tuple-element.69, f32[8,16,512]{2,1,0:T(8,128)S(1)} %get-tuple-element.11, ...), kind=kLoop, calls=%fused_computation.307 | loop fusion | flops 2096640 | bytes 4065280 | tf_op jit(solution)/shard_map/reduce_sum | solution.py:283
  109.8 6.8 %all-to-all-start.2 = ((f32[32,1,32]{2,1,0:T(1,128)}), f32[32,1,32]{2,1,0:T(1,128)S(1)}, u32[]{:S(2)}, u32[]{:S(2)}) async-start(f32[32,1,32]{2,1,0:T(1,128)} %broadcast_in_dim.35), calls=%async_computation.2 | async-start | bytes 32768 | tf_op jit(solution)/shard_map/all_to_all | solution.py:140
  118.2 3.0 %collective-permute-start.17 = (f32[8,1,512]{2,1,0:T(1,128)S(1)}, f32[8,1,512]{2,1,0:T(1,128)S(1)}, u32[]{:S(2)}, u32[]{:S(2)}) collective-permute-start(f32[8,1,512]{2,1,0:T(1,128)S(1)} %get-tuple-element.31), channel_id=1, source_target_pairs={{0,8},{8,16},{16,24},{24,2},{2,10},{10,18},{18,26},{26,4},{4,12},{... | collective-permute-start | bytes 49160 | tf_op jit(solution)/shard_map/ppermute | solution.py:48
  121.3 2.6 %all-to-all-done.2 = f32[32,1,32]{2,1,0:T(1,128)S(1)} async-done(((f32[32,1,32]{2,1,0:T(1,128)}), f32[32,1,32]{2,1,0:T(1,128)S(1)}, u32[]{:S(2)}, u32[]{:S(2)}) %all-to-all-start.2) | async-done | bytes 4128 | tf_op jit(solution)/shard_map/all_to_all | solution.py:140
  126.5 2.1 %fusion.40 = f32[1,256]{1,0:T(1,128)} fusion(f32[512,1]{0,1:T(1,128)S(1)} %bitcast.225, f32[4,256,512]{2,1,0:T(8,128)} %param.14), kind=kOutput, calls=%fused_computation.52 | convolution fusion | flops 1572864 | bytes 527360 | tf_op jit(solution)/shard_map/dot_general | solution.py:184
  130.0 2.2 %fusion.28 = f32[1,256]{1,0:T(1,128)} fusion(f32[512,1]{0,1:T(1,128)S(1)} %bitcast.223, f32[4,256,512]{2,1,0:T(8,128)} %param.14), kind=kOutput, calls=%fused_computation.40 | convolution fusion | flops 1572864 | bytes 527360 | tf_op jit(solution)/shard_map/dot_general | solution.py:184
  134.5 2.2 %fusion.158 = f32[8,16,512]{2,1,0:T(8,128)S(1)} fusion(f32[8,16,512]{2,1,0:T(8,128)S(1)} %mul.287, f32[8,16,512]{2,1,0:T(8,128)} %copy-done.4, f32[8,16,512]{2,1,0:T(8,128)} %get-tuple-element.12, f32[8,16,511]{2,1,0:T(8,128)} %get-tuple-element.33, f32[8,16,1]{2,1,0:T(8,128)} %select_n.479, f32[8,16,512]{2,1,0:T(8,128)} %copy-done.1, ...), kind=kLoop, calls=%fused_computation.207 | loop fusion | flops 1900544 | bytes 4161536 | tf_op jit(solution)/shard_map/add | solution.py:114
  142.6 2.1 %collective-permute-done.18 = f32[384]{0:T(512)S(1)} collective-permute-done((f32[384]{0:T(512)S(1)}, f32[384]{0:T(512)S(1)}, u32[]{:S(2)}, u32[]{:S(2)}) %collective-permute-start.18) | collective-permute-done | bytes 1568 | tf_op jit(solution)/shard_map/ppermute | solution.py:166
  148.0 1.9 %collective-permute-start.24 = (f32[8,1,512]{2,1,0:T(1,128)}, f32[8,1,512]{2,1,0:T(1,128)}, u32[]{:S(2)}, u32[]{:S(2)}) collective-permute-start(f32[8,1,512]{2,1,0:T(1,128)} %get-tuple-element.22), channel_id=1, source_target_pairs={{0,8},{8,16},{16,24},{24,2},{2,10},{10,18},{18,26},{26,4},{4,12},{... | collective-permute-start | bytes 49160 | tf_op jit(solution)/shard_map/ppermute | solution.py:48
  166.8 2.2 %collective-permute-done.22 = f32[1024]{0:T(1024)S(1)} collective-permute-done((f32[1024]{0:T(1024)S(1)}, f32[1024]{0:T(1024)S(1)}, u32[]{:S(2)}, u32[]{:S(2)}) %collective-permute-start.22) | collective-permute-done | bytes 4128 | tf_op jit(solution)/shard_map/ppermute | solution.py:165
  171.8 3.7 %fusion.121 = f32[8,16,512]{2,1,0:T(8,128)} fusion(f32[8,16,512]{2,1,0:T(8,128)} %copy-done.4, f32[1,16,512]{2,1,0:T(8,128)S(1)} %multiply_bitcast_fusion.1, f32[8,16,512]{2,1,0:T(8,128)} %get-tuple-element.13, f32[8,1,512]{2,1,0:T(1,128)} %collective-permute-done.23, f32[8,15,512]{2,1,0:T(8,128)} %get-tuple-element.25, ...), kind=kLoop, calls=%fused_computation.133 | loop fusion | flops 3997696 | bytes 5996544 | tf_op jit(solution)/shard_map/add | solution.py:299
  175.6 4.3 %all-to-all-start.3 = ((f32[8,16,512]{2,1,0:T(8,128)}), f32[8,16,512]{2,1,0:T(8,128)S(1)}, u32[]{:S(2)}, u32[]{:S(2)}) async-start(f32[8,16,512]{2,1,0:T(8,128)} %fusion.121), calls=%async_computation.3 | async-start | bytes 524288 | tf_op jit(solution)/shard_map/all_to_all | solution.py:311
  180.4 5.4 %all-to-all-done.3 = f32[8,16,512]{2,1,0:T(8,128)S(1)} async-done(((f32[8,16,512]{2,1,0:T(8,128)}), f32[8,16,512]{2,1,0:T(8,128)S(1)}, u32[]{:S(2)}, u32[]{:S(2)}) %all-to-all-start.3) | async-done | bytes 262176 | tf_op jit(solution)/shard_map/all_to_all | solution.py:311
  (249 shorter events, 84.8 us)
Async XLA Ops:
  4.3 15.9 %all-to-all-start = ((f32[3,2,64,512]{3,1,0,2:T(2,128)}), f32[3,2,64,512]{3,1,0,2:T(2,128)S(1)}, u32[]{:S(2)}, u32[]{:S(2)}) async-start(f32[3,2,64,512]{3,1,0,2:T(2,128)} %copy.52), calls=%async_computation | async-start | bytes 1572864 | tf_op jit(solution)/shard_map/all_to_all | solution.py:235
  9.3 90.2 %copy-start.10 = (s32[1,4,4,128]{3,1,2,0:T(4,128)}, s32[1,4,4,128]{3,1,2,0:T(4,128)S(1)}, u32[]{:S(2)}) copy-start(s32[1,4,4,128]{3,1,2,0:T(4,128)S(1)} %copy.67) | copy-start | bytes 24580
  10.7 28.5 %copy-start.14 = (s32[2048]{0:T(1024)}, s32[2048]{0:T(1024)S(1)}, u32[]{:S(2)}) copy-start(s32[2048]{0:T(1024)S(1)} %get-tuple-element.85) | copy-start | bytes 24580
  23.3 16.0 %all-to-all-start.1 = ((f32[32,1,32]{2,1,0:T(1,128)}), f32[32,1,32]{2,1,0:T(1,128)S(1)}, u32[]{:S(2)}, u32[]{:S(2)}) async-start(f32[32,1,32]{2,1,0:T(1,128)} %broadcast_in_dim.27), calls=%async_computation.1 | async-start | bytes 32768 | tf_op jit(solution)/shard_map/all_to_all | solution.py:140
  29.6 13.2 %collective-permute-start = (f32[8,1,512]{2,1,0:T(1,128)S(1)}, f32[8,1,512]{2,1,0:T(1,128)S(1)}, u32[]{:S(2)}, u32[]{:S(2)}) collective-permute-start(f32[8,1,512]{2,1,0:T(1,128)S(1)} %get-tuple-element.60), channel_id=1, source_target_pairs={{8,0},{16,8},{24,16},{2,24},{10,2},{18,10},{26,18},{4,26},{12,4},{... | collective-permute-start | bytes 49160 | tf_op jit(solution)/shard_map/ppermute | solution.py:49
  30.9 12.0 %collective-permute-start.1 = (f32[8,1,512]{2,1,0:T(1,128)S(1)}, f32[8,1,512]{2,1,0:T(1,128)S(1)}, u32[]{:S(2)}, u32[]{:S(2)}) collective-permute-start(f32[8,1,512]{2,1,0:T(1,128)S(1)} %get-tuple-element.61), channel_id=1, source_target_pairs={{0,8},{8,16},{16,24},{24,2},{2,10},{10,18},{18,26},{26,4},{4,12},{... | collective-permute-start | bytes 49160 | tf_op jit(solution)/shard_map/ppermute | solution.py:48
  34.1 4.5 %collective-permute-start.2 = (f32[8,16,1]{2,1,0:T(8,128)S(1)}, f32[8,16,1]{2,1,0:T(8,128)S(1)}, u32[]{:S(2)}, u32[]{:S(2)}) collective-permute-start(f32[8,16,1]{2,1,0:T(8,128)S(1)} %slice_select_fusion.5), channel_id=1, source_target_pairs={{0,1},{1,0},{2,3},{3,2},{4,5},{5,4},{6,7},{7,6},{8,9},{9,8},{10,11... | collective-permute-start | bytes 1544 | tf_op jit(solution)/shard_map/ppermute | solution.py:45
  45.7 58.8 %copy-start.1 = (f32[8,16,512]{2,1,0:T(8,128)}, f32[8,16,512]{2,1,0:T(8,128)S(1)}, u32[]{:S(2)}) copy-start(f32[8,16,512]{2,1,0:T(8,128)S(1)} %get-tuple-element.11) | copy-start | bytes 786436
  48.5 6.3 %collective-permute-start.3 = (f32[384]{0:T(512)S(1)}, f32[384]{0:T(512)S(1)}, u32[]{:S(2)}, u32[]{:S(2)}) collective-permute-start(f32[384]{0:T(512)S(1)} %pad_maximum_fusion.4), channel_id=1, source_target_pairs={{0,1},{1,0},{2,3},{3,2},{4,5},{5,4},{6,7},{7,6},{8,9},{9,8},{10,11... | collective-permute-start | bytes 4616 | tf_op jit(solution)/shard_map/ppermute | solution.py:166
  50.5 7.5 %collective-permute-start.4 = (f32[8,1,512]{2,1,0:T(1,128)S(1)}, f32[8,1,512]{2,1,0:T(1,128)S(1)}, u32[]{:S(2)}, u32[]{:S(2)}) collective-permute-start(f32[8,1,512]{2,1,0:T(1,128)S(1)} %get-tuple-element.54), channel_id=1, source_target_pairs={{8,0},{16,8},{24,16},{2,24},{10,2},{18,10},{26,18},{4,26},{12,4},{... | collective-permute-start | bytes 49160 | tf_op jit(solution)/shard_map/ppermute | solution.py:49
  51.8 6.3 %collective-permute-start.5 = (f32[8,1,512]{2,1,0:T(1,128)S(1)}, f32[8,1,512]{2,1,0:T(1,128)S(1)}, u32[]{:S(2)}, u32[]{:S(2)}) collective-permute-start(f32[8,1,512]{2,1,0:T(1,128)S(1)} %get-tuple-element.55), channel_id=1, source_target_pairs={{0,8},{8,16},{16,24},{24,2},{2,10},{10,18},{18,26},{26,4},{4,12},{... | collective-permute-start | bytes 49160 | tf_op jit(solution)/shard_map/ppermute | solution.py:48
  63.6 5.1 %collective-permute-start.6 = (f32[384]{0:T(512)S(1)}, f32[384]{0:T(512)S(1)}, u32[]{:S(2)}, u32[]{:S(2)}) collective-permute-start(f32[384]{0:T(512)S(1)} %pad_maximum_fusion.5), channel_id=1, source_target_pairs={{0,1},{1,0},{2,3},{3,2},{4,5},{5,4},{6,7},{7,6},{8,9},{9,8},{10,11... | collective-permute-start | bytes 4616 | tf_op jit(solution)/shard_map/ppermute | solution.py:166
  64.5 8.1 %collective-permute-start.8 = (f32[8,1,512]{2,1,0:T(1,128)}, f32[8,1,512]{2,1,0:T(1,128)S(1)}, u32[]{:S(2)}, u32[]{:S(2)}) collective-permute-start(f32[8,1,512]{2,1,0:T(1,128)} %get-tuple-element.46), channel_id=1, source_target_pairs={{0,8},{8,16},{16,24},{24,2},{2,10},{10,18},{18,26},{26,4},{4,12},{... | collective-permute-start | bytes 49160 | tf_op jit(solution)/shard_map/ppermute | solution.py:48
  67.4 5.1 %collective-permute-start.7 = (f32[8,1,512]{2,1,0:T(1,128)}, f32[8,1,512]{2,1,0:T(1,128)S(1)}, u32[]{:S(2)}, u32[]{:S(2)}) collective-permute-start(f32[8,1,512]{2,1,0:T(1,128)} %get-tuple-element.47), channel_id=1, source_target_pairs={{8,0},{16,8},{24,16},{2,24},{10,2},{18,10},{26,18},{4,26},{12,4},{... | collective-permute-start | bytes 49160 | tf_op jit(solution)/shard_map/ppermute | solution.py:49
  77.5 8.0 %collective-permute-start.9 = (f32[384]{0:T(512)S(1)}, f32[384]{0:T(512)S(1)}, u32[]{:S(2)}, u32[]{:S(2)}) collective-permute-start(f32[384]{0:T(512)S(1)} %pad_maximum_fusion.6), channel_id=1, source_target_pairs={{0,1},{1,0},{2,3},{3,2},{4,5},{5,4},{6,7},{7,6},{8,9},{9,8},{10,11... | collective-permute-start | bytes 4616 | tf_op jit(solution)/shard_map/ppermute | solution.py:166
  79.9 24.5 %collective-permute-start.13 = (f32[8,1,512]{2,1,0:T(1,128)}, f32[8,1,512]{2,1,0:T(1,128)}, u32[]{:S(2)}, u32[]{:S(2)}) collective-permute-start(f32[8,1,512]{2,1,0:T(1,128)} %get-tuple-element.38), channel_id=1, source_target_pairs={{8,0},{16,8},{24,16},{2,24},{10,2},{18,10},{26,18},{4,26},{12,4},{... | collective-permute-start | bytes 49160 | tf_op jit(solution)/shard_map/ppermute | solution.py:49
  81.2 23.2 %collective-permute-start.14 = (f32[8,1,512]{2,1,0:T(1,128)}, f32[8,1,512]{2,1,0:T(1,128)}, u32[]{:S(2)}, u32[]{:S(2)}) collective-permute-start(f32[8,1,512]{2,1,0:T(1,128)} %get-tuple-element.39), channel_id=1, source_target_pairs={{0,8},{8,16},{16,24},{24,2},{2,10},{10,18},{18,26},{26,4},{4,12},{... | collective-permute-start | bytes 49160 | tf_op jit(solution)/shard_map/ppermute | solution.py:48
  87.6 3.6 %collective-permute-start.10 = (f32[512]{0:T(512)S(1)}, f32[512]{0:T(512)S(1)}, u32[]{:S(2)}, u32[]{:S(2)}) collective-permute-start(f32[512]{0:T(512)S(1)} %pad_maximum_fusion.7), channel_id=1, source_target_pairs={{0,1},{1,0},{2,3},{3,2},{4,5},{5,4},{6,7},{7,6},{8,9},{9,8},{10,11... | collective-permute-start | bytes 6152 | tf_op jit(solution)/shard_map/ppermute | solution.py:165
  91.7 3.6 %collective-permute-start.11 = (f32[512]{0:T(512)S(1)}, f32[512]{0:T(512)S(1)}, u32[]{:S(2)}, u32[]{:S(2)}) collective-permute-start(f32[512]{0:T(512)S(1)} %pad_maximum_fusion.8), channel_id=1, source_target_pairs={{0,1},{1,0},{2,3},{3,2},{4,5},{5,4},{6,7},{7,6},{8,9},{9,8},{10,11... | collective-permute-start | bytes 6152 | tf_op jit(solution)/shard_map/ppermute | solution.py:165
  95.8 3.7 %collective-permute-start.12 = (f32[1024]{0:T(1024)S(1)}, f32[1024]{0:T(1024)S(1)}, u32[]{:S(2)}, u32[]{:S(2)}) collective-permute-start(f32[1024]{0:T(1024)S(1)} %pad_maximum_fusion.2), channel_id=1, source_target_pairs={{0,1},{1,0},{2,3},{3,2},{4,5},{5,4},{6,7},{7,6},{8,9},{9,8},{10,11... | collective-permute-start | bytes 12296 | tf_op jit(solution)/shard_map/ppermute | solution.py:165
  109.8 14.0 %all-to-all-start.2 = ((f32[32,1,32]{2,1,0:T(1,128)}), f32[32,1,32]{2,1,0:T(1,128)S(1)}, u32[]{:S(2)}, u32[]{:S(2)}) async-start(f32[32,1,32]{2,1,0:T(1,128)} %broadcast_in_dim.35), calls=%async_computation.2 | async-start | bytes 32768 | tf_op jit(solution)/shard_map/all_to_all | solution.py:140
  116.9 17.0 %collective-permute-start.16 = (f32[8,1,512]{2,1,0:T(1,128)S(1)}, f32[8,1,512]{2,1,0:T(1,128)S(1)}, u32[]{:S(2)}, u32[]{:S(2)}) collective-permute-start(f32[8,1,512]{2,1,0:T(1,128)S(1)} %get-tuple-element.30), channel_id=1, source_target_pairs={{8,0},{16,8},{24,16},{2,24},{10,2},{18,10},{26,18},{4,26},{12,4},{... | collective-permute-start | bytes 49160 | tf_op jit(solution)/shard_map/ppermute | solution.py:49
  118.2 15.7 %collective-permute-start.17 = (f32[8,1,512]{2,1,0:T(1,128)S(1)}, f32[8,1,512]{2,1,0:T(1,128)S(1)}, u32[]{:S(2)}, u32[]{:S(2)}) collective-permute-start(f32[8,1,512]{2,1,0:T(1,128)S(1)} %get-tuple-element.31), channel_id=1, source_target_pairs={{0,8},{8,16},{16,24},{24,2},{2,10},{10,18},{18,26},{26,4},{4,12},{... | collective-permute-start | bytes 49160 | tf_op jit(solution)/shard_map/ppermute | solution.py:48
  125.9 3.6 %collective-permute-start.15 = (f32[384]{0:T(512)S(1)}, f32[384]{0:T(512)S(1)}, u32[]{:S(2)}, u32[]{:S(2)}) collective-permute-start(f32[384]{0:T(512)S(1)} %pad_maximum_fusion.9), channel_id=1, source_target_pairs={{0,1},{1,0},{2,3},{3,2},{4,5},{5,4},{6,7},{7,6},{8,9},{9,8},{10,11... | collective-permute-start | bytes 4616 | tf_op jit(solution)/shard_map/ppermute | solution.py:166
  141.2 3.6 %collective-permute-start.18 = (f32[384]{0:T(512)S(1)}, f32[384]{0:T(512)S(1)}, u32[]{:S(2)}, u32[]{:S(2)}) collective-permute-start(f32[384]{0:T(512)S(1)} %pad_maximum_fusion.10), channel_id=1, source_target_pairs={{0,1},{1,0},{2,3},{3,2},{4,5},{5,4},{6,7},{7,6},{8,9},{9,8},{10,11... | collective-permute-start | bytes 4616 | tf_op jit(solution)/shard_map/ppermute | solution.py:166
  146.8 4.4 %collective-permute-start.19 = (f32[256]{0:T(256)S(1)}, f32[256]{0:T(256)S(1)}, u32[]{:S(2)}, u32[]{:S(2)}) collective-permute-start(f32[256]{0:T(256)S(1)} %dynamic-slice_subtract_fusion), channel_id=1, source_target_pairs={{0,1},{1,0},{2,3},{3,2},{4,5},{5,4},{6,7},{7,6},{8,9},{9,8},{10,11... | collective-permute-start | bytes 3080 | tf_op jit(solution)/shard_map/ppermute | solution.py:165
  148.0 23.8 %collective-permute-start.24 = (f32[8,1,512]{2,1,0:T(1,128)}, f32[8,1,512]{2,1,0:T(1,128)}, u32[]{:S(2)}, u32[]{:S(2)}) collective-permute-start(f32[8,1,512]{2,1,0:T(1,128)} %get-tuple-element.22), channel_id=1, source_target_pairs={{0,8},{8,16},{16,24},{24,2},{2,10},{10,18},{18,26},{26,4},{4,12},{... | collective-permute-start | bytes 49160 | tf_op jit(solution)/shard_map/ppermute | solution.py:48
  149.9 21.9 %collective-permute-start.23 = (f32[8,1,512]{2,1,0:T(1,128)}, f32[8,1,512]{2,1,0:T(1,128)}, u32[]{:S(2)}, u32[]{:S(2)}) collective-permute-start(f32[8,1,512]{2,1,0:T(1,128)} %get-tuple-element.23), channel_id=1, source_target_pairs={{8,0},{16,8},{24,16},{2,24},{10,2},{18,10},{26,18},{4,26},{12,4},{... | collective-permute-start | bytes 49160 | tf_op jit(solution)/shard_map/ppermute | solution.py:49
  153.2 3.6 %collective-permute-start.20 = (f32[512]{0:T(512)S(1)}, f32[512]{0:T(512)S(1)}, u32[]{:S(2)}, u32[]{:S(2)}) collective-permute-start(f32[512]{0:T(512)S(1)} %pad_maximum_fusion.11), channel_id=1, source_target_pairs={{0,1},{1,0},{2,3},{3,2},{4,5},{5,4},{6,7},{7,6},{8,9},{9,8},{10,11... | collective-permute-start | bytes 6152 | tf_op jit(solution)/shard_map/ppermute | solution.py:165
  158.6 5.0 %collective-permute-start.21 = (f32[512]{0:T(512)}, f32[512]{0:T(512)}, u32[]{:S(2)}, u32[]{:S(2)}) collective-permute-start(f32[512]{0:T(512)} %pad_maximum_fusion.12), channel_id=1, source_target_pairs={{0,1},{1,0},{2,3},{3,2},{4,5},{5,4},{6,7},{7,6},{8,9},{9,8},{10,11... | collective-permute-start | bytes 6152 | tf_op jit(solution)/shard_map/ppermute | solution.py:165
  165.4 3.6 %collective-permute-start.22 = (f32[1024]{0:T(1024)S(1)}, f32[1024]{0:T(1024)S(1)}, u32[]{:S(2)}, u32[]{:S(2)}) collective-permute-start(f32[1024]{0:T(1024)S(1)} %pad_maximum_fusion.3), channel_id=1, source_target_pairs={{0,1},{1,0},{2,3},{3,2},{4,5},{5,4},{6,7},{7,6},{8,9},{9,8},{10,11... | collective-permute-start | bytes 12296 | tf_op jit(solution)/shard_map/ppermute | solution.py:165
  175.6 10.3 %all-to-all-start.3 = ((f32[8,16,512]{2,1,0:T(8,128)}), f32[8,16,512]{2,1,0:T(8,128)S(1)}, u32[]{:S(2)}, u32[]{:S(2)}) async-start(f32[8,16,512]{2,1,0:T(8,128)} %fusion.121), calls=%async_computation.3 | async-start | bytes 524288 | tf_op jit(solution)/shard_map/all_to_all | solution.py:311
  (20 other events, 187.5 us)

commit v8 on v6

--- a/solution.py
+++ b/solution.py
@@ -185,8 +185,9 @@
 def shards(sources, conduct, via_cond, via_map, pad_map, port_tile, pivots, coupling):
     layer_count = lax.axis_size("layer")
     vertical = via_cond * via_map.astype(jnp.float32)
-    packed = lax.all_to_all(jnp.stack((sources, conduct, vertical)), "layer", 2, 1, tiled=True)
-    sources, conduct, vertical = packed[0], packed[1], packed[2]
+    packed = lax.all_to_all(jnp.stack((conduct, vertical)), "layer", 2, 1, tiled=True)
+    conduct, vertical = packed[0], packed[1]
+    sources = lax.all_to_all(sources, "layer", 1, 0, tiled=True)
     local_layers, grid_rows, grid_cols = sources.shape
     pad_rows = lax.dynamic_slice_in_dim(pad_map, lax.axis_index("layer") * grid_rows, grid_rows, 0)
     row_halo = rims(conduct, ROW_AXES, 1)

time: 171 us -> 169 us (0.988)
  waiting for transfers between devices: 48.8 us -> 53.7 us
  other arithmetic: 17.6 us -> 12.8 us
  local copies, waits for them, and re-layouts: 24.1 us -> 19.6 us
  starting transfers between devices: 64.3 us -> 67.3 us
    all_to_all x1 -> x2, waiting for transfers between devices: 10.6 us -> 4.06 us  [the longest x1 4.06 us: shards(): sources = lax.all_to_all(sources, 'layer', 1, 0, tiled=True)]
    all_to_all x2, waiting for transfers between devices: 6.51 us -> 12.1 us  [share_tiles(): got = lax.all_to_all(payload, ('layer', 'row', 'col'), 0, 0, tiled=True)]
    all_to_all x1 -> x2, starting transfers between devices: 4.24 us -> 7.71 us  [the longest x1 4.24 us: shards(): sources = lax.all_to_all(sources, 'layer', 1, 0, tiled=True)]
    slice x12, local copies, waits for them, and re-layouts: 7.01 us -> 3.94 us  [neighbours(): lax.slice_in_dim(field, 1, size, axis=dim)]
    unnamed x99 -> x82, local copies, waits for them, and re-layouts: 0.23 us -> 2.79 us
    ppermute x6, waiting for transfers between devices: 1.57 us -> 3.83 us  [rims(): lax.ppermute(head, axis, [(place[i + 1], place[i]) for i in range(count -...]
    ppermute x6, waiting for transfers between devices: 3.54 us -> 5.76 us  [rims(): got = lax.ppermute(jnp.where(low, tail, head), axis, [(0, 1), (1, 0)])]
    ppermute x12, starting transfers between devices: 5.71 us -> 7.84 us  [swap_col(): return lax.ppermute(value, 'col', [(0, 1), (1, 0)])]
  transfers between devices with their start and end apart: 34 -> 35, of which waited for: 17 -> 19; matrix products, arithmetic and copies ran while one was open for 21% -> 18% of each run, Pallas kernels for 0% -> 0%
where the time goes in v8:
time: 169 us; the launch traced here: 168 us
  starting transfers between devices  67.3 us (40%)
  waiting for transfers between devices  53.7 us (32%)
  local copies, waits for them, and re-layouts  19.6 us (12%)
  matrix products  13 us (8%)
  other arithmetic  12.8 us (8%)
  between operations  1.79 us (1%)
    ppermute x12, waiting for transfers between devices, swap_col(): return lax.ppermute(value, 'col', [(0, 1), (1, 0)])  21.6 us
    ppermute x6, starting transfers between devices, rims(): lax.ppermute(tail, axis, [(place[i], place[i + 1]) for i in range(count -...  19 us
    all_to_all x2, starting transfers between devices, share_tiles(): got = lax.all_to_all(payload, ('layer', 'row', 'col'), 0, 0, tiled=True)  14.2 us
    all_to_all x2, waiting for transfers between devices, share_tiles(): got = lax.all_to_all(payload, ('layer', 'row', 'col'), 0, 0, tiled=True)  12.1 us
    ppermute x6, starting transfers between devices, rims(): lax.ppermute(head, axis, [(place[i + 1], place[i]) for i in range(count -...  7.87 us
    ppermute x12, starting transfers between devices, swap_col(): return lax.ppermute(value, 'col', [(0, 1), (1, 0)])  7.84 us
    ppermute x6, starting transfers between devices, rims(): got = lax.ppermute(jnp.where(low, tail, head), axis, [(0, 1), (1, 0)])  6.36 us
    ppermute x6, waiting for transfers between devices, rims(): got = lax.ppermute(jnp.where(low, tail, head), axis, [(0, 1), (1, 0)])  5.76 us
  transfers between devices with their start and end apart: 35, of which 19 were waited for; matrix products, arithmetic and copies ran while one was open for 18% of the time, Pallas kernels for 0%

profile of v8, /device:TPU:0, one launch (start us, length us, event | category | flops | bytes accessed | tf_op | source)
XLA Modules:
  0.0 168.2 jit_solution(18184637643003525990)
XLA Ops:
  0.6 1.9 %copy.24 = f32[2,64,512]{2,0,1:T(2,128)} copy(f32[2,64,512]{2,1,0:T(8,128)} %param.8) | data formatting | bytes 524288 | tf_op args[0]
  2.5 4.2 %all-to-all-start = ((f32[2,64,512]{2,0,1:T(2,128)}), f32[2,64,512]{2,0,1:T(2,128)S(1)}, u32[]{:S(2)}, u32[]{:S(2)}) async-start(f32[2,64,512]{2,0,1:T(2,128)} %copy.24), calls=%async_computation | async-start | bytes 524288 | tf_op jit(solution)/shard_map/all_to_all | solution.py:190
  8.7 4.1 %all-to-all-done = f32[2,64,512]{2,0,1:T(2,128)S(1)} async-done(((f32[2,64,512]{2,0,1:T(2,128)}), f32[2,64,512]{2,0,1:T(2,128)S(1)}, u32[]{:S(2)}, u32[]{:S(2)}) %all-to-all-start) | async-done | bytes 262176 | tf_op jit(solution)/shard_map/all_to_all | solution.py:190
  13.7 5.5 %all-to-all-start.1 = ((f32[32,1,32]{2,1,0:T(1,128)}), f32[32,1,32]{2,1,0:T(1,128)S(1)}, u32[]{:S(2)}, u32[]{:S(2)}) async-start(f32[32,1,32]{2,1,0:T(1,128)} %broadcast_in_dim.27), calls=%async_computation.1 | async-start | bytes 32768 | tf_op jit(solution)/shard_map/all_to_all | solution.py:106
  20.5 5.8 %all-to-all-done.1 = f32[32,1,32]{2,1,0:T(1,128)S(1)} async-done(((f32[32,1,32]{2,1,0:T(1,128)}), f32[32,1,32]{2,1,0:T(1,128)S(1)}, u32[]{:S(2)}, u32[]{:S(2)}) %all-to-all-start.1) | async-done | bytes 4128 | tf_op jit(solution)/shard_map/all_to_all | solution.py:106
  26.3 3.5 %all-to-all-start.2 = ((f32[2,2,64,512]{3,1,0,2:T(2,128)}), f32[2,2,64,512]{3,1,0,2:T(2,128)S(1)}, u32[]{:S(2)}, u32[]{:S(2)}) async-start(f32[2,2,64,512]{3,1,0,2:T(2,128)} %copy.25), calls=%async_computation.2 | async-start | bytes 1048576 | tf_op jit(solution)/shard_map/all_to_all | solution.py:188
  36.1 1.5 fusion.42
  40.8 2.4 %collective-permute-done.2 = f32[256]{0:T(256)S(1)} collective-permute-done((f32[256]{0:T(256)S(1)}, f32[256]{0:T(256)S(1)}, u32[]{:S(2)}, u32[]{:S(2)}) %collective-permute-start.2) | collective-permute-done | bytes 1056 | tf_op jit(solution)/shard_map/ppermute | solution.py:118
  45.4 2.5 %collective-permute-done.3 = f32[512]{0:T(512)S(1)} collective-permute-done((f32[512]{0:T(512)S(1)}, f32[512]{0:T(512)S(1)}, u32[]{:S(2)}, u32[]{:S(2)}) %collective-permute-start.3) | collective-permute-done | bytes 2080 | tf_op jit(solution)/shard_map/ppermute | solution.py:118
  49.0 3.0 %collective-permute-done.4 = f32[512]{0:T(512)S(1)} collective-permute-done((f32[512]{0:T(512)S(1)}, f32[512]{0:T(512)S(1)}, u32[]{:S(2)}, u32[]{:S(2)}) %collective-permute-start.4) | collective-permute-done | bytes 2080 | tf_op jit(solution)/shard_map/ppermute | solution.py:118
  53.1 3.0 %collective-permute-done.5 = f32[1024]{0:T(1024)S(1)} collective-permute-done((f32[1024]{0:T(1024)S(1)}, f32[1024]{0:T(1024)S(1)}, u32[]{:S(2)}, u32[]{:S(2)}) %collective-permute-start.5) | collective-permute-done | bytes 4128 | tf_op jit(solution)/shard_map/ppermute | solution.py:118
  58.5 1.4 collective-permute-start.6
  59.9 3.0 %collective-permute-start.7 = (f32[8,1,512]{2,1,0:T(1,128)S(1)}, f32[8,1,512]{2,1,0:T(1,128)S(1)}, u32[]{:S(2)}, u32[]{:S(2)}) collective-permute-start(f32[8,1,512]{2,1,0:T(1,128)S(1)} %get-tuple-element.59), channel_id=1, source_target_pairs={{0,8},{8,16},{16,24},{24,2},{2,10},{10,18},{18,26},{26,4},{4,12},{... | collective-permute-start | bytes 49160 | tf_op jit(solution)/shard_map/ppermute | solution.py:48
  63.8 3.6 %collective-permute-done.8 = f32[8,16,1]{2,1,0:T(8,128)S(1)} collective-permute-done((f32[8,16,1]{2,1,0:T(8,128)S(1)}, f32[8,16,1]{2,1,0:T(8,128)S(1)}, u32[]{:S(2)}, u32[]{:S(2)}) %collective-permute-start.8) | collective-permute-done | bytes 544 | tf_op jit(solution)/shard_map/ppermute | solution.py:45
  70.4 3.0 %collective-permute-start.10 = (f32[8,1,512]{2,1,0:T(1,128)S(1)}, f32[8,1,512]{2,1,0:T(1,128)S(1)}, u32[]{:S(2)}, u32[]{:S(2)}) collective-permute-start(f32[8,1,512]{2,1,0:T(1,128)S(1)} %get-tuple-element.53), channel_id=1, source_target_pairs={{0,8},{8,16},{16,24},{24,2},{2,10},{10,18},{18,26},{26,4},{4,12},{... | collective-permute-start | bytes 49160 | tf_op jit(solution)/shard_map/ppermute | solution.py:48
  75.0 1.5 collective-permute-start.14
  76.5 3.2 %collective-permute-start.13 = (f32[8,1,512]{2,1,0:T(1,128)S(1)}, f32[8,1,512]{2,1,0:T(1,128)S(1)}, u32[]{:S(2)}, u32[]{:S(2)}) collective-permute-start(f32[8,1,512]{2,1,0:T(1,128)S(1)} %get-tuple-element.44), channel_id=1, source_target_pairs={{0,8},{8,16},{16,24},{24,2},{2,10},{10,18},{18,26},{26,4},{4,12},{... | collective-permute-start | bytes 49160 | tf_op jit(solution)/shard_map/ppermute | solution.py:48
  81.1 3.8 %collective-permute-done.12 = f32[8,1,512]{2,1,0:T(1,128)S(1)} collective-permute-done((f32[8,1,512]{2,1,0:T(1,128)S(1)}, f32[8,1,512]{2,1,0:T(1,128)S(1)}, u32[]{:S(2)}, u32[]{:S(2)}) %collective-permute-start.12) | collective-permute-done | bytes 16416 | tf_op jit(solution)/shard_map/ppermute | solution.py:49
  87.8 4.7 %collective-permute-start.16 = (f32[8,1,512]{2,1,0:T(1,128)S(1)}, f32[8,1,512]{2,1,0:T(1,128)S(1)}, u32[]{:S(2)}, u32[]{:S(2)}) collective-permute-start(f32[8,1,512]{2,1,0:T(1,128)S(1)} %get-tuple-element.37), channel_id=1, source_target_pairs={{0,8},{8,16},{16,24},{24,2},{2,10},{10,18},{18,26},{26,4},{4,12},{... | collective-permute-start | bytes 49160 | tf_op jit(solution)/shard_map/ppermute | solution.py:48
  97.3 8.6 %all-to-all-start.3 = ((f32[32,1,32]{2,1,0:T(1,128)}), f32[32,1,32]{2,1,0:T(1,128)S(1)}, u32[]{:S(2)}, u32[]{:S(2)}) async-start(f32[32,1,32]{2,1,0:T(1,128)} %broadcast_in_dim.35), calls=%async_computation.3 | async-start | bytes 32768 | tf_op jit(solution)/shard_map/all_to_all | solution.py:106
  106.6 6.3 %all-to-all-done.3 = f32[32,1,32]{2,1,0:T(1,128)S(1)} async-done(((f32[32,1,32]{2,1,0:T(1,128)}), f32[32,1,32]{2,1,0:T(1,128)S(1)}, u32[]{:S(2)}, u32[]{:S(2)}) %all-to-all-start.3) | async-done | bytes 4128 | tf_op jit(solution)/shard_map/all_to_all | solution.py:106
  116.5 3.0 %collective-permute-start.25 = (f32[8,1,512]{2,1,0:T(1,128)}, f32[8,1,512]{2,1,0:T(1,128)S(1)}, u32[]{:S(2)}, u32[]{:S(2)}) collective-permute-start(f32[8,1,512]{2,1,0:T(1,128)} %get-tuple-element.29), channel_id=1, source_target_pairs={{0,8},{8,16},{16,24},{24,2},{2,10},{10,18},{18,26},{26,4},{4,12},{... | collective-permute-start | bytes 49160 | tf_op jit(solution)/shard_map/ppermute | solution.py:48
  119.5 1.5 collective-permute-start.26
  122.2 2.1 %collective-permute-done.26 = f32[8,16,1]{2,1,0:T(8,128)S(1)} collective-permute-done((f32[8,16,1]{2,1,0:T(8,128)S(1)}, f32[8,16,1]{2,1,0:T(8,128)S(1)}, u32[]{:S(2)}, u32[]{:S(2)}) %collective-permute-start.26) | collective-permute-done | bytes 544 | tf_op jit(solution)/shard_map/ppermute | solution.py:45
  126.9 2.4 %collective-permute-done.20 = f32[256]{0:T(256)S(1)} collective-permute-done((f32[256]{0:T(256)S(1)}, f32[256]{0:T(256)S(1)}, u32[]{:S(2)}, u32[]{:S(2)}) %collective-permute-start.20) | collective-permute-done | bytes 1056 | tf_op jit(solution)/shard_map/ppermute | solution.py:118
  131.6 2.4 %collective-permute-done.21 = f32[512]{0:T(512)S(1)} collective-permute-done((f32[512]{0:T(512)S(1)}, f32[512]{0:T(512)S(1)}, u32[]{:S(2)}, u32[]{:S(2)}) %collective-permute-start.21) | collective-permute-done | bytes 2080 | tf_op jit(solution)/shard_map/ppermute | solution.py:118
  135.7 2.4 %collective-permute-done.22 = f32[512]{0:T(512)S(1)} collective-permute-done((f32[512]{0:T(512)S(1)}, f32[512]{0:T(512)S(1)}, u32[]{:S(2)}, u32[]{:S(2)}) %collective-permute-start.22) | collective-permute-done | bytes 2080 | tf_op jit(solution)/shard_map/ppermute | solution.py:118
  144.7 2.0 %collective-permute-start.28 = (f32[8,1,512]{2,1,0:T(1,128)}, f32[8,1,512]{2,1,0:T(1,128)}, u32[]{:S(2)}, u32[]{:S(2)}) collective-permute-start(f32[8,1,512]{2,1,0:T(1,128)} %get-tuple-element.20), channel_id=1, source_target_pairs={{0,8},{8,16},{16,24},{24,2},{2,10},{10,18},{18,26},{26,4},{4,12},{... | collective-permute-start | bytes 49160 | tf_op jit(solution)/shard_map/ppermute | solution.py:48
  151.0 1.7 %reshape.592 = f32[512,18]{0,1:T(8,128)} reshape(f32[32,16,18]{1,0,2:T(8,128)} %broadcast_in_dim.36) | data formatting | bytes 73728 | tf_op jit(solution)/shard_map/reshape | solution.py:179
  153.8 3.3 %fusion.121 = f32[8,16,512]{2,1,0:T(8,128)} fusion(f32[8,16,512]{2,1,0:T(8,128)S(1)} %copy-done.12, f32[1,16,512]{2,1,0:T(8,128)S(1)} %multiply_bitcast_fusion.1, f32[8,16,512]{2,1,0:T(8,128)S(1)} %copy-done.6, f32[8,1,512]{2,1,0:T(1,128)} %collective-permute-done.27, f32[8,15,512]{2,1,0:T(8,128)} %get-tuple-element.23, ...), kind=kLoop, calls=%fused_computation.133 | loop fusion | flops 3997696 | bytes 5996544 | tf_op jit(solution)/shard_map/add | solution.py:247
  157.1 4.4 %all-to-all-start.4 = ((f32[8,16,512]{2,1,0:T(8,128)}), f32[8,16,512]{2,1,0:T(8,128)S(1)}, u32[]{:S(2)}, u32[]{:S(2)}) async-start(f32[8,16,512]{2,1,0:T(8,128)} %fusion.121), calls=%async_computation.4 | async-start | bytes 524288 | tf_op jit(solution)/shard_map/all_to_all | solution.py:259
  162.7 4.7 %all-to-all-done.4 = f32[8,16,512]{2,1,0:T(8,128)S(1)} async-done(((f32[8,16,512]{2,1,0:T(8,128)}), f32[8,16,512]{2,1,0:T(8,128)S(1)}, u32[]{:S(2)}, u32[]{:S(2)}) %all-to-all-start.4) | async-done | bytes 262176 | tf_op jit(solution)/shard_map/all_to_all | solution.py:259
  (270 shorter events, 59.8 us)
Async XLA Ops:
  2.5 10.2 %all-to-all-start = ((f32[2,64,512]{2,0,1:T(2,128)}), f32[2,64,512]{2,0,1:T(2,128)S(1)}, u32[]{:S(2)}, u32[]{:S(2)}) async-start(f32[2,64,512]{2,0,1:T(2,128)} %copy.24), calls=%async_computation | async-start | bytes 524288 | tf_op jit(solution)/shard_map/all_to_all | solution.py:190
  13.7 12.6 %all-to-all-start.1 = ((f32[32,1,32]{2,1,0:T(1,128)}), f32[32,1,32]{2,1,0:T(1,128)S(1)}, u32[]{:S(2)}, u32[]{:S(2)}) async-start(f32[32,1,32]{2,1,0:T(1,128)} %broadcast_in_dim.27), calls=%async_computation.1 | async-start | bytes 32768 | tf_op jit(solution)/shard_map/all_to_all | solution.py:106
  26.3 31.7 %all-to-all-start.2 = ((f32[2,2,64,512]{3,1,0,2:T(2,128)}), f32[2,2,64,512]{3,1,0,2:T(2,128)S(1)}, u32[]{:S(2)}, u32[]{:S(2)}) async-start(f32[2,2,64,512]{3,1,0,2:T(2,128)} %copy.25), calls=%async_computation.2 | async-start | bytes 1048576 | tf_op jit(solution)/shard_map/all_to_all | solution.py:188
  35.5 3.6 %collective-permute-start.1 = (f32[256]{0:T(256)S(1)}, f32[256]{0:T(256)S(1)}, u32[]{:S(2)}, u32[]{:S(2)}) collective-permute-start(f32[256]{0:T(256)S(1)} %dynamic-slice_subtract_fusion.4), channel_id=1, source_target_pairs={{0,1},{1,0},{2,3},{3,2},{4,5},{5,4},{6,7},{7,6},{8,9},{9,8},{10,11... | collective-permute-start | bytes 3080 | tf_op jit(solution)/shard_map/ppermute | solution.py:118
  39.7 3.6 %collective-permute-start.2 = (f32[256]{0:T(256)S(1)}, f32[256]{0:T(256)S(1)}, u32[]{:S(2)}, u32[]{:S(2)}) collective-permute-start(f32[256]{0:T(256)S(1)} %dynamic-slice_subtract_fusion.3), channel_id=1, source_target_pairs={{0,1},{1,0},{2,3},{3,2},{4,5},{5,4},{6,7},{7,6},{8,9},{9,8},{10,11... | collective-permute-start | bytes 3080 | tf_op jit(solution)/shard_map/ppermute | solution.py:118
  44.2 3.6 %collective-permute-start.3 = (f32[512]{0:T(512)S(1)}, f32[512]{0:T(512)S(1)}, u32[]{:S(2)}, u32[]{:S(2)}) collective-permute-start(f32[512]{0:T(512)S(1)} %pad_maximum_fusion.4), channel_id=1, source_target_pairs={{0,1},{1,0},{2,3},{3,2},{4,5},{5,4},{6,7},{7,6},{8,9},{9,8},{10,11... | collective-permute-start | bytes 6152 | tf_op jit(solution)/shard_map/ppermute | solution.py:118
  48.4 3.6 %collective-permute-start.4 = (f32[512]{0:T(512)S(1)}, f32[512]{0:T(512)S(1)}, u32[]{:S(2)}, u32[]{:S(2)}) collective-permute-start(f32[512]{0:T(512)S(1)} %pad_maximum_fusion.5), channel_id=1, source_target_pairs={{0,1},{1,0},{2,3},{3,2},{4,5},{5,4},{6,7},{7,6},{8,9},{9,8},{10,11... | collective-permute-start | bytes 6152 | tf_op jit(solution)/shard_map/ppermute | solution.py:118
  52.4 3.7 %collective-permute-start.5 = (f32[1024]{0:T(1024)S(1)}, f32[1024]{0:T(1024)S(1)}, u32[]{:S(2)}, u32[]{:S(2)}) collective-permute-start(f32[1024]{0:T(1024)S(1)} %pad_maximum_fusion.2), channel_id=1, source_target_pairs={{0,1},{1,0},{2,3},{3,2},{4,5},{5,4},{6,7},{7,6},{8,9},{9,8},{10,11... | collective-permute-start | bytes 12296 | tf_op jit(solution)/shard_map/ppermute | solution.py:118
  58.5 8.9 %collective-permute-start.6 = (f32[8,1,512]{2,1,0:T(1,128)S(1)}, f32[8,1,512]{2,1,0:T(1,128)S(1)}, u32[]{:S(2)}, u32[]{:S(2)}) collective-permute-start(f32[8,1,512]{2,1,0:T(1,128)S(1)} %get-tuple-element.58), channel_id=1, source_target_pairs={{8,0},{16,8},{24,16},{2,24},{10,2},{18,10},{26,18},{4,26},{12,4},{... | collective-permute-start | bytes 49160 | tf_op jit(solution)/shard_map/ppermute | solution.py:49
  59.9 7.5 %collective-permute-start.7 = (f32[8,1,512]{2,1,0:T(1,128)S(1)}, f32[8,1,512]{2,1,0:T(1,128)S(1)}, u32[]{:S(2)}, u32[]{:S(2)}) collective-permute-start(f32[8,1,512]{2,1,0:T(1,128)S(1)} %get-tuple-element.59), channel_id=1, source_target_pairs={{0,8},{8,16},{16,24},{24,2},{2,10},{10,18},{18,26},{26,4},{4,12},{... | collective-permute-start | bytes 49160 | tf_op jit(solution)/shard_map/ppermute | solution.py:48
  63.0 4.4 %collective-permute-start.8 = (f32[8,16,1]{2,1,0:T(8,128)S(1)}, f32[8,16,1]{2,1,0:T(8,128)S(1)}, u32[]{:S(2)}, u32[]{:S(2)}) collective-permute-start(f32[8,16,1]{2,1,0:T(8,128)S(1)} %slice_select_fusion.5), channel_id=1, source_target_pairs={{0,1},{1,0},{2,3},{3,2},{4,5},{5,4},{6,7},{7,6},{8,9},{9,8},{10,11... | collective-permute-start | bytes 1544 | tf_op jit(solution)/shard_map/ppermute | solution.py:45
  68.3 5.1 %collective-permute-start.11 = (f32[8,16,1]{2,1,0:T(8,128)S(1)}, f32[8,16,1]{2,1,0:T(8,128)S(1)}, u32[]{:S(2)}, u32[]{:S(2)}) collective-permute-start(f32[8,16,1]{2,1,0:T(8,128)S(1)} %slice_select_fusion.4), channel_id=1, source_target_pairs={{0,1},{1,0},{2,3},{3,2},{4,5},{5,4},{6,7},{7,6},{8,9},{9,8},{10,11... | collective-permute-start | bytes 1544 | tf_op jit(solution)/shard_map/ppermute | solution.py:45
  69.1 4.4 %collective-permute-start.9 = (f32[8,1,512]{2,1,0:T(1,128)S(1)}, f32[8,1,512]{2,1,0:T(1,128)S(1)}, u32[]{:S(2)}, u32[]{:S(2)}) collective-permute-start(f32[8,1,512]{2,1,0:T(1,128)S(1)} %get-tuple-element.52), channel_id=1, source_target_pairs={{8,0},{16,8},{24,16},{2,24},{10,2},{18,10},{26,18},{4,26},{12,4},{... | collective-permute-start | bytes 49160 | tf_op jit(solution)/shard_map/ppermute | solution.py:49
  70.4 3.9 %collective-permute-start.10 = (f32[8,1,512]{2,1,0:T(1,128)S(1)}, f32[8,1,512]{2,1,0:T(1,128)S(1)}, u32[]{:S(2)}, u32[]{:S(2)}) collective-permute-start(f32[8,1,512]{2,1,0:T(1,128)S(1)} %get-tuple-element.53), channel_id=1, source_target_pairs={{0,8},{8,16},{16,24},{24,2},{2,10},{10,18},{18,26},{26,4},{4,12},{... | collective-permute-start | bytes 49160 | tf_op jit(solution)/shard_map/ppermute | solution.py:48
  75.0 6.0 %collective-permute-start.14 = (f32[8,16,1]{2,1,0:T(8,128)S(1)}, f32[8,16,1]{2,1,0:T(8,128)S(1)}, u32[]{:S(2)}, u32[]{:S(2)}) collective-permute-start(f32[8,16,1]{2,1,0:T(8,128)S(1)} %slice_select_fusion.3), channel_id=1, source_target_pairs={{0,1},{1,0},{2,3},{3,2},{4,5},{5,4},{6,7},{7,6},{8,9},{9,8},{10,11... | collective-permute-start | bytes 1544 | tf_op jit(solution)/shard_map/ppermute | solution.py:45
  76.5 4.5 %collective-permute-start.13 = (f32[8,1,512]{2,1,0:T(1,128)S(1)}, f32[8,1,512]{2,1,0:T(1,128)S(1)}, u32[]{:S(2)}, u32[]{:S(2)}) collective-permute-start(f32[8,1,512]{2,1,0:T(1,128)S(1)} %get-tuple-element.44), channel_id=1, source_target_pairs={{0,8},{8,16},{16,24},{24,2},{2,10},{10,18},{18,26},{26,4},{4,12},{... | collective-permute-start | bytes 49160 | tf_op jit(solution)/shard_map/ppermute | solution.py:48
  79.7 5.2 %collective-permute-start.12 = (f32[8,1,512]{2,1,0:T(1,128)S(1)}, f32[8,1,512]{2,1,0:T(1,128)S(1)}, u32[]{:S(2)}, u32[]{:S(2)}) collective-permute-start(f32[8,1,512]{2,1,0:T(1,128)S(1)} %get-tuple-element.45), channel_id=1, source_target_pairs={{8,0},{16,8},{24,16},{2,24},{10,2},{18,10},{26,18},{4,26},{12,4},{... | collective-permute-start | bytes 49160 | tf_op jit(solution)/shard_map/ppermute | solution.py:49
  85.8 6.8 %collective-permute-start.17 = (f32[8,16,1]{2,1,0:T(8,128)S(1)}, f32[8,16,1]{2,1,0:T(8,128)S(1)}, u32[]{:S(2)}, u32[]{:S(2)}) collective-permute-start(f32[8,16,1]{2,1,0:T(8,128)S(1)} %slice_select_fusion.2), channel_id=1, source_target_pairs={{0,1},{1,0},{2,3},{3,2},{4,5},{5,4},{6,7},{7,6},{8,9},{9,8},{10,11... | collective-permute-start | bytes 1544 | tf_op jit(solution)/shard_map/ppermute | solution.py:45
  86.5 6.1 %collective-permute-start.15 = (f32[8,1,512]{2,1,0:T(1,128)S(1)}, f32[8,1,512]{2,1,0:T(1,128)S(1)}, u32[]{:S(2)}, u32[]{:S(2)}) collective-permute-start(f32[8,1,512]{2,1,0:T(1,128)S(1)} %get-tuple-element.36), channel_id=1, source_target_pairs={{8,0},{16,8},{24,16},{2,24},{10,2},{18,10},{26,18},{4,26},{12,4},{... | collective-permute-start | bytes 49160 | tf_op jit(solution)/shard_map/ppermute | solution.py:49
  87.8 5.6 %collective-permute-start.16 = (f32[8,1,512]{2,1,0:T(1,128)S(1)}, f32[8,1,512]{2,1,0:T(1,128)S(1)}, u32[]{:S(2)}, u32[]{:S(2)}) collective-permute-start(f32[8,1,512]{2,1,0:T(1,128)S(1)} %get-tuple-element.37), channel_id=1, source_target_pairs={{0,8},{8,16},{16,24},{24,2},{2,10},{10,18},{18,26},{26,4},{4,12},{... | collective-permute-start | bytes 49160 | tf_op jit(solution)/shard_map/ppermute | solution.py:48
  97.3 15.6 %all-to-all-start.3 = ((f32[32,1,32]{2,1,0:T(1,128)}), f32[32,1,32]{2,1,0:T(1,128)S(1)}, u32[]{:S(2)}, u32[]{:S(2)}) async-start(f32[32,1,32]{2,1,0:T(1,128)} %broadcast_in_dim.35), calls=%async_computation.3 | async-start | bytes 32768 | tf_op jit(solution)/shard_map/all_to_all | solution.py:106
  114.4 6.5 %collective-permute-start.18 = (f32[256]{0:T(256)S(1)}, f32[256]{0:T(256)S(1)}, u32[]{:S(2)}, u32[]{:S(2)}) collective-permute-start(f32[256]{0:T(256)S(1)} %dynamic-slice_subtract_fusion.2), channel_id=1, source_target_pairs={{0,1},{1,0},{2,3},{3,2},{4,5},{5,4},{6,7},{7,6},{8,9},{9,8},{10,11... | collective-permute-start | bytes 3080 | tf_op jit(solution)/shard_map/ppermute | solution.py:118
  115.2 24.2 %collective-permute-start.24 = (f32[8,1,512]{2,1,0:T(1,128)}, f32[8,1,512]{2,1,0:T(1,128)S(1)}, u32[]{:S(2)}, u32[]{:S(2)}) collective-permute-start(f32[8,1,512]{2,1,0:T(1,128)} %get-tuple-element.28), channel_id=1, source_target_pairs={{8,0},{16,8},{24,16},{2,24},{10,2},{18,10},{26,18},{4,26},{12,4},{... | collective-permute-start | bytes 49160 | tf_op jit(solution)/shard_map/ppermute | solution.py:49
  116.5 22.9 %collective-permute-start.25 = (f32[8,1,512]{2,1,0:T(1,128)}, f32[8,1,512]{2,1,0:T(1,128)S(1)}, u32[]{:S(2)}, u32[]{:S(2)}) collective-permute-start(f32[8,1,512]{2,1,0:T(1,128)} %get-tuple-element.29), channel_id=1, source_target_pairs={{0,8},{8,16},{16,24},{24,2},{2,10},{10,18},{18,26},{26,4},{4,12},{... | collective-permute-start | bytes 49160 | tf_op jit(solution)/shard_map/ppermute | solution.py:48
  119.5 4.9 %collective-permute-start.26 = (f32[8,16,1]{2,1,0:T(8,128)S(1)}, f32[8,16,1]{2,1,0:T(8,128)S(1)}, u32[]{:S(2)}, u32[]{:S(2)}) collective-permute-start(f32[8,16,1]{2,1,0:T(8,128)S(1)} %slice_select_fusion.1), channel_id=1, source_target_pairs={{0,1},{1,0},{2,3},{3,2},{4,5},{5,4},{6,7},{7,6},{8,9},{9,8},{10,11... | collective-permute-start | bytes 1544 | tf_op jit(solution)/shard_map/ppermute | solution.py:45
  130.4 3.6 %collective-permute-start.21 = (f32[512]{0:T(512)S(1)}, f32[512]{0:T(512)S(1)}, u32[]{:S(2)}, u32[]{:S(2)}) collective-permute-start(f32[512]{0:T(512)S(1)} %pad_maximum_fusion.6), channel_id=1, source_target_pairs={{0,1},{1,0},{2,3},{3,2},{4,5},{5,4},{6,7},{7,6},{8,9},{9,8},{10,11... | collective-permute-start | bytes 6152 | tf_op jit(solution)/shard_map/ppermute | solution.py:118
  134.5 3.6 %collective-permute-start.22 = (f32[512]{0:T(512)S(1)}, f32[512]{0:T(512)S(1)}, u32[]{:S(2)}, u32[]{:S(2)}) collective-permute-start(f32[512]{0:T(512)S(1)} %pad_maximum_fusion.7), channel_id=1, source_target_pairs={{0,1},{1,0},{2,3},{3,2},{4,5},{5,4},{6,7},{7,6},{8,9},{9,8},{10,11... | collective-permute-start | bytes 6152 | tf_op jit(solution)/shard_map/ppermute | solution.py:118
  138.6 10.1 %collective-permute-start.23 = (f32[1024]{0:T(1024)S(1)}, f32[1024]{0:T(1024)S(1)}, u32[]{:S(2)}, u32[]{:S(2)}) collective-permute-start(f32[1024]{0:T(1024)S(1)} %pad_maximum_fusion.3), channel_id=1, source_target_pairs={{0,1},{1,0},{2,3},{3,2},{4,5},{5,4},{6,7},{7,6},{8,9},{9,8},{10,11... | collective-permute-start | bytes 12296 | tf_op jit(solution)/shard_map/ppermute | solution.py:118
  142.7 5.3 %collective-permute-start.29 = (f32[8,16,1]{2,1,0:T(8,128)S(1)}, f32[8,16,1]{2,1,0:T(8,128)S(1)}, u32[]{:S(2)}, u32[]{:S(2)}) collective-permute-start(f32[8,16,1]{2,1,0:T(8,128)S(1)} %slice_select_fusion), channel_id=1, source_target_pairs={{0,1},{1,0},{2,3},{3,2},{4,5},{5,4},{6,7},{7,6},{8,9},{9,8},{10,11... | collective-permute-start | bytes 1544 | tf_op jit(solution)/shard_map/ppermute | solution.py:45
  144.7 9.1 %collective-permute-start.28 = (f32[8,1,512]{2,1,0:T(1,128)}, f32[8,1,512]{2,1,0:T(1,128)}, u32[]{:S(2)}, u32[]{:S(2)}) collective-permute-start(f32[8,1,512]{2,1,0:T(1,128)} %get-tuple-element.20), channel_id=1, source_target_pairs={{0,8},{8,16},{16,24},{24,2},{2,10},{10,18},{18,26},{26,4},{4,12},{... | collective-permute-start | bytes 49160 | tf_op jit(solution)/shard_map/ppermute | solution.py:48
  146.7 7.1 %collective-permute-start.27 = (f32[8,1,512]{2,1,0:T(1,128)}, f32[8,1,512]{2,1,0:T(1,128)}, u32[]{:S(2)}, u32[]{:S(2)}) collective-permute-start(f32[8,1,512]{2,1,0:T(1,128)} %get-tuple-element.21), channel_id=1, source_target_pairs={{8,0},{16,8},{24,16},{2,24},{10,2},{18,10},{26,18},{4,26},{12,4},{... | collective-permute-start | bytes 49160 | tf_op jit(solution)/shard_map/ppermute | solution.py:49
  157.1 10.4 %all-to-all-start.4 = ((f32[8,16,512]{2,1,0:T(8,128)}), f32[8,16,512]{2,1,0:T(8,128)S(1)}, u32[]{:S(2)}, u32[]{:S(2)}) async-start(f32[8,16,512]{2,1,0:T(8,128)} %fusion.121), calls=%async_computation.4 | async-start | bytes 524288 | tf_op jit(solution)/shard_map/all_to_all | solution.py:259
  (42 other events, 485.8 us)

commit v9 on v8

--- a/solution.py
+++ b/solution.py
@@ -152,6 +152,40 @@
     return jnp.stack(results)
 
 
+def coarse_rows(rhs, pivots, coupling):
+    share = pivots.shape[1]
+    low = lax.axis_index("col") == 0
+    start = lax.axis_index("col") * share
+    own = lambda vector: lax.dynamic_slice_in_dim(vector, start, share)
+    forward = [rhs[0]]
+    for section in range(1, NPANEL):
+        forward.append(rhs[section] - jnp.dot(coupling[section - 1], forward[-1], precision=highest))
+    scaled = [jnp.dot(pivots[section], forward[section], precision=highest) for section in range(NPANEL)]
+    results = [None] * NPANEL
+    mine = scaled[NPANEL - 1]
+    for section in range(NPANEL - 2, 0, -1):
+        later = join_halves(mine, swap_col(mine), low)
+        results[section + 1] = later
+        mine = scaled[section] - own(jnp.dot(later, coupling[section], precision=highest))
+    got = swap_col(jnp.concatenate([mine, scaled[0]]))
+    results[1] = join_halves(mine, got[:share], low)
+    first = join_halves(scaled[0], got[share:], low)
+    results[0] = first - jnp.dot(results[1], coupling[0], precision=highest)
+    return jnp.stack(results)
+
+
+def whole_coupling(coupling):
+    layers = lax.axis_size("layer")
+    quarter = coupling.shape[1] // 2
+    core = lax.axis_index("layer") % 2
+    piece = lax.dynamic_slice_in_dim(coupling, core * quarter, quarter, 1)
+    first = swap_col(piece)
+    second = lax.ppermute(first, "layer", [(i, i ^ 1) for i in range(layers)])
+    other = jnp.where(core == 0, jnp.concatenate([first, second], 1), jnp.concatenate([second, first], 1))
+    low = lax.axis_index("col") == 0
+    return jnp.where(low, jnp.concatenate([coupling, other], 1), jnp.concatenate([other, coupling], 1))
+
+
 def coarse_general(rhs, pivots, coupling):
     share = pivots.shape[1]
     start = lax.axis_index("col") * share
@@ -185,6 +219,9 @@
 def shards(sources, conduct, via_cond, via_map, pad_map, port_tile, pivots, coupling):
     layer_count = lax.axis_size("layer")
     vertical = via_cond * via_map.astype(jnp.float32)
+    split_coupling = lax.axis_size("col") == 2 and layer_count % 2 == 0 and coupling.shape[1] % 2 == 0
+    if split_coupling:
+        full_coupling = whole_coupling(coupling)
     packed = lax.all_to_all(jnp.stack((conduct, vertical)), "layer", 2, 1, tiled=True)
     conduct, vertical = packed[0], packed[1]
     sources = lax.all_to_all(sources, "layer", 1, 0, tiled=True)
@@ -237,7 +274,10 @@
         plane = jnp.sum(resid, axis=0)
         tiles = plane.reshape(own_rows, TILE, own_cols, TILE).sum(axis=(1, 3)).reshape(-1)
         rhs = share_tiles(tiles, own_rows, own_cols, flat_tiles).reshape(NPANEL, PANEL) * (restrict_scale / TILE)
-        ports = coarse(rhs, pivots, coupling)
+        if split_coupling:
+            ports = coarse_rows(rhs, pivots, full_coupling)
+        else:
+            ports = coarse(rhs, pivots, coupling)
         tile_values = jnp.dot(scatter_ring, ports.reshape(-1), precision=highest).reshape(own_rows + 2, own_cols + 2)
         ring = expand(expand(tile_values, True).T, True).T * prolong_scale
         centre = ring[1:-1, 1:-1]

time: 169 us -> 169 us (level)
  waiting for transfers between devices: 53.7 us -> 39.5 us
  other arithmetic: 12.8 us -> 19.1 us
  matrix products: 13 us -> 18.3 us
  local copies, waits for them, and re-layouts: 19.6 us -> 21.3 us
    ppermute x12 -> x7, waiting for transfers between devices: 21.6 us -> 15.1 us  [swap_col(): return lax.ppermute(value, 'col', [(0, 1), (1, 0)])]
    all_to_all x2, waiting for transfers between devices: 12.1 us -> 5.65 us  [share_tiles(): got = lax.all_to_all(payload, ('layer', 'row', 'col'), 0, 0, tiled=True)]
    all_to_all x1, waiting for transfers between devices: 0.01 us -> 6.36 us  [shards(): lax.all_to_all(jnp.stack((conduct, vertical)), 'layer', 2, 1, tiled=True)]
    ppermute x6, waiting for transfers between devices: 5.76 us -> 0.02 us  [rims(): got = lax.ppermute(jnp.where(low, tail, head), axis, [(0, 1), (1, 0)])]
    dot_general x20, matrix products: 10.3 us -> 14.7 us  [the longest x6 5.94 us: coarse_rows(): jnp.dot(coupling[section - 1], forward[-1], precision=highest)]
    ppermute x6, waiting for transfers between devices: 3.83 us -> 0.02 us  [rims(): lax.ppermute(head, axis, [(place[i + 1], place[i]) for i in range(count -...]
    all_to_all x2, starting transfers between devices: 14.2 us -> 10.9 us  [share_tiles(): got = lax.all_to_all(payload, ('layer', 'row', 'col'), 0, 0, tiled=True)]
    reduce_sum x4, other arithmetic: 0.79 us -> 3.73 us  [shards(): plane.reshape(own_rows, TILE, own_cols, TILE).sum(axis=(1, 3)).reshape(-1)]
  transfers between devices with their start and end apart: 35 -> 31, of which waited for: 19 -> 15; matrix products, arithmetic and copies ran while one was open for 18% -> 26% of each run, Pallas kernels for 0% -> 0%
where the time goes in v9:
time: 169 us; the launch traced here: 167 us
  starting transfers between devices  67.2 us (40%)
  waiting for transfers between devices  39.5 us (23%)
  local copies, waits for them, and re-layouts  21.3 us (13%)
  other arithmetic  19.1 us (11%)
  matrix products  18.3 us (11%)
  between operations  1.92 us (1%)
    ppermute x6, starting transfers between devices, rims(): lax.ppermute(tail, axis, [(place[i], place[i + 1]) for i in range(count -...  21 us
    ppermute x7, waiting for transfers between devices, swap_col(): return lax.ppermute(value, 'col', [(0, 1), (1, 0)])  15.1 us
    all_to_all x2, starting transfers between devices, share_tiles(): got = lax.all_to_all(payload, ('layer', 'row', 'col'), 0, 0, tiled=True)  10.9 us
    ppermute x7, starting transfers between devices, swap_col(): return lax.ppermute(value, 'col', [(0, 1), (1, 0)])  7.9 us
    ppermute x6, starting transfers between devices, rims(): lax.ppermute(head, axis, [(place[i + 1], place[i]) for i in range(count -...  7.73 us
    all_to_all x1, waiting for transfers between devices, shards(): lax.all_to_all(jnp.stack((conduct, vertical)), 'layer', 2, 1, tiled=True)  6.36 us
    ppermute x6, starting transfers between devices, rims(): got = lax.ppermute(jnp.where(low, tail, head), axis, [(0, 1), (1, 0)])  6.04 us
    dot_general x6, matrix products, coarse_rows(): jnp.dot(coupling[section - 1], forward[-1], precision=highest)  5.94 us
  transfers between devices with their start and end apart: 31, of which 15 were waited for; matrix products, arithmetic and copies ran while one was open for 26% of the time, Pallas kernels for 0%

profile of v9, /device:TPU:0, one launch (start us, length us, event | category | flops | bytes accessed | tf_op | source)
XLA Modules:
  0.0 167.2 jit_solution(9271538658385154359)
XLA Ops:
  0.7 2.1 %constant_dynamic-slice_fusion = f32[3,128,512]{2,1,0:T(8,128)} fusion(f32[3,256,512]{2,1,0:T(8,128)} %param.15, s32[]{:T(128)S(6)} %select_n.296), kind=kLoop, calls=%fused_computation.273 | loop fusion | bytes 1572868 | tf_op jit(solution)/shard_map/dynamic_slice | solution.py:181
  2.8 3.0 %collective-permute-start = (f32[3,128,512]{2,1,0:T(8,128)}, f32[3,128,512]{2,1,0:T(8,128)}, u32[]{:S(2)}, u32[]{:S(2)}) collective-permute-start(f32[3,128,512]{2,1,0:T(8,128)} %constant_dynamic-slice_fusion), channel_id=1, source_target_pairs={{0,1},{1,0},{2,3},{3,2},{4,5},{5,4},{6,7},{7,6},{8,9},{9,8},{10,11... | collective-permute-start | bytes 2359304 | tf_op jit(solution)/shard_map/ppermute | solution.py:118
  5.8 1.9 %copy.24 = f32[2,64,512]{2,0,1:T(2,128)} copy(f32[2,64,512]{2,1,0:T(8,128)} %param.8) | data formatting | bytes 524288 | tf_op args[0]
  7.6 3.4 %all-to-all-start = ((f32[2,64,512]{2,0,1:T(2,128)}), f32[2,64,512]{2,0,1:T(2,128)S(1)}, u32[]{:S(2)}, u32[]{:S(2)}) async-start(f32[2,64,512]{2,0,1:T(2,128)} %copy.24), calls=%async_computation | async-start | bytes 524288 | tf_op jit(solution)/shard_map/all_to_all | solution.py:227
  13.1 3.9 %all-to-all-done = f32[2,64,512]{2,0,1:T(2,128)S(1)} async-done(((f32[2,64,512]{2,0,1:T(2,128)}), f32[2,64,512]{2,0,1:T(2,128)S(1)}, u32[]{:S(2)}, u32[]{:S(2)}) %all-to-all-start) | async-done | bytes 262176 | tf_op jit(solution)/shard_map/all_to_all | solution.py:227
  18.0 4.0 %all-to-all-start.1 = ((f32[32,1,32]{2,1,0:T(1,128)}), f32[32,1,32]{2,1,0:T(1,128)S(1)}, u32[]{:S(2)}, u32[]{:S(2)}) async-start(f32[32,1,32]{2,1,0:T(1,128)} %broadcast_in_dim.27), calls=%async_computation.1 | async-start | bytes 32768 | tf_op jit(solution)/shard_map/all_to_all | solution.py:106
  24.1 4.9 %all-to-all-done.1 = f32[32,1,32]{2,1,0:T(1,128)S(1)} async-done(((f32[32,1,32]{2,1,0:T(1,128)}), f32[32,1,32]{2,1,0:T(1,128)S(1)}, u32[]{:S(2)}, u32[]{:S(2)}) %all-to-all-start.1) | async-done | bytes 4128 | tf_op jit(solution)/shard_map/all_to_all | solution.py:106
  29.0 3.5 %all-to-all-start.2 = ((f32[2,2,64,512]{3,1,0,2:T(2,128)}), f32[2,2,64,512]{3,1,0,2:T(2,128)S(1)}, u32[]{:S(2)}, u32[]{:S(2)}) async-start(f32[2,2,64,512]{3,1,0,2:T(2,128)} %copy.25), calls=%async_computation.2 | async-start | bytes 1048576 | tf_op jit(solution)/shard_map/all_to_all | solution.py:225
  33.4 1.5 fusion.30
  34.9 6.4 %all-to-all-done.2 = f32[2,2,64,512]{3,1,0,2:T(2,128)S(1)} async-done(((f32[2,2,64,512]{3,1,0,2:T(2,128)}), f32[2,2,64,512]{3,1,0,2:T(2,128)S(1)}, u32[]{:S(2)}, u32[]{:S(2)}) %all-to-all-start.2) | async-done | bytes 524320 | tf_op jit(solution)/shard_map/all_to_all | solution.py:225
  43.7 3.0 %collective-permute-start.6 = (f32[8,1,512]{2,1,0:T(1,128)S(1)}, f32[8,1,512]{2,1,0:T(1,128)S(1)}, u32[]{:S(2)}, u32[]{:S(2)}) collective-permute-start(f32[8,1,512]{2,1,0:T(1,128)S(1)} %get-tuple-element.59), channel_id=1, source_target_pairs={{0,8},{8,16},{16,24},{24,2},{2,10},{10,18},{18,26},{26,4},{4,12},{... | collective-permute-start | bytes 49160 | tf_op jit(solution)/shard_map/ppermute | solution.py:48
  48.5 1.5 collective-permute-start.10
  51.3 3.0 %collective-permute-start.9 = (f32[8,1,512]{2,1,0:T(1,128)S(1)}, f32[8,1,512]{2,1,0:T(1,128)S(1)}, u32[]{:S(2)}, u32[]{:S(2)}) collective-permute-start(f32[8,1,512]{2,1,0:T(1,128)S(1)} %get-tuple-element.53), channel_id=1, source_target_pairs={{0,8},{8,16},{16,24},{24,2},{2,10},{10,18},{18,26},{26,4},{4,12},{... | collective-permute-start | bytes 49160 | tf_op jit(solution)/shard_map/ppermute | solution.py:48
  58.0 4.6 %collective-permute-start.12 = (f32[8,1,512]{2,1,0:T(1,128)S(1)}, f32[8,1,512]{2,1,0:T(1,128)S(1)}, u32[]{:S(2)}, u32[]{:S(2)}) collective-permute-start(f32[8,1,512]{2,1,0:T(1,128)S(1)} %get-tuple-element.44), channel_id=1, source_target_pairs={{0,8},{8,16},{16,24},{24,2},{2,10},{10,18},{18,26},{26,4},{4,12},{... | collective-permute-start | bytes 49160 | tf_op jit(solution)/shard_map/ppermute | solution.py:48
  65.7 2.6 %collective-permute-start.1 = (f32[3,128,512]{2,1,0:T(8,128)}, f32[3,128,512]{2,1,0:T(8,128)S(1)}, u32[]{:S(2)}, u32[]{:S(2)}) collective-permute-start(f32[3,128,512]{2,1,0:T(8,128)} %collective-permute-done), channel_id=1, source_target_pairs={{0,8},{8,0},{16,24},{24,16},{1,9},{9,1},{17,25},{25,17},{2,10},{10... | collective-permute-start | bytes 2359304 | tf_op jit(solution)/shard_map/ppermute | solution.py:183
  72.7 3.6 %collective-permute-start.15 = (f32[8,1,512]{2,1,0:T(1,128)}, f32[8,1,512]{2,1,0:T(1,128)}, u32[]{:S(2)}, u32[]{:S(2)}) collective-permute-start(f32[8,1,512]{2,1,0:T(1,128)} %get-tuple-element.37), channel_id=1, source_target_pairs={{0,8},{8,16},{16,24},{24,2},{2,10},{10,18},{18,26},{26,4},{4,12},{... | collective-permute-start | bytes 49160 | tf_op jit(solution)/shard_map/ppermute | solution.py:48
  76.9 1.6 maximum_select_fusion.1
  84.2 2.4 %collective-permute-done.2 = f32[256]{0:T(256)S(1)} collective-permute-done((f32[256]{0:T(256)S(1)}, f32[256]{0:T(256)S(1)}, u32[]{:S(2)}, u32[]{:S(2)}) %collective-permute-start.2) | collective-permute-done | bytes 1056 | tf_op jit(solution)/shard_map/ppermute | solution.py:118
  87.9 2.9 %collective-permute-done.3 = f32[256]{0:T(256)S(1)} collective-permute-done((f32[256]{0:T(256)S(1)}, f32[256]{0:T(256)S(1)}, u32[]{:S(2)}, u32[]{:S(2)}) %collective-permute-start.3) | collective-permute-done | bytes 1056 | tf_op jit(solution)/shard_map/ppermute | solution.py:118
  92.2 3.0 %collective-permute-done.4 = f32[512]{0:T(512)S(1)} collective-permute-done((f32[512]{0:T(512)S(1)}, f32[512]{0:T(512)S(1)}, u32[]{:S(2)}, u32[]{:S(2)}) %collective-permute-start.4) | collective-permute-done | bytes 2080 | tf_op jit(solution)/shard_map/ppermute | solution.py:118
  100.3 2.8 %fusion.148 = (f32[512]{0:T(512)}, f32[8,16,512]{2,1,0:T(8,128)S(1)}) fusion(f32[8,16,512]{2,1,0:T(8,128)} %copy-done.13, f32[8,16,511]{2,1,0:T(8,128)} %get-tuple-element.39, f32[8,16,1]{2,1,0:T(8,128)} %get-tuple-element.69, f32[16,512]{1,0:T(8,128)S(1)} %get-tuple-element.77, f32[8,16,512]{2,1,0:T(8,128)} %copy-done.11, ...), kind=kLoop, calls=%fused_computation.276 | loop fusion | flops 2096640 | bytes 4065280 | tf_op jit(solution)/shard_map/reduce_sum | solution.py:275
  110.4 6.9 %all-to-all-start.3 = ((f32[32,1,32]{2,1,0:T(1,128)}), f32[32,1,32]{2,1,0:T(1,128)}, u32[]{:S(2)}, u32[]{:S(2)}) async-start(f32[32,1,32]{2,1,0:T(1,128)} %broadcast_in_dim.35), calls=%async_computation.3 | async-start | bytes 32768 | tf_op jit(solution)/shard_map/all_to_all | solution.py:106
  118.6 3.6 %collective-permute-start.21 = (f32[8,1,512]{2,1,0:T(1,128)}, f32[8,1,512]{2,1,0:T(1,128)}, u32[]{:S(2)}, u32[]{:S(2)}) collective-permute-start(f32[8,1,512]{2,1,0:T(1,128)} %get-tuple-element.29), channel_id=1, source_target_pairs={{0,8},{8,16},{16,24},{24,2},{2,10},{10,18},{18,26},{26,4},{4,12},{... | collective-permute-start | bytes 49160 | tf_op jit(solution)/shard_map/ppermute | solution.py:48
  124.4 1.7 %fusion.1 = f32[2048]{0:T(1024)S(1)} fusion(f32[32,32]{1,0:T(8,128)} %bitcast.50, s32[2048]{0:T(1024)} %copy-done.42, s32[2048]{0:T(1024)} %copy-done.41), kind=kOutput, calls=%fused_computation.5 | convolution fusion | flops 25425920 | bytes 28672 | tf_op jit(solution)/shard_map/dot_general | solution.py:114
  131.7 2.1 %collective-permute-done.17 = f32[256]{0:T(256)S(1)} collective-permute-done((f32[256]{0:T(256)S(1)}, f32[256]{0:T(256)S(1)}, u32[]{:S(2)}, u32[]{:S(2)}) %collective-permute-start.17) | collective-permute-done | bytes 1056 | tf_op jit(solution)/shard_map/ppermute | solution.py:118
  136.0 2.1 %collective-permute-done.18 = f32[256]{0:T(256)S(1)} collective-permute-done((f32[256]{0:T(256)S(1)}, f32[256]{0:T(256)S(1)}, u32[]{:S(2)}, u32[]{:S(2)}) %collective-permute-start.18) | collective-permute-done | bytes 1056 | tf_op jit(solution)/shard_map/ppermute | solution.py:118
  139.8 2.6 %collective-permute-done.19 = f32[512]{0:T(512)S(1)} collective-permute-done((f32[512]{0:T(512)S(1)}, f32[512]{0:T(512)S(1)}, u32[]{:S(2)}, u32[]{:S(2)}) %collective-permute-start.19) | collective-permute-done | bytes 2080 | tf_op jit(solution)/shard_map/ppermute | solution.py:118
  144.6 2.6 %fusion.129 = f32[8,16,512]{2,1,0:T(8,128)S(1)} fusion(f32[8,16,512]{2,1,0:T(8,128)S(1)} %mul.293, f32[8,16,512]{2,1,0:T(8,128)} %copy-done.20, f32[8,16,512]{2,1,0:T(8,128)} %copy-done.13, f32[8,16,511]{2,1,0:T(8,128)} %get-tuple-element.31, f32[8,16,1]{2,1,0:T(8,128)} %get-tuple-element.67, f32[8,16,512]{2,1,0:T(8,128)} %copy-done.11, ...), kind=kLoop, calls=%fused_computation.196 | loop fusion | flops 1900544 | bytes 4161536 | tf_op jit(solution)/shard_map/add | solution.py:84
  149.9 3.0 %collective-permute-start.24 = (f32[8,1,512]{2,1,0:T(1,128)S(1)}, f32[8,1,512]{2,1,0:T(1,128)S(1)}, u32[]{:S(2)}, u32[]{:S(2)}) collective-permute-start(f32[8,1,512]{2,1,0:T(1,128)S(1)} %get-tuple-element.20), channel_id=1, source_target_pairs={{0,8},{8,16},{16,24},{24,2},{2,10},{10,18},{18,26},{26,4},{4,12},{... | collective-permute-start | bytes 49160 | tf_op jit(solution)/shard_map/ppermute | solution.py:48
  154.0 2.3 %fusion.97 = f32[8,16,512]{2,1,0:T(8,128)} fusion(f32[8,16,512]{2,1,0:T(8,128)S(1)} %copy-done.21, f32[1,16,512]{2,1,0:T(8,128)S(1)} %multiply_bitcast_fusion.1, f32[8,16,512]{2,1,0:T(8,128)S(1)} %copy-done.16, f32[8,1,512]{2,1,0:T(1,128)S(1)} %collective-permute-done.23, f32[8,15,512]{2,1,0:T(8,128)S(1)} %get-tuple-element.23, ...), kind=kLoop, calls=%fused_computation.114 | loop fusion | flops 3997696 | bytes 5996544 | tf_op jit(solution)/shard_map/add | solution.py:287
  156.3 4.2 %all-to-all-start.4 = ((f32[8,16,512]{2,1,0:T(8,128)}), f32[8,16,512]{2,1,0:T(8,128)S(1)}, u32[]{:S(2)}, u32[]{:S(2)}) async-start(f32[8,16,512]{2,1,0:T(8,128)} %fusion.97), calls=%async_computation.4 | async-start | bytes 524288 | tf_op jit(solution)/shard_map/all_to_all | solution.py:299
  161.2 5.4 %all-to-all-done.4 = f32[8,16,512]{2,1,0:T(8,128)S(1)} async-done(((f32[8,16,512]{2,1,0:T(8,128)}), f32[8,16,512]{2,1,0:T(8,128)S(1)}, u32[]{:S(2)}, u32[]{:S(2)}) %all-to-all-start.4) | async-done | bytes 262176 | tf_op jit(solution)/shard_map/all_to_all | solution.py:299
  (269 shorter events, 62.9 us)
Async XLA Ops:
  2.8 62.9 %collective-permute-start = (f32[3,128,512]{2,1,0:T(8,128)}, f32[3,128,512]{2,1,0:T(8,128)}, u32[]{:S(2)}, u32[]{:S(2)}) collective-permute-start(f32[3,128,512]{2,1,0:T(8,128)} %constant_dynamic-slice_fusion), channel_id=1, source_target_pairs={{0,1},{1,0},{2,3},{3,2},{4,5},{5,4},{6,7},{7,6},{8,9},{9,8},{10,11... | collective-permute-start | bytes 2359304 | tf_op jit(solution)/shard_map/ppermute | solution.py:118
  7.6 9.4 %all-to-all-start = ((f32[2,64,512]{2,0,1:T(2,128)}), f32[2,64,512]{2,0,1:T(2,128)S(1)}, u32[]{:S(2)}, u32[]{:S(2)}) async-start(f32[2,64,512]{2,0,1:T(2,128)} %copy.24), calls=%async_computation | async-start | bytes 524288 | tf_op jit(solution)/shard_map/all_to_all | solution.py:227
  11.8 84.1 %copy-start.31 = (s32[1,4,4,128]{3,1,2,0:T(4,128)}, s32[1,4,4,128]{3,1,2,0:T(4,128)S(1)}, u32[]{:S(2)}) copy-start(s32[1,4,4,128]{3,1,2,0:T(4,128)S(1)} %copy.30) | copy-start | bytes 24580
  18.0 11.0 %all-to-all-start.1 = ((f32[32,1,32]{2,1,0:T(1,128)}), f32[32,1,32]{2,1,0:T(1,128)S(1)}, u32[]{:S(2)}, u32[]{:S(2)}) async-start(f32[32,1,32]{2,1,0:T(1,128)} %broadcast_in_dim.27), calls=%async_computation.1 | async-start | bytes 32768 | tf_op jit(solution)/shard_map/all_to_all | solution.py:106
  29.0 12.3 %all-to-all-start.2 = ((f32[2,2,64,512]{3,1,0,2:T(2,128)}), f32[2,2,64,512]{3,1,0,2:T(2,128)S(1)}, u32[]{:S(2)}, u32[]{:S(2)}) async-start(f32[2,2,64,512]{3,1,0,2:T(2,128)} %copy.25), calls=%async_computation.2 | async-start | bytes 1048576 | tf_op jit(solution)/shard_map/all_to_all | solution.py:225
  41.7 5.1 %collective-permute-start.7 = (f32[8,16,1]{2,1,0:T(8,128)S(1)}, f32[8,16,1]{2,1,0:T(8,128)S(1)}, u32[]{:S(2)}, u32[]{:S(2)}) collective-permute-start(f32[8,16,1]{2,1,0:T(8,128)S(1)} %slice_select_fusion.5), channel_id=1, source_target_pairs={{0,1},{1,0},{2,3},{3,2},{4,5},{5,4},{6,7},{7,6},{8,9},{9,8},{10,11... | collective-permute-start | bytes 1544 | tf_op jit(solution)/shard_map/ppermute | solution.py:45
  42.4 4.5 %collective-permute-start.5 = (f32[8,1,512]{2,1,0:T(1,128)S(1)}, f32[8,1,512]{2,1,0:T(1,128)S(1)}, u32[]{:S(2)}, u32[]{:S(2)}) collective-permute-start(f32[8,1,512]{2,1,0:T(1,128)S(1)} %get-tuple-element.58), channel_id=1, source_target_pairs={{8,0},{16,8},{24,16},{2,24},{10,2},{18,10},{26,18},{4,26},{12,4},{... | collective-permute-start | bytes 49160 | tf_op jit(solution)/shard_map/ppermute | solution.py:49
  43.7 3.9 %collective-permute-start.6 = (f32[8,1,512]{2,1,0:T(1,128)S(1)}, f32[8,1,512]{2,1,0:T(1,128)S(1)}, u32[]{:S(2)}, u32[]{:S(2)}) collective-permute-start(f32[8,1,512]{2,1,0:T(1,128)S(1)} %get-tuple-element.59), channel_id=1, source_target_pairs={{0,8},{8,16},{16,24},{24,2},{2,10},{10,18},{18,26},{26,4},{4,12},{... | collective-permute-start | bytes 49160 | tf_op jit(solution)/shard_map/ppermute | solution.py:48
  48.5 5.8 %collective-permute-start.10 = (f32[8,16,1]{2,1,0:T(8,128)S(1)}, f32[8,16,1]{2,1,0:T(8,128)S(1)}, u32[]{:S(2)}, u32[]{:S(2)}) collective-permute-start(f32[8,16,1]{2,1,0:T(8,128)S(1)} %slice_select_fusion.4), channel_id=1, source_target_pairs={{0,1},{1,0},{2,3},{3,2},{4,5},{5,4},{6,7},{7,6},{8,9},{9,8},{10,11... | collective-permute-start | bytes 1544 | tf_op jit(solution)/shard_map/ppermute | solution.py:45
  50.0 4.4 %collective-permute-start.8 = (f32[8,1,512]{2,1,0:T(1,128)S(1)}, f32[8,1,512]{2,1,0:T(1,128)S(1)}, u32[]{:S(2)}, u32[]{:S(2)}) collective-permute-start(f32[8,1,512]{2,1,0:T(1,128)S(1)} %get-tuple-element.52), channel_id=1, source_target_pairs={{8,0},{16,8},{24,16},{2,24},{10,2},{18,10},{26,18},{4,26},{12,4},{... | collective-permute-start | bytes 49160 | tf_op jit(solution)/shard_map/ppermute | solution.py:49
  51.3 3.9 %collective-permute-start.9 = (f32[8,1,512]{2,1,0:T(1,128)S(1)}, f32[8,1,512]{2,1,0:T(1,128)S(1)}, u32[]{:S(2)}, u32[]{:S(2)}) collective-permute-start(f32[8,1,512]{2,1,0:T(1,128)S(1)} %get-tuple-element.53), channel_id=1, source_target_pairs={{0,8},{8,16},{16,24},{24,2},{2,10},{10,18},{18,26},{26,4},{4,12},{... | collective-permute-start | bytes 49160 | tf_op jit(solution)/shard_map/ppermute | solution.py:48
  56.0 6.6 %collective-permute-start.13 = (f32[8,16,1]{2,1,0:T(8,128)S(1)}, f32[8,16,1]{2,1,0:T(8,128)S(1)}, u32[]{:S(2)}, u32[]{:S(2)}) collective-permute-start(f32[8,16,1]{2,1,0:T(8,128)S(1)} %slice_select_fusion.3), channel_id=1, source_target_pairs={{0,1},{1,0},{2,3},{3,2},{4,5},{5,4},{6,7},{7,6},{8,9},{9,8},{10,11... | collective-permute-start | bytes 1544 | tf_op jit(solution)/shard_map/ppermute | solution.py:45
  56.7 5.9 %collective-permute-start.11 = (f32[8,1,512]{2,1,0:T(1,128)S(1)}, f32[8,1,512]{2,1,0:T(1,128)S(1)}, u32[]{:S(2)}, u32[]{:S(2)}) collective-permute-start(f32[8,1,512]{2,1,0:T(1,128)S(1)} %get-tuple-element.45), channel_id=1, source_target_pairs={{8,0},{16,8},{24,16},{2,24},{10,2},{18,10},{26,18},{4,26},{12,4},{... | collective-permute-start | bytes 49160 | tf_op jit(solution)/shard_map/ppermute | solution.py:49
  58.0 5.4 %collective-permute-start.12 = (f32[8,1,512]{2,1,0:T(1,128)S(1)}, f32[8,1,512]{2,1,0:T(1,128)S(1)}, u32[]{:S(2)}, u32[]{:S(2)}) collective-permute-start(f32[8,1,512]{2,1,0:T(1,128)S(1)} %get-tuple-element.44), channel_id=1, source_target_pairs={{0,8},{8,16},{16,24},{24,2},{2,10},{10,18},{18,26},{26,4},{4,12},{... | collective-permute-start | bytes 49160 | tf_op jit(solution)/shard_map/ppermute | solution.py:48
  65.7 11.2 %collective-permute-start.1 = (f32[3,128,512]{2,1,0:T(8,128)}, f32[3,128,512]{2,1,0:T(8,128)S(1)}, u32[]{:S(2)}, u32[]{:S(2)}) collective-permute-start(f32[3,128,512]{2,1,0:T(8,128)} %collective-permute-done), channel_id=1, source_target_pairs={{0,8},{8,0},{16,24},{24,16},{1,9},{9,1},{17,25},{25,17},{2,10},{10... | collective-permute-start | bytes 2359304 | tf_op jit(solution)/shard_map/ppermute | solution.py:183
  68.4 7.9 %collective-permute-start.16 = (f32[8,16,1]{2,1,0:T(8,128)S(1)}, f32[8,16,1]{2,1,0:T(8,128)S(1)}, u32[]{:S(2)}, u32[]{:S(2)}) collective-permute-start(f32[8,16,1]{2,1,0:T(8,128)S(1)} %slice_select_fusion.2), channel_id=1, source_target_pairs={{0,1},{1,0},{2,3},{3,2},{4,5},{5,4},{6,7},{7,6},{8,9},{9,8},{10,11... | collective-permute-start | bytes 1544 | tf_op jit(solution)/shard_map/ppermute | solution.py:45
  71.4 28.9 %collective-permute-start.14 = (f32[8,1,512]{2,1,0:T(1,128)}, f32[8,1,512]{2,1,0:T(1,128)}, u32[]{:S(2)}, u32[]{:S(2)}) collective-permute-start(f32[8,1,512]{2,1,0:T(1,128)} %get-tuple-element.36), channel_id=1, source_target_pairs={{8,0},{16,8},{24,16},{2,24},{10,2},{18,10},{26,18},{4,26},{12,4},{... | collective-permute-start | bytes 49160 | tf_op jit(solution)/shard_map/ppermute | solution.py:49
  72.7 27.6 %collective-permute-start.15 = (f32[8,1,512]{2,1,0:T(1,128)}, f32[8,1,512]{2,1,0:T(1,128)}, u32[]{:S(2)}, u32[]{:S(2)}) collective-permute-start(f32[8,1,512]{2,1,0:T(1,128)} %get-tuple-element.37), channel_id=1, source_target_pairs={{0,8},{8,16},{16,24},{24,2},{2,10},{10,18},{18,26},{26,4},{4,12},{... | collective-permute-start | bytes 49160 | tf_op jit(solution)/shard_map/ppermute | solution.py:48
  83.0 3.6 %collective-permute-start.2 = (f32[256]{0:T(256)S(1)}, f32[256]{0:T(256)S(1)}, u32[]{:S(2)}, u32[]{:S(2)}) collective-permute-start(f32[256]{0:T(256)S(1)} %bitcast.230), channel_id=1, source_target_pairs={{0,1},{1,0},{2,3},{3,2},{4,5},{5,4},{6,7},{7,6},{8,9},{9,8},{10,11... | collective-permute-start | bytes 3080 | tf_op jit(solution)/shard_map/ppermute | solution.py:118
  87.3 3.6 %collective-permute-start.3 = (f32[256]{0:T(256)S(1)}, f32[256]{0:T(256)S(1)}, u32[]{:S(2)}, u32[]{:S(2)}) collective-permute-start(f32[256]{0:T(256)S(1)} %dynamic-slice_subtract_fusion.3), channel_id=1, source_target_pairs={{0,1},{1,0},{2,3},{3,2},{4,5},{5,4},{6,7},{7,6},{8,9},{9,8},{10,11... | collective-permute-start | bytes 3080 | tf_op jit(solution)/shard_map/ppermute | solution.py:118
  91.6 3.6 %collective-permute-start.4 = (f32[512]{0:T(512)S(1)}, f32[512]{0:T(512)S(1)}, u32[]{:S(2)}, u32[]{:S(2)}) collective-permute-start(f32[512]{0:T(512)S(1)} %pad_maximum_fusion.3), channel_id=1, source_target_pairs={{0,1},{1,0},{2,3},{3,2},{4,5},{5,4},{6,7},{7,6},{8,9},{9,8},{10,11... | collective-permute-start | bytes 6152 | tf_op jit(solution)/shard_map/ppermute | solution.py:118
  106.5 15.8 %collective-permute-start.22 = (f32[8,16,1]{2,1,0:T(8,128)S(1)}, f32[8,16,1]{2,1,0:T(8,128)}, u32[]{:S(2)}, u32[]{:S(2)}) collective-permute-start(f32[8,16,1]{2,1,0:T(8,128)S(1)} %slice_select_fusion.1), channel_id=1, source_target_pairs={{0,1},{1,0},{2,3},{3,2},{4,5},{5,4},{6,7},{7,6},{8,9},{9,8},{10,11... | collective-permute-start | bytes 1544 | tf_op jit(solution)/shard_map/ppermute | solution.py:45
  110.4 14.0 %all-to-all-start.3 = ((f32[32,1,32]{2,1,0:T(1,128)}), f32[32,1,32]{2,1,0:T(1,128)}, u32[]{:S(2)}, u32[]{:S(2)}) async-start(f32[32,1,32]{2,1,0:T(1,128)} %broadcast_in_dim.35), calls=%async_computation.3 | async-start | bytes 32768 | tf_op jit(solution)/shard_map/all_to_all | solution.py:106
  117.3 27.1 %collective-permute-start.20 = (f32[8,1,512]{2,1,0:T(1,128)}, f32[8,1,512]{2,1,0:T(1,128)S(1)}, u32[]{:S(2)}, u32[]{:S(2)}) collective-permute-start(f32[8,1,512]{2,1,0:T(1,128)} %get-tuple-element.28), channel_id=1, source_target_pairs={{8,0},{16,8},{24,16},{2,24},{10,2},{18,10},{26,18},{4,26},{12,4},{... | collective-permute-start | bytes 49160 | tf_op jit(solution)/shard_map/ppermute | solution.py:49
  118.6 25.8 %collective-permute-start.21 = (f32[8,1,512]{2,1,0:T(1,128)}, f32[8,1,512]{2,1,0:T(1,128)}, u32[]{:S(2)}, u32[]{:S(2)}) collective-permute-start(f32[8,1,512]{2,1,0:T(1,128)} %get-tuple-element.29), channel_id=1, source_target_pairs={{0,8},{8,16},{16,24},{24,2},{2,10},{10,18},{18,26},{26,4},{4,12},{... | collective-permute-start | bytes 49160 | tf_op jit(solution)/shard_map/ppermute | solution.py:48
  130.2 3.6 %collective-permute-start.17 = (f32[256]{0:T(256)S(1)}, f32[256]{0:T(256)S(1)}, u32[]{:S(2)}, u32[]{:S(2)}) collective-permute-start(f32[256]{0:T(256)S(1)} %bitcast.226), channel_id=1, source_target_pairs={{0,1},{1,0},{2,3},{3,2},{4,5},{5,4},{6,7},{7,6},{8,9},{9,8},{10,11... | collective-permute-start | bytes 3080 | tf_op jit(solution)/shard_map/ppermute | solution.py:118
  134.5 3.6 %collective-permute-start.18 = (f32[256]{0:T(256)S(1)}, f32[256]{0:T(256)S(1)}, u32[]{:S(2)}, u32[]{:S(2)}) collective-permute-start(f32[256]{0:T(256)S(1)} %dynamic-slice_subtract_fusion.1), channel_id=1, source_target_pairs={{0,1},{1,0},{2,3},{3,2},{4,5},{5,4},{6,7},{7,6},{8,9},{9,8},{10,11... | collective-permute-start | bytes 3080 | tf_op jit(solution)/shard_map/ppermute | solution.py:118
  138.8 3.6 %collective-permute-start.19 = (f32[512]{0:T(512)S(1)}, f32[512]{0:T(512)S(1)}, u32[]{:S(2)}, u32[]{:S(2)}) collective-permute-start(f32[512]{0:T(512)S(1)} %pad_maximum_fusion.6), channel_id=1, source_target_pairs={{0,1},{1,0},{2,3},{3,2},{4,5},{5,4},{6,7},{7,6},{8,9},{9,8},{10,11... | collective-permute-start | bytes 6152 | tf_op jit(solution)/shard_map/ppermute | solution.py:118
  147.6 5.4 %collective-permute-start.25 = (f32[8,16,1]{2,1,0:T(8,128)S(1)}, f32[8,16,1]{2,1,0:T(8,128)S(1)}, u32[]{:S(2)}, u32[]{:S(2)}) collective-permute-start(f32[8,16,1]{2,1,0:T(8,128)S(1)} %slice_select_fusion), channel_id=1, source_target_pairs={{0,1},{1,0},{2,3},{3,2},{4,5},{5,4},{6,7},{7,6},{8,9},{9,8},{10,11... | collective-permute-start | bytes 1544 | tf_op jit(solution)/shard_map/ppermute | solution.py:45
  148.6 4.4 %collective-permute-start.23 = (f32[8,1,512]{2,1,0:T(1,128)S(1)}, f32[8,1,512]{2,1,0:T(1,128)S(1)}, u32[]{:S(2)}, u32[]{:S(2)}) collective-permute-start(f32[8,1,512]{2,1,0:T(1,128)S(1)} %get-tuple-element.21), channel_id=1, source_target_pairs={{8,0},{16,8},{24,16},{2,24},{10,2},{18,10},{26,18},{4,26},{12,4},{... | collective-permute-start | bytes 49160 | tf_op jit(solution)/shard_map/ppermute | solution.py:49
  149.9 3.9 %collective-permute-start.24 = (f32[8,1,512]{2,1,0:T(1,128)S(1)}, f32[8,1,512]{2,1,0:T(1,128)S(1)}, u32[]{:S(2)}, u32[]{:S(2)}) collective-permute-start(f32[8,1,512]{2,1,0:T(1,128)S(1)} %get-tuple-element.20), channel_id=1, source_target_pairs={{0,8},{8,16},{16,24},{24,2},{2,10},{10,18},{18,26},{26,4},{4,12},{... | collective-permute-start | bytes 49160 | tf_op jit(solution)/shard_map/ppermute | solution.py:48
  156.3 10.2 %all-to-all-start.4 = ((f32[8,16,512]{2,1,0:T(8,128)}), f32[8,16,512]{2,1,0:T(8,128)S(1)}, u32[]{:S(2)}, u32[]{:S(2)}) async-start(f32[8,16,512]{2,1,0:T(8,128)} %fusion.97), calls=%async_computation.4 | async-start | bytes 524288 | tf_op jit(solution)/shard_map/all_to_all | solution.py:299
  (44 other events, 566.6 us)

commit v10 on v6

--- a/solution.py
+++ b/solution.py
@@ -182,7 +182,7 @@
     return body
 
 
-def shards(sources, conduct, via_cond, via_map, pad_map, port_tile, pivots, coupling):
+def shards_blocks(sources, conduct, via_cond, via_map, pad_map, port_tile, pivots, coupling):
     layer_count = lax.axis_size("layer")
     vertical = via_cond * via_map.astype(jnp.float32)
     packed = lax.all_to_all(jnp.stack((sources, conduct, vertical)), "layer", 2, 1, tiled=True)
@@ -259,6 +259,131 @@
     return (drop, ports)
 
 
+def shards_rows(sources, conduct, via_cond, via_map, pad_map, port_tile, pivots, coupling):
+    layer_count, row_count, col_count = (lax.axis_size(axis) for axis, _ in GRID_AXES)
+    vertical = via_cond * via_map.astype(jnp.float32)
+    local_layers, block_rows, block_cols = sources.shape
+    group = layer_count * col_count
+    rows = block_rows // group
+    pad_plane = jnp.broadcast_to(pad_map.astype(jnp.float32)[None], sources.shape)
+    packed = jnp.stack((sources, conduct, vertical, pad_plane)).reshape(4, local_layers, group, rows, block_cols)
+    packed = lax.all_to_all(packed, ("layer", "col"), 2, 2, tiled=True)
+    packed = packed.reshape(4, local_layers, layer_count, col_count, rows, block_cols)
+    packed = packed.transpose(0, 2, 1, 4, 3, 5).reshape(4, layer_count * local_layers, rows, col_count * block_cols)
+    sources, conduct, vertical = packed[0], packed[1], packed[2]
+    pad_rows = packed[3][-1]
+    layers, _, grid_cols = sources.shape
+    blocks = row_count * group
+    place = []
+    for block in range(blocks):
+        r, rest = divmod(block, group)
+        l, c = divmod(rest, col_count)
+        place.append((l * row_count + r) * col_count + c)
+    block = lax.axis_index("row") * group + lax.axis_index("layer") * col_count + lax.axis_index("col")
+
+    def row_rims(field):
+        head, tail = field[:, :1], field[:, -1:]
+        below = lax.ppermute(tail, ("layer", "row", "col"), [(place[i], place[i + 1]) for i in range(blocks - 1)])
+        above = lax.ppermute(head, ("layer", "row", "col"), [(place[i + 1], place[i]) for i in range(blocks - 1)])
+        return above, below
+
+    def halo_of(field, row_halo):
+        return [rims(field, None, 0), row_halo, rims(field, None, 2)]
+
+    def grid_apply(field, row_halo):
+        return apply_grid(field, neighbours(field, halo_of(field, row_halo)), weights, pad_term)
+
+    near_vert = neighbours(vertical, halo_of(vertical, row_rims(vertical)))
+    near_plane = neighbours(conduct, halo_of(conduct, row_rims(conduct)))
+    weights = (
+        jnp.sqrt(vertical * near_vert[0]),
+        jnp.sqrt(vertical * near_vert[1]),
+        jnp.sqrt(conduct * near_plane[2]),
+        jnp.sqrt(conduct * near_plane[3]),
+        jnp.sqrt(conduct * near_plane[4]),
+        jnp.sqrt(conduct * near_plane[5]),
+    )
+    pad_term = jnp.concatenate((jnp.zeros((layers - 1, rows, grid_cols), jnp.float32), (pad_gain * pad_rows)[None]), 0)
+    diagonal = pad_term
+    for weight in weights:
+        diagonal = diagonal + weight
+    inverse = 1.0 / diagonal
+
+    theta = (bound_high + bound_low) / 2.0
+    delta = (bound_high - bound_low) / 2.0
+    sigma = theta / delta
+
+    def smooth_rows(resid):
+        rho = 1.0 / sigma
+        change = inverse * resid / theta
+        total = change
+        for sweep in range(DEG - 1):
+            remain = resid - grid_apply(total, row_rims(total))
+            rho_new = 1.0 / (2.0 * sigma - rho)
+            change = rho_new * rho * change + 2.0 * rho_new / delta * inverse * remain
+            total = total + change
+            rho = rho_new
+        return total
+
+    tile_cols = grid_cols // TILE
+    tile_rows = rows * blocks // TILE
+    flat_tiles = port_tile.reshape(-1)
+    port_row, port_col = flat_tiles // tile_cols, flat_tiles % tile_cols
+    devices = jnp.arange(layer_count * row_count * col_count, dtype=jnp.int32)
+    device_block = (devices // (row_count * col_count)) * col_count + (devices // col_count) % row_count * group + devices % col_count
+    pick_device = ((device_block * rows) // TILE == port_row[:, None]).astype(jnp.float32)
+    pick_slot = (port_col[:, None] == jnp.arange(tile_cols, dtype=jnp.int32)[None, :]).astype(jnp.float32)
+    first_ring = (block * rows - 1) // TILE
+    ring_count = rows // TILE + 2
+    ring_rows = first_ring + jnp.arange(ring_count, dtype=jnp.int32)
+    ring_ids = jnp.where(((ring_rows >= 0) & (ring_rows < tile_rows))[:, None], ring_rows[:, None] * tile_cols + jnp.arange(tile_cols, dtype=jnp.int32)[None, :], -1).reshape(-1)
+    scatter_ring = (ring_ids[:, None] == flat_tiles[None, :]).astype(jnp.float32)
+    node_rows = block * rows - 1 + jnp.arange(rows + 2, dtype=jnp.int32)
+    pick_ring = ((node_rows // TILE - first_ring)[:, None] == jnp.arange(ring_count, dtype=jnp.int32)[None, :]).astype(jnp.float32)
+
+    drop = None
+    for outer in range(ITERS):
+        if drop is None:
+            resid = sources
+        else:
+            resid = sources - grid_apply(drop, drop_halo)
+        plane = jnp.sum(resid, axis=0)
+        tiles = plane.reshape(rows, tile_cols, TILE).sum(axis=(0, 2))
+        count = layer_count * row_count * col_count
+        got = lax.all_to_all(jnp.broadcast_to(tiles[None], (count, tile_cols)), ("layer", "row", "col"), 0, 0, tiled=True)
+        rhs = jnp.sum(jnp.dot(pick_device, got, precision=highest) * pick_slot, axis=1)
+        rhs = rhs.reshape(NPANEL, PANEL) * (restrict_scale / TILE)
+        ports = coarse_pair(rhs, pivots, coupling) if col_count == 2 else coarse_general(rhs, pivots, coupling)
+        tile_values = jnp.dot(scatter_ring, ports.reshape(-1), precision=highest).reshape(ring_count, tile_cols)
+        ring = jnp.repeat(jnp.dot(pick_ring, tile_values, precision=highest), TILE, axis=1) * prolong_scale
+        lifted = jnp.broadcast_to(ring[None, 1:-1], (layers, rows, grid_cols))
+        total = smooth_rows(resid)
+        if outer == ITERS - 1:
+            drop = (lifted if drop is None else drop + lifted) + total
+            break
+        above, below = row_rims(total)
+        lifted_above = jnp.broadcast_to(ring[None, -1:], above.shape)
+        lifted_below = jnp.broadcast_to(ring[None, :1], below.shape)
+        if drop is None:
+            drop = lifted + total
+            drop_halo = (lifted_above + above, lifted_below + below)
+        else:
+            drop = drop + lifted + total
+            drop_halo = ((drop_halo[0] + lifted_above) + above, (drop_halo[1] + lifted_below) + below)
+    back = drop.reshape(layer_count, local_layers, rows, col_count, block_cols).transpose(0, 3, 1, 2, 4)
+    back = lax.all_to_all(back.reshape(group, local_layers, rows, block_cols), ("layer", "col"), 0, 0, tiled=True)
+    drop = back.transpose(1, 0, 2, 3).reshape(local_layers, block_rows, block_cols)
+    return (drop, ports)
+
+
+def shards(*args):
+    group = lax.axis_size("layer") * lax.axis_size("col")
+    block_rows = args[0].shape[1]
+    if block_rows % group == 0 and TILE % (block_rows // group) == 0:
+        return shards_rows(*args)
+    return shards_blocks(*args)
+
+
 def solution(mesh):
     placed = (
         P("layer", "row", "col"),

time: 171 us -> 172 us (level)
  blocking collectives: 0 us -> 10.7 us
  local copies, waits for them, and re-layouts: 24.1 us -> 14.2 us
  other arithmetic: 17.6 us -> 9.84 us
  waiting for transfers between devices: 48.8 us -> 53.1 us
  matrix products: 13 us -> 16.4 us
    ppermute x12, starting transfers between devices: 5.71 us -> 21.5 us  [swap_col(): return lax.ppermute(value, 'col', [(0, 1), (1, 0)])]
    all_to_all x0 -> x1, blocking collectives: none -> 10.7 us  [shards_rows(): lax.all_to_all(back.reshape(group, local_layers, rows, block_cols), ('lay...]
    ppermute x12, waiting for transfers between devices: 21.1 us -> 11.2 us  [swap_col(): return lax.ppermute(value, 'col', [(0, 1), (1, 0)])]
    ppermute x18 -> x12, waiting for transfers between devices: 5.91 us -> 14.8 us  [the longest x6 12.7 us: row_rims(): lax.ppermute(head, ('layer', 'row', 'col'), [(place[i + 1], place[i]) for...]
    all_to_all x4 -> x3, starting transfers between devices: 23.8 us -> 16.3 us  [the longest x2 11 us: shards_rows(): lax.all_to_all(jnp.broadcast_to(tiles[None], (count, tile_cols)), ('layer...]
    ppermute x18 -> x12, starting transfers between devices: 34.9 us -> 27.8 us  [the longest x6 19.8 us: row_rims(): lax.ppermute(tail, ('layer', 'row', 'col'), [(place[i], place[i + 1]) for...]
    all_to_all x4 -> x3, waiting for transfers between devices: 21.7 us -> 27.2 us  [the longest x1 14.3 us: shards_rows(): packed = lax.all_to_all(packed, ('layer', 'col'), 2, 2, tiled=True)]
    slice x12 -> x15, local copies, waits for them, and re-layouts: 7.01 us -> 4.25 us  [neighbours(): lax.slice_in_dim(field, 1, size, axis=dim)]
  transfers between devices with their start and end apart: 34 -> 27, of which waited for: 17 -> 18; matrix products, arithmetic and copies ran while one was open for 21% -> 11% of each run, Pallas kernels for 0% -> 0%
where the time goes in v10:
time: 172 us; the launch traced here: 171 us
  starting transfers between devices  65.6 us (38%)
  waiting for transfers between devices  53.1 us (31%)
  matrix products  16.4 us (10%)
  local copies, waits for them, and re-layouts  14.2 us (8%)
  blocking collectives  10.7 us (6%)
  other arithmetic  9.84 us (6%)
    ppermute x12, starting transfers between devices, swap_col(): return lax.ppermute(value, 'col', [(0, 1), (1, 0)])  21.5 us
    ppermute x6, starting transfers between devices, row_rims(): lax.ppermute(tail, ('layer', 'row', 'col'), [(place[i], place[i + 1]) for...  19.8 us
    all_to_all x1, waiting for transfers between devices, shards_rows(): packed = lax.all_to_all(packed, ('layer', 'col'), 2, 2, tiled=True)  14.3 us
    all_to_all x2, waiting for transfers between devices, shards_rows(): lax.all_to_all(jnp.broadcast_to(tiles[None], (count, tile_cols)), ('layer...  12.9 us
    ppermute x6, waiting for transfers between devices, row_rims(): lax.ppermute(head, ('layer', 'row', 'col'), [(place[i + 1], place[i]) for...  12.7 us
    ppermute x12, waiting for transfers between devices, swap_col(): return lax.ppermute(value, 'col', [(0, 1), (1, 0)])  11.2 us
    all_to_all x2, starting transfers between devices, shards_rows(): lax.all_to_all(jnp.broadcast_to(tiles[None], (count, tile_cols)), ('layer...  11 us
    all_to_all x1, blocking collectives, shards_rows(): lax.all_to_all(back.reshape(group, local_layers, rows, block_cols), ('lay...  10.7 us
  transfers between devices with their start and end apart: 27, of which 18 were waited for; matrix products, arithmetic and copies ran while one was open for 11% of the time, Pallas kernels for 0%

profile of v10, /device:TPU:0, one launch (start us, length us, event | category | flops | bytes accessed | tf_op | source)
XLA Modules:
  0.0 171.4 jit_solution(13632850004973194009)
XLA Ops:
  3.9 5.3 %all-to-all-start = ((f32[4,2,8,8,512]{4,3,1,0,2:T(8,128)}), f32[4,2,8,8,512]{4,3,1,0,2:T(8,128)S(1)}, u32[]{:S(2)}, u32[]{:S(2)}) async-start(f32[4,2,8,8,512]{4,3,1,0,2:T(8,128)} %copy.28), calls=%async_computation | async-start | bytes 2097152 | tf_op jit(solution)/shard_map/all_to_all | solution.py:270
  9.5 14.3 %all-to-all-done = f32[4,2,8,8,512]{4,3,1,0,2:T(8,128)S(1)} async-done(((f32[4,2,8,8,512]{4,3,1,0,2:T(8,128)}), f32[4,2,8,8,512]{4,3,1,0,2:T(8,128)S(1)}, u32[]{:S(2)}, u32[]{:S(2)}) %all-to-all-start) | async-done | bytes 1048608 | tf_op jit(solution)/shard_map/all_to_all | solution.py:270
  28.3 4.9 %all-to-all-start.1 = ((f32[32,1,64]{2,1,0:T(1,128)}), f32[32,1,64]{2,1,0:T(1,128)S(1)}, u32[]{:S(2)}, u32[]{:S(2)}) async-start(f32[32,1,64]{2,1,0:T(1,128)} %broadcast_in_dim.38), calls=%async_computation.1 | async-start | bytes 32768 | tf_op jit(solution)/shard_map/all_to_all | solution.py:353
  33.6 6.6 %all-to-all-done.1 = f32[32,1,64]{2,1,0:T(1,128)S(1)} async-done(((f32[32,1,64]{2,1,0:T(1,128)}), f32[32,1,64]{2,1,0:T(1,128)S(1)}, u32[]{:S(2)}, u32[]{:S(2)}) %all-to-all-start.1) | async-done | bytes 8224 | tf_op jit(solution)/shard_map/all_to_all | solution.py:353
  43.5 3.4 %collective-permute-start.7 = (f32[8,1,1024]{2,1,0:T(1,128)S(1)}, f32[8,1,1024]{2,1,0:T(1,128)S(1)}, u32[]{:S(2)}, u32[]{:S(2)}) collective-permute-start(f32[8,1,1024]{2,1,0:T(1,128)S(1)} %get-tuple-element.63), channel_id=1, source_target_pairs={{0,1},{1,8},{8,9},{9,16},{16,17},{17,24},{24,25},{25,2},{2,3},{3,1... | collective-permute-start | bytes 98312 | tf_op jit(solution)/shard_map/ppermute | solution.py:286
  48.9 2.6 %collective-permute-start.1 = (f32[256]{0:T(256)S(1)}, f32[256]{0:T(256)S(1)}, u32[]{:S(2)}, u32[]{:S(2)}) collective-permute-start(f32[256]{0:T(256)S(1)} %dynamic-slice_subtract_fusion.4), channel_id=1, source_target_pairs={{0,1},{1,0},{2,3},{3,2},{4,5},{5,4},{6,7},{7,6},{8,9},{9,8},{10,11... | collective-permute-start | bytes 3080 | tf_op jit(solution)/shard_map/ppermute | solution.py:118
  51.6 1.5 fusion.50
  53.7 2.0 %collective-permute-start.2 = (f32[256]{0:T(256)S(1)}, f32[256]{0:T(256)S(1)}, u32[]{:S(2)}, u32[]{:S(2)}) collective-permute-start(f32[256]{0:T(256)S(1)} %dynamic-slice_subtract_fusion.3), channel_id=1, source_target_pairs={{0,1},{1,0},{2,3},{3,2},{4,5},{5,4},{6,7},{7,6},{8,9},{9,8},{10,11... | collective-permute-start | bytes 3080 | tf_op jit(solution)/shard_map/ppermute | solution.py:118
  58.3 2.0 %collective-permute-start.3 = (f32[512]{0:T(512)S(1)}, f32[512]{0:T(512)S(1)}, u32[]{:S(2)}, u32[]{:S(2)}) collective-permute-start(f32[512]{0:T(512)S(1)} %pad_maximum_fusion.5), channel_id=1, source_target_pairs={{0,1},{1,0},{2,3},{3,2},{4,5},{5,4},{6,7},{7,6},{8,9},{9,8},{10,11... | collective-permute-start | bytes 6152 | tf_op jit(solution)/shard_map/ppermute | solution.py:118
  62.4 2.0 %collective-permute-start.4 = (f32[512]{0:T(512)S(1)}, f32[512]{0:T(512)S(1)}, u32[]{:S(2)}, u32[]{:S(2)}) collective-permute-start(f32[512]{0:T(512)S(1)} %pad_maximum_fusion.6), channel_id=1, source_target_pairs={{0,1},{1,0},{2,3},{3,2},{4,5},{5,4},{6,7},{7,6},{8,9},{9,8},{10,11... | collective-permute-start | bytes 6152 | tf_op jit(solution)/shard_map/ppermute | solution.py:118
  64.4 1.6 collective-permute-done.4
  66.5 2.1 %collective-permute-start.5 = (f32[1024]{0:T(1024)S(1)}, f32[1024]{0:T(1024)S(1)}, u32[]{:S(2)}, u32[]{:S(2)}) collective-permute-start(f32[1024]{0:T(1024)S(1)} %pad_maximum_fusion.3), channel_id=1, source_target_pairs={{0,1},{1,0},{2,3},{3,2},{4,5},{5,4},{6,7},{7,6},{8,9},{9,8},{10,11... | collective-permute-start | bytes 12296 | tf_op jit(solution)/shard_map/ppermute | solution.py:118
  68.5 1.6 collective-permute-done.5
  71.9 2.1 %fusion.163 = (f32[8,8,1024]{2,1,0:T(8,128)S(1)}, f32[8,8,1024]{2,1,0:T(8,128)S(1)}, f32[8,8,1024]{2,1,0:T(8,128)S(1)}, f32[8,8,1024]{2,1,0:T(8,128)S(1)}, f32[8...) fusion(f32[8,8,1024]{2,1,0:T(8,128)} %squeeze.32, ...), kind=kLoop, calls=%fused_computation.260 | loop fusion | flops 1048576 | bytes 4161024 | tf_op jit(solution)/shard_map/mul | solution.py:318
  74.2 3.9 %collective-permute-start.9 = (f32[8,1,1024]{2,1,0:T(1,128)S(1)}, f32[8,1,1024]{2,1,0:T(1,128)S(1)}, u32[]{:S(2)}, u32[]{:S(2)}) collective-permute-start(f32[8,1,1024]{2,1,0:T(1,128)S(1)} %get-tuple-element.57), channel_id=1, source_target_pairs={{0,1},{1,8},{8,9},{9,16},{16,17},{17,24},{24,25},{25,2},{2,3},{3,1... | collective-permute-start | bytes 98312 | tf_op jit(solution)/shard_map/ppermute | solution.py:286
  79.7 4.2 %collective-permute-done.8 = f32[8,1,1024]{2,1,0:T(1,128)S(1)} collective-permute-done((f32[8,1,1024]{2,1,0:T(1,128)S(1)}, f32[8,1,1024]{2,1,0:T(1,128)S(1)}, u32[]{:S(2)}, u32[]{:S(2)}) %collective-permute-start.8) | collective-permute-done | bytes 32800 | tf_op jit(solution)/shard_map/ppermute | solution.py:287
  84.6 1.6 collective-permute-start.11
  87.8 4.2 %collective-permute-done.10 = f32[8,1,1024]{2,1,0:T(1,128)S(1)} collective-permute-done((f32[8,1,1024]{2,1,0:T(1,128)S(1)}, f32[8,1,1024]{2,1,0:T(1,128)S(1)}, u32[]{:S(2)}, u32[]{:S(2)}) %collective-permute-start.10) | collective-permute-done | bytes 32800 | tf_op jit(solution)/shard_map/ppermute | solution.py:287
  92.8 2.9 %collective-permute-start.13 = (f32[8,1,1024]{2,1,0:T(1,128)S(1)}, f32[8,1,1024]{2,1,0:T(1,128)S(1)}, u32[]{:S(2)}, u32[]{:S(2)}) collective-permute-start(f32[8,1,1024]{2,1,0:T(1,128)S(1)} %get-tuple-element.41), channel_id=1, source_target_pairs={{0,1},{1,8},{8,9},{9,16},{16,17},{17,24},{24,25},{25,2},{2,3},{3,1... | collective-permute-start | bytes 98312 | tf_op jit(solution)/shard_map/ppermute | solution.py:286
  97.4 4.2 %collective-permute-done.12 = f32[8,1,1024]{2,1,0:T(1,128)S(1)} collective-permute-done((f32[8,1,1024]{2,1,0:T(1,128)S(1)}, f32[8,1,1024]{2,1,0:T(1,128)S(1)}, u32[]{:S(2)}, u32[]{:S(2)}) %collective-permute-start.12) | collective-permute-done | bytes 32800 | tf_op jit(solution)/shard_map/ppermute | solution.py:287
  103.9 6.1 %all-to-all-start.2 = ((f32[32,1,64]{2,1,0:T(1,128)}), f32[32,1,64]{2,1,0:T(1,128)S(1)}, u32[]{:S(2)}, u32[]{:S(2)}) async-start(f32[32,1,64]{2,1,0:T(1,128)} %broadcast_in_dim.85), calls=%async_computation.2 | async-start | bytes 32768 | tf_op jit(solution)/shard_map/all_to_all | solution.py:353
  110.9 6.3 %all-to-all-done.2 = f32[32,1,64]{2,1,0:T(1,128)S(1)} async-done(((f32[32,1,64]{2,1,0:T(1,128)}), f32[32,1,64]{2,1,0:T(1,128)S(1)}, u32[]{:S(2)}, u32[]{:S(2)}) %all-to-all-start.2) | async-done | bytes 8224 | tf_op jit(solution)/shard_map/all_to_all | solution.py:353
  120.2 2.1 %collective-permute-done.14 = f32[256]{0:T(256)S(1)} collective-permute-done((f32[256]{0:T(256)S(1)}, f32[256]{0:T(256)S(1)}, u32[]{:S(2)}, u32[]{:S(2)}) %collective-permute-start.14) | collective-permute-done | bytes 1056 | tf_op jit(solution)/shard_map/ppermute | solution.py:118
  124.2 3.3 %collective-permute-start.21 = (f32[8,1,1024]{2,1,0:T(1,128)}, f32[8,1,1024]{2,1,0:T(1,128)S(1)}, u32[]{:S(2)}, u32[]{:S(2)}) collective-permute-start(f32[8,1,1024]{2,1,0:T(1,128)} %get-tuple-element.33), channel_id=1, source_target_pairs={{0,1},{1,8},{8,9},{9,16},{16,17},{17,24},{24,25},{25,2},{2,3},{3,1... | collective-permute-start | bytes 98312 | tf_op jit(solution)/shard_map/ppermute | solution.py:286
  129.4 2.6 %collective-permute-start.16 = (f32[256]{0:T(256)S(1)}, f32[256]{0:T(256)S(1)}, u32[]{:S(2)}, u32[]{:S(2)}) collective-permute-start(f32[256]{0:T(256)S(1)} %dynamic-slice_subtract_fusion), channel_id=1, source_target_pairs={{0,1},{1,0},{2,3},{3,2},{4,5},{5,4},{6,7},{7,6},{8,9},{9,8},{10,11... | collective-permute-start | bytes 3080 | tf_op jit(solution)/shard_map/ppermute | solution.py:118
  134.6 2.1 %collective-permute-start.17 = (f32[512]{0:T(512)S(1)}, f32[512]{0:T(512)S(1)}, u32[]{:S(2)}, u32[]{:S(2)}) collective-permute-start(f32[512]{0:T(512)S(1)} %pad_maximum_fusion.7), channel_id=1, source_target_pairs={{0,1},{1,0},{2,3},{3,2},{4,5},{5,4},{6,7},{7,6},{8,9},{9,8},{10,11... | collective-permute-start | bytes 6152 | tf_op jit(solution)/shard_map/ppermute | solution.py:118
  138.8 2.0 %collective-permute-start.18 = (f32[512]{0:T(512)S(1)}, f32[512]{0:T(512)S(1)}, u32[]{:S(2)}, u32[]{:S(2)}) collective-permute-start(f32[512]{0:T(512)S(1)} %pad_maximum_fusion.8), channel_id=1, source_target_pairs={{0,1},{1,0},{2,3},{3,2},{4,5},{5,4},{6,7},{7,6},{8,9},{9,8},{10,11... | collective-permute-start | bytes 6152 | tf_op jit(solution)/shard_map/ppermute | solution.py:118
  142.9 2.1 %collective-permute-start.19 = (f32[1024]{0:T(1024)S(1)}, f32[1024]{0:T(1024)S(1)}, u32[]{:S(2)}, u32[]{:S(2)}) collective-permute-start(f32[1024]{0:T(1024)S(1)} %pad_maximum_fusion.4), channel_id=1, source_target_pairs={{0,1},{1,0},{2,3},{3,2},{4,5},{5,4},{6,7},{7,6},{8,9},{9,8},{10,11... | collective-permute-start | bytes 12296 | tf_op jit(solution)/shard_map/ppermute | solution.py:118
  144.9 1.6 collective-permute-done.19
  149.2 1.8 %fusion.144 = f32[8,8,1024]{2,1,0:T(8,128)S(1)} fusion(f32[8,8,1024]{2,1,0:T(8,128)S(1)} %copy-done.5, f32[8,8,1024]{2,1,0:T(8,128)S(1)} %get-tuple-element.13, f32[8,8,1023]{2,1,0:T(8,128)} %get-tuple-element.35, f32[8,8,1024]{2,1,0:T(8,128)S(1)} %get-tuple-element.12, f32[8,8,1023]{2,1,0:T(8,128)} %get-tuple-element.34, ...), kind=kLoop, calls=%fused_computation.169 | loop fusion | flops 2293760 | bytes 3636736 | tf_op jit(solution)/shard_map/add | solution.py:324
  152.7 4.6 %collective-permute-start.23 = (f32[8,1,1024]{2,1,0:T(1,128)S(1)}, f32[8,1,1024]{2,1,0:T(1,128)S(1)}, u32[]{:S(2)}, u32[]{:S(2)}) collective-permute-start(f32[8,1,1024]{2,1,0:T(1,128)S(1)} %get-tuple-element.24), channel_id=1, source_target_pairs={{0,1},{1,8},{8,9},{9,16},{16,17},{17,24},{24,25},{25,2},{2,3},{3,1... | collective-permute-start | bytes 98312 | tf_op jit(solution)/shard_map/ppermute | solution.py:286
  160.0 10.7 %all_to_all.28 = f32[8,2,8,512]{3,2,1,0:T(8,128)S(1)} all-to-all(f32[8,2,8,512]{3,2,1,0:T(8,128)S(1)} %bitcast.157), channel_id=1, replica_groups=mesh['layer'=4,'row'=4,'col'=2] {'layer','col'}, dimensions={0} | all-to-all | bytes 524288 | tf_op jit(solution)/shard_map/all_to_all | solution.py:374
  (222 shorter events, 51.4 us)
Async XLA Ops:
  3.9 19.9 %all-to-all-start = ((f32[4,2,8,8,512]{4,3,1,0,2:T(8,128)}), f32[4,2,8,8,512]{4,3,1,0,2:T(8,128)S(1)}, u32[]{:S(2)}, u32[]{:S(2)}) async-start(f32[4,2,8,8,512]{4,3,1,0,2:T(8,128)} %copy.28), calls=%async_computation | async-start | bytes 2097152 | tf_op jit(solution)/shard_map/all_to_all | solution.py:270
  9.3 30.9 %copy-start.25 = (s32[32]{0:T(128)}, s32[32]{0:T(128)S(1)}, u32[]{:S(2)}) copy-start(s32[32]{0:T(128)S(1)} %and_select_fusion) | copy-start | bytes 388
  9.4 61.7 %copy-start.24 = (s32[10]{0:T(128)}, s32[10]{0:T(128)S(1)}, u32[]{:S(2)}) copy-start(s32[10]{0:T(128)S(1)} %fusion.161) | copy-start | bytes 124
  9.4 60.8 %copy-start.23 = (s32[2,64]{1,0:T(2,128)}, s32[2,64]{1,0:T(2,128)S(1)}, u32[]{:S(2)}) copy-start(s32[2,64]{1,0:T(2,128)S(1)} %add_select_fusion.2) | copy-start | bytes 1540
  9.5 30.7 %copy-start.18 = (s32[2048]{0:T(1024)}, s32[2048]{0:T(1024)S(1)}, u32[]{:S(2)}) copy-start(s32[2048]{0:T(1024)S(1)} %get-tuple-element.78) | copy-start | bytes 24580
  9.5 30.7 %copy-start.20 = (s32[2048]{0:T(1024)}, s32[2048]{0:T(1024)S(1)}, u32[]{:S(2)}) copy-start(s32[2048]{0:T(1024)S(1)} %get-tuple-element.79) | copy-start | bytes 24580
  28.3 11.9 %all-to-all-start.1 = ((f32[32,1,64]{2,1,0:T(1,128)}), f32[32,1,64]{2,1,0:T(1,128)S(1)}, u32[]{:S(2)}, u32[]{:S(2)}) async-start(f32[32,1,64]{2,1,0:T(1,128)} %broadcast_in_dim.38), calls=%async_computation.1 | async-start | bytes 32768 | tf_op jit(solution)/shard_map/all_to_all | solution.py:353
  41.8 6.5 %collective-permute-start = (f32[256]{0:T(256)S(1)}, f32[256]{0:T(256)S(1)}, u32[]{:S(2)}, u32[]{:S(2)}) collective-permute-start(f32[256]{0:T(256)S(1)} %dynamic-slice_subtract_fusion.5), channel_id=1, source_target_pairs={{0,1},{1,0},{2,3},{3,2},{4,5},{5,4},{6,7},{7,6},{8,9},{9,8},{10,11... | collective-permute-start | bytes 3080 | tf_op jit(solution)/shard_map/ppermute | solution.py:118
  43.5 28.3 %collective-permute-start.7 = (f32[8,1,1024]{2,1,0:T(1,128)S(1)}, f32[8,1,1024]{2,1,0:T(1,128)S(1)}, u32[]{:S(2)}, u32[]{:S(2)}) collective-permute-start(f32[8,1,1024]{2,1,0:T(1,128)S(1)} %get-tuple-element.63), channel_id=1, source_target_pairs={{0,1},{1,8},{8,9},{9,16},{16,17},{17,24},{24,25},{25,2},{2,3},{3,1... | collective-permute-start | bytes 98312 | tf_op jit(solution)/shard_map/ppermute | solution.py:286
  47.0 24.9 %collective-permute-start.6 = (f32[8,1,1024]{2,1,0:T(1,128)S(1)}, f32[8,1,1024]{2,1,0:T(1,128)S(1)}, u32[]{:S(2)}, u32[]{:S(2)}) collective-permute-start(f32[8,1,1024]{2,1,0:T(1,128)S(1)} %get-tuple-element.62), channel_id=1, source_target_pairs={{1,0},{8,1},{9,8},{16,9},{17,16},{24,17},{25,24},{2,25},{3,2},{10,... | collective-permute-start | bytes 98312 | tf_op jit(solution)/shard_map/ppermute | solution.py:287
  48.9 4.2 %collective-permute-start.1 = (f32[256]{0:T(256)S(1)}, f32[256]{0:T(256)S(1)}, u32[]{:S(2)}, u32[]{:S(2)}) collective-permute-start(f32[256]{0:T(256)S(1)} %dynamic-slice_subtract_fusion.4), channel_id=1, source_target_pairs={{0,1},{1,0},{2,3},{3,2},{4,5},{5,4},{6,7},{7,6},{8,9},{9,8},{10,11... | collective-permute-start | bytes 3080 | tf_op jit(solution)/shard_map/ppermute | solution.py:118
  53.7 3.6 %collective-permute-start.2 = (f32[256]{0:T(256)S(1)}, f32[256]{0:T(256)S(1)}, u32[]{:S(2)}, u32[]{:S(2)}) collective-permute-start(f32[256]{0:T(256)S(1)} %dynamic-slice_subtract_fusion.3), channel_id=1, source_target_pairs={{0,1},{1,0},{2,3},{3,2},{4,5},{5,4},{6,7},{7,6},{8,9},{9,8},{10,11... | collective-permute-start | bytes 3080 | tf_op jit(solution)/shard_map/ppermute | solution.py:118
  58.3 3.6 %collective-permute-start.3 = (f32[512]{0:T(512)S(1)}, f32[512]{0:T(512)S(1)}, u32[]{:S(2)}, u32[]{:S(2)}) collective-permute-start(f32[512]{0:T(512)S(1)} %pad_maximum_fusion.5), channel_id=1, source_target_pairs={{0,1},{1,0},{2,3},{3,2},{4,5},{5,4},{6,7},{7,6},{8,9},{9,8},{10,11... | collective-permute-start | bytes 6152 | tf_op jit(solution)/shard_map/ppermute | solution.py:118
  62.4 3.6 %collective-permute-start.4 = (f32[512]{0:T(512)S(1)}, f32[512]{0:T(512)S(1)}, u32[]{:S(2)}, u32[]{:S(2)}) collective-permute-start(f32[512]{0:T(512)S(1)} %pad_maximum_fusion.6), channel_id=1, source_target_pairs={{0,1},{1,0},{2,3},{3,2},{4,5},{5,4},{6,7},{7,6},{8,9},{9,8},{10,11... | collective-permute-start | bytes 6152 | tf_op jit(solution)/shard_map/ppermute | solution.py:118
  66.5 3.7 %collective-permute-start.5 = (f32[1024]{0:T(1024)S(1)}, f32[1024]{0:T(1024)S(1)}, u32[]{:S(2)}, u32[]{:S(2)}) collective-permute-start(f32[1024]{0:T(1024)S(1)} %pad_maximum_fusion.3), channel_id=1, source_target_pairs={{0,1},{1,0},{2,3},{3,2},{4,5},{5,4},{6,7},{7,6},{8,9},{9,8},{10,11... | collective-permute-start | bytes 12296 | tf_op jit(solution)/shard_map/ppermute | solution.py:118
  74.2 5.5 %collective-permute-start.9 = (f32[8,1,1024]{2,1,0:T(1,128)S(1)}, f32[8,1,1024]{2,1,0:T(1,128)S(1)}, u32[]{:S(2)}, u32[]{:S(2)}) collective-permute-start(f32[8,1,1024]{2,1,0:T(1,128)S(1)} %get-tuple-element.57), channel_id=1, source_target_pairs={{0,1},{1,8},{8,9},{9,16},{16,17},{17,24},{24,25},{25,2},{2,3},{3,1... | collective-permute-start | bytes 98312 | tf_op jit(solution)/shard_map/ppermute | solution.py:286
  78.1 5.8 %collective-permute-start.8 = (f32[8,1,1024]{2,1,0:T(1,128)S(1)}, f32[8,1,1024]{2,1,0:T(1,128)S(1)}, u32[]{:S(2)}, u32[]{:S(2)}) collective-permute-start(f32[8,1,1024]{2,1,0:T(1,128)S(1)} %get-tuple-element.56), channel_id=1, source_target_pairs={{1,0},{8,1},{9,8},{16,9},{17,16},{24,17},{25,24},{2,25},{3,2},{10,... | collective-permute-start | bytes 98312 | tf_op jit(solution)/shard_map/ppermute | solution.py:287
  84.6 3.2 %collective-permute-start.11 = (f32[8,1,1024]{2,1,0:T(1,128)S(1)}, f32[8,1,1024]{2,1,0:T(1,128)S(1)}, u32[]{:S(2)}, u32[]{:S(2)}) collective-permute-start(f32[8,1,1024]{2,1,0:T(1,128)S(1)} %get-tuple-element.49), channel_id=1, source_target_pairs={{0,1},{1,8},{8,9},{9,16},{16,17},{17,24},{24,25},{25,2},{2,3},{3,1... | collective-permute-start | bytes 98312 | tf_op jit(solution)/shard_map/ppermute | solution.py:286
  86.2 5.8 %collective-permute-start.10 = (f32[8,1,1024]{2,1,0:T(1,128)S(1)}, f32[8,1,1024]{2,1,0:T(1,128)S(1)}, u32[]{:S(2)}, u32[]{:S(2)}) collective-permute-start(f32[8,1,1024]{2,1,0:T(1,128)S(1)} %get-tuple-element.48), channel_id=1, source_target_pairs={{1,0},{8,1},{9,8},{16,9},{17,16},{24,17},{25,24},{2,25},{3,2},{10,... | collective-permute-start | bytes 98312 | tf_op jit(solution)/shard_map/ppermute | solution.py:287
  92.8 4.5 %collective-permute-start.13 = (f32[8,1,1024]{2,1,0:T(1,128)S(1)}, f32[8,1,1024]{2,1,0:T(1,128)S(1)}, u32[]{:S(2)}, u32[]{:S(2)}) collective-permute-start(f32[8,1,1024]{2,1,0:T(1,128)S(1)} %get-tuple-element.41), channel_id=1, source_target_pairs={{0,1},{1,8},{8,9},{9,16},{16,17},{17,24},{24,25},{25,2},{2,3},{3,1... | collective-permute-start | bytes 98312 | tf_op jit(solution)/shard_map/ppermute | solution.py:286
  95.8 5.8 %collective-permute-start.12 = (f32[8,1,1024]{2,1,0:T(1,128)S(1)}, f32[8,1,1024]{2,1,0:T(1,128)S(1)}, u32[]{:S(2)}, u32[]{:S(2)}) collective-permute-start(f32[8,1,1024]{2,1,0:T(1,128)S(1)} %get-tuple-element.40), channel_id=1, source_target_pairs={{1,0},{8,1},{9,8},{16,9},{17,16},{24,17},{25,24},{2,25},{3,2},{10,... | collective-permute-start | bytes 98312 | tf_op jit(solution)/shard_map/ppermute | solution.py:287
  103.9 13.2 %all-to-all-start.2 = ((f32[32,1,64]{2,1,0:T(1,128)}), f32[32,1,64]{2,1,0:T(1,128)S(1)}, u32[]{:S(2)}, u32[]{:S(2)}) async-start(f32[32,1,64]{2,1,0:T(1,128)} %broadcast_in_dim.85), calls=%async_computation.2 | async-start | bytes 32768 | tf_op jit(solution)/shard_map/all_to_all | solution.py:353
  118.7 3.6 %collective-permute-start.14 = (f32[256]{0:T(256)S(1)}, f32[256]{0:T(256)S(1)}, u32[]{:S(2)}, u32[]{:S(2)}) collective-permute-start(f32[256]{0:T(256)S(1)} %dynamic-slice_subtract_fusion.2), channel_id=1, source_target_pairs={{0,1},{1,0},{2,3},{3,2},{4,5},{5,4},{6,7},{7,6},{8,9},{9,8},{10,11... | collective-permute-start | bytes 3080 | tf_op jit(solution)/shard_map/ppermute | solution.py:118
  122.9 5.9 %collective-permute-start.15 = (f32[256]{0:T(256)S(1)}, f32[256]{0:T(256)S(1)}, u32[]{:S(2)}, u32[]{:S(2)}) collective-permute-start(f32[256]{0:T(256)S(1)} %dynamic-slice_subtract_fusion.1), channel_id=1, source_target_pairs={{0,1},{1,0},{2,3},{3,2},{4,5},{5,4},{6,7},{7,6},{8,9},{9,8},{10,11... | collective-permute-start | bytes 3080 | tf_op jit(solution)/shard_map/ppermute | solution.py:118
  124.2 25.0 %collective-permute-start.21 = (f32[8,1,1024]{2,1,0:T(1,128)}, f32[8,1,1024]{2,1,0:T(1,128)S(1)}, u32[]{:S(2)}, u32[]{:S(2)}) collective-permute-start(f32[8,1,1024]{2,1,0:T(1,128)} %get-tuple-element.33), channel_id=1, source_target_pairs={{0,1},{1,8},{8,9},{9,16},{16,17},{17,24},{24,25},{25,2},{2,3},{3,1... | collective-permute-start | bytes 98312 | tf_op jit(solution)/shard_map/ppermute | solution.py:286
  127.5 21.7 %collective-permute-start.20 = (f32[8,1,1024]{2,1,0:T(1,128)}, f32[8,1,1024]{2,1,0:T(1,128)S(1)}, u32[]{:S(2)}, u32[]{:S(2)}) collective-permute-start(f32[8,1,1024]{2,1,0:T(1,128)} %get-tuple-element.32), channel_id=1, source_target_pairs={{1,0},{8,1},{9,8},{16,9},{17,16},{24,17},{25,24},{2,25},{3,2},{10,... | collective-permute-start | bytes 98312 | tf_op jit(solution)/shard_map/ppermute | solution.py:287
  129.4 4.2 %collective-permute-start.16 = (f32[256]{0:T(256)S(1)}, f32[256]{0:T(256)S(1)}, u32[]{:S(2)}, u32[]{:S(2)}) collective-permute-start(f32[256]{0:T(256)S(1)} %dynamic-slice_subtract_fusion), channel_id=1, source_target_pairs={{0,1},{1,0},{2,3},{3,2},{4,5},{5,4},{6,7},{7,6},{8,9},{9,8},{10,11... | collective-permute-start | bytes 3080 | tf_op jit(solution)/shard_map/ppermute | solution.py:118
  134.6 3.7 %collective-permute-start.17 = (f32[512]{0:T(512)S(1)}, f32[512]{0:T(512)S(1)}, u32[]{:S(2)}, u32[]{:S(2)}) collective-permute-start(f32[512]{0:T(512)S(1)} %pad_maximum_fusion.7), channel_id=1, source_target_pairs={{0,1},{1,0},{2,3},{3,2},{4,5},{5,4},{6,7},{7,6},{8,9},{9,8},{10,11... | collective-permute-start | bytes 6152 | tf_op jit(solution)/shard_map/ppermute | solution.py:118
  138.8 3.6 %collective-permute-start.18 = (f32[512]{0:T(512)S(1)}, f32[512]{0:T(512)S(1)}, u32[]{:S(2)}, u32[]{:S(2)}) collective-permute-start(f32[512]{0:T(512)S(1)} %pad_maximum_fusion.8), channel_id=1, source_target_pairs={{0,1},{1,0},{2,3},{3,2},{4,5},{5,4},{6,7},{7,6},{8,9},{9,8},{10,11... | collective-permute-start | bytes 6152 | tf_op jit(solution)/shard_map/ppermute | solution.py:118
  142.9 3.7 %collective-permute-start.19 = (f32[1024]{0:T(1024)S(1)}, f32[1024]{0:T(1024)S(1)}, u32[]{:S(2)}, u32[]{:S(2)}) collective-permute-start(f32[1024]{0:T(1024)S(1)} %pad_maximum_fusion.4), channel_id=1, source_target_pairs={{0,1},{1,0},{2,3},{3,2},{4,5},{5,4},{6,7},{7,6},{8,9},{9,8},{10,11... | collective-permute-start | bytes 12296 | tf_op jit(solution)/shard_map/ppermute | solution.py:118
  151.3 6.0 %collective-permute-start.22 = (f32[8,1,1024]{2,1,0:T(1,128)S(1)}, f32[8,1,1024]{2,1,0:T(1,128)S(1)}, u32[]{:S(2)}, u32[]{:S(2)}) collective-permute-start(f32[8,1,1024]{2,1,0:T(1,128)S(1)} %get-tuple-element.25), channel_id=1, source_target_pairs={{1,0},{8,1},{9,8},{16,9},{17,16},{24,17},{25,24},{2,25},{3,2},{10,... | collective-permute-start | bytes 98312 | tf_op jit(solution)/shard_map/ppermute | solution.py:287
  152.7 6.1 %collective-permute-start.23 = (f32[8,1,1024]{2,1,0:T(1,128)S(1)}, f32[8,1,1024]{2,1,0:T(1,128)S(1)}, u32[]{:S(2)}, u32[]{:S(2)}) collective-permute-start(f32[8,1,1024]{2,1,0:T(1,128)S(1)} %get-tuple-element.24), channel_id=1, source_target_pairs={{0,1},{1,8},{8,9},{9,16},{16,17},{17,24},{24,25},{25,2},{2,3},{3,1... | collective-permute-start | bytes 98312 | tf_op jit(solution)/shard_map/ppermute | solution.py:286
  (22 other events, 207.0 us)

commit v11 on v8

--- a/solution.py
+++ b/solution.py
@@ -17,6 +17,7 @@
 prolong_scale = 0.5
 
 highest = lax.Precision.HIGHEST
+solve_precision = lax.Precision.HIGH
 GRID_AXES = (("layer", 0), ("row", 1), ("col", 2))
 ROW_AXES = ("layer", "row")
 
@@ -131,18 +132,18 @@
     full = rhs[0]
     forward = [full]
     for section in range(1, NPANEL):
-        piece = own(rhs[section]) - jnp.dot(coupling[section - 1], full, precision=highest)
+        piece = own(rhs[section]) - jnp.dot(coupling[section - 1], full, precision=solve_precision)
         full = join_halves(piece, swap_col(piece), low)
         forward.append(full)
-    scaled = [jnp.dot(pivots[section], forward[section], precision=highest) for section in range(NPANEL)]
+    scaled = [jnp.dot(pivots[section], forward[section], precision=solve_precision) for section in range(NPANEL)]
     mine = scaled[NPANEL - 1]
     results = [None] * NPANEL
     for section in range(NPANEL - 2, 0, -1):
-        partial = jnp.dot(mine, coupling[section], precision=highest)
+        partial = jnp.dot(mine, coupling[section], precision=solve_precision)
         got = swap_col(jnp.concatenate([other_half(partial), mine]))
         results[section + 1] = join_halves(mine, got[share:], low)
         mine = scaled[section] - (own(partial) + got[:share])
-    partial = jnp.dot(mine, coupling[0], precision=highest)
+    partial = jnp.dot(mine, coupling[0], precision=solve_precision)
     got = swap_col(jnp.concatenate([partial, scaled[0], mine]))
     results[1] = join_halves(mine, got[PANEL + share:], low)
     first = join_halves(scaled[0], got[PANEL:PANEL + share], low)
@@ -159,17 +160,17 @@
     forward = [full]
     for section in range(1, NPANEL):
         piece = lax.dynamic_slice_in_dim(rhs[section], start, share) - jnp.dot(
-            coupling[section - 1], full, precision=highest
+            coupling[section - 1], full, precision=solve_precision
         )
         full = lax.all_gather(piece, "col", axis=0, tiled=True)
         forward.append(full)
-    scaled = [jnp.dot(pivots[section], forward[section], precision=highest) for section in range(NPANEL)]
+    scaled = [jnp.dot(pivots[section], forward[section], precision=solve_precision) for section in range(NPANEL)]
     results = [None] * NPANEL
     for section in range(NPANEL - 1, -1, -1):
         placed = lax.dynamic_update_slice_in_dim(jnp.zeros((PANEL,), jnp.float32), scaled[section], start, 0)
         if section < NPANEL - 1:
             later_rows = lax.dynamic_slice_in_dim(results[section + 1], start, share)
-            placed = placed - jnp.dot(later_rows, coupling[section], precision=highest)
+            placed = placed - jnp.dot(later_rows, coupling[section], precision=solve_precision)
         results[section] = lax.psum(placed, "col")
     return jnp.stack(results)
 

time: 169 us -> 167 us (0.988)
  matrix products: 13 us -> 9.51 us
    dot_general x20, matrix products: 10.3 us -> 6.78 us  [the longest x8 3.51 us: coarse_pair(): jnp.dot(pivots[section], forward[section], precision=solve_precision)]
  transfers between devices with their start and end apart: 35 -> 35, of which waited for: 19 -> 19; matrix products, arithmetic and copies ran while one was open for 18% -> 16% of each run, Pallas kernels for 0% -> 0%
where the time goes in v11:
time: 167 us; the launch traced here: 166 us
  starting transfers between devices  67.9 us (41%)
  waiting for transfers between devices  54.4 us (33%)
  local copies, waits for them, and re-layouts  19.6 us (12%)
  other arithmetic  12.8 us (8%)
  matrix products  9.51 us (6%)
  between operations  1.77 us (1%)
    ppermute x12, waiting for transfers between devices, swap_col(): return lax.ppermute(value, 'col', [(0, 1), (1, 0)])  22 us
    ppermute x6, starting transfers between devices, rims(): lax.ppermute(tail, axis, [(place[i], place[i + 1]) for i in range(count -...  19.2 us
    all_to_all x2, starting transfers between devices, share_tiles(): got = lax.all_to_all(payload, ('layer', 'row', 'col'), 0, 0, tiled=True)  14 us
    all_to_all x2, waiting for transfers between devices, share_tiles(): got = lax.all_to_all(payload, ('layer', 'row', 'col'), 0, 0, tiled=True)  12.3 us
    ppermute x12, starting transfers between devices, swap_col(): return lax.ppermute(value, 'col', [(0, 1), (1, 0)])  8.6 us
    ppermute x6, starting transfers between devices, rims(): lax.ppermute(head, axis, [(place[i + 1], place[i]) for i in range(count -...  7.87 us
    ppermute x6, starting transfers between devices, rims(): got = lax.ppermute(jnp.where(low, tail, head), axis, [(0, 1), (1, 0)])  6.16 us
    ppermute x6, waiting for transfers between devices, rims(): got = lax.ppermute(jnp.where(low, tail, head), axis, [(0, 1), (1, 0)])  5.96 us
  transfers between devices with their start and end apart: 35, of which 19 were waited for; matrix products, arithmetic and copies ran while one was open for 16% of the time, Pallas kernels for 0%

profile of v11, /device:TPU:0, one launch (start us, length us, event | category | flops | bytes accessed | tf_op | source)
XLA Modules:
  0.0 166.0 jit_solution(1680504734173785301)
XLA Ops:
  0.6 1.9 %copy.24 = f32[2,64,512]{2,0,1:T(2,128)} copy(f32[2,64,512]{2,1,0:T(8,128)} %param.8) | data formatting | bytes 524288 | tf_op args[0]
  2.5 4.2 %all-to-all-start = ((f32[2,64,512]{2,0,1:T(2,128)}), f32[2,64,512]{2,0,1:T(2,128)S(1)}, u32[]{:S(2)}, u32[]{:S(2)}) async-start(f32[2,64,512]{2,0,1:T(2,128)} %copy.24), calls=%async_computation | async-start | bytes 524288 | tf_op jit(solution)/shard_map/all_to_all | solution.py:191
  8.7 4.1 %all-to-all-done = f32[2,64,512]{2,0,1:T(2,128)S(1)} async-done(((f32[2,64,512]{2,0,1:T(2,128)}), f32[2,64,512]{2,0,1:T(2,128)S(1)}, u32[]{:S(2)}, u32[]{:S(2)}) %all-to-all-start) | async-done | bytes 262176 | tf_op jit(solution)/shard_map/all_to_all | solution.py:191
  13.7 5.5 %all-to-all-start.1 = ((f32[32,1,32]{2,1,0:T(1,128)}), f32[32,1,32]{2,1,0:T(1,128)S(1)}, u32[]{:S(2)}, u32[]{:S(2)}) async-start(f32[32,1,32]{2,1,0:T(1,128)} %broadcast_in_dim.27), calls=%async_computation.1 | async-start | bytes 32768 | tf_op jit(solution)/shard_map/all_to_all | solution.py:107
  20.5 5.8 %all-to-all-done.1 = f32[32,1,32]{2,1,0:T(1,128)S(1)} async-done(((f32[32,1,32]{2,1,0:T(1,128)}), f32[32,1,32]{2,1,0:T(1,128)S(1)}, u32[]{:S(2)}, u32[]{:S(2)}) %all-to-all-start.1) | async-done | bytes 4128 | tf_op jit(solution)/shard_map/all_to_all | solution.py:107
  26.3 3.5 %all-to-all-start.2 = ((f32[2,2,64,512]{3,1,0,2:T(2,128)}), f32[2,2,64,512]{3,1,0,2:T(2,128)S(1)}, u32[]{:S(2)}, u32[]{:S(2)}) async-start(f32[2,2,64,512]{3,1,0,2:T(2,128)} %copy.25), calls=%async_computation.2 | async-start | bytes 1048576 | tf_op jit(solution)/shard_map/all_to_all | solution.py:189
  37.1 1.6 collective-permute-done.1
  40.0 2.6 %collective-permute-done.2 = f32[256]{0:T(256)S(1)} collective-permute-done((f32[256]{0:T(256)S(1)}, f32[256]{0:T(256)S(1)}, u32[]{:S(2)}, u32[]{:S(2)}) %collective-permute-start.2) | collective-permute-done | bytes 1056 | tf_op jit(solution)/shard_map/ppermute | solution.py:119
  44.3 2.7 %collective-permute-done.3 = f32[512]{0:T(512)S(1)} collective-permute-done((f32[512]{0:T(512)S(1)}, f32[512]{0:T(512)S(1)}, u32[]{:S(2)}, u32[]{:S(2)}) %collective-permute-start.3) | collective-permute-done | bytes 2080 | tf_op jit(solution)/shard_map/ppermute | solution.py:119
  48.0 3.0 %collective-permute-done.4 = f32[512]{0:T(512)S(1)} collective-permute-done((f32[512]{0:T(512)S(1)}, f32[512]{0:T(512)S(1)}, u32[]{:S(2)}, u32[]{:S(2)}) %collective-permute-start.4) | collective-permute-done | bytes 2080 | tf_op jit(solution)/shard_map/ppermute | solution.py:119
  51.9 3.0 %collective-permute-done.5 = f32[1024]{0:T(1024)S(1)} collective-permute-done((f32[1024]{0:T(1024)S(1)}, f32[1024]{0:T(1024)S(1)}, u32[]{:S(2)}, u32[]{:S(2)}) %collective-permute-start.5) | collective-permute-done | bytes 4128 | tf_op jit(solution)/shard_map/ppermute | solution.py:119
  57.3 1.4 collective-permute-start.6
  58.8 3.0 %collective-permute-start.7 = (f32[8,1,512]{2,1,0:T(1,128)S(1)}, f32[8,1,512]{2,1,0:T(1,128)S(1)}, u32[]{:S(2)}, u32[]{:S(2)}) collective-permute-start(f32[8,1,512]{2,1,0:T(1,128)S(1)} %get-tuple-element.59), channel_id=1, source_target_pairs={{0,8},{8,16},{16,24},{24,2},{2,10},{10,18},{18,26},{26,4},{4,12},{... | collective-permute-start | bytes 49160 | tf_op jit(solution)/shard_map/ppermute | solution.py:49
  62.6 3.6 %collective-permute-done.8 = f32[8,16,1]{2,1,0:T(8,128)S(1)} collective-permute-done((f32[8,16,1]{2,1,0:T(8,128)S(1)}, f32[8,16,1]{2,1,0:T(8,128)S(1)}, u32[]{:S(2)}, u32[]{:S(2)}) %collective-permute-start.8) | collective-permute-done | bytes 544 | tf_op jit(solution)/shard_map/ppermute | solution.py:46
  69.2 3.0 %collective-permute-start.10 = (f32[8,1,512]{2,1,0:T(1,128)S(1)}, f32[8,1,512]{2,1,0:T(1,128)S(1)}, u32[]{:S(2)}, u32[]{:S(2)}) collective-permute-start(f32[8,1,512]{2,1,0:T(1,128)S(1)} %get-tuple-element.53), channel_id=1, source_target_pairs={{0,8},{8,16},{16,24},{24,2},{2,10},{10,18},{18,26},{26,4},{4,12},{... | collective-permute-start | bytes 49160 | tf_op jit(solution)/shard_map/ppermute | solution.py:49
  73.9 1.5 collective-permute-start.14
  75.4 3.2 %collective-permute-start.13 = (f32[8,1,512]{2,1,0:T(1,128)S(1)}, f32[8,1,512]{2,1,0:T(1,128)S(1)}, u32[]{:S(2)}, u32[]{:S(2)}) collective-permute-start(f32[8,1,512]{2,1,0:T(1,128)S(1)} %get-tuple-element.44), channel_id=1, source_target_pairs={{0,8},{8,16},{16,24},{24,2},{2,10},{10,18},{18,26},{26,4},{4,12},{... | collective-permute-start | bytes 49160 | tf_op jit(solution)/shard_map/ppermute | solution.py:49
  79.9 3.8 %collective-permute-done.12 = f32[8,1,512]{2,1,0:T(1,128)S(1)} collective-permute-done((f32[8,1,512]{2,1,0:T(1,128)S(1)}, f32[8,1,512]{2,1,0:T(1,128)S(1)}, u32[]{:S(2)}, u32[]{:S(2)}) %collective-permute-start.12) | collective-permute-done | bytes 16416 | tf_op jit(solution)/shard_map/ppermute | solution.py:50
  86.6 4.7 %collective-permute-start.16 = (f32[8,1,512]{2,1,0:T(1,128)S(1)}, f32[8,1,512]{2,1,0:T(1,128)S(1)}, u32[]{:S(2)}, u32[]{:S(2)}) collective-permute-start(f32[8,1,512]{2,1,0:T(1,128)S(1)} %get-tuple-element.37), channel_id=1, source_target_pairs={{0,8},{8,16},{16,24},{24,2},{2,10},{10,18},{18,26},{26,4},{4,12},{... | collective-permute-start | bytes 49160 | tf_op jit(solution)/shard_map/ppermute | solution.py:49
  96.2 8.5 %all-to-all-start.3 = ((f32[32,1,32]{2,1,0:T(1,128)}), f32[32,1,32]{2,1,0:T(1,128)S(1)}, u32[]{:S(2)}, u32[]{:S(2)}) async-start(f32[32,1,32]{2,1,0:T(1,128)} %broadcast_in_dim.35), calls=%async_computation.3 | async-start | bytes 32768 | tf_op jit(solution)/shard_map/all_to_all | solution.py:107
  105.3 6.5 %all-to-all-done.3 = f32[32,1,32]{2,1,0:T(1,128)S(1)} async-done(((f32[32,1,32]{2,1,0:T(1,128)}), f32[32,1,32]{2,1,0:T(1,128)S(1)}, u32[]{:S(2)}, u32[]{:S(2)}) %all-to-all-start.3) | async-done | bytes 4128 | tf_op jit(solution)/shard_map/all_to_all | solution.py:107
  115.1 3.2 %collective-permute-start.25 = (f32[8,1,512]{2,1,0:T(1,128)}, f32[8,1,512]{2,1,0:T(1,128)S(1)}, u32[]{:S(2)}, u32[]{:S(2)}) collective-permute-start(f32[8,1,512]{2,1,0:T(1,128)} %get-tuple-element.29), channel_id=1, source_target_pairs={{0,8},{8,16},{16,24},{24,2},{2,10},{10,18},{18,26},{26,4},{4,12},{... | collective-permute-start | bytes 49160 | tf_op jit(solution)/shard_map/ppermute | solution.py:49
  118.3 1.5 collective-permute-start.26
  120.8 2.3 %collective-permute-done.26 = f32[8,16,1]{2,1,0:T(8,128)S(1)} collective-permute-done((f32[8,16,1]{2,1,0:T(8,128)S(1)}, f32[8,16,1]{2,1,0:T(8,128)S(1)}, u32[]{:S(2)}, u32[]{:S(2)}) %collective-permute-start.26) | collective-permute-done | bytes 544 | tf_op jit(solution)/shard_map/ppermute | solution.py:46
  125.4 2.4 %collective-permute-done.20 = f32[256]{0:T(256)S(1)} collective-permute-done((f32[256]{0:T(256)S(1)}, f32[256]{0:T(256)S(1)}, u32[]{:S(2)}, u32[]{:S(2)}) %collective-permute-start.20) | collective-permute-done | bytes 1056 | tf_op jit(solution)/shard_map/ppermute | solution.py:119
  129.7 2.4 %collective-permute-done.21 = f32[512]{0:T(512)S(1)} collective-permute-done((f32[512]{0:T(512)S(1)}, f32[512]{0:T(512)S(1)}, u32[]{:S(2)}, u32[]{:S(2)}) %collective-permute-start.21) | collective-permute-done | bytes 2080 | tf_op jit(solution)/shard_map/ppermute | solution.py:119
  133.7 2.4 %collective-permute-done.22 = f32[512]{0:T(512)S(1)} collective-permute-done((f32[512]{0:T(512)S(1)}, f32[512]{0:T(512)S(1)}, u32[]{:S(2)}, u32[]{:S(2)}) %collective-permute-start.22) | collective-permute-done | bytes 2080 | tf_op jit(solution)/shard_map/ppermute | solution.py:119
  142.5 2.0 %collective-permute-start.28 = (f32[8,1,512]{2,1,0:T(1,128)}, f32[8,1,512]{2,1,0:T(1,128)}, u32[]{:S(2)}, u32[]{:S(2)}) collective-permute-start(f32[8,1,512]{2,1,0:T(1,128)} %get-tuple-element.20), channel_id=1, source_target_pairs={{0,8},{8,16},{16,24},{24,2},{2,10},{10,18},{18,26},{26,4},{4,12},{... | collective-permute-start | bytes 49160 | tf_op jit(solution)/shard_map/ppermute | solution.py:49
  148.9 1.7 %reshape.592 = f32[512,18]{0,1:T(8,128)} reshape(f32[32,16,18]{1,0,2:T(8,128)} %broadcast_in_dim.36) | data formatting | bytes 73728 | tf_op jit(solution)/shard_map/reshape | solution.py:180
  151.7 3.3 %fusion.121 = f32[8,16,512]{2,1,0:T(8,128)} fusion(f32[8,16,512]{2,1,0:T(8,128)S(1)} %copy-done.12, f32[1,16,512]{2,1,0:T(8,128)S(1)} %multiply_bitcast_fusion.1, f32[8,16,512]{2,1,0:T(8,128)S(1)} %copy-done.6, f32[8,1,512]{2,1,0:T(1,128)} %collective-permute-done.27, f32[8,15,512]{2,1,0:T(8,128)} %get-tuple-element.23, ...), kind=kLoop, calls=%fused_computation.133 | loop fusion | flops 3997696 | bytes 5996544 | tf_op jit(solution)/shard_map/add | solution.py:248
  154.9 4.4 %all-to-all-start.4 = ((f32[8,16,512]{2,1,0:T(8,128)}), f32[8,16,512]{2,1,0:T(8,128)S(1)}, u32[]{:S(2)}, u32[]{:S(2)}) async-start(f32[8,16,512]{2,1,0:T(8,128)} %fusion.121), calls=%async_computation.4 | async-start | bytes 524288 | tf_op jit(solution)/shard_map/all_to_all | solution.py:260
  160.6 4.7 %all-to-all-done.4 = f32[8,16,512]{2,1,0:T(8,128)S(1)} async-done(((f32[8,16,512]{2,1,0:T(8,128)}), f32[8,16,512]{2,1,0:T(8,128)S(1)}, u32[]{:S(2)}, u32[]{:S(2)}) %all-to-all-start.4) | async-done | bytes 262176 | tf_op jit(solution)/shard_map/all_to_all | solution.py:260
  (270 shorter events, 56.8 us)
Async XLA Ops:
  2.5 10.2 %all-to-all-start = ((f32[2,64,512]{2,0,1:T(2,128)}), f32[2,64,512]{2,0,1:T(2,128)S(1)}, u32[]{:S(2)}, u32[]{:S(2)}) async-start(f32[2,64,512]{2,0,1:T(2,128)} %copy.24), calls=%async_computation | async-start | bytes 524288 | tf_op jit(solution)/shard_map/all_to_all | solution.py:191
  13.7 12.6 %all-to-all-start.1 = ((f32[32,1,32]{2,1,0:T(1,128)}), f32[32,1,32]{2,1,0:T(1,128)S(1)}, u32[]{:S(2)}, u32[]{:S(2)}) async-start(f32[32,1,32]{2,1,0:T(1,128)} %broadcast_in_dim.27), calls=%async_computation.1 | async-start | bytes 32768 | tf_op jit(solution)/shard_map/all_to_all | solution.py:107
  26.3 30.6 %all-to-all-start.2 = ((f32[2,2,64,512]{3,1,0,2:T(2,128)}), f32[2,2,64,512]{3,1,0,2:T(2,128)S(1)}, u32[]{:S(2)}, u32[]{:S(2)}) async-start(f32[2,2,64,512]{3,1,0,2:T(2,128)} %copy.25), calls=%async_computation.2 | async-start | bytes 1048576 | tf_op jit(solution)/shard_map/all_to_all | solution.py:189
  31.1 3.6 %collective-permute-start = (f32[256]{0:T(256)S(1)}, f32[256]{0:T(256)S(1)}, u32[]{:S(2)}, u32[]{:S(2)}) collective-permute-start(f32[256]{0:T(256)S(1)} %dynamic-slice_subtract_fusion.5), channel_id=1, source_target_pairs={{0,1},{1,0},{2,3},{3,2},{4,5},{5,4},{6,7},{7,6},{8,9},{9,8},{10,11... | collective-permute-start | bytes 3080 | tf_op jit(solution)/shard_map/ppermute | solution.py:119
  35.1 3.6 %collective-permute-start.1 = (f32[256]{0:T(256)S(1)}, f32[256]{0:T(256)S(1)}, u32[]{:S(2)}, u32[]{:S(2)}) collective-permute-start(f32[256]{0:T(256)S(1)} %dynamic-slice_subtract_fusion.4), channel_id=1, source_target_pairs={{0,1},{1,0},{2,3},{3,2},{4,5},{5,4},{6,7},{7,6},{8,9},{9,8},{10,11... | collective-permute-start | bytes 3080 | tf_op jit(solution)/shard_map/ppermute | solution.py:119
  43.3 3.6 %collective-permute-start.3 = (f32[512]{0:T(512)S(1)}, f32[512]{0:T(512)S(1)}, u32[]{:S(2)}, u32[]{:S(2)}) collective-permute-start(f32[512]{0:T(512)S(1)} %pad_maximum_fusion.4), channel_id=1, source_target_pairs={{0,1},{1,0},{2,3},{3,2},{4,5},{5,4},{6,7},{7,6},{8,9},{9,8},{10,11... | collective-permute-start | bytes 6152 | tf_op jit(solution)/shard_map/ppermute | solution.py:119
  47.3 3.6 %collective-permute-start.4 = (f32[512]{0:T(512)S(1)}, f32[512]{0:T(512)S(1)}, u32[]{:S(2)}, u32[]{:S(2)}) collective-permute-start(f32[512]{0:T(512)S(1)} %pad_maximum_fusion.5), channel_id=1, source_target_pairs={{0,1},{1,0},{2,3},{3,2},{4,5},{5,4},{6,7},{7,6},{8,9},{9,8},{10,11... | collective-permute-start | bytes 6152 | tf_op jit(solution)/shard_map/ppermute | solution.py:119
  51.2 3.7 %collective-permute-start.5 = (f32[1024]{0:T(1024)S(1)}, f32[1024]{0:T(1024)S(1)}, u32[]{:S(2)}, u32[]{:S(2)}) collective-permute-start(f32[1024]{0:T(1024)S(1)} %pad_maximum_fusion.2), channel_id=1, source_target_pairs={{0,1},{1,0},{2,3},{3,2},{4,5},{5,4},{6,7},{7,6},{8,9},{9,8},{10,11... | collective-permute-start | bytes 12296 | tf_op jit(solution)/shard_map/ppermute | solution.py:119
  57.3 8.9 %collective-permute-start.6 = (f32[8,1,512]{2,1,0:T(1,128)S(1)}, f32[8,1,512]{2,1,0:T(1,128)S(1)}, u32[]{:S(2)}, u32[]{:S(2)}) collective-permute-start(f32[8,1,512]{2,1,0:T(1,128)S(1)} %get-tuple-element.58), channel_id=1, source_target_pairs={{8,0},{16,8},{24,16},{2,24},{10,2},{18,10},{26,18},{4,26},{12,4},{... | collective-permute-start | bytes 49160 | tf_op jit(solution)/shard_map/ppermute | solution.py:50
  58.8 7.5 %collective-permute-start.7 = (f32[8,1,512]{2,1,0:T(1,128)S(1)}, f32[8,1,512]{2,1,0:T(1,128)S(1)}, u32[]{:S(2)}, u32[]{:S(2)}) collective-permute-start(f32[8,1,512]{2,1,0:T(1,128)S(1)} %get-tuple-element.59), channel_id=1, source_target_pairs={{0,8},{8,16},{16,24},{24,2},{2,10},{10,18},{18,26},{26,4},{4,12},{... | collective-permute-start | bytes 49160 | tf_op jit(solution)/shard_map/ppermute | solution.py:49
  61.8 4.4 %collective-permute-start.8 = (f32[8,16,1]{2,1,0:T(8,128)S(1)}, f32[8,16,1]{2,1,0:T(8,128)S(1)}, u32[]{:S(2)}, u32[]{:S(2)}) collective-permute-start(f32[8,16,1]{2,1,0:T(8,128)S(1)} %slice_select_fusion.5), channel_id=1, source_target_pairs={{0,1},{1,0},{2,3},{3,2},{4,5},{5,4},{6,7},{7,6},{8,9},{9,8},{10,11... | collective-permute-start | bytes 1544 | tf_op jit(solution)/shard_map/ppermute | solution.py:46
  67.2 5.1 %collective-permute-start.11 = (f32[8,16,1]{2,1,0:T(8,128)S(1)}, f32[8,16,1]{2,1,0:T(8,128)S(1)}, u32[]{:S(2)}, u32[]{:S(2)}) collective-permute-start(f32[8,16,1]{2,1,0:T(8,128)S(1)} %slice_select_fusion.4), channel_id=1, source_target_pairs={{0,1},{1,0},{2,3},{3,2},{4,5},{5,4},{6,7},{7,6},{8,9},{9,8},{10,11... | collective-permute-start | bytes 1544 | tf_op jit(solution)/shard_map/ppermute | solution.py:46
  67.9 4.4 %collective-permute-start.9 = (f32[8,1,512]{2,1,0:T(1,128)S(1)}, f32[8,1,512]{2,1,0:T(1,128)S(1)}, u32[]{:S(2)}, u32[]{:S(2)}) collective-permute-start(f32[8,1,512]{2,1,0:T(1,128)S(1)} %get-tuple-element.52), channel_id=1, source_target_pairs={{8,0},{16,8},{24,16},{2,24},{10,2},{18,10},{26,18},{4,26},{12,4},{... | collective-permute-start | bytes 49160 | tf_op jit(solution)/shard_map/ppermute | solution.py:50
  69.2 3.9 %collective-permute-start.10 = (f32[8,1,512]{2,1,0:T(1,128)S(1)}, f32[8,1,512]{2,1,0:T(1,128)S(1)}, u32[]{:S(2)}, u32[]{:S(2)}) collective-permute-start(f32[8,1,512]{2,1,0:T(1,128)S(1)} %get-tuple-element.53), channel_id=1, source_target_pairs={{0,8},{8,16},{16,24},{24,2},{2,10},{10,18},{18,26},{26,4},{4,12},{... | collective-permute-start | bytes 49160 | tf_op jit(solution)/shard_map/ppermute | solution.py:49
  73.9 6.0 %collective-permute-start.14 = (f32[8,16,1]{2,1,0:T(8,128)S(1)}, f32[8,16,1]{2,1,0:T(8,128)S(1)}, u32[]{:S(2)}, u32[]{:S(2)}) collective-permute-start(f32[8,16,1]{2,1,0:T(8,128)S(1)} %slice_select_fusion.3), channel_id=1, source_target_pairs={{0,1},{1,0},{2,3},{3,2},{4,5},{5,4},{6,7},{7,6},{8,9},{9,8},{10,11... | collective-permute-start | bytes 1544 | tf_op jit(solution)/shard_map/ppermute | solution.py:46
  75.4 4.5 %collective-permute-start.13 = (f32[8,1,512]{2,1,0:T(1,128)S(1)}, f32[8,1,512]{2,1,0:T(1,128)S(1)}, u32[]{:S(2)}, u32[]{:S(2)}) collective-permute-start(f32[8,1,512]{2,1,0:T(1,128)S(1)} %get-tuple-element.44), channel_id=1, source_target_pairs={{0,8},{8,16},{16,24},{24,2},{2,10},{10,18},{18,26},{26,4},{4,12},{... | collective-permute-start | bytes 49160 | tf_op jit(solution)/shard_map/ppermute | solution.py:49
  78.6 5.2 %collective-permute-start.12 = (f32[8,1,512]{2,1,0:T(1,128)S(1)}, f32[8,1,512]{2,1,0:T(1,128)S(1)}, u32[]{:S(2)}, u32[]{:S(2)}) collective-permute-start(f32[8,1,512]{2,1,0:T(1,128)S(1)} %get-tuple-element.45), channel_id=1, source_target_pairs={{8,0},{16,8},{24,16},{2,24},{10,2},{18,10},{26,18},{4,26},{12,4},{... | collective-permute-start | bytes 49160 | tf_op jit(solution)/shard_map/ppermute | solution.py:50
  84.6 6.8 %collective-permute-start.17 = (f32[8,16,1]{2,1,0:T(8,128)S(1)}, f32[8,16,1]{2,1,0:T(8,128)S(1)}, u32[]{:S(2)}, u32[]{:S(2)}) collective-permute-start(f32[8,16,1]{2,1,0:T(8,128)S(1)} %slice_select_fusion.2), channel_id=1, source_target_pairs={{0,1},{1,0},{2,3},{3,2},{4,5},{5,4},{6,7},{7,6},{8,9},{9,8},{10,11... | collective-permute-start | bytes 1544 | tf_op jit(solution)/shard_map/ppermute | solution.py:46
  85.3 6.1 %collective-permute-start.15 = (f32[8,1,512]{2,1,0:T(1,128)S(1)}, f32[8,1,512]{2,1,0:T(1,128)S(1)}, u32[]{:S(2)}, u32[]{:S(2)}) collective-permute-start(f32[8,1,512]{2,1,0:T(1,128)S(1)} %get-tuple-element.36), channel_id=1, source_target_pairs={{8,0},{16,8},{24,16},{2,24},{10,2},{18,10},{26,18},{4,26},{12,4},{... | collective-permute-start | bytes 49160 | tf_op jit(solution)/shard_map/ppermute | solution.py:50
  86.6 5.6 %collective-permute-start.16 = (f32[8,1,512]{2,1,0:T(1,128)S(1)}, f32[8,1,512]{2,1,0:T(1,128)S(1)}, u32[]{:S(2)}, u32[]{:S(2)}) collective-permute-start(f32[8,1,512]{2,1,0:T(1,128)S(1)} %get-tuple-element.37), channel_id=1, source_target_pairs={{0,8},{8,16},{16,24},{24,2},{2,10},{10,18},{18,26},{26,4},{4,12},{... | collective-permute-start | bytes 49160 | tf_op jit(solution)/shard_map/ppermute | solution.py:49
  96.2 15.6 %all-to-all-start.3 = ((f32[32,1,32]{2,1,0:T(1,128)}), f32[32,1,32]{2,1,0:T(1,128)S(1)}, u32[]{:S(2)}, u32[]{:S(2)}) async-start(f32[32,1,32]{2,1,0:T(1,128)} %broadcast_in_dim.35), calls=%async_computation.3 | async-start | bytes 32768 | tf_op jit(solution)/shard_map/all_to_all | solution.py:107
  113.1 6.7 %collective-permute-start.18 = (f32[256]{0:T(256)S(1)}, f32[256]{0:T(256)S(1)}, u32[]{:S(2)}, u32[]{:S(2)}) collective-permute-start(f32[256]{0:T(256)S(1)} %dynamic-slice_subtract_fusion.2), channel_id=1, source_target_pairs={{0,1},{1,0},{2,3},{3,2},{4,5},{5,4},{6,7},{7,6},{8,9},{9,8},{10,11... | collective-permute-start | bytes 3080 | tf_op jit(solution)/shard_map/ppermute | solution.py:119
  113.8 23.6 %collective-permute-start.24 = (f32[8,1,512]{2,1,0:T(1,128)}, f32[8,1,512]{2,1,0:T(1,128)S(1)}, u32[]{:S(2)}, u32[]{:S(2)}) collective-permute-start(f32[8,1,512]{2,1,0:T(1,128)} %get-tuple-element.28), channel_id=1, source_target_pairs={{8,0},{16,8},{24,16},{2,24},{10,2},{18,10},{26,18},{4,26},{12,4},{... | collective-permute-start | bytes 49160 | tf_op jit(solution)/shard_map/ppermute | solution.py:50
  115.1 22.3 %collective-permute-start.25 = (f32[8,1,512]{2,1,0:T(1,128)}, f32[8,1,512]{2,1,0:T(1,128)S(1)}, u32[]{:S(2)}, u32[]{:S(2)}) collective-permute-start(f32[8,1,512]{2,1,0:T(1,128)} %get-tuple-element.29), channel_id=1, source_target_pairs={{0,8},{8,16},{16,24},{24,2},{2,10},{10,18},{18,26},{26,4},{4,12},{... | collective-permute-start | bytes 49160 | tf_op jit(solution)/shard_map/ppermute | solution.py:49
  118.3 4.9 %collective-permute-start.26 = (f32[8,16,1]{2,1,0:T(8,128)S(1)}, f32[8,16,1]{2,1,0:T(8,128)S(1)}, u32[]{:S(2)}, u32[]{:S(2)}) collective-permute-start(f32[8,16,1]{2,1,0:T(8,128)S(1)} %slice_select_fusion.1), channel_id=1, source_target_pairs={{0,1},{1,0},{2,3},{3,2},{4,5},{5,4},{6,7},{7,6},{8,9},{9,8},{10,11... | collective-permute-start | bytes 1544 | tf_op jit(solution)/shard_map/ppermute | solution.py:46
  128.5 3.6 %collective-permute-start.21 = (f32[512]{0:T(512)S(1)}, f32[512]{0:T(512)S(1)}, u32[]{:S(2)}, u32[]{:S(2)}) collective-permute-start(f32[512]{0:T(512)S(1)} %pad_maximum_fusion.6), channel_id=1, source_target_pairs={{0,1},{1,0},{2,3},{3,2},{4,5},{5,4},{6,7},{7,6},{8,9},{9,8},{10,11... | collective-permute-start | bytes 6152 | tf_op jit(solution)/shard_map/ppermute | solution.py:119
  132.5 3.6 %collective-permute-start.22 = (f32[512]{0:T(512)S(1)}, f32[512]{0:T(512)S(1)}, u32[]{:S(2)}, u32[]{:S(2)}) collective-permute-start(f32[512]{0:T(512)S(1)} %pad_maximum_fusion.7), channel_id=1, source_target_pairs={{0,1},{1,0},{2,3},{3,2},{4,5},{5,4},{6,7},{7,6},{8,9},{9,8},{10,11... | collective-permute-start | bytes 6152 | tf_op jit(solution)/shard_map/ppermute | solution.py:119
  136.4 10.1 %collective-permute-start.23 = (f32[1024]{0:T(1024)S(1)}, f32[1024]{0:T(1024)S(1)}, u32[]{:S(2)}, u32[]{:S(2)}) collective-permute-start(f32[1024]{0:T(1024)S(1)} %pad_maximum_fusion.3), channel_id=1, source_target_pairs={{0,1},{1,0},{2,3},{3,2},{4,5},{5,4},{6,7},{7,6},{8,9},{9,8},{10,11... | collective-permute-start | bytes 12296 | tf_op jit(solution)/shard_map/ppermute | solution.py:119
  140.7 5.1 %collective-permute-start.29 = (f32[8,16,1]{2,1,0:T(8,128)S(1)}, f32[8,16,1]{2,1,0:T(8,128)S(1)}, u32[]{:S(2)}, u32[]{:S(2)}) collective-permute-start(f32[8,16,1]{2,1,0:T(8,128)S(1)} %slice_select_fusion), channel_id=1, source_target_pairs={{0,1},{1,0},{2,3},{3,2},{4,5},{5,4},{6,7},{7,6},{8,9},{9,8},{10,11... | collective-permute-start | bytes 1544 | tf_op jit(solution)/shard_map/ppermute | solution.py:46
  142.5 9.1 %collective-permute-start.28 = (f32[8,1,512]{2,1,0:T(1,128)}, f32[8,1,512]{2,1,0:T(1,128)}, u32[]{:S(2)}, u32[]{:S(2)}) collective-permute-start(f32[8,1,512]{2,1,0:T(1,128)} %get-tuple-element.20), channel_id=1, source_target_pairs={{0,8},{8,16},{16,24},{24,2},{2,10},{10,18},{18,26},{26,4},{4,12},{... | collective-permute-start | bytes 49160 | tf_op jit(solution)/shard_map/ppermute | solution.py:49
  144.5 7.1 %collective-permute-start.27 = (f32[8,1,512]{2,1,0:T(1,128)}, f32[8,1,512]{2,1,0:T(1,128)}, u32[]{:S(2)}, u32[]{:S(2)}) collective-permute-start(f32[8,1,512]{2,1,0:T(1,128)} %get-tuple-element.21), channel_id=1, source_target_pairs={{8,0},{16,8},{24,16},{2,24},{10,2},{18,10},{26,18},{4,26},{12,4},{... | collective-permute-start | bytes 49160 | tf_op jit(solution)/shard_map/ppermute | solution.py:50
  154.9 10.4 %all-to-all-start.4 = ((f32[8,16,512]{2,1,0:T(8,128)}), f32[8,16,512]{2,1,0:T(8,128)S(1)}, u32[]{:S(2)}, u32[]{:S(2)}) async-start(f32[8,16,512]{2,1,0:T(8,128)} %fusion.121), calls=%async_computation.4 | async-start | bytes 524288 | tf_op jit(solution)/shard_map/all_to_all | solution.py:260
  (42 other events, 476.9 us)

commit v12 on v11

--- a/solution.py
+++ b/solution.py
@@ -123,7 +123,7 @@
     return jnp.where(low, jnp.concatenate([mine, other]), jnp.concatenate([other, mine]))
 
 
-def coarse_pair(rhs, pivots, coupling):
+def coarse_pair(rhs, pivots, coupling, tie=None):
     share = pivots.shape[1]
     low = lax.axis_index("col") == 0
     start = lax.axis_index("col") * share
@@ -138,6 +138,8 @@
     scaled = [jnp.dot(pivots[section], forward[section], precision=solve_precision) for section in range(NPANEL)]
     mine = scaled[NPANEL - 1]
     results = [None] * NPANEL
+    if tie is not None:
+        mine, _ = lax.optimization_barrier((mine, tie))
     for section in range(NPANEL - 2, 0, -1):
         partial = jnp.dot(mine, coupling[section], precision=solve_precision)
         got = swap_col(jnp.concatenate([other_half(partial), mine]))
@@ -186,6 +188,14 @@
 def shards(sources, conduct, via_cond, via_map, pad_map, port_tile, pivots, coupling):
     layer_count = lax.axis_size("layer")
     vertical = via_cond * via_map.astype(jnp.float32)
+    given_rows = sources.shape[1] // TILE
+    given_cols = sources.shape[2] // TILE
+    given_tile_cols = given_cols * lax.axis_size("col")
+    given_ids = (
+        (lax.axis_index("row") * given_rows + jnp.arange(given_rows, dtype=jnp.int32))[:, None] * given_tile_cols
+        + (lax.axis_index("col") * given_cols + jnp.arange(given_cols, dtype=jnp.int32))[None, :]
+    ).reshape(-1)
+    given_pick = (given_ids[:, None] == port_tile.reshape(-1)[None, :]).astype(jnp.float32)
     packed = lax.all_to_all(jnp.stack((conduct, vertical)), "layer", 2, 1, tiled=True)
     conduct, vertical = packed[0], packed[1]
     sources = lax.all_to_all(sources, "layer", 1, 0, tiled=True)
@@ -238,12 +248,21 @@
         plane = jnp.sum(resid, axis=0)
         tiles = plane.reshape(own_rows, TILE, own_cols, TILE).sum(axis=(1, 3)).reshape(-1)
         rhs = share_tiles(tiles, own_rows, own_cols, flat_tiles).reshape(NPANEL, PANEL) * (restrict_scale / TILE)
-        ports = coarse(rhs, pivots, coupling)
+        total = smooth(resid, weights, pad_term, inverse)
+        if col_count == 2 and outer == ITERS - 1 and drop is not None:
+            ports = coarse_pair(rhs, pivots, coupling, total)
+        else:
+            ports = coarse(rhs, pivots, coupling)
         tile_values = jnp.dot(scatter_ring, ports.reshape(-1), precision=highest).reshape(own_rows + 2, own_cols + 2)
         ring = expand(expand(tile_values, True).T, True).T * prolong_scale
         centre = ring[1:-1, 1:-1]
         lifted = jnp.broadcast_to(centre[None], (local_layers, grid_rows, grid_cols))
-        total = smooth(resid, weights, pad_term, inverse)
+        if outer == ITERS - 1 and drop is not None:
+            both = lax.all_to_all(jnp.stack((drop, total)), "layer", 1, 2, tiled=True)
+            given_values = jnp.dot(given_pick, ports.reshape(-1), precision=highest).reshape(given_rows, given_cols)
+            given_field = jnp.repeat(jnp.repeat(given_values, TILE, axis=0), TILE, axis=1) * prolong_scale
+            given_lifted = jnp.broadcast_to(given_field[None], both.shape[1:])
+            return ((both[0] + given_lifted) + both[1], ports)
         if outer == ITERS - 1:
             drop = (lifted if drop is None else drop + lifted) + total
             break

time: 167 us -> 157 us (0.940)
  local copies, waits for them, and re-layouts: 19.6 us -> 11.9 us
  waiting for transfers between devices: 54.4 us -> 48.6 us
  starting transfers between devices: 67.9 us -> 70.5 us
  matrix products: 9.51 us -> 12.1 us
    all_to_all x2, waiting for transfers between devices: 12.3 us -> 6.2 us  [share_tiles(): got = lax.all_to_all(payload, ('layer', 'row', 'col'), 0, 0, tiled=True)]
    ppermute x12, waiting for transfers between devices: 22 us -> 26.1 us  [swap_col(): return lax.ppermute(value, 'col', [(0, 1), (1, 0)])]
    add x1 -> x3, other arithmetic: 3.26 us -> 0.82 us  [the longest x1 0.75 us: shards(): return (both[0] + given_lifted + both[1], ports)]
    ppermute x6, waiting for transfers between devices: 3.83 us -> 1.64 us  [rims(): lax.ppermute(head, axis, [(place[i + 1], place[i]) for i in range(count -...]
    another operation x0 -> x2, other arithmetic: none -> 2.06 us  [shards(): both = lax.all_to_all(jnp.stack((drop, total)), 'layer', 1, 2, tiled=True)]
    ppermute x6, starting transfers between devices: 19.2 us -> 21 us  [rims(): lax.ppermute(tail, axis, [(place[i], place[i + 1]) for i in range(count -...]
    reshape x4 -> x2, local copies, waits for them, and re-layouts: 1.91 us -> 0.17 us  [expand(): body = jnp.repeat(inner, TILE, axis=0)]
    slice x6 -> x5, local copies, waits for them, and re-layouts: 2.08 us -> 0.4 us  [neighbours(): lax.slice_in_dim(field, 0, size - 1, axis=dim)]
  transfers between devices with their start and end apart: 35 -> 35, of which waited for: 19 -> 21; matrix products, arithmetic and copies ran while one was open for 16% -> 13% of each run, Pallas kernels for 0% -> 0%
where the time goes in v12:
time: 157 us; the launch traced here: 156 us
  starting transfers between devices  70.5 us (45%)
  waiting for transfers between devices  48.6 us (31%)
  matrix products  12.1 us (8%)
  local copies, waits for them, and re-layouts  11.9 us (8%)
  other arithmetic  11.4 us (7%)
    ppermute x12, waiting for transfers between devices, swap_col(): return lax.ppermute(value, 'col', [(0, 1), (1, 0)])  26.1 us
    ppermute x6, starting transfers between devices, rims(): lax.ppermute(tail, axis, [(place[i], place[i + 1]) for i in range(count -...  21 us
    all_to_all x2, starting transfers between devices, share_tiles(): got = lax.all_to_all(payload, ('layer', 'row', 'col'), 0, 0, tiled=True)  13.9 us
    ppermute x12, starting transfers between devices, swap_col(): return lax.ppermute(value, 'col', [(0, 1), (1, 0)])  9.25 us
    ppermute x6, starting transfers between devices, rims(): lax.ppermute(head, axis, [(place[i + 1], place[i]) for i in range(count -...  7.75 us
    all_to_all x2, waiting for transfers between devices, share_tiles(): got = lax.all_to_all(payload, ('layer', 'row', 'col'), 0, 0, tiled=True)  6.2 us
    ppermute x6, starting transfers between devices, rims(): got = lax.ppermute(jnp.where(low, tail, head), axis, [(0, 1), (1, 0)])  5.9 us
    all_to_all x1, starting transfers between devices, shards(): both = lax.all_to_all(jnp.stack((drop, total)), 'layer', 1, 2, tiled=True)  4.97 us
  transfers between devices with their start and end apart: 35, of which 21 were waited for; matrix products, arithmetic and copies ran while one was open for 13% of the time, Pallas kernels for 0%

profile of v12, /device:TPU:0, one launch (start us, length us, event | category | flops | bytes accessed | tf_op | source)
XLA Modules:
  0.0 156.0 jit_solution(14053399769616611960)
XLA Ops:
  0.6 1.9 %copy.34 = f32[2,64,512]{2,0,1:T(2,128)} copy(f32[2,64,512]{2,1,0:T(8,128)} %param.8) | data formatting | bytes 524288 | tf_op args[0]
  2.5 4.2 %all-to-all-start = ((f32[2,64,512]{2,0,1:T(2,128)}), f32[2,64,512]{2,0,1:T(2,128)S(1)}, u32[]{:S(2)}, u32[]{:S(2)}) async-start(f32[2,64,512]{2,0,1:T(2,128)} %copy.34), calls=%async_computation | async-start | bytes 524288 | tf_op jit(solution)/shard_map/all_to_all | solution.py:201
  8.8 4.0 %all-to-all-done = f32[2,64,512]{2,0,1:T(2,128)S(1)} async-done(((f32[2,64,512]{2,0,1:T(2,128)}), f32[2,64,512]{2,0,1:T(2,128)S(1)}, u32[]{:S(2)}, u32[]{:S(2)}) %all-to-all-start) | async-done | bytes 262176 | tf_op jit(solution)/shard_map/all_to_all | solution.py:201
  13.7 5.5 %all-to-all-start.1 = ((f32[32,1,32]{2,1,0:T(1,128)}), f32[32,1,32]{2,1,0:T(1,128)S(1)}, u32[]{:S(2)}, u32[]{:S(2)}) async-start(f32[32,1,32]{2,1,0:T(1,128)} %broadcast_in_dim.29), calls=%async_computation.1 | async-start | bytes 32768 | tf_op jit(solution)/shard_map/all_to_all | solution.py:107
  20.5 5.8 %all-to-all-done.1 = f32[32,1,32]{2,1,0:T(1,128)S(1)} async-done(((f32[32,1,32]{2,1,0:T(1,128)}), f32[32,1,32]{2,1,0:T(1,128)S(1)}, u32[]{:S(2)}, u32[]{:S(2)}) %all-to-all-start.1) | async-done | bytes 4128 | tf_op jit(solution)/shard_map/all_to_all | solution.py:107
  26.3 3.5 %all-to-all-start.2 = ((f32[2,2,64,512]{3,1,0,2:T(2,128)}), f32[2,2,64,512]{3,1,0,2:T(2,128)S(1)}, u32[]{:S(2)}, u32[]{:S(2)}) async-start(f32[2,2,64,512]{3,1,0,2:T(2,128)} %copy.35), calls=%async_computation.2 | async-start | bytes 1048576 | tf_op jit(solution)/shard_map/all_to_all | solution.py:199
  32.7 2.1 %collective-permute-done = f32[256]{0:T(256)S(1)} collective-permute-done((f32[256]{0:T(256)S(1)}, f32[256]{0:T(256)S(1)}, u32[]{:S(2)}, u32[]{:S(2)}) %collective-permute-start) | collective-permute-done | bytes 1056 | tf_op jit(solution)/shard_map/ppermute | solution.py:119
  37.1 1.6 %collective-permute-done.1 = f32[256]{0:T(256)S(1)} collective-permute-done((f32[256]{0:T(256)S(1)}, f32[256]{0:T(256)S(1)}, u32[]{:S(2)}, u32[]{:S(2)}) %collective-permute-start.1) | collective-permute-done | bytes 1056 | tf_op jit(solution)/shard_map/ppermute | solution.py:119
  40.0 2.6 %collective-permute-done.2 = f32[256]{0:T(256)S(1)} collective-permute-done((f32[256]{0:T(256)S(1)}, f32[256]{0:T(256)S(1)}, u32[]{:S(2)}, u32[]{:S(2)}) %collective-permute-start.2) | collective-permute-done | bytes 1056 | tf_op jit(solution)/shard_map/ppermute | solution.py:119
  44.3 2.7 %collective-permute-done.3 = f32[512]{0:T(512)S(1)} collective-permute-done((f32[512]{0:T(512)S(1)}, f32[512]{0:T(512)S(1)}, u32[]{:S(2)}, u32[]{:S(2)}) %collective-permute-start.3) | collective-permute-done | bytes 2080 | tf_op jit(solution)/shard_map/ppermute | solution.py:119
  48.0 3.0 %collective-permute-done.4 = f32[512]{0:T(512)S(1)} collective-permute-done((f32[512]{0:T(512)S(1)}, f32[512]{0:T(512)S(1)}, u32[]{:S(2)}, u32[]{:S(2)}) %collective-permute-start.4) | collective-permute-done | bytes 2080 | tf_op jit(solution)/shard_map/ppermute | solution.py:119
  51.9 3.0 %collective-permute-done.5 = f32[1024]{0:T(1024)S(1)} collective-permute-done((f32[1024]{0:T(1024)S(1)}, f32[1024]{0:T(1024)S(1)}, u32[]{:S(2)}, u32[]{:S(2)}) %collective-permute-start.5) | collective-permute-done | bytes 4128 | tf_op jit(solution)/shard_map/ppermute | solution.py:119
  60.7 3.5 %collective-permute-done.8 = f32[8,16,1]{2,1,0:T(8,128)S(1)} collective-permute-done((f32[8,16,1]{2,1,0:T(8,128)S(1)}, f32[8,16,1]{2,1,0:T(8,128)S(1)}, u32[]{:S(2)}, u32[]{:S(2)}) %collective-permute-start.8) | collective-permute-done | bytes 544 | tf_op jit(solution)/shard_map/ppermute | solution.py:46
  67.2 4.4 %collective-permute-start.10 = (f32[8,1,512]{2,1,0:T(1,128)S(1)}, f32[8,1,512]{2,1,0:T(1,128)S(1)}, u32[]{:S(2)}, u32[]{:S(2)}) collective-permute-start(f32[8,1,512]{2,1,0:T(1,128)S(1)} %get-tuple-element.61), channel_id=1, source_target_pairs={{0,8},{8,16},{16,24},{24,2},{2,10},{10,18},{18,26},{26,4},{4,12},{... | collective-permute-start | bytes 49160 | tf_op jit(solution)/shard_map/ppermute | solution.py:49
  73.3 1.5 collective-permute-start.14
  76.1 5.4 %collective-permute-start.13 = (f32[8,1,512]{2,1,0:T(1,128)S(1)}, f32[8,1,512]{2,1,0:T(1,128)S(1)}, u32[]{:S(2)}, u32[]{:S(2)}) collective-permute-start(f32[8,1,512]{2,1,0:T(1,128)S(1)} %get-tuple-element.53), channel_id=1, source_target_pairs={{0,8},{8,16},{16,24},{24,2},{2,10},{10,18},{18,26},{26,4},{4,12},{... | collective-permute-start | bytes 49160 | tf_op jit(solution)/shard_map/ppermute | solution.py:49
  86.0 4.9 %collective-permute-start.16 = (f32[8,1,512]{2,1,0:T(1,128)S(1)}, f32[8,1,512]{2,1,0:T(1,128)S(1)}, u32[]{:S(2)}, u32[]{:S(2)}) collective-permute-start(f32[8,1,512]{2,1,0:T(1,128)S(1)} %get-tuple-element.45), channel_id=1, source_target_pairs={{0,8},{8,16},{16,24},{24,2},{2,10},{10,18},{18,26},{26,4},{4,12},{... | collective-permute-start | bytes 49160 | tf_op jit(solution)/shard_map/ppermute | solution.py:49
  96.2 8.4 %all-to-all-start.4 = ((f32[32,1,32]{2,1,0:T(1,128)}), f32[32,1,32]{2,1,0:T(1,128)}, u32[]{:S(2)}, u32[]{:S(2)}) async-start(f32[32,1,32]{2,1,0:T(1,128)} %broadcast_in_dim.37), calls=%async_computation.4 | async-start | bytes 32768 | tf_op jit(solution)/shard_map/all_to_all | solution.py:107
  106.0 3.6 %collective-permute-start.19 = (f32[8,1,512]{2,1,0:T(1,128)}, f32[8,1,512]{2,1,0:T(1,128)}, u32[]{:S(2)}, u32[]{:S(2)}) collective-permute-start(f32[8,1,512]{2,1,0:T(1,128)} %get-tuple-element.37), channel_id=1, source_target_pairs={{0,8},{8,16},{16,24},{24,2},{2,10},{10,18},{18,26},{26,4},{4,12},{... | collective-permute-start | bytes 49160 | tf_op jit(solution)/shard_map/ppermute | solution.py:49
  109.6 1.7 %collective-permute-start.20 = (f32[8,16,1]{2,1,0:T(8,128)S(1)}, f32[8,16,1]{2,1,0:T(8,128)}, u32[]{:S(2)}, u32[]{:S(2)}) collective-permute-start(f32[8,16,1]{2,1,0:T(8,128)S(1)} %slice_select_fusion.1), channel_id=1, source_target_pairs={{0,1},{1,0},{2,3},{3,2},{4,5},{5,4},{6,7},{7,6},{8,9},{9,8},{10,11... | collective-permute-start | bytes 1544 | tf_op jit(solution)/shard_map/ppermute | solution.py:46
  111.7 1.7 %fusion.1 = f32[2048]{0:T(1024)S(1)} fusion(f32[32,32]{1,0:T(8,128)} %bitcast.56, s32[2048]{0:T(1024)} %copy-done.19, s32[2048]{0:T(1024)S(1)} %copy-done.18), kind=kOutput, calls=%fused_computation.3 | convolution fusion | flops 25425920 | bytes 28672 | tf_op jit(solution)/shard_map/dot_general | solution.py:115
  115.5 2.1 %collective-permute-done.24 = f32[256]{0:T(256)S(1)} collective-permute-done((f32[256]{0:T(256)S(1)}, f32[256]{0:T(256)S(1)}, u32[]{:S(2)}, u32[]{:S(2)}) %collective-permute-start.24) | collective-permute-done | bytes 1056 | tf_op jit(solution)/shard_map/ppermute | solution.py:119
  119.9 1.6 %collective-permute-done.25 = f32[256]{0:T(256)S(1)} collective-permute-done((f32[256]{0:T(256)S(1)}, f32[256]{0:T(256)S(1)}, u32[]{:S(2)}, u32[]{:S(2)}) %collective-permute-start.25) | collective-permute-done | bytes 1056 | tf_op jit(solution)/shard_map/ppermute | solution.py:119
  122.9 2.6 %collective-permute-done.26 = f32[256]{0:T(256)S(1)} collective-permute-done((f32[256]{0:T(256)S(1)}, f32[256]{0:T(256)S(1)}, u32[]{:S(2)}, u32[]{:S(2)}) %collective-permute-start.26) | collective-permute-done | bytes 1056 | tf_op jit(solution)/shard_map/ppermute | solution.py:119
  125.9 1.5 fusion.170
  132.1 1.6 %collective-permute-done.21 = f32[8,1,512]{2,1,0:T(1,128)S(1)} collective-permute-done((f32[8,1,512]{2,1,0:T(1,128)S(1)}, f32[8,1,512]{2,1,0:T(1,128)S(1)}, u32[]{:S(2)}, u32[]{:S(2)}) %collective-permute-start.21) | collective-permute-done | bytes 16416 | tf_op jit(solution)/shard_map/ppermute | solution.py:50
  134.6 1.5 collective-permute-start.27
  136.4 1.8 %collective-permute-done.27 = f32[512]{0:T(512)S(1)} collective-permute-done((f32[512]{0:T(512)S(1)}, f32[512]{0:T(512)S(1)}, u32[]{:S(2)}, u32[]{:S(2)}) %collective-permute-start.27) | collective-permute-done | bytes 2080 | tf_op jit(solution)/shard_map/ppermute | solution.py:119
  138.6 1.5 collective-permute-start.28
  140.9 5.0 %all-to-all-start.3 = ((f32[2,8,16,512]{3,2,0,1:T(8,128)}), f32[2,8,16,512]{3,2,0,1:T(8,128)S(1)}, u32[]{:S(2)}, u32[]{:S(2)}) async-start(f32[2,8,16,512]{3,2,0,1:T(8,128)} %pad_maximum_fusion.1), calls=%async_computation.3 | async-start | bytes 1048576 | tf_op jit(solution)/shard_map/all_to_all | solution.py:261
  146.8 3.0 %collective-permute-done.29 = f32[1024]{0:T(1024)S(1)} collective-permute-done((f32[1024]{0:T(1024)S(1)}, f32[1024]{0:T(1024)S(1)}, u32[]{:S(2)}, u32[]{:S(2)}) %collective-permute-start.29) | collective-permute-done | bytes 4128 | tf_op jit(solution)/shard_map/ppermute | solution.py:119
  151.4 3.7 %all-to-all-done.3 = f32[2,8,16,512]{3,2,0,1:T(8,128)S(1)} async-done(((f32[2,8,16,512]{3,2,0,1:T(8,128)}), f32[2,8,16,512]{3,2,0,1:T(8,128)S(1)}, u32[]{:S(2)}, u32[]{:S(2)}) %all-to-all-start.3) | async-done | bytes 524320 | tf_op jit(solution)/shard_map/all_to_all | solution.py:261
  (234 shorter events, 53.5 us)
Async XLA Ops:
  2.5 10.2 %all-to-all-start = ((f32[2,64,512]{2,0,1:T(2,128)}), f32[2,64,512]{2,0,1:T(2,128)S(1)}, u32[]{:S(2)}, u32[]{:S(2)}) async-start(f32[2,64,512]{2,0,1:T(2,128)} %copy.34), calls=%async_computation | async-start | bytes 524288 | tf_op jit(solution)/shard_map/all_to_all | solution.py:201
  13.7 12.6 %all-to-all-start.1 = ((f32[32,1,32]{2,1,0:T(1,128)}), f32[32,1,32]{2,1,0:T(1,128)S(1)}, u32[]{:S(2)}, u32[]{:S(2)}) async-start(f32[32,1,32]{2,1,0:T(1,128)} %broadcast_in_dim.29), calls=%async_computation.1 | async-start | bytes 32768 | tf_op jit(solution)/shard_map/all_to_all | solution.py:107
  26.3 30.6 %all-to-all-start.2 = ((f32[2,2,64,512]{3,1,0,2:T(2,128)}), f32[2,2,64,512]{3,1,0,2:T(2,128)S(1)}, u32[]{:S(2)}, u32[]{:S(2)}) async-start(f32[2,2,64,512]{3,1,0,2:T(2,128)} %copy.35), calls=%async_computation.2 | async-start | bytes 1048576 | tf_op jit(solution)/shard_map/all_to_all | solution.py:199
  31.1 3.6 %collective-permute-start = (f32[256]{0:T(256)S(1)}, f32[256]{0:T(256)S(1)}, u32[]{:S(2)}, u32[]{:S(2)}) collective-permute-start(f32[256]{0:T(256)S(1)} %dynamic-slice_subtract_fusion.5), channel_id=1, source_target_pairs={{0,1},{1,0},{2,3},{3,2},{4,5},{5,4},{6,7},{7,6},{8,9},{9,8},{10,11... | collective-permute-start | bytes 3080 | tf_op jit(solution)/shard_map/ppermute | solution.py:119
  35.1 3.6 %collective-permute-start.1 = (f32[256]{0:T(256)S(1)}, f32[256]{0:T(256)S(1)}, u32[]{:S(2)}, u32[]{:S(2)}) collective-permute-start(f32[256]{0:T(256)S(1)} %dynamic-slice_subtract_fusion.4), channel_id=1, source_target_pairs={{0,1},{1,0},{2,3},{3,2},{4,5},{5,4},{6,7},{7,6},{8,9},{9,8},{10,11... | collective-permute-start | bytes 3080 | tf_op jit(solution)/shard_map/ppermute | solution.py:119
  39.1 3.6 %collective-permute-start.2 = (f32[256]{0:T(256)S(1)}, f32[256]{0:T(256)S(1)}, u32[]{:S(2)}, u32[]{:S(2)}) collective-permute-start(f32[256]{0:T(256)S(1)} %dynamic-slice_subtract_fusion.3), channel_id=1, source_target_pairs={{0,1},{1,0},{2,3},{3,2},{4,5},{5,4},{6,7},{7,6},{8,9},{9,8},{10,11... | collective-permute-start | bytes 3080 | tf_op jit(solution)/shard_map/ppermute | solution.py:119
  43.3 3.6 %collective-permute-start.3 = (f32[512]{0:T(512)S(1)}, f32[512]{0:T(512)S(1)}, u32[]{:S(2)}, u32[]{:S(2)}) collective-permute-start(f32[512]{0:T(512)S(1)} %pad_maximum_fusion.5), channel_id=1, source_target_pairs={{0,1},{1,0},{2,3},{3,2},{4,5},{5,4},{6,7},{7,6},{8,9},{9,8},{10,11... | collective-permute-start | bytes 6152 | tf_op jit(solution)/shard_map/ppermute | solution.py:119
  47.3 3.6 %collective-permute-start.4 = (f32[512]{0:T(512)S(1)}, f32[512]{0:T(512)S(1)}, u32[]{:S(2)}, u32[]{:S(2)}) collective-permute-start(f32[512]{0:T(512)S(1)} %pad_maximum_fusion.6), channel_id=1, source_target_pairs={{0,1},{1,0},{2,3},{3,2},{4,5},{5,4},{6,7},{7,6},{8,9},{9,8},{10,11... | collective-permute-start | bytes 6152 | tf_op jit(solution)/shard_map/ppermute | solution.py:119
  51.2 3.7 %collective-permute-start.5 = (f32[1024]{0:T(1024)S(1)}, f32[1024]{0:T(1024)S(1)}, u32[]{:S(2)}, u32[]{:S(2)}) collective-permute-start(f32[1024]{0:T(1024)S(1)} %pad_maximum_fusion.3), channel_id=1, source_target_pairs={{0,1},{1,0},{2,3},{3,2},{4,5},{5,4},{6,7},{7,6},{8,9},{9,8},{10,11... | collective-permute-start | bytes 12296 | tf_op jit(solution)/shard_map/ppermute | solution.py:119
  57.3 6.9 %collective-permute-start.7 = (f32[8,1,512]{2,1,0:T(1,128)S(1)}, f32[8,1,512]{2,1,0:T(1,128)S(1)}, u32[]{:S(2)}, u32[]{:S(2)}) collective-permute-start(f32[8,1,512]{2,1,0:T(1,128)S(1)} %get-tuple-element.66), channel_id=1, source_target_pairs={{0,8},{8,16},{16,24},{24,2},{2,10},{10,18},{18,26},{26,4},{4,12},{... | collective-permute-start | bytes 49160 | tf_op jit(solution)/shard_map/ppermute | solution.py:49
  58.6 5.7 %collective-permute-start.6 = (f32[8,1,512]{2,1,0:T(1,128)S(1)}, f32[8,1,512]{2,1,0:T(1,128)S(1)}, u32[]{:S(2)}, u32[]{:S(2)}) collective-permute-start(f32[8,1,512]{2,1,0:T(1,128)S(1)} %get-tuple-element.67), channel_id=1, source_target_pairs={{8,0},{16,8},{24,16},{2,24},{10,2},{18,10},{26,18},{4,26},{12,4},{... | collective-permute-start | bytes 49160 | tf_op jit(solution)/shard_map/ppermute | solution.py:50
  59.9 4.3 %collective-permute-start.8 = (f32[8,16,1]{2,1,0:T(8,128)S(1)}, f32[8,16,1]{2,1,0:T(8,128)S(1)}, u32[]{:S(2)}, u32[]{:S(2)}) collective-permute-start(f32[8,16,1]{2,1,0:T(8,128)S(1)} %slice_select_fusion.5), channel_id=1, source_target_pairs={{0,1},{1,0},{2,3},{3,2},{4,5},{5,4},{6,7},{7,6},{8,9},{9,8},{10,11... | collective-permute-start | bytes 1544 | tf_op jit(solution)/shard_map/ppermute | solution.py:46
  65.2 6.5 %collective-permute-start.11 = (f32[8,16,1]{2,1,0:T(8,128)S(1)}, f32[8,16,1]{2,1,0:T(8,128)S(1)}, u32[]{:S(2)}, u32[]{:S(2)}) collective-permute-start(f32[8,16,1]{2,1,0:T(8,128)S(1)} %slice_select_fusion.4), channel_id=1, source_target_pairs={{0,1},{1,0},{2,3},{3,2},{4,5},{5,4},{6,7},{7,6},{8,9},{9,8},{10,11... | collective-permute-start | bytes 1544 | tf_op jit(solution)/shard_map/ppermute | solution.py:46
  65.9 5.8 %collective-permute-start.9 = (f32[8,1,512]{2,1,0:T(1,128)S(1)}, f32[8,1,512]{2,1,0:T(1,128)S(1)}, u32[]{:S(2)}, u32[]{:S(2)}) collective-permute-start(f32[8,1,512]{2,1,0:T(1,128)S(1)} %get-tuple-element.60), channel_id=1, source_target_pairs={{8,0},{16,8},{24,16},{2,24},{10,2},{18,10},{26,18},{4,26},{12,4},{... | collective-permute-start | bytes 49160 | tf_op jit(solution)/shard_map/ppermute | solution.py:50
  67.2 5.3 %collective-permute-start.10 = (f32[8,1,512]{2,1,0:T(1,128)S(1)}, f32[8,1,512]{2,1,0:T(1,128)S(1)}, u32[]{:S(2)}, u32[]{:S(2)}) collective-permute-start(f32[8,1,512]{2,1,0:T(1,128)S(1)} %get-tuple-element.61), channel_id=1, source_target_pairs={{0,8},{8,16},{16,24},{24,2},{2,10},{10,18},{18,26},{26,4},{4,12},{... | collective-permute-start | bytes 49160 | tf_op jit(solution)/shard_map/ppermute | solution.py:49
  73.3 8.3 %collective-permute-start.14 = (f32[8,16,1]{2,1,0:T(8,128)S(1)}, f32[8,16,1]{2,1,0:T(8,128)S(1)}, u32[]{:S(2)}, u32[]{:S(2)}) collective-permute-start(f32[8,16,1]{2,1,0:T(8,128)S(1)} %slice_select_fusion.3), channel_id=1, source_target_pairs={{0,1},{1,0},{2,3},{3,2},{4,5},{5,4},{6,7},{7,6},{8,9},{9,8},{10,11... | collective-permute-start | bytes 1544 | tf_op jit(solution)/shard_map/ppermute | solution.py:46
  74.8 6.8 %collective-permute-start.12 = (f32[8,1,512]{2,1,0:T(1,128)S(1)}, f32[8,1,512]{2,1,0:T(1,128)S(1)}, u32[]{:S(2)}, u32[]{:S(2)}) collective-permute-start(f32[8,1,512]{2,1,0:T(1,128)S(1)} %get-tuple-element.52), channel_id=1, source_target_pairs={{8,0},{16,8},{24,16},{2,24},{10,2},{18,10},{26,18},{4,26},{12,4},{... | collective-permute-start | bytes 49160 | tf_op jit(solution)/shard_map/ppermute | solution.py:50
  76.1 6.3 %collective-permute-start.13 = (f32[8,1,512]{2,1,0:T(1,128)S(1)}, f32[8,1,512]{2,1,0:T(1,128)S(1)}, u32[]{:S(2)}, u32[]{:S(2)}) collective-permute-start(f32[8,1,512]{2,1,0:T(1,128)S(1)} %get-tuple-element.53), channel_id=1, source_target_pairs={{0,8},{8,16},{16,24},{24,2},{2,10},{10,18},{18,26},{26,4},{4,12},{... | collective-permute-start | bytes 49160 | tf_op jit(solution)/shard_map/ppermute | solution.py:49
  84.0 6.9 %collective-permute-start.17 = (f32[8,16,1]{2,1,0:T(8,128)S(1)}, f32[8,16,1]{2,1,0:T(8,128)S(1)}, u32[]{:S(2)}, u32[]{:S(2)}) collective-permute-start(f32[8,16,1]{2,1,0:T(8,128)S(1)} %slice_select_fusion.2), channel_id=1, source_target_pairs={{0,1},{1,0},{2,3},{3,2},{4,5},{5,4},{6,7},{7,6},{8,9},{9,8},{10,11... | collective-permute-start | bytes 1544 | tf_op jit(solution)/shard_map/ppermute | solution.py:46
  84.7 6.2 %collective-permute-start.15 = (f32[8,1,512]{2,1,0:T(1,128)S(1)}, f32[8,1,512]{2,1,0:T(1,128)S(1)}, u32[]{:S(2)}, u32[]{:S(2)}) collective-permute-start(f32[8,1,512]{2,1,0:T(1,128)S(1)} %get-tuple-element.44), channel_id=1, source_target_pairs={{8,0},{16,8},{24,16},{2,24},{10,2},{18,10},{26,18},{4,26},{12,4},{... | collective-permute-start | bytes 49160 | tf_op jit(solution)/shard_map/ppermute | solution.py:50
  86.0 5.7 %collective-permute-start.16 = (f32[8,1,512]{2,1,0:T(1,128)S(1)}, f32[8,1,512]{2,1,0:T(1,128)S(1)}, u32[]{:S(2)}, u32[]{:S(2)}) collective-permute-start(f32[8,1,512]{2,1,0:T(1,128)S(1)} %get-tuple-element.45), channel_id=1, source_target_pairs={{0,8},{8,16},{16,24},{24,2},{2,10},{10,18},{18,26},{26,4},{4,12},{... | collective-permute-start | bytes 49160 | tf_op jit(solution)/shard_map/ppermute | solution.py:49
  96.2 15.5 %all-to-all-start.4 = ((f32[32,1,32]{2,1,0:T(1,128)}), f32[32,1,32]{2,1,0:T(1,128)}, u32[]{:S(2)}, u32[]{:S(2)}) async-start(f32[32,1,32]{2,1,0:T(1,128)} %broadcast_in_dim.37), calls=%async_computation.4 | async-start | bytes 32768 | tf_op jit(solution)/shard_map/all_to_all | solution.py:107
  104.7 21.1 %collective-permute-start.18 = (f32[8,1,512]{2,1,0:T(1,128)}, f32[8,1,512]{2,1,0:T(1,128)S(1)}, u32[]{:S(2)}, u32[]{:S(2)}) collective-permute-start(f32[8,1,512]{2,1,0:T(1,128)} %get-tuple-element.36), channel_id=1, source_target_pairs={{8,0},{16,8},{24,16},{2,24},{10,2},{18,10},{26,18},{4,26},{12,4},{... | collective-permute-start | bytes 49160 | tf_op jit(solution)/shard_map/ppermute | solution.py:50
  106.0 19.9 %collective-permute-start.19 = (f32[8,1,512]{2,1,0:T(1,128)}, f32[8,1,512]{2,1,0:T(1,128)}, u32[]{:S(2)}, u32[]{:S(2)}) collective-permute-start(f32[8,1,512]{2,1,0:T(1,128)} %get-tuple-element.37), channel_id=1, source_target_pairs={{0,8},{8,16},{16,24},{24,2},{2,10},{10,18},{18,26},{26,4},{4,12},{... | collective-permute-start | bytes 49160 | tf_op jit(solution)/shard_map/ppermute | solution.py:49
  109.6 5.0 %collective-permute-start.20 = (f32[8,16,1]{2,1,0:T(8,128)S(1)}, f32[8,16,1]{2,1,0:T(8,128)}, u32[]{:S(2)}, u32[]{:S(2)}) collective-permute-start(f32[8,16,1]{2,1,0:T(8,128)S(1)} %slice_select_fusion.1), channel_id=1, source_target_pairs={{0,1},{1,0},{2,3},{3,2},{4,5},{5,4},{6,7},{7,6},{8,9},{9,8},{10,11... | collective-permute-start | bytes 1544 | tf_op jit(solution)/shard_map/ppermute | solution.py:46
  127.8 4.3 %collective-permute-start.23 = (f32[8,16,1]{2,1,0:T(8,128)S(1)}, f32[8,16,1]{2,1,0:T(8,128)S(1)}, u32[]{:S(2)}, u32[]{:S(2)}) collective-permute-start(f32[8,16,1]{2,1,0:T(8,128)S(1)} %slice_select_fusion), channel_id=1, source_target_pairs={{0,1},{1,0},{2,3},{3,2},{4,5},{5,4},{6,7},{7,6},{8,9},{9,8},{10,11... | collective-permute-start | bytes 1544 | tf_op jit(solution)/shard_map/ppermute | solution.py:46
  128.5 3.6 %collective-permute-start.22 = (f32[8,1,512]{2,1,0:T(1,128)S(1)}, f32[8,1,512]{2,1,0:T(1,128)S(1)}, u32[]{:S(2)}, u32[]{:S(2)}) collective-permute-start(f32[8,1,512]{2,1,0:T(1,128)S(1)} %get-tuple-element.28), channel_id=1, source_target_pairs={{0,8},{8,16},{16,24},{24,2},{2,10},{10,18},{18,26},{26,4},{4,12},{... | collective-permute-start | bytes 49160 | tf_op jit(solution)/shard_map/ppermute | solution.py:49
  129.8 4.0 %collective-permute-start.21 = (f32[8,1,512]{2,1,0:T(1,128)S(1)}, f32[8,1,512]{2,1,0:T(1,128)S(1)}, u32[]{:S(2)}, u32[]{:S(2)}) collective-permute-start(f32[8,1,512]{2,1,0:T(1,128)S(1)} %get-tuple-element.29), channel_id=1, source_target_pairs={{8,0},{16,8},{24,16},{2,24},{10,2},{18,10},{26,18},{4,26},{12,4},{... | collective-permute-start | bytes 49160 | tf_op jit(solution)/shard_map/ppermute | solution.py:50
  134.6 3.6 %collective-permute-start.27 = (f32[512]{0:T(512)S(1)}, f32[512]{0:T(512)S(1)}, u32[]{:S(2)}, u32[]{:S(2)}) collective-permute-start(f32[512]{0:T(512)S(1)} %pad_maximum_fusion.7), channel_id=1, source_target_pairs={{0,1},{1,0},{2,3},{3,2},{4,5},{5,4},{6,7},{7,6},{8,9},{9,8},{10,11... | collective-permute-start | bytes 6152 | tf_op jit(solution)/shard_map/ppermute | solution.py:119
  138.6 7.3 %collective-permute-start.28 = (f32[512]{0:T(512)S(1)}, f32[512]{0:T(512)S(1)}, u32[]{:S(2)}, u32[]{:S(2)}) collective-permute-start(f32[512]{0:T(512)S(1)} %pad_maximum_fusion.8), channel_id=1, source_target_pairs={{0,1},{1,0},{2,3},{3,2},{4,5},{5,4},{6,7},{7,6},{8,9},{9,8},{10,11... | collective-permute-start | bytes 6152 | tf_op jit(solution)/shard_map/ppermute | solution.py:119
  140.9 14.2 %all-to-all-start.3 = ((f32[2,8,16,512]{3,2,0,1:T(8,128)}), f32[2,8,16,512]{3,2,0,1:T(8,128)S(1)}, u32[]{:S(2)}, u32[]{:S(2)}) async-start(f32[2,8,16,512]{3,2,0,1:T(8,128)} %pad_maximum_fusion.1), calls=%async_computation.3 | async-start | bytes 1048576 | tf_op jit(solution)/shard_map/all_to_all | solution.py:261
  146.2 3.7 %collective-permute-start.29 = (f32[1024]{0:T(1024)S(1)}, f32[1024]{0:T(1024)S(1)}, u32[]{:S(2)}, u32[]{:S(2)}) collective-permute-start(f32[1024]{0:T(1024)S(1)} %pad_maximum_fusion.4), channel_id=1, source_target_pairs={{0,1},{1,0},{2,3},{3,2},{4,5},{5,4},{6,7},{7,6},{8,9},{9,8},{10,11... | collective-permute-start | bytes 12296 | tf_op jit(solution)/shard_map/ppermute | solution.py:119
  (23 other events, 263.7 us)

commit v13 on v12

--- a/solution.py
+++ b/solution.py
@@ -249,7 +249,7 @@
         tiles = plane.reshape(own_rows, TILE, own_cols, TILE).sum(axis=(1, 3)).reshape(-1)
         rhs = share_tiles(tiles, own_rows, own_cols, flat_tiles).reshape(NPANEL, PANEL) * (restrict_scale / TILE)
         total = smooth(resid, weights, pad_term, inverse)
-        if col_count == 2 and outer == ITERS - 1 and drop is not None:
+        if col_count == 2:
             ports = coarse_pair(rhs, pivots, coupling, total)
         else:
             ports = coarse(rhs, pivots, coupling)

time: 157 us -> 159 us (1.013)
  starting transfers between devices: 70.5 us -> 65.7 us
  local copies, waits for them, and re-layouts: 11.9 us -> 16.6 us
  other arithmetic: 11.4 us -> 14.8 us
    all_to_all x2, starting transfers between devices: 13.9 us -> 9.23 us  [share_tiles(): got = lax.all_to_all(payload, ('layer', 'row', 'col'), 0, 0, tiled=True)]
    ppermute x6, waiting for transfers between devices: 1.64 us -> 5.5 us  [rims(): lax.ppermute(head, axis, [(place[i + 1], place[i]) for i in range(count -...]
    slice x13 -> x11, local copies, waits for them, and re-layouts: 3.26 us -> 5.42 us  [neighbours(): lax.slice_in_dim(field, 1, size, axis=dim)]
    ppermute x12, waiting for transfers between devices: 26.1 us -> 24.1 us  [swap_col(): return lax.ppermute(value, 'col', [(0, 1), (1, 0)])]
  transfers between devices with their start and end apart: 35 -> 35, of which waited for: 21 -> 19; matrix products, arithmetic and copies ran while one was open for 13% -> 15% of each run, Pallas kernels for 0% -> 0%
where the time goes in v13:
time: 159 us; the launch traced here: 158 us
  starting transfers between devices  65.7 us (41%)
  waiting for transfers between devices  47.6 us (30%)
  local copies, waits for them, and re-layouts  16.6 us (10%)
  other arithmetic  14.8 us (9%)
  matrix products  12 us (8%)
    ppermute x12, waiting for transfers between devices, swap_col(): return lax.ppermute(value, 'col', [(0, 1), (1, 0)])  24.1 us
    ppermute x6, starting transfers between devices, rims(): lax.ppermute(tail, axis, [(place[i], place[i + 1]) for i in range(count -...  20.1 us
    ppermute x12, starting transfers between devices, swap_col(): return lax.ppermute(value, 'col', [(0, 1), (1, 0)])  10 us
    all_to_all x2, starting transfers between devices, share_tiles(): got = lax.all_to_all(payload, ('layer', 'row', 'col'), 0, 0, tiled=True)  9.23 us
    ppermute x6, starting transfers between devices, rims(): lax.ppermute(head, axis, [(place[i + 1], place[i]) for i in range(count -...  7.74 us
    ppermute x6, starting transfers between devices, rims(): got = lax.ppermute(jnp.where(low, tail, head), axis, [(0, 1), (1, 0)])  5.97 us
    all_to_all x2, waiting for transfers between devices, share_tiles(): got = lax.all_to_all(payload, ('layer', 'row', 'col'), 0, 0, tiled=True)  5.65 us
    ppermute x6, waiting for transfers between devices, rims(): lax.ppermute(head, axis, [(place[i + 1], place[i]) for i in range(count -...  5.5 us
  transfers between devices with their start and end apart: 35, of which 19 were waited for; matrix products, arithmetic and copies ran while one was open for 15% of the time, Pallas kernels for 0%

profile of v13, /device:TPU:0, one launch (start us, length us, event | category | flops | bytes accessed | tf_op | source)
XLA Modules:
  0.0 158.2 jit_solution(16884112685665853914)
XLA Ops:
  0.6 1.9 %copy.34 = f32[2,64,512]{2,0,1:T(2,128)} copy(f32[2,64,512]{2,1,0:T(8,128)} %param.8) | data formatting | bytes 524288 | tf_op args[0]
  2.5 4.2 %all-to-all-start = ((f32[2,64,512]{2,0,1:T(2,128)}), f32[2,64,512]{2,0,1:T(2,128)S(1)}, u32[]{:S(2)}, u32[]{:S(2)}) async-start(f32[2,64,512]{2,0,1:T(2,128)} %copy.34), calls=%async_computation | async-start | bytes 524288 | tf_op jit(solution)/shard_map/all_to_all | solution.py:201
  9.5 3.3 %all-to-all-done = f32[2,64,512]{2,0,1:T(2,128)S(1)} async-done(((f32[2,64,512]{2,0,1:T(2,128)}), f32[2,64,512]{2,0,1:T(2,128)S(1)}, u32[]{:S(2)}, u32[]{:S(2)}) %all-to-all-start) | async-done | bytes 262176 | tf_op jit(solution)/shard_map/all_to_all | solution.py:201
  13.7 5.5 %all-to-all-start.1 = ((f32[32,1,32]{2,1,0:T(1,128)}), f32[32,1,32]{2,1,0:T(1,128)S(1)}, u32[]{:S(2)}, u32[]{:S(2)}) async-start(f32[32,1,32]{2,1,0:T(1,128)} %broadcast_in_dim.29), calls=%async_computation.1 | async-start | bytes 32768 | tf_op jit(solution)/shard_map/all_to_all | solution.py:107
  21.4 4.9 %all-to-all-done.1 = f32[32,1,32]{2,1,0:T(1,128)S(1)} async-done(((f32[32,1,32]{2,1,0:T(1,128)}), f32[32,1,32]{2,1,0:T(1,128)S(1)}, u32[]{:S(2)}, u32[]{:S(2)}) %all-to-all-start.1) | async-done | bytes 4128 | tf_op jit(solution)/shard_map/all_to_all | solution.py:107
  26.3 3.5 %all-to-all-start.2 = ((f32[2,2,64,512]{3,1,0,2:T(2,128)}), f32[2,2,64,512]{3,1,0,2:T(2,128)S(1)}, u32[]{:S(2)}, u32[]{:S(2)}) async-start(f32[2,2,64,512]{3,1,0,2:T(2,128)} %copy.35), calls=%async_computation.2 | async-start | bytes 1048576 | tf_op jit(solution)/shard_map/all_to_all | solution.py:199
  33.1 1.6 %collective-permute-done = f32[256]{0:T(256)S(1)} collective-permute-done((f32[256]{0:T(256)S(1)}, f32[256]{0:T(256)S(1)}, u32[]{:S(2)}, u32[]{:S(2)}) %collective-permute-start) | collective-permute-done | bytes 1056 | tf_op jit(solution)/shard_map/ppermute | solution.py:119
  36.1 2.6 %collective-permute-done.1 = f32[256]{0:T(256)S(1)} collective-permute-done((f32[256]{0:T(256)S(1)}, f32[256]{0:T(256)S(1)}, u32[]{:S(2)}, u32[]{:S(2)}) %collective-permute-start.1) | collective-permute-done | bytes 1056 | tf_op jit(solution)/shard_map/ppermute | solution.py:119
  40.1 2.6 %collective-permute-done.2 = f32[256]{0:T(256)S(1)} collective-permute-done((f32[256]{0:T(256)S(1)}, f32[256]{0:T(256)S(1)}, u32[]{:S(2)}, u32[]{:S(2)}) %collective-permute-start.2) | collective-permute-done | bytes 1056 | tf_op jit(solution)/shard_map/ppermute | solution.py:119
  46.8 3.5 %collective-permute-done.5 = f32[8,16,1]{2,1,0:T(8,128)S(1)} collective-permute-done((f32[8,16,1]{2,1,0:T(8,128)S(1)}, f32[8,16,1]{2,1,0:T(8,128)S(1)}, u32[]{:S(2)}, u32[]{:S(2)}) %collective-permute-start.5) | collective-permute-done | bytes 544 | tf_op jit(solution)/shard_map/ppermute | solution.py:46
  53.4 4.4 %collective-permute-start.7 = (f32[8,1,512]{2,1,0:T(1,128)S(1)}, f32[8,1,512]{2,1,0:T(1,128)S(1)}, u32[]{:S(2)}, u32[]{:S(2)}) collective-permute-start(f32[8,1,512]{2,1,0:T(1,128)S(1)} %get-tuple-element.61), channel_id=1, source_target_pairs={{0,8},{8,16},{16,24},{24,2},{2,10},{10,18},{18,26},{26,4},{4,12},{... | collective-permute-start | bytes 49160 | tf_op jit(solution)/shard_map/ppermute | solution.py:49
  59.5 1.5 collective-permute-start.11
  61.0 4.8 %collective-permute-start.10 = (f32[8,1,512]{2,1,0:T(1,128)S(1)}, f32[8,1,512]{2,1,0:T(1,128)S(1)}, u32[]{:S(2)}, u32[]{:S(2)}) collective-permute-start(f32[8,1,512]{2,1,0:T(1,128)S(1)} %get-tuple-element.52), channel_id=1, source_target_pairs={{0,8},{8,16},{16,24},{24,2},{2,10},{10,18},{18,26},{26,4},{4,12},{... | collective-permute-start | bytes 49160 | tf_op jit(solution)/shard_map/ppermute | solution.py:49
  67.1 3.8 %collective-permute-done.9 = f32[8,1,512]{2,1,0:T(1,128)S(1)} collective-permute-done((f32[8,1,512]{2,1,0:T(1,128)S(1)}, f32[8,1,512]{2,1,0:T(1,128)S(1)}, u32[]{:S(2)}, u32[]{:S(2)}) %collective-permute-start.9) | collective-permute-done | bytes 16416 | tf_op jit(solution)/shard_map/ppermute | solution.py:50
  78.4 5.0 %collective-permute-start.16 = (f32[8,1,512]{2,1,0:T(1,128)}, f32[8,1,512]{2,1,0:T(1,128)}, u32[]{:S(2)}, u32[]{:S(2)}) collective-permute-start(f32[8,1,512]{2,1,0:T(1,128)} %get-tuple-element.45), channel_id=1, source_target_pairs={{0,8},{8,16},{16,24},{24,2},{2,10},{10,18},{18,26},{26,4},{4,12},{... | collective-permute-start | bytes 49160 | tf_op jit(solution)/shard_map/ppermute | solution.py:49
  85.1 3.0 %collective-permute-done.13 = f32[512]{0:T(512)S(1)} collective-permute-done((f32[512]{0:T(512)S(1)}, f32[512]{0:T(512)S(1)}, u32[]{:S(2)}, u32[]{:S(2)}) %collective-permute-start.13) | collective-permute-done | bytes 2080 | tf_op jit(solution)/shard_map/ppermute | solution.py:119
  89.1 3.0 %collective-permute-done.14 = f32[1024]{0:T(1024)S(1)} collective-permute-done((f32[1024]{0:T(1024)S(1)}, f32[1024]{0:T(1024)S(1)}, u32[]{:S(2)}, u32[]{:S(2)}) %collective-permute-start.14) | collective-permute-done | bytes 4128 | tf_op jit(solution)/shard_map/ppermute | solution.py:119
  97.2 1.9 %fusion.166 = (f32[512]{0:T(512)S(1)}, f32[8,16,512]{2,1,0:T(8,128)S(1)}) fusion(f32[8,16,512]{2,1,0:T(8,128)} %copy-done.1, f32[8,16,511]{2,1,0:T(8,128)} %get-tuple-element.47, f32[8,16,1]{2,1,0:T(8,128)} %get-tuple-element.77, f32[16,512]{1,0:T(8,128)S(1)} %get-tuple-element.85, f32[8,16,512]{2,1,0:T(8,128)S(1)} %get-tuple-element.18, ...), kind=kLoop, calls=%fused_computation.294 | loop fusion | flops 2096640 | bytes 4065280 | tf_op jit(solution)/shard_map/reduce_sum | solution.py:249
  103.1 3.7 %all-to-all-start.4 = ((f32[32,1,32]{2,1,0:T(1,128)}), f32[32,1,32]{2,1,0:T(1,128)S(1)}, u32[]{:S(2)}, u32[]{:S(2)}) async-start(f32[32,1,32]{2,1,0:T(1,128)} %broadcast_in_dim.37), calls=%async_computation.4 | async-start | bytes 32768 | tf_op jit(solution)/shard_map/all_to_all | solution.py:107
  108.2 3.2 %collective-permute-start.19 = (f32[8,1,512]{2,1,0:T(1,128)}, f32[8,1,512]{2,1,0:T(1,128)S(1)}, u32[]{:S(2)}, u32[]{:S(2)}) collective-permute-start(f32[8,1,512]{2,1,0:T(1,128)} %get-tuple-element.37), channel_id=1, source_target_pairs={{0,8},{8,16},{16,24},{24,2},{2,10},{10,18},{18,26},{26,4},{4,12},{... | collective-permute-start | bytes 49160 | tf_op jit(solution)/shard_map/ppermute | solution.py:49
  111.4 1.8 %collective-permute-start.20 = (f32[8,16,1]{2,1,0:T(8,128)S(1)}, f32[8,16,1]{2,1,0:T(8,128)}, u32[]{:S(2)}, u32[]{:S(2)}) collective-permute-start(f32[8,16,1]{2,1,0:T(8,128)S(1)} %slice_select_fusion.1), channel_id=1, source_target_pairs={{0,1},{1,0},{2,3},{3,2},{4,5},{5,4},{6,7},{7,6},{8,9},{9,8},{10,11... | collective-permute-start | bytes 1544 | tf_op jit(solution)/shard_map/ppermute | solution.py:46
  114.0 1.7 %fusion.1 = f32[2048]{0:T(1024)S(1)} fusion(f32[32,32]{1,0:T(8,128)S(1)} %bitcast.244, s32[2048]{0:T(1024)} %copy-done.20, s32[2048]{0:T(1024)} %copy-done.19), kind=kOutput, calls=%fused_computation.3 | convolution fusion | flops 25425920 | bytes 28672 | tf_op jit(solution)/shard_map/dot_general | solution.py:115
  117.7 2.1 %collective-permute-done.24 = f32[256]{0:T(256)S(1)} collective-permute-done((f32[256]{0:T(256)S(1)}, f32[256]{0:T(256)S(1)}, u32[]{:S(2)}, u32[]{:S(2)}) %collective-permute-start.24) | collective-permute-done | bytes 1056 | tf_op jit(solution)/shard_map/ppermute | solution.py:119
  122.1 1.6 %collective-permute-done.25 = f32[256]{0:T(256)S(1)} collective-permute-done((f32[256]{0:T(256)S(1)}, f32[256]{0:T(256)S(1)}, u32[]{:S(2)}, u32[]{:S(2)}) %collective-permute-start.25) | collective-permute-done | bytes 1056 | tf_op jit(solution)/shard_map/ppermute | solution.py:119
  125.1 2.6 %collective-permute-done.26 = f32[256]{0:T(256)S(1)} collective-permute-done((f32[256]{0:T(256)S(1)}, f32[256]{0:T(256)S(1)}, u32[]{:S(2)}, u32[]{:S(2)}) %collective-permute-start.26) | collective-permute-done | bytes 1056 | tf_op jit(solution)/shard_map/ppermute | solution.py:119
  134.3 1.7 %collective-permute-done.21 = f32[8,1,512]{2,1,0:T(1,128)S(1)} collective-permute-done((f32[8,1,512]{2,1,0:T(1,128)S(1)}, f32[8,1,512]{2,1,0:T(1,128)S(1)}, u32[]{:S(2)}, u32[]{:S(2)}) %collective-permute-start.21) | collective-permute-done | bytes 16416 | tf_op jit(solution)/shard_map/ppermute | solution.py:50
  136.9 1.5 collective-permute-start.27
  138.6 1.8 %collective-permute-done.27 = f32[512]{0:T(512)S(1)} collective-permute-done((f32[512]{0:T(512)S(1)}, f32[512]{0:T(512)S(1)}, u32[]{:S(2)}, u32[]{:S(2)}) %collective-permute-start.27) | collective-permute-done | bytes 2080 | tf_op jit(solution)/shard_map/ppermute | solution.py:119
  140.9 1.5 collective-permute-start.28
  143.2 5.0 %all-to-all-start.3 = ((f32[2,8,16,512]{3,2,0,1:T(8,128)}), f32[2,8,16,512]{3,2,0,1:T(8,128)S(1)}, u32[]{:S(2)}, u32[]{:S(2)}) async-start(f32[2,8,16,512]{3,2,0,1:T(8,128)} %pad_maximum_fusion.1), calls=%async_computation.3 | async-start | bytes 1048576 | tf_op jit(solution)/shard_map/all_to_all | solution.py:261
  149.1 3.0 %collective-permute-done.29 = f32[1024]{0:T(1024)S(1)} collective-permute-done((f32[1024]{0:T(1024)S(1)}, f32[1024]{0:T(1024)S(1)}, u32[]{:S(2)}, u32[]{:S(2)}) %collective-permute-start.29) | collective-permute-done | bytes 4128 | tf_op jit(solution)/shard_map/ppermute | solution.py:119
  153.7 3.7 %all-to-all-done.3 = f32[2,8,16,512]{3,2,0,1:T(8,128)S(1)} async-done(((f32[2,8,16,512]{3,2,0,1:T(8,128)}), f32[2,8,16,512]{3,2,0,1:T(8,128)S(1)}, u32[]{:S(2)}, u32[]{:S(2)}) %all-to-all-start.3) | async-done | bytes 524320 | tf_op jit(solution)/shard_map/all_to_all | solution.py:261
  (239 shorter events, 60.5 us)
Async XLA Ops:
  2.5 10.2 %all-to-all-start = ((f32[2,64,512]{2,0,1:T(2,128)}), f32[2,64,512]{2,0,1:T(2,128)S(1)}, u32[]{:S(2)}, u32[]{:S(2)}) async-start(f32[2,64,512]{2,0,1:T(2,128)} %copy.34), calls=%async_computation | async-start | bytes 524288 | tf_op jit(solution)/shard_map/all_to_all | solution.py:201
  13.7 12.6 %all-to-all-start.1 = ((f32[32,1,32]{2,1,0:T(1,128)}), f32[32,1,32]{2,1,0:T(1,128)S(1)}, u32[]{:S(2)}, u32[]{:S(2)}) async-start(f32[32,1,32]{2,1,0:T(1,128)} %broadcast_in_dim.29), calls=%async_computation.1 | async-start | bytes 32768 | tf_op jit(solution)/shard_map/all_to_all | solution.py:107
  26.3 16.7 %all-to-all-start.2 = ((f32[2,2,64,512]{3,1,0,2:T(2,128)}), f32[2,2,64,512]{3,1,0,2:T(2,128)S(1)}, u32[]{:S(2)}, u32[]{:S(2)}) async-start(f32[2,2,64,512]{3,1,0,2:T(2,128)} %copy.35), calls=%async_computation.2 | async-start | bytes 1048576 | tf_op jit(solution)/shard_map/all_to_all | solution.py:199
  31.1 3.6 %collective-permute-start = (f32[256]{0:T(256)S(1)}, f32[256]{0:T(256)S(1)}, u32[]{:S(2)}, u32[]{:S(2)}) collective-permute-start(f32[256]{0:T(256)S(1)} %dynamic-slice_subtract_fusion.5), channel_id=1, source_target_pairs={{0,1},{1,0},{2,3},{3,2},{4,5},{5,4},{6,7},{7,6},{8,9},{9,8},{10,11... | collective-permute-start | bytes 3080 | tf_op jit(solution)/shard_map/ppermute | solution.py:119
  35.1 3.6 %collective-permute-start.1 = (f32[256]{0:T(256)S(1)}, f32[256]{0:T(256)S(1)}, u32[]{:S(2)}, u32[]{:S(2)}) collective-permute-start(f32[256]{0:T(256)S(1)} %dynamic-slice_subtract_fusion.4), channel_id=1, source_target_pairs={{0,1},{1,0},{2,3},{3,2},{4,5},{5,4},{6,7},{7,6},{8,9},{9,8},{10,11... | collective-permute-start | bytes 3080 | tf_op jit(solution)/shard_map/ppermute | solution.py:119
  39.1 3.6 %collective-permute-start.2 = (f32[256]{0:T(256)S(1)}, f32[256]{0:T(256)S(1)}, u32[]{:S(2)}, u32[]{:S(2)}) collective-permute-start(f32[256]{0:T(256)S(1)} %dynamic-slice_subtract_fusion.3), channel_id=1, source_target_pairs={{0,1},{1,0},{2,3},{3,2},{4,5},{5,4},{6,7},{7,6},{8,9},{9,8},{10,11... | collective-permute-start | bytes 3080 | tf_op jit(solution)/shard_map/ppermute | solution.py:119
  43.5 6.9 %collective-permute-start.4 = (f32[8,1,512]{2,1,0:T(1,128)S(1)}, f32[8,1,512]{2,1,0:T(1,128)S(1)}, u32[]{:S(2)}, u32[]{:S(2)}) collective-permute-start(f32[8,1,512]{2,1,0:T(1,128)S(1)} %get-tuple-element.66), channel_id=1, source_target_pairs={{0,8},{8,16},{16,24},{24,2},{2,10},{10,18},{18,26},{26,4},{4,12},{... | collective-permute-start | bytes 49160 | tf_op jit(solution)/shard_map/ppermute | solution.py:49
  44.8 5.7 %collective-permute-start.3 = (f32[8,1,512]{2,1,0:T(1,128)S(1)}, f32[8,1,512]{2,1,0:T(1,128)S(1)}, u32[]{:S(2)}, u32[]{:S(2)}) collective-permute-start(f32[8,1,512]{2,1,0:T(1,128)S(1)} %get-tuple-element.67), channel_id=1, source_target_pairs={{8,0},{16,8},{24,16},{2,24},{10,2},{18,10},{26,18},{4,26},{12,4},{... | collective-permute-start | bytes 49160 | tf_op jit(solution)/shard_map/ppermute | solution.py:50
  46.1 4.3 %collective-permute-start.5 = (f32[8,16,1]{2,1,0:T(8,128)S(1)}, f32[8,16,1]{2,1,0:T(8,128)S(1)}, u32[]{:S(2)}, u32[]{:S(2)}) collective-permute-start(f32[8,16,1]{2,1,0:T(8,128)S(1)} %slice_select_fusion.5), channel_id=1, source_target_pairs={{0,1},{1,0},{2,3},{3,2},{4,5},{5,4},{6,7},{7,6},{8,9},{9,8},{10,11... | collective-permute-start | bytes 1544 | tf_op jit(solution)/shard_map/ppermute | solution.py:46
  51.4 6.5 %collective-permute-start.8 = (f32[8,16,1]{2,1,0:T(8,128)S(1)}, f32[8,16,1]{2,1,0:T(8,128)S(1)}, u32[]{:S(2)}, u32[]{:S(2)}) collective-permute-start(f32[8,16,1]{2,1,0:T(8,128)S(1)} %slice_select_fusion.4), channel_id=1, source_target_pairs={{0,1},{1,0},{2,3},{3,2},{4,5},{5,4},{6,7},{7,6},{8,9},{9,8},{10,11... | collective-permute-start | bytes 1544 | tf_op jit(solution)/shard_map/ppermute | solution.py:46
  52.1 5.8 %collective-permute-start.6 = (f32[8,1,512]{2,1,0:T(1,128)S(1)}, f32[8,1,512]{2,1,0:T(1,128)S(1)}, u32[]{:S(2)}, u32[]{:S(2)}) collective-permute-start(f32[8,1,512]{2,1,0:T(1,128)S(1)} %get-tuple-element.60), channel_id=1, source_target_pairs={{8,0},{16,8},{24,16},{2,24},{10,2},{18,10},{26,18},{4,26},{12,4},{... | collective-permute-start | bytes 49160 | tf_op jit(solution)/shard_map/ppermute | solution.py:50
  53.4 5.3 %collective-permute-start.7 = (f32[8,1,512]{2,1,0:T(1,128)S(1)}, f32[8,1,512]{2,1,0:T(1,128)S(1)}, u32[]{:S(2)}, u32[]{:S(2)}) collective-permute-start(f32[8,1,512]{2,1,0:T(1,128)S(1)} %get-tuple-element.61), channel_id=1, source_target_pairs={{0,8},{8,16},{16,24},{24,2},{2,10},{10,18},{18,26},{26,4},{4,12},{... | collective-permute-start | bytes 49160 | tf_op jit(solution)/shard_map/ppermute | solution.py:49
  59.5 7.6 %collective-permute-start.11 = (f32[8,16,1]{2,1,0:T(8,128)S(1)}, f32[8,16,1]{2,1,0:T(8,128)S(1)}, u32[]{:S(2)}, u32[]{:S(2)}) collective-permute-start(f32[8,16,1]{2,1,0:T(8,128)S(1)} %slice_select_fusion.3), channel_id=1, source_target_pairs={{0,1},{1,0},{2,3},{3,2},{4,5},{5,4},{6,7},{7,6},{8,9},{9,8},{10,11... | collective-permute-start | bytes 1544 | tf_op jit(solution)/shard_map/ppermute | solution.py:46
  61.0 6.2 %collective-permute-start.10 = (f32[8,1,512]{2,1,0:T(1,128)S(1)}, f32[8,1,512]{2,1,0:T(1,128)S(1)}, u32[]{:S(2)}, u32[]{:S(2)}) collective-permute-start(f32[8,1,512]{2,1,0:T(1,128)S(1)} %get-tuple-element.52), channel_id=1, source_target_pairs={{0,8},{8,16},{16,24},{24,2},{2,10},{10,18},{18,26},{26,4},{4,12},{... | collective-permute-start | bytes 49160 | tf_op jit(solution)/shard_map/ppermute | solution.py:49
  65.8 5.2 %collective-permute-start.9 = (f32[8,1,512]{2,1,0:T(1,128)S(1)}, f32[8,1,512]{2,1,0:T(1,128)S(1)}, u32[]{:S(2)}, u32[]{:S(2)}) collective-permute-start(f32[8,1,512]{2,1,0:T(1,128)S(1)} %get-tuple-element.53), channel_id=1, source_target_pairs={{8,0},{16,8},{24,16},{2,24},{10,2},{18,10},{26,18},{4,26},{12,4},{... | collective-permute-start | bytes 49160 | tf_op jit(solution)/shard_map/ppermute | solution.py:50
  75.0 8.5 %collective-permute-start.17 = (f32[8,16,1]{2,1,0:T(8,128)S(1)}, f32[8,16,1]{2,1,0:T(8,128)S(1)}, u32[]{:S(2)}, u32[]{:S(2)}) collective-permute-start(f32[8,16,1]{2,1,0:T(8,128)S(1)} %slice_select_fusion.2), channel_id=1, source_target_pairs={{0,1},{1,0},{2,3},{3,2},{4,5},{5,4},{6,7},{7,6},{8,9},{9,8},{10,11... | collective-permute-start | bytes 1544 | tf_op jit(solution)/shard_map/ppermute | solution.py:46
  75.7 8.4 %collective-permute-start.12 = (f32[512]{0:T(512)S(1)}, f32[512]{0:T(512)S(1)}, u32[]{:S(2)}, u32[]{:S(2)}) collective-permute-start(f32[512]{0:T(512)S(1)} %pad_maximum_fusion.5), channel_id=1, source_target_pairs={{0,1},{1,0},{2,3},{3,2},{4,5},{5,4},{6,7},{7,6},{8,9},{9,8},{10,11... | collective-permute-start | bytes 6152 | tf_op jit(solution)/shard_map/ppermute | solution.py:119
  77.1 20.0 %collective-permute-start.15 = (f32[8,1,512]{2,1,0:T(1,128)}, f32[8,1,512]{2,1,0:T(1,128)}, u32[]{:S(2)}, u32[]{:S(2)}) collective-permute-start(f32[8,1,512]{2,1,0:T(1,128)} %get-tuple-element.44), channel_id=1, source_target_pairs={{8,0},{16,8},{24,16},{2,24},{10,2},{18,10},{26,18},{4,26},{12,4},{... | collective-permute-start | bytes 49160 | tf_op jit(solution)/shard_map/ppermute | solution.py:50
  78.4 18.8 %collective-permute-start.16 = (f32[8,1,512]{2,1,0:T(1,128)}, f32[8,1,512]{2,1,0:T(1,128)}, u32[]{:S(2)}, u32[]{:S(2)}) collective-permute-start(f32[8,1,512]{2,1,0:T(1,128)} %get-tuple-element.45), channel_id=1, source_target_pairs={{0,8},{8,16},{16,24},{24,2},{2,10},{10,18},{18,26},{26,4},{4,12},{... | collective-permute-start | bytes 49160 | tf_op jit(solution)/shard_map/ppermute | solution.py:49
  84.5 3.6 %collective-permute-start.13 = (f32[512]{0:T(512)S(1)}, f32[512]{0:T(512)S(1)}, u32[]{:S(2)}, u32[]{:S(2)}) collective-permute-start(f32[512]{0:T(512)S(1)} %pad_maximum_fusion.6), channel_id=1, source_target_pairs={{0,1},{1,0},{2,3},{3,2},{4,5},{5,4},{6,7},{7,6},{8,9},{9,8},{10,11... | collective-permute-start | bytes 6152 | tf_op jit(solution)/shard_map/ppermute | solution.py:119
  88.4 3.7 %collective-permute-start.14 = (f32[1024]{0:T(1024)S(1)}, f32[1024]{0:T(1024)S(1)}, u32[]{:S(2)}, u32[]{:S(2)}) collective-permute-start(f32[1024]{0:T(1024)S(1)} %pad_maximum_fusion.3), channel_id=1, source_target_pairs={{0,1},{1,0},{2,3},{3,2},{4,5},{5,4},{6,7},{7,6},{8,9},{9,8},{10,11... | collective-permute-start | bytes 12296 | tf_op jit(solution)/shard_map/ppermute | solution.py:119
  103.1 10.8 %all-to-all-start.4 = ((f32[32,1,32]{2,1,0:T(1,128)}), f32[32,1,32]{2,1,0:T(1,128)S(1)}, u32[]{:S(2)}, u32[]{:S(2)}) async-start(f32[32,1,32]{2,1,0:T(1,128)} %broadcast_in_dim.37), calls=%async_computation.4 | async-start | bytes 32768 | tf_op jit(solution)/shard_map/all_to_all | solution.py:107
  106.9 21.1 %collective-permute-start.18 = (f32[8,1,512]{2,1,0:T(1,128)}, f32[8,1,512]{2,1,0:T(1,128)S(1)}, u32[]{:S(2)}, u32[]{:S(2)}) collective-permute-start(f32[8,1,512]{2,1,0:T(1,128)} %get-tuple-element.36), channel_id=1, source_target_pairs={{8,0},{16,8},{24,16},{2,24},{10,2},{18,10},{26,18},{4,26},{12,4},{... | collective-permute-start | bytes 49160 | tf_op jit(solution)/shard_map/ppermute | solution.py:50
  108.2 19.9 %collective-permute-start.19 = (f32[8,1,512]{2,1,0:T(1,128)}, f32[8,1,512]{2,1,0:T(1,128)S(1)}, u32[]{:S(2)}, u32[]{:S(2)}) collective-permute-start(f32[8,1,512]{2,1,0:T(1,128)} %get-tuple-element.37), channel_id=1, source_target_pairs={{0,8},{8,16},{16,24},{24,2},{2,10},{10,18},{18,26},{26,4},{4,12},{... | collective-permute-start | bytes 49160 | tf_op jit(solution)/shard_map/ppermute | solution.py:49
  111.4 5.4 %collective-permute-start.20 = (f32[8,16,1]{2,1,0:T(8,128)S(1)}, f32[8,16,1]{2,1,0:T(8,128)}, u32[]{:S(2)}, u32[]{:S(2)}) collective-permute-start(f32[8,16,1]{2,1,0:T(8,128)S(1)} %slice_select_fusion.1), channel_id=1, source_target_pairs={{0,1},{1,0},{2,3},{3,2},{4,5},{5,4},{6,7},{7,6},{8,9},{9,8},{10,11... | collective-permute-start | bytes 1544 | tf_op jit(solution)/shard_map/ppermute | solution.py:46
  129.9 4.3 %collective-permute-start.23 = (f32[8,16,1]{2,1,0:T(8,128)S(1)}, f32[8,16,1]{2,1,0:T(8,128)S(1)}, u32[]{:S(2)}, u32[]{:S(2)}) collective-permute-start(f32[8,16,1]{2,1,0:T(8,128)S(1)} %slice_select_fusion), channel_id=1, source_target_pairs={{0,1},{1,0},{2,3},{3,2},{4,5},{5,4},{6,7},{7,6},{8,9},{9,8},{10,11... | collective-permute-start | bytes 1544 | tf_op jit(solution)/shard_map/ppermute | solution.py:46
  130.7 3.6 %collective-permute-start.22 = (f32[8,1,512]{2,1,0:T(1,128)S(1)}, f32[8,1,512]{2,1,0:T(1,128)S(1)}, u32[]{:S(2)}, u32[]{:S(2)}) collective-permute-start(f32[8,1,512]{2,1,0:T(1,128)S(1)} %get-tuple-element.28), channel_id=1, source_target_pairs={{0,8},{8,16},{16,24},{24,2},{2,10},{10,18},{18,26},{26,4},{4,12},{... | collective-permute-start | bytes 49160 | tf_op jit(solution)/shard_map/ppermute | solution.py:49
  132.0 4.0 %collective-permute-start.21 = (f32[8,1,512]{2,1,0:T(1,128)S(1)}, f32[8,1,512]{2,1,0:T(1,128)S(1)}, u32[]{:S(2)}, u32[]{:S(2)}) collective-permute-start(f32[8,1,512]{2,1,0:T(1,128)S(1)} %get-tuple-element.29), channel_id=1, source_target_pairs={{8,0},{16,8},{24,16},{2,24},{10,2},{18,10},{26,18},{4,26},{12,4},{... | collective-permute-start | bytes 49160 | tf_op jit(solution)/shard_map/ppermute | solution.py:50
  136.9 3.6 %collective-permute-start.27 = (f32[512]{0:T(512)S(1)}, f32[512]{0:T(512)S(1)}, u32[]{:S(2)}, u32[]{:S(2)}) collective-permute-start(f32[512]{0:T(512)S(1)} %pad_maximum_fusion.7), channel_id=1, source_target_pairs={{0,1},{1,0},{2,3},{3,2},{4,5},{5,4},{6,7},{7,6},{8,9},{9,8},{10,11... | collective-permute-start | bytes 6152 | tf_op jit(solution)/shard_map/ppermute | solution.py:119
  140.9 7.3 %collective-permute-start.28 = (f32[512]{0:T(512)S(1)}, f32[512]{0:T(512)S(1)}, u32[]{:S(2)}, u32[]{:S(2)}) collective-permute-start(f32[512]{0:T(512)S(1)} %pad_maximum_fusion.8), channel_id=1, source_target_pairs={{0,1},{1,0},{2,3},{3,2},{4,5},{5,4},{6,7},{7,6},{8,9},{9,8},{10,11... | collective-permute-start | bytes 6152 | tf_op jit(solution)/shard_map/ppermute | solution.py:119
  143.2 14.2 %all-to-all-start.3 = ((f32[2,8,16,512]{3,2,0,1:T(8,128)}), f32[2,8,16,512]{3,2,0,1:T(8,128)S(1)}, u32[]{:S(2)}, u32[]{:S(2)}) async-start(f32[2,8,16,512]{3,2,0,1:T(8,128)} %pad_maximum_fusion.1), calls=%async_computation.3 | async-start | bytes 1048576 | tf_op jit(solution)/shard_map/all_to_all | solution.py:261
  148.5 3.7 %collective-permute-start.29 = (f32[1024]{0:T(1024)S(1)}, f32[1024]{0:T(1024)S(1)}, u32[]{:S(2)}, u32[]{:S(2)}) collective-permute-start(f32[1024]{0:T(1024)S(1)} %pad_maximum_fusion.4), channel_id=1, source_target_pairs={{0,1},{1,0},{2,3},{3,2},{4,5},{5,4},{6,7},{7,6},{8,9},{9,8},{10,11... | collective-permute-start | bytes 12296 | tf_op jit(solution)/shard_map/ppermute | solution.py:119
  (25 other events, 366.4 us)

commit v14 on v12

--- a/solution.py
+++ b/solution.py
@@ -196,6 +196,21 @@
         + (lax.axis_index("col") * given_cols + jnp.arange(given_cols, dtype=jnp.int32))[None, :]
     ).reshape(-1)
     given_pick = (given_ids[:, None] == port_tile.reshape(-1)[None, :]).astype(jnp.float32)
+    start_rhs = None
+    pair_cols = lax.axis_size("col")
+    if pair_cols == 2:
+        layer_n, row_n = layer_count, lax.axis_size("row")
+        start_plane = jnp.sum(sources, axis=0)
+        start_tiles = start_plane.reshape(given_rows, TILE, given_cols, TILE).sum(axis=(1, 3)).reshape(-1)
+        count = layer_n * row_n * pair_cols
+        got = lax.all_to_all(jnp.broadcast_to(start_tiles[None], (count, start_tiles.size)), ("layer", "row", "col"), 0, 0, tiled=True)
+        flat = port_tile.reshape(-1)
+        tr, tc = flat // given_tile_cols, flat % given_tile_cols
+        devices = jnp.arange(count, dtype=jnp.int32)
+        same = ((devices // pair_cols) % row_n == (tr // given_rows)[:, None]) & (devices % pair_cols == (tc // given_cols)[:, None])
+        slot = (tr % given_rows) * given_cols + tc % given_cols
+        pick_slot = (slot[:, None] == jnp.arange(start_tiles.size, dtype=jnp.int32)[None, :]).astype(jnp.float32)
+        start_rhs = jnp.sum(jnp.dot(same.astype(jnp.float32), got, precision=highest) * pick_slot, axis=1)
     packed = lax.all_to_all(jnp.stack((conduct, vertical)), "layer", 2, 1, tiled=True)
     conduct, vertical = packed[0], packed[1]
     sources = lax.all_to_all(sources, "layer", 1, 0, tiled=True)
@@ -247,7 +262,10 @@
             resid = sources - apply_grid(drop, drop_near, weights, pad_term)
         plane = jnp.sum(resid, axis=0)
         tiles = plane.reshape(own_rows, TILE, own_cols, TILE).sum(axis=(1, 3)).reshape(-1)
-        rhs = share_tiles(tiles, own_rows, own_cols, flat_tiles).reshape(NPANEL, PANEL) * (restrict_scale / TILE)
+        if drop is None and start_rhs is not None:
+            rhs = start_rhs.reshape(NPANEL, PANEL) * (restrict_scale / TILE)
+        else:
+            rhs = share_tiles(tiles, own_rows, own_cols, flat_tiles).reshape(NPANEL, PANEL) * (restrict_scale / TILE)
         total = smooth(resid, weights, pad_term, inverse)
         if col_count == 2 and outer == ITERS - 1 and drop is not None:
             ports = coarse_pair(rhs, pivots, coupling, total)

time: 157 us -> 160 us (1.019)
  waiting for transfers between devices: 48.6 us -> 51.2 us
    all_to_all x2 -> x1, starting transfers between devices: 13.9 us -> 6.18 us  [share_tiles(): got = lax.all_to_all(payload, ('layer', 'row', 'col'), 0, 0, tiled=True)]
    all_to_all x1, waiting for transfers between devices: 0.01 us -> 7.47 us  [shards(): lax.all_to_all(jnp.stack((conduct, vertical)), 'layer', 2, 1, tiled=True)]
    all_to_all x0 -> x1, starting transfers between devices: none -> 7.33 us  [shards(): lax.all_to_all(jnp.broadcast_to(start_tiles[None], (count, start_tiles.si...]
    ppermute x6, waiting for transfers between devices: 1.64 us -> 7.31 us  [rims(): lax.ppermute(head, axis, [(place[i + 1], place[i]) for i in range(count -...]
    all_to_all x0 -> x1, waiting for transfers between devices: none -> 5.2 us  [shards(): lax.all_to_all(jnp.broadcast_to(start_tiles[None], (count, start_tiles.si...]
    all_to_all x2 -> x1, waiting for transfers between devices: 6.2 us -> 1.5 us  [share_tiles(): got = lax.all_to_all(payload, ('layer', 'row', 'col'), 0, 0, tiled=True)]
    ppermute x6, waiting for transfers between devices: 4.59 us -> 0.02 us  [rims(): got = lax.ppermute(jnp.where(low, tail, head), axis, [(0, 1), (1, 0)])]
    all_to_all x1, waiting for transfers between devices: 3.96 us -> 0.01 us  [shards(): sources = lax.all_to_all(sources, 'layer', 1, 0, tiled=True)]
  transfers between devices with their start and end apart: 35 -> 35, of which waited for: 21 -> 20; matrix products, arithmetic and copies ran while one was open for 13% -> 14% of each run, Pallas kernels for 0% -> 0%
where the time goes in v14:
time: 160 us; the launch traced here: 158 us
  starting transfers between devices  69.3 us (43%)
  waiting for transfers between devices  51.2 us (32%)
  matrix products  13.7 us (9%)
  other arithmetic  11.7 us (7%)
  local copies, waits for them, and re-layouts  10.5 us (7%)
  between operations  1.63 us (1%)
    ppermute x12, waiting for transfers between devices, swap_col(): return lax.ppermute(value, 'col', [(0, 1), (1, 0)])  24.8 us
    ppermute x6, starting transfers between devices, rims(): lax.ppermute(tail, axis, [(place[i], place[i + 1]) for i in range(count -...  19.5 us
    ppermute x12, starting transfers between devices, swap_col(): return lax.ppermute(value, 'col', [(0, 1), (1, 0)])  9.14 us
    ppermute x6, starting transfers between devices, rims(): lax.ppermute(head, axis, [(place[i + 1], place[i]) for i in range(count -...  7.93 us
    all_to_all x1, waiting for transfers between devices, shards(): lax.all_to_all(jnp.stack((conduct, vertical)), 'layer', 2, 1, tiled=True)  7.47 us
    all_to_all x1, starting transfers between devices, shards(): lax.all_to_all(jnp.broadcast_to(start_tiles[None], (count, start_tiles.si...  7.33 us
    ppermute x6, waiting for transfers between devices, rims(): lax.ppermute(head, axis, [(place[i + 1], place[i]) for i in range(count -...  7.31 us
    ppermute x6, starting transfers between devices, rims(): got = lax.ppermute(jnp.where(low, tail, head), axis, [(0, 1), (1, 0)])  6.69 us
  transfers between devices with their start and end apart: 35, of which 20 were waited for; matrix products, arithmetic and copies ran while one was open for 14% of the time, Pallas kernels for 0%

profile of v14, /device:TPU:0, one launch (start us, length us, event | category | flops | bytes accessed | tf_op | source)
XLA Modules:
  0.0 158.0 jit_solution(9020308451953048650)
XLA Ops:
  3.0 7.3 %all-to-all-start = ((f32[32,1,128]{2,1,0:T(1,128)}), f32[32,1,128]{2,1,0:T(1,128)S(1)}, u32[]{:S(2)}, u32[]{:S(2)}) async-start(f32[32,1,128]{2,1,0:T(1,128)} %broadcast_in_dim.32), calls=%async_computation | async-start | bytes 32768 | tf_op jit(solution)/shard_map/all_to_all | solution.py:206
  12.2 5.2 %all-to-all-done = f32[32,1,128]{2,1,0:T(1,128)S(1)} async-done(((f32[32,1,128]{2,1,0:T(1,128)}), f32[32,1,128]{2,1,0:T(1,128)S(1)}, u32[]{:S(2)}, u32[]{:S(2)}) %all-to-all-start) | async-done | bytes 16416 | tf_op jit(solution)/shard_map/all_to_all | solution.py:206
  17.4 3.4 %all-to-all-start.2 = ((f32[2,64,512]{2,0,1:T(2,128)}), f32[2,64,512]{2,0,1:T(2,128)S(1)}, u32[]{:S(2)}, u32[]{:S(2)}) async-start(f32[2,64,512]{2,0,1:T(2,128)} %copy.37), calls=%async_computation.2 | async-start | bytes 524288 | tf_op jit(solution)/shard_map/all_to_all | solution.py:216
  28.7 1.6 %collective-permute-done.1 = f32[256]{0:T(256)S(1)} collective-permute-done((f32[256]{0:T(256)S(1)}, f32[256]{0:T(256)S(1)}, u32[]{:S(2)}, u32[]{:S(2)}) %collective-permute-start.1) | collective-permute-done | bytes 1056 | tf_op jit(solution)/shard_map/ppermute | solution.py:119
  32.7 1.6 %collective-permute-done.2 = f32[256]{0:T(256)S(1)} collective-permute-done((f32[256]{0:T(256)S(1)}, f32[256]{0:T(256)S(1)}, u32[]{:S(2)}, u32[]{:S(2)}) %collective-permute-start.2) | collective-permute-done | bytes 1056 | tf_op jit(solution)/shard_map/ppermute | solution.py:119
  35.9 2.7 %collective-permute-done.3 = f32[512]{0:T(512)S(1)} collective-permute-done((f32[512]{0:T(512)S(1)}, f32[512]{0:T(512)S(1)}, u32[]{:S(2)}, u32[]{:S(2)}) %collective-permute-start.3) | collective-permute-done | bytes 2080 | tf_op jit(solution)/shard_map/ppermute | solution.py:119
  39.6 3.0 %collective-permute-done.4 = f32[512]{0:T(512)S(1)} collective-permute-done((f32[512]{0:T(512)S(1)}, f32[512]{0:T(512)S(1)}, u32[]{:S(2)}, u32[]{:S(2)}) %collective-permute-start.4) | collective-permute-done | bytes 2080 | tf_op jit(solution)/shard_map/ppermute | solution.py:119
  43.5 3.0 %collective-permute-done.5 = f32[1024]{0:T(1024)S(1)} collective-permute-done((f32[1024]{0:T(1024)S(1)}, f32[1024]{0:T(1024)S(1)}, u32[]{:S(2)}, u32[]{:S(2)}) %collective-permute-start.5) | collective-permute-done | bytes 4128 | tf_op jit(solution)/shard_map/ppermute | solution.py:119
  47.2 3.5 %all-to-all-start.1 = ((f32[2,2,64,512]{3,1,0,2:T(2,128)}), f32[2,2,64,512]{3,1,0,2:T(2,128)S(1)}, u32[]{:S(2)}, u32[]{:S(2)}) async-start(f32[2,2,64,512]{3,1,0,2:T(2,128)} %copy.34), calls=%async_computation.1 | async-start | bytes 1048576 | tf_op jit(solution)/shard_map/all_to_all | solution.py:214
  52.0 7.5 %all-to-all-done.1 = f32[2,2,64,512]{3,1,0,2:T(2,128)S(1)} async-done(((f32[2,2,64,512]{3,1,0,2:T(2,128)}), f32[2,2,64,512]{3,1,0,2:T(2,128)S(1)}, u32[]{:S(2)}, u32[]{:S(2)}) %all-to-all-start.1) | async-done | bytes 524320 | tf_op jit(solution)/shard_map/all_to_all | solution.py:214
  62.0 3.0 %collective-permute-start.7 = (f32[8,1,512]{2,1,0:T(1,128)S(1)}, f32[8,1,512]{2,1,0:T(1,128)S(1)}, u32[]{:S(2)}, u32[]{:S(2)}) collective-permute-start(f32[8,1,512]{2,1,0:T(1,128)S(1)} %get-tuple-element.70), channel_id=1, source_target_pairs={{0,8},{8,16},{16,24},{24,2},{2,10},{10,18},{18,26},{26,4},{4,12},{... | collective-permute-start | bytes 49160 | tf_op jit(solution)/shard_map/ppermute | solution.py:49
  66.8 1.5 collective-permute-start.11
  68.3 2.2 %collective-permute-start.10 = (f32[8,1,512]{2,1,0:T(1,128)S(1)}, f32[8,1,512]{2,1,0:T(1,128)S(1)}, u32[]{:S(2)}, u32[]{:S(2)}) collective-permute-start(f32[8,1,512]{2,1,0:T(1,128)S(1)} %get-tuple-element.65), channel_id=1, source_target_pairs={{0,8},{8,16},{16,24},{24,2},{2,10},{10,18},{18,26},{26,4},{4,12},{... | collective-permute-start | bytes 49160 | tf_op jit(solution)/shard_map/ppermute | solution.py:49
  71.8 3.8 %collective-permute-done.9 = f32[8,1,512]{2,1,0:T(1,128)S(1)} collective-permute-done((f32[8,1,512]{2,1,0:T(1,128)S(1)}, f32[8,1,512]{2,1,0:T(1,128)S(1)}, u32[]{:S(2)}, u32[]{:S(2)}) %collective-permute-start.9) | collective-permute-done | bytes 16416 | tf_op jit(solution)/shard_map/ppermute | solution.py:50
  77.1 4.1 %collective-permute-start.13 = (f32[8,1,512]{2,1,0:T(1,128)S(1)}, f32[8,1,512]{2,1,0:T(1,128)S(1)}, u32[]{:S(2)}, u32[]{:S(2)}) collective-permute-start(f32[8,1,512]{2,1,0:T(1,128)S(1)} %get-tuple-element.57), channel_id=1, source_target_pairs={{0,8},{8,16},{16,24},{24,2},{2,10},{10,18},{18,26},{26,4},{4,12},{... | collective-permute-start | bytes 49160 | tf_op jit(solution)/shard_map/ppermute | solution.py:49
  82.6 1.7 %collective-permute-done.12 = f32[8,1,512]{2,1,0:T(1,128)S(1)} collective-permute-done((f32[8,1,512]{2,1,0:T(1,128)S(1)}, f32[8,1,512]{2,1,0:T(1,128)S(1)}, u32[]{:S(2)}, u32[]{:S(2)}) %collective-permute-start.12) | collective-permute-done | bytes 16416 | tf_op jit(solution)/shard_map/ppermute | solution.py:50
  87.4 5.4 %collective-permute-start.16 = (f32[8,1,512]{2,1,0:T(1,128)S(1)}, f32[8,1,512]{2,1,0:T(1,128)S(1)}, u32[]{:S(2)}, u32[]{:S(2)}) collective-permute-start(f32[8,1,512]{2,1,0:T(1,128)S(1)} %get-tuple-element.49), channel_id=1, source_target_pairs={{0,8},{8,16},{16,24},{24,2},{2,10},{10,18},{18,26},{26,4},{4,12},{... | collective-permute-start | bytes 49160 | tf_op jit(solution)/shard_map/ppermute | solution.py:49
  94.2 1.7 %collective-permute-done.15 = f32[8,1,512]{2,1,0:T(1,128)S(1)} collective-permute-done((f32[8,1,512]{2,1,0:T(1,128)S(1)}, f32[8,1,512]{2,1,0:T(1,128)S(1)}, u32[]{:S(2)}, u32[]{:S(2)}) %collective-permute-start.15) | collective-permute-done | bytes 16416 | tf_op jit(solution)/shard_map/ppermute | solution.py:50
  100.5 6.2 %all-to-all-start.4 = ((f32[32,1,32]{2,1,0:T(1,128)}), f32[32,1,32]{2,1,0:T(1,128)}, u32[]{:S(2)}, u32[]{:S(2)}) async-start(f32[32,1,32]{2,1,0:T(1,128)} %broadcast_in_dim.40), calls=%async_computation.4 | async-start | bytes 32768 | tf_op jit(solution)/shard_map/all_to_all | solution.py:107
  107.3 1.7 %collective-permute-start.20 = (f32[8,16,1]{2,1,0:T(8,128)}, f32[8,16,1]{2,1,0:T(8,128)S(1)}, u32[]{:S(2)}, u32[]{:S(2)}) collective-permute-start(f32[8,16,1]{2,1,0:T(8,128)} %slice_select_fusion.1), channel_id=1, source_target_pairs={{0,1},{1,0},{2,3},{3,2},{4,5},{5,4},{6,7},{7,6},{8,9},{9,8},{10,11... | collective-permute-start | bytes 1544 | tf_op jit(solution)/shard_map/ppermute | solution.py:46
  109.0 1.7 %collective-permute-start.19 = (f32[8,1,512]{2,1,0:T(1,128)}, f32[8,1,512]{2,1,0:T(1,128)S(1)}, u32[]{:S(2)}, u32[]{:S(2)}) collective-permute-start(f32[8,1,512]{2,1,0:T(1,128)} %get-tuple-element.41), channel_id=1, source_target_pairs={{0,8},{8,16},{16,24},{24,2},{2,10},{10,18},{18,26},{26,4},{4,12},{... | collective-permute-start | bytes 49160 | tf_op jit(solution)/shard_map/ppermute | solution.py:49
  110.8 1.5 collective-permute-start.18
  112.3 1.5 all-to-all-done.4
  113.8 1.7 %fusion.1 = f32[2048]{0:T(1024)S(1)} fusion(f32[32,32]{1,0:T(8,128)} %bitcast.56, s32[2048]{0:T(1024)} %get-tuple-element.4, s32[2048]{0:T(1024)} %get-tuple-element.105), kind=kOutput, calls=%fused_computation.3 | convolution fusion | flops 25425920 | bytes 28672 | tf_op jit(solution)/shard_map/dot_general | solution.py:115
  116.6 2.9 %collective-permute-done.24 = f32[256]{0:T(256)S(1)} collective-permute-done((f32[256]{0:T(256)S(1)}, f32[256]{0:T(256)S(1)}, u32[]{:S(2)}, u32[]{:S(2)}) %collective-permute-start.24) | collective-permute-done | bytes 1056 | tf_op jit(solution)/shard_map/ppermute | solution.py:119
  121.9 1.6 %collective-permute-done.25 = f32[256]{0:T(256)S(1)} collective-permute-done((f32[256]{0:T(256)S(1)}, f32[256]{0:T(256)S(1)}, u32[]{:S(2)}, u32[]{:S(2)}) %collective-permute-start.25) | collective-permute-done | bytes 1056 | tf_op jit(solution)/shard_map/ppermute | solution.py:119
  124.9 2.6 %collective-permute-done.26 = f32[256]{0:T(256)S(1)} collective-permute-done((f32[256]{0:T(256)S(1)}, f32[256]{0:T(256)S(1)}, u32[]{:S(2)}, u32[]{:S(2)}) %collective-permute-start.26) | collective-permute-done | bytes 1056 | tf_op jit(solution)/shard_map/ppermute | solution.py:119
  131.8 3.0 %collective-permute-start.22 = (f32[8,1,512]{2,1,0:T(1,128)S(1)}, f32[8,1,512]{2,1,0:T(1,128)S(1)}, u32[]{:S(2)}, u32[]{:S(2)}) collective-permute-start(f32[8,1,512]{2,1,0:T(1,128)S(1)} %get-tuple-element.32), channel_id=1, source_target_pairs={{0,8},{8,16},{16,24},{24,2},{2,10},{10,18},{18,26},{26,4},{4,12},{... | collective-permute-start | bytes 49160 | tf_op jit(solution)/shard_map/ppermute | solution.py:49
  138.2 1.9 %collective-permute-done.27 = f32[512]{0:T(512)S(1)} collective-permute-done((f32[512]{0:T(512)S(1)}, f32[512]{0:T(512)S(1)}, u32[]{:S(2)}, u32[]{:S(2)}) %collective-permute-start.27) | collective-permute-done | bytes 2080 | tf_op jit(solution)/shard_map/ppermute | solution.py:119
  142.8 5.6 %all-to-all-start.3 = ((f32[2,8,16,512]{3,2,0,1:T(8,128)}), f32[2,8,16,512]{3,2,0,1:T(8,128)S(1)}, u32[]{:S(2)}, u32[]{:S(2)}) async-start(f32[2,8,16,512]{3,2,0,1:T(8,128)} %pad_maximum_fusion.1), calls=%async_computation.3 | async-start | bytes 1048576 | tf_op jit(solution)/shard_map/all_to_all | solution.py:279
  149.3 3.0 %collective-permute-done.29 = f32[1024]{0:T(1024)S(1)} collective-permute-done((f32[1024]{0:T(1024)S(1)}, f32[1024]{0:T(1024)S(1)}, u32[]{:S(2)}, u32[]{:S(2)}) %collective-permute-start.29) | collective-permute-done | bytes 4128 | tf_op jit(solution)/shard_map/ppermute | solution.py:119
  153.9 3.3 %all-to-all-done.3 = f32[2,8,16,512]{3,2,0,1:T(8,128)S(1)} async-done(((f32[2,8,16,512]{3,2,0,1:T(8,128)}), f32[2,8,16,512]{3,2,0,1:T(8,128)S(1)}, u32[]{:S(2)}, u32[]{:S(2)}) %all-to-all-start.3) | async-done | bytes 524320 | tf_op jit(solution)/shard_map/all_to_all | solution.py:279
  (239 shorter events, 55.9 us)
Async XLA Ops:
  3.0 14.5 %all-to-all-start = ((f32[32,1,128]{2,1,0:T(1,128)}), f32[32,1,128]{2,1,0:T(1,128)S(1)}, u32[]{:S(2)}, u32[]{:S(2)}) async-start(f32[32,1,128]{2,1,0:T(1,128)} %broadcast_in_dim.32), calls=%async_computation | async-start | bytes 32768 | tf_op jit(solution)/shard_map/all_to_all | solution.py:206
  17.4 29.8 %all-to-all-start.2 = ((f32[2,64,512]{2,0,1:T(2,128)}), f32[2,64,512]{2,0,1:T(2,128)S(1)}, u32[]{:S(2)}, u32[]{:S(2)}) async-start(f32[2,64,512]{2,0,1:T(2,128)} %copy.37), calls=%async_computation.2 | async-start | bytes 524288 | tf_op jit(solution)/shard_map/all_to_all | solution.py:216
  22.7 3.6 %collective-permute-start = (f32[256]{0:T(256)S(1)}, f32[256]{0:T(256)S(1)}, u32[]{:S(2)}, u32[]{:S(2)}) collective-permute-start(f32[256]{0:T(256)S(1)} %dynamic-slice_subtract_fusion.5), channel_id=1, source_target_pairs={{0,1},{1,0},{2,3},{3,2},{4,5},{5,4},{6,7},{7,6},{8,9},{9,8},{10,11... | collective-permute-start | bytes 3080 | tf_op jit(solution)/shard_map/ppermute | solution.py:119
  26.7 3.6 %collective-permute-start.1 = (f32[256]{0:T(256)S(1)}, f32[256]{0:T(256)S(1)}, u32[]{:S(2)}, u32[]{:S(2)}) collective-permute-start(f32[256]{0:T(256)S(1)} %dynamic-slice_subtract_fusion.4), channel_id=1, source_target_pairs={{0,1},{1,0},{2,3},{3,2},{4,5},{5,4},{6,7},{7,6},{8,9},{9,8},{10,11... | collective-permute-start | bytes 3080 | tf_op jit(solution)/shard_map/ppermute | solution.py:119
  30.7 3.6 %collective-permute-start.2 = (f32[256]{0:T(256)S(1)}, f32[256]{0:T(256)S(1)}, u32[]{:S(2)}, u32[]{:S(2)}) collective-permute-start(f32[256]{0:T(256)S(1)} %dynamic-slice_subtract_fusion.3), channel_id=1, source_target_pairs={{0,1},{1,0},{2,3},{3,2},{4,5},{5,4},{6,7},{7,6},{8,9},{9,8},{10,11... | collective-permute-start | bytes 3080 | tf_op jit(solution)/shard_map/ppermute | solution.py:119
  34.9 3.6 %collective-permute-start.3 = (f32[512]{0:T(512)S(1)}, f32[512]{0:T(512)S(1)}, u32[]{:S(2)}, u32[]{:S(2)}) collective-permute-start(f32[512]{0:T(512)S(1)} %pad_maximum_fusion.5), channel_id=1, source_target_pairs={{0,1},{1,0},{2,3},{3,2},{4,5},{5,4},{6,7},{7,6},{8,9},{9,8},{10,11... | collective-permute-start | bytes 6152 | tf_op jit(solution)/shard_map/ppermute | solution.py:119
  38.9 3.6 %collective-permute-start.4 = (f32[512]{0:T(512)S(1)}, f32[512]{0:T(512)S(1)}, u32[]{:S(2)}, u32[]{:S(2)}) collective-permute-start(f32[512]{0:T(512)S(1)} %pad_maximum_fusion.6), channel_id=1, source_target_pairs={{0,1},{1,0},{2,3},{3,2},{4,5},{5,4},{6,7},{7,6},{8,9},{9,8},{10,11... | collective-permute-start | bytes 6152 | tf_op jit(solution)/shard_map/ppermute | solution.py:119
  42.9 3.7 %collective-permute-start.5 = (f32[1024]{0:T(1024)S(1)}, f32[1024]{0:T(1024)S(1)}, u32[]{:S(2)}, u32[]{:S(2)}) collective-permute-start(f32[1024]{0:T(1024)S(1)} %pad_maximum_fusion.3), channel_id=1, source_target_pairs={{0,1},{1,0},{2,3},{3,2},{4,5},{5,4},{6,7},{7,6},{8,9},{9,8},{10,11... | collective-permute-start | bytes 12296 | tf_op jit(solution)/shard_map/ppermute | solution.py:119
  47.2 12.3 %all-to-all-start.1 = ((f32[2,2,64,512]{3,1,0,2:T(2,128)}), f32[2,2,64,512]{3,1,0,2:T(2,128)S(1)}, u32[]{:S(2)}, u32[]{:S(2)}) async-start(f32[2,2,64,512]{3,1,0,2:T(2,128)} %copy.34), calls=%async_computation.1 | async-start | bytes 1048576 | tf_op jit(solution)/shard_map/all_to_all | solution.py:214
  60.0 5.1 %collective-permute-start.8 = (f32[8,16,1]{2,1,0:T(8,128)S(1)}, f32[8,16,1]{2,1,0:T(8,128)S(1)}, u32[]{:S(2)}, u32[]{:S(2)}) collective-permute-start(f32[8,16,1]{2,1,0:T(8,128)S(1)} %slice_select_fusion.5), channel_id=1, source_target_pairs={{0,1},{1,0},{2,3},{3,2},{4,5},{5,4},{6,7},{7,6},{8,9},{9,8},{10,11... | collective-permute-start | bytes 1544 | tf_op jit(solution)/shard_map/ppermute | solution.py:46
  60.7 4.4 %collective-permute-start.6 = (f32[8,1,512]{2,1,0:T(1,128)S(1)}, f32[8,1,512]{2,1,0:T(1,128)S(1)}, u32[]{:S(2)}, u32[]{:S(2)}) collective-permute-start(f32[8,1,512]{2,1,0:T(1,128)S(1)} %get-tuple-element.71), channel_id=1, source_target_pairs={{8,0},{16,8},{24,16},{2,24},{10,2},{18,10},{26,18},{4,26},{12,4},{... | collective-permute-start | bytes 49160 | tf_op jit(solution)/shard_map/ppermute | solution.py:50
  62.0 3.9 %collective-permute-start.7 = (f32[8,1,512]{2,1,0:T(1,128)S(1)}, f32[8,1,512]{2,1,0:T(1,128)S(1)}, u32[]{:S(2)}, u32[]{:S(2)}) collective-permute-start(f32[8,1,512]{2,1,0:T(1,128)S(1)} %get-tuple-element.70), channel_id=1, source_target_pairs={{0,8},{8,16},{16,24},{24,2},{2,10},{10,18},{18,26},{26,4},{4,12},{... | collective-permute-start | bytes 49160 | tf_op jit(solution)/shard_map/ppermute | solution.py:49
  66.8 5.0 %collective-permute-start.11 = (f32[8,16,1]{2,1,0:T(8,128)S(1)}, f32[8,16,1]{2,1,0:T(8,128)S(1)}, u32[]{:S(2)}, u32[]{:S(2)}) collective-permute-start(f32[8,16,1]{2,1,0:T(8,128)S(1)} %slice_select_fusion.4), channel_id=1, source_target_pairs={{0,1},{1,0},{2,3},{3,2},{4,5},{5,4},{6,7},{7,6},{8,9},{9,8},{10,11... | collective-permute-start | bytes 1544 | tf_op jit(solution)/shard_map/ppermute | solution.py:46
  70.4 5.2 %collective-permute-start.9 = (f32[8,1,512]{2,1,0:T(1,128)S(1)}, f32[8,1,512]{2,1,0:T(1,128)S(1)}, u32[]{:S(2)}, u32[]{:S(2)}) collective-permute-start(f32[8,1,512]{2,1,0:T(1,128)S(1)} %get-tuple-element.64), channel_id=1, source_target_pairs={{8,0},{16,8},{24,16},{2,24},{10,2},{18,10},{26,18},{4,26},{12,4},{... | collective-permute-start | bytes 49160 | tf_op jit(solution)/shard_map/ppermute | solution.py:50
  76.4 6.1 %collective-permute-start.14 = (f32[8,16,1]{2,1,0:T(8,128)S(1)}, f32[8,16,1]{2,1,0:T(8,128)S(1)}, u32[]{:S(2)}, u32[]{:S(2)}) collective-permute-start(f32[8,16,1]{2,1,0:T(8,128)S(1)} %slice_select_fusion.3), channel_id=1, source_target_pairs={{0,1},{1,0},{2,3},{3,2},{4,5},{5,4},{6,7},{7,6},{8,9},{9,8},{10,11... | collective-permute-start | bytes 1544 | tf_op jit(solution)/shard_map/ppermute | solution.py:46
  77.1 5.4 %collective-permute-start.13 = (f32[8,1,512]{2,1,0:T(1,128)S(1)}, f32[8,1,512]{2,1,0:T(1,128)S(1)}, u32[]{:S(2)}, u32[]{:S(2)}) collective-permute-start(f32[8,1,512]{2,1,0:T(1,128)S(1)} %get-tuple-element.57), channel_id=1, source_target_pairs={{0,8},{8,16},{16,24},{24,2},{2,10},{10,18},{18,26},{26,4},{4,12},{... | collective-permute-start | bytes 49160 | tf_op jit(solution)/shard_map/ppermute | solution.py:49
  85.9 8.3 %collective-permute-start.17 = (f32[8,16,1]{2,1,0:T(8,128)S(1)}, f32[8,16,1]{2,1,0:T(8,128)S(1)}, u32[]{:S(2)}, u32[]{:S(2)}) collective-permute-start(f32[8,16,1]{2,1,0:T(8,128)S(1)} %slice_select_fusion.2), channel_id=1, source_target_pairs={{0,1},{1,0},{2,3},{3,2},{4,5},{5,4},{6,7},{7,6},{8,9},{9,8},{10,11... | collective-permute-start | bytes 1544 | tf_op jit(solution)/shard_map/ppermute | solution.py:46
  87.4 6.8 %collective-permute-start.16 = (f32[8,1,512]{2,1,0:T(1,128)S(1)}, f32[8,1,512]{2,1,0:T(1,128)S(1)}, u32[]{:S(2)}, u32[]{:S(2)}) collective-permute-start(f32[8,1,512]{2,1,0:T(1,128)S(1)} %get-tuple-element.49), channel_id=1, source_target_pairs={{0,8},{8,16},{16,24},{24,2},{2,10},{10,18},{18,26},{26,4},{4,12},{... | collective-permute-start | bytes 49160 | tf_op jit(solution)/shard_map/ppermute | solution.py:49
  100.5 13.3 %all-to-all-start.4 = ((f32[32,1,32]{2,1,0:T(1,128)}), f32[32,1,32]{2,1,0:T(1,128)}, u32[]{:S(2)}, u32[]{:S(2)}) async-start(f32[32,1,32]{2,1,0:T(1,128)} %broadcast_in_dim.40), calls=%async_computation.4 | async-start | bytes 32768 | tf_op jit(solution)/shard_map/all_to_all | solution.py:107
  107.3 9.3 %collective-permute-start.20 = (f32[8,16,1]{2,1,0:T(8,128)}, f32[8,16,1]{2,1,0:T(8,128)S(1)}, u32[]{:S(2)}, u32[]{:S(2)}) collective-permute-start(f32[8,16,1]{2,1,0:T(8,128)} %slice_select_fusion.1), channel_id=1, source_target_pairs={{0,1},{1,0},{2,3},{3,2},{4,5},{5,4},{6,7},{7,6},{8,9},{9,8},{10,11... | collective-permute-start | bytes 1544 | tf_op jit(solution)/shard_map/ppermute | solution.py:46
  109.0 18.8 %collective-permute-start.19 = (f32[8,1,512]{2,1,0:T(1,128)}, f32[8,1,512]{2,1,0:T(1,128)S(1)}, u32[]{:S(2)}, u32[]{:S(2)}) collective-permute-start(f32[8,1,512]{2,1,0:T(1,128)} %get-tuple-element.41), channel_id=1, source_target_pairs={{0,8},{8,16},{16,24},{24,2},{2,10},{10,18},{18,26},{26,4},{4,12},{... | collective-permute-start | bytes 49160 | tf_op jit(solution)/shard_map/ppermute | solution.py:49
  110.8 17.1 %collective-permute-start.18 = (f32[8,1,512]{2,1,0:T(1,128)S(1)}, f32[8,1,512]{2,1,0:T(1,128)}, u32[]{:S(2)}, u32[]{:S(2)}) collective-permute-start(f32[8,1,512]{2,1,0:T(1,128)S(1)} %get-tuple-element.40), channel_id=1, source_target_pairs={{8,0},{16,8},{24,16},{2,24},{10,2},{18,10},{26,18},{4,26},{12,4},{... | collective-permute-start | bytes 49160 | tf_op jit(solution)/shard_map/ppermute | solution.py:50
  116.0 3.6 %collective-permute-start.24 = (f32[256]{0:T(256)S(1)}, f32[256]{0:T(256)S(1)}, u32[]{:S(2)}, u32[]{:S(2)}) collective-permute-start(f32[256]{0:T(256)S(1)} %dynamic-slice_subtract_fusion.2), channel_id=1, source_target_pairs={{0,1},{1,0},{2,3},{3,2},{4,5},{5,4},{6,7},{7,6},{8,9},{9,8},{10,11... | collective-permute-start | bytes 3080 | tf_op jit(solution)/shard_map/ppermute | solution.py:119
  120.0 3.6 %collective-permute-start.25 = (f32[256]{0:T(256)S(1)}, f32[256]{0:T(256)S(1)}, u32[]{:S(2)}, u32[]{:S(2)}) collective-permute-start(f32[256]{0:T(256)S(1)} %dynamic-slice_subtract_fusion.1), channel_id=1, source_target_pairs={{0,1},{1,0},{2,3},{3,2},{4,5},{5,4},{6,7},{7,6},{8,9},{9,8},{10,11... | collective-permute-start | bytes 3080 | tf_op jit(solution)/shard_map/ppermute | solution.py:119
  124.0 3.6 %collective-permute-start.26 = (f32[256]{0:T(256)S(1)}, f32[256]{0:T(256)S(1)}, u32[]{:S(2)}, u32[]{:S(2)}) collective-permute-start(f32[256]{0:T(256)S(1)} %dynamic-slice_subtract_fusion), channel_id=1, source_target_pairs={{0,1},{1,0},{2,3},{3,2},{4,5},{5,4},{6,7},{7,6},{8,9},{9,8},{10,11... | collective-permute-start | bytes 3080 | tf_op jit(solution)/shard_map/ppermute | solution.py:119
  129.8 5.1 %collective-permute-start.23 = (f32[8,16,1]{2,1,0:T(8,128)S(1)}, f32[8,16,1]{2,1,0:T(8,128)S(1)}, u32[]{:S(2)}, u32[]{:S(2)}) collective-permute-start(f32[8,16,1]{2,1,0:T(8,128)S(1)} %slice_select_fusion), channel_id=1, source_target_pairs={{0,1},{1,0},{2,3},{3,2},{4,5},{5,4},{6,7},{7,6},{8,9},{9,8},{10,11... | collective-permute-start | bytes 1544 | tf_op jit(solution)/shard_map/ppermute | solution.py:46
  130.5 4.4 %collective-permute-start.21 = (f32[8,1,512]{2,1,0:T(1,128)S(1)}, f32[8,1,512]{2,1,0:T(1,128)S(1)}, u32[]{:S(2)}, u32[]{:S(2)}) collective-permute-start(f32[8,1,512]{2,1,0:T(1,128)S(1)} %get-tuple-element.33), channel_id=1, source_target_pairs={{8,0},{16,8},{24,16},{2,24},{10,2},{18,10},{26,18},{4,26},{12,4},{... | collective-permute-start | bytes 49160 | tf_op jit(solution)/shard_map/ppermute | solution.py:50
  131.8 3.9 %collective-permute-start.22 = (f32[8,1,512]{2,1,0:T(1,128)S(1)}, f32[8,1,512]{2,1,0:T(1,128)S(1)}, u32[]{:S(2)}, u32[]{:S(2)}) collective-permute-start(f32[8,1,512]{2,1,0:T(1,128)S(1)} %get-tuple-element.32), channel_id=1, source_target_pairs={{0,8},{8,16},{16,24},{24,2},{2,10},{10,18},{18,26},{26,4},{4,12},{... | collective-permute-start | bytes 49160 | tf_op jit(solution)/shard_map/ppermute | solution.py:49
  136.5 3.6 %collective-permute-start.27 = (f32[512]{0:T(512)S(1)}, f32[512]{0:T(512)S(1)}, u32[]{:S(2)}, u32[]{:S(2)}) collective-permute-start(f32[512]{0:T(512)S(1)} %pad_maximum_fusion.7), channel_id=1, source_target_pairs={{0,1},{1,0},{2,3},{3,2},{4,5},{5,4},{6,7},{7,6},{8,9},{9,8},{10,11... | collective-permute-start | bytes 6152 | tf_op jit(solution)/shard_map/ppermute | solution.py:119
  140.5 7.9 %collective-permute-start.28 = (f32[512]{0:T(512)S(1)}, f32[512]{0:T(512)S(1)}, u32[]{:S(2)}, u32[]{:S(2)}) collective-permute-start(f32[512]{0:T(512)S(1)} %pad_maximum_fusion.8), channel_id=1, source_target_pairs={{0,1},{1,0},{2,3},{3,2},{4,5},{5,4},{6,7},{7,6},{8,9},{9,8},{10,11... | collective-permute-start | bytes 6152 | tf_op jit(solution)/shard_map/ppermute | solution.py:119
  142.8 14.4 %all-to-all-start.3 = ((f32[2,8,16,512]{3,2,0,1:T(8,128)}), f32[2,8,16,512]{3,2,0,1:T(8,128)S(1)}, u32[]{:S(2)}, u32[]{:S(2)}) async-start(f32[2,8,16,512]{3,2,0,1:T(8,128)} %pad_maximum_fusion.1), calls=%async_computation.3 | async-start | bytes 1048576 | tf_op jit(solution)/shard_map/all_to_all | solution.py:279
  148.7 3.7 %collective-permute-start.29 = (f32[1024]{0:T(1024)S(1)}, f32[1024]{0:T(1024)S(1)}, u32[]{:S(2)}, u32[]{:S(2)}) collective-permute-start(f32[1024]{0:T(1024)S(1)} %pad_maximum_fusion.4), channel_id=1, source_target_pairs={{0,1},{1,0},{2,3},{3,2},{4,5},{5,4},{6,7},{7,6},{8,9},{9,8},{10,11... | collective-permute-start | bytes 12296 | tf_op jit(solution)/shard_map/ppermute | solution.py:119
  (24 other events, 238.4 us)

commit v15 on v13

--- a/solution.py
+++ b/solution.py
@@ -155,6 +155,42 @@
     return jnp.stack(results)
 
 
+def coarse_rows(rhs, pivots, coupling, tie=None):
+    share = pivots.shape[1]
+    low = lax.axis_index("col") == 0
+    start = lax.axis_index("col") * share
+    own = lambda vector: lax.dynamic_slice_in_dim(vector, start, share)
+    forward = [rhs[0]]
+    for section in range(1, NPANEL):
+        forward.append(rhs[section] - jnp.dot(coupling[section - 1], forward[-1], precision=solve_precision))
+    scaled = [jnp.dot(pivots[section], forward[section], precision=solve_precision) for section in range(NPANEL)]
+    results = [None] * NPANEL
+    mine = scaled[NPANEL - 1]
+    if tie is not None:
+        mine, _ = lax.optimization_barrier((mine, tie))
+    for section in range(NPANEL - 2, 0, -1):
+        later = join_halves(mine, swap_col(mine), low)
+        results[section + 1] = later
+        mine = scaled[section] - own(jnp.dot(later, coupling[section], precision=solve_precision))
+    got = swap_col(jnp.concatenate([mine, scaled[0]]))
+    results[1] = join_halves(mine, got[:share], low)
+    first = join_halves(scaled[0], got[share:], low)
+    results[0] = first - jnp.dot(results[1], coupling[0], precision=solve_precision)
+    return jnp.stack(results)
+
+
+def whole_coupling(coupling):
+    layers = lax.axis_size("layer")
+    quarter = coupling.shape[1] // 2
+    core = lax.axis_index("layer") % 2
+    piece = lax.dynamic_slice_in_dim(coupling, core * quarter, quarter, 1)
+    first = swap_col(piece)
+    second = lax.ppermute(first, "layer", [(i, i ^ 1) for i in range(layers)])
+    other = jnp.where(core == 0, jnp.concatenate([first, second], 1), jnp.concatenate([second, first], 1))
+    low = lax.axis_index("col") == 0
+    return jnp.where(low, jnp.concatenate([coupling, other], 1), jnp.concatenate([other, coupling], 1))
+
+
 def coarse_general(rhs, pivots, coupling):
     share = pivots.shape[1]
     start = lax.axis_index("col") * share
@@ -196,6 +232,9 @@
         + (lax.axis_index("col") * given_cols + jnp.arange(given_cols, dtype=jnp.int32))[None, :]
     ).reshape(-1)
     given_pick = (given_ids[:, None] == port_tile.reshape(-1)[None, :]).astype(jnp.float32)
+    split_coupling = lax.axis_size("col") == 2 and layer_count % 2 == 0 and coupling.shape[1] % 2 == 0
+    if split_coupling:
+        full_coupling = whole_coupling(coupling)
     packed = lax.all_to_all(jnp.stack((conduct, vertical)), "layer", 2, 1, tiled=True)
     conduct, vertical = packed[0], packed[1]
     sources = lax.all_to_all(sources, "layer", 1, 0, tiled=True)
@@ -249,7 +288,9 @@
         tiles = plane.reshape(own_rows, TILE, own_cols, TILE).sum(axis=(1, 3)).reshape(-1)
         rhs = share_tiles(tiles, own_rows, own_cols, flat_tiles).reshape(NPANEL, PANEL) * (restrict_scale / TILE)
         total = smooth(resid, weights, pad_term, inverse)
-        if col_count == 2:
+        if split_coupling:
+            ports = coarse_rows(rhs, pivots, full_coupling, total if outer == ITERS - 1 and drop is not None else None)
+        elif col_count == 2 and outer == ITERS - 1 and drop is not None:
             ports = coarse_pair(rhs, pivots, coupling, total)
         else:
             ports = coarse(rhs, pivots, coupling)

time: 159 us -> 172 us (1.082)
  other arithmetic: 14.8 us -> 19.4 us
  local copies, waits for them, and re-layouts: 16.6 us -> 21.2 us
  matrix products: 12 us -> 14.1 us
    ppermute x12 -> x7, waiting for transfers between devices: 24.1 us -> 14.3 us  [swap_col(): return lax.ppermute(value, 'col', [(0, 1), (1, 0)])]
    all_to_all x2, waiting for transfers between devices: 5.65 us -> 13 us  [share_tiles(): got = lax.all_to_all(payload, ('layer', 'row', 'col'), 0, 0, tiled=True)]
    all_to_all x1, waiting for transfers between devices: 0.01 us -> 6.56 us  [shards(): lax.all_to_all(jnp.stack((conduct, vertical)), 'layer', 2, 1, tiled=True)]
    ppermute x6, waiting for transfers between devices: 5.5 us -> 9.31 us  [rims(): lax.ppermute(head, axis, [(place[i + 1], place[i]) for i in range(count -...]
    ppermute x12 -> x7, starting transfers between devices: 10 us -> 6.67 us  [swap_col(): return lax.ppermute(value, 'col', [(0, 1), (1, 0)])]
    all_to_all x1, waiting for transfers between devices: 3.32 us -> 0.01 us  [shards(): sources = lax.all_to_all(sources, 'layer', 1, 0, tiled=True)]
    ppermute x6, waiting for transfers between devices: 4.58 us -> 1.28 us  [rims(): got = lax.ppermute(jnp.where(low, tail, head), axis, [(0, 1), (1, 0)])]
    ppermute x6, starting transfers between devices: 20.1 us -> 17.3 us  [rims(): lax.ppermute(tail, axis, [(place[i], place[i + 1]) for i in range(count -...]
  transfers between devices with their start and end apart: 35 -> 31, of which waited for: 19 -> 15; matrix products, arithmetic and copies ran while one was open for 15% -> 24% of each run, Pallas kernels for 0% -> 0%
where the time goes in v15:
time: 172 us; the launch traced here: 170 us
  starting transfers between devices  64.3 us (37%)
  waiting for transfers between devices  49 us (28%)
  local copies, waits for them, and re-layouts  21.2 us (12%)
  other arithmetic  19.4 us (11%)
  matrix products  14.1 us (8%)
  between operations  1.84 us (1%)
    ppermute x6, starting transfers between devices, rims(): lax.ppermute(tail, axis, [(place[i], place[i + 1]) for i in range(count -...  17.3 us
    ppermute x7, waiting for transfers between devices, swap_col(): return lax.ppermute(value, 'col', [(0, 1), (1, 0)])  14.3 us
    all_to_all x2, waiting for transfers between devices, share_tiles(): got = lax.all_to_all(payload, ('layer', 'row', 'col'), 0, 0, tiled=True)  13 us
    all_to_all x2, starting transfers between devices, share_tiles(): got = lax.all_to_all(payload, ('layer', 'row', 'col'), 0, 0, tiled=True)  11.6 us
    ppermute x6, waiting for transfers between devices, rims(): lax.ppermute(head, axis, [(place[i + 1], place[i]) for i in range(count -...  9.31 us
    ppermute x6, starting transfers between devices, rims(): lax.ppermute(head, axis, [(place[i + 1], place[i]) for i in range(count -...  7.74 us
    ppermute x7, starting transfers between devices, swap_col(): return lax.ppermute(value, 'col', [(0, 1), (1, 0)])  6.67 us
    all_to_all x1, waiting for transfers between devices, shards(): lax.all_to_all(jnp.stack((conduct, vertical)), 'layer', 2, 1, tiled=True)  6.56 us
  transfers between devices with their start and end apart: 31, of which 15 were waited for; matrix products, arithmetic and copies ran while one was open for 24% of the time, Pallas kernels for 0%

profile of v15, /device:TPU:0, one launch (start us, length us, event | category | flops | bytes accessed | tf_op | source)
XLA Modules:
  0.0 169.9 jit_solution(3282477542165894085)
XLA Ops:
  0.6 1.9 %copy.34 = f32[2,64,512]{2,0,1:T(2,128)} copy(f32[2,64,512]{2,1,0:T(8,128)} %param.8) | data formatting | bytes 524288 | tf_op args[0]
  2.5 4.2 %all-to-all-start = ((f32[2,64,512]{2,0,1:T(2,128)}), f32[2,64,512]{2,0,1:T(2,128)S(1)}, u32[]{:S(2)}, u32[]{:S(2)}) async-start(f32[2,64,512]{2,0,1:T(2,128)} %copy.34), calls=%async_computation | async-start | bytes 524288 | tf_op jit(solution)/shard_map/all_to_all | solution.py:240
  6.8 2.1 %constant_dynamic-slice_fusion = f32[3,128,512]{2,1,0:T(8,128)} fusion(f32[3,256,512]{2,1,0:T(8,128)} %param.15, s32[]{:T(128)S(6)} %select_n.296), kind=kLoop, calls=%fused_computation.273 | loop fusion | bytes 1572868 | tf_op jit(solution)/shard_map/dynamic_slice | solution.py:186
  8.8 2.2 %collective-permute-start = (f32[3,128,512]{2,1,0:T(8,128)}, f32[3,128,512]{2,1,0:T(8,128)}, u32[]{:S(2)}, u32[]{:S(2)}) collective-permute-start(f32[3,128,512]{2,1,0:T(8,128)} %constant_dynamic-slice_fusion), channel_id=1, source_target_pairs={{0,1},{1,0},{2,3},{3,2},{4,5},{5,4},{6,7},{7,6},{8,9},{9,8},{10,11... | collective-permute-start | bytes 2359304 | tf_op jit(solution)/shard_map/ppermute | solution.py:119
  14.7 5.4 %all-to-all-start.1 = ((f32[32,1,32]{2,1,0:T(1,128)}), f32[32,1,32]{2,1,0:T(1,128)S(1)}, u32[]{:S(2)}, u32[]{:S(2)}) async-start(f32[32,1,32]{2,1,0:T(1,128)} %broadcast_in_dim.29), calls=%async_computation.1 | async-start | bytes 32768 | tf_op jit(solution)/shard_map/all_to_all | solution.py:107
  22.1 7.5 %all-to-all-done.1 = f32[32,1,32]{2,1,0:T(1,128)S(1)} async-done(((f32[32,1,32]{2,1,0:T(1,128)}), f32[32,1,32]{2,1,0:T(1,128)S(1)}, u32[]{:S(2)}, u32[]{:S(2)}) %all-to-all-start.1) | async-done | bytes 4128 | tf_op jit(solution)/shard_map/all_to_all | solution.py:107
  29.7 3.5 %all-to-all-start.2 = ((f32[2,2,64,512]{3,1,0,2:T(2,128)}), f32[2,2,64,512]{3,1,0,2:T(2,128)S(1)}, u32[]{:S(2)}, u32[]{:S(2)}) async-start(f32[2,2,64,512]{3,1,0,2:T(2,128)} %copy.35), calls=%async_computation.2 | async-start | bytes 1048576 | tf_op jit(solution)/shard_map/all_to_all | solution.py:238
  35.4 6.6 %all-to-all-done.2 = f32[2,2,64,512]{3,1,0,2:T(2,128)S(1)} async-done(((f32[2,2,64,512]{3,1,0,2:T(2,128)}), f32[2,2,64,512]{3,1,0,2:T(2,128)S(1)}, u32[]{:S(2)}, u32[]{:S(2)}) %all-to-all-start.2) | async-done | bytes 524320 | tf_op jit(solution)/shard_map/all_to_all | solution.py:238
  42.4 1.8 %collective-permute-start.7 = (f32[8,16,1]{2,1,0:T(8,128)S(1)}, f32[8,16,1]{2,1,0:T(8,128)S(1)}, u32[]{:S(2)}, u32[]{:S(2)}) collective-permute-start(f32[8,16,1]{2,1,0:T(8,128)S(1)} %slice_select_fusion.5), channel_id=1, source_target_pairs={{0,1},{1,0},{2,3},{3,2},{4,5},{5,4},{6,7},{7,6},{8,9},{9,8},{10,11... | collective-permute-start | bytes 1544 | tf_op jit(solution)/shard_map/ppermute | solution.py:46
  45.6 3.0 %collective-permute-start.6 = (f32[8,1,512]{2,1,0:T(1,128)S(1)}, f32[8,1,512]{2,1,0:T(1,128)S(1)}, u32[]{:S(2)}, u32[]{:S(2)}) collective-permute-start(f32[8,1,512]{2,1,0:T(1,128)S(1)} %get-tuple-element.66), channel_id=1, source_target_pairs={{0,8},{8,16},{16,24},{24,2},{2,10},{10,18},{18,26},{26,4},{4,12},{... | collective-permute-start | bytes 49160 | tf_op jit(solution)/shard_map/ppermute | solution.py:49
  50.8 2.2 %collective-permute-start.9 = (f32[8,1,512]{2,1,0:T(1,128)S(1)}, f32[8,1,512]{2,1,0:T(1,128)S(1)}, u32[]{:S(2)}, u32[]{:S(2)}) collective-permute-start(f32[8,1,512]{2,1,0:T(1,128)S(1)} %get-tuple-element.61), channel_id=1, source_target_pairs={{0,8},{8,16},{16,24},{24,2},{2,10},{10,18},{18,26},{26,4},{4,12},{... | collective-permute-start | bytes 49160 | tf_op jit(solution)/shard_map/ppermute | solution.py:49
  55.0 3.1 %collective-permute-done.8 = f32[8,1,512]{2,1,0:T(1,128)S(1)} collective-permute-done((f32[8,1,512]{2,1,0:T(1,128)S(1)}, f32[8,1,512]{2,1,0:T(1,128)S(1)}, u32[]{:S(2)}, u32[]{:S(2)}) %collective-permute-start.8) | collective-permute-done | bytes 16416 | tf_op jit(solution)/shard_map/ppermute | solution.py:50
  61.1 2.5 %collective-permute-start.1 = (f32[3,128,512]{2,1,0:T(8,128)}, f32[3,128,512]{2,1,0:T(8,128)S(1)}, u32[]{:S(2)}, u32[]{:S(2)}) collective-permute-start(f32[3,128,512]{2,1,0:T(8,128)} %collective-permute-done), channel_id=1, source_target_pairs={{0,8},{8,0},{16,24},{24,16},{1,9},{9,1},{17,25},{25,17},{2,10},{10... | collective-permute-start | bytes 2359304 | tf_op jit(solution)/shard_map/ppermute | solution.py:188
  63.6 1.8 %collective-permute-start.13 = (f32[8,16,1]{2,1,0:T(8,128)S(1)}, f32[8,16,1]{2,1,0:T(8,128)S(1)}, u32[]{:S(2)}, u32[]{:S(2)}) collective-permute-start(f32[8,16,1]{2,1,0:T(8,128)S(1)} %slice_select_fusion.3), channel_id=1, source_target_pairs={{0,1},{1,0},{2,3},{3,2},{4,5},{5,4},{6,7},{7,6},{8,9},{9,8},{10,11... | collective-permute-start | bytes 1544 | tf_op jit(solution)/shard_map/ppermute | solution.py:46
  66.9 2.2 %collective-permute-start.12 = (f32[8,1,512]{2,1,0:T(1,128)}, f32[8,1,512]{2,1,0:T(1,128)}, u32[]{:S(2)}, u32[]{:S(2)}) collective-permute-start(f32[8,1,512]{2,1,0:T(1,128)} %get-tuple-element.53), channel_id=1, source_target_pairs={{0,8},{8,16},{16,24},{24,2},{2,10},{10,18},{18,26},{26,4},{4,12},{... | collective-permute-start | bytes 49160 | tf_op jit(solution)/shard_map/ppermute | solution.py:49
  71.0 1.6 maximum_select_fusion.1
  76.0 3.0 %collective-permute-done.2 = f32[256]{0:T(256)S(1)} collective-permute-done((f32[256]{0:T(256)S(1)}, f32[256]{0:T(256)S(1)}, u32[]{:S(2)}, u32[]{:S(2)}) %collective-permute-start.2) | collective-permute-done | bytes 1056 | tf_op jit(solution)/shard_map/ppermute | solution.py:119
  79.7 3.3 %collective-permute-done.3 = f32[256]{0:T(256)S(1)} collective-permute-done((f32[256]{0:T(256)S(1)}, f32[256]{0:T(256)S(1)}, u32[]{:S(2)}, u32[]{:S(2)}) %collective-permute-start.3) | collective-permute-done | bytes 1056 | tf_op jit(solution)/shard_map/ppermute | solution.py:119
  83.7 3.3 %collective-permute-done.4 = f32[512]{0:T(512)S(1)} collective-permute-done((f32[512]{0:T(512)S(1)}, f32[512]{0:T(512)S(1)}, u32[]{:S(2)}, u32[]{:S(2)}) %collective-permute-start.4) | collective-permute-done | bytes 2080 | tf_op jit(solution)/shard_map/ppermute | solution.py:119
  91.8 3.3 %add_bitcast_fusion = (f32[1,8,16,512]{3,2,0,1:T(8,128)}, f32[8,16,512]{2,1,0:T(8,128)S(1)}) fusion(f32[16,512]{1,0:T(8,128)S(1)} %get-tuple-element.88, f32[8,16,512]{2,1,0:T(8,128)} %copy-done.18, f32[8,16,511]{2,1,0:T(8,128)} %get-tuple-element.55, f32[8,16,1]{2,1,0:T(8,128)} %get-tuple-element.79, f32[8,16,512]{2,1,0:T(8,128)} %copy-done.15, ...), kind=kLoop, calls=%fused_computation.173 | loop fusion | flops 2097152 | bytes 4456448 | tf_op jit(solution)/shard_map/stack | solution.py:302
  95.9 2.8 %collective-permute-start.15 = (f32[8,1,512]{2,1,0:T(1,128)S(1)}, f32[8,1,512]{2,1,0:T(1,128)S(1)}, u32[]{:S(2)}, u32[]{:S(2)}) collective-permute-start(f32[8,1,512]{2,1,0:T(1,128)S(1)} %get-tuple-element.45), channel_id=1, source_target_pairs={{0,8},{8,16},{16,24},{24,2},{2,10},{10,18},{18,26},{26,4},{4,12},{... | collective-permute-start | bytes 49160 | tf_op jit(solution)/shard_map/ppermute | solution.py:49
  100.5 6.2 %collective-permute-done.14 = f32[8,1,512]{2,1,0:T(1,128)S(1)} collective-permute-done((f32[8,1,512]{2,1,0:T(1,128)S(1)}, f32[8,1,512]{2,1,0:T(1,128)S(1)}, u32[]{:S(2)}, u32[]{:S(2)}) %collective-permute-start.14) | collective-permute-done | bytes 16416 | tf_op jit(solution)/shard_map/ppermute | solution.py:50
  113.3 4.1 %collective-permute-start.18 = (f32[8,1,512]{2,1,0:T(1,128)}, f32[8,1,512]{2,1,0:T(1,128)S(1)}, u32[]{:S(2)}, u32[]{:S(2)}) collective-permute-start(f32[8,1,512]{2,1,0:T(1,128)} %get-tuple-element.37), channel_id=1, source_target_pairs={{0,8},{8,16},{16,24},{24,2},{2,10},{10,18},{18,26},{26,4},{4,12},{... | collective-permute-start | bytes 49160 | tf_op jit(solution)/shard_map/ppermute | solution.py:49
  121.3 6.3 %all-to-all-start.4 = ((f32[32,1,32]{2,1,0:T(1,128)}), f32[32,1,32]{2,1,0:T(1,128)S(1)}, u32[]{:S(2)}, u32[]{:S(2)}) async-start(f32[32,1,32]{2,1,0:T(1,128)} %broadcast_in_dim.37), calls=%async_computation.4 | async-start | bytes 32768 | tf_op jit(solution)/shard_map/all_to_all | solution.py:107
  129.0 5.5 %all-to-all-done.4 = f32[32,1,32]{2,1,0:T(1,128)S(1)} async-done(((f32[32,1,32]{2,1,0:T(1,128)}), f32[32,1,32]{2,1,0:T(1,128)S(1)}, u32[]{:S(2)}, u32[]{:S(2)}) %all-to-all-start.4) | async-done | bytes 4128 | tf_op jit(solution)/shard_map/all_to_all | solution.py:107
  134.6 1.7 fusion.1
  140.1 1.6 fusion.149
  144.1 3.0 %collective-permute-start.21 = (f32[8,1,512]{2,1,0:T(1,128)S(1)}, f32[8,1,512]{2,1,0:T(1,128)S(1)}, u32[]{:S(2)}, u32[]{:S(2)}) collective-permute-start(f32[8,1,512]{2,1,0:T(1,128)S(1)} %get-tuple-element.28), channel_id=1, source_target_pairs={{0,8},{8,16},{16,24},{24,2},{2,10},{10,18},{18,26},{26,4},{4,12},{... | collective-permute-start | bytes 49160 | tf_op jit(solution)/shard_map/ppermute | solution.py:49
  150.3 1.9 %collective-permute-done.23 = f32[256]{0:T(256)S(1)} collective-permute-done((f32[256]{0:T(256)S(1)}, f32[256]{0:T(256)S(1)}, u32[]{:S(2)}, u32[]{:S(2)}) %collective-permute-start.23) | collective-permute-done | bytes 1056 | tf_op jit(solution)/shard_map/ppermute | solution.py:119
  154.8 4.3 %all-to-all-start.3 = ((f32[2,8,16,512]{3,2,0,1:T(8,128)}), f32[2,8,16,512]{3,2,0,1:T(8,128)}, u32[]{:S(2)}, u32[]{:S(2)}) async-start(f32[2,8,16,512]{3,2,0,1:T(8,128)} %pad_maximum_fusion.1), calls=%async_computation.3 | async-start | bytes 1048576 | tf_op jit(solution)/shard_map/all_to_all | solution.py:302
  160.2 3.0 %collective-permute-done.25 = f32[512]{0:T(512)S(1)} collective-permute-done((f32[512]{0:T(512)S(1)}, f32[512]{0:T(512)S(1)}, u32[]{:S(2)}, u32[]{:S(2)}) %collective-permute-start.25) | collective-permute-done | bytes 2080 | tf_op jit(solution)/shard_map/ppermute | solution.py:119
  165.1 2.9 %all-to-all-done.3 = f32[2,8,16,512]{3,2,0,1:T(8,128)} async-done(((f32[2,8,16,512]{3,2,0,1:T(8,128)}), f32[2,8,16,512]{3,2,0,1:T(8,128)}, u32[]{:S(2)}, u32[]{:S(2)}) %all-to-all-start.3) | async-done | bytes 524320 | tf_op jit(solution)/shard_map/all_to_all | solution.py:302
  (263 shorter events, 60.5 us)
Async XLA Ops:
  2.5 11.2 %all-to-all-start = ((f32[2,64,512]{2,0,1:T(2,128)}), f32[2,64,512]{2,0,1:T(2,128)S(1)}, u32[]{:S(2)}, u32[]{:S(2)}) async-start(f32[2,64,512]{2,0,1:T(2,128)} %copy.34), calls=%async_computation | async-start | bytes 524288 | tf_op jit(solution)/shard_map/all_to_all | solution.py:240
  8.8 52.2 %collective-permute-start = (f32[3,128,512]{2,1,0:T(8,128)}, f32[3,128,512]{2,1,0:T(8,128)}, u32[]{:S(2)}, u32[]{:S(2)}) collective-permute-start(f32[3,128,512]{2,1,0:T(8,128)} %constant_dynamic-slice_fusion), channel_id=1, source_target_pairs={{0,1},{1,0},{2,3},{3,2},{4,5},{5,4},{6,7},{7,6},{8,9},{9,8},{10,11... | collective-permute-start | bytes 2359304 | tf_op jit(solution)/shard_map/ppermute | solution.py:119
  11.8 75.6 %copy-start.35 = (s32[1,4,4,128]{3,1,2,0:T(4,128)}, s32[1,4,4,128]{3,1,2,0:T(4,128)S(1)}, u32[]{:S(2)}) copy-start(s32[1,4,4,128]{3,1,2,0:T(4,128)S(1)} %copy.45) | copy-start | bytes 24580
  14.7 15.0 %all-to-all-start.1 = ((f32[32,1,32]{2,1,0:T(1,128)}), f32[32,1,32]{2,1,0:T(1,128)S(1)}, u32[]{:S(2)}, u32[]{:S(2)}) async-start(f32[32,1,32]{2,1,0:T(1,128)} %broadcast_in_dim.29), calls=%async_computation.1 | async-start | bytes 32768 | tf_op jit(solution)/shard_map/all_to_all | solution.py:107
  29.7 12.3 %all-to-all-start.2 = ((f32[2,2,64,512]{3,1,0,2:T(2,128)}), f32[2,2,64,512]{3,1,0,2:T(2,128)S(1)}, u32[]{:S(2)}, u32[]{:S(2)}) async-start(f32[2,2,64,512]{3,1,0,2:T(2,128)} %copy.35), calls=%async_computation.2 | async-start | bytes 1048576 | tf_op jit(solution)/shard_map/all_to_all | solution.py:238
  42.4 6.2 %collective-permute-start.7 = (f32[8,16,1]{2,1,0:T(8,128)S(1)}, f32[8,16,1]{2,1,0:T(8,128)S(1)}, u32[]{:S(2)}, u32[]{:S(2)}) collective-permute-start(f32[8,16,1]{2,1,0:T(8,128)S(1)} %slice_select_fusion.5), channel_id=1, source_target_pairs={{0,1},{1,0},{2,3},{3,2},{4,5},{5,4},{6,7},{7,6},{8,9},{9,8},{10,11... | collective-permute-start | bytes 1544 | tf_op jit(solution)/shard_map/ppermute | solution.py:46
  44.3 4.4 %collective-permute-start.5 = (f32[8,1,512]{2,1,0:T(1,128)S(1)}, f32[8,1,512]{2,1,0:T(1,128)S(1)}, u32[]{:S(2)}, u32[]{:S(2)}) collective-permute-start(f32[8,1,512]{2,1,0:T(1,128)S(1)} %get-tuple-element.67), channel_id=1, source_target_pairs={{8,0},{16,8},{24,16},{2,24},{10,2},{18,10},{26,18},{4,26},{12,4},{... | collective-permute-start | bytes 49160 | tf_op jit(solution)/shard_map/ppermute | solution.py:50
  45.6 3.9 %collective-permute-start.6 = (f32[8,1,512]{2,1,0:T(1,128)S(1)}, f32[8,1,512]{2,1,0:T(1,128)S(1)}, u32[]{:S(2)}, u32[]{:S(2)}) collective-permute-start(f32[8,1,512]{2,1,0:T(1,128)S(1)} %get-tuple-element.66), channel_id=1, source_target_pairs={{0,8},{8,16},{16,24},{24,2},{2,10},{10,18},{18,26},{26,4},{4,12},{... | collective-permute-start | bytes 49160 | tf_op jit(solution)/shard_map/ppermute | solution.py:49
  50.4 4.6 %collective-permute-start.10 = (f32[8,16,1]{2,1,0:T(8,128)S(1)}, f32[8,16,1]{2,1,0:T(8,128)S(1)}, u32[]{:S(2)}, u32[]{:S(2)}) collective-permute-start(f32[8,16,1]{2,1,0:T(8,128)S(1)} %slice_select_fusion.4), channel_id=1, source_target_pairs={{0,1},{1,0},{2,3},{3,2},{4,5},{5,4},{6,7},{7,6},{8,9},{9,8},{10,11... | collective-permute-start | bytes 1544 | tf_op jit(solution)/shard_map/ppermute | solution.py:46
  50.8 4.2 %collective-permute-start.9 = (f32[8,1,512]{2,1,0:T(1,128)S(1)}, f32[8,1,512]{2,1,0:T(1,128)S(1)}, u32[]{:S(2)}, u32[]{:S(2)}) collective-permute-start(f32[8,1,512]{2,1,0:T(1,128)S(1)} %get-tuple-element.61), channel_id=1, source_target_pairs={{0,8},{8,16},{16,24},{24,2},{2,10},{10,18},{18,26},{26,4},{4,12},{... | collective-permute-start | bytes 49160 | tf_op jit(solution)/shard_map/ppermute | solution.py:49
  53.0 5.2 %collective-permute-start.8 = (f32[8,1,512]{2,1,0:T(1,128)S(1)}, f32[8,1,512]{2,1,0:T(1,128)S(1)}, u32[]{:S(2)}, u32[]{:S(2)}) collective-permute-start(f32[8,1,512]{2,1,0:T(1,128)S(1)} %get-tuple-element.60), channel_id=1, source_target_pairs={{8,0},{16,8},{24,16},{2,24},{10,2},{18,10},{26,18},{4,26},{12,4},{... | collective-permute-start | bytes 49160 | tf_op jit(solution)/shard_map/ppermute | solution.py:50
  61.1 10.0 %collective-permute-start.1 = (f32[3,128,512]{2,1,0:T(8,128)}, f32[3,128,512]{2,1,0:T(8,128)S(1)}, u32[]{:S(2)}, u32[]{:S(2)}) collective-permute-start(f32[3,128,512]{2,1,0:T(8,128)} %collective-permute-done), channel_id=1, source_target_pairs={{0,8},{8,0},{16,24},{24,16},{1,9},{9,1},{17,25},{25,17},{2,10},{10... | collective-permute-start | bytes 2359304 | tf_op jit(solution)/shard_map/ppermute | solution.py:188
  63.6 6.8 %collective-permute-start.13 = (f32[8,16,1]{2,1,0:T(8,128)S(1)}, f32[8,16,1]{2,1,0:T(8,128)S(1)}, u32[]{:S(2)}, u32[]{:S(2)}) collective-permute-start(f32[8,16,1]{2,1,0:T(8,128)S(1)} %slice_select_fusion.3), channel_id=1, source_target_pairs={{0,1},{1,0},{2,3},{3,2},{4,5},{5,4},{6,7},{7,6},{8,9},{9,8},{10,11... | collective-permute-start | bytes 1544 | tf_op jit(solution)/shard_map/ppermute | solution.py:46
  66.9 24.8 %collective-permute-start.12 = (f32[8,1,512]{2,1,0:T(1,128)}, f32[8,1,512]{2,1,0:T(1,128)}, u32[]{:S(2)}, u32[]{:S(2)}) collective-permute-start(f32[8,1,512]{2,1,0:T(1,128)} %get-tuple-element.53), channel_id=1, source_target_pairs={{0,8},{8,16},{16,24},{24,2},{2,10},{10,18},{18,26},{26,4},{4,12},{... | collective-permute-start | bytes 49160 | tf_op jit(solution)/shard_map/ppermute | solution.py:49
  69.1 22.6 %collective-permute-start.11 = (f32[8,1,512]{2,1,0:T(1,128)}, f32[8,1,512]{2,1,0:T(1,128)}, u32[]{:S(2)}, u32[]{:S(2)}) collective-permute-start(f32[8,1,512]{2,1,0:T(1,128)} %get-tuple-element.52), channel_id=1, source_target_pairs={{8,0},{16,8},{24,16},{2,24},{10,2},{18,10},{26,18},{4,26},{12,4},{... | collective-permute-start | bytes 49160 | tf_op jit(solution)/shard_map/ppermute | solution.py:50
  75.3 3.6 %collective-permute-start.2 = (f32[256]{0:T(256)S(1)}, f32[256]{0:T(256)S(1)}, u32[]{:S(2)}, u32[]{:S(2)}) collective-permute-start(f32[256]{0:T(256)S(1)} %bitcast.227), channel_id=1, source_target_pairs={{0,1},{1,0},{2,3},{3,2},{4,5},{5,4},{6,7},{7,6},{8,9},{9,8},{10,11... | collective-permute-start | bytes 3080 | tf_op jit(solution)/shard_map/ppermute | solution.py:119
  79.4 3.6 %collective-permute-start.3 = (f32[256]{0:T(256)S(1)}, f32[256]{0:T(256)S(1)}, u32[]{:S(2)}, u32[]{:S(2)}) collective-permute-start(f32[256]{0:T(256)S(1)} %dynamic-slice_subtract_fusion.3), channel_id=1, source_target_pairs={{0,1},{1,0},{2,3},{3,2},{4,5},{5,4},{6,7},{7,6},{8,9},{9,8},{10,11... | collective-permute-start | bytes 3080 | tf_op jit(solution)/shard_map/ppermute | solution.py:119
  83.4 3.6 %collective-permute-start.4 = (f32[512]{0:T(512)S(1)}, f32[512]{0:T(512)S(1)}, u32[]{:S(2)}, u32[]{:S(2)}) collective-permute-start(f32[512]{0:T(512)S(1)} %pad_maximum_fusion.4), channel_id=1, source_target_pairs={{0,1},{1,0},{2,3},{3,2},{4,5},{5,4},{6,7},{7,6},{8,9},{9,8},{10,11... | collective-permute-start | bytes 6152 | tf_op jit(solution)/shard_map/ppermute | solution.py:119
  95.5 5.0 %collective-permute-start.16 = (f32[8,16,1]{2,1,0:T(8,128)S(1)}, f32[8,16,1]{2,1,0:T(8,128)S(1)}, u32[]{:S(2)}, u32[]{:S(2)}) collective-permute-start(f32[8,16,1]{2,1,0:T(8,128)S(1)} %slice_select_fusion.2), channel_id=1, source_target_pairs={{0,1},{1,0},{2,3},{3,2},{4,5},{5,4},{6,7},{7,6},{8,9},{9,8},{10,11... | collective-permute-start | bytes 1544 | tf_op jit(solution)/shard_map/ppermute | solution.py:46
  95.9 4.6 %collective-permute-start.15 = (f32[8,1,512]{2,1,0:T(1,128)S(1)}, f32[8,1,512]{2,1,0:T(1,128)S(1)}, u32[]{:S(2)}, u32[]{:S(2)}) collective-permute-start(f32[8,1,512]{2,1,0:T(1,128)S(1)} %get-tuple-element.45), channel_id=1, source_target_pairs={{0,8},{8,16},{16,24},{24,2},{2,10},{10,18},{18,26},{26,4},{4,12},{... | collective-permute-start | bytes 49160 | tf_op jit(solution)/shard_map/ppermute | solution.py:49
  98.7 8.0 %collective-permute-start.14 = (f32[8,1,512]{2,1,0:T(1,128)S(1)}, f32[8,1,512]{2,1,0:T(1,128)S(1)}, u32[]{:S(2)}, u32[]{:S(2)}) collective-permute-start(f32[8,1,512]{2,1,0:T(1,128)S(1)} %get-tuple-element.44), channel_id=1, source_target_pairs={{8,0},{16,8},{24,16},{2,24},{10,2},{18,10},{26,18},{4,26},{12,4},{... | collective-permute-start | bytes 49160 | tf_op jit(solution)/shard_map/ppermute | solution.py:50
  111.1 16.5 %collective-permute-start.19 = (f32[8,16,1]{2,1,0:T(8,128)S(1)}, f32[8,16,1]{2,1,0:T(8,128)}, u32[]{:S(2)}, u32[]{:S(2)}) collective-permute-start(f32[8,16,1]{2,1,0:T(8,128)S(1)} %slice_select_fusion.1), channel_id=1, source_target_pairs={{0,1},{1,0},{2,3},{3,2},{4,5},{5,4},{6,7},{7,6},{8,9},{9,8},{10,11... | collective-permute-start | bytes 1544 | tf_op jit(solution)/shard_map/ppermute | solution.py:46
  113.3 26.7 %collective-permute-start.18 = (f32[8,1,512]{2,1,0:T(1,128)}, f32[8,1,512]{2,1,0:T(1,128)S(1)}, u32[]{:S(2)}, u32[]{:S(2)}) collective-permute-start(f32[8,1,512]{2,1,0:T(1,128)} %get-tuple-element.37), channel_id=1, source_target_pairs={{0,8},{8,16},{16,24},{24,2},{2,10},{10,18},{18,26},{26,4},{4,12},{... | collective-permute-start | bytes 49160 | tf_op jit(solution)/shard_map/ppermute | solution.py:49
  117.4 22.6 %collective-permute-start.17 = (f32[8,1,512]{2,1,0:T(1,128)}, f32[8,1,512]{2,1,0:T(1,128)S(1)}, u32[]{:S(2)}, u32[]{:S(2)}) collective-permute-start(f32[8,1,512]{2,1,0:T(1,128)} %get-tuple-element.36), channel_id=1, source_target_pairs={{8,0},{16,8},{24,16},{2,24},{10,2},{18,10},{26,18},{4,26},{12,4},{... | collective-permute-start | bytes 49160 | tf_op jit(solution)/shard_map/ppermute | solution.py:50
  121.3 13.2 %all-to-all-start.4 = ((f32[32,1,32]{2,1,0:T(1,128)}), f32[32,1,32]{2,1,0:T(1,128)S(1)}, u32[]{:S(2)}, u32[]{:S(2)}) async-start(f32[32,1,32]{2,1,0:T(1,128)} %broadcast_in_dim.37), calls=%async_computation.4 | async-start | bytes 32768 | tf_op jit(solution)/shard_map/all_to_all | solution.py:107
  142.0 5.1 %collective-permute-start.22 = (f32[8,16,1]{2,1,0:T(8,128)S(1)}, f32[8,16,1]{2,1,0:T(8,128)S(1)}, u32[]{:S(2)}, u32[]{:S(2)}) collective-permute-start(f32[8,16,1]{2,1,0:T(8,128)S(1)} %slice_select_fusion), channel_id=1, source_target_pairs={{0,1},{1,0},{2,3},{3,2},{4,5},{5,4},{6,7},{7,6},{8,9},{9,8},{10,11... | collective-permute-start | bytes 1544 | tf_op jit(solution)/shard_map/ppermute | solution.py:46
  142.8 4.4 %collective-permute-start.20 = (f32[8,1,512]{2,1,0:T(1,128)S(1)}, f32[8,1,512]{2,1,0:T(1,128)S(1)}, u32[]{:S(2)}, u32[]{:S(2)}) collective-permute-start(f32[8,1,512]{2,1,0:T(1,128)S(1)} %get-tuple-element.29), channel_id=1, source_target_pairs={{8,0},{16,8},{24,16},{2,24},{10,2},{18,10},{26,18},{4,26},{12,4},{... | collective-permute-start | bytes 49160 | tf_op jit(solution)/shard_map/ppermute | solution.py:50
  144.1 3.9 %collective-permute-start.21 = (f32[8,1,512]{2,1,0:T(1,128)S(1)}, f32[8,1,512]{2,1,0:T(1,128)S(1)}, u32[]{:S(2)}, u32[]{:S(2)}) collective-permute-start(f32[8,1,512]{2,1,0:T(1,128)S(1)} %get-tuple-element.28), channel_id=1, source_target_pairs={{0,8},{8,16},{16,24},{24,2},{2,10},{10,18},{18,26},{26,4},{4,12},{... | collective-permute-start | bytes 49160 | tf_op jit(solution)/shard_map/ppermute | solution.py:49
  148.5 3.6 %collective-permute-start.23 = (f32[256]{0:T(256)S(1)}, f32[256]{0:T(256)S(1)}, u32[]{:S(2)}, u32[]{:S(2)}) collective-permute-start(f32[256]{0:T(256)S(1)} %bitcast.223), channel_id=1, source_target_pairs={{0,1},{1,0},{2,3},{3,2},{4,5},{5,4},{6,7},{7,6},{8,9},{9,8},{10,11... | collective-permute-start | bytes 3080 | tf_op jit(solution)/shard_map/ppermute | solution.py:119
  152.6 6.5 %collective-permute-start.24 = (f32[256]{0:T(256)S(1)}, f32[256]{0:T(256)S(1)}, u32[]{:S(2)}, u32[]{:S(2)}) collective-permute-start(f32[256]{0:T(256)S(1)} %dynamic-slice_subtract_fusion.1), channel_id=1, source_target_pairs={{0,1},{1,0},{2,3},{3,2},{4,5},{5,4},{6,7},{7,6},{8,9},{9,8},{10,11... | collective-permute-start | bytes 3080 | tf_op jit(solution)/shard_map/ppermute | solution.py:119
  154.8 13.2 %all-to-all-start.3 = ((f32[2,8,16,512]{3,2,0,1:T(8,128)}), f32[2,8,16,512]{3,2,0,1:T(8,128)}, u32[]{:S(2)}, u32[]{:S(2)}) async-start(f32[2,8,16,512]{3,2,0,1:T(8,128)} %pad_maximum_fusion.1), calls=%async_computation.3 | async-start | bytes 1048576 | tf_op jit(solution)/shard_map/all_to_all | solution.py:302
  159.5 3.6 %collective-permute-start.25 = (f32[512]{0:T(512)S(1)}, f32[512]{0:T(512)S(1)}, u32[]{:S(2)}, u32[]{:S(2)}) collective-permute-start(f32[512]{0:T(512)S(1)} %pad_maximum_fusion.7), channel_id=1, source_target_pairs={{0,1},{1,0},{2,3},{3,2},{4,5},{5,4},{6,7},{7,6},{8,9},{9,8},{10,11... | collective-permute-start | bytes 6152 | tf_op jit(solution)/shard_map/ppermute | solution.py:119
  (40 other events, 458.6 us)

commit v16 on v12

--- a/solution.py
+++ b/solution.py
@@ -197,6 +197,7 @@
     ).reshape(-1)
     given_pick = (given_ids[:, None] == port_tile.reshape(-1)[None, :]).astype(jnp.float32)
     packed = lax.all_to_all(jnp.stack((conduct, vertical)), "layer", 2, 1, tiled=True)
+    sources, packed = lax.optimization_barrier((sources, packed))
     conduct, vertical = packed[0], packed[1]
     sources = lax.all_to_all(sources, "layer", 1, 0, tiled=True)
     local_layers, grid_rows, grid_cols = sources.shape

time: 157 us -> 171 us (1.089)
  other arithmetic: 11.4 us -> 20.7 us
  local copies, waits for them, and re-layouts: 11.9 us -> 20.1 us
  waiting for transfers between devices: 48.6 us -> 44.3 us
    all_to_all x1, waiting for transfers between devices: 0.01 us -> 5.95 us  [shards(): lax.all_to_all(jnp.stack((conduct, vertical)), 'layer', 2, 1, tiled=True)]
    ppermute x6, starting transfers between devices: 21 us -> 15.5 us  [rims(): lax.ppermute(tail, axis, [(place[i], place[i + 1]) for i in range(count -...]
    all_to_all x2, waiting for transfers between devices: 6.2 us -> 1.49 us  [share_tiles(): got = lax.all_to_all(payload, ('layer', 'row', 'col'), 0, 0, tiled=True)]
    slice x13, local copies, waits for them, and re-layouts: 3.26 us -> 7.93 us  [neighbours(): lax.slice_in_dim(field, 1, size, axis=dim)]
    ppermute x6, waiting for transfers between devices: 4.59 us -> 1.03 us  [rims(): got = lax.ppermute(jnp.where(low, tail, head), axis, [(0, 1), (1, 0)])]
    ppermute x6, starting transfers between devices: 5.9 us -> 8.64 us  [rims(): got = lax.ppermute(jnp.where(low, tail, head), axis, [(0, 1), (1, 0)])]
    unnamed x43 -> x64, local copies, waits for them, and re-layouts: 2.72 us -> 0.16 us
    ppermute x12, waiting for transfers between devices: 26.1 us -> 23.9 us  [swap_col(): return lax.ppermute(value, 'col', [(0, 1), (1, 0)])]
  transfers between devices with their start and end apart: 35 -> 35, of which waited for: 21 -> 18; matrix products, arithmetic and copies ran while one was open for 13% -> 17% of each run, Pallas kernels for 0% -> 0%
where the time goes in v16:
time: 171 us; the launch traced here: 170 us
  starting transfers between devices  69.9 us (41%)
  waiting for transfers between devices  44.3 us (26%)
  other arithmetic  20.7 us (12%)
  local copies, waits for them, and re-layouts  20.1 us (12%)
  matrix products  12.9 us (8%)
    ppermute x12, waiting for transfers between devices, swap_col(): return lax.ppermute(value, 'col', [(0, 1), (1, 0)])  23.9 us
    ppermute x6, starting transfers between devices, rims(): lax.ppermute(tail, axis, [(place[i], place[i + 1]) for i in range(count -...  15.5 us
    all_to_all x2, starting transfers between devices, share_tiles(): got = lax.all_to_all(payload, ('layer', 'row', 'col'), 0, 0, tiled=True)  14.1 us
    ppermute x12, starting transfers between devices, swap_col(): return lax.ppermute(value, 'col', [(0, 1), (1, 0)])  9.5 us
    ppermute x6, starting transfers between devices, rims(): got = lax.ppermute(jnp.where(low, tail, head), axis, [(0, 1), (1, 0)])  8.64 us
    slice x13, local copies, waits for them, and re-layouts, neighbours(): lax.slice_in_dim(field, 1, size, axis=dim)  7.93 us
    ppermute x6, starting transfers between devices, rims(): lax.ppermute(head, axis, [(place[i + 1], place[i]) for i in range(count -...  7.74 us
    all_to_all x1, waiting for transfers between devices, shards(): lax.all_to_all(jnp.stack((conduct, vertical)), 'layer', 2, 1, tiled=True)  5.95 us
  transfers between devices with their start and end apart: 35, of which 18 were waited for; matrix products, arithmetic and copies ran while one was open for 17% of the time, Pallas kernels for 0%

profile of v16, /device:TPU:0, one launch (start us, length us, event | category | flops | bytes accessed | tf_op | source)
XLA Modules:
  0.0 169.5 jit_solution(11882756467312503416)
XLA Ops:
  3.9 4.2 %all-to-all-start = ((f32[2,2,64,512]{3,1,0,2:T(2,128)}), f32[2,2,64,512]{3,1,0,2:T(2,128)S(1)}, u32[]{:S(2)}, u32[]{:S(2)}) async-start(f32[2,2,64,512]{3,1,0,2:T(2,128)} %copy.33), calls=%async_computation | async-start | bytes 1048576 | tf_op jit(solution)/shard_map/all_to_all | solution.py:199
  11.0 6.0 %all-to-all-done = f32[2,2,64,512]{3,1,0,2:T(2,128)S(1)} async-done(((f32[2,2,64,512]{3,1,0,2:T(2,128)}), f32[2,2,64,512]{3,1,0,2:T(2,128)S(1)}, u32[]{:S(2)}, u32[]{:S(2)}) %all-to-all-start) | async-done | bytes 524320 | tf_op jit(solution)/shard_map/all_to_all | solution.py:199
  19.1 2.3 %collective-permute-start.8 = (f32[8,16,1]{2,1,0:T(8,128)S(1)}, f32[8,16,1]{2,1,0:T(8,128)S(1)}, u32[]{:S(2)}, u32[]{:S(2)}) collective-permute-start(f32[8,16,1]{2,1,0:T(8,128)S(1)} %slice_select_fusion.5), channel_id=1, source_target_pairs={{0,1},{1,0},{2,3},{3,2},{4,5},{5,4},{6,7},{7,6},{8,9},{9,8},{10,11... | collective-permute-start | bytes 1544 | tf_op jit(solution)/shard_map/ppermute | solution.py:46
  24.9 5.3 %all-to-all-start.1 = ((f32[2,64,512]{2,0,1:T(2,128)}), f32[2,64,512]{2,0,1:T(2,128)S(1)}, u32[]{:S(2)}, u32[]{:S(2)}) async-start(f32[2,64,512]{2,0,1:T(2,128)} %copy.35), calls=%async_computation.1 | async-start | bytes 524288 | tf_op jit(solution)/shard_map/all_to_all | solution.py:202
  30.8 5.7 %all-to-all-done.1 = f32[2,64,512]{2,0,1:T(2,128)S(1)} async-done(((f32[2,64,512]{2,0,1:T(2,128)}), f32[2,64,512]{2,0,1:T(2,128)S(1)}, u32[]{:S(2)}, u32[]{:S(2)}) %all-to-all-start.1) | async-done | bytes 262176 | tf_op jit(solution)/shard_map/all_to_all | solution.py:202
  36.6 2.6 %bitcast_multiply_fusion = (f32[8,16,512]{2,1,0:T(8,128)S(1)}, f32[8,16,512]{2,1,0:T(8,128)S(1)}, f32[8,16,512]{2,1,0:T(8,128)S(1)}, f32[8,16,512]{2,1,0:T(8,128...) fusion(f32[4,2,16,512]{3,2,1,0:T(8,128)S(1)} %copy.36, ...), kind=kLoop, calls=%fused_computation.186 | loop fusion | flops 1179648 | bytes 4423680 | tf_op jit(solution)/shard_map/mul | solution.py:79
  44.4 5.7 %all-to-all-start.2 = ((f32[32,1,32]{2,1,0:T(1,128)}), f32[32,1,32]{2,1,0:T(1,128)}, u32[]{:S(2)}, u32[]{:S(2)}) async-start(f32[32,1,32]{2,1,0:T(1,128)} %broadcast_in_dim.29), calls=%async_computation.2 | async-start | bytes 32768 | tf_op jit(solution)/shard_map/all_to_all | solution.py:107
  51.5 3.0 %collective-permute-start.10 = (f32[8,1,512]{2,1,0:T(1,128)}, f32[8,1,512]{2,1,0:T(1,128)S(1)}, u32[]{:S(2)}, u32[]{:S(2)}) collective-permute-start(f32[8,1,512]{2,1,0:T(1,128)} %get-tuple-element.65), channel_id=1, source_target_pairs={{0,8},{8,16},{16,24},{24,2},{2,10},{10,18},{18,26},{26,4},{4,12},{... | collective-permute-start | bytes 49160 | tf_op jit(solution)/shard_map/ppermute | solution.py:49
  54.5 1.8 %collective-permute-start.11 = (f32[8,16,1]{2,1,0:T(8,128)S(1)}, f32[8,16,1]{2,1,0:T(8,128)S(1)}, u32[]{:S(2)}, u32[]{:S(2)}) collective-permute-start(f32[8,16,1]{2,1,0:T(8,128)S(1)} %slice_select_fusion.4), channel_id=1, source_target_pairs={{0,1},{1,0},{2,3},{3,2},{4,5},{5,4},{6,7},{7,6},{8,9},{9,8},{10,11... | collective-permute-start | bytes 1544 | tf_op jit(solution)/shard_map/ppermute | solution.py:46
  57.0 1.7 %fusion = f32[2048]{0:T(1024)S(1)} fusion(f32[32,32]{1,0:T(8,128)} %bitcast.5, s32[2048]{0:T(1024)} %get-tuple-element.102, s32[2048]{0:T(1024)S(1)} %get-tuple-element.101), kind=kOutput, calls=%fused_computation.2 | convolution fusion | flops 25425920 | bytes 28672 | tf_op jit(solution)/shard_map/dot_general | solution.py:115
  59.9 2.9 %collective-permute-done = f32[256]{0:T(256)S(1)} collective-permute-done((f32[256]{0:T(256)S(1)}, f32[256]{0:T(256)S(1)}, u32[]{:S(2)}, u32[]{:S(2)}) %collective-permute-start) | collective-permute-done | bytes 1056 | tf_op jit(solution)/shard_map/ppermute | solution.py:119
  65.2 1.6 collective-permute-done.1
  68.3 2.6 %collective-permute-done.2 = f32[256]{0:T(256)S(1)} collective-permute-done((f32[256]{0:T(256)S(1)}, f32[256]{0:T(256)S(1)}, u32[]{:S(2)}, u32[]{:S(2)}) %collective-permute-start.2) | collective-permute-done | bytes 1056 | tf_op jit(solution)/shard_map/ppermute | solution.py:119
  72.5 2.6 %collective-permute-done.3 = f32[512]{0:T(512)S(1)} collective-permute-done((f32[512]{0:T(512)S(1)}, f32[512]{0:T(512)S(1)}, u32[]{:S(2)}, u32[]{:S(2)}) %collective-permute-start.3) | collective-permute-done | bytes 2080 | tf_op jit(solution)/shard_map/ppermute | solution.py:119
  76.2 2.9 %collective-permute-done.4 = f32[512]{0:T(512)S(1)} collective-permute-done((f32[512]{0:T(512)S(1)}, f32[512]{0:T(512)S(1)}, u32[]{:S(2)}, u32[]{:S(2)}) %collective-permute-start.4) | collective-permute-done | bytes 2080 | tf_op jit(solution)/shard_map/ppermute | solution.py:119
  87.4 3.6 %collective-permute-start.13 = (f32[8,1,512]{2,1,0:T(1,128)}, f32[8,1,512]{2,1,0:T(1,128)}, u32[]{:S(2)}, u32[]{:S(2)}) collective-permute-start(f32[8,1,512]{2,1,0:T(1,128)} %get-tuple-element.57), channel_id=1, source_target_pairs={{0,8},{8,16},{16,24},{24,2},{2,10},{10,18},{18,26},{26,4},{4,12},{... | collective-permute-start | bytes 49160 | tf_op jit(solution)/shard_map/ppermute | solution.py:49
  96.1 2.8 %add_bitcast_fusion = (f32[1,8,16,512]{3,2,0,1:T(8,128)}, f32[8,16,512]{2,1,0:T(8,128)S(1)}) fusion(f32[16,512]{1,0:T(8,128)S(1)} %get-tuple-element.90, f32[8,16,512]{2,1,0:T(8,128)S(1)} %copy-done.1, f32[8,16,511]{2,1,0:T(8,128)} %get-tuple-element.59, f32[8,16,1]{2,1,0:T(8,128)} %get-tuple-element.81, f32[8,16,512]{2,1,0:T(8,128)S(1)} %get-tuple-element.22, ...), kind=kLoop, calls=%fused_computation.195 | loop fusion | flops 2097152 | bytes 4456448 | tf_op jit(solution)/shard_map/stack | solution.py:262
  101.2 3.0 %collective-permute-start.16 = (f32[8,1,512]{2,1,0:T(1,128)S(1)}, f32[8,1,512]{2,1,0:T(1,128)S(1)}, u32[]{:S(2)}, u32[]{:S(2)}) collective-permute-start(f32[8,1,512]{2,1,0:T(1,128)S(1)} %get-tuple-element.49), channel_id=1, source_target_pairs={{0,8},{8,16},{16,24},{24,2},{2,10},{10,18},{18,26},{26,4},{4,12},{... | collective-permute-start | bytes 49160 | tf_op jit(solution)/shard_map/ppermute | solution.py:49
  109.7 8.4 %all-to-all-start.4 = ((f32[32,1,32]{2,1,0:T(1,128)}), f32[32,1,32]{2,1,0:T(1,128)S(1)}, u32[]{:S(2)}, u32[]{:S(2)}) async-start(f32[32,1,32]{2,1,0:T(1,128)} %broadcast_in_dim.37), calls=%async_computation.4 | async-start | bytes 32768 | tf_op jit(solution)/shard_map/all_to_all | solution.py:107
  119.5 3.2 %collective-permute-start.19 = (f32[8,1,512]{2,1,0:T(1,128)}, f32[8,1,512]{2,1,0:T(1,128)S(1)}, u32[]{:S(2)}, u32[]{:S(2)}) collective-permute-start(f32[8,1,512]{2,1,0:T(1,128)} %get-tuple-element.41), channel_id=1, source_target_pairs={{0,8},{8,16},{16,24},{24,2},{2,10},{10,18},{18,26},{26,4},{4,12},{... | collective-permute-start | bytes 49160 | tf_op jit(solution)/shard_map/ppermute | solution.py:49
  122.7 1.8 %collective-permute-start.20 = (f32[8,16,1]{2,1,0:T(8,128)S(1)}, f32[8,16,1]{2,1,0:T(8,128)}, u32[]{:S(2)}, u32[]{:S(2)}) collective-permute-start(f32[8,16,1]{2,1,0:T(8,128)S(1)} %slice_select_fusion.1), channel_id=1, source_target_pairs={{0,1},{1,0},{2,3},{3,2},{4,5},{5,4},{6,7},{7,6},{8,9},{9,8},{10,11... | collective-permute-start | bytes 1544 | tf_op jit(solution)/shard_map/ppermute | solution.py:46
  125.2 1.7 %fusion.1 = f32[2048]{0:T(1024)S(1)} fusion(f32[32,32]{1,0:T(8,128)S(1)} %bitcast.255, s32[2048]{0:T(1024)} %get-tuple-element.102, s32[2048]{0:T(1024)} %copy-done.27), kind=kOutput, calls=%fused_computation.3 | convolution fusion | flops 25425920 | bytes 28672 | tf_op jit(solution)/shard_map/dot_general | solution.py:115
  128.9 2.1 %collective-permute-done.24 = f32[256]{0:T(256)S(1)} collective-permute-done((f32[256]{0:T(256)S(1)}, f32[256]{0:T(256)S(1)}, u32[]{:S(2)}, u32[]{:S(2)}) %collective-permute-start.24) | collective-permute-done | bytes 1056 | tf_op jit(solution)/shard_map/ppermute | solution.py:119
  133.4 1.6 collective-permute-done.25
  136.4 2.6 %collective-permute-done.26 = f32[256]{0:T(256)S(1)} collective-permute-done((f32[256]{0:T(256)S(1)}, f32[256]{0:T(256)S(1)}, u32[]{:S(2)}, u32[]{:S(2)}) %collective-permute-start.26) | collective-permute-done | bytes 1056 | tf_op jit(solution)/shard_map/ppermute | solution.py:119
  145.6 1.7 collective-permute-done.21
  148.1 1.5 collective-permute-start.27
  149.9 1.8 %collective-permute-done.27 = f32[512]{0:T(512)S(1)} collective-permute-done((f32[512]{0:T(512)S(1)}, f32[512]{0:T(512)S(1)}, u32[]{:S(2)}, u32[]{:S(2)}) %collective-permute-start.27) | collective-permute-done | bytes 2080 | tf_op jit(solution)/shard_map/ppermute | solution.py:119
  152.1 1.5 collective-permute-start.28
  154.4 5.0 %all-to-all-start.3 = ((f32[2,8,16,512]{3,2,0,1:T(8,128)}), f32[2,8,16,512]{3,2,0,1:T(8,128)S(1)}, u32[]{:S(2)}, u32[]{:S(2)}) async-start(f32[2,8,16,512]{3,2,0,1:T(8,128)} %pad_maximum_fusion.1), calls=%async_computation.3 | async-start | bytes 1048576 | tf_op jit(solution)/shard_map/all_to_all | solution.py:262
  160.4 3.0 %collective-permute-done.29 = f32[1024]{0:T(1024)S(1)} collective-permute-done((f32[1024]{0:T(1024)S(1)}, f32[1024]{0:T(1024)S(1)}, u32[]{:S(2)}, u32[]{:S(2)}) %collective-permute-start.29) | collective-permute-done | bytes 4128 | tf_op jit(solution)/shard_map/ppermute | solution.py:119
  164.9 3.7 %all-to-all-done.3 = f32[2,8,16,512]{3,2,0,1:T(8,128)S(1)} async-done(((f32[2,8,16,512]{3,2,0,1:T(8,128)}), f32[2,8,16,512]{3,2,0,1:T(8,128)S(1)}, u32[]{:S(2)}, u32[]{:S(2)}) %all-to-all-start.3) | async-done | bytes 524320 | tf_op jit(solution)/shard_map/all_to_all | solution.py:262
  (255 shorter events, 67.9 us)
Async XLA Ops:
  3.9 13.1 %all-to-all-start = ((f32[2,2,64,512]{3,1,0,2:T(2,128)}), f32[2,2,64,512]{3,1,0,2:T(2,128)S(1)}, u32[]{:S(2)}, u32[]{:S(2)}) async-start(f32[2,2,64,512]{3,1,0,2:T(2,128)} %copy.33), calls=%async_computation | async-start | bytes 1048576 | tf_op jit(solution)/shard_map/all_to_all | solution.py:199
  19.1 11.1 %collective-permute-start.8 = (f32[8,16,1]{2,1,0:T(8,128)S(1)}, f32[8,16,1]{2,1,0:T(8,128)S(1)}, u32[]{:S(2)}, u32[]{:S(2)}) collective-permute-start(f32[8,16,1]{2,1,0:T(8,128)S(1)} %slice_select_fusion.5), channel_id=1, source_target_pairs={{0,1},{1,0},{2,3},{3,2},{4,5},{5,4},{6,7},{7,6},{8,9},{9,8},{10,11... | collective-permute-start | bytes 1544 | tf_op jit(solution)/shard_map/ppermute | solution.py:46
  21.4 15.2 %collective-permute-start.7 = (f32[8,1,512]{2,1,0:T(1,128)S(1)}, f32[8,1,512]{2,1,0:T(1,128)S(1)}, u32[]{:S(2)}, u32[]{:S(2)}) collective-permute-start(f32[8,1,512]{2,1,0:T(1,128)S(1)} %get-tuple-element.70), channel_id=1, source_target_pairs={{0,8},{8,16},{16,24},{24,2},{2,10},{10,18},{18,26},{26,4},{4,12},{... | collective-permute-start | bytes 49160 | tf_op jit(solution)/shard_map/ppermute | solution.py:49
  22.7 13.9 %collective-permute-start.6 = (f32[8,1,512]{2,1,0:T(1,128)S(1)}, f32[8,1,512]{2,1,0:T(1,128)S(1)}, u32[]{:S(2)}, u32[]{:S(2)}) collective-permute-start(f32[8,1,512]{2,1,0:T(1,128)S(1)} %get-tuple-element.71), channel_id=1, source_target_pairs={{8,0},{16,8},{24,16},{2,24},{10,2},{18,10},{26,18},{4,26},{12,4},{... | collective-permute-start | bytes 49160 | tf_op jit(solution)/shard_map/ppermute | solution.py:50
  24.9 11.6 %all-to-all-start.1 = ((f32[2,64,512]{2,0,1:T(2,128)}), f32[2,64,512]{2,0,1:T(2,128)S(1)}, u32[]{:S(2)}, u32[]{:S(2)}) async-start(f32[2,64,512]{2,0,1:T(2,128)} %copy.35), calls=%async_computation.1 | async-start | bytes 524288 | tf_op jit(solution)/shard_map/all_to_all | solution.py:202
  44.4 12.7 %all-to-all-start.2 = ((f32[32,1,32]{2,1,0:T(1,128)}), f32[32,1,32]{2,1,0:T(1,128)}, u32[]{:S(2)}, u32[]{:S(2)}) async-start(f32[32,1,32]{2,1,0:T(1,128)} %broadcast_in_dim.29), calls=%async_computation.2 | async-start | bytes 32768 | tf_op jit(solution)/shard_map/all_to_all | solution.py:107
  50.2 30.0 %collective-permute-start.9 = (f32[8,1,512]{2,1,0:T(1,128)}, f32[8,1,512]{2,1,0:T(1,128)S(1)}, u32[]{:S(2)}, u32[]{:S(2)}) collective-permute-start(f32[8,1,512]{2,1,0:T(1,128)} %get-tuple-element.64), channel_id=1, source_target_pairs={{8,0},{16,8},{24,16},{2,24},{10,2},{18,10},{26,18},{4,26},{12,4},{... | collective-permute-start | bytes 49160 | tf_op jit(solution)/shard_map/ppermute | solution.py:50
  51.5 28.7 %collective-permute-start.10 = (f32[8,1,512]{2,1,0:T(1,128)}, f32[8,1,512]{2,1,0:T(1,128)S(1)}, u32[]{:S(2)}, u32[]{:S(2)}) collective-permute-start(f32[8,1,512]{2,1,0:T(1,128)} %get-tuple-element.65), channel_id=1, source_target_pairs={{0,8},{8,16},{16,24},{24,2},{2,10},{10,18},{18,26},{26,4},{4,12},{... | collective-permute-start | bytes 49160 | tf_op jit(solution)/shard_map/ppermute | solution.py:49
  54.5 5.4 %collective-permute-start.11 = (f32[8,16,1]{2,1,0:T(8,128)S(1)}, f32[8,16,1]{2,1,0:T(8,128)S(1)}, u32[]{:S(2)}, u32[]{:S(2)}) collective-permute-start(f32[8,16,1]{2,1,0:T(8,128)S(1)} %slice_select_fusion.4), channel_id=1, source_target_pairs={{0,1},{1,0},{2,3},{3,2},{4,5},{5,4},{6,7},{7,6},{8,9},{9,8},{10,11... | collective-permute-start | bytes 1544 | tf_op jit(solution)/shard_map/ppermute | solution.py:46
  59.2 3.6 %collective-permute-start = (f32[256]{0:T(256)S(1)}, f32[256]{0:T(256)S(1)}, u32[]{:S(2)}, u32[]{:S(2)}) collective-permute-start(f32[256]{0:T(256)S(1)} %dynamic-slice_subtract_fusion.5), channel_id=1, source_target_pairs={{0,1},{1,0},{2,3},{3,2},{4,5},{5,4},{6,7},{7,6},{8,9},{9,8},{10,11... | collective-permute-start | bytes 3080 | tf_op jit(solution)/shard_map/ppermute | solution.py:119
  63.2 3.6 %collective-permute-start.1 = (f32[256]{0:T(256)S(1)}, f32[256]{0:T(256)S(1)}, u32[]{:S(2)}, u32[]{:S(2)}) collective-permute-start(f32[256]{0:T(256)S(1)} %dynamic-slice_subtract_fusion.4), channel_id=1, source_target_pairs={{0,1},{1,0},{2,3},{3,2},{4,5},{5,4},{6,7},{7,6},{8,9},{9,8},{10,11... | collective-permute-start | bytes 3080 | tf_op jit(solution)/shard_map/ppermute | solution.py:119
  67.3 3.6 %collective-permute-start.2 = (f32[256]{0:T(256)S(1)}, f32[256]{0:T(256)S(1)}, u32[]{:S(2)}, u32[]{:S(2)}) collective-permute-start(f32[256]{0:T(256)S(1)} %dynamic-slice_subtract_fusion.3), channel_id=1, source_target_pairs={{0,1},{1,0},{2,3},{3,2},{4,5},{5,4},{6,7},{7,6},{8,9},{9,8},{10,11... | collective-permute-start | bytes 3080 | tf_op jit(solution)/shard_map/ppermute | solution.py:119
  71.6 3.6 %collective-permute-start.3 = (f32[512]{0:T(512)S(1)}, f32[512]{0:T(512)S(1)}, u32[]{:S(2)}, u32[]{:S(2)}) collective-permute-start(f32[512]{0:T(512)S(1)} %pad_maximum_fusion.5), channel_id=1, source_target_pairs={{0,1},{1,0},{2,3},{3,2},{4,5},{5,4},{6,7},{7,6},{8,9},{9,8},{10,11... | collective-permute-start | bytes 6152 | tf_op jit(solution)/shard_map/ppermute | solution.py:119
  75.5 3.6 %collective-permute-start.4 = (f32[512]{0:T(512)S(1)}, f32[512]{0:T(512)S(1)}, u32[]{:S(2)}, u32[]{:S(2)}) collective-permute-start(f32[512]{0:T(512)S(1)} %pad_maximum_fusion.6), channel_id=1, source_target_pairs={{0,1},{1,0},{2,3},{3,2},{4,5},{5,4},{6,7},{7,6},{8,9},{9,8},{10,11... | collective-permute-start | bytes 6152 | tf_op jit(solution)/shard_map/ppermute | solution.py:119
  79.5 12.2 %collective-permute-start.5 = (f32[1024]{0:T(1024)S(1)}, f32[1024]{0:T(1024)S(1)}, u32[]{:S(2)}, u32[]{:S(2)}) collective-permute-start(f32[1024]{0:T(1024)S(1)} %pad_maximum_fusion.3), channel_id=1, source_target_pairs={{0,1},{1,0},{2,3},{3,2},{4,5},{5,4},{6,7},{7,6},{8,9},{9,8},{10,11... | collective-permute-start | bytes 12296 | tf_op jit(solution)/shard_map/ppermute | solution.py:119
  84.1 6.9 %collective-permute-start.14 = (f32[8,16,1]{2,1,0:T(8,128)S(1)}, f32[8,16,1]{2,1,0:T(8,128)S(1)}, u32[]{:S(2)}, u32[]{:S(2)}) collective-permute-start(f32[8,16,1]{2,1,0:T(8,128)S(1)} %slice_select_fusion.3), channel_id=1, source_target_pairs={{0,1},{1,0},{2,3},{3,2},{4,5},{5,4},{6,7},{7,6},{8,9},{9,8},{10,11... | collective-permute-start | bytes 1544 | tf_op jit(solution)/shard_map/ppermute | solution.py:46
  86.1 9.9 %collective-permute-start.12 = (f32[8,1,512]{2,1,0:T(1,128)}, f32[8,1,512]{2,1,0:T(1,128)}, u32[]{:S(2)}, u32[]{:S(2)}) collective-permute-start(f32[8,1,512]{2,1,0:T(1,128)} %get-tuple-element.56), channel_id=1, source_target_pairs={{8,0},{16,8},{24,16},{2,24},{10,2},{18,10},{26,18},{4,26},{12,4},{... | collective-permute-start | bytes 49160 | tf_op jit(solution)/shard_map/ppermute | solution.py:50
  87.4 8.6 %collective-permute-start.13 = (f32[8,1,512]{2,1,0:T(1,128)}, f32[8,1,512]{2,1,0:T(1,128)}, u32[]{:S(2)}, u32[]{:S(2)}) collective-permute-start(f32[8,1,512]{2,1,0:T(1,128)} %get-tuple-element.57), channel_id=1, source_target_pairs={{0,8},{8,16},{16,24},{24,2},{2,10},{10,18},{18,26},{26,4},{4,12},{... | collective-permute-start | bytes 49160 | tf_op jit(solution)/shard_map/ppermute | solution.py:49
  99.2 5.1 %collective-permute-start.17 = (f32[8,16,1]{2,1,0:T(8,128)S(1)}, f32[8,16,1]{2,1,0:T(8,128)S(1)}, u32[]{:S(2)}, u32[]{:S(2)}) collective-permute-start(f32[8,16,1]{2,1,0:T(8,128)S(1)} %slice_select_fusion.2), channel_id=1, source_target_pairs={{0,1},{1,0},{2,3},{3,2},{4,5},{5,4},{6,7},{7,6},{8,9},{9,8},{10,11... | collective-permute-start | bytes 1544 | tf_op jit(solution)/shard_map/ppermute | solution.py:46
  99.9 4.4 %collective-permute-start.15 = (f32[8,1,512]{2,1,0:T(1,128)S(1)}, f32[8,1,512]{2,1,0:T(1,128)S(1)}, u32[]{:S(2)}, u32[]{:S(2)}) collective-permute-start(f32[8,1,512]{2,1,0:T(1,128)S(1)} %get-tuple-element.48), channel_id=1, source_target_pairs={{8,0},{16,8},{24,16},{2,24},{10,2},{18,10},{26,18},{4,26},{12,4},{... | collective-permute-start | bytes 49160 | tf_op jit(solution)/shard_map/ppermute | solution.py:50
  101.2 3.9 %collective-permute-start.16 = (f32[8,1,512]{2,1,0:T(1,128)S(1)}, f32[8,1,512]{2,1,0:T(1,128)S(1)}, u32[]{:S(2)}, u32[]{:S(2)}) collective-permute-start(f32[8,1,512]{2,1,0:T(1,128)S(1)} %get-tuple-element.49), channel_id=1, source_target_pairs={{0,8},{8,16},{16,24},{24,2},{2,10},{10,18},{18,26},{26,4},{4,12},{... | collective-permute-start | bytes 49160 | tf_op jit(solution)/shard_map/ppermute | solution.py:49
  109.7 15.5 %all-to-all-start.4 = ((f32[32,1,32]{2,1,0:T(1,128)}), f32[32,1,32]{2,1,0:T(1,128)S(1)}, u32[]{:S(2)}, u32[]{:S(2)}) async-start(f32[32,1,32]{2,1,0:T(1,128)} %broadcast_in_dim.37), calls=%async_computation.4 | async-start | bytes 32768 | tf_op jit(solution)/shard_map/all_to_all | solution.py:107
  118.2 21.1 %collective-permute-start.18 = (f32[8,1,512]{2,1,0:T(1,128)}, f32[8,1,512]{2,1,0:T(1,128)S(1)}, u32[]{:S(2)}, u32[]{:S(2)}) collective-permute-start(f32[8,1,512]{2,1,0:T(1,128)} %get-tuple-element.40), channel_id=1, source_target_pairs={{8,0},{16,8},{24,16},{2,24},{10,2},{18,10},{26,18},{4,26},{12,4},{... | collective-permute-start | bytes 49160 | tf_op jit(solution)/shard_map/ppermute | solution.py:50
  119.5 19.9 %collective-permute-start.19 = (f32[8,1,512]{2,1,0:T(1,128)}, f32[8,1,512]{2,1,0:T(1,128)S(1)}, u32[]{:S(2)}, u32[]{:S(2)}) collective-permute-start(f32[8,1,512]{2,1,0:T(1,128)} %get-tuple-element.41), channel_id=1, source_target_pairs={{0,8},{8,16},{16,24},{24,2},{2,10},{10,18},{18,26},{26,4},{4,12},{... | collective-permute-start | bytes 49160 | tf_op jit(solution)/shard_map/ppermute | solution.py:49
  122.7 5.4 %collective-permute-start.20 = (f32[8,16,1]{2,1,0:T(8,128)S(1)}, f32[8,16,1]{2,1,0:T(8,128)}, u32[]{:S(2)}, u32[]{:S(2)}) collective-permute-start(f32[8,16,1]{2,1,0:T(8,128)S(1)} %slice_select_fusion.1), channel_id=1, source_target_pairs={{0,1},{1,0},{2,3},{3,2},{4,5},{5,4},{6,7},{7,6},{8,9},{9,8},{10,11... | collective-permute-start | bytes 1544 | tf_op jit(solution)/shard_map/ppermute | solution.py:46
  141.2 4.3 %collective-permute-start.23 = (f32[8,16,1]{2,1,0:T(8,128)S(1)}, f32[8,16,1]{2,1,0:T(8,128)S(1)}, u32[]{:S(2)}, u32[]{:S(2)}) collective-permute-start(f32[8,16,1]{2,1,0:T(8,128)S(1)} %slice_select_fusion), channel_id=1, source_target_pairs={{0,1},{1,0},{2,3},{3,2},{4,5},{5,4},{6,7},{7,6},{8,9},{9,8},{10,11... | collective-permute-start | bytes 1544 | tf_op jit(solution)/shard_map/ppermute | solution.py:46
  141.9 3.6 %collective-permute-start.22 = (f32[8,1,512]{2,1,0:T(1,128)S(1)}, f32[8,1,512]{2,1,0:T(1,128)S(1)}, u32[]{:S(2)}, u32[]{:S(2)}) collective-permute-start(f32[8,1,512]{2,1,0:T(1,128)S(1)} %get-tuple-element.32), channel_id=1, source_target_pairs={{0,8},{8,16},{16,24},{24,2},{2,10},{10,18},{18,26},{26,4},{4,12},{... | collective-permute-start | bytes 49160 | tf_op jit(solution)/shard_map/ppermute | solution.py:49
  143.2 4.0 %collective-permute-start.21 = (f32[8,1,512]{2,1,0:T(1,128)S(1)}, f32[8,1,512]{2,1,0:T(1,128)S(1)}, u32[]{:S(2)}, u32[]{:S(2)}) collective-permute-start(f32[8,1,512]{2,1,0:T(1,128)S(1)} %get-tuple-element.33), channel_id=1, source_target_pairs={{8,0},{16,8},{24,16},{2,24},{10,2},{18,10},{26,18},{4,26},{12,4},{... | collective-permute-start | bytes 49160 | tf_op jit(solution)/shard_map/ppermute | solution.py:50
  148.1 3.6 %collective-permute-start.27 = (f32[512]{0:T(512)S(1)}, f32[512]{0:T(512)S(1)}, u32[]{:S(2)}, u32[]{:S(2)}) collective-permute-start(f32[512]{0:T(512)S(1)} %pad_maximum_fusion.7), channel_id=1, source_target_pairs={{0,1},{1,0},{2,3},{3,2},{4,5},{5,4},{6,7},{7,6},{8,9},{9,8},{10,11... | collective-permute-start | bytes 6152 | tf_op jit(solution)/shard_map/ppermute | solution.py:119
  152.1 7.3 %collective-permute-start.28 = (f32[512]{0:T(512)S(1)}, f32[512]{0:T(512)S(1)}, u32[]{:S(2)}, u32[]{:S(2)}) collective-permute-start(f32[512]{0:T(512)S(1)} %pad_maximum_fusion.8), channel_id=1, source_target_pairs={{0,1},{1,0},{2,3},{3,2},{4,5},{5,4},{6,7},{7,6},{8,9},{9,8},{10,11... | collective-permute-start | bytes 6152 | tf_op jit(solution)/shard_map/ppermute | solution.py:119
  154.4 14.2 %all-to-all-start.3 = ((f32[2,8,16,512]{3,2,0,1:T(8,128)}), f32[2,8,16,512]{3,2,0,1:T(8,128)S(1)}, u32[]{:S(2)}, u32[]{:S(2)}) async-start(f32[2,8,16,512]{3,2,0,1:T(8,128)} %pad_maximum_fusion.1), calls=%async_computation.3 | async-start | bytes 1048576 | tf_op jit(solution)/shard_map/all_to_all | solution.py:262
  159.7 3.7 %collective-permute-start.29 = (f32[1024]{0:T(1024)S(1)}, f32[1024]{0:T(1024)S(1)}, u32[]{:S(2)}, u32[]{:S(2)}) collective-permute-start(f32[1024]{0:T(1024)S(1)} %pad_maximum_fusion.4), channel_id=1, source_target_pairs={{0,1},{1,0},{2,3},{3,2},{4,5},{5,4},{6,7},{7,6},{8,9},{9,8},{10,11... | collective-permute-start | bytes 12296 | tf_op jit(solution)/shard_map/ppermute | solution.py:119
  (34 other events, 441.6 us)

commit v17 on v12

--- a/solution.py
+++ b/solution.py
@@ -196,9 +196,8 @@
         + (lax.axis_index("col") * given_cols + jnp.arange(given_cols, dtype=jnp.int32))[None, :]
     ).reshape(-1)
     given_pick = (given_ids[:, None] == port_tile.reshape(-1)[None, :]).astype(jnp.float32)
-    packed = lax.all_to_all(jnp.stack((conduct, vertical)), "layer", 2, 1, tiled=True)
-    conduct, vertical = packed[0], packed[1]
-    sources = lax.all_to_all(sources, "layer", 1, 0, tiled=True)
+    packed = lax.all_to_all(jnp.stack((sources, conduct, vertical)), "layer", 2, 1, tiled=True)
+    sources, conduct, vertical = packed[0], packed[1], packed[2]
     local_layers, grid_rows, grid_cols = sources.shape
     pad_rows = lax.dynamic_slice_in_dim(pad_map, lax.axis_index("layer") * grid_rows, grid_rows, 0)
     row_halo = rims(conduct, ROW_AXES, 1)

time: 157 us -> 161 us (1.025)
  waiting for transfers between devices: 48.6 us -> 42.9 us
  other arithmetic: 11.4 us -> 16.8 us
  local copies, waits for them, and re-layouts: 11.9 us -> 17.3 us
    all_to_all x2 -> x1, waiting for transfers between devices: 3.97 us -> 9.92 us  [shards(): lax.all_to_all(jnp.stack((sources, conduct, vertical)), 'layer', 2, 1, ti...]
    all_to_all x2, waiting for transfers between devices: 6.2 us -> 0.93 us  [share_tiles(): got = lax.all_to_all(payload, ('layer', 'row', 'col'), 0, 0, tiled=True)]
    all_to_all x2 -> x1, starting transfers between devices: 7.71 us -> 4.24 us  [shards(): lax.all_to_all(jnp.stack((sources, conduct, vertical)), 'layer', 2, 1, ti...]
    ppermute x6, waiting for transfers between devices: 4.59 us -> 1.51 us  [rims(): got = lax.ppermute(jnp.where(low, tail, head), axis, [(0, 1), (1, 0)])]
    ppermute x12, waiting for transfers between devices: 26.1 us -> 23.6 us  [swap_col(): return lax.ppermute(value, 'col', [(0, 1), (1, 0)])]
    unnamed x43 -> x62, local copies, waits for them, and re-layouts: 2.72 us -> 0.16 us
    slice x13, local copies, waits for them, and re-layouts: 3.26 us -> 5.61 us  [neighbours(): lax.slice_in_dim(field, 1, size, axis=dim)]
    slice x5, local copies, waits for them, and re-layouts: 0.4 us -> 2.74 us  [neighbours(): lax.slice_in_dim(field, 0, size - 1, axis=dim)]
  transfers between devices with their start and end apart: 35 -> 34, of which waited for: 21 -> 19; matrix products, arithmetic and copies ran while one was open for 13% -> 17% of each run, Pallas kernels for 0% -> 0%
where the time goes in v17:
time: 161 us; the launch traced here: 160 us
  starting transfers between devices  69.4 us (43%)
  waiting for transfers between devices  42.9 us (27%)
  local copies, waits for them, and re-layouts  17.3 us (11%)
  other arithmetic  16.8 us (10%)
  matrix products  12.1 us (8%)
    ppermute x12, waiting for transfers between devices, swap_col(): return lax.ppermute(value, 'col', [(0, 1), (1, 0)])  23.6 us
    ppermute x6, starting transfers between devices, rims(): lax.ppermute(tail, axis, [(place[i], place[i + 1]) for i in range(count -...  19 us
    all_to_all x2, starting transfers between devices, share_tiles(): got = lax.all_to_all(payload, ('layer', 'row', 'col'), 0, 0, tiled=True)  16.3 us
    all_to_all x1, waiting for transfers between devices, shards(): lax.all_to_all(jnp.stack((sources, conduct, vertical)), 'layer', 2, 1, ti...  9.92 us
    ppermute x12, starting transfers between devices, swap_col(): return lax.ppermute(value, 'col', [(0, 1), (1, 0)])  9.3 us
    ppermute x6, starting transfers between devices, rims(): got = lax.ppermute(jnp.where(low, tail, head), axis, [(0, 1), (1, 0)])  7.84 us
    ppermute x6, starting transfers between devices, rims(): lax.ppermute(head, axis, [(place[i + 1], place[i]) for i in range(count -...  7.74 us
    slice x13, local copies, waits for them, and re-layouts, neighbours(): lax.slice_in_dim(field, 1, size, axis=dim)  5.61 us
  transfers between devices with their start and end apart: 34, of which 19 were waited for; matrix products, arithmetic and copies ran while one was open for 17% of the time, Pallas kernels for 0%

profile of v17, /device:TPU:0, one launch (start us, length us, event | category | flops | bytes accessed | tf_op | source)
XLA Modules:
  0.0 160.0 jit_solution(11506531766375543858)
XLA Ops:
  2.8 1.5 copy.31
  4.3 4.2 %all-to-all-start = ((f32[3,2,64,512]{3,1,0,2:T(2,128)}), f32[3,2,64,512]{3,1,0,2:T(2,128)S(1)}, u32[]{:S(2)}, u32[]{:S(2)}) async-start(f32[3,2,64,512]{3,1,0,2:T(2,128)} %copy.31), calls=%async_computation | async-start | bytes 1572864 | tf_op jit(solution)/shard_map/all_to_all | solution.py:199
  10.3 9.9 %all-to-all-done = f32[3,2,64,512]{3,1,0,2:T(2,128)S(1)} async-done(((f32[3,2,64,512]{3,1,0,2:T(2,128)}), f32[3,2,64,512]{3,1,0,2:T(2,128)S(1)}, u32[]{:S(2)}, u32[]{:S(2)}) %all-to-all-start) | async-done | bytes 786464 | tf_op jit(solution)/shard_map/all_to_all | solution.py:199
  23.2 5.6 %all-to-all-start.1 = ((f32[32,1,32]{2,1,0:T(1,128)}), f32[32,1,32]{2,1,0:T(1,128)S(1)}, u32[]{:S(2)}, u32[]{:S(2)}) async-start(f32[32,1,32]{2,1,0:T(1,128)} %broadcast_in_dim.29), calls=%async_computation.1 | async-start | bytes 32768 | tf_op jit(solution)/shard_map/all_to_all | solution.py:107
  29.6 2.1 %collective-permute-start.7 = (f32[8,1,512]{2,1,0:T(1,128)S(1)}, f32[8,1,512]{2,1,0:T(1,128)S(1)}, u32[]{:S(2)}, u32[]{:S(2)}) collective-permute-start(f32[8,1,512]{2,1,0:T(1,128)S(1)} %get-tuple-element.68), channel_id=1, source_target_pairs={{0,8},{8,16},{16,24},{24,2},{2,10},{10,18},{18,26},{26,4},{4,12},{... | collective-permute-start | bytes 49160 | tf_op jit(solution)/shard_map/ppermute | solution.py:49
  34.0 1.7 %collective-permute-start.8 = (f32[8,16,1]{2,1,0:T(8,128)S(1)}, f32[8,16,1]{2,1,0:T(8,128)S(1)}, u32[]{:S(2)}, u32[]{:S(2)}) collective-permute-start(f32[8,16,1]{2,1,0:T(8,128)S(1)} %slice_select_fusion.5), channel_id=1, source_target_pairs={{0,1},{1,0},{2,3},{3,2},{4,5},{5,4},{6,7},{7,6},{8,9},{9,8},{10,11... | collective-permute-start | bytes 1544 | tf_op jit(solution)/shard_map/ppermute | solution.py:46
  38.4 2.5 %collective-permute-done = f32[256]{0:T(256)S(1)} collective-permute-done((f32[256]{0:T(256)S(1)}, f32[256]{0:T(256)S(1)}, u32[]{:S(2)}, u32[]{:S(2)}) %collective-permute-start) | collective-permute-done | bytes 1056 | tf_op jit(solution)/shard_map/ppermute | solution.py:119
  43.2 1.6 %collective-permute-done.1 = f32[256]{0:T(256)S(1)} collective-permute-done((f32[256]{0:T(256)S(1)}, f32[256]{0:T(256)S(1)}, u32[]{:S(2)}, u32[]{:S(2)}) %collective-permute-start.1) | collective-permute-done | bytes 1056 | tf_op jit(solution)/shard_map/ppermute | solution.py:119
  46.3 2.6 %collective-permute-done.2 = f32[256]{0:T(256)S(1)} collective-permute-done((f32[256]{0:T(256)S(1)}, f32[256]{0:T(256)S(1)}, u32[]{:S(2)}, u32[]{:S(2)}) %collective-permute-start.2) | collective-permute-done | bytes 1056 | tf_op jit(solution)/shard_map/ppermute | solution.py:119
  50.5 2.7 %collective-permute-done.3 = f32[512]{0:T(512)S(1)} collective-permute-done((f32[512]{0:T(512)S(1)}, f32[512]{0:T(512)S(1)}, u32[]{:S(2)}, u32[]{:S(2)}) %collective-permute-start.3) | collective-permute-done | bytes 2080 | tf_op jit(solution)/shard_map/ppermute | solution.py:119
  54.2 3.0 %collective-permute-done.4 = f32[512]{0:T(512)S(1)} collective-permute-done((f32[512]{0:T(512)S(1)}, f32[512]{0:T(512)S(1)}, u32[]{:S(2)}, u32[]{:S(2)}) %collective-permute-start.4) | collective-permute-done | bytes 2080 | tf_op jit(solution)/shard_map/ppermute | solution.py:119
  62.2 1.4 collective-permute-start.11
  65.6 3.6 %collective-permute-start.10 = (f32[8,1,512]{2,1,0:T(1,128)}, f32[8,1,512]{2,1,0:T(1,128)}, u32[]{:S(2)}, u32[]{:S(2)}) collective-permute-start(f32[8,1,512]{2,1,0:T(1,128)} %get-tuple-element.63), channel_id=1, source_target_pairs={{0,8},{8,16},{16,24},{24,2},{2,10},{10,18},{18,26},{26,4},{4,12},{... | collective-permute-start | bytes 49160 | tf_op jit(solution)/shard_map/ppermute | solution.py:49
  74.2 1.9 %fusion.150 = (f32[8,16,512]{2,1,0:T(8,128)S(1)}, f32[8,16,512]{2,1,0:T(8,128)S(1)}) fusion(f32[8,16,512]{2,1,0:T(8,128)S(1)} %get-tuple-element.13, f32[1,4,2,16,512]{4,3,2,1,0:T(8,128)} %copy.34, f32[8,16,512]{2,1,0:T(8,128)S(1)} %copy-done.1, f32[8,16,511]{2,1,0:T(8,128)} %get-tuple-element.65, f32[8,16,1]{2,1,0:T(8,128)} %get-tuple-element.83, ...), kind=kLoop, calls=%fused_computation.193 | loop fusion | flops 1966080 | bytes 4161536 | tf_op jit(solution)/shard_map/add | solution.py:85
  78.5 4.7 %collective-permute-start.13 = (f32[8,1,512]{2,1,0:T(1,128)S(1)}, f32[8,1,512]{2,1,0:T(1,128)S(1)}, u32[]{:S(2)}, u32[]{:S(2)}) collective-permute-start(f32[8,1,512]{2,1,0:T(1,128)S(1)} %get-tuple-element.55), channel_id=1, source_target_pairs={{0,8},{8,16},{16,24},{24,2},{2,10},{10,18},{18,26},{26,4},{4,12},{... | collective-permute-start | bytes 49160 | tf_op jit(solution)/shard_map/ppermute | solution.py:49
  85.6 1.5 collective-permute-start.17
  88.5 4.0 %collective-permute-start.16 = (f32[8,1,512]{2,1,0:T(1,128)S(1)}, f32[8,1,512]{2,1,0:T(1,128)S(1)}, u32[]{:S(2)}, u32[]{:S(2)}) collective-permute-start(f32[8,1,512]{2,1,0:T(1,128)S(1)} %get-tuple-element.47), channel_id=1, source_target_pairs={{0,8},{8,16},{16,24},{24,2},{2,10},{10,18},{18,26},{26,4},{4,12},{... | collective-permute-start | bytes 49160 | tf_op jit(solution)/shard_map/ppermute | solution.py:49
  97.9 10.6 %all-to-all-start.3 = ((f32[32,1,32]{2,1,0:T(1,128)}), f32[32,1,32]{2,1,0:T(1,128)S(1)}, u32[]{:S(2)}, u32[]{:S(2)}) async-start(f32[32,1,32]{2,1,0:T(1,128)} %broadcast_in_dim.37), calls=%async_computation.3 | async-start | bytes 32768 | tf_op jit(solution)/shard_map/all_to_all | solution.py:107
  109.9 3.2 %collective-permute-start.19 = (f32[8,1,512]{2,1,0:T(1,128)}, f32[8,1,512]{2,1,0:T(1,128)S(1)}, u32[]{:S(2)}, u32[]{:S(2)}) collective-permute-start(f32[8,1,512]{2,1,0:T(1,128)} %get-tuple-element.39), channel_id=1, source_target_pairs={{0,8},{8,16},{16,24},{24,2},{2,10},{10,18},{18,26},{26,4},{4,12},{... | collective-permute-start | bytes 49160 | tf_op jit(solution)/shard_map/ppermute | solution.py:49
  113.1 1.8 %collective-permute-start.20 = (f32[8,16,1]{2,1,0:T(8,128)S(1)}, f32[8,16,1]{2,1,0:T(8,128)}, u32[]{:S(2)}, u32[]{:S(2)}) collective-permute-start(f32[8,16,1]{2,1,0:T(8,128)S(1)} %slice_select_fusion.1), channel_id=1, source_target_pairs={{0,1},{1,0},{2,3},{3,2},{4,5},{5,4},{6,7},{7,6},{8,9},{9,8},{10,11... | collective-permute-start | bytes 1544 | tf_op jit(solution)/shard_map/ppermute | solution.py:46
  115.7 1.7 %fusion.1 = f32[2048]{0:T(1024)S(1)} fusion(f32[32,32]{1,0:T(8,128)S(1)} %bitcast.242, s32[2048]{0:T(1024)} %copy-done.27, s32[2048]{0:T(1024)} %copy-done.26), kind=kOutput, calls=%fused_computation.3 | convolution fusion | flops 25425920 | bytes 28672 | tf_op jit(solution)/shard_map/dot_general | solution.py:115
  119.4 2.1 %collective-permute-done.24 = f32[256]{0:T(256)S(1)} collective-permute-done((f32[256]{0:T(256)S(1)}, f32[256]{0:T(256)S(1)}, u32[]{:S(2)}, u32[]{:S(2)}) %collective-permute-start.24) | collective-permute-done | bytes 1056 | tf_op jit(solution)/shard_map/ppermute | solution.py:119
  123.8 1.6 %collective-permute-done.25 = f32[256]{0:T(256)S(1)} collective-permute-done((f32[256]{0:T(256)S(1)}, f32[256]{0:T(256)S(1)}, u32[]{:S(2)}, u32[]{:S(2)}) %collective-permute-start.25) | collective-permute-done | bytes 1056 | tf_op jit(solution)/shard_map/ppermute | solution.py:119
  126.8 2.6 %collective-permute-done.26 = f32[256]{0:T(256)S(1)} collective-permute-done((f32[256]{0:T(256)S(1)}, f32[256]{0:T(256)S(1)}, u32[]{:S(2)}, u32[]{:S(2)}) %collective-permute-start.26) | collective-permute-done | bytes 1056 | tf_op jit(solution)/shard_map/ppermute | solution.py:119
  129.9 1.4 fusion.170
  136.0 1.7 %collective-permute-done.21 = f32[8,1,512]{2,1,0:T(1,128)S(1)} collective-permute-done((f32[8,1,512]{2,1,0:T(1,128)S(1)}, f32[8,1,512]{2,1,0:T(1,128)S(1)}, u32[]{:S(2)}, u32[]{:S(2)}) %collective-permute-start.21) | collective-permute-done | bytes 16416 | tf_op jit(solution)/shard_map/ppermute | solution.py:50
  138.6 1.5 collective-permute-start.27
  140.4 1.8 %collective-permute-done.27 = f32[512]{0:T(512)S(1)} collective-permute-done((f32[512]{0:T(512)S(1)}, f32[512]{0:T(512)S(1)}, u32[]{:S(2)}, u32[]{:S(2)}) %collective-permute-start.27) | collective-permute-done | bytes 2080 | tf_op jit(solution)/shard_map/ppermute | solution.py:119
  142.6 1.5 collective-permute-start.28
  144.9 5.0 %all-to-all-start.2 = ((f32[2,8,16,512]{3,2,0,1:T(8,128)}), f32[2,8,16,512]{3,2,0,1:T(8,128)S(1)}, u32[]{:S(2)}, u32[]{:S(2)}) async-start(f32[2,8,16,512]{3,2,0,1:T(8,128)} %pad_maximum_fusion.1), calls=%async_computation.2 | async-start | bytes 1048576 | tf_op jit(solution)/shard_map/all_to_all | solution.py:260
  150.8 3.0 %collective-permute-done.29 = f32[1024]{0:T(1024)S(1)} collective-permute-done((f32[1024]{0:T(1024)S(1)}, f32[1024]{0:T(1024)S(1)}, u32[]{:S(2)}, u32[]{:S(2)}) %collective-permute-start.29) | collective-permute-done | bytes 4128 | tf_op jit(solution)/shard_map/ppermute | solution.py:119
  155.4 3.7 %all-to-all-done.2 = f32[2,8,16,512]{3,2,0,1:T(8,128)S(1)} async-done(((f32[2,8,16,512]{3,2,0,1:T(8,128)}), f32[2,8,16,512]{3,2,0,1:T(8,128)S(1)}, u32[]{:S(2)}, u32[]{:S(2)}) %all-to-all-start.2) | async-done | bytes 524320 | tf_op jit(solution)/shard_map/all_to_all | solution.py:260
  (250 shorter events, 60.3 us)
Async XLA Ops:
  4.3 15.9 %all-to-all-start = ((f32[3,2,64,512]{3,1,0,2:T(2,128)}), f32[3,2,64,512]{3,1,0,2:T(2,128)S(1)}, u32[]{:S(2)}, u32[]{:S(2)}) async-start(f32[3,2,64,512]{3,1,0,2:T(2,128)} %copy.31), calls=%async_computation | async-start | bytes 1572864 | tf_op jit(solution)/shard_map/all_to_all | solution.py:199
  23.2 12.8 %all-to-all-start.1 = ((f32[32,1,32]{2,1,0:T(1,128)}), f32[32,1,32]{2,1,0:T(1,128)S(1)}, u32[]{:S(2)}, u32[]{:S(2)}) async-start(f32[32,1,32]{2,1,0:T(1,128)} %broadcast_in_dim.29), calls=%async_computation.1 | async-start | bytes 32768 | tf_op jit(solution)/shard_map/all_to_all | solution.py:107
  29.6 28.6 %collective-permute-start.7 = (f32[8,1,512]{2,1,0:T(1,128)S(1)}, f32[8,1,512]{2,1,0:T(1,128)S(1)}, u32[]{:S(2)}, u32[]{:S(2)}) collective-permute-start(f32[8,1,512]{2,1,0:T(1,128)S(1)} %get-tuple-element.68), channel_id=1, source_target_pairs={{0,8},{8,16},{16,24},{24,2},{2,10},{10,18},{18,26},{26,4},{4,12},{... | collective-permute-start | bytes 49160 | tf_op jit(solution)/shard_map/ppermute | solution.py:49
  31.7 26.5 %collective-permute-start.6 = (f32[8,1,512]{2,1,0:T(1,128)S(1)}, f32[8,1,512]{2,1,0:T(1,128)S(1)}, u32[]{:S(2)}, u32[]{:S(2)}) collective-permute-start(f32[8,1,512]{2,1,0:T(1,128)S(1)} %get-tuple-element.69), channel_id=1, source_target_pairs={{8,0},{16,8},{24,16},{2,24},{10,2},{18,10},{26,18},{4,26},{12,4},{... | collective-permute-start | bytes 49160 | tf_op jit(solution)/shard_map/ppermute | solution.py:50
  34.0 4.3 %collective-permute-start.8 = (f32[8,16,1]{2,1,0:T(8,128)S(1)}, f32[8,16,1]{2,1,0:T(8,128)S(1)}, u32[]{:S(2)}, u32[]{:S(2)}) collective-permute-start(f32[8,16,1]{2,1,0:T(8,128)S(1)} %slice_select_fusion.5), channel_id=1, source_target_pairs={{0,1},{1,0},{2,3},{3,2},{4,5},{5,4},{6,7},{7,6},{8,9},{9,8},{10,11... | collective-permute-start | bytes 1544 | tf_op jit(solution)/shard_map/ppermute | solution.py:46
  37.3 3.6 %collective-permute-start = (f32[256]{0:T(256)S(1)}, f32[256]{0:T(256)S(1)}, u32[]{:S(2)}, u32[]{:S(2)}) collective-permute-start(f32[256]{0:T(256)S(1)} %dynamic-slice_subtract_fusion.5), channel_id=1, source_target_pairs={{0,1},{1,0},{2,3},{3,2},{4,5},{5,4},{6,7},{7,6},{8,9},{9,8},{10,11... | collective-permute-start | bytes 3080 | tf_op jit(solution)/shard_map/ppermute | solution.py:119
  41.3 3.6 %collective-permute-start.1 = (f32[256]{0:T(256)S(1)}, f32[256]{0:T(256)S(1)}, u32[]{:S(2)}, u32[]{:S(2)}) collective-permute-start(f32[256]{0:T(256)S(1)} %dynamic-slice_subtract_fusion.4), channel_id=1, source_target_pairs={{0,1},{1,0},{2,3},{3,2},{4,5},{5,4},{6,7},{7,6},{8,9},{9,8},{10,11... | collective-permute-start | bytes 3080 | tf_op jit(solution)/shard_map/ppermute | solution.py:119
  45.3 3.6 %collective-permute-start.2 = (f32[256]{0:T(256)S(1)}, f32[256]{0:T(256)S(1)}, u32[]{:S(2)}, u32[]{:S(2)}) collective-permute-start(f32[256]{0:T(256)S(1)} %dynamic-slice_subtract_fusion.3), channel_id=1, source_target_pairs={{0,1},{1,0},{2,3},{3,2},{4,5},{5,4},{6,7},{7,6},{8,9},{9,8},{10,11... | collective-permute-start | bytes 3080 | tf_op jit(solution)/shard_map/ppermute | solution.py:119
  49.6 3.6 %collective-permute-start.3 = (f32[512]{0:T(512)S(1)}, f32[512]{0:T(512)S(1)}, u32[]{:S(2)}, u32[]{:S(2)}) collective-permute-start(f32[512]{0:T(512)S(1)} %pad_maximum_fusion.5), channel_id=1, source_target_pairs={{0,1},{1,0},{2,3},{3,2},{4,5},{5,4},{6,7},{7,6},{8,9},{9,8},{10,11... | collective-permute-start | bytes 6152 | tf_op jit(solution)/shard_map/ppermute | solution.py:119
  53.6 3.6 %collective-permute-start.4 = (f32[512]{0:T(512)S(1)}, f32[512]{0:T(512)S(1)}, u32[]{:S(2)}, u32[]{:S(2)}) collective-permute-start(f32[512]{0:T(512)S(1)} %pad_maximum_fusion.6), channel_id=1, source_target_pairs={{0,1},{1,0},{2,3},{3,2},{4,5},{5,4},{6,7},{7,6},{8,9},{9,8},{10,11... | collective-permute-start | bytes 6152 | tf_op jit(solution)/shard_map/ppermute | solution.py:119
  57.5 12.3 %collective-permute-start.5 = (f32[1024]{0:T(1024)S(1)}, f32[1024]{0:T(1024)S(1)}, u32[]{:S(2)}, u32[]{:S(2)}) collective-permute-start(f32[1024]{0:T(1024)S(1)} %pad_maximum_fusion.3), channel_id=1, source_target_pairs={{0,1},{1,0},{2,3},{3,2},{4,5},{5,4},{6,7},{7,6},{8,9},{9,8},{10,11... | collective-permute-start | bytes 12296 | tf_op jit(solution)/shard_map/ppermute | solution.py:119
  62.2 7.0 %collective-permute-start.11 = (f32[8,16,1]{2,1,0:T(8,128)S(1)}, f32[8,16,1]{2,1,0:T(8,128)S(1)}, u32[]{:S(2)}, u32[]{:S(2)}) collective-permute-start(f32[8,16,1]{2,1,0:T(8,128)S(1)} %slice_select_fusion.4), channel_id=1, source_target_pairs={{0,1},{1,0},{2,3},{3,2},{4,5},{5,4},{6,7},{7,6},{8,9},{9,8},{10,11... | collective-permute-start | bytes 1544 | tf_op jit(solution)/shard_map/ppermute | solution.py:46
  64.3 9.9 %collective-permute-start.9 = (f32[8,1,512]{2,1,0:T(1,128)}, f32[8,1,512]{2,1,0:T(1,128)}, u32[]{:S(2)}, u32[]{:S(2)}) collective-permute-start(f32[8,1,512]{2,1,0:T(1,128)} %get-tuple-element.62), channel_id=1, source_target_pairs={{8,0},{16,8},{24,16},{2,24},{10,2},{18,10},{26,18},{4,26},{12,4},{... | collective-permute-start | bytes 49160 | tf_op jit(solution)/shard_map/ppermute | solution.py:50
  65.6 8.6 %collective-permute-start.10 = (f32[8,1,512]{2,1,0:T(1,128)}, f32[8,1,512]{2,1,0:T(1,128)}, u32[]{:S(2)}, u32[]{:S(2)}) collective-permute-start(f32[8,1,512]{2,1,0:T(1,128)} %get-tuple-element.63), channel_id=1, source_target_pairs={{0,8},{8,16},{16,24},{24,2},{2,10},{10,18},{18,26},{26,4},{4,12},{... | collective-permute-start | bytes 49160 | tf_op jit(solution)/shard_map/ppermute | solution.py:49
  76.5 6.7 %collective-permute-start.14 = (f32[8,16,1]{2,1,0:T(8,128)S(1)}, f32[8,16,1]{2,1,0:T(8,128)S(1)}, u32[]{:S(2)}, u32[]{:S(2)}) collective-permute-start(f32[8,16,1]{2,1,0:T(8,128)S(1)} %slice_select_fusion.3), channel_id=1, source_target_pairs={{0,1},{1,0},{2,3},{3,2},{4,5},{5,4},{6,7},{7,6},{8,9},{9,8},{10,11... | collective-permute-start | bytes 1544 | tf_op jit(solution)/shard_map/ppermute | solution.py:46
  77.2 6.1 %collective-permute-start.12 = (f32[8,1,512]{2,1,0:T(1,128)S(1)}, f32[8,1,512]{2,1,0:T(1,128)S(1)}, u32[]{:S(2)}, u32[]{:S(2)}) collective-permute-start(f32[8,1,512]{2,1,0:T(1,128)S(1)} %get-tuple-element.54), channel_id=1, source_target_pairs={{8,0},{16,8},{24,16},{2,24},{10,2},{18,10},{26,18},{4,26},{12,4},{... | collective-permute-start | bytes 49160 | tf_op jit(solution)/shard_map/ppermute | solution.py:50
  78.5 5.6 %collective-permute-start.13 = (f32[8,1,512]{2,1,0:T(1,128)S(1)}, f32[8,1,512]{2,1,0:T(1,128)S(1)}, u32[]{:S(2)}, u32[]{:S(2)}) collective-permute-start(f32[8,1,512]{2,1,0:T(1,128)S(1)} %get-tuple-element.55), channel_id=1, source_target_pairs={{0,8},{8,16},{16,24},{24,2},{2,10},{10,18},{18,26},{26,4},{4,12},{... | collective-permute-start | bytes 49160 | tf_op jit(solution)/shard_map/ppermute | solution.py:49
  85.6 6.9 %collective-permute-start.17 = (f32[8,16,1]{2,1,0:T(8,128)S(1)}, f32[8,16,1]{2,1,0:T(8,128)S(1)}, u32[]{:S(2)}, u32[]{:S(2)}) collective-permute-start(f32[8,16,1]{2,1,0:T(8,128)S(1)} %slice_select_fusion.2), channel_id=1, source_target_pairs={{0,1},{1,0},{2,3},{3,2},{4,5},{5,4},{6,7},{7,6},{8,9},{9,8},{10,11... | collective-permute-start | bytes 1544 | tf_op jit(solution)/shard_map/ppermute | solution.py:46
  87.2 5.4 %collective-permute-start.15 = (f32[8,1,512]{2,1,0:T(1,128)S(1)}, f32[8,1,512]{2,1,0:T(1,128)S(1)}, u32[]{:S(2)}, u32[]{:S(2)}) collective-permute-start(f32[8,1,512]{2,1,0:T(1,128)S(1)} %get-tuple-element.46), channel_id=1, source_target_pairs={{8,0},{16,8},{24,16},{2,24},{10,2},{18,10},{26,18},{4,26},{12,4},{... | collective-permute-start | bytes 49160 | tf_op jit(solution)/shard_map/ppermute | solution.py:50
  88.5 4.8 %collective-permute-start.16 = (f32[8,1,512]{2,1,0:T(1,128)S(1)}, f32[8,1,512]{2,1,0:T(1,128)S(1)}, u32[]{:S(2)}, u32[]{:S(2)}) collective-permute-start(f32[8,1,512]{2,1,0:T(1,128)S(1)} %get-tuple-element.47), channel_id=1, source_target_pairs={{0,8},{8,16},{16,24},{24,2},{2,10},{10,18},{18,26},{26,4},{4,12},{... | collective-permute-start | bytes 49160 | tf_op jit(solution)/shard_map/ppermute | solution.py:49
  97.9 17.8 %all-to-all-start.3 = ((f32[32,1,32]{2,1,0:T(1,128)}), f32[32,1,32]{2,1,0:T(1,128)S(1)}, u32[]{:S(2)}, u32[]{:S(2)}) async-start(f32[32,1,32]{2,1,0:T(1,128)} %broadcast_in_dim.37), calls=%async_computation.3 | async-start | bytes 32768 | tf_op jit(solution)/shard_map/all_to_all | solution.py:107
  108.6 21.1 %collective-permute-start.18 = (f32[8,1,512]{2,1,0:T(1,128)}, f32[8,1,512]{2,1,0:T(1,128)S(1)}, u32[]{:S(2)}, u32[]{:S(2)}) collective-permute-start(f32[8,1,512]{2,1,0:T(1,128)} %get-tuple-element.38), channel_id=1, source_target_pairs={{8,0},{16,8},{24,16},{2,24},{10,2},{18,10},{26,18},{4,26},{12,4},{... | collective-permute-start | bytes 49160 | tf_op jit(solution)/shard_map/ppermute | solution.py:50
  109.9 19.9 %collective-permute-start.19 = (f32[8,1,512]{2,1,0:T(1,128)}, f32[8,1,512]{2,1,0:T(1,128)S(1)}, u32[]{:S(2)}, u32[]{:S(2)}) collective-permute-start(f32[8,1,512]{2,1,0:T(1,128)} %get-tuple-element.39), channel_id=1, source_target_pairs={{0,8},{8,16},{16,24},{24,2},{2,10},{10,18},{18,26},{26,4},{4,12},{... | collective-permute-start | bytes 49160 | tf_op jit(solution)/shard_map/ppermute | solution.py:49
  113.1 5.4 %collective-permute-start.20 = (f32[8,16,1]{2,1,0:T(8,128)S(1)}, f32[8,16,1]{2,1,0:T(8,128)}, u32[]{:S(2)}, u32[]{:S(2)}) collective-permute-start(f32[8,16,1]{2,1,0:T(8,128)S(1)} %slice_select_fusion.1), channel_id=1, source_target_pairs={{0,1},{1,0},{2,3},{3,2},{4,5},{5,4},{6,7},{7,6},{8,9},{9,8},{10,11... | collective-permute-start | bytes 1544 | tf_op jit(solution)/shard_map/ppermute | solution.py:46
  121.9 3.6 %collective-permute-start.25 = (f32[256]{0:T(256)S(1)}, f32[256]{0:T(256)S(1)}, u32[]{:S(2)}, u32[]{:S(2)}) collective-permute-start(f32[256]{0:T(256)S(1)} %dynamic-slice_subtract_fusion.1), channel_id=1, source_target_pairs={{0,1},{1,0},{2,3},{3,2},{4,5},{5,4},{6,7},{7,6},{8,9},{9,8},{10,11... | collective-permute-start | bytes 3080 | tf_op jit(solution)/shard_map/ppermute | solution.py:119
  131.7 4.3 %collective-permute-start.23 = (f32[8,16,1]{2,1,0:T(8,128)S(1)}, f32[8,16,1]{2,1,0:T(8,128)S(1)}, u32[]{:S(2)}, u32[]{:S(2)}) collective-permute-start(f32[8,16,1]{2,1,0:T(8,128)S(1)} %slice_select_fusion), channel_id=1, source_target_pairs={{0,1},{1,0},{2,3},{3,2},{4,5},{5,4},{6,7},{7,6},{8,9},{9,8},{10,11... | collective-permute-start | bytes 1544 | tf_op jit(solution)/shard_map/ppermute | solution.py:46
  132.4 3.6 %collective-permute-start.22 = (f32[8,1,512]{2,1,0:T(1,128)S(1)}, f32[8,1,512]{2,1,0:T(1,128)S(1)}, u32[]{:S(2)}, u32[]{:S(2)}) collective-permute-start(f32[8,1,512]{2,1,0:T(1,128)S(1)} %get-tuple-element.30), channel_id=1, source_target_pairs={{0,8},{8,16},{16,24},{24,2},{2,10},{10,18},{18,26},{26,4},{4,12},{... | collective-permute-start | bytes 49160 | tf_op jit(solution)/shard_map/ppermute | solution.py:49
  133.7 4.0 %collective-permute-start.21 = (f32[8,1,512]{2,1,0:T(1,128)S(1)}, f32[8,1,512]{2,1,0:T(1,128)S(1)}, u32[]{:S(2)}, u32[]{:S(2)}) collective-permute-start(f32[8,1,512]{2,1,0:T(1,128)S(1)} %get-tuple-element.31), channel_id=1, source_target_pairs={{8,0},{16,8},{24,16},{2,24},{10,2},{18,10},{26,18},{4,26},{12,4},{... | collective-permute-start | bytes 49160 | tf_op jit(solution)/shard_map/ppermute | solution.py:50
  138.6 3.6 %collective-permute-start.27 = (f32[512]{0:T(512)S(1)}, f32[512]{0:T(512)S(1)}, u32[]{:S(2)}, u32[]{:S(2)}) collective-permute-start(f32[512]{0:T(512)S(1)} %pad_maximum_fusion.7), channel_id=1, source_target_pairs={{0,1},{1,0},{2,3},{3,2},{4,5},{5,4},{6,7},{7,6},{8,9},{9,8},{10,11... | collective-permute-start | bytes 6152 | tf_op jit(solution)/shard_map/ppermute | solution.py:119
  142.6 7.3 %collective-permute-start.28 = (f32[512]{0:T(512)S(1)}, f32[512]{0:T(512)S(1)}, u32[]{:S(2)}, u32[]{:S(2)}) collective-permute-start(f32[512]{0:T(512)S(1)} %pad_maximum_fusion.8), channel_id=1, source_target_pairs={{0,1},{1,0},{2,3},{3,2},{4,5},{5,4},{6,7},{7,6},{8,9},{9,8},{10,11... | collective-permute-start | bytes 6152 | tf_op jit(solution)/shard_map/ppermute | solution.py:119
  144.9 14.2 %all-to-all-start.2 = ((f32[2,8,16,512]{3,2,0,1:T(8,128)}), f32[2,8,16,512]{3,2,0,1:T(8,128)S(1)}, u32[]{:S(2)}, u32[]{:S(2)}) async-start(f32[2,8,16,512]{3,2,0,1:T(8,128)} %pad_maximum_fusion.1), calls=%async_computation.2 | async-start | bytes 1048576 | tf_op jit(solution)/shard_map/all_to_all | solution.py:260
  150.2 3.7 %collective-permute-start.29 = (f32[1024]{0:T(1024)S(1)}, f32[1024]{0:T(1024)S(1)}, u32[]{:S(2)}, u32[]{:S(2)}) collective-permute-start(f32[1024]{0:T(1024)S(1)} %pad_maximum_fusion.4), channel_id=1, source_target_pairs={{0,1},{1,0},{2,3},{3,2},{4,5},{5,4},{6,7},{7,6},{8,9},{9,8},{10,11... | collective-permute-start | bytes 12296 | tf_op jit(solution)/shard_map/ppermute | solution.py:119
  (32 other events, 418.0 us)

commit v18 on v12

--- a/solution.py
+++ b/solution.py
@@ -112,7 +112,7 @@
     slot = (tile_row % own_rows) * own_cols + tile_col % own_cols
     pick_device = (device[:, None] == jnp.arange(count, dtype=jnp.int32)[None, :]).astype(jnp.float32)
     pick_slot = (slot[:, None] == jnp.arange(tiles.size, dtype=jnp.int32)[None, :]).astype(jnp.float32)
-    return jnp.sum(jnp.dot(pick_device, got, precision=highest) * pick_slot, axis=1)
+    return jnp.sum(jnp.dot(pick_device, got, precision=solve_precision) * pick_slot, axis=1)
 
 
 def swap_col(value):
@@ -253,13 +253,13 @@
             ports = coarse_pair(rhs, pivots, coupling, total)
         else:
             ports = coarse(rhs, pivots, coupling)
-        tile_values = jnp.dot(scatter_ring, ports.reshape(-1), precision=highest).reshape(own_rows + 2, own_cols + 2)
+        tile_values = jnp.dot(scatter_ring, ports.reshape(-1), precision=solve_precision).reshape(own_rows + 2, own_cols + 2)
         ring = expand(expand(tile_values, True).T, True).T * prolong_scale
         centre = ring[1:-1, 1:-1]
         lifted = jnp.broadcast_to(centre[None], (local_layers, grid_rows, grid_cols))
         if outer == ITERS - 1 and drop is not None:
             both = lax.all_to_all(jnp.stack((drop, total)), "layer", 1, 2, tiled=True)
-            given_values = jnp.dot(given_pick, ports.reshape(-1), precision=highest).reshape(given_rows, given_cols)
+            given_values = jnp.dot(given_pick, ports.reshape(-1), precision=solve_precision).reshape(given_rows, given_cols)
             given_field = jnp.repeat(jnp.repeat(given_values, TILE, axis=0), TILE, axis=1) * prolong_scale
             given_lifted = jnp.broadcast_to(given_field[None], both.shape[1:])
             return ((both[0] + given_lifted) + both[1], ports)

time: 157 us -> 157 us (level)
  transfers between devices with their start and end apart: 35 -> 35, of which waited for: 21 -> 22; matrix products, arithmetic and copies ran while one was open for 13% -> 13% of each run, Pallas kernels for 0% -> 0%
where the time goes in v18:
time: 157 us; the launch traced here: 156 us
  starting transfers between devices  70.5 us (45%)
  waiting for transfers between devices  48.9 us (31%)
  local copies, waits for them, and re-layouts  11.9 us (8%)
  other arithmetic  11.4 us (7%)
  matrix products  11.3 us (7%)
    ppermute x12, waiting for transfers between devices, swap_col(): return lax.ppermute(value, 'col', [(0, 1), (1, 0)])  25.9 us
    ppermute x6, starting transfers between devices, rims(): lax.ppermute(tail, axis, [(place[i], place[i + 1]) for i in range(count -...  21 us
    all_to_all x2, starting transfers between devices, share_tiles(): got = lax.all_to_all(payload, ('layer', 'row', 'col'), 0, 0, tiled=True)  13.9 us
    ppermute x12, starting transfers between devices, swap_col(): return lax.ppermute(value, 'col', [(0, 1), (1, 0)])  9.25 us
    ppermute x6, starting transfers between devices, rims(): lax.ppermute(head, axis, [(place[i + 1], place[i]) for i in range(count -...  7.75 us
    all_to_all x2, waiting for transfers between devices, share_tiles(): got = lax.all_to_all(payload, ('layer', 'row', 'col'), 0, 0, tiled=True)  6.2 us
    ppermute x6, starting transfers between devices, rims(): got = lax.ppermute(jnp.where(low, tail, head), axis, [(0, 1), (1, 0)])  5.9 us
    all_to_all x1, starting transfers between devices, shards(): both = lax.all_to_all(jnp.stack((drop, total)), 'layer', 1, 2, tiled=True)  4.97 us
  transfers between devices with their start and end apart: 35, of which 22 were waited for; matrix products, arithmetic and copies ran while one was open for 13% of the time, Pallas kernels for 0%

profile of v18, /device:TPU:0, one launch (start us, length us, event | category | flops | bytes accessed | tf_op | source)
XLA Modules:
  0.0 155.5 jit_solution(5909698155078172328)
XLA Ops:
  0.6 1.9 %copy.34 = f32[2,64,512]{2,0,1:T(2,128)} copy(f32[2,64,512]{2,1,0:T(8,128)} %param.8) | data formatting | bytes 524288 | tf_op args[0]
  2.5 4.2 %all-to-all-start = ((f32[2,64,512]{2,0,1:T(2,128)}), f32[2,64,512]{2,0,1:T(2,128)S(1)}, u32[]{:S(2)}, u32[]{:S(2)}) async-start(f32[2,64,512]{2,0,1:T(2,128)} %copy.34), calls=%async_computation | async-start | bytes 524288 | tf_op jit(solution)/shard_map/all_to_all | solution.py:201
  8.8 4.0 %all-to-all-done = f32[2,64,512]{2,0,1:T(2,128)S(1)} async-done(((f32[2,64,512]{2,0,1:T(2,128)}), f32[2,64,512]{2,0,1:T(2,128)S(1)}, u32[]{:S(2)}, u32[]{:S(2)}) %all-to-all-start) | async-done | bytes 262176 | tf_op jit(solution)/shard_map/all_to_all | solution.py:201
  13.7 5.5 %all-to-all-start.1 = ((f32[32,1,32]{2,1,0:T(1,128)}), f32[32,1,32]{2,1,0:T(1,128)S(1)}, u32[]{:S(2)}, u32[]{:S(2)}) async-start(f32[32,1,32]{2,1,0:T(1,128)} %broadcast_in_dim.29), calls=%async_computation.1 | async-start | bytes 32768 | tf_op jit(solution)/shard_map/all_to_all | solution.py:107
  20.5 5.8 %all-to-all-done.1 = f32[32,1,32]{2,1,0:T(1,128)S(1)} async-done(((f32[32,1,32]{2,1,0:T(1,128)}), f32[32,1,32]{2,1,0:T(1,128)S(1)}, u32[]{:S(2)}, u32[]{:S(2)}) %all-to-all-start.1) | async-done | bytes 4128 | tf_op jit(solution)/shard_map/all_to_all | solution.py:107
  26.3 3.5 %all-to-all-start.2 = ((f32[2,2,64,512]{3,1,0,2:T(2,128)}), f32[2,2,64,512]{3,1,0,2:T(2,128)S(1)}, u32[]{:S(2)}, u32[]{:S(2)}) async-start(f32[2,2,64,512]{3,1,0,2:T(2,128)} %copy.35), calls=%async_computation.2 | async-start | bytes 1048576 | tf_op jit(solution)/shard_map/all_to_all | solution.py:199
  32.5 2.1 %collective-permute-done = f32[256]{0:T(256)S(1)} collective-permute-done((f32[256]{0:T(256)S(1)}, f32[256]{0:T(256)S(1)}, u32[]{:S(2)}, u32[]{:S(2)}) %collective-permute-start) | collective-permute-done | bytes 1056 | tf_op jit(solution)/shard_map/ppermute | solution.py:119
  36.9 1.6 %collective-permute-done.1 = f32[256]{0:T(256)S(1)} collective-permute-done((f32[256]{0:T(256)S(1)}, f32[256]{0:T(256)S(1)}, u32[]{:S(2)}, u32[]{:S(2)}) %collective-permute-start.1) | collective-permute-done | bytes 1056 | tf_op jit(solution)/shard_map/ppermute | solution.py:119
  39.9 2.6 %collective-permute-done.2 = f32[256]{0:T(256)S(1)} collective-permute-done((f32[256]{0:T(256)S(1)}, f32[256]{0:T(256)S(1)}, u32[]{:S(2)}, u32[]{:S(2)}) %collective-permute-start.2) | collective-permute-done | bytes 1056 | tf_op jit(solution)/shard_map/ppermute | solution.py:119
  44.1 2.7 %collective-permute-done.3 = f32[512]{0:T(512)S(1)} collective-permute-done((f32[512]{0:T(512)S(1)}, f32[512]{0:T(512)S(1)}, u32[]{:S(2)}, u32[]{:S(2)}) %collective-permute-start.3) | collective-permute-done | bytes 2080 | tf_op jit(solution)/shard_map/ppermute | solution.py:119
  47.8 3.0 %collective-permute-done.4 = f32[512]{0:T(512)S(1)} collective-permute-done((f32[512]{0:T(512)S(1)}, f32[512]{0:T(512)S(1)}, u32[]{:S(2)}, u32[]{:S(2)}) %collective-permute-start.4) | collective-permute-done | bytes 2080 | tf_op jit(solution)/shard_map/ppermute | solution.py:119
  51.8 3.0 %collective-permute-done.5 = f32[1024]{0:T(1024)S(1)} collective-permute-done((f32[1024]{0:T(1024)S(1)}, f32[1024]{0:T(1024)S(1)}, u32[]{:S(2)}, u32[]{:S(2)}) %collective-permute-start.5) | collective-permute-done | bytes 4128 | tf_op jit(solution)/shard_map/ppermute | solution.py:119
  60.4 3.5 %collective-permute-done.8 = f32[8,16,1]{2,1,0:T(8,128)S(1)} collective-permute-done((f32[8,16,1]{2,1,0:T(8,128)S(1)}, f32[8,16,1]{2,1,0:T(8,128)S(1)}, u32[]{:S(2)}, u32[]{:S(2)}) %collective-permute-start.8) | collective-permute-done | bytes 544 | tf_op jit(solution)/shard_map/ppermute | solution.py:46
  66.9 4.4 %collective-permute-start.10 = (f32[8,1,512]{2,1,0:T(1,128)S(1)}, f32[8,1,512]{2,1,0:T(1,128)S(1)}, u32[]{:S(2)}, u32[]{:S(2)}) collective-permute-start(f32[8,1,512]{2,1,0:T(1,128)S(1)} %get-tuple-element.61), channel_id=1, source_target_pairs={{0,8},{8,16},{16,24},{24,2},{2,10},{10,18},{18,26},{26,4},{4,12},{... | collective-permute-start | bytes 49160 | tf_op jit(solution)/shard_map/ppermute | solution.py:49
  73.0 1.5 collective-permute-start.14
  75.8 5.4 %collective-permute-start.13 = (f32[8,1,512]{2,1,0:T(1,128)S(1)}, f32[8,1,512]{2,1,0:T(1,128)S(1)}, u32[]{:S(2)}, u32[]{:S(2)}) collective-permute-start(f32[8,1,512]{2,1,0:T(1,128)S(1)} %get-tuple-element.53), channel_id=1, source_target_pairs={{0,8},{8,16},{16,24},{24,2},{2,10},{10,18},{18,26},{26,4},{4,12},{... | collective-permute-start | bytes 49160 | tf_op jit(solution)/shard_map/ppermute | solution.py:49
  85.7 4.9 %collective-permute-start.16 = (f32[8,1,512]{2,1,0:T(1,128)S(1)}, f32[8,1,512]{2,1,0:T(1,128)S(1)}, u32[]{:S(2)}, u32[]{:S(2)}) collective-permute-start(f32[8,1,512]{2,1,0:T(1,128)S(1)} %get-tuple-element.45), channel_id=1, source_target_pairs={{0,8},{8,16},{16,24},{24,2},{2,10},{10,18},{18,26},{26,4},{4,12},{... | collective-permute-start | bytes 49160 | tf_op jit(solution)/shard_map/ppermute | solution.py:49
  95.9 8.4 %all-to-all-start.4 = ((f32[32,1,32]{2,1,0:T(1,128)}), f32[32,1,32]{2,1,0:T(1,128)}, u32[]{:S(2)}, u32[]{:S(2)}) async-start(f32[32,1,32]{2,1,0:T(1,128)} %broadcast_in_dim.37), calls=%async_computation.4 | async-start | bytes 32768 | tf_op jit(solution)/shard_map/all_to_all | solution.py:107
  105.7 3.6 %collective-permute-start.19 = (f32[8,1,512]{2,1,0:T(1,128)}, f32[8,1,512]{2,1,0:T(1,128)}, u32[]{:S(2)}, u32[]{:S(2)}) collective-permute-start(f32[8,1,512]{2,1,0:T(1,128)} %get-tuple-element.37), channel_id=1, source_target_pairs={{0,8},{8,16},{16,24},{24,2},{2,10},{10,18},{18,26},{26,4},{4,12},{... | collective-permute-start | bytes 49160 | tf_op jit(solution)/shard_map/ppermute | solution.py:49
  109.3 1.7 %collective-permute-start.20 = (f32[8,16,1]{2,1,0:T(8,128)S(1)}, f32[8,16,1]{2,1,0:T(8,128)}, u32[]{:S(2)}, u32[]{:S(2)}) collective-permute-start(f32[8,16,1]{2,1,0:T(8,128)S(1)} %slice_select_fusion.1), channel_id=1, source_target_pairs={{0,1},{1,0},{2,3},{3,2},{4,5},{5,4},{6,7},{7,6},{8,9},{9,8},{10,11... | collective-permute-start | bytes 1544 | tf_op jit(solution)/shard_map/ppermute | solution.py:46
  111.4 1.6 %fusion.1 = f32[2048]{0:T(1024)S(1)} fusion(f32[32,32]{1,0:T(8,128)} %bitcast.56, s32[2048]{0:T(1024)} %copy-done.19, s32[2048]{0:T(1024)S(1)} %copy-done.18), kind=kOutput, calls=%fused_computation.3 | convolution fusion | flops 12843008 | bytes 28672 | tf_op jit(solution)/shard_map/dot_general | solution.py:115
  115.2 1.9 %collective-permute-done.24 = f32[256]{0:T(256)S(1)} collective-permute-done((f32[256]{0:T(256)S(1)}, f32[256]{0:T(256)S(1)}, u32[]{:S(2)}, u32[]{:S(2)}) %collective-permute-start.24) | collective-permute-done | bytes 1056 | tf_op jit(solution)/shard_map/ppermute | solution.py:119
  119.5 1.6 %collective-permute-done.25 = f32[256]{0:T(256)S(1)} collective-permute-done((f32[256]{0:T(256)S(1)}, f32[256]{0:T(256)S(1)}, u32[]{:S(2)}, u32[]{:S(2)}) %collective-permute-start.25) | collective-permute-done | bytes 1056 | tf_op jit(solution)/shard_map/ppermute | solution.py:119
  122.4 2.6 %collective-permute-done.26 = f32[256]{0:T(256)S(1)} collective-permute-done((f32[256]{0:T(256)S(1)}, f32[256]{0:T(256)S(1)}, u32[]{:S(2)}, u32[]{:S(2)}) %collective-permute-start.26) | collective-permute-done | bytes 1056 | tf_op jit(solution)/shard_map/ppermute | solution.py:119
  125.5 1.5 fusion.170
  131.7 1.6 %collective-permute-done.21 = f32[8,1,512]{2,1,0:T(1,128)S(1)} collective-permute-done((f32[8,1,512]{2,1,0:T(1,128)S(1)}, f32[8,1,512]{2,1,0:T(1,128)S(1)}, u32[]{:S(2)}, u32[]{:S(2)}) %collective-permute-start.21) | collective-permute-done | bytes 16416 | tf_op jit(solution)/shard_map/ppermute | solution.py:50
  134.2 1.5 collective-permute-start.27
  136.0 1.8 %collective-permute-done.27 = f32[512]{0:T(512)S(1)} collective-permute-done((f32[512]{0:T(512)S(1)}, f32[512]{0:T(512)S(1)}, u32[]{:S(2)}, u32[]{:S(2)}) %collective-permute-start.27) | collective-permute-done | bytes 2080 | tf_op jit(solution)/shard_map/ppermute | solution.py:119
  138.2 1.5 collective-permute-start.28
  140.5 5.0 %all-to-all-start.3 = ((f32[2,8,16,512]{3,2,0,1:T(8,128)}), f32[2,8,16,512]{3,2,0,1:T(8,128)S(1)}, u32[]{:S(2)}, u32[]{:S(2)}) async-start(f32[2,8,16,512]{3,2,0,1:T(8,128)} %pad_maximum_fusion.1), calls=%async_computation.3 | async-start | bytes 1048576 | tf_op jit(solution)/shard_map/all_to_all | solution.py:261
  146.4 3.0 %collective-permute-done.29 = f32[1024]{0:T(1024)S(1)} collective-permute-done((f32[1024]{0:T(1024)S(1)}, f32[1024]{0:T(1024)S(1)}, u32[]{:S(2)}, u32[]{:S(2)}) %collective-permute-start.29) | collective-permute-done | bytes 4128 | tf_op jit(solution)/shard_map/ppermute | solution.py:119
  150.6 4.1 %all-to-all-done.3 = f32[2,8,16,512]{3,2,0,1:T(8,128)S(1)} async-done(((f32[2,8,16,512]{3,2,0,1:T(8,128)}), f32[2,8,16,512]{3,2,0,1:T(8,128)S(1)}, u32[]{:S(2)}, u32[]{:S(2)}) %all-to-all-start.3) | async-done | bytes 524320 | tf_op jit(solution)/shard_map/all_to_all | solution.py:261
  (234 shorter events, 53.0 us)
Async XLA Ops:
  2.5 10.2 %all-to-all-start = ((f32[2,64,512]{2,0,1:T(2,128)}), f32[2,64,512]{2,0,1:T(2,128)S(1)}, u32[]{:S(2)}, u32[]{:S(2)}) async-start(f32[2,64,512]{2,0,1:T(2,128)} %copy.34), calls=%async_computation | async-start | bytes 524288 | tf_op jit(solution)/shard_map/all_to_all | solution.py:201
  13.7 12.6 %all-to-all-start.1 = ((f32[32,1,32]{2,1,0:T(1,128)}), f32[32,1,32]{2,1,0:T(1,128)S(1)}, u32[]{:S(2)}, u32[]{:S(2)}) async-start(f32[32,1,32]{2,1,0:T(1,128)} %broadcast_in_dim.29), calls=%async_computation.1 | async-start | bytes 32768 | tf_op jit(solution)/shard_map/all_to_all | solution.py:107
  26.3 30.3 %all-to-all-start.2 = ((f32[2,2,64,512]{3,1,0,2:T(2,128)}), f32[2,2,64,512]{3,1,0,2:T(2,128)S(1)}, u32[]{:S(2)}, u32[]{:S(2)}) async-start(f32[2,2,64,512]{3,1,0,2:T(2,128)} %copy.35), calls=%async_computation.2 | async-start | bytes 1048576 | tf_op jit(solution)/shard_map/all_to_all | solution.py:199
  31.0 3.6 %collective-permute-start = (f32[256]{0:T(256)S(1)}, f32[256]{0:T(256)S(1)}, u32[]{:S(2)}, u32[]{:S(2)}) collective-permute-start(f32[256]{0:T(256)S(1)} %dynamic-slice_subtract_fusion.5), channel_id=1, source_target_pairs={{0,1},{1,0},{2,3},{3,2},{4,5},{5,4},{6,7},{7,6},{8,9},{9,8},{10,11... | collective-permute-start | bytes 3080 | tf_op jit(solution)/shard_map/ppermute | solution.py:119
  35.0 3.6 %collective-permute-start.1 = (f32[256]{0:T(256)S(1)}, f32[256]{0:T(256)S(1)}, u32[]{:S(2)}, u32[]{:S(2)}) collective-permute-start(f32[256]{0:T(256)S(1)} %dynamic-slice_subtract_fusion.4), channel_id=1, source_target_pairs={{0,1},{1,0},{2,3},{3,2},{4,5},{5,4},{6,7},{7,6},{8,9},{9,8},{10,11... | collective-permute-start | bytes 3080 | tf_op jit(solution)/shard_map/ppermute | solution.py:119
  38.9 3.6 %collective-permute-start.2 = (f32[256]{0:T(256)S(1)}, f32[256]{0:T(256)S(1)}, u32[]{:S(2)}, u32[]{:S(2)}) collective-permute-start(f32[256]{0:T(256)S(1)} %dynamic-slice_subtract_fusion.3), channel_id=1, source_target_pairs={{0,1},{1,0},{2,3},{3,2},{4,5},{5,4},{6,7},{7,6},{8,9},{9,8},{10,11... | collective-permute-start | bytes 3080 | tf_op jit(solution)/shard_map/ppermute | solution.py:119
  43.2 3.6 %collective-permute-start.3 = (f32[512]{0:T(512)S(1)}, f32[512]{0:T(512)S(1)}, u32[]{:S(2)}, u32[]{:S(2)}) collective-permute-start(f32[512]{0:T(512)S(1)} %pad_maximum_fusion.5), channel_id=1, source_target_pairs={{0,1},{1,0},{2,3},{3,2},{4,5},{5,4},{6,7},{7,6},{8,9},{9,8},{10,11... | collective-permute-start | bytes 6152 | tf_op jit(solution)/shard_map/ppermute | solution.py:119
  47.2 3.6 %collective-permute-start.4 = (f32[512]{0:T(512)S(1)}, f32[512]{0:T(512)S(1)}, u32[]{:S(2)}, u32[]{:S(2)}) collective-permute-start(f32[512]{0:T(512)S(1)} %pad_maximum_fusion.6), channel_id=1, source_target_pairs={{0,1},{1,0},{2,3},{3,2},{4,5},{5,4},{6,7},{7,6},{8,9},{9,8},{10,11... | collective-permute-start | bytes 6152 | tf_op jit(solution)/shard_map/ppermute | solution.py:119
  51.1 3.7 %collective-permute-start.5 = (f32[1024]{0:T(1024)S(1)}, f32[1024]{0:T(1024)S(1)}, u32[]{:S(2)}, u32[]{:S(2)}) collective-permute-start(f32[1024]{0:T(1024)S(1)} %pad_maximum_fusion.3), channel_id=1, source_target_pairs={{0,1},{1,0},{2,3},{3,2},{4,5},{5,4},{6,7},{7,6},{8,9},{9,8},{10,11... | collective-permute-start | bytes 12296 | tf_op jit(solution)/shard_map/ppermute | solution.py:119
  57.0 6.9 %collective-permute-start.7 = (f32[8,1,512]{2,1,0:T(1,128)S(1)}, f32[8,1,512]{2,1,0:T(1,128)S(1)}, u32[]{:S(2)}, u32[]{:S(2)}) collective-permute-start(f32[8,1,512]{2,1,0:T(1,128)S(1)} %get-tuple-element.66), channel_id=1, source_target_pairs={{0,8},{8,16},{16,24},{24,2},{2,10},{10,18},{18,26},{26,4},{4,12},{... | collective-permute-start | bytes 49160 | tf_op jit(solution)/shard_map/ppermute | solution.py:49
  58.3 5.7 %collective-permute-start.6 = (f32[8,1,512]{2,1,0:T(1,128)S(1)}, f32[8,1,512]{2,1,0:T(1,128)S(1)}, u32[]{:S(2)}, u32[]{:S(2)}) collective-permute-start(f32[8,1,512]{2,1,0:T(1,128)S(1)} %get-tuple-element.67), channel_id=1, source_target_pairs={{8,0},{16,8},{24,16},{2,24},{10,2},{18,10},{26,18},{4,26},{12,4},{... | collective-permute-start | bytes 49160 | tf_op jit(solution)/shard_map/ppermute | solution.py:50
  59.6 4.3 %collective-permute-start.8 = (f32[8,16,1]{2,1,0:T(8,128)S(1)}, f32[8,16,1]{2,1,0:T(8,128)S(1)}, u32[]{:S(2)}, u32[]{:S(2)}) collective-permute-start(f32[8,16,1]{2,1,0:T(8,128)S(1)} %slice_select_fusion.5), channel_id=1, source_target_pairs={{0,1},{1,0},{2,3},{3,2},{4,5},{5,4},{6,7},{7,6},{8,9},{9,8},{10,11... | collective-permute-start | bytes 1544 | tf_op jit(solution)/shard_map/ppermute | solution.py:46
  64.9 6.5 %collective-permute-start.11 = (f32[8,16,1]{2,1,0:T(8,128)S(1)}, f32[8,16,1]{2,1,0:T(8,128)S(1)}, u32[]{:S(2)}, u32[]{:S(2)}) collective-permute-start(f32[8,16,1]{2,1,0:T(8,128)S(1)} %slice_select_fusion.4), channel_id=1, source_target_pairs={{0,1},{1,0},{2,3},{3,2},{4,5},{5,4},{6,7},{7,6},{8,9},{9,8},{10,11... | collective-permute-start | bytes 1544 | tf_op jit(solution)/shard_map/ppermute | solution.py:46
  65.6 5.8 %collective-permute-start.9 = (f32[8,1,512]{2,1,0:T(1,128)S(1)}, f32[8,1,512]{2,1,0:T(1,128)S(1)}, u32[]{:S(2)}, u32[]{:S(2)}) collective-permute-start(f32[8,1,512]{2,1,0:T(1,128)S(1)} %get-tuple-element.60), channel_id=1, source_target_pairs={{8,0},{16,8},{24,16},{2,24},{10,2},{18,10},{26,18},{4,26},{12,4},{... | collective-permute-start | bytes 49160 | tf_op jit(solution)/shard_map/ppermute | solution.py:50
  66.9 5.3 %collective-permute-start.10 = (f32[8,1,512]{2,1,0:T(1,128)S(1)}, f32[8,1,512]{2,1,0:T(1,128)S(1)}, u32[]{:S(2)}, u32[]{:S(2)}) collective-permute-start(f32[8,1,512]{2,1,0:T(1,128)S(1)} %get-tuple-element.61), channel_id=1, source_target_pairs={{0,8},{8,16},{16,24},{24,2},{2,10},{10,18},{18,26},{26,4},{4,12},{... | collective-permute-start | bytes 49160 | tf_op jit(solution)/shard_map/ppermute | solution.py:49
  73.0 8.3 %collective-permute-start.14 = (f32[8,16,1]{2,1,0:T(8,128)S(1)}, f32[8,16,1]{2,1,0:T(8,128)S(1)}, u32[]{:S(2)}, u32[]{:S(2)}) collective-permute-start(f32[8,16,1]{2,1,0:T(8,128)S(1)} %slice_select_fusion.3), channel_id=1, source_target_pairs={{0,1},{1,0},{2,3},{3,2},{4,5},{5,4},{6,7},{7,6},{8,9},{9,8},{10,11... | collective-permute-start | bytes 1544 | tf_op jit(solution)/shard_map/ppermute | solution.py:46
  74.5 6.8 %collective-permute-start.12 = (f32[8,1,512]{2,1,0:T(1,128)S(1)}, f32[8,1,512]{2,1,0:T(1,128)S(1)}, u32[]{:S(2)}, u32[]{:S(2)}) collective-permute-start(f32[8,1,512]{2,1,0:T(1,128)S(1)} %get-tuple-element.52), channel_id=1, source_target_pairs={{8,0},{16,8},{24,16},{2,24},{10,2},{18,10},{26,18},{4,26},{12,4},{... | collective-permute-start | bytes 49160 | tf_op jit(solution)/shard_map/ppermute | solution.py:50
  75.8 6.3 %collective-permute-start.13 = (f32[8,1,512]{2,1,0:T(1,128)S(1)}, f32[8,1,512]{2,1,0:T(1,128)S(1)}, u32[]{:S(2)}, u32[]{:S(2)}) collective-permute-start(f32[8,1,512]{2,1,0:T(1,128)S(1)} %get-tuple-element.53), channel_id=1, source_target_pairs={{0,8},{8,16},{16,24},{24,2},{2,10},{10,18},{18,26},{26,4},{4,12},{... | collective-permute-start | bytes 49160 | tf_op jit(solution)/shard_map/ppermute | solution.py:49
  83.7 6.9 %collective-permute-start.17 = (f32[8,16,1]{2,1,0:T(8,128)S(1)}, f32[8,16,1]{2,1,0:T(8,128)S(1)}, u32[]{:S(2)}, u32[]{:S(2)}) collective-permute-start(f32[8,16,1]{2,1,0:T(8,128)S(1)} %slice_select_fusion.2), channel_id=1, source_target_pairs={{0,1},{1,0},{2,3},{3,2},{4,5},{5,4},{6,7},{7,6},{8,9},{9,8},{10,11... | collective-permute-start | bytes 1544 | tf_op jit(solution)/shard_map/ppermute | solution.py:46
  84.4 6.2 %collective-permute-start.15 = (f32[8,1,512]{2,1,0:T(1,128)S(1)}, f32[8,1,512]{2,1,0:T(1,128)S(1)}, u32[]{:S(2)}, u32[]{:S(2)}) collective-permute-start(f32[8,1,512]{2,1,0:T(1,128)S(1)} %get-tuple-element.44), channel_id=1, source_target_pairs={{8,0},{16,8},{24,16},{2,24},{10,2},{18,10},{26,18},{4,26},{12,4},{... | collective-permute-start | bytes 49160 | tf_op jit(solution)/shard_map/ppermute | solution.py:50
  85.7 5.7 %collective-permute-start.16 = (f32[8,1,512]{2,1,0:T(1,128)S(1)}, f32[8,1,512]{2,1,0:T(1,128)S(1)}, u32[]{:S(2)}, u32[]{:S(2)}) collective-permute-start(f32[8,1,512]{2,1,0:T(1,128)S(1)} %get-tuple-element.45), channel_id=1, source_target_pairs={{0,8},{8,16},{16,24},{24,2},{2,10},{10,18},{18,26},{26,4},{4,12},{... | collective-permute-start | bytes 49160 | tf_op jit(solution)/shard_map/ppermute | solution.py:49
  95.9 15.5 %all-to-all-start.4 = ((f32[32,1,32]{2,1,0:T(1,128)}), f32[32,1,32]{2,1,0:T(1,128)}, u32[]{:S(2)}, u32[]{:S(2)}) async-start(f32[32,1,32]{2,1,0:T(1,128)} %broadcast_in_dim.37), calls=%async_computation.4 | async-start | bytes 32768 | tf_op jit(solution)/shard_map/all_to_all | solution.py:107
  104.4 21.0 %collective-permute-start.18 = (f32[8,1,512]{2,1,0:T(1,128)}, f32[8,1,512]{2,1,0:T(1,128)S(1)}, u32[]{:S(2)}, u32[]{:S(2)}) collective-permute-start(f32[8,1,512]{2,1,0:T(1,128)} %get-tuple-element.36), channel_id=1, source_target_pairs={{8,0},{16,8},{24,16},{2,24},{10,2},{18,10},{26,18},{4,26},{12,4},{... | collective-permute-start | bytes 49160 | tf_op jit(solution)/shard_map/ppermute | solution.py:50
  105.7 19.7 %collective-permute-start.19 = (f32[8,1,512]{2,1,0:T(1,128)}, f32[8,1,512]{2,1,0:T(1,128)}, u32[]{:S(2)}, u32[]{:S(2)}) collective-permute-start(f32[8,1,512]{2,1,0:T(1,128)} %get-tuple-element.37), channel_id=1, source_target_pairs={{0,8},{8,16},{16,24},{24,2},{2,10},{10,18},{18,26},{26,4},{4,12},{... | collective-permute-start | bytes 49160 | tf_op jit(solution)/shard_map/ppermute | solution.py:49
  109.3 5.0 %collective-permute-start.20 = (f32[8,16,1]{2,1,0:T(8,128)S(1)}, f32[8,16,1]{2,1,0:T(8,128)}, u32[]{:S(2)}, u32[]{:S(2)}) collective-permute-start(f32[8,16,1]{2,1,0:T(8,128)S(1)} %slice_select_fusion.1), channel_id=1, source_target_pairs={{0,1},{1,0},{2,3},{3,2},{4,5},{5,4},{6,7},{7,6},{8,9},{9,8},{10,11... | collective-permute-start | bytes 1544 | tf_op jit(solution)/shard_map/ppermute | solution.py:46
  127.3 4.3 %collective-permute-start.23 = (f32[8,16,1]{2,1,0:T(8,128)S(1)}, f32[8,16,1]{2,1,0:T(8,128)S(1)}, u32[]{:S(2)}, u32[]{:S(2)}) collective-permute-start(f32[8,16,1]{2,1,0:T(8,128)S(1)} %slice_select_fusion), channel_id=1, source_target_pairs={{0,1},{1,0},{2,3},{3,2},{4,5},{5,4},{6,7},{7,6},{8,9},{9,8},{10,11... | collective-permute-start | bytes 1544 | tf_op jit(solution)/shard_map/ppermute | solution.py:46
  128.0 3.6 %collective-permute-start.22 = (f32[8,1,512]{2,1,0:T(1,128)S(1)}, f32[8,1,512]{2,1,0:T(1,128)S(1)}, u32[]{:S(2)}, u32[]{:S(2)}) collective-permute-start(f32[8,1,512]{2,1,0:T(1,128)S(1)} %get-tuple-element.28), channel_id=1, source_target_pairs={{0,8},{8,16},{16,24},{24,2},{2,10},{10,18},{18,26},{26,4},{4,12},{... | collective-permute-start | bytes 49160 | tf_op jit(solution)/shard_map/ppermute | solution.py:49
  129.3 4.0 %collective-permute-start.21 = (f32[8,1,512]{2,1,0:T(1,128)S(1)}, f32[8,1,512]{2,1,0:T(1,128)S(1)}, u32[]{:S(2)}, u32[]{:S(2)}) collective-permute-start(f32[8,1,512]{2,1,0:T(1,128)S(1)} %get-tuple-element.29), channel_id=1, source_target_pairs={{8,0},{16,8},{24,16},{2,24},{10,2},{18,10},{26,18},{4,26},{12,4},{... | collective-permute-start | bytes 49160 | tf_op jit(solution)/shard_map/ppermute | solution.py:50
  134.2 3.6 %collective-permute-start.27 = (f32[512]{0:T(512)S(1)}, f32[512]{0:T(512)S(1)}, u32[]{:S(2)}, u32[]{:S(2)}) collective-permute-start(f32[512]{0:T(512)S(1)} %pad_maximum_fusion.7), channel_id=1, source_target_pairs={{0,1},{1,0},{2,3},{3,2},{4,5},{5,4},{6,7},{7,6},{8,9},{9,8},{10,11... | collective-permute-start | bytes 6152 | tf_op jit(solution)/shard_map/ppermute | solution.py:119
  138.2 7.3 %collective-permute-start.28 = (f32[512]{0:T(512)S(1)}, f32[512]{0:T(512)S(1)}, u32[]{:S(2)}, u32[]{:S(2)}) collective-permute-start(f32[512]{0:T(512)S(1)} %pad_maximum_fusion.8), channel_id=1, source_target_pairs={{0,1},{1,0},{2,3},{3,2},{4,5},{5,4},{6,7},{7,6},{8,9},{9,8},{10,11... | collective-permute-start | bytes 6152 | tf_op jit(solution)/shard_map/ppermute | solution.py:119
  140.5 14.2 %all-to-all-start.3 = ((f32[2,8,16,512]{3,2,0,1:T(8,128)}), f32[2,8,16,512]{3,2,0,1:T(8,128)S(1)}, u32[]{:S(2)}, u32[]{:S(2)}) async-start(f32[2,8,16,512]{3,2,0,1:T(8,128)} %pad_maximum_fusion.1), calls=%async_computation.3 | async-start | bytes 1048576 | tf_op jit(solution)/shard_map/all_to_all | solution.py:261
  145.8 3.7 %collective-permute-start.29 = (f32[1024]{0:T(1024)S(1)}, f32[1024]{0:T(1024)S(1)}, u32[]{:S(2)}, u32[]{:S(2)}) collective-permute-start(f32[1024]{0:T(1024)S(1)} %pad_maximum_fusion.4), channel_id=1, source_target_pairs={{0,1},{1,0},{2,3},{3,2},{4,5},{5,4},{6,7},{7,6},{8,9},{9,8},{10,11... | collective-permute-start | bytes 12296 | tf_op jit(solution)/shard_map/ppermute | solution.py:119
  (23 other events, 263.4 us)

commit v19 on v18

--- a/solution.py
+++ b/solution.py
@@ -201,18 +201,20 @@
     sources = lax.all_to_all(sources, "layer", 1, 0, tiled=True)
     local_layers, grid_rows, grid_cols = sources.shape
     pad_rows = lax.dynamic_slice_in_dim(pad_map, lax.axis_index("layer") * grid_rows, grid_rows, 0)
-    row_halo = rims(conduct, ROW_AXES, 1)
-    col_halo = rims(conduct, "col", 2)
-    layer_halo = rims(vertical, None, 0)
-    near_vert = neighbours(vertical, [layer_halo, row_halo, col_halo])
-    near_plane = neighbours(conduct, [layer_halo, row_halo, col_halo])
+    root_plane = jnp.sqrt(conduct)
+    root_vert = jnp.sqrt(vertical)
+    row_halo = rims(root_plane, ROW_AXES, 1)
+    col_halo = rims(root_plane, "col", 2)
+    layer_halo = rims(root_vert, None, 0)
+    near_vert = neighbours(root_vert, [layer_halo, row_halo, col_halo])
+    near_plane = neighbours(root_plane, [layer_halo, row_halo, col_halo])
     weights = (
-        jnp.sqrt(vertical * near_vert[0]),
-        jnp.sqrt(vertical * near_vert[1]),
-        jnp.sqrt(conduct * near_plane[2]),
-        jnp.sqrt(conduct * near_plane[3]),
-        jnp.sqrt(conduct * near_plane[4]),
-        jnp.sqrt(conduct * near_plane[5]),
+        root_vert * near_vert[0],
+        root_vert * near_vert[1],
+        root_plane * near_plane[2],
+        root_plane * near_plane[3],
+        root_plane * near_plane[4],
+        root_plane * near_plane[5],
     )
     top_layer = pad_gain * pad_rows.astype(jnp.float32)
     pad_term = jnp.concatenate(

time: 157 us -> 156 us (level)
  no operation moved by 1% of the time
where the time goes in v19:
time: 156 us; the launch traced here: 155 us
  starting transfers between devices  70.5 us (45%)
  waiting for transfers between devices  49 us (31%)
  local copies, waits for them, and re-layouts  12.1 us (8%)
  matrix products  11.3 us (7%)
  other arithmetic  11.1 us (7%)
  between operations  1.56 us (1%)
    ppermute x12, waiting for transfers between devices, swap_col(): return lax.ppermute(value, 'col', [(0, 1), (1, 0)])  25.9 us
    ppermute x6, starting transfers between devices, rims(): lax.ppermute(tail, axis, [(place[i], place[i + 1]) for i in range(count -...  21 us
    all_to_all x2, starting transfers between devices, share_tiles(): got = lax.all_to_all(payload, ('layer', 'row', 'col'), 0, 0, tiled=True)  13.9 us
    ppermute x12, starting transfers between devices, swap_col(): return lax.ppermute(value, 'col', [(0, 1), (1, 0)])  9.25 us
    ppermute x6, starting transfers between devices, rims(): lax.ppermute(head, axis, [(place[i + 1], place[i]) for i in range(count -...  7.75 us
    all_to_all x2, waiting for transfers between devices, share_tiles(): got = lax.all_to_all(payload, ('layer', 'row', 'col'), 0, 0, tiled=True)  6.2 us
    ppermute x6, starting transfers between devices, rims(): got = lax.ppermute(jnp.where(low, tail, head), axis, [(0, 1), (1, 0)])  5.9 us
    all_to_all x1, starting transfers between devices, shards(): both = lax.all_to_all(jnp.stack((drop, total)), 'layer', 1, 2, tiled=True)  4.97 us
  transfers between devices with their start and end apart: 35, of which 22 were waited for; matrix products, arithmetic and copies ran while one was open for 13% of the time, Pallas kernels for 0%

profile of v19, /device:TPU:0, one launch (start us, length us, event | category | flops | bytes accessed | tf_op | source)
XLA Modules:
  0.0 155.5 jit_solution(12809675660856463628)
XLA Ops:
  0.6 1.9 %copy.42 = f32[2,64,512]{2,0,1:T(2,128)} copy(f32[2,64,512]{2,1,0:T(8,128)} %param.8) | data formatting | bytes 524288 | tf_op args[0]
  2.5 4.2 %all-to-all-start = ((f32[2,64,512]{2,0,1:T(2,128)}), f32[2,64,512]{2,0,1:T(2,128)S(1)}, u32[]{:S(2)}, u32[]{:S(2)}) async-start(f32[2,64,512]{2,0,1:T(2,128)} %copy.42), calls=%async_computation | async-start | bytes 524288 | tf_op jit(solution)/shard_map/all_to_all | solution.py:201
  8.8 4.0 %all-to-all-done = f32[2,64,512]{2,0,1:T(2,128)S(1)} async-done(((f32[2,64,512]{2,0,1:T(2,128)}), f32[2,64,512]{2,0,1:T(2,128)S(1)}, u32[]{:S(2)}, u32[]{:S(2)}) %all-to-all-start) | async-done | bytes 262176 | tf_op jit(solution)/shard_map/all_to_all | solution.py:201
  13.7 5.5 %all-to-all-start.1 = ((f32[32,1,32]{2,1,0:T(1,128)}), f32[32,1,32]{2,1,0:T(1,128)S(1)}, u32[]{:S(2)}, u32[]{:S(2)}) async-start(f32[32,1,32]{2,1,0:T(1,128)} %broadcast_in_dim.29), calls=%async_computation.1 | async-start | bytes 32768 | tf_op jit(solution)/shard_map/all_to_all | solution.py:107
  20.5 5.8 %all-to-all-done.1 = f32[32,1,32]{2,1,0:T(1,128)S(1)} async-done(((f32[32,1,32]{2,1,0:T(1,128)}), f32[32,1,32]{2,1,0:T(1,128)S(1)}, u32[]{:S(2)}, u32[]{:S(2)}) %all-to-all-start.1) | async-done | bytes 4128 | tf_op jit(solution)/shard_map/all_to_all | solution.py:107
  26.3 3.5 %all-to-all-start.2 = ((f32[2,2,64,512]{3,1,0,2:T(2,128)}), f32[2,2,64,512]{3,1,0,2:T(2,128)S(1)}, u32[]{:S(2)}, u32[]{:S(2)}) async-start(f32[2,2,64,512]{3,1,0,2:T(2,128)} %copy.43), calls=%async_computation.2 | async-start | bytes 1048576 | tf_op jit(solution)/shard_map/all_to_all | solution.py:199
  32.5 2.1 %collective-permute-done = f32[256]{0:T(256)S(1)} collective-permute-done((f32[256]{0:T(256)S(1)}, f32[256]{0:T(256)S(1)}, u32[]{:S(2)}, u32[]{:S(2)}) %collective-permute-start) | collective-permute-done | bytes 1056 | tf_op jit(solution)/shard_map/ppermute | solution.py:119
  36.9 1.6 %collective-permute-done.1 = f32[256]{0:T(256)S(1)} collective-permute-done((f32[256]{0:T(256)S(1)}, f32[256]{0:T(256)S(1)}, u32[]{:S(2)}, u32[]{:S(2)}) %collective-permute-start.1) | collective-permute-done | bytes 1056 | tf_op jit(solution)/shard_map/ppermute | solution.py:119
  39.9 2.6 %collective-permute-done.2 = f32[256]{0:T(256)S(1)} collective-permute-done((f32[256]{0:T(256)S(1)}, f32[256]{0:T(256)S(1)}, u32[]{:S(2)}, u32[]{:S(2)}) %collective-permute-start.2) | collective-permute-done | bytes 1056 | tf_op jit(solution)/shard_map/ppermute | solution.py:119
  44.1 2.7 %collective-permute-done.3 = f32[512]{0:T(512)S(1)} collective-permute-done((f32[512]{0:T(512)S(1)}, f32[512]{0:T(512)S(1)}, u32[]{:S(2)}, u32[]{:S(2)}) %collective-permute-start.3) | collective-permute-done | bytes 2080 | tf_op jit(solution)/shard_map/ppermute | solution.py:119
  47.8 3.0 %collective-permute-done.4 = f32[512]{0:T(512)S(1)} collective-permute-done((f32[512]{0:T(512)S(1)}, f32[512]{0:T(512)S(1)}, u32[]{:S(2)}, u32[]{:S(2)}) %collective-permute-start.4) | collective-permute-done | bytes 2080 | tf_op jit(solution)/shard_map/ppermute | solution.py:119
  51.8 3.0 %collective-permute-done.5 = f32[1024]{0:T(1024)S(1)} collective-permute-done((f32[1024]{0:T(1024)S(1)}, f32[1024]{0:T(1024)S(1)}, u32[]{:S(2)}, u32[]{:S(2)}) %collective-permute-start.5) | collective-permute-done | bytes 4128 | tf_op jit(solution)/shard_map/ppermute | solution.py:119
  60.6 3.6 %collective-permute-done.8 = f32[8,16,1]{2,1,0:T(8,128)S(1)} collective-permute-done((f32[8,16,1]{2,1,0:T(8,128)S(1)}, f32[8,16,1]{2,1,0:T(8,128)S(1)}, u32[]{:S(2)}, u32[]{:S(2)}) %collective-permute-start.8) | collective-permute-done | bytes 544 | tf_op jit(solution)/shard_map/ppermute | solution.py:46
  66.9 4.4 %collective-permute-start.10 = (f32[8,1,512]{2,1,0:T(1,128)S(1)}, f32[8,1,512]{2,1,0:T(1,128)S(1)}, u32[]{:S(2)}, u32[]{:S(2)}) collective-permute-start(f32[8,1,512]{2,1,0:T(1,128)S(1)} %get-tuple-element.61), channel_id=1, source_target_pairs={{0,8},{8,16},{16,24},{24,2},{2,10},{10,18},{18,26},{26,4},{4,12},{... | collective-permute-start | bytes 49160 | tf_op jit(solution)/shard_map/ppermute | solution.py:49
  72.9 1.5 collective-permute-start.14
  75.7 5.4 %collective-permute-start.13 = (f32[8,1,512]{2,1,0:T(1,128)S(1)}, f32[8,1,512]{2,1,0:T(1,128)S(1)}, u32[]{:S(2)}, u32[]{:S(2)}) collective-permute-start(f32[8,1,512]{2,1,0:T(1,128)S(1)} %get-tuple-element.53), channel_id=1, source_target_pairs={{0,8},{8,16},{16,24},{24,2},{2,10},{10,18},{18,26},{26,4},{4,12},{... | collective-permute-start | bytes 49160 | tf_op jit(solution)/shard_map/ppermute | solution.py:49
  85.6 4.9 %collective-permute-start.16 = (f32[8,1,512]{2,1,0:T(1,128)S(1)}, f32[8,1,512]{2,1,0:T(1,128)S(1)}, u32[]{:S(2)}, u32[]{:S(2)}) collective-permute-start(f32[8,1,512]{2,1,0:T(1,128)S(1)} %get-tuple-element.45), channel_id=1, source_target_pairs={{0,8},{8,16},{16,24},{24,2},{2,10},{10,18},{18,26},{26,4},{4,12},{... | collective-permute-start | bytes 49160 | tf_op jit(solution)/shard_map/ppermute | solution.py:49
  95.9 8.4 %all-to-all-start.4 = ((f32[32,1,32]{2,1,0:T(1,128)}), f32[32,1,32]{2,1,0:T(1,128)}, u32[]{:S(2)}, u32[]{:S(2)}) async-start(f32[32,1,32]{2,1,0:T(1,128)} %broadcast_in_dim.37), calls=%async_computation.4 | async-start | bytes 32768 | tf_op jit(solution)/shard_map/all_to_all | solution.py:107
  105.6 3.6 %collective-permute-start.19 = (f32[8,1,512]{2,1,0:T(1,128)}, f32[8,1,512]{2,1,0:T(1,128)}, u32[]{:S(2)}, u32[]{:S(2)}) collective-permute-start(f32[8,1,512]{2,1,0:T(1,128)} %get-tuple-element.37), channel_id=1, source_target_pairs={{0,8},{8,16},{16,24},{24,2},{2,10},{10,18},{18,26},{26,4},{4,12},{... | collective-permute-start | bytes 49160 | tf_op jit(solution)/shard_map/ppermute | solution.py:49
  109.3 1.7 %collective-permute-start.20 = (f32[8,16,1]{2,1,0:T(8,128)S(1)}, f32[8,16,1]{2,1,0:T(8,128)}, u32[]{:S(2)}, u32[]{:S(2)}) collective-permute-start(f32[8,16,1]{2,1,0:T(8,128)S(1)} %slice_select_fusion.1), channel_id=1, source_target_pairs={{0,1},{1,0},{2,3},{3,2},{4,5},{5,4},{6,7},{7,6},{8,9},{9,8},{10,11... | collective-permute-start | bytes 1544 | tf_op jit(solution)/shard_map/ppermute | solution.py:46
  111.4 1.6 %fusion.1 = f32[2048]{0:T(1024)S(1)} fusion(f32[32,32]{1,0:T(8,128)} %bitcast.55, s32[2048]{0:T(1024)} %copy-done.19, s32[2048]{0:T(1024)S(1)} %copy-done.18), kind=kOutput, calls=%fused_computation.3 | convolution fusion | flops 12843008 | bytes 28672 | tf_op jit(solution)/shard_map/dot_general | solution.py:115
  115.1 1.9 %collective-permute-done.24 = f32[256]{0:T(256)S(1)} collective-permute-done((f32[256]{0:T(256)S(1)}, f32[256]{0:T(256)S(1)}, u32[]{:S(2)}, u32[]{:S(2)}) %collective-permute-start.24) | collective-permute-done | bytes 1056 | tf_op jit(solution)/shard_map/ppermute | solution.py:119
  119.4 1.6 %collective-permute-done.25 = f32[256]{0:T(256)S(1)} collective-permute-done((f32[256]{0:T(256)S(1)}, f32[256]{0:T(256)S(1)}, u32[]{:S(2)}, u32[]{:S(2)}) %collective-permute-start.25) | collective-permute-done | bytes 1056 | tf_op jit(solution)/shard_map/ppermute | solution.py:119
  122.4 2.6 %collective-permute-done.26 = f32[256]{0:T(256)S(1)} collective-permute-done((f32[256]{0:T(256)S(1)}, f32[256]{0:T(256)S(1)}, u32[]{:S(2)}, u32[]{:S(2)}) %collective-permute-start.26) | collective-permute-done | bytes 1056 | tf_op jit(solution)/shard_map/ppermute | solution.py:119
  125.4 1.5 fusion.166
  131.6 1.6 %collective-permute-done.21 = f32[8,1,512]{2,1,0:T(1,128)S(1)} collective-permute-done((f32[8,1,512]{2,1,0:T(1,128)S(1)}, f32[8,1,512]{2,1,0:T(1,128)S(1)}, u32[]{:S(2)}, u32[]{:S(2)}) %collective-permute-start.21) | collective-permute-done | bytes 16416 | tf_op jit(solution)/shard_map/ppermute | solution.py:50
  134.1 1.5 collective-permute-start.27
  135.9 1.8 %collective-permute-done.27 = f32[512]{0:T(512)S(1)} collective-permute-done((f32[512]{0:T(512)S(1)}, f32[512]{0:T(512)S(1)}, u32[]{:S(2)}, u32[]{:S(2)}) %collective-permute-start.27) | collective-permute-done | bytes 2080 | tf_op jit(solution)/shard_map/ppermute | solution.py:119
  138.1 1.5 collective-permute-start.28
  140.4 5.0 %all-to-all-start.3 = ((f32[2,8,16,512]{3,2,0,1:T(8,128)}), f32[2,8,16,512]{3,2,0,1:T(8,128)S(1)}, u32[]{:S(2)}, u32[]{:S(2)}) async-start(f32[2,8,16,512]{3,2,0,1:T(8,128)} %pad_maximum_fusion.1), calls=%async_computation.3 | async-start | bytes 1048576 | tf_op jit(solution)/shard_map/all_to_all | solution.py:263
  146.3 3.0 %collective-permute-done.29 = f32[1024]{0:T(1024)S(1)} collective-permute-done((f32[1024]{0:T(1024)S(1)}, f32[1024]{0:T(1024)S(1)}, u32[]{:S(2)}, u32[]{:S(2)}) %collective-permute-start.29) | collective-permute-done | bytes 4128 | tf_op jit(solution)/shard_map/ppermute | solution.py:119
  150.6 4.1 %all-to-all-done.3 = f32[2,8,16,512]{3,2,0,1:T(8,128)S(1)} async-done(((f32[2,8,16,512]{3,2,0,1:T(8,128)}), f32[2,8,16,512]{3,2,0,1:T(8,128)S(1)}, u32[]{:S(2)}, u32[]{:S(2)}) %all-to-all-start.3) | async-done | bytes 524320 | tf_op jit(solution)/shard_map/all_to_all | solution.py:263
  (233 shorter events, 52.9 us)
Async XLA Ops:
  2.5 10.2 %all-to-all-start = ((f32[2,64,512]{2,0,1:T(2,128)}), f32[2,64,512]{2,0,1:T(2,128)S(1)}, u32[]{:S(2)}, u32[]{:S(2)}) async-start(f32[2,64,512]{2,0,1:T(2,128)} %copy.42), calls=%async_computation | async-start | bytes 524288 | tf_op jit(solution)/shard_map/all_to_all | solution.py:201
  13.7 12.6 %all-to-all-start.1 = ((f32[32,1,32]{2,1,0:T(1,128)}), f32[32,1,32]{2,1,0:T(1,128)S(1)}, u32[]{:S(2)}, u32[]{:S(2)}) async-start(f32[32,1,32]{2,1,0:T(1,128)} %broadcast_in_dim.29), calls=%async_computation.1 | async-start | bytes 32768 | tf_op jit(solution)/shard_map/all_to_all | solution.py:107
  26.3 30.3 %all-to-all-start.2 = ((f32[2,2,64,512]{3,1,0,2:T(2,128)}), f32[2,2,64,512]{3,1,0,2:T(2,128)S(1)}, u32[]{:S(2)}, u32[]{:S(2)}) async-start(f32[2,2,64,512]{3,1,0,2:T(2,128)} %copy.43), calls=%async_computation.2 | async-start | bytes 1048576 | tf_op jit(solution)/shard_map/all_to_all | solution.py:199
  31.0 3.6 %collective-permute-start = (f32[256]{0:T(256)S(1)}, f32[256]{0:T(256)S(1)}, u32[]{:S(2)}, u32[]{:S(2)}) collective-permute-start(f32[256]{0:T(256)S(1)} %dynamic-slice_subtract_fusion.5), channel_id=1, source_target_pairs={{0,1},{1,0},{2,3},{3,2},{4,5},{5,4},{6,7},{7,6},{8,9},{9,8},{10,11... | collective-permute-start | bytes 3080 | tf_op jit(solution)/shard_map/ppermute | solution.py:119
  35.0 3.6 %collective-permute-start.1 = (f32[256]{0:T(256)S(1)}, f32[256]{0:T(256)S(1)}, u32[]{:S(2)}, u32[]{:S(2)}) collective-permute-start(f32[256]{0:T(256)S(1)} %dynamic-slice_subtract_fusion.4), channel_id=1, source_target_pairs={{0,1},{1,0},{2,3},{3,2},{4,5},{5,4},{6,7},{7,6},{8,9},{9,8},{10,11... | collective-permute-start | bytes 3080 | tf_op jit(solution)/shard_map/ppermute | solution.py:119
  38.9 3.6 %collective-permute-start.2 = (f32[256]{0:T(256)S(1)}, f32[256]{0:T(256)S(1)}, u32[]{:S(2)}, u32[]{:S(2)}) collective-permute-start(f32[256]{0:T(256)S(1)} %dynamic-slice_subtract_fusion.3), channel_id=1, source_target_pairs={{0,1},{1,0},{2,3},{3,2},{4,5},{5,4},{6,7},{7,6},{8,9},{9,8},{10,11... | collective-permute-start | bytes 3080 | tf_op jit(solution)/shard_map/ppermute | solution.py:119
  43.2 3.6 %collective-permute-start.3 = (f32[512]{0:T(512)S(1)}, f32[512]{0:T(512)S(1)}, u32[]{:S(2)}, u32[]{:S(2)}) collective-permute-start(f32[512]{0:T(512)S(1)} %pad_maximum_fusion.5), channel_id=1, source_target_pairs={{0,1},{1,0},{2,3},{3,2},{4,5},{5,4},{6,7},{7,6},{8,9},{9,8},{10,11... | collective-permute-start | bytes 6152 | tf_op jit(solution)/shard_map/ppermute | solution.py:119
  47.2 3.6 %collective-permute-start.4 = (f32[512]{0:T(512)S(1)}, f32[512]{0:T(512)S(1)}, u32[]{:S(2)}, u32[]{:S(2)}) collective-permute-start(f32[512]{0:T(512)S(1)} %pad_maximum_fusion.6), channel_id=1, source_target_pairs={{0,1},{1,0},{2,3},{3,2},{4,5},{5,4},{6,7},{7,6},{8,9},{9,8},{10,11... | collective-permute-start | bytes 6152 | tf_op jit(solution)/shard_map/ppermute | solution.py:119
  51.1 3.7 %collective-permute-start.5 = (f32[1024]{0:T(1024)S(1)}, f32[1024]{0:T(1024)S(1)}, u32[]{:S(2)}, u32[]{:S(2)}) collective-permute-start(f32[1024]{0:T(1024)S(1)} %pad_maximum_fusion.3), channel_id=1, source_target_pairs={{0,1},{1,0},{2,3},{3,2},{4,5},{5,4},{6,7},{7,6},{8,9},{9,8},{10,11... | collective-permute-start | bytes 12296 | tf_op jit(solution)/shard_map/ppermute | solution.py:119
  57.2 6.9 %collective-permute-start.7 = (f32[8,1,512]{2,1,0:T(1,128)S(1)}, f32[8,1,512]{2,1,0:T(1,128)S(1)}, u32[]{:S(2)}, u32[]{:S(2)}) collective-permute-start(f32[8,1,512]{2,1,0:T(1,128)S(1)} %get-tuple-element.66), channel_id=1, source_target_pairs={{0,8},{8,16},{16,24},{24,2},{2,10},{10,18},{18,26},{26,4},{4,12},{... | collective-permute-start | bytes 49160 | tf_op jit(solution)/shard_map/ppermute | solution.py:49
  58.5 5.7 %collective-permute-start.6 = (f32[8,1,512]{2,1,0:T(1,128)S(1)}, f32[8,1,512]{2,1,0:T(1,128)S(1)}, u32[]{:S(2)}, u32[]{:S(2)}) collective-permute-start(f32[8,1,512]{2,1,0:T(1,128)S(1)} %get-tuple-element.67), channel_id=1, source_target_pairs={{8,0},{16,8},{24,16},{2,24},{10,2},{18,10},{26,18},{4,26},{12,4},{... | collective-permute-start | bytes 49160 | tf_op jit(solution)/shard_map/ppermute | solution.py:50
  59.8 4.3 %collective-permute-start.8 = (f32[8,16,1]{2,1,0:T(8,128)S(1)}, f32[8,16,1]{2,1,0:T(8,128)S(1)}, u32[]{:S(2)}, u32[]{:S(2)}) collective-permute-start(f32[8,16,1]{2,1,0:T(8,128)S(1)} %slice_select_fusion.5), channel_id=1, source_target_pairs={{0,1},{1,0},{2,3},{3,2},{4,5},{5,4},{6,7},{7,6},{8,9},{9,8},{10,11... | collective-permute-start | bytes 1544 | tf_op jit(solution)/shard_map/ppermute | solution.py:46
  64.8 6.5 %collective-permute-start.11 = (f32[8,16,1]{2,1,0:T(8,128)S(1)}, f32[8,16,1]{2,1,0:T(8,128)S(1)}, u32[]{:S(2)}, u32[]{:S(2)}) collective-permute-start(f32[8,16,1]{2,1,0:T(8,128)S(1)} %slice_select_fusion.4), channel_id=1, source_target_pairs={{0,1},{1,0},{2,3},{3,2},{4,5},{5,4},{6,7},{7,6},{8,9},{9,8},{10,11... | collective-permute-start | bytes 1544 | tf_op jit(solution)/shard_map/ppermute | solution.py:46
  65.6 5.8 %collective-permute-start.9 = (f32[8,1,512]{2,1,0:T(1,128)S(1)}, f32[8,1,512]{2,1,0:T(1,128)S(1)}, u32[]{:S(2)}, u32[]{:S(2)}) collective-permute-start(f32[8,1,512]{2,1,0:T(1,128)S(1)} %get-tuple-element.60), channel_id=1, source_target_pairs={{8,0},{16,8},{24,16},{2,24},{10,2},{18,10},{26,18},{4,26},{12,4},{... | collective-permute-start | bytes 49160 | tf_op jit(solution)/shard_map/ppermute | solution.py:50
  66.9 5.3 %collective-permute-start.10 = (f32[8,1,512]{2,1,0:T(1,128)S(1)}, f32[8,1,512]{2,1,0:T(1,128)S(1)}, u32[]{:S(2)}, u32[]{:S(2)}) collective-permute-start(f32[8,1,512]{2,1,0:T(1,128)S(1)} %get-tuple-element.61), channel_id=1, source_target_pairs={{0,8},{8,16},{16,24},{24,2},{2,10},{10,18},{18,26},{26,4},{4,12},{... | collective-permute-start | bytes 49160 | tf_op jit(solution)/shard_map/ppermute | solution.py:49
  72.9 8.3 %collective-permute-start.14 = (f32[8,16,1]{2,1,0:T(8,128)S(1)}, f32[8,16,1]{2,1,0:T(8,128)S(1)}, u32[]{:S(2)}, u32[]{:S(2)}) collective-permute-start(f32[8,16,1]{2,1,0:T(8,128)S(1)} %slice_select_fusion.3), channel_id=1, source_target_pairs={{0,1},{1,0},{2,3},{3,2},{4,5},{5,4},{6,7},{7,6},{8,9},{9,8},{10,11... | collective-permute-start | bytes 1544 | tf_op jit(solution)/shard_map/ppermute | solution.py:46
  74.4 6.8 %collective-permute-start.12 = (f32[8,1,512]{2,1,0:T(1,128)S(1)}, f32[8,1,512]{2,1,0:T(1,128)S(1)}, u32[]{:S(2)}, u32[]{:S(2)}) collective-permute-start(f32[8,1,512]{2,1,0:T(1,128)S(1)} %get-tuple-element.52), channel_id=1, source_target_pairs={{8,0},{16,8},{24,16},{2,24},{10,2},{18,10},{26,18},{4,26},{12,4},{... | collective-permute-start | bytes 49160 | tf_op jit(solution)/shard_map/ppermute | solution.py:50
  75.7 6.3 %collective-permute-start.13 = (f32[8,1,512]{2,1,0:T(1,128)S(1)}, f32[8,1,512]{2,1,0:T(1,128)S(1)}, u32[]{:S(2)}, u32[]{:S(2)}) collective-permute-start(f32[8,1,512]{2,1,0:T(1,128)S(1)} %get-tuple-element.53), channel_id=1, source_target_pairs={{0,8},{8,16},{16,24},{24,2},{2,10},{10,18},{18,26},{26,4},{4,12},{... | collective-permute-start | bytes 49160 | tf_op jit(solution)/shard_map/ppermute | solution.py:49
  83.6 6.9 %collective-permute-start.17 = (f32[8,16,1]{2,1,0:T(8,128)S(1)}, f32[8,16,1]{2,1,0:T(8,128)S(1)}, u32[]{:S(2)}, u32[]{:S(2)}) collective-permute-start(f32[8,16,1]{2,1,0:T(8,128)S(1)} %slice_select_fusion.2), channel_id=1, source_target_pairs={{0,1},{1,0},{2,3},{3,2},{4,5},{5,4},{6,7},{7,6},{8,9},{9,8},{10,11... | collective-permute-start | bytes 1544 | tf_op jit(solution)/shard_map/ppermute | solution.py:46
  84.3 6.2 %collective-permute-start.15 = (f32[8,1,512]{2,1,0:T(1,128)S(1)}, f32[8,1,512]{2,1,0:T(1,128)S(1)}, u32[]{:S(2)}, u32[]{:S(2)}) collective-permute-start(f32[8,1,512]{2,1,0:T(1,128)S(1)} %get-tuple-element.44), channel_id=1, source_target_pairs={{8,0},{16,8},{24,16},{2,24},{10,2},{18,10},{26,18},{4,26},{12,4},{... | collective-permute-start | bytes 49160 | tf_op jit(solution)/shard_map/ppermute | solution.py:50
  85.6 5.7 %collective-permute-start.16 = (f32[8,1,512]{2,1,0:T(1,128)S(1)}, f32[8,1,512]{2,1,0:T(1,128)S(1)}, u32[]{:S(2)}, u32[]{:S(2)}) collective-permute-start(f32[8,1,512]{2,1,0:T(1,128)S(1)} %get-tuple-element.45), channel_id=1, source_target_pairs={{0,8},{8,16},{16,24},{24,2},{2,10},{10,18},{18,26},{26,4},{4,12},{... | collective-permute-start | bytes 49160 | tf_op jit(solution)/shard_map/ppermute | solution.py:49
  95.9 15.5 %all-to-all-start.4 = ((f32[32,1,32]{2,1,0:T(1,128)}), f32[32,1,32]{2,1,0:T(1,128)}, u32[]{:S(2)}, u32[]{:S(2)}) async-start(f32[32,1,32]{2,1,0:T(1,128)} %broadcast_in_dim.37), calls=%async_computation.4 | async-start | bytes 32768 | tf_op jit(solution)/shard_map/all_to_all | solution.py:107
  104.3 21.0 %collective-permute-start.18 = (f32[8,1,512]{2,1,0:T(1,128)}, f32[8,1,512]{2,1,0:T(1,128)S(1)}, u32[]{:S(2)}, u32[]{:S(2)}) collective-permute-start(f32[8,1,512]{2,1,0:T(1,128)} %get-tuple-element.36), channel_id=1, source_target_pairs={{8,0},{16,8},{24,16},{2,24},{10,2},{18,10},{26,18},{4,26},{12,4},{... | collective-permute-start | bytes 49160 | tf_op jit(solution)/shard_map/ppermute | solution.py:50
  105.6 19.7 %collective-permute-start.19 = (f32[8,1,512]{2,1,0:T(1,128)}, f32[8,1,512]{2,1,0:T(1,128)}, u32[]{:S(2)}, u32[]{:S(2)}) collective-permute-start(f32[8,1,512]{2,1,0:T(1,128)} %get-tuple-element.37), channel_id=1, source_target_pairs={{0,8},{8,16},{16,24},{24,2},{2,10},{10,18},{18,26},{26,4},{4,12},{... | collective-permute-start | bytes 49160 | tf_op jit(solution)/shard_map/ppermute | solution.py:49
  109.3 5.0 %collective-permute-start.20 = (f32[8,16,1]{2,1,0:T(8,128)S(1)}, f32[8,16,1]{2,1,0:T(8,128)}, u32[]{:S(2)}, u32[]{:S(2)}) collective-permute-start(f32[8,16,1]{2,1,0:T(8,128)S(1)} %slice_select_fusion.1), channel_id=1, source_target_pairs={{0,1},{1,0},{2,3},{3,2},{4,5},{5,4},{6,7},{7,6},{8,9},{9,8},{10,11... | collective-permute-start | bytes 1544 | tf_op jit(solution)/shard_map/ppermute | solution.py:46
  127.2 4.3 %collective-permute-start.23 = (f32[8,16,1]{2,1,0:T(8,128)S(1)}, f32[8,16,1]{2,1,0:T(8,128)S(1)}, u32[]{:S(2)}, u32[]{:S(2)}) collective-permute-start(f32[8,16,1]{2,1,0:T(8,128)S(1)} %slice_select_fusion), channel_id=1, source_target_pairs={{0,1},{1,0},{2,3},{3,2},{4,5},{5,4},{6,7},{7,6},{8,9},{9,8},{10,11... | collective-permute-start | bytes 1544 | tf_op jit(solution)/shard_map/ppermute | solution.py:46
  127.9 3.6 %collective-permute-start.22 = (f32[8,1,512]{2,1,0:T(1,128)S(1)}, f32[8,1,512]{2,1,0:T(1,128)S(1)}, u32[]{:S(2)}, u32[]{:S(2)}) collective-permute-start(f32[8,1,512]{2,1,0:T(1,128)S(1)} %get-tuple-element.28), channel_id=1, source_target_pairs={{0,8},{8,16},{16,24},{24,2},{2,10},{10,18},{18,26},{26,4},{4,12},{... | collective-permute-start | bytes 49160 | tf_op jit(solution)/shard_map/ppermute | solution.py:49
  129.2 4.0 %collective-permute-start.21 = (f32[8,1,512]{2,1,0:T(1,128)S(1)}, f32[8,1,512]{2,1,0:T(1,128)S(1)}, u32[]{:S(2)}, u32[]{:S(2)}) collective-permute-start(f32[8,1,512]{2,1,0:T(1,128)S(1)} %get-tuple-element.29), channel_id=1, source_target_pairs={{8,0},{16,8},{24,16},{2,24},{10,2},{18,10},{26,18},{4,26},{12,4},{... | collective-permute-start | bytes 49160 | tf_op jit(solution)/shard_map/ppermute | solution.py:50
  134.1 3.6 %collective-permute-start.27 = (f32[512]{0:T(512)S(1)}, f32[512]{0:T(512)S(1)}, u32[]{:S(2)}, u32[]{:S(2)}) collective-permute-start(f32[512]{0:T(512)S(1)} %pad_maximum_fusion.7), channel_id=1, source_target_pairs={{0,1},{1,0},{2,3},{3,2},{4,5},{5,4},{6,7},{7,6},{8,9},{9,8},{10,11... | collective-permute-start | bytes 6152 | tf_op jit(solution)/shard_map/ppermute | solution.py:119
  138.1 7.3 %collective-permute-start.28 = (f32[512]{0:T(512)S(1)}, f32[512]{0:T(512)S(1)}, u32[]{:S(2)}, u32[]{:S(2)}) collective-permute-start(f32[512]{0:T(512)S(1)} %pad_maximum_fusion.8), channel_id=1, source_target_pairs={{0,1},{1,0},{2,3},{3,2},{4,5},{5,4},{6,7},{7,6},{8,9},{9,8},{10,11... | collective-permute-start | bytes 6152 | tf_op jit(solution)/shard_map/ppermute | solution.py:119
  140.4 14.2 %all-to-all-start.3 = ((f32[2,8,16,512]{3,2,0,1:T(8,128)}), f32[2,8,16,512]{3,2,0,1:T(8,128)S(1)}, u32[]{:S(2)}, u32[]{:S(2)}) async-start(f32[2,8,16,512]{3,2,0,1:T(8,128)} %pad_maximum_fusion.1), calls=%async_computation.3 | async-start | bytes 1048576 | tf_op jit(solution)/shard_map/all_to_all | solution.py:263
  145.7 3.7 %collective-permute-start.29 = (f32[1024]{0:T(1024)S(1)}, f32[1024]{0:T(1024)S(1)}, u32[]{:S(2)}, u32[]{:S(2)}) collective-permute-start(f32[1024]{0:T(1024)S(1)} %pad_maximum_fusion.4), channel_id=1, source_target_pairs={{0,1},{1,0},{2,3},{3,2},{4,5},{5,4},{6,7},{7,6},{8,9},{9,8},{10,11... | collective-permute-start | bytes 12296 | tf_op jit(solution)/shard_map/ppermute | solution.py:119
  (23 other events, 263.4 us)

commit v20 on v19

--- a/solution.py
+++ b/solution.py
@@ -30,7 +30,7 @@
     return count
 
 
-def rims(field, axis, dim):
+def rims(field, axis, dim, ends_free=False):
     size = field.shape[dim]
     head = lax.slice_in_dim(field, 0, 1, axis=dim)
     tail = lax.slice_in_dim(field, size - 1, size, axis=dim)
@@ -44,6 +44,8 @@
     if count == 2:
         low = lax.axis_index(axis) == 0
         got = lax.ppermute(jnp.where(low, tail, head), axis, [(0, 1), (1, 0)])
+        if ends_free:
+            return got, got
         zero = jnp.zeros_like(got)
         return jnp.where(low, got, zero), jnp.where(low, zero, got)
     below = lax.ppermute(tail, axis, [(place[i], place[i + 1]) for i in range(count - 1)])
@@ -61,7 +63,7 @@
 
 
 def exchange(field):
-    return [rims(field, axis, dim) for axis, dim in ((None, 0), (ROW_AXES, 1), ("col", 2))]
+    return [rims(field, axis, dim, True) for axis, dim in ((None, 0), (ROW_AXES, 1), ("col", 2))]
 
 
 def apply_grid(field, near, weights, pad_term):

time: 156 us -> 158 us (1.013)
  waiting for transfers between devices: 49 us -> 61.2 us
  starting transfers between devices: 70.5 us -> 62.5 us
    ppermute x6, waiting for transfers between devices: 4.81 us -> 17.6 us  [rims(): got = lax.ppermute(jnp.where(low, tail, head), axis, [(0, 1), (1, 0)])]
    all_to_all x2, waiting for transfers between devices: 6.2 us -> 12.8 us  [share_tiles(): got = lax.all_to_all(payload, ('layer', 'row', 'col'), 0, 0, tiled=True)]
    all_to_all x2, starting transfers between devices: 13.9 us -> 9.44 us  [share_tiles(): got = lax.all_to_all(payload, ('layer', 'row', 'col'), 0, 0, tiled=True)]
    ppermute x6, starting transfers between devices: 21 us -> 18.1 us  [rims(): lax.ppermute(tail, axis, [(place[i], place[i + 1]) for i in range(count -...]
    ppermute x12, waiting for transfers between devices: 25.9 us -> 23.2 us  [swap_col(): return lax.ppermute(value, 'col', [(0, 1), (1, 0)])]
    ppermute x6, waiting for transfers between devices: 2.36 us -> 0.02 us  [rims(): lax.ppermute(tail, axis, [(place[i], place[i + 1]) for i in range(count -...]
    ppermute x6, waiting for transfers between devices: 1.64 us -> 0.03 us  [rims(): lax.ppermute(head, axis, [(place[i + 1], place[i]) for i in range(count -...]
  transfers between devices with their start and end apart: 35 -> 35, of which waited for: 22 -> 19; matrix products, arithmetic and copies ran while one was open for 13% -> 11% of each run, Pallas kernels for 0% -> 0%
where the time goes in v20:
time: 158 us; the launch traced here: 157 us
  starting transfers between devices  62.5 us (40%)
  waiting for transfers between devices  61.2 us (39%)
  local copies, waits for them, and re-layouts  11.4 us (7%)
  matrix products  10.4 us (7%)
  other arithmetic  10.2 us (6%)
    ppermute x12, waiting for transfers between devices, swap_col(): return lax.ppermute(value, 'col', [(0, 1), (1, 0)])  23.2 us
    ppermute x6, starting transfers between devices, rims(): lax.ppermute(tail, axis, [(place[i], place[i + 1]) for i in range(count -...  18.1 us
    ppermute x6, waiting for transfers between devices, rims(): got = lax.ppermute(jnp.where(low, tail, head), axis, [(0, 1), (1, 0)])  17.6 us
    all_to_all x2, waiting for transfers between devices, share_tiles(): got = lax.all_to_all(payload, ('layer', 'row', 'col'), 0, 0, tiled=True)  12.8 us
    ppermute x12, starting transfers between devices, swap_col(): return lax.ppermute(value, 'col', [(0, 1), (1, 0)])  9.69 us
    all_to_all x2, starting transfers between devices, share_tiles(): got = lax.all_to_all(payload, ('layer', 'row', 'col'), 0, 0, tiled=True)  9.44 us
    ppermute x6, starting transfers between devices, rims(): lax.ppermute(head, axis, [(place[i + 1], place[i]) for i in range(count -...  7.75 us
    ppermute x6, starting transfers between devices, rims(): got = lax.ppermute(jnp.where(low, tail, head), axis, [(0, 1), (1, 0)])  5.15 us
  transfers between devices with their start and end apart: 35, of which 19 were waited for; matrix products, arithmetic and copies ran while one was open for 11% of the time, Pallas kernels for 0%

profile of v20, /device:TPU:0, one launch (start us, length us, event | category | flops | bytes accessed | tf_op | source)
XLA Modules:
  0.0 157.3 jit_solution(13403692954036872981)
XLA Ops:
  0.6 1.9 %copy.42 = f32[2,64,512]{2,0,1:T(2,128)} copy(f32[2,64,512]{2,1,0:T(8,128)} %param.8) | data formatting | bytes 524288 | tf_op args[0]
  2.5 4.2 %all-to-all-start = ((f32[2,64,512]{2,0,1:T(2,128)}), f32[2,64,512]{2,0,1:T(2,128)S(1)}, u32[]{:S(2)}, u32[]{:S(2)}) async-start(f32[2,64,512]{2,0,1:T(2,128)} %copy.42), calls=%async_computation | async-start | bytes 524288 | tf_op jit(solution)/shard_map/all_to_all | solution.py:203
  8.8 4.0 %all-to-all-done = f32[2,64,512]{2,0,1:T(2,128)S(1)} async-done(((f32[2,64,512]{2,0,1:T(2,128)}), f32[2,64,512]{2,0,1:T(2,128)S(1)}, u32[]{:S(2)}, u32[]{:S(2)}) %all-to-all-start) | async-done | bytes 262176 | tf_op jit(solution)/shard_map/all_to_all | solution.py:203
  13.7 5.5 %all-to-all-start.1 = ((f32[32,1,32]{2,1,0:T(1,128)}), f32[32,1,32]{2,1,0:T(1,128)S(1)}, u32[]{:S(2)}, u32[]{:S(2)}) async-start(f32[32,1,32]{2,1,0:T(1,128)} %broadcast_in_dim.31), calls=%async_computation.1 | async-start | bytes 32768 | tf_op jit(solution)/shard_map/all_to_all | solution.py:109
  20.5 5.8 %all-to-all-done.1 = f32[32,1,32]{2,1,0:T(1,128)S(1)} async-done(((f32[32,1,32]{2,1,0:T(1,128)}), f32[32,1,32]{2,1,0:T(1,128)S(1)}, u32[]{:S(2)}, u32[]{:S(2)}) %all-to-all-start.1) | async-done | bytes 4128 | tf_op jit(solution)/shard_map/all_to_all | solution.py:109
  26.3 3.5 %all-to-all-start.2 = ((f32[2,2,64,512]{3,1,0,2:T(2,128)}), f32[2,2,64,512]{3,1,0,2:T(2,128)S(1)}, u32[]{:S(2)}, u32[]{:S(2)}) async-start(f32[2,2,64,512]{3,1,0,2:T(2,128)} %copy.43), calls=%async_computation.2 | async-start | bytes 1048576 | tf_op jit(solution)/shard_map/all_to_all | solution.py:201
  32.5 2.1 %collective-permute-done = f32[256]{0:T(256)S(1)} collective-permute-done((f32[256]{0:T(256)S(1)}, f32[256]{0:T(256)S(1)}, u32[]{:S(2)}, u32[]{:S(2)}) %collective-permute-start) | collective-permute-done | bytes 1056 | tf_op jit(solution)/shard_map/ppermute | solution.py:121
  36.9 1.6 %collective-permute-done.1 = f32[256]{0:T(256)S(1)} collective-permute-done((f32[256]{0:T(256)S(1)}, f32[256]{0:T(256)S(1)}, u32[]{:S(2)}, u32[]{:S(2)}) %collective-permute-start.1) | collective-permute-done | bytes 1056 | tf_op jit(solution)/shard_map/ppermute | solution.py:121
  39.9 2.6 %collective-permute-done.2 = f32[256]{0:T(256)S(1)} collective-permute-done((f32[256]{0:T(256)S(1)}, f32[256]{0:T(256)S(1)}, u32[]{:S(2)}, u32[]{:S(2)}) %collective-permute-start.2) | collective-permute-done | bytes 1056 | tf_op jit(solution)/shard_map/ppermute | solution.py:121
  44.1 2.7 %collective-permute-done.3 = f32[512]{0:T(512)S(1)} collective-permute-done((f32[512]{0:T(512)S(1)}, f32[512]{0:T(512)S(1)}, u32[]{:S(2)}, u32[]{:S(2)}) %collective-permute-start.3) | collective-permute-done | bytes 2080 | tf_op jit(solution)/shard_map/ppermute | solution.py:121
  47.8 3.0 %collective-permute-done.4 = f32[512]{0:T(512)S(1)} collective-permute-done((f32[512]{0:T(512)S(1)}, f32[512]{0:T(512)S(1)}, u32[]{:S(2)}, u32[]{:S(2)}) %collective-permute-start.4) | collective-permute-done | bytes 2080 | tf_op jit(solution)/shard_map/ppermute | solution.py:121
  51.8 3.0 %collective-permute-done.5 = f32[1024]{0:T(1024)S(1)} collective-permute-done((f32[1024]{0:T(1024)S(1)}, f32[1024]{0:T(1024)S(1)}, u32[]{:S(2)}, u32[]{:S(2)}) %collective-permute-start.5) | collective-permute-done | bytes 4128 | tf_op jit(solution)/shard_map/ppermute | solution.py:121
  60.6 3.6 %collective-permute-done.8 = f32[8,16,1]{2,1,0:T(8,128)S(1)} collective-permute-done((f32[8,16,1]{2,1,0:T(8,128)S(1)}, f32[8,16,1]{2,1,0:T(8,128)S(1)}, u32[]{:S(2)}, u32[]{:S(2)}) %collective-permute-start.8) | collective-permute-done | bytes 544 | tf_op jit(solution)/shard_map/ppermute | solution.py:46
  66.1 4.7 %collective-permute-start.10 = (f32[8,1,512]{2,1,0:T(1,128)S(1)}, f32[8,1,512]{2,1,0:T(1,128)S(1)}, u32[]{:S(2)}, u32[]{:S(2)}) collective-permute-start(f32[8,1,512]{2,1,0:T(1,128)S(1)} %get-tuple-element.61), channel_id=1, source_target_pairs={{0,8},{8,16},{16,24},{24,2},{2,10},{10,18},{18,26},{26,4},{4,12},{... | collective-permute-start | bytes 49160 | tf_op jit(solution)/shard_map/ppermute | solution.py:51
  71.6 3.6 %collective-permute-done.11 = f32[8,16,1]{2,1,0:T(8,128)S(1)} collective-permute-done((f32[8,16,1]{2,1,0:T(8,128)S(1)}, f32[8,16,1]{2,1,0:T(8,128)S(1)}, u32[]{:S(2)}, u32[]{:S(2)}) %collective-permute-start.11) | collective-permute-done | bytes 544 | tf_op jit(solution)/shard_map/ppermute | solution.py:46
  77.3 4.3 %collective-permute-start.13 = (f32[8,1,512]{2,1,0:T(1,128)S(1)}, f32[8,1,512]{2,1,0:T(1,128)S(1)}, u32[]{:S(2)}, u32[]{:S(2)}) collective-permute-start(f32[8,1,512]{2,1,0:T(1,128)S(1)} %get-tuple-element.53), channel_id=1, source_target_pairs={{0,8},{8,16},{16,24},{24,2},{2,10},{10,18},{18,26},{26,4},{4,12},{... | collective-permute-start | bytes 49160 | tf_op jit(solution)/shard_map/ppermute | solution.py:51
  82.3 3.6 %collective-permute-done.14 = f32[8,16,1]{2,1,0:T(8,128)S(1)} collective-permute-done((f32[8,16,1]{2,1,0:T(8,128)S(1)}, f32[8,16,1]{2,1,0:T(8,128)S(1)}, u32[]{:S(2)}, u32[]{:S(2)}) %collective-permute-start.14) | collective-permute-done | bytes 544 | tf_op jit(solution)/shard_map/ppermute | solution.py:46
  88.8 3.3 %collective-permute-start.16 = (f32[8,1,512]{2,1,0:T(1,128)S(1)}, f32[8,1,512]{2,1,0:T(1,128)S(1)}, u32[]{:S(2)}, u32[]{:S(2)}) collective-permute-start(f32[8,1,512]{2,1,0:T(1,128)S(1)} %get-tuple-element.45), channel_id=1, source_target_pairs={{0,8},{8,16},{16,24},{24,2},{2,10},{10,18},{18,26},{26,4},{4,12},{... | collective-permute-start | bytes 49160 | tf_op jit(solution)/shard_map/ppermute | solution.py:51
  92.8 3.6 %collective-permute-done.17 = f32[8,16,1]{2,1,0:T(8,128)S(1)} collective-permute-done((f32[8,16,1]{2,1,0:T(8,128)S(1)}, f32[8,16,1]{2,1,0:T(8,128)S(1)}, u32[]{:S(2)}, u32[]{:S(2)}) %collective-permute-start.17) | collective-permute-done | bytes 544 | tf_op jit(solution)/shard_map/ppermute | solution.py:46
  100.3 3.9 %all-to-all-start.4 = ((f32[32,1,32]{2,1,0:T(1,128)}), f32[32,1,32]{2,1,0:T(1,128)S(1)}, u32[]{:S(2)}, u32[]{:S(2)}) async-start(f32[32,1,32]{2,1,0:T(1,128)} %broadcast_in_dim.40), calls=%async_computation.4 | async-start | bytes 32768 | tf_op jit(solution)/shard_map/all_to_all | solution.py:109
  104.3 7.0 %all-to-all-done.4 = f32[32,1,32]{2,1,0:T(1,128)S(1)} async-done(((f32[32,1,32]{2,1,0:T(1,128)}), f32[32,1,32]{2,1,0:T(1,128)S(1)}, u32[]{:S(2)}, u32[]{:S(2)}) %all-to-all-start.4) | async-done | bytes 4128 | tf_op jit(solution)/shard_map/all_to_all | solution.py:109
  114.5 3.2 %collective-permute-start.19 = (f32[8,1,512]{2,1,0:T(1,128)S(1)}, f32[8,1,512]{2,1,0:T(1,128)S(1)}, u32[]{:S(2)}, u32[]{:S(2)}) collective-permute-start(f32[8,1,512]{2,1,0:T(1,128)S(1)} %get-tuple-element.37), channel_id=1, source_target_pairs={{0,8},{8,16},{16,24},{24,2},{2,10},{10,18},{18,26},{26,4},{4,12},{... | collective-permute-start | bytes 49160 | tf_op jit(solution)/shard_map/ppermute | solution.py:51
  117.7 1.4 collective-permute-start.20
  121.6 1.5 collective-permute-done.25
  124.8 2.3 %collective-permute-done.26 = f32[256]{0:T(256)S(1)} collective-permute-done((f32[256]{0:T(256)S(1)}, f32[256]{0:T(256)S(1)}, u32[]{:S(2)}, u32[]{:S(2)}) %collective-permute-start.26) | collective-permute-done | bytes 1056 | tf_op jit(solution)/shard_map/ppermute | solution.py:121
  127.5 1.5 fusion.166
  133.0 3.2 %collective-permute-done.23 = f32[8,16,1]{2,1,0:T(8,128)S(1)} collective-permute-done((f32[8,16,1]{2,1,0:T(8,128)S(1)}, f32[8,16,1]{2,1,0:T(8,128)S(1)}, u32[]{:S(2)}, u32[]{:S(2)}) %collective-permute-start.23) | collective-permute-done | bytes 544 | tf_op jit(solution)/shard_map/ppermute | solution.py:46
  138.4 2.3 %collective-permute-done.27 = f32[512]{0:T(512)S(1)} collective-permute-done((f32[512]{0:T(512)S(1)}, f32[512]{0:T(512)S(1)}, u32[]{:S(2)}, u32[]{:S(2)}) %collective-permute-start.27) | collective-permute-done | bytes 2080 | tf_op jit(solution)/shard_map/ppermute | solution.py:121
  142.9 4.7 %all-to-all-start.3 = ((f32[2,8,16,512]{3,2,0,1:T(8,128)}), f32[2,8,16,512]{3,2,0,1:T(8,128)S(1)}, u32[]{:S(2)}, u32[]{:S(2)}) async-start(f32[2,8,16,512]{3,2,0,1:T(8,128)} %pad_maximum_fusion.1), calls=%async_computation.3 | async-start | bytes 1048576 | tf_op jit(solution)/shard_map/all_to_all | solution.py:265
  147.9 1.5 collective-permute-start.29
  149.4 2.2 %collective-permute-done.29 = f32[1024]{0:T(1024)S(1)} collective-permute-done((f32[1024]{0:T(1024)S(1)}, f32[1024]{0:T(1024)S(1)}, u32[]{:S(2)}, u32[]{:S(2)}) %collective-permute-start.29) | collective-permute-done | bytes 4128 | tf_op jit(solution)/shard_map/ppermute | solution.py:121
  152.8 3.6 %all-to-all-done.3 = f32[2,8,16,512]{3,2,0,1:T(8,128)S(1)} async-done(((f32[2,8,16,512]{3,2,0,1:T(8,128)}), f32[2,8,16,512]{3,2,0,1:T(8,128)S(1)}, u32[]{:S(2)}, u32[]{:S(2)}) %all-to-all-start.3) | async-done | bytes 524320 | tf_op jit(solution)/shard_map/all_to_all | solution.py:265
  (230 shorter events, 51.0 us)
Async XLA Ops:
  2.5 10.2 %all-to-all-start = ((f32[2,64,512]{2,0,1:T(2,128)}), f32[2,64,512]{2,0,1:T(2,128)S(1)}, u32[]{:S(2)}, u32[]{:S(2)}) async-start(f32[2,64,512]{2,0,1:T(2,128)} %copy.42), calls=%async_computation | async-start | bytes 524288 | tf_op jit(solution)/shard_map/all_to_all | solution.py:203
  13.7 12.6 %all-to-all-start.1 = ((f32[32,1,32]{2,1,0:T(1,128)}), f32[32,1,32]{2,1,0:T(1,128)S(1)}, u32[]{:S(2)}, u32[]{:S(2)}) async-start(f32[32,1,32]{2,1,0:T(1,128)} %broadcast_in_dim.31), calls=%async_computation.1 | async-start | bytes 32768 | tf_op jit(solution)/shard_map/all_to_all | solution.py:109
  26.3 30.3 %all-to-all-start.2 = ((f32[2,2,64,512]{3,1,0,2:T(2,128)}), f32[2,2,64,512]{3,1,0,2:T(2,128)S(1)}, u32[]{:S(2)}, u32[]{:S(2)}) async-start(f32[2,2,64,512]{3,1,0,2:T(2,128)} %copy.43), calls=%async_computation.2 | async-start | bytes 1048576 | tf_op jit(solution)/shard_map/all_to_all | solution.py:201
  31.0 3.6 %collective-permute-start = (f32[256]{0:T(256)S(1)}, f32[256]{0:T(256)S(1)}, u32[]{:S(2)}, u32[]{:S(2)}) collective-permute-start(f32[256]{0:T(256)S(1)} %dynamic-slice_subtract_fusion.5), channel_id=1, source_target_pairs={{0,1},{1,0},{2,3},{3,2},{4,5},{5,4},{6,7},{7,6},{8,9},{9,8},{10,11... | collective-permute-start | bytes 3080 | tf_op jit(solution)/shard_map/ppermute | solution.py:121
  35.0 3.6 %collective-permute-start.1 = (f32[256]{0:T(256)S(1)}, f32[256]{0:T(256)S(1)}, u32[]{:S(2)}, u32[]{:S(2)}) collective-permute-start(f32[256]{0:T(256)S(1)} %dynamic-slice_subtract_fusion.4), channel_id=1, source_target_pairs={{0,1},{1,0},{2,3},{3,2},{4,5},{5,4},{6,7},{7,6},{8,9},{9,8},{10,11... | collective-permute-start | bytes 3080 | tf_op jit(solution)/shard_map/ppermute | solution.py:121
  43.2 3.6 %collective-permute-start.3 = (f32[512]{0:T(512)S(1)}, f32[512]{0:T(512)S(1)}, u32[]{:S(2)}, u32[]{:S(2)}) collective-permute-start(f32[512]{0:T(512)S(1)} %pad_maximum_fusion.5), channel_id=1, source_target_pairs={{0,1},{1,0},{2,3},{3,2},{4,5},{5,4},{6,7},{7,6},{8,9},{9,8},{10,11... | collective-permute-start | bytes 6152 | tf_op jit(solution)/shard_map/ppermute | solution.py:121
  47.2 3.6 %collective-permute-start.4 = (f32[512]{0:T(512)S(1)}, f32[512]{0:T(512)S(1)}, u32[]{:S(2)}, u32[]{:S(2)}) collective-permute-start(f32[512]{0:T(512)S(1)} %pad_maximum_fusion.6), channel_id=1, source_target_pairs={{0,1},{1,0},{2,3},{3,2},{4,5},{5,4},{6,7},{7,6},{8,9},{9,8},{10,11... | collective-permute-start | bytes 6152 | tf_op jit(solution)/shard_map/ppermute | solution.py:121
  51.1 3.7 %collective-permute-start.5 = (f32[1024]{0:T(1024)S(1)}, f32[1024]{0:T(1024)S(1)}, u32[]{:S(2)}, u32[]{:S(2)}) collective-permute-start(f32[1024]{0:T(1024)S(1)} %pad_maximum_fusion.3), channel_id=1, source_target_pairs={{0,1},{1,0},{2,3},{3,2},{4,5},{5,4},{6,7},{7,6},{8,9},{9,8},{10,11... | collective-permute-start | bytes 12296 | tf_op jit(solution)/shard_map/ppermute | solution.py:121
  57.2 6.9 %collective-permute-start.7 = (f32[8,1,512]{2,1,0:T(1,128)S(1)}, f32[8,1,512]{2,1,0:T(1,128)S(1)}, u32[]{:S(2)}, u32[]{:S(2)}) collective-permute-start(f32[8,1,512]{2,1,0:T(1,128)S(1)} %get-tuple-element.66), channel_id=1, source_target_pairs={{0,8},{8,16},{16,24},{24,2},{2,10},{10,18},{18,26},{26,4},{4,12},{... | collective-permute-start | bytes 49160 | tf_op jit(solution)/shard_map/ppermute | solution.py:51
  58.5 5.7 %collective-permute-start.6 = (f32[8,1,512]{2,1,0:T(1,128)S(1)}, f32[8,1,512]{2,1,0:T(1,128)S(1)}, u32[]{:S(2)}, u32[]{:S(2)}) collective-permute-start(f32[8,1,512]{2,1,0:T(1,128)S(1)} %get-tuple-element.67), channel_id=1, source_target_pairs={{8,0},{16,8},{24,16},{2,24},{10,2},{18,10},{26,18},{4,26},{12,4},{... | collective-permute-start | bytes 49160 | tf_op jit(solution)/shard_map/ppermute | solution.py:52
  59.8 4.3 %collective-permute-start.8 = (f32[8,16,1]{2,1,0:T(8,128)S(1)}, f32[8,16,1]{2,1,0:T(8,128)S(1)}, u32[]{:S(2)}, u32[]{:S(2)}) collective-permute-start(f32[8,16,1]{2,1,0:T(8,128)S(1)} %slice_select_fusion.5), channel_id=1, source_target_pairs={{0,1},{1,0},{2,3},{3,2},{4,5},{5,4},{6,7},{7,6},{8,9},{9,8},{10,11... | collective-permute-start | bytes 1544 | tf_op jit(solution)/shard_map/ppermute | solution.py:46
  64.8 10.4 %collective-permute-start.9 = (f32[8,1,512]{2,1,0:T(1,128)S(1)}, f32[8,1,512]{2,1,0:T(1,128)S(1)}, u32[]{:S(2)}, u32[]{:S(2)}) collective-permute-start(f32[8,1,512]{2,1,0:T(1,128)S(1)} %get-tuple-element.60), channel_id=1, source_target_pairs={{8,0},{16,8},{24,16},{2,24},{10,2},{18,10},{26,18},{4,26},{12,4},{... | collective-permute-start | bytes 49160 | tf_op jit(solution)/shard_map/ppermute | solution.py:52
  66.1 9.1 %collective-permute-start.10 = (f32[8,1,512]{2,1,0:T(1,128)S(1)}, f32[8,1,512]{2,1,0:T(1,128)S(1)}, u32[]{:S(2)}, u32[]{:S(2)}) collective-permute-start(f32[8,1,512]{2,1,0:T(1,128)S(1)} %get-tuple-element.61), channel_id=1, source_target_pairs={{0,8},{8,16},{16,24},{24,2},{2,10},{10,18},{18,26},{26,4},{4,12},{... | collective-permute-start | bytes 49160 | tf_op jit(solution)/shard_map/ppermute | solution.py:51
  70.8 4.3 %collective-permute-start.11 = (f32[8,16,1]{2,1,0:T(8,128)S(1)}, f32[8,16,1]{2,1,0:T(8,128)S(1)}, u32[]{:S(2)}, u32[]{:S(2)}) collective-permute-start(f32[8,16,1]{2,1,0:T(8,128)S(1)} %slice_select_fusion.4), channel_id=1, source_target_pairs={{0,1},{1,0},{2,3},{3,2},{4,5},{5,4},{6,7},{7,6},{8,9},{9,8},{10,11... | collective-permute-start | bytes 1544 | tf_op jit(solution)/shard_map/ppermute | solution.py:46
  76.0 9.9 %collective-permute-start.12 = (f32[8,1,512]{2,1,0:T(1,128)S(1)}, f32[8,1,512]{2,1,0:T(1,128)S(1)}, u32[]{:S(2)}, u32[]{:S(2)}) collective-permute-start(f32[8,1,512]{2,1,0:T(1,128)S(1)} %get-tuple-element.52), channel_id=1, source_target_pairs={{8,0},{16,8},{24,16},{2,24},{10,2},{18,10},{26,18},{4,26},{12,4},{... | collective-permute-start | bytes 49160 | tf_op jit(solution)/shard_map/ppermute | solution.py:52
  77.3 8.6 %collective-permute-start.13 = (f32[8,1,512]{2,1,0:T(1,128)S(1)}, f32[8,1,512]{2,1,0:T(1,128)S(1)}, u32[]{:S(2)}, u32[]{:S(2)}) collective-permute-start(f32[8,1,512]{2,1,0:T(1,128)S(1)} %get-tuple-element.53), channel_id=1, source_target_pairs={{0,8},{8,16},{16,24},{24,2},{2,10},{10,18},{18,26},{26,4},{4,12},{... | collective-permute-start | bytes 49160 | tf_op jit(solution)/shard_map/ppermute | solution.py:51
  81.6 4.3 %collective-permute-start.14 = (f32[8,16,1]{2,1,0:T(8,128)S(1)}, f32[8,16,1]{2,1,0:T(8,128)S(1)}, u32[]{:S(2)}, u32[]{:S(2)}) collective-permute-start(f32[8,16,1]{2,1,0:T(8,128)S(1)} %slice_select_fusion.3), channel_id=1, source_target_pairs={{0,1},{1,0},{2,3},{3,2},{4,5},{5,4},{6,7},{7,6},{8,9},{9,8},{10,11... | collective-permute-start | bytes 1544 | tf_op jit(solution)/shard_map/ppermute | solution.py:46
  87.5 8.9 %collective-permute-start.15 = (f32[8,1,512]{2,1,0:T(1,128)S(1)}, f32[8,1,512]{2,1,0:T(1,128)S(1)}, u32[]{:S(2)}, u32[]{:S(2)}) collective-permute-start(f32[8,1,512]{2,1,0:T(1,128)S(1)} %get-tuple-element.44), channel_id=1, source_target_pairs={{8,0},{16,8},{24,16},{2,24},{10,2},{18,10},{26,18},{4,26},{12,4},{... | collective-permute-start | bytes 49160 | tf_op jit(solution)/shard_map/ppermute | solution.py:52
  88.8 7.6 %collective-permute-start.16 = (f32[8,1,512]{2,1,0:T(1,128)S(1)}, f32[8,1,512]{2,1,0:T(1,128)S(1)}, u32[]{:S(2)}, u32[]{:S(2)}) collective-permute-start(f32[8,1,512]{2,1,0:T(1,128)S(1)} %get-tuple-element.45), channel_id=1, source_target_pairs={{0,8},{8,16},{16,24},{24,2},{2,10},{10,18},{18,26},{26,4},{4,12},{... | collective-permute-start | bytes 49160 | tf_op jit(solution)/shard_map/ppermute | solution.py:51
  92.1 4.3 %collective-permute-start.17 = (f32[8,16,1]{2,1,0:T(8,128)S(1)}, f32[8,16,1]{2,1,0:T(8,128)S(1)}, u32[]{:S(2)}, u32[]{:S(2)}) collective-permute-start(f32[8,16,1]{2,1,0:T(8,128)S(1)} %slice_select_fusion.2), channel_id=1, source_target_pairs={{0,1},{1,0},{2,3},{3,2},{4,5},{5,4},{6,7},{7,6},{8,9},{9,8},{10,11... | collective-permute-start | bytes 1544 | tf_op jit(solution)/shard_map/ppermute | solution.py:46
  100.3 10.9 %all-to-all-start.4 = ((f32[32,1,32]{2,1,0:T(1,128)}), f32[32,1,32]{2,1,0:T(1,128)S(1)}, u32[]{:S(2)}, u32[]{:S(2)}) async-start(f32[32,1,32]{2,1,0:T(1,128)} %broadcast_in_dim.40), calls=%async_computation.4 | async-start | bytes 32768 | tf_op jit(solution)/shard_map/all_to_all | solution.py:109
  112.4 6.7 %collective-permute-start.24 = (f32[256]{0:T(256)S(1)}, f32[256]{0:T(256)S(1)}, u32[]{:S(2)}, u32[]{:S(2)}) collective-permute-start(f32[256]{0:T(256)S(1)} %dynamic-slice_subtract_fusion.2), channel_id=1, source_target_pairs={{0,1},{1,0},{2,3},{3,2},{4,5},{5,4},{6,7},{7,6},{8,9},{9,8},{10,11... | collective-permute-start | bytes 3080 | tf_op jit(solution)/shard_map/ppermute | solution.py:121
  113.2 14.2 %collective-permute-start.18 = (f32[8,1,512]{2,1,0:T(1,128)S(1)}, f32[8,1,512]{2,1,0:T(1,128)S(1)}, u32[]{:S(2)}, u32[]{:S(2)}) collective-permute-start(f32[8,1,512]{2,1,0:T(1,128)S(1)} %get-tuple-element.36), channel_id=1, source_target_pairs={{8,0},{16,8},{24,16},{2,24},{10,2},{18,10},{26,18},{4,26},{12,4},{... | collective-permute-start | bytes 49160 | tf_op jit(solution)/shard_map/ppermute | solution.py:52
  114.5 12.9 %collective-permute-start.19 = (f32[8,1,512]{2,1,0:T(1,128)S(1)}, f32[8,1,512]{2,1,0:T(1,128)S(1)}, u32[]{:S(2)}, u32[]{:S(2)}) collective-permute-start(f32[8,1,512]{2,1,0:T(1,128)S(1)} %get-tuple-element.37), channel_id=1, source_target_pairs={{0,8},{8,16},{16,24},{24,2},{2,10},{10,18},{18,26},{26,4},{4,12},{... | collective-permute-start | bytes 49160 | tf_op jit(solution)/shard_map/ppermute | solution.py:51
  117.7 9.7 %collective-permute-start.20 = (f32[8,16,1]{2,1,0:T(8,128)S(1)}, f32[8,16,1]{2,1,0:T(8,128)S(1)}, u32[]{:S(2)}, u32[]{:S(2)}) collective-permute-start(f32[8,16,1]{2,1,0:T(8,128)S(1)} %slice_select_fusion.1), channel_id=1, source_target_pairs={{0,1},{1,0},{2,3},{3,2},{4,5},{5,4},{6,7},{7,6},{8,9},{9,8},{10,11... | collective-permute-start | bytes 1544 | tf_op jit(solution)/shard_map/ppermute | solution.py:46
  129.3 6.9 %collective-permute-start.22 = (f32[8,1,512]{2,1,0:T(1,128)S(1)}, f32[8,1,512]{2,1,0:T(1,128)S(1)}, u32[]{:S(2)}, u32[]{:S(2)}) collective-permute-start(f32[8,1,512]{2,1,0:T(1,128)S(1)} %get-tuple-element.28), channel_id=1, source_target_pairs={{0,8},{8,16},{16,24},{24,2},{2,10},{10,18},{18,26},{26,4},{4,12},{... | collective-permute-start | bytes 49160 | tf_op jit(solution)/shard_map/ppermute | solution.py:51
  130.6 5.6 %collective-permute-start.21 = (f32[8,1,512]{2,1,0:T(1,128)S(1)}, f32[8,1,512]{2,1,0:T(1,128)S(1)}, u32[]{:S(2)}, u32[]{:S(2)}) collective-permute-start(f32[8,1,512]{2,1,0:T(1,128)S(1)} %get-tuple-element.29), channel_id=1, source_target_pairs={{8,0},{16,8},{24,16},{2,24},{10,2},{18,10},{26,18},{4,26},{12,4},{... | collective-permute-start | bytes 49160 | tf_op jit(solution)/shard_map/ppermute | solution.py:52
  131.9 4.3 %collective-permute-start.23 = (f32[8,16,1]{2,1,0:T(8,128)S(1)}, f32[8,16,1]{2,1,0:T(8,128)S(1)}, u32[]{:S(2)}, u32[]{:S(2)}) collective-permute-start(f32[8,16,1]{2,1,0:T(8,128)S(1)} %slice_select_fusion), channel_id=1, source_target_pairs={{0,1},{1,0},{2,3},{3,2},{4,5},{5,4},{6,7},{7,6},{8,9},{9,8},{10,11... | collective-permute-start | bytes 1544 | tf_op jit(solution)/shard_map/ppermute | solution.py:46
  137.1 3.6 %collective-permute-start.27 = (f32[512]{0:T(512)S(1)}, f32[512]{0:T(512)S(1)}, u32[]{:S(2)}, u32[]{:S(2)}) collective-permute-start(f32[512]{0:T(512)S(1)} %pad_maximum_fusion.7), channel_id=1, source_target_pairs={{0,1},{1,0},{2,3},{3,2},{4,5},{5,4},{6,7},{7,6},{8,9},{9,8},{10,11... | collective-permute-start | bytes 6152 | tf_op jit(solution)/shard_map/ppermute | solution.py:121
  141.1 6.5 %collective-permute-start.28 = (f32[512]{0:T(512)S(1)}, f32[512]{0:T(512)S(1)}, u32[]{:S(2)}, u32[]{:S(2)}) collective-permute-start(f32[512]{0:T(512)S(1)} %pad_maximum_fusion.8), channel_id=1, source_target_pairs={{0,1},{1,0},{2,3},{3,2},{4,5},{5,4},{6,7},{7,6},{8,9},{9,8},{10,11... | collective-permute-start | bytes 6152 | tf_op jit(solution)/shard_map/ppermute | solution.py:121
  142.9 13.5 %all-to-all-start.3 = ((f32[2,8,16,512]{3,2,0,1:T(8,128)}), f32[2,8,16,512]{3,2,0,1:T(8,128)S(1)}, u32[]{:S(2)}, u32[]{:S(2)}) async-start(f32[2,8,16,512]{3,2,0,1:T(8,128)} %pad_maximum_fusion.1), calls=%async_computation.3 | async-start | bytes 1048576 | tf_op jit(solution)/shard_map/all_to_all | solution.py:265
  147.9 3.7 %collective-permute-start.29 = (f32[1024]{0:T(1024)S(1)}, f32[1024]{0:T(1024)S(1)}, u32[]{:S(2)}, u32[]{:S(2)}) collective-permute-start(f32[1024]{0:T(1024)S(1)} %pad_maximum_fusion.4), channel_id=1, source_target_pairs={{0,1},{1,0},{2,3},{3,2},{4,5},{5,4},{6,7},{7,6},{8,9},{9,8},{10,11... | collective-permute-start | bytes 12296 | tf_op jit(solution)/shard_map/ppermute | solution.py:121
  (24 other events, 303.7 us)
